TPU v7x, 32 devices: a whole 2x2x4 slice. The times are simulated.
32 devices in a mesh: alt: 8 (over z, y), raan: 4 (over x, core).
Axes of the slice: x: 2, y: 2, z: 4, core: 2. Of those that a mesh axis runs over, the one named last changes fastest.
Arguments:
- source: float32 [32, 64, 1024], P('alt', None, 'raan'), may hold values from -6 to 6
- k_alt: float32 [32, 64, 1024], P('alt', None, 'raan'), may hold values from 20 to 400
- k_inc: float32 [32, 64, 1024], P('alt', None, 'raan'), may hold values from 20 to 400
- k_raan: float32 [32, 64, 1024], P('alt', None, 'raan'), may hold values from 20 to 400
Outputs:
- density: float32 [32, 64, 1024], P('alt', None, 'raan')
- scaled_residual: float32 [32, 64, 1024], P('alt', None, 'raan')
All inputs are finite; a program needn't handle non-finite values.
Results may differ from a plain program's by a relative error of at most 0.00018.
Values sent between devices are 32-bit elements; how exact they have to be, the bound alone decides.
No kernel may reach another device: no remote copies, remote signals or barrier semaphores. Data moves between devices by JAX's collectives and lax.ppermute only.
A program may use at most 128 MiB of HBM per device.

v0:
```python
import jax
import jax.numpy as jnp
from jax import lax
from jax.sharding import PartitionSpec as P

SWEEPS = 2
COARSE_SWEEPS = 4


OMEGA = 0.75


def with_halo(shard, sides, width, wrap):
    for axis, dim in sides:
        count, length = (lax.axis_size(axis), shard.shape[dim])
        up = [(i, (i + 1) % count) for i in range(count if wrap else count - 1)]
        down = [(j, i) for i, j in up]
        last = lax.slice_in_dim(shard, length - width, length, axis=dim)
        leading = lax.slice_in_dim(shard, 0, width, axis=dim)
        before = lax.ppermute(last, axis, up)
        after = lax.ppermute(leading, axis, down)
        shard = jnp.concatenate([before, shard, after], axis=dim)
    return shard


def shifted(block, axis, distance):
    devices = range(lax.axis_size(axis))
    route = [(i - distance, i) for i in devices if i - distance in devices]
    return lax.ppermute(block, axis, route)


def from_partner(block, axis, distance):
    count = lax.axis_size(axis)
    route = []
    for low in range(count):
        high = low | 1 << distance
        if high != low and high < count:
            route += [(low, high), (high, low)]
    return lax.ppermute(block, axis, route)


def coarsen(values):
    depth, width, length = values.shape
    return values.reshape(depth // 2, 2, width // 2, 2, length // 2, 2).mean(axis=(1, 3, 5))


def refine(values):
    return jnp.repeat(jnp.repeat(jnp.repeat(values, 2, 0), 2, 1), 2, 2)


def alt_ext(values):
    return with_halo(values, (("alt", 0),), 1, False)


def raan_ext(values):
    return with_halo(values, (("raan", 2),), 1, True)


def plain_alt(values):
    padded = alt_ext(values)
    return (padded[:-2], padded[2:])


def fold_alt(values):
    below = shifted(values[-1:], "alt", 2)
    above = shifted(values[:1], "alt", -2)
    v_down = jnp.concatenate([below, values[:-1]], 0)
    v_up = jnp.concatenate([values[1:], above], 0)
    return (v_down, v_up)


def field_near(field):
    v_down, v_up = plain_alt(field)
    wrapped = raan_ext(field)
    return (v_down, v_up, wrapped[:, :, :-2], wrapped[:, :, 2:])


def fold_near(field):
    v_down, v_up = fold_alt(field)
    wrapped = raan_ext(field)
    return (v_down, v_up, wrapped[:, :, :-2], wrapped[:, :, 2:])


def make_weights(coef_alt, coef_inc, coef_raan, factor, alt_pair):
    alt_down, alt_up = alt_pair(coef_alt)
    w_alt_lo = factor * 0.5 * (coef_alt + alt_down)
    w_alt_hi = factor * 0.5 * (coef_alt + alt_up)
    inner_faces = factor * 0.5 * (coef_inc[:, :-1] + coef_inc[:, 1:])
    zero_inc = jnp.zeros_like(coef_inc[:, :1])
    w_inc_lo = jnp.concatenate([zero_inc, inner_faces], 1)
    w_inc_hi = jnp.concatenate([inner_faces, zero_inc], 1)
    wrapped = raan_ext(coef_raan)
    w_raan_lo = factor * 0.5 * (coef_raan + wrapped[:, :, :-2])
    w_raan_hi = factor * 0.5 * (coef_raan + wrapped[:, :, 2:])
    diagonal = 1.0 + (w_alt_lo + w_alt_hi + w_inc_lo + w_inc_hi + w_raan_lo + w_raan_hi)
    return (w_alt_lo, w_alt_hi, w_inc_lo, w_inc_hi, w_raan_lo, w_raan_hi, diagonal)


def apply_op(weights, field, near):
    w_alt_lo, w_alt_hi, w_inc_lo, w_inc_hi, w_raan_lo, w_raan_hi, diagonal = weights
    v_down, v_up, v_left, v_right = near(field)
    zero_inc = jnp.zeros_like(field[:, :1])
    v_prev = jnp.concatenate([zero_inc, field[:, :-1]], 1)
    v_next = jnp.concatenate([field[:, 1:], zero_inc], 1)
    beside = (
        w_alt_lo * v_down
        + w_alt_hi * v_up
        + w_inc_lo * v_prev
        + w_inc_hi * v_next
        + w_raan_lo * v_left
        + w_raan_hi * v_right
    )
    return diagonal * field - beside


def smooth(field, target, weights, near, repeats):
    for _ in range(repeats):
        field = field + OMEGA * (target - apply_op(weights, field, near)) / weights[6]
    return field


def coarse_solve(target, weights, near):
    field = OMEGA * target / weights[6]
    return smooth(field, target, weights, near, COARSE_SWEEPS - 1)


def shards(source, k_alt, k_inc, k_raan):
    weights_one = make_weights(k_alt, k_inc, k_raan, 1.0, plain_alt)
    coef_two = (coarsen(k_alt), coarsen(k_inc), coarsen(k_raan))
    weights_two = make_weights(coef_two[0], coef_two[1], coef_two[2], 0.25, plain_alt)
    coef_three = (coarsen(coef_two[0]), coarsen(coef_two[1]), coarsen(coef_two[2]))
    density = smooth(source, source, weights_one, field_near, SWEEPS)
    rhs_two = coarsen(source - apply_op(weights_one, density, field_near))
    correction = OMEGA * rhs_two / weights_two[6]
    correction = smooth(correction, rhs_two, weights_two, field_near, SWEEPS - 1)
    rhs_three = coarsen(rhs_two - apply_op(weights_two, correction, field_near))
    height = rhs_three.shape[0]
    parity = lax.axis_index("alt") % 2
    own_part = jnp.stack((rhs_three, coef_three[0], coef_three[1], coef_three[2]))
    theirs = from_partner(own_part, "alt", 0)
    low_half = jnp.where(parity == 0, own_part, theirs)
    high_half = jnp.where(parity == 0, theirs, own_part)
    pair_block = jnp.concatenate([low_half, high_half], axis=1)
    weights_three = make_weights(pair_block[1], pair_block[2], pair_block[3], 0.0625, fold_alt)
    pair_result = coarse_solve(pair_block[0], weights_three, fold_near)
    coarse_part = lax.dynamic_slice_in_dim(pair_result, parity * height, height, 0)
    correction = correction + refine(coarse_part)
    correction = smooth(correction, rhs_two, weights_two, field_near, SWEEPS)
    density = density + refine(correction)
    density = smooth(density, source, weights_one, field_near, SWEEPS)
    scaled_residual = (source - apply_op(weights_one, density, field_near)) / weights_one[6]
    return (density, scaled_residual)


def solution(mesh):
    in_specs = (
        P("alt", None, "raan"),
        P("alt", None, "raan"),
        P("alt", None, "raan"),
        P("alt", None, "raan"),
    )
    out_specs = (P("alt", None, "raan"), P("alt", None, "raan"))
    return jax.shard_map(shards, mesh=mesh, in_specs=in_specs, out_specs=out_specs, check_vma=False)
```

profile of v0, /device:TPU:8, one launch (start us, length us, event | category | flops | bytes accessed | tf_op | source)
XLA Modules:
  0.0 303.8 jit_solution(8655892247528024936)
XLA Ops:
  2.6 3.4 %collective-permute-start = (f32[1,64,256]{1,2,0:T(8,128)}, f32[1,64,256]{1,2,0:T(8,128)S(1)}, u32[]{:S(2)}, u32[]{:S(2)}) collective-permute-start(f32[1,64,256]{1,2,0:T(8,128)} %get-tuple-element.47), channel_id=1, source_target_pairs={{0,4},{4,8},{8,12},{12,16},{16,20},{20,24},{24,28},{1,5},{5,9},{9,... | collective-permute-start | bytes 196616 | tf_op jit(solution)/shard_map/ppermute | solution.py:20
  6.0 3.3 %collective-permute-start.1 = (f32[1,64,256]{1,2,0:T(8,128)}, f32[1,64,256]{1,2,0:T(8,128)S(1)}, u32[]{:S(2)}, u32[]{:S(2)}) collective-permute-start(f32[1,64,256]{1,2,0:T(8,128)} %get-tuple-element.46), channel_id=1, source_target_pairs={{4,0},{8,4},{12,8},{16,12},{20,16},{24,20},{28,24},{5,1},{9,5},{13... | collective-permute-start | bytes 196616 | tf_op jit(solution)/shard_map/ppermute | solution.py:21
  11.1 1.7 collective-permute-start.3
  15.3 18.9 %reshape.97 = f32[2,2,32,2,128,2]{5,4,3,2,1,0:T(8,128)} reshape(f32[4,64,256]{2,1,0:T(8,128)} %param.5) | data formatting | bytes 524288 | tf_op jit(solution)/shard_map/reshape | solution.py:44
  34.2 18.1 %reshape.98 = f32[2,2,32,2,128,2]{5,4,3,2,1,0:T(8,128)} reshape(f32[4,64,256]{2,1,0:T(8,128)S(1)} %copy-done) | data formatting | bytes 524288 | tf_op jit(solution)/shard_map/reshape | solution.py:44
  52.3 18.1 %reshape.99 = f32[2,2,32,2,128,2]{5,4,3,2,1,0:T(8,128)} reshape(f32[4,64,256]{2,1,0:T(8,128)S(1)} %copy-done.1) | data formatting | bytes 524288 | tf_op jit(solution)/shard_map/reshape | solution.py:44
  71.6 7.0 %reduce_sum.82 = f32[2,32,128]{2,1,0:T(8,128)S(1)} reduce(f32[2,2,32,2,128,2]{5,4,3,2,1,0:T(8,128)} %reshape.97, f32[]{:T(128)} %constant.19.clone.1), dimensions={1,3,5}, to_apply=%region_1.0 | reduce | flops 57344 | bytes 294916 | tf_op jit(solution)/shard_map/reduce_sum | solution.py:44
  79.2 7.0 %reduce_sum.83 = f32[2,32,128]{2,1,0:T(8,128)S(1)} reduce(f32[2,2,32,2,128,2]{5,4,3,2,1,0:T(8,128)} %reshape.98, f32[]{:T(128)} %constant.19.clone.1), dimensions={1,3,5}, to_apply=%region_2.0 | reduce | flops 57344 | bytes 294916 | tf_op jit(solution)/shard_map/reduce_sum | solution.py:44
  86.2 7.0 %reduce_sum.87 = f32[2,32,128]{2,1,0:T(8,128)S(1)} reduce(f32[2,2,32,2,128,2]{5,4,3,2,1,0:T(8,128)} %reshape.99, f32[]{:T(128)} %constant.19.clone.1), dimensions={1,3,5}, to_apply=%region_3.0 | reduce | flops 57344 | bytes 294916 | tf_op jit(solution)/shard_map/reduce_sum | solution.py:44
  97.7 2.1 fusion.227
  100.3 2.0 reduce_sum.108
  103.7 2.5 collective-permute-start.4
  106.3 4.2 %collective-permute-start.5 = (f32[1,64,256]{1,2,0:T(8,128)}, f32[1,64,256]{1,2,0:T(8,128)S(1)}, u32[]{:S(2)}, u32[]{:S(2)}) collective-permute-start(f32[1,64,256]{1,2,0:T(8,128)} %get-tuple-element.53), channel_id=1, source_target_pairs={{4,0},{8,4},{12,8},{16,12},{20,16},{24,20},{28,24},{5,1},{9,5},{13... | collective-permute-start | bytes 196616 | tf_op jit(solution)/shard_map/ppermute | solution.py:21
  113.7 2.5 collective-permute-start.16
  116.2 2.0 fusion.71
  118.2 4.5 %collective-permute-start.8 = (f32[1,64,256]{1,2,0:T(8,128)S(1)}, f32[1,64,256]{1,2,0:T(8,128)S(1)}, u32[]{:S(2)}, u32[]{:S(2)}) collective-permute-start(f32[1,64,256]{1,2,0:T(8,128)S(1)} %get-tuple-element.42), channel_id=1, source_target_pairs={{0,4},{4,8},{8,12},{12,16},{16,20},{20,24},{24,28},{1,5},{5,9},{9,... | collective-permute-start | bytes 196616 | tf_op jit(solution)/shard_map/ppermute | solution.py:20
  122.8 2.2 collective-permute-start.9
  128.1 2.6 collective-permute-done.9
  131.7 3.2 %collective-permute-start.12 = (f32[1,64,256]{1,2,0:T(8,128)S(1)}, f32[1,64,256]{1,2,0:T(8,128)S(1)}, u32[]{:S(2)}, u32[]{:S(2)}) collective-permute-start(f32[1,64,256]{1,2,0:T(8,128)S(1)} %get-tuple-element.36), channel_id=1, source_target_pairs={{0,4},{4,8},{8,12},{12,16},{16,20},{20,24},{24,28},{1,5},{5,9},{9,... | collective-permute-start | bytes 196616 | tf_op jit(solution)/shard_map/ppermute | solution.py:20
  134.9 3.5 %collective-permute-start.13 = (f32[1,64,256]{1,2,0:T(8,128)S(1)}, f32[1,64,256]{1,2,0:T(8,128)S(1)}, u32[]{:S(2)}, u32[]{:S(2)}) collective-permute-start(f32[1,64,256]{1,2,0:T(8,128)S(1)} %get-tuple-element.37), channel_id=1, source_target_pairs={{4,0},{8,4},{12,8},{16,12},{20,16},{24,20},{28,24},{5,1},{9,5},{13... | collective-permute-start | bytes 196616 | tf_op jit(solution)/shard_map/ppermute | solution.py:21
  138.5 1.7 collective-permute-start.15
  141.5 2.2 collective-permute-start.17
  147.2 18.9 %reshape.96 = f32[2,2,32,2,128,2]{5,4,3,2,1,0:T(8,128)} reshape(f32[4,64,256]{2,1,0:T(8,128)} %copy.70) | data formatting | bytes 524288 | tf_op jit(solution)/shard_map/reshape | solution.py:44
  166.1 7.0 %reduce_sum.81 = f32[2,32,128]{2,1,0:T(8,128)S(1)} reduce(f32[2,2,32,2,128,2]{5,4,3,2,1,0:T(8,128)} %reshape.96, f32[]{:T(128)} %constant.19.clone.1), dimensions={1,3,5}, to_apply=%region_0.0 | reduce | flops 57344 | bytes 294916 | tf_op jit(solution)/shard_map/reduce_sum | solution.py:44
  174.1 1.7 collective-permute-start.23
  175.9 3.6 %collective-permute-start.20 = (f32[1,32,128]{2,1,0:T(8,128)S(1)}, f32[1,32,128]{2,1,0:T(8,128)S(1)}, u32[]{:S(2)}, u32[]{:S(2)}) collective-permute-start(f32[1,32,128]{2,1,0:T(8,128)S(1)} %get-tuple-element.88), channel_id=1, source_target_pairs={{0,4},{4,8},{8,12},{12,16},{16,20},{20,24},{24,28},{1,5},{5,9},{9,... | collective-permute-start | bytes 49160 | tf_op jit(solution)/shard_map/ppermute | solution.py:20
  179.5 3.1 %collective-permute-start.21 = (f32[1,32,128]{2,1,0:T(8,128)S(1)}, f32[1,32,128]{2,1,0:T(8,128)S(1)}, u32[]{:S(2)}, u32[]{:S(2)}) collective-permute-start(f32[1,32,128]{2,1,0:T(8,128)S(1)} %get-tuple-element.89), channel_id=1, source_target_pairs={{4,0},{8,4},{12,8},{16,12},{20,16},{24,20},{28,24},{5,1},{9,5},{13... | collective-permute-start | bytes 49160 | tf_op jit(solution)/shard_map/ppermute | solution.py:21
  182.7 2.5 collective-permute-done.21
  187.1 4.1 %collective-permute-start.24 = (f32[1,32,128]{2,1,0:T(8,128)S(1)}, f32[1,32,128]{2,1,0:T(8,128)S(1)}, u32[]{:S(2)}, u32[]{:S(2)}) collective-permute-start(f32[1,32,128]{2,1,0:T(8,128)S(1)} %get-tuple-element.76), channel_id=1, source_target_pairs={{0,4},{4,8},{8,12},{12,16},{16,20},{20,24},{24,28},{1,5},{5,9},{9,... | collective-permute-start | bytes 49160 | tf_op jit(solution)/shard_map/ppermute | solution.py:20
  191.2 2.6 collective-permute-start.25
  193.9 3.0 collective-permute-done.25
  196.9 2.0 reduce_sum.105
  200.4 1.8 collective-permute-start.28
  202.2 2.2 collective-permute-done.28
  204.5 1.7 collective-permute-start.32
  206.2 3.1 %collective-permute-start.29 = (f32[1,16,64]{2,1,0:T(8,128)S(1)}, f32[1,16,64]{2,1,0:T(8,128)S(1)}, u32[]{:S(2)}, u32[]{:S(2)}) collective-permute-start(f32[1,16,64]{2,1,0:T(8,128)S(1)} %slice_bitcast_fusion.1), channel_id=1, source_target_pairs={{0,8},{4,12},{8,16},{12,20},{16,24},{20,28},{1,9},{5,13},{9,17},{1... | collective-permute-start | bytes 12296 | tf_op jit(solution)/shard_map/ppermute | solution.py:29
  209.3 2.8 collective-permute-start.30
  212.1 2.7 collective-permute-done.30
  215.0 1.7 collective-permute-start.36
  216.8 1.9 collective-permute-start.33
  218.7 3.9 %collective-permute-start.34 = (f32[1,16,64]{2,1,0:T(8,128)S(1)}, f32[1,16,64]{2,1,0:T(8,128)S(1)}, u32[]{:S(2)}, u32[]{:S(2)}) collective-permute-start(f32[1,16,64]{2,1,0:T(8,128)S(1)} %get-tuple-element.113), channel_id=1, source_target_pairs={{8,0},{12,4},{16,8},{20,12},{24,16},{28,20},{9,1},{13,5},{17,9},{2... | collective-permute-start | bytes 12296 | tf_op jit(solution)/shard_map/ppermute | solution.py:29
  224.4 1.7 collective-permute-start.40
  226.1 1.9 collective-permute-start.37
  228.1 3.9 %collective-permute-start.38 = (f32[1,16,64]{2,1,0:T(8,128)S(1)}, f32[1,16,64]{2,1,0:T(8,128)S(1)}, u32[]{:S(2)}, u32[]{:S(2)}) collective-permute-start(f32[1,16,64]{2,1,0:T(8,128)S(1)} %get-tuple-element.107), channel_id=1, source_target_pairs={{8,0},{12,4},{16,8},{20,12},{24,16},{28,20},{9,1},{13,5},{17,9},{2... | collective-permute-start | bytes 12296 | tf_op jit(solution)/shard_map/ppermute | solution.py:29
  233.8 1.7 collective-permute-start.44
  235.5 1.9 collective-permute-start.41
  237.4 3.9 %collective-permute-start.42 = (f32[1,16,64]{2,1,0:T(8,128)S(1)}, f32[1,16,64]{2,1,0:T(8,128)S(1)}, u32[]{:S(2)}, u32[]{:S(2)}) collective-permute-start(f32[1,16,64]{2,1,0:T(8,128)S(1)} %get-tuple-element.101), channel_id=1, source_target_pairs={{8,0},{12,4},{16,8},{20,12},{24,16},{28,20},{9,1},{13,5},{17,9},{2... | collective-permute-start | bytes 12296 | tf_op jit(solution)/shard_map/ppermute | solution.py:29
  245.2 3.2 %collective-permute-start.45 = (f32[1,32,128]{2,1,0:T(8,128)S(1)}, f32[1,32,128]{2,1,0:T(8,128)S(1)}, u32[]{:S(2)}, u32[]{:S(2)}) collective-permute-start(f32[1,32,128]{2,1,0:T(8,128)S(1)} %get-tuple-element.70), channel_id=1, source_target_pairs={{0,4},{4,8},{8,12},{12,16},{16,20},{20,24},{24,28},{1,5},{5,9},{9,... | collective-permute-start | bytes 49160 | tf_op jit(solution)/shard_map/ppermute | solution.py:20
  248.3 3.6 %collective-permute-start.46 = (f32[1,32,128]{2,1,0:T(8,128)S(1)}, f32[1,32,128]{2,1,0:T(8,128)S(1)}, u32[]{:S(2)}, u32[]{:S(2)}) collective-permute-start(f32[1,32,128]{2,1,0:T(8,128)S(1)} %get-tuple-element.71), channel_id=1, source_target_pairs={{4,0},{8,4},{12,8},{16,12},{20,16},{24,20},{28,24},{5,1},{9,5},{13... | collective-permute-start | bytes 49160 | tf_op jit(solution)/shard_map/ppermute | solution.py:21
  252.0 2.0 collective-permute-done.46
  254.2 1.7 collective-permute-start.52
  255.9 3.0 collective-permute-start.49
  258.9 3.7 %collective-permute-start.50 = (f32[1,32,128]{2,1,0:T(8,128)S(1)}, f32[1,32,128]{2,1,0:T(8,128)S(1)}, u32[]{:S(2)}, u32[]{:S(2)}) collective-permute-start(f32[1,32,128]{2,1,0:T(8,128)S(1)} %get-tuple-element.65), channel_id=1, source_target_pairs={{4,0},{8,4},{12,8},{16,12},{20,16},{24,20},{28,24},{5,1},{9,5},{13... | collective-permute-start | bytes 49160 | tf_op jit(solution)/shard_map/ppermute | solution.py:21
  262.7 1.9 collective-permute-done.50
  265.2 3.2 %collective-permute-start.53 = (f32[1,64,256]{1,2,0:T(8,128)S(1)}, f32[1,64,256]{1,2,0:T(8,128)S(1)}, u32[]{:S(2)}, u32[]{:S(2)}) collective-permute-start(f32[1,64,256]{1,2,0:T(8,128)S(1)} %get-tuple-element.30), channel_id=1, source_target_pairs={{0,4},{4,8},{8,12},{12,16},{16,20},{20,24},{24,28},{1,5},{5,9},{9,... | collective-permute-start | bytes 196616 | tf_op jit(solution)/shard_map/ppermute | solution.py:20
  268.3 3.6 %collective-permute-start.54 = (f32[1,64,256]{1,2,0:T(8,128)S(1)}, f32[1,64,256]{1,2,0:T(8,128)S(1)}, u32[]{:S(2)}, u32[]{:S(2)}) collective-permute-start(f32[1,64,256]{1,2,0:T(8,128)S(1)} %get-tuple-element.31), channel_id=1, source_target_pairs={{4,0},{8,4},{12,8},{16,12},{20,16},{24,20},{28,24},{5,1},{9,5},{13... | collective-permute-start | bytes 196616 | tf_op jit(solution)/shard_map/ppermute | solution.py:21
  272.0 1.7 collective-permute-start.56
  276.2 2.8 collective-permute-start.57
  279.0 3.9 %collective-permute-start.58 = (f32[1,64,256]{1,2,0:T(8,128)S(1)}, f32[1,64,256]{1,2,0:T(8,128)S(1)}, u32[]{:S(2)}, u32[]{:S(2)}) collective-permute-start(f32[1,64,256]{1,2,0:T(8,128)S(1)} %get-tuple-element.25), channel_id=1, source_target_pairs={{4,0},{8,4},{12,8},{16,12},{20,16},{24,20},{28,24},{5,1},{9,5},{13... | collective-permute-start | bytes 196616 | tf_op jit(solution)/shard_map/ppermute | solution.py:21
  286.0 2.1 collective-permute-done.58
  289.1 2.1 collective-permute-start.61
  291.2 4.7 %collective-permute-start.62 = (f32[1,64,256]{1,2,0:T(8,128)S(1)}, f32[1,64,256]{1,2,0:T(8,128)S(1)}, u32[]{:S(2)}, u32[]{:S(2)}) collective-permute-start(f32[1,64,256]{1,2,0:T(8,128)S(1)} %get-tuple-element.19), channel_id=1, source_target_pairs={{4,0},{8,4},{12,8},{16,12},{20,16},{24,20},{28,24},{5,1},{9,5},{13... | collective-permute-start | bytes 196616 | tf_op jit(solution)/shard_map/ppermute | solution.py:21
  295.9 1.7 collective-permute-start.64
  300.8 2.1 fusion.4
  (186 shorter events, 50.0 us)
Async XLA Ops:
  2.6 113.6 %collective-permute-start = (f32[1,64,256]{1,2,0:T(8,128)}, f32[1,64,256]{1,2,0:T(8,128)S(1)}, u32[]{:S(2)}, u32[]{:S(2)}) collective-permute-start(f32[1,64,256]{1,2,0:T(8,128)} %get-tuple-element.47), channel_id=1, source_target_pairs={{0,4},{4,8},{8,12},{12,16},{16,20},{20,24},{24,28},{1,5},{5,9},{9,... | collective-permute-start | bytes 196616 | tf_op jit(solution)/shard_map/ppermute | solution.py:20
  6.0 110.2 %collective-permute-start.1 = (f32[1,64,256]{1,2,0:T(8,128)}, f32[1,64,256]{1,2,0:T(8,128)S(1)}, u32[]{:S(2)}, u32[]{:S(2)}) collective-permute-start(f32[1,64,256]{1,2,0:T(8,128)} %get-tuple-element.46), channel_id=1, source_target_pairs={{4,0},{8,4},{12,8},{16,12},{20,16},{24,20},{28,24},{5,1},{9,5},{13... | collective-permute-start | bytes 196616 | tf_op jit(solution)/shard_map/ppermute | solution.py:21
  11.1 92.7 %collective-permute-start.2 = (f32[4,64,1]{1,2,0:T(1,128)}, f32[4,64,1]{1,2,0:T(1,128)S(1)}, u32[]{:S(2)}, u32[]{:S(2)}) collective-permute-start(f32[4,64,1]{1,2,0:T(1,128)} %get-tuple-element.49), channel_id=1, source_target_pairs={{0,1},{1,2},{2,3},{3,0},{4,5},{5,6},{6,7},{7,4},{8,9},{9,10},{10,1... | collective-permute-start | bytes 3080 | tf_op jit(solution)/shard_map/ppermute | solution.py:20
  11.1 95.2 %collective-permute-start.3 = (f32[4,64,1]{1,2,0:T(1,128)S(1)}, f32[4,64,1]{1,2,0:T(1,128)S(1)}, u32[]{:S(2)}, u32[]{:S(2)}) collective-permute-start(f32[4,64,1]{1,2,0:T(1,128)S(1)} %get-tuple-element.48), channel_id=1, source_target_pairs={{1,0},{2,1},{3,2},{0,3},{5,4},{6,5},{7,6},{4,7},{9,8},{10,9},{11,1... | collective-permute-start | bytes 3080 | tf_op jit(solution)/shard_map/ppermute | solution.py:21
  14.6 96.0 %collective-permute-start.6 = (f32[4,64,1]{1,2,0:T(1,128)}, f32[4,64,1]{1,2,0:T(1,128)S(1)}, u32[]{:S(2)}, u32[]{:S(2)}) collective-permute-start(f32[4,64,1]{1,2,0:T(1,128)} %get-tuple-element.54), channel_id=1, source_target_pairs={{0,1},{1,2},{2,3},{3,0},{4,5},{5,6},{6,7},{7,4},{8,9},{9,10},{10,1... | collective-permute-start | bytes 3080 | tf_op jit(solution)/shard_map/ppermute | solution.py:20
  103.7 12.4 %collective-permute-start.4 = (f32[1,64,256]{1,2,0:T(8,128)}, f32[1,64,256]{1,2,0:T(8,128)S(1)}, u32[]{:S(2)}, u32[]{:S(2)}) collective-permute-start(f32[1,64,256]{1,2,0:T(8,128)} %get-tuple-element.52), channel_id=1, source_target_pairs={{0,4},{4,8},{8,12},{12,16},{16,20},{20,24},{24,28},{1,5},{5,9},{9,... | collective-permute-start | bytes 196616 | tf_op jit(solution)/shard_map/ppermute | solution.py:20
  106.3 9.9 %collective-permute-start.5 = (f32[1,64,256]{1,2,0:T(8,128)}, f32[1,64,256]{1,2,0:T(8,128)S(1)}, u32[]{:S(2)}, u32[]{:S(2)}) collective-permute-start(f32[1,64,256]{1,2,0:T(8,128)} %get-tuple-element.53), channel_id=1, source_target_pairs={{4,0},{8,4},{12,8},{16,12},{20,16},{24,20},{28,24},{5,1},{9,5},{13... | collective-permute-start | bytes 196616 | tf_op jit(solution)/shard_map/ppermute | solution.py:21
  111.1 2.5 collective-permute-start.7
  113.7 59.5 %collective-permute-start.16 = (f32[1,32,128]{2,1,0:T(8,128)}, f32[1,32,128]{2,1,0:T(8,128)S(1)}, u32[]{:S(2)}, u32[]{:S(2)}) collective-permute-start(f32[1,32,128]{2,1,0:T(8,128)} %get-tuple-element.95), channel_id=1, source_target_pairs={{0,4},{4,8},{8,12},{12,16},{16,20},{20,24},{24,28},{1,5},{5,9},{9,... | collective-permute-start | bytes 49160 | tf_op jit(solution)/shard_map/ppermute | solution.py:20
  118.2 9.9 %collective-permute-start.8 = (f32[1,64,256]{1,2,0:T(8,128)S(1)}, f32[1,64,256]{1,2,0:T(8,128)S(1)}, u32[]{:S(2)}, u32[]{:S(2)}) collective-permute-start(f32[1,64,256]{1,2,0:T(8,128)S(1)} %get-tuple-element.42), channel_id=1, source_target_pairs={{0,4},{4,8},{8,12},{12,16},{16,20},{20,24},{24,28},{1,5},{5,9},{9,... | collective-permute-start | bytes 196616 | tf_op jit(solution)/shard_map/ppermute | solution.py:20
  122.8 7.9 %collective-permute-start.9 = (f32[1,64,256]{1,2,0:T(8,128)S(1)}, f32[1,64,256]{1,2,0:T(8,128)S(1)}, u32[]{:S(2)}, u32[]{:S(2)}) collective-permute-start(f32[1,64,256]{1,2,0:T(8,128)S(1)} %get-tuple-element.43), channel_id=1, source_target_pairs={{4,0},{8,4},{12,8},{16,12},{20,16},{24,20},{28,24},{5,1},{9,5},{13... | collective-permute-start | bytes 196616 | tf_op jit(solution)/shard_map/ppermute | solution.py:21
  125.0 3.1 %collective-permute-start.10 = (f32[4,64,1]{1,2,0:T(1,128)S(1)}, f32[4,64,1]{1,2,0:T(1,128)S(1)}, u32[]{:S(2)}, u32[]{:S(2)}) collective-permute-start(f32[4,64,1]{1,2,0:T(1,128)S(1)} %get-tuple-element.44), channel_id=1, source_target_pairs={{0,1},{1,2},{2,3},{3,0},{4,5},{5,6},{6,7},{7,4},{8,9},{9,10},{10,1... | collective-permute-start | bytes 3080 | tf_op jit(solution)/shard_map/ppermute | solution.py:20
  131.7 12.1 %collective-permute-start.12 = (f32[1,64,256]{1,2,0:T(8,128)S(1)}, f32[1,64,256]{1,2,0:T(8,128)S(1)}, u32[]{:S(2)}, u32[]{:S(2)}) collective-permute-start(f32[1,64,256]{1,2,0:T(8,128)S(1)} %get-tuple-element.36), channel_id=1, source_target_pairs={{0,4},{4,8},{8,12},{12,16},{16,20},{20,24},{24,28},{1,5},{5,9},{9,... | collective-permute-start | bytes 196616 | tf_op jit(solution)/shard_map/ppermute | solution.py:20
  134.9 10.6 %collective-permute-start.13 = (f32[1,64,256]{1,2,0:T(8,128)S(1)}, f32[1,64,256]{1,2,0:T(8,128)S(1)}, u32[]{:S(2)}, u32[]{:S(2)}) collective-permute-start(f32[1,64,256]{1,2,0:T(8,128)S(1)} %get-tuple-element.37), channel_id=1, source_target_pairs={{4,0},{8,4},{12,8},{16,12},{20,16},{24,20},{28,24},{5,1},{9,5},{13... | collective-permute-start | bytes 196616 | tf_op jit(solution)/shard_map/ppermute | solution.py:21
  138.4 3.1 %collective-permute-start.14 = (f32[4,64,1]{1,2,0:T(1,128)S(1)}, f32[4,64,1]{1,2,0:T(1,128)S(1)}, u32[]{:S(2)}, u32[]{:S(2)}) collective-permute-start(f32[4,64,1]{1,2,0:T(1,128)S(1)} %get-tuple-element.38), channel_id=1, source_target_pairs={{0,1},{1,2},{2,3},{3,0},{4,5},{5,6},{6,7},{7,4},{8,9},{9,10},{10,1... | collective-permute-start | bytes 3080 | tf_op jit(solution)/shard_map/ppermute | solution.py:20
  138.5 5.2 %collective-permute-start.15 = (f32[4,64,1]{1,2,0:T(1,128)S(1)}, f32[4,64,1]{1,2,0:T(1,128)S(1)}, u32[]{:S(2)}, u32[]{:S(2)}) collective-permute-start(f32[4,64,1]{1,2,0:T(1,128)S(1)} %get-tuple-element.39), channel_id=1, source_target_pairs={{1,0},{2,1},{3,2},{0,3},{5,4},{6,5},{7,6},{4,7},{9,8},{10,9},{11,1... | collective-permute-start | bytes 3080 | tf_op jit(solution)/shard_map/ppermute | solution.py:21
  141.5 31.6 %collective-permute-start.17 = (f32[1,32,128]{2,1,0:T(8,128)}, f32[1,32,128]{2,1,0:T(8,128)S(1)}, u32[]{:S(2)}, u32[]{:S(2)}) collective-permute-start(f32[1,32,128]{2,1,0:T(8,128)} %get-tuple-element.94), channel_id=1, source_target_pairs={{4,0},{8,4},{12,8},{16,12},{20,16},{24,20},{28,24},{5,1},{9,5},{13... | collective-permute-start | bytes 49160 | tf_op jit(solution)/shard_map/ppermute | solution.py:21
  143.7 29.4 %collective-permute-start.18 = (f32[2,32,1]{2,1,0:T(8,128)}, f32[2,32,1]{2,1,0:T(8,128)}, u32[]{:S(2)}, u32[]{:S(2)}) collective-permute-start(f32[2,32,1]{2,1,0:T(8,128)} %get-tuple-element.93), channel_id=1, source_target_pairs={{0,1},{1,2},{2,3},{3,0},{4,5},{5,6},{6,7},{7,4},{8,9},{9,10},{10,1... | collective-permute-start | bytes 776 | tf_op jit(solution)/shard_map/ppermute | solution.py:20
  143.8 29.3 %collective-permute-start.19 = (f32[2,32,1]{2,1,0:T(8,128)}, f32[2,32,1]{2,1,0:T(8,128)}, u32[]{:S(2)}, u32[]{:S(2)}) collective-permute-start(f32[2,32,1]{2,1,0:T(8,128)} %get-tuple-element.92), channel_id=1, source_target_pairs={{1,0},{2,1},{3,2},{0,3},{5,4},{6,5},{7,6},{4,7},{9,8},{10,9},{11,1... | collective-permute-start | bytes 776 | tf_op jit(solution)/shard_map/ppermute | solution.py:21
  174.1 8.5 %collective-permute-start.22 = (f32[2,32,1]{2,1,0:T(8,128)S(1)}, f32[2,32,1]{2,1,0:T(8,128)S(1)}, u32[]{:S(2)}, u32[]{:S(2)}) collective-permute-start(f32[2,32,1]{2,1,0:T(8,128)S(1)} %get-tuple-element.90), channel_id=1, source_target_pairs={{0,1},{1,2},{2,3},{3,0},{4,5},{5,6},{6,7},{7,4},{8,9},{9,10},{10,1... | collective-permute-start | bytes 776 | tf_op jit(solution)/shard_map/ppermute | solution.py:20
  174.1 8.5 %collective-permute-start.23 = (f32[2,32,1]{2,1,0:T(8,128)S(1)}, f32[2,32,1]{2,1,0:T(8,128)S(1)}, u32[]{:S(2)}, u32[]{:S(2)}) collective-permute-start(f32[2,32,1]{2,1,0:T(8,128)S(1)} %get-tuple-element.91), channel_id=1, source_target_pairs={{1,0},{2,1},{3,2},{0,3},{5,4},{6,5},{7,6},{4,7},{9,8},{10,9},{11,1... | collective-permute-start | bytes 776 | tf_op jit(solution)/shard_map/ppermute | solution.py:21
  175.9 6.8 %collective-permute-start.20 = (f32[1,32,128]{2,1,0:T(8,128)S(1)}, f32[1,32,128]{2,1,0:T(8,128)S(1)}, u32[]{:S(2)}, u32[]{:S(2)}) collective-permute-start(f32[1,32,128]{2,1,0:T(8,128)S(1)} %get-tuple-element.88), channel_id=1, source_target_pairs={{0,4},{4,8},{8,12},{12,16},{16,20},{20,24},{24,28},{1,5},{5,9},{9,... | collective-permute-start | bytes 49160 | tf_op jit(solution)/shard_map/ppermute | solution.py:20
  179.5 5.6 %collective-permute-start.21 = (f32[1,32,128]{2,1,0:T(8,128)S(1)}, f32[1,32,128]{2,1,0:T(8,128)S(1)}, u32[]{:S(2)}, u32[]{:S(2)}) collective-permute-start(f32[1,32,128]{2,1,0:T(8,128)S(1)} %get-tuple-element.89), channel_id=1, source_target_pairs={{4,0},{8,4},{12,8},{16,12},{20,16},{24,20},{28,24},{5,1},{9,5},{13... | collective-permute-start | bytes 49160 | tf_op jit(solution)/shard_map/ppermute | solution.py:21
  185.3 8.5 %collective-permute-start.26 = (f32[2,32,1]{2,1,0:T(8,128)S(1)}, f32[2,32,1]{2,1,0:T(8,128)S(1)}, u32[]{:S(2)}, u32[]{:S(2)}) collective-permute-start(f32[2,32,1]{2,1,0:T(8,128)S(1)} %get-tuple-element.78), channel_id=1, source_target_pairs={{0,1},{1,2},{2,3},{3,0},{4,5},{5,6},{6,7},{7,4},{8,9},{9,10},{10,1... | collective-permute-start | bytes 776 | tf_op jit(solution)/shard_map/ppermute | solution.py:20
  185.3 8.5 %collective-permute-start.27 = (f32[2,32,1]{2,1,0:T(8,128)S(1)}, f32[2,32,1]{2,1,0:T(8,128)S(1)}, u32[]{:S(2)}, u32[]{:S(2)}) collective-permute-start(f32[2,32,1]{2,1,0:T(8,128)S(1)} %get-tuple-element.79), channel_id=1, source_target_pairs={{1,0},{2,1},{3,2},{0,3},{5,4},{6,5},{7,6},{4,7},{9,8},{10,9},{11,1... | collective-permute-start | bytes 776 | tf_op jit(solution)/shard_map/ppermute | solution.py:21
  187.1 6.8 %collective-permute-start.24 = (f32[1,32,128]{2,1,0:T(8,128)S(1)}, f32[1,32,128]{2,1,0:T(8,128)S(1)}, u32[]{:S(2)}, u32[]{:S(2)}) collective-permute-start(f32[1,32,128]{2,1,0:T(8,128)S(1)} %get-tuple-element.76), channel_id=1, source_target_pairs={{0,4},{4,8},{8,12},{12,16},{16,20},{20,24},{24,28},{1,5},{5,9},{9,... | collective-permute-start | bytes 49160 | tf_op jit(solution)/shard_map/ppermute | solution.py:20
  191.2 5.6 %collective-permute-start.25 = (f32[1,32,128]{2,1,0:T(8,128)S(1)}, f32[1,32,128]{2,1,0:T(8,128)S(1)}, u32[]{:S(2)}, u32[]{:S(2)}) collective-permute-start(f32[1,32,128]{2,1,0:T(8,128)S(1)} %get-tuple-element.77), channel_id=1, source_target_pairs={{4,0},{8,4},{12,8},{16,12},{20,16},{24,20},{28,24},{5,1},{9,5},{13... | collective-permute-start | bytes 49160 | tf_op jit(solution)/shard_map/ppermute | solution.py:21
  200.4 4.0 %collective-permute-start.28 = (f32[4,1,16,64]{3,2,1,0:T(8,128)S(1)}, f32[4,1,16,64]{3,2,1,0:T(8,128)S(1)}, u32[]{:S(2)}, u32[]{:S(2)}) collective-permute-start(f32[4,1,16,64]{3,2,1,0:T(8,128)S(1)} %pad_maximum_fusion.48), channel_id=1, source_target_pairs={{0,4},{4,0},{8,12},{12,8},{16,20},{20,16},{24,28},{28,24},{1,5},{5... | collective-permute-start | bytes 49160 | tf_op jit(solution)/shard_map/ppermute | solution.py:39
  204.5 7.6 %collective-permute-start.31 = (f32[2,16,1]{2,1,0:T(8,128)S(1)}, f32[2,16,1]{2,1,0:T(8,128)S(1)}, u32[]{:S(2)}, u32[]{:S(2)}) collective-permute-start(f32[2,16,1]{2,1,0:T(8,128)S(1)} %get-tuple-element.117), channel_id=1, source_target_pairs={{0,1},{1,2},{2,3},{3,0},{4,5},{5,6},{6,7},{7,4},{8,9},{9,10},{10,1... | collective-permute-start | bytes 392 | tf_op jit(solution)/shard_map/ppermute | solution.py:20
  204.5 7.6 %collective-permute-start.32 = (f32[2,16,1]{2,1,0:T(8,128)S(1)}, f32[2,16,1]{2,1,0:T(8,128)S(1)}, u32[]{:S(2)}, u32[]{:S(2)}) collective-permute-start(f32[2,16,1]{2,1,0:T(8,128)S(1)} %get-tuple-element.116), channel_id=1, source_target_pairs={{1,0},{2,1},{3,2},{0,3},{5,4},{6,5},{7,6},{4,7},{9,8},{10,9},{11,1... | collective-permute-start | bytes 392 | tf_op jit(solution)/shard_map/ppermute | solution.py:21
  206.2 5.9 %collective-permute-start.29 = (f32[1,16,64]{2,1,0:T(8,128)S(1)}, f32[1,16,64]{2,1,0:T(8,128)S(1)}, u32[]{:S(2)}, u32[]{:S(2)}) collective-permute-start(f32[1,16,64]{2,1,0:T(8,128)S(1)} %slice_bitcast_fusion.1), channel_id=1, source_target_pairs={{0,8},{4,12},{8,16},{12,20},{16,24},{20,28},{1,9},{5,13},{9,17},{1... | collective-permute-start | bytes 12296 | tf_op jit(solution)/shard_map/ppermute | solution.py:29
  209.3 5.5 %collective-permute-start.30 = (f32[1,16,64]{2,1,0:T(8,128)S(1)}, f32[1,16,64]{2,1,0:T(8,128)S(1)}, u32[]{:S(2)}, u32[]{:S(2)}) collective-permute-start(f32[1,16,64]{2,1,0:T(8,128)S(1)} %slice_bitcast_fusion), channel_id=1, source_target_pairs={{8,0},{12,4},{16,8},{20,12},{24,16},{28,20},{9,1},{13,5},{17,9},{2... | collective-permute-start | bytes 12296 | tf_op jit(solution)/shard_map/ppermute | solution.py:29
  215.0 7.6 %collective-permute-start.35 = (f32[2,16,1]{2,1,0:T(8,128)S(1)}, f32[2,16,1]{2,1,0:T(8,128)S(1)}, u32[]{:S(2)}, u32[]{:S(2)}) collective-permute-start(f32[2,16,1]{2,1,0:T(8,128)S(1)} %get-tuple-element.114), channel_id=1, source_target_pairs={{0,1},{1,2},{2,3},{3,0},{4,5},{5,6},{6,7},{7,4},{8,9},{9,10},{10,1... | collective-permute-start | bytes 392 | tf_op jit(solution)/shard_map/ppermute | solution.py:20
  215.0 7.6 %collective-permute-start.36 = (f32[2,16,1]{2,1,0:T(8,128)S(1)}, f32[2,16,1]{2,1,0:T(8,128)S(1)}, u32[]{:S(2)}, u32[]{:S(2)}) collective-permute-start(f32[2,16,1]{2,1,0:T(8,128)S(1)} %get-tuple-element.115), channel_id=1, source_target_pairs={{1,0},{2,1},{3,2},{0,3},{5,4},{6,5},{7,6},{4,7},{9,8},{10,9},{11,1... | collective-permute-start | bytes 392 | tf_op jit(solution)/shard_map/ppermute | solution.py:21
  216.8 5.9 %collective-permute-start.33 = (f32[1,16,64]{2,1,0:T(8,128)S(1)}, f32[1,16,64]{2,1,0:T(8,128)S(1)}, u32[]{:S(2)}, u32[]{:S(2)}) collective-permute-start(f32[1,16,64]{2,1,0:T(8,128)S(1)} %get-tuple-element.112), channel_id=1, source_target_pairs={{0,8},{4,12},{8,16},{12,20},{16,24},{20,28},{1,9},{5,13},{9,17},{1... | collective-permute-start | bytes 12296 | tf_op jit(solution)/shard_map/ppermute | solution.py:29
  218.7 5.5 %collective-permute-start.34 = (f32[1,16,64]{2,1,0:T(8,128)S(1)}, f32[1,16,64]{2,1,0:T(8,128)S(1)}, u32[]{:S(2)}, u32[]{:S(2)}) collective-permute-start(f32[1,16,64]{2,1,0:T(8,128)S(1)} %get-tuple-element.113), channel_id=1, source_target_pairs={{8,0},{12,4},{16,8},{20,12},{24,16},{28,20},{9,1},{13,5},{17,9},{2... | collective-permute-start | bytes 12296 | tf_op jit(solution)/shard_map/ppermute | solution.py:29
  224.4 7.6 %collective-permute-start.39 = (f32[2,16,1]{2,1,0:T(8,128)S(1)}, f32[2,16,1]{2,1,0:T(8,128)S(1)}, u32[]{:S(2)}, u32[]{:S(2)}) collective-permute-start(f32[2,16,1]{2,1,0:T(8,128)S(1)} %get-tuple-element.108), channel_id=1, source_target_pairs={{0,1},{1,2},{2,3},{3,0},{4,5},{5,6},{6,7},{7,4},{8,9},{9,10},{10,1... | collective-permute-start | bytes 392 | tf_op jit(solution)/shard_map/ppermute | solution.py:20
  224.4 7.6 %collective-permute-start.40 = (f32[2,16,1]{2,1,0:T(8,128)S(1)}, f32[2,16,1]{2,1,0:T(8,128)S(1)}, u32[]{:S(2)}, u32[]{:S(2)}) collective-permute-start(f32[2,16,1]{2,1,0:T(8,128)S(1)} %get-tuple-element.109), channel_id=1, source_target_pairs={{1,0},{2,1},{3,2},{0,3},{5,4},{6,5},{7,6},{4,7},{9,8},{10,9},{11,1... | collective-permute-start | bytes 392 | tf_op jit(solution)/shard_map/ppermute | solution.py:21
  226.1 5.9 %collective-permute-start.37 = (f32[1,16,64]{2,1,0:T(8,128)S(1)}, f32[1,16,64]{2,1,0:T(8,128)S(1)}, u32[]{:S(2)}, u32[]{:S(2)}) collective-permute-start(f32[1,16,64]{2,1,0:T(8,128)S(1)} %get-tuple-element.106), channel_id=1, source_target_pairs={{0,8},{4,12},{8,16},{12,20},{16,24},{20,28},{1,9},{5,13},{9,17},{1... | collective-permute-start | bytes 12296 | tf_op jit(solution)/shard_map/ppermute | solution.py:29
  228.1 5.5 %collective-permute-start.38 = (f32[1,16,64]{2,1,0:T(8,128)S(1)}, f32[1,16,64]{2,1,0:T(8,128)S(1)}, u32[]{:S(2)}, u32[]{:S(2)}) collective-permute-start(f32[1,16,64]{2,1,0:T(8,128)S(1)} %get-tuple-element.107), channel_id=1, source_target_pairs={{8,0},{12,4},{16,8},{20,12},{24,16},{28,20},{9,1},{13,5},{17,9},{2... | collective-permute-start | bytes 12296 | tf_op jit(solution)/shard_map/ppermute | solution.py:29
  233.8 7.6 %collective-permute-start.43 = (f32[2,16,1]{2,1,0:T(8,128)S(1)}, f32[2,16,1]{2,1,0:T(8,128)S(1)}, u32[]{:S(2)}, u32[]{:S(2)}) collective-permute-start(f32[2,16,1]{2,1,0:T(8,128)S(1)} %get-tuple-element.102), channel_id=1, source_target_pairs={{0,1},{1,2},{2,3},{3,0},{4,5},{5,6},{6,7},{7,4},{8,9},{9,10},{10,1... | collective-permute-start | bytes 392 | tf_op jit(solution)/shard_map/ppermute | solution.py:20
  233.8 7.6 %collective-permute-start.44 = (f32[2,16,1]{2,1,0:T(8,128)S(1)}, f32[2,16,1]{2,1,0:T(8,128)S(1)}, u32[]{:S(2)}, u32[]{:S(2)}) collective-permute-start(f32[2,16,1]{2,1,0:T(8,128)S(1)} %get-tuple-element.103), channel_id=1, source_target_pairs={{1,0},{2,1},{3,2},{0,3},{5,4},{6,5},{7,6},{4,7},{9,8},{10,9},{11,1... | collective-permute-start | bytes 392 | tf_op jit(solution)/shard_map/ppermute | solution.py:21
  235.5 5.9 %collective-permute-start.41 = (f32[1,16,64]{2,1,0:T(8,128)S(1)}, f32[1,16,64]{2,1,0:T(8,128)S(1)}, u32[]{:S(2)}, u32[]{:S(2)}) collective-permute-start(f32[1,16,64]{2,1,0:T(8,128)S(1)} %get-tuple-element.100), channel_id=1, source_target_pairs={{0,8},{4,12},{8,16},{12,20},{16,24},{20,28},{1,9},{5,13},{9,17},{1... | collective-permute-start | bytes 12296 | tf_op jit(solution)/shard_map/ppermute | solution.py:29
  237.4 5.5 %collective-permute-start.42 = (f32[1,16,64]{2,1,0:T(8,128)S(1)}, f32[1,16,64]{2,1,0:T(8,128)S(1)}, u32[]{:S(2)}, u32[]{:S(2)}) collective-permute-start(f32[1,16,64]{2,1,0:T(8,128)S(1)} %get-tuple-element.101), channel_id=1, source_target_pairs={{8,0},{12,4},{16,8},{20,12},{24,16},{28,20},{9,1},{13,5},{17,9},{2... | collective-permute-start | bytes 12296 | tf_op jit(solution)/shard_map/ppermute | solution.py:29
  243.4 8.5 %collective-permute-start.47 = (f32[2,32,1]{2,1,0:T(8,128)S(1)}, f32[2,32,1]{2,1,0:T(8,128)S(1)}, u32[]{:S(2)}, u32[]{:S(2)}) collective-permute-start(f32[2,32,1]{2,1,0:T(8,128)S(1)} %get-tuple-element.72), channel_id=1, source_target_pairs={{0,1},{1,2},{2,3},{3,0},{4,5},{5,6},{6,7},{7,4},{8,9},{9,10},{10,1... | collective-permute-start | bytes 776 | tf_op jit(solution)/shard_map/ppermute | solution.py:20
  243.4 8.5 %collective-permute-start.48 = (f32[2,32,1]{2,1,0:T(8,128)S(1)}, f32[2,32,1]{2,1,0:T(8,128)S(1)}, u32[]{:S(2)}, u32[]{:S(2)}) collective-permute-start(f32[2,32,1]{2,1,0:T(8,128)S(1)} %get-tuple-element.73), channel_id=1, source_target_pairs={{1,0},{2,1},{3,2},{0,3},{5,4},{6,5},{7,6},{4,7},{9,8},{10,9},{11,1... | collective-permute-start | bytes 776 | tf_op jit(solution)/shard_map/ppermute | solution.py:21
  245.2 6.8 %collective-permute-start.45 = (f32[1,32,128]{2,1,0:T(8,128)S(1)}, f32[1,32,128]{2,1,0:T(8,128)S(1)}, u32[]{:S(2)}, u32[]{:S(2)}) collective-permute-start(f32[1,32,128]{2,1,0:T(8,128)S(1)} %get-tuple-element.70), channel_id=1, source_target_pairs={{0,4},{4,8},{8,12},{12,16},{16,20},{20,24},{24,28},{1,5},{5,9},{9,... | collective-permute-start | bytes 49160 | tf_op jit(solution)/shard_map/ppermute | solution.py:20
  248.3 5.6 %collective-permute-start.46 = (f32[1,32,128]{2,1,0:T(8,128)S(1)}, f32[1,32,128]{2,1,0:T(8,128)S(1)}, u32[]{:S(2)}, u32[]{:S(2)}) collective-permute-start(f32[1,32,128]{2,1,0:T(8,128)S(1)} %get-tuple-element.71), channel_id=1, source_target_pairs={{4,0},{8,4},{12,8},{16,12},{20,16},{24,20},{28,24},{5,1},{9,5},{13... | collective-permute-start | bytes 49160 | tf_op jit(solution)/shard_map/ppermute | solution.py:21
  254.1 8.5 %collective-permute-start.51 = (f32[2,32,1]{2,1,0:T(8,128)S(1)}, f32[2,32,1]{2,1,0:T(8,128)S(1)}, u32[]{:S(2)}, u32[]{:S(2)}) collective-permute-start(f32[2,32,1]{2,1,0:T(8,128)S(1)} %get-tuple-element.66), channel_id=1, source_target_pairs={{0,1},{1,2},{2,3},{3,0},{4,5},{5,6},{6,7},{7,4},{8,9},{9,10},{10,1... | collective-permute-start | bytes 776 | tf_op jit(solution)/shard_map/ppermute | solution.py:20
  254.2 8.5 %collective-permute-start.52 = (f32[2,32,1]{2,1,0:T(8,128)S(1)}, f32[2,32,1]{2,1,0:T(8,128)S(1)}, u32[]{:S(2)}, u32[]{:S(2)}) collective-permute-start(f32[2,32,1]{2,1,0:T(8,128)S(1)} %get-tuple-element.67), channel_id=1, source_target_pairs={{1,0},{2,1},{3,2},{0,3},{5,4},{6,5},{7,6},{4,7},{9,8},{10,9},{11,1... | collective-permute-start | bytes 776 | tf_op jit(solution)/shard_map/ppermute | solution.py:21
  255.9 6.8 %collective-permute-start.49 = (f32[1,32,128]{2,1,0:T(8,128)S(1)}, f32[1,32,128]{2,1,0:T(8,128)S(1)}, u32[]{:S(2)}, u32[]{:S(2)}) collective-permute-start(f32[1,32,128]{2,1,0:T(8,128)S(1)} %get-tuple-element.64), channel_id=1, source_target_pairs={{0,4},{4,8},{8,12},{12,16},{16,20},{20,24},{24,28},{1,5},{5,9},{9,... | collective-permute-start | bytes 49160 | tf_op jit(solution)/shard_map/ppermute | solution.py:20
  258.9 5.6 %collective-permute-start.50 = (f32[1,32,128]{2,1,0:T(8,128)S(1)}, f32[1,32,128]{2,1,0:T(8,128)S(1)}, u32[]{:S(2)}, u32[]{:S(2)}) collective-permute-start(f32[1,32,128]{2,1,0:T(8,128)S(1)} %get-tuple-element.65), channel_id=1, source_target_pairs={{4,0},{8,4},{12,8},{16,12},{20,16},{24,20},{28,24},{5,1},{9,5},{13... | collective-permute-start | bytes 49160 | tf_op jit(solution)/shard_map/ppermute | solution.py:21
  265.2 9.9 %collective-permute-start.53 = (f32[1,64,256]{1,2,0:T(8,128)S(1)}, f32[1,64,256]{1,2,0:T(8,128)S(1)}, u32[]{:S(2)}, u32[]{:S(2)}) collective-permute-start(f32[1,64,256]{1,2,0:T(8,128)S(1)} %get-tuple-element.30), channel_id=1, source_target_pairs={{0,4},{4,8},{8,12},{12,16},{16,20},{20,24},{24,28},{1,5},{5,9},{9,... | collective-permute-start | bytes 196616 | tf_op jit(solution)/shard_map/ppermute | solution.py:20
  268.3 6.9 %collective-permute-start.54 = (f32[1,64,256]{1,2,0:T(8,128)S(1)}, f32[1,64,256]{1,2,0:T(8,128)S(1)}, u32[]{:S(2)}, u32[]{:S(2)}) collective-permute-start(f32[1,64,256]{1,2,0:T(8,128)S(1)} %get-tuple-element.31), channel_id=1, source_target_pairs={{4,0},{8,4},{12,8},{16,12},{20,16},{24,20},{28,24},{5,1},{9,5},{13... | collective-permute-start | bytes 196616 | tf_op jit(solution)/shard_map/ppermute | solution.py:21
  271.9 3.1 %collective-permute-start.55 = (f32[4,64,1]{1,2,0:T(1,128)S(1)}, f32[4,64,1]{1,2,0:T(1,128)S(1)}, u32[]{:S(2)}, u32[]{:S(2)}) collective-permute-start(f32[4,64,1]{1,2,0:T(1,128)S(1)} %get-tuple-element.32), channel_id=1, source_target_pairs={{0,1},{1,2},{2,3},{3,0},{4,5},{5,6},{6,7},{7,4},{8,9},{9,10},{10,1... | collective-permute-start | bytes 3080 | tf_op jit(solution)/shard_map/ppermute | solution.py:20
  272.0 3.0 %collective-permute-start.56 = (f32[4,64,1]{1,2,0:T(1,128)S(1)}, f32[4,64,1]{1,2,0:T(1,128)S(1)}, u32[]{:S(2)}, u32[]{:S(2)}) collective-permute-start(f32[4,64,1]{1,2,0:T(1,128)S(1)} %get-tuple-element.33), channel_id=1, source_target_pairs={{1,0},{2,1},{3,2},{0,3},{5,4},{6,5},{7,6},{4,7},{9,8},{10,9},{11,1... | collective-permute-start | bytes 3080 | tf_op jit(solution)/shard_map/ppermute | solution.py:21
  276.2 9.9 %collective-permute-start.57 = (f32[1,64,256]{1,2,0:T(8,128)S(1)}, f32[1,64,256]{1,2,0:T(8,128)S(1)}, u32[]{:S(2)}, u32[]{:S(2)}) collective-permute-start(f32[1,64,256]{1,2,0:T(8,128)S(1)} %get-tuple-element.24), channel_id=1, source_target_pairs={{0,4},{4,8},{8,12},{12,16},{16,20},{20,24},{24,28},{1,5},{5,9},{9,... | collective-permute-start | bytes 196616 | tf_op jit(solution)/shard_map/ppermute | solution.py:20
  279.0 9.1 %collective-permute-start.58 = (f32[1,64,256]{1,2,0:T(8,128)S(1)}, f32[1,64,256]{1,2,0:T(8,128)S(1)}, u32[]{:S(2)}, u32[]{:S(2)}) collective-permute-start(f32[1,64,256]{1,2,0:T(8,128)S(1)} %get-tuple-element.25), channel_id=1, source_target_pairs={{4,0},{8,4},{12,8},{16,12},{20,16},{24,20},{28,24},{5,1},{9,5},{13... | collective-permute-start | bytes 196616 | tf_op jit(solution)/shard_map/ppermute | solution.py:21
  282.9 3.1 %collective-permute-start.59 = (f32[4,64,1]{1,2,0:T(1,128)S(1)}, f32[4,64,1]{1,2,0:T(1,128)S(1)}, u32[]{:S(2)}, u32[]{:S(2)}) collective-permute-start(f32[4,64,1]{1,2,0:T(1,128)S(1)} %get-tuple-element.26), channel_id=1, source_target_pairs={{0,1},{1,2},{2,3},{3,0},{4,5},{5,6},{6,7},{7,4},{8,9},{9,10},{10,1... | collective-permute-start | bytes 3080 | tf_op jit(solution)/shard_map/ppermute | solution.py:20
  283.8 2.2 collective-permute-start.60
  289.1 10.6 %collective-permute-start.61 = (f32[1,64,256]{1,2,0:T(8,128)S(1)}, f32[1,64,256]{1,2,0:T(8,128)S(1)}, u32[]{:S(2)}, u32[]{:S(2)}) collective-permute-start(f32[1,64,256]{1,2,0:T(8,128)S(1)} %get-tuple-element.18), channel_id=1, source_target_pairs={{0,4},{4,8},{8,12},{12,16},{16,20},{20,24},{24,28},{1,5},{5,9},{9,... | collective-permute-start | bytes 196616 | tf_op jit(solution)/shard_map/ppermute | solution.py:20
  291.2 9.0 %collective-permute-start.62 = (f32[1,64,256]{1,2,0:T(8,128)S(1)}, f32[1,64,256]{1,2,0:T(8,128)S(1)}, u32[]{:S(2)}, u32[]{:S(2)}) collective-permute-start(f32[1,64,256]{1,2,0:T(8,128)S(1)} %get-tuple-element.19), channel_id=1, source_target_pairs={{4,0},{8,4},{12,8},{16,12},{20,16},{24,20},{28,24},{5,1},{9,5},{13... | collective-permute-start | bytes 196616 | tf_op jit(solution)/shard_map/ppermute | solution.py:21
  295.9 3.8 %collective-permute-start.63 = (f32[4,64,1]{1,2,0:T(1,128)S(1)}, f32[4,64,1]{1,2,0:T(1,128)S(1)}, u32[]{:S(2)}, u32[]{:S(2)}) collective-permute-start(f32[4,64,1]{1,2,0:T(1,128)S(1)} %get-tuple-element.20), channel_id=1, source_target_pairs={{0,1},{1,2},{2,3},{3,0},{4,5},{5,6},{6,7},{7,4},{8,9},{9,10},{10,1... | collective-permute-start | bytes 3080 | tf_op jit(solution)/shard_map/ppermute | solution.py:20
  295.9 3.7 %collective-permute-start.64 = (f32[4,64,1]{1,2,0:T(1,128)S(1)}, f32[4,64,1]{1,2,0:T(1,128)S(1)}, u32[]{:S(2)}, u32[]{:S(2)}) collective-permute-start(f32[4,64,1]{1,2,0:T(1,128)S(1)} %get-tuple-element.21), channel_id=1, source_target_pairs={{1,0},{2,1},{3,2},{0,3},{5,4},{6,5},{7,6},{4,7},{9,8},{10,9},{11,1... | collective-permute-start | bytes 3080 | tf_op jit(solution)/shard_map/ppermute | solution.py:21
  (7 other events, 180.1 us)
where the time goes:
time: 307 us; the launch traced here: 304 us
  starting transfers between devices  132 us (43%)
  local copies, waits for them, and re-layouts  96.4 us (31%)
  other arithmetic  44 us (14%)
  waiting for transfers between devices  30.2 us (10%)
    reshape x4, local copies, waits for them, and re-layouts, coarsen(): values.reshape(depth // 2, 2, width // 2, 2, length // 2, 2)  73.9 us
    ppermute x28, starting transfers between devices, with_halo(): after = lax.ppermute(leading, axis, down)  66 us
    ppermute x28, starting transfers between devices, with_halo(): before = lax.ppermute(last, axis, up)  40.4 us
    reduce_sum x12, other arithmetic, coarsen(): values.reshape(depth // 2, 2, width // 2, 2, length // 2, 2)  31.9 us
    ppermute x8, starting transfers between devices, shifted(): return lax.ppermute(block, axis, route)  23.3 us
    ppermute x28, waiting for transfers between devices, with_halo(): after = lax.ppermute(leading, axis, down)  16.2 us
    unnamed x19, local copies, waits for them, and re-layouts  7.73 us
    ppermute x8, waiting for transfers between devices, shifted(): return lax.ppermute(block, axis, route)  7.45 us
  transfers between devices with their start and end apart: 65, of which 18 were waited for; matrix products, arithmetic and copies ran while one was open for 41% of the time, Pallas kernels for 0%

commit v1 on v0

--- a/solution.py
+++ b/solution.py
@@ -39,13 +39,29 @@
     return lax.ppermute(block, axis, route)
 
 
+HIGH = lax.Precision.HIGHEST
+
+
+def pairing(fine):
+    rows = lax.broadcasted_iota(jnp.int32, (fine, fine // 2), 0) // 2
+    cols = lax.broadcasted_iota(jnp.int32, (fine, fine // 2), 1)
+    return (rows == cols).astype(jnp.float32)
+
+
 def coarsen(values):
     depth, width, length = values.shape
-    return values.reshape(depth // 2, 2, width // 2, 2, length // 2, 2).mean(axis=(1, 3, 5))
+    summed = values.reshape(depth // 2, 2, width, length).sum(axis=1)
+    summed = jnp.matmul(summed, pairing(length), precision=HIGH)
+    summed = jnp.matmul(pairing(width).T[None], summed, precision=HIGH)
+    return summed * 0.125
 
 
 def refine(values):
-    return jnp.repeat(jnp.repeat(jnp.repeat(values, 2, 0), 2, 1), 2, 2)
+    depth, width, length = values.shape
+    grown = jnp.matmul(values, pairing(2 * length).T, precision=HIGH)
+    grown = jnp.matmul(pairing(2 * width)[None], grown, precision=HIGH)
+    grown = jnp.broadcast_to(grown[:, None], (depth, 2, 2 * width, 2 * length))
+    return grown.reshape(2 * depth, 2 * width, 2 * length)
 
 
 def alt_ext(values):

time: 307 us -> 172 us (0.56)
  local copies, waits for them, and re-layouts: 96.4 us -> 3.54 us
  other arithmetic: 44 us -> 4.04 us
  starting transfers between devices: 132 us -> 114 us
  waiting for transfers between devices: 30.2 us -> 40.2 us
  matrix products: 0 us -> 5.19 us
    reshape x5 -> x0, local copies, waits for them, and re-layouts: 74.1 us -> none  [the longest x4 73.9 us: coarsen(): values.reshape(depth // 2, 2, width // 2, 2, length // 2, 2)]
    reduce_sum x12 -> x5, other arithmetic: 31.9 us -> 0.51 us  [coarsen(): summed = values.reshape(depth // 2, 2, width, length).sum(axis=1)]
    ppermute x28, starting transfers between devices: 66 us -> 44.6 us  [with_halo(): after = lax.ppermute(leading, axis, down)]
    ppermute x28, waiting for transfers between devices: 4.32 us -> 25.4 us  [with_halo(): before = lax.ppermute(last, axis, up)]
    ppermute x28, waiting for transfers between devices: 16.2 us -> 6.44 us  [with_halo(): after = lax.ppermute(leading, axis, down)]
    unnamed x19 -> x10, local copies, waits for them, and re-layouts: 7.73 us -> 0.89 us
    reduce_sum x4 -> x0, local copies, waits for them, and re-layouts: 6.68 us -> none  [coarsen(): values.reshape(depth // 2, 2, width // 2, 2, length // 2, 2)]
    dot_general x0 -> x20, matrix products: none -> 5.19 us  [the longest x8 2.37 us: coarsen(): summed = jnp.matmul(summed, pairing(length), precision=HIGH)]
  transfers between devices with their start and end apart: 65 -> 65, of which waited for: 18 -> 19; matrix products, arithmetic and copies ran while one was open for 41% -> 3% of each run, Pallas kernels for 0% -> 0%
where the time goes in v1:
time: 172 us; the launch traced here: 169 us
  starting transfers between devices  114 us (66%)
  waiting for transfers between devices  40.2 us (23%)
  matrix products  5.19 us (3%)
  other arithmetic  4.04 us (2%)
  local copies, waits for them, and re-layouts  3.54 us (2%)
    ppermute x28, starting transfers between devices, with_halo(): before = lax.ppermute(last, axis, up)  44.9 us
    ppermute x28, starting transfers between devices, with_halo(): after = lax.ppermute(leading, axis, down)  44.6 us
    ppermute x28, waiting for transfers between devices, with_halo(): before = lax.ppermute(last, axis, up)  25.4 us
    ppermute x8, starting transfers between devices, shifted(): return lax.ppermute(block, axis, route)  23.6 us
    ppermute x28, waiting for transfers between devices, with_halo(): after = lax.ppermute(leading, axis, down)  6.44 us
    ppermute x8, waiting for transfers between devices, shifted(): return lax.ppermute(block, axis, route)  5.63 us
  transfers between devices with their start and end apart: 65, of which 19 were waited for; matrix products, arithmetic and copies ran while one was open for 3% of the time, Pallas kernels for 0%

profile of v1, /device:TPU:8, one launch (start us, length us, event | category | flops | bytes accessed | tf_op | source)
XLA Modules:
  0.0 168.9 jit_solution(6403704342883911917)
XLA Ops:
  0.6 1.1 fusion.326
  1.8 1.0 collective-permute-start.7
  2.8 3.3 %collective-permute-start.5 = (f32[1,64,256]{2,1,0:T(8,128)S(1)}, f32[1,64,256]{2,1,0:T(8,128)S(1)}, u32[]{:S(2)}, u32[]{:S(2)}) collective-permute-start(f32[1,64,256]{2,1,0:T(8,128)S(1)} %get-tuple-element.52), channel_id=1, source_target_pairs={{4,0},{8,4},{12,8},{16,12},{20,16},{24,20},{28,24},{5,1},{9,5},{13... | collective-permute-start | bytes 196616 | tf_op jit(solution)/shard_map/ppermute | solution.py:21
  6.1 2.7 %collective-permute-start.4 = (f32[1,64,256]{2,1,0:T(8,128)S(1)}, f32[1,64,256]{2,1,0:T(8,128)S(1)}, u32[]{:S(2)}, u32[]{:S(2)}) collective-permute-start(f32[1,64,256]{2,1,0:T(8,128)S(1)} %get-tuple-element.51), channel_id=1, source_target_pairs={{0,4},{4,8},{8,12},{12,16},{16,20},{20,24},{24,28},{1,5},{5,9},{9,... | collective-permute-start | bytes 196616 | tf_op jit(solution)/shard_map/ppermute | solution.py:20
  9.3 0.9 copy-done.1
  12.2 4.3 %collective-permute-start = (f32[1,64,256]{2,1,0:T(8,128)S(1)}, f32[1,64,256]{2,1,0:T(8,128)S(1)}, u32[]{:S(2)}, u32[]{:S(2)}) collective-permute-start(f32[1,64,256]{2,1,0:T(8,128)S(1)} %get-tuple-element.48), channel_id=1, source_target_pairs={{0,4},{4,8},{8,12},{12,16},{16,20},{20,24},{24,28},{1,5},{5,9},{9,... | collective-permute-start | bytes 196616 | tf_op jit(solution)/shard_map/ppermute | solution.py:20
  16.5 2.4 %collective-permute-start.1 = (f32[1,64,256]{2,1,0:T(8,128)S(1)}, f32[1,64,256]{2,1,0:T(8,128)S(1)}, u32[]{:S(2)}, u32[]{:S(2)}) collective-permute-start(f32[1,64,256]{2,1,0:T(8,128)S(1)} %get-tuple-element.47), channel_id=1, source_target_pairs={{4,0},{8,4},{12,8},{16,12},{20,16},{24,20},{28,24},{5,1},{9,5},{13... | collective-permute-start | bytes 196616 | tf_op jit(solution)/shard_map/ppermute | solution.py:21
  19.0 1.1 collective-permute-start.3
  20.3 2.3 %collective-permute-done.3 = f32[4,64,1]{2,1,0:T(8,128)S(1)} collective-permute-done((f32[4,64,1]{2,1,0:T(8,128)S(1)}, f32[4,64,1]{2,1,0:T(8,128)S(1)}, u32[]{:S(2)}, u32[]{:S(2)}) %collective-permute-start.3) | collective-permute-done | bytes 1056 | tf_op jit(solution)/shard_map/ppermute | solution.py:21
  22.6 3.4 %collective-permute-start.16 = (f32[1,32,128]{2,1,0:T(8,128)S(1)}, f32[1,32,128]{2,1,0:T(8,128)S(1)}, u32[]{:S(2)}, u32[]{:S(2)}) collective-permute-start(f32[1,32,128]{2,1,0:T(8,128)S(1)} %get-tuple-element.88), channel_id=1, source_target_pairs={{0,4},{4,8},{8,12},{12,16},{16,20},{20,24},{24,28},{1,5},{5,9},{9,... | collective-permute-start | bytes 49160 | tf_op jit(solution)/shard_map/ppermute | solution.py:20
  26.6 1.6 collective-permute-start.11
  28.3 3.3 %collective-permute-start.9 = (f32[1,64,256]{2,1,0:T(8,128)S(1)}, f32[1,64,256]{2,1,0:T(8,128)S(1)}, u32[]{:S(2)}, u32[]{:S(2)}) collective-permute-start(f32[1,64,256]{2,1,0:T(8,128)S(1)} %get-tuple-element.42), channel_id=1, source_target_pairs={{4,0},{8,4},{12,8},{16,12},{20,16},{24,20},{28,24},{5,1},{9,5},{13... | collective-permute-start | bytes 196616 | tf_op jit(solution)/shard_map/ppermute | solution.py:21
  31.6 2.5 %collective-permute-start.8 = (f32[1,64,256]{2,1,0:T(8,128)S(1)}, f32[1,64,256]{2,1,0:T(8,128)S(1)}, u32[]{:S(2)}, u32[]{:S(2)}) collective-permute-start(f32[1,64,256]{2,1,0:T(8,128)S(1)} %get-tuple-element.41), channel_id=1, source_target_pairs={{0,4},{4,8},{8,12},{12,16},{16,20},{20,24},{24,28},{1,5},{5,9},{9,... | collective-permute-start | bytes 196616 | tf_op jit(solution)/shard_map/ppermute | solution.py:20
  34.2 0.7 collective-permute-done.9
  34.9 4.4 %collective-permute-done.8 = f32[1,64,256]{2,1,0:T(8,128)S(1)} collective-permute-done((f32[1,64,256]{2,1,0:T(8,128)S(1)}, f32[1,64,256]{2,1,0:T(8,128)S(1)}, u32[]{:S(2)}, u32[]{:S(2)}) %collective-permute-start.8) | collective-permute-done | bytes 65568 | tf_op jit(solution)/shard_map/ppermute | solution.py:20
  40.3 1.9 %collective-permute-start.13 = (f32[1,64,256]{2,1,0:T(8,128)S(1)}, f32[1,64,256]{2,1,0:T(8,128)S(1)}, u32[]{:S(2)}, u32[]{:S(2)}) collective-permute-start(f32[1,64,256]{2,1,0:T(8,128)S(1)} %get-tuple-element.34), channel_id=1, source_target_pairs={{4,0},{8,4},{12,8},{16,12},{20,16},{24,20},{28,24},{5,1},{9,5},{13... | collective-permute-start | bytes 196616 | tf_op jit(solution)/shard_map/ppermute | solution.py:21
  42.3 3.9 %collective-permute-start.12 = (f32[1,64,256]{2,1,0:T(8,128)S(1)}, f32[1,64,256]{2,1,0:T(8,128)S(1)}, u32[]{:S(2)}, u32[]{:S(2)}) collective-permute-start(f32[1,64,256]{2,1,0:T(8,128)S(1)} %get-tuple-element.33), channel_id=1, source_target_pairs={{0,4},{4,8},{8,12},{12,16},{16,20},{20,24},{24,28},{1,5},{5,9},{9,... | collective-permute-start | bytes 196616 | tf_op jit(solution)/shard_map/ppermute | solution.py:20
  46.2 2.8 %collective-permute-start.17 = (f32[1,32,128]{2,1,0:T(8,128)S(1)}, f32[1,32,128]{2,1,0:T(8,128)S(1)}, u32[]{:S(2)}, u32[]{:S(2)}) collective-permute-start(f32[1,32,128]{2,1,0:T(8,128)S(1)} %get-tuple-element.87), channel_id=1, source_target_pairs={{4,0},{8,4},{12,8},{16,12},{20,16},{24,20},{28,24},{5,1},{9,5},{13... | collective-permute-start | bytes 49160 | tf_op jit(solution)/shard_map/ppermute | solution.py:21
  49.1 0.8 collective-permute-start.18
  49.9 1.0 collective-permute-start.19
  51.6 0.9 collective-permute-done.18
  52.7 1.8 %collective-permute-start.23 = (f32[2,32,1]{2,1,0:T(8,128)S(1)}, f32[2,32,1]{2,1,0:T(8,128)S(1)}, u32[]{:S(2)}, u32[]{:S(2)}) collective-permute-start(f32[2,32,1]{2,1,0:T(8,128)S(1)} %get-tuple-element.84), channel_id=1, source_target_pairs={{1,0},{2,1},{3,2},{0,3},{5,4},{6,5},{7,6},{4,7},{9,8},{10,9},{11,1... | collective-permute-start | bytes 776 | tf_op jit(solution)/shard_map/ppermute | solution.py:21
  54.5 2.2 %collective-permute-start.21 = (f32[1,32,128]{2,1,0:T(8,128)S(1)}, f32[1,32,128]{2,1,0:T(8,128)S(1)}, u32[]{:S(2)}, u32[]{:S(2)}) collective-permute-start(f32[1,32,128]{2,1,0:T(8,128)S(1)} %get-tuple-element.82), channel_id=1, source_target_pairs={{4,0},{8,4},{12,8},{16,12},{20,16},{24,20},{28,24},{5,1},{9,5},{13... | collective-permute-start | bytes 49160 | tf_op jit(solution)/shard_map/ppermute | solution.py:21
  56.7 3.6 %collective-permute-start.20 = (f32[1,32,128]{2,1,0:T(8,128)S(1)}, f32[1,32,128]{2,1,0:T(8,128)S(1)}, u32[]{:S(2)}, u32[]{:S(2)}) collective-permute-start(f32[1,32,128]{2,1,0:T(8,128)S(1)} %get-tuple-element.81), channel_id=1, source_target_pairs={{0,4},{4,8},{8,12},{12,16},{16,20},{20,24},{24,28},{1,5},{5,9},{9,... | collective-permute-start | bytes 49160 | tf_op jit(solution)/shard_map/ppermute | solution.py:20
  61.5 2.0 %collective-permute-done.20 = f32[1,32,128]{2,1,0:T(8,128)S(1)} collective-permute-done((f32[1,32,128]{2,1,0:T(8,128)S(1)}, f32[1,32,128]{2,1,0:T(8,128)S(1)}, u32[]{:S(2)}, u32[]{:S(2)}) %collective-permute-start.20) | collective-permute-done | bytes 16416 | tf_op jit(solution)/shard_map/ppermute | solution.py:20
  64.1 1.9 %collective-permute-start.25 = (f32[1,32,128]{2,1,0:T(8,128)S(1)}, f32[1,32,128]{2,1,0:T(8,128)S(1)}, u32[]{:S(2)}, u32[]{:S(2)}) collective-permute-start(f32[1,32,128]{2,1,0:T(8,128)S(1)} %get-tuple-element.74), channel_id=1, source_target_pairs={{4,0},{8,4},{12,8},{16,12},{20,16},{24,20},{28,24},{5,1},{9,5},{13... | collective-permute-start | bytes 49160 | tf_op jit(solution)/shard_map/ppermute | solution.py:21
  66.1 3.9 %collective-permute-start.24 = (f32[1,32,128]{2,1,0:T(8,128)S(1)}, f32[1,32,128]{2,1,0:T(8,128)S(1)}, u32[]{:S(2)}, u32[]{:S(2)}) collective-permute-start(f32[1,32,128]{2,1,0:T(8,128)S(1)} %get-tuple-element.73), channel_id=1, source_target_pairs={{0,4},{4,8},{8,12},{12,16},{16,20},{20,24},{24,28},{1,5},{5,9},{9,... | collective-permute-start | bytes 49160 | tf_op jit(solution)/shard_map/ppermute | solution.py:20
  70.0 2.6 %collective-permute-done.24 = f32[1,32,128]{2,1,0:T(8,128)S(1)} collective-permute-done((f32[1,32,128]{2,1,0:T(8,128)S(1)}, f32[1,32,128]{2,1,0:T(8,128)S(1)}, u32[]{:S(2)}, u32[]{:S(2)}) %collective-permute-start.24) | collective-permute-done | bytes 16416 | tf_op jit(solution)/shard_map/ppermute | solution.py:20
  73.2 1.3 collective-permute-start.28
  74.5 2.7 %collective-permute-done.28 = f32[4,1,16,64]{3,2,1,0:T(8,128)S(1)} collective-permute-done((f32[4,1,16,64]{3,2,1,0:T(8,128)S(1)}, f32[4,1,16,64]{3,2,1,0:T(8,128)S(1)}, u32[]{:S(2)}, u32[]{:S(2)}) %collective-permute-start.28) | collective-permute-done | bytes 16416 | tf_op jit(solution)/shard_map/ppermute | solution.py:39
  77.3 1.9 %collective-permute-start.30 = (f32[1,16,64]{2,1,0:T(8,128)S(1)}, f32[1,16,64]{2,1,0:T(8,128)S(1)}, u32[]{:S(2)}, u32[]{:S(2)}) collective-permute-start(f32[1,16,64]{2,1,0:T(8,128)S(1)} %slice_bitcast_fusion), channel_id=1, source_target_pairs={{8,0},{12,4},{16,8},{20,12},{24,16},{28,20},{9,1},{13,5},{17,9},{2... | collective-permute-start | bytes 12296 | tf_op jit(solution)/shard_map/ppermute | solution.py:29
  79.2 4.2 %collective-permute-start.29 = (f32[1,16,64]{2,1,0:T(8,128)S(1)}, f32[1,16,64]{2,1,0:T(8,128)S(1)}, u32[]{:S(2)}, u32[]{:S(2)}) collective-permute-start(f32[1,16,64]{2,1,0:T(8,128)S(1)} %slice_bitcast_fusion.1), channel_id=1, source_target_pairs={{0,8},{4,12},{8,16},{12,20},{16,24},{20,28},{1,9},{5,13},{9,17},{1... | collective-permute-start | bytes 12296 | tf_op jit(solution)/shard_map/ppermute | solution.py:29
  83.4 1.7 %collective-permute-start.32 = (f32[2,16,1]{2,1,0:T(8,128)S(1)}, f32[2,16,1]{2,1,0:T(8,128)S(1)}, u32[]{:S(2)}, u32[]{:S(2)}) collective-permute-start(f32[2,16,1]{2,1,0:T(8,128)S(1)} %get-tuple-element.109), channel_id=1, source_target_pairs={{1,0},{2,1},{3,2},{0,3},{5,4},{6,5},{7,6},{4,7},{9,8},{10,9},{11,1... | collective-permute-start | bytes 392 | tf_op jit(solution)/shard_map/ppermute | solution.py:21
  85.2 1.4 collective-permute-done.31
  86.8 1.7 %collective-permute-start.36 = (f32[2,16,1]{2,1,0:T(8,128)S(1)}, f32[2,16,1]{2,1,0:T(8,128)S(1)}, u32[]{:S(2)}, u32[]{:S(2)}) collective-permute-start(f32[2,16,1]{2,1,0:T(8,128)S(1)} %get-tuple-element.108), channel_id=1, source_target_pairs={{1,0},{2,1},{3,2},{0,3},{5,4},{6,5},{7,6},{4,7},{9,8},{10,9},{11,1... | collective-permute-start | bytes 392 | tf_op jit(solution)/shard_map/ppermute | solution.py:21
  88.5 3.9 %collective-permute-start.33 = (f32[1,16,64]{2,1,0:T(8,128)S(1)}, f32[1,16,64]{2,1,0:T(8,128)S(1)}, u32[]{:S(2)}, u32[]{:S(2)}) collective-permute-start(f32[1,16,64]{2,1,0:T(8,128)S(1)} %get-tuple-element.105), channel_id=1, source_target_pairs={{0,8},{4,12},{8,16},{12,20},{16,24},{20,28},{1,9},{5,13},{9,17},{1... | collective-permute-start | bytes 12296 | tf_op jit(solution)/shard_map/ppermute | solution.py:29
  92.5 1.9 %collective-permute-start.34 = (f32[1,16,64]{2,1,0:T(8,128)S(1)}, f32[1,16,64]{2,1,0:T(8,128)S(1)}, u32[]{:S(2)}, u32[]{:S(2)}) collective-permute-start(f32[1,16,64]{2,1,0:T(8,128)S(1)} %get-tuple-element.106), channel_id=1, source_target_pairs={{8,0},{12,4},{16,8},{20,12},{24,16},{28,20},{9,1},{13,5},{17,9},{2... | collective-permute-start | bytes 12296 | tf_op jit(solution)/shard_map/ppermute | solution.py:29
  94.4 3.6 %collective-permute-done.34 = f32[1,16,64]{2,1,0:T(8,128)S(1)} collective-permute-done((f32[1,16,64]{2,1,0:T(8,128)S(1)}, f32[1,16,64]{2,1,0:T(8,128)S(1)}, u32[]{:S(2)}, u32[]{:S(2)}) %collective-permute-start.34) | collective-permute-done | bytes 4128 | tf_op jit(solution)/shard_map/ppermute | solution.py:29
  98.7 2.3 %collective-permute-start.37 = (f32[1,16,64]{2,1,0:T(8,128)S(1)}, f32[1,16,64]{2,1,0:T(8,128)S(1)}, u32[]{:S(2)}, u32[]{:S(2)}) collective-permute-start(f32[1,16,64]{2,1,0:T(8,128)S(1)} %get-tuple-element.99), channel_id=1, source_target_pairs={{0,8},{4,12},{8,16},{12,20},{16,24},{20,28},{1,9},{5,13},{9,17},{1... | collective-permute-start | bytes 12296 | tf_op jit(solution)/shard_map/ppermute | solution.py:29
  101.0 3.5 %collective-permute-start.38 = (f32[1,16,64]{2,1,0:T(8,128)S(1)}, f32[1,16,64]{2,1,0:T(8,128)S(1)}, u32[]{:S(2)}, u32[]{:S(2)}) collective-permute-start(f32[1,16,64]{2,1,0:T(8,128)S(1)} %get-tuple-element.100), channel_id=1, source_target_pairs={{8,0},{12,4},{16,8},{20,12},{24,16},{28,20},{9,1},{13,5},{17,9},{2... | collective-permute-start | bytes 12296 | tf_op jit(solution)/shard_map/ppermute | solution.py:29
  104.6 2.0 %collective-permute-done.38 = f32[1,16,64]{2,1,0:T(8,128)S(1)} collective-permute-done((f32[1,16,64]{2,1,0:T(8,128)S(1)}, f32[1,16,64]{2,1,0:T(8,128)S(1)}, u32[]{:S(2)}, u32[]{:S(2)}) %collective-permute-start.38) | collective-permute-done | bytes 4128 | tf_op jit(solution)/shard_map/ppermute | solution.py:29
  106.9 1.9 %collective-permute-start.41 = (f32[1,16,64]{2,1,0:T(8,128)S(1)}, f32[1,16,64]{2,1,0:T(8,128)S(1)}, u32[]{:S(2)}, u32[]{:S(2)}) collective-permute-start(f32[1,16,64]{2,1,0:T(8,128)S(1)} %get-tuple-element.93), channel_id=1, source_target_pairs={{0,8},{4,12},{8,16},{12,20},{16,24},{20,28},{1,9},{5,13},{9,17},{1... | collective-permute-start | bytes 12296 | tf_op jit(solution)/shard_map/ppermute | solution.py:29
  108.8 3.9 %collective-permute-start.42 = (f32[1,16,64]{2,1,0:T(8,128)S(1)}, f32[1,16,64]{2,1,0:T(8,128)S(1)}, u32[]{:S(2)}, u32[]{:S(2)}) collective-permute-start(f32[1,16,64]{2,1,0:T(8,128)S(1)} %get-tuple-element.94), channel_id=1, source_target_pairs={{8,0},{12,4},{16,8},{20,12},{24,16},{28,20},{9,1},{13,5},{17,9},{2... | collective-permute-start | bytes 12296 | tf_op jit(solution)/shard_map/ppermute | solution.py:29
  112.7 1.1 collective-permute-start.44
  113.9 1.4 collective-permute-done.44
  116.0 1.7 %collective-permute-start.48 = (f32[2,32,1]{2,1,0:T(8,128)S(1)}, f32[2,32,1]{2,1,0:T(8,128)S(1)}, u32[]{:S(2)}, u32[]{:S(2)}) collective-permute-start(f32[2,32,1]{2,1,0:T(8,128)S(1)} %get-tuple-element.70), channel_id=1, source_target_pairs={{1,0},{2,1},{3,2},{0,3},{5,4},{6,5},{7,6},{4,7},{9,8},{10,9},{11,1... | collective-permute-start | bytes 776 | tf_op jit(solution)/shard_map/ppermute | solution.py:21
  117.7 2.5 %collective-permute-start.46 = (f32[1,32,128]{2,1,0:T(8,128)S(1)}, f32[1,32,128]{2,1,0:T(8,128)S(1)}, u32[]{:S(2)}, u32[]{:S(2)}) collective-permute-start(f32[1,32,128]{2,1,0:T(8,128)S(1)} %get-tuple-element.68), channel_id=1, source_target_pairs={{4,0},{8,4},{12,8},{16,12},{20,16},{24,20},{28,24},{5,1},{9,5},{13... | collective-permute-start | bytes 49160 | tf_op jit(solution)/shard_map/ppermute | solution.py:21
  120.2 3.3 %collective-permute-start.45 = (f32[1,32,128]{2,1,0:T(8,128)S(1)}, f32[1,32,128]{2,1,0:T(8,128)S(1)}, u32[]{:S(2)}, u32[]{:S(2)}) collective-permute-start(f32[1,32,128]{2,1,0:T(8,128)S(1)} %get-tuple-element.67), channel_id=1, source_target_pairs={{0,4},{4,8},{8,12},{12,16},{16,20},{20,24},{24,28},{1,5},{5,9},{9,... | collective-permute-start | bytes 49160 | tf_op jit(solution)/shard_map/ppermute | solution.py:20
  123.6 3.1 %collective-permute-done.45 = f32[1,32,128]{2,1,0:T(8,128)S(1)} collective-permute-done((f32[1,32,128]{2,1,0:T(8,128)S(1)}, f32[1,32,128]{2,1,0:T(8,128)S(1)}, u32[]{:S(2)}, u32[]{:S(2)}) %collective-permute-start.45) | collective-permute-done | bytes 16416 | tf_op jit(solution)/shard_map/ppermute | solution.py:20
  127.5 1.9 %collective-permute-start.50 = (f32[1,32,128]{2,1,0:T(8,128)S(1)}, f32[1,32,128]{2,1,0:T(8,128)S(1)}, u32[]{:S(2)}, u32[]{:S(2)}) collective-permute-start(f32[1,32,128]{2,1,0:T(8,128)S(1)} %get-tuple-element.62), channel_id=1, source_target_pairs={{4,0},{8,4},{12,8},{16,12},{20,16},{24,20},{28,24},{5,1},{9,5},{13... | collective-permute-start | bytes 49160 | tf_op jit(solution)/shard_map/ppermute | solution.py:21
  129.5 3.9 %collective-permute-start.49 = (f32[1,32,128]{2,1,0:T(8,128)S(1)}, f32[1,32,128]{2,1,0:T(8,128)S(1)}, u32[]{:S(2)}, u32[]{:S(2)}) collective-permute-start(f32[1,32,128]{2,1,0:T(8,128)S(1)} %get-tuple-element.61), channel_id=1, source_target_pairs={{0,4},{4,8},{8,12},{12,16},{16,20},{20,24},{24,28},{1,5},{5,9},{9,... | collective-permute-start | bytes 49160 | tf_op jit(solution)/shard_map/ppermute | solution.py:20
  133.4 2.6 %collective-permute-done.49 = f32[1,32,128]{2,1,0:T(8,128)S(1)} collective-permute-done((f32[1,32,128]{2,1,0:T(8,128)S(1)}, f32[1,32,128]{2,1,0:T(8,128)S(1)}, u32[]{:S(2)}, u32[]{:S(2)}) %collective-permute-start.49) | collective-permute-done | bytes 16416 | tf_op jit(solution)/shard_map/ppermute | solution.py:20
  137.4 1.9 %collective-permute-start.54 = (f32[1,64,256]{2,1,0:T(8,128)S(1)}, f32[1,64,256]{2,1,0:T(8,128)S(1)}, u32[]{:S(2)}, u32[]{:S(2)}) collective-permute-start(f32[1,64,256]{2,1,0:T(8,128)S(1)} %get-tuple-element.30), channel_id=1, source_target_pairs={{4,0},{8,4},{12,8},{16,12},{20,16},{24,20},{28,24},{5,1},{9,5},{13... | collective-permute-start | bytes 196616 | tf_op jit(solution)/shard_map/ppermute | solution.py:21
  139.3 3.9 %collective-permute-start.53 = (f32[1,64,256]{2,1,0:T(8,128)S(1)}, f32[1,64,256]{2,1,0:T(8,128)S(1)}, u32[]{:S(2)}, u32[]{:S(2)}) collective-permute-start(f32[1,64,256]{2,1,0:T(8,128)S(1)} %get-tuple-element.29), channel_id=1, source_target_pairs={{0,4},{4,8},{8,12},{12,16},{16,20},{20,24},{24,28},{1,5},{5,9},{9,... | collective-permute-start | bytes 196616 | tf_op jit(solution)/shard_map/ppermute | solution.py:20
  143.8 2.8 %collective-permute-done.53 = f32[1,64,256]{2,1,0:T(8,128)S(1)} collective-permute-done((f32[1,64,256]{2,1,0:T(8,128)S(1)}, f32[1,64,256]{2,1,0:T(8,128)S(1)}, u32[]{:S(2)}, u32[]{:S(2)}) %collective-permute-start.53) | collective-permute-done | bytes 65568 | tf_op jit(solution)/shard_map/ppermute | solution.py:20
  147.8 1.9 %collective-permute-start.58 = (f32[1,64,256]{2,1,0:T(8,128)S(1)}, f32[1,64,256]{2,1,0:T(8,128)S(1)}, u32[]{:S(2)}, u32[]{:S(2)}) collective-permute-start(f32[1,64,256]{2,1,0:T(8,128)S(1)} %get-tuple-element.24), channel_id=1, source_target_pairs={{4,0},{8,4},{12,8},{16,12},{20,16},{24,20},{28,24},{5,1},{9,5},{13... | collective-permute-start | bytes 196616 | tf_op jit(solution)/shard_map/ppermute | solution.py:21
  149.7 3.9 %collective-permute-start.57 = (f32[1,64,256]{2,1,0:T(8,128)S(1)}, f32[1,64,256]{2,1,0:T(8,128)S(1)}, u32[]{:S(2)}, u32[]{:S(2)}) collective-permute-start(f32[1,64,256]{2,1,0:T(8,128)S(1)} %get-tuple-element.23), channel_id=1, source_target_pairs={{0,4},{4,8},{8,12},{12,16},{16,20},{20,24},{24,28},{1,5},{5,9},{9,... | collective-permute-start | bytes 196616 | tf_op jit(solution)/shard_map/ppermute | solution.py:20
  153.7 0.7 collective-permute-done.58
  154.5 2.8 %collective-permute-done.57 = f32[1,64,256]{2,1,0:T(8,128)S(1)} collective-permute-done((f32[1,64,256]{2,1,0:T(8,128)S(1)}, f32[1,64,256]{2,1,0:T(8,128)S(1)}, u32[]{:S(2)}, u32[]{:S(2)}) %collective-permute-start.57) | collective-permute-done | bytes 65568 | tf_op jit(solution)/shard_map/ppermute | solution.py:20
  158.4 1.9 %collective-permute-start.62 = (f32[1,64,256]{2,1,0:T(8,128)S(1)}, f32[1,64,256]{2,1,0:T(8,128)S(1)}, u32[]{:S(2)}, u32[]{:S(2)}) collective-permute-start(f32[1,64,256]{2,1,0:T(8,128)S(1)} %get-tuple-element.18), channel_id=1, source_target_pairs={{4,0},{8,4},{12,8},{16,12},{20,16},{24,20},{28,24},{5,1},{9,5},{13... | collective-permute-start | bytes 196616 | tf_op jit(solution)/shard_map/ppermute | solution.py:21
  160.3 3.9 %collective-permute-start.61 = (f32[1,64,256]{2,1,0:T(8,128)S(1)}, f32[1,64,256]{2,1,0:T(8,128)S(1)}, u32[]{:S(2)}, u32[]{:S(2)}) collective-permute-start(f32[1,64,256]{2,1,0:T(8,128)S(1)} %get-tuple-element.17), channel_id=1, source_target_pairs={{0,4},{4,8},{8,12},{12,16},{16,20},{20,24},{24,28},{1,5},{5,9},{9,... | collective-permute-start | bytes 196616 | tf_op jit(solution)/shard_map/ppermute | solution.py:20
  164.3 0.7 collective-permute-done.62
  165.0 2.8 %collective-permute-done.61 = f32[1,64,256]{2,1,0:T(8,128)S(1)} collective-permute-done((f32[1,64,256]{2,1,0:T(8,128)S(1)}, f32[1,64,256]{2,1,0:T(8,128)S(1)}, u32[]{:S(2)}, u32[]{:S(2)}) %collective-permute-start.61) | collective-permute-done | bytes 65568 | tf_op jit(solution)/shard_map/ppermute | solution.py:20
  167.8 1.1 fusion.11
  (174 shorter events, 14.7 us)
Async XLA Ops:
  1.8 10.4 %collective-permute-start.7 = (f32[4,64,1]{2,1,0:T(8,128)S(1)}, f32[4,64,1]{2,1,0:T(8,128)S(1)}, u32[]{:S(2)}, u32[]{:S(2)}) collective-permute-start(f32[4,64,1]{2,1,0:T(8,128)S(1)} %get-tuple-element.54), channel_id=1, source_target_pairs={{1,0},{2,1},{3,2},{0,3},{5,4},{6,5},{7,6},{4,7},{9,8},{10,9},{11,1... | collective-permute-start | bytes 3080 | tf_op jit(solution)/shard_map/ppermute | solution.py:21
  2.7 13.8 %collective-permute-start.6 = (f32[4,64,1]{2,1,0:T(8,128)S(1)}, f32[4,64,1]{2,1,0:T(8,128)S(1)}, u32[]{:S(2)}, u32[]{:S(2)}) collective-permute-start(f32[4,64,1]{2,1,0:T(8,128)S(1)} %get-tuple-element.53), channel_id=1, source_target_pairs={{0,1},{1,2},{2,3},{3,0},{4,5},{5,6},{6,7},{7,4},{8,9},{9,10},{10,1... | collective-permute-start | bytes 3080 | tf_op jit(solution)/shard_map/ppermute | solution.py:20
  2.8 23.2 %collective-permute-start.5 = (f32[1,64,256]{2,1,0:T(8,128)S(1)}, f32[1,64,256]{2,1,0:T(8,128)S(1)}, u32[]{:S(2)}, u32[]{:S(2)}) collective-permute-start(f32[1,64,256]{2,1,0:T(8,128)S(1)} %get-tuple-element.52), channel_id=1, source_target_pairs={{4,0},{8,4},{12,8},{16,12},{20,16},{24,20},{28,24},{5,1},{9,5},{13... | collective-permute-start | bytes 196616 | tf_op jit(solution)/shard_map/ppermute | solution.py:21
  6.1 19.9 %collective-permute-start.4 = (f32[1,64,256]{2,1,0:T(8,128)S(1)}, f32[1,64,256]{2,1,0:T(8,128)S(1)}, u32[]{:S(2)}, u32[]{:S(2)}) collective-permute-start(f32[1,64,256]{2,1,0:T(8,128)S(1)} %get-tuple-element.51), channel_id=1, source_target_pairs={{0,4},{4,8},{8,12},{12,16},{16,20},{20,24},{24,28},{1,5},{5,9},{9,... | collective-permute-start | bytes 196616 | tf_op jit(solution)/shard_map/ppermute | solution.py:20
  8.9 10.1 %collective-permute-start.2 = (f32[4,64,1]{2,1,0:T(8,128)S(1)}, f32[4,64,1]{2,1,0:T(8,128)S(1)}, u32[]{:S(2)}, u32[]{:S(2)}) collective-permute-start(f32[4,64,1]{2,1,0:T(8,128)S(1)} %get-tuple-element.46), channel_id=1, source_target_pairs={{0,1},{1,2},{2,3},{3,0},{4,5},{5,6},{6,7},{7,4},{8,9},{9,10},{10,1... | collective-permute-start | bytes 3080 | tf_op jit(solution)/shard_map/ppermute | solution.py:20
  12.2 13.8 %collective-permute-start = (f32[1,64,256]{2,1,0:T(8,128)S(1)}, f32[1,64,256]{2,1,0:T(8,128)S(1)}, u32[]{:S(2)}, u32[]{:S(2)}) collective-permute-start(f32[1,64,256]{2,1,0:T(8,128)S(1)} %get-tuple-element.48), channel_id=1, source_target_pairs={{0,4},{4,8},{8,12},{12,16},{16,20},{20,24},{24,28},{1,5},{5,9},{9,... | collective-permute-start | bytes 196616 | tf_op jit(solution)/shard_map/ppermute | solution.py:20
  16.5 9.5 %collective-permute-start.1 = (f32[1,64,256]{2,1,0:T(8,128)S(1)}, f32[1,64,256]{2,1,0:T(8,128)S(1)}, u32[]{:S(2)}, u32[]{:S(2)}) collective-permute-start(f32[1,64,256]{2,1,0:T(8,128)S(1)} %get-tuple-element.47), channel_id=1, source_target_pairs={{4,0},{8,4},{12,8},{16,12},{20,16},{24,20},{28,24},{5,1},{9,5},{13... | collective-permute-start | bytes 196616 | tf_op jit(solution)/shard_map/ppermute | solution.py:21
  19.0 3.6 %collective-permute-start.3 = (f32[4,64,1]{2,1,0:T(8,128)S(1)}, f32[4,64,1]{2,1,0:T(8,128)S(1)}, u32[]{:S(2)}, u32[]{:S(2)}) collective-permute-start(f32[4,64,1]{2,1,0:T(8,128)S(1)} %get-tuple-element.45), channel_id=1, source_target_pairs={{1,0},{2,1},{3,2},{0,3},{5,4},{6,5},{7,6},{4,7},{9,8},{10,9},{11,1... | collective-permute-start | bytes 3080 | tf_op jit(solution)/shard_map/ppermute | solution.py:21
  22.6 29.9 %collective-permute-start.16 = (f32[1,32,128]{2,1,0:T(8,128)S(1)}, f32[1,32,128]{2,1,0:T(8,128)S(1)}, u32[]{:S(2)}, u32[]{:S(2)}) collective-permute-start(f32[1,32,128]{2,1,0:T(8,128)S(1)} %get-tuple-element.88), channel_id=1, source_target_pairs={{0,4},{4,8},{8,12},{12,16},{16,20},{20,24},{24,28},{1,5},{5,9},{9,... | collective-permute-start | bytes 49160 | tf_op jit(solution)/shard_map/ppermute | solution.py:20
  26.6 7.5 %collective-permute-start.11 = (f32[4,64,1]{2,1,0:T(8,128)S(1)}, f32[4,64,1]{2,1,0:T(8,128)S(1)}, u32[]{:S(2)}, u32[]{:S(2)}) collective-permute-start(f32[4,64,1]{2,1,0:T(8,128)S(1)} %get-tuple-element.44), channel_id=1, source_target_pairs={{1,0},{2,1},{3,2},{0,3},{5,4},{6,5},{7,6},{4,7},{9,8},{10,9},{11,1... | collective-permute-start | bytes 3080 | tf_op jit(solution)/shard_map/ppermute | solution.py:21
  28.3 5.9 %collective-permute-start.10 = (f32[4,64,1]{2,1,0:T(8,128)S(1)}, f32[4,64,1]{2,1,0:T(8,128)S(1)}, u32[]{:S(2)}, u32[]{:S(2)}) collective-permute-start(f32[4,64,1]{2,1,0:T(8,128)S(1)} %get-tuple-element.43), channel_id=1, source_target_pairs={{0,1},{1,2},{2,3},{3,0},{4,5},{5,6},{6,7},{7,4},{8,9},{9,10},{10,1... | collective-permute-start | bytes 3080 | tf_op jit(solution)/shard_map/ppermute | solution.py:20
  28.3 6.6 %collective-permute-start.9 = (f32[1,64,256]{2,1,0:T(8,128)S(1)}, f32[1,64,256]{2,1,0:T(8,128)S(1)}, u32[]{:S(2)}, u32[]{:S(2)}) collective-permute-start(f32[1,64,256]{2,1,0:T(8,128)S(1)} %get-tuple-element.42), channel_id=1, source_target_pairs={{4,0},{8,4},{12,8},{16,12},{20,16},{24,20},{28,24},{5,1},{9,5},{13... | collective-permute-start | bytes 196616 | tf_op jit(solution)/shard_map/ppermute | solution.py:21
  31.6 7.7 %collective-permute-start.8 = (f32[1,64,256]{2,1,0:T(8,128)S(1)}, f32[1,64,256]{2,1,0:T(8,128)S(1)}, u32[]{:S(2)}, u32[]{:S(2)}) collective-permute-start(f32[1,64,256]{2,1,0:T(8,128)S(1)} %get-tuple-element.41), channel_id=1, source_target_pairs={{0,4},{4,8},{8,12},{12,16},{16,20},{20,24},{24,28},{1,5},{5,9},{9,... | collective-permute-start | bytes 196616 | tf_op jit(solution)/shard_map/ppermute | solution.py:20
  39.8 6.5 %collective-permute-start.15 = (f32[4,64,1]{2,1,0:T(8,128)S(1)}, f32[4,64,1]{2,1,0:T(8,128)S(1)}, u32[]{:S(2)}, u32[]{:S(2)}) collective-permute-start(f32[4,64,1]{2,1,0:T(8,128)S(1)} %get-tuple-element.38), channel_id=1, source_target_pairs={{1,0},{2,1},{3,2},{0,3},{5,4},{6,5},{7,6},{4,7},{9,8},{10,9},{11,1... | collective-permute-start | bytes 3080 | tf_op jit(solution)/shard_map/ppermute | solution.py:21
  40.3 8.7 %collective-permute-start.14 = (f32[4,64,1]{2,1,0:T(8,128)S(1)}, f32[4,64,1]{2,1,0:T(8,128)S(1)}, u32[]{:S(2)}, u32[]{:S(2)}) collective-permute-start(f32[4,64,1]{2,1,0:T(8,128)S(1)} %get-tuple-element.37), channel_id=1, source_target_pairs={{0,1},{1,2},{2,3},{3,0},{4,5},{5,6},{6,7},{7,4},{8,9},{9,10},{10,1... | collective-permute-start | bytes 3080 | tf_op jit(solution)/shard_map/ppermute | solution.py:20
  40.3 9.5 %collective-permute-start.13 = (f32[1,64,256]{2,1,0:T(8,128)S(1)}, f32[1,64,256]{2,1,0:T(8,128)S(1)}, u32[]{:S(2)}, u32[]{:S(2)}) collective-permute-start(f32[1,64,256]{2,1,0:T(8,128)S(1)} %get-tuple-element.34), channel_id=1, source_target_pairs={{4,0},{8,4},{12,8},{16,12},{20,16},{24,20},{28,24},{5,1},{9,5},{13... | collective-permute-start | bytes 196616 | tf_op jit(solution)/shard_map/ppermute | solution.py:21
  42.3 8.6 %collective-permute-start.12 = (f32[1,64,256]{2,1,0:T(8,128)S(1)}, f32[1,64,256]{2,1,0:T(8,128)S(1)}, u32[]{:S(2)}, u32[]{:S(2)}) collective-permute-start(f32[1,64,256]{2,1,0:T(8,128)S(1)} %get-tuple-element.33), channel_id=1, source_target_pairs={{0,4},{4,8},{8,12},{12,16},{16,20},{20,24},{24,28},{1,5},{5,9},{9,... | collective-permute-start | bytes 196616 | tf_op jit(solution)/shard_map/ppermute | solution.py:20
  46.2 6.2 %collective-permute-start.17 = (f32[1,32,128]{2,1,0:T(8,128)S(1)}, f32[1,32,128]{2,1,0:T(8,128)S(1)}, u32[]{:S(2)}, u32[]{:S(2)}) collective-permute-start(f32[1,32,128]{2,1,0:T(8,128)S(1)} %get-tuple-element.87), channel_id=1, source_target_pairs={{4,0},{8,4},{12,8},{16,12},{20,16},{24,20},{28,24},{5,1},{9,5},{13... | collective-permute-start | bytes 49160 | tf_op jit(solution)/shard_map/ppermute | solution.py:21
  49.1 3.4 %collective-permute-start.18 = (f32[2,32,1]{2,1,0:T(8,128)S(1)}, f32[2,32,1]{2,1,0:T(8,128)S(1)}, u32[]{:S(2)}, u32[]{:S(2)}) collective-permute-start(f32[2,32,1]{2,1,0:T(8,128)S(1)} %get-tuple-element.86), channel_id=1, source_target_pairs={{0,1},{1,2},{2,3},{3,0},{4,5},{5,6},{6,7},{7,4},{8,9},{9,10},{10,1... | collective-permute-start | bytes 776 | tf_op jit(solution)/shard_map/ppermute | solution.py:20
  49.9 2.6 %collective-permute-start.19 = (f32[2,32,1]{2,1,0:T(8,128)S(1)}, f32[2,32,1]{2,1,0:T(8,128)S(1)}, u32[]{:S(2)}, u32[]{:S(2)}) collective-permute-start(f32[2,32,1]{2,1,0:T(8,128)S(1)} %get-tuple-element.85), channel_id=1, source_target_pairs={{1,0},{2,1},{3,2},{0,3},{5,4},{6,5},{7,6},{4,7},{9,8},{10,9},{11,1... | collective-permute-start | bytes 776 | tf_op jit(solution)/shard_map/ppermute | solution.py:21
  52.7 8.7 %collective-permute-start.23 = (f32[2,32,1]{2,1,0:T(8,128)S(1)}, f32[2,32,1]{2,1,0:T(8,128)S(1)}, u32[]{:S(2)}, u32[]{:S(2)}) collective-permute-start(f32[2,32,1]{2,1,0:T(8,128)S(1)} %get-tuple-element.84), channel_id=1, source_target_pairs={{1,0},{2,1},{3,2},{0,3},{5,4},{6,5},{7,6},{4,7},{9,8},{10,9},{11,1... | collective-permute-start | bytes 776 | tf_op jit(solution)/shard_map/ppermute | solution.py:21
  54.5 6.9 %collective-permute-start.22 = (f32[2,32,1]{2,1,0:T(8,128)S(1)}, f32[2,32,1]{2,1,0:T(8,128)S(1)}, u32[]{:S(2)}, u32[]{:S(2)}) collective-permute-start(f32[2,32,1]{2,1,0:T(8,128)S(1)} %get-tuple-element.83), channel_id=1, source_target_pairs={{0,1},{1,2},{2,3},{3,0},{4,5},{5,6},{6,7},{7,4},{8,9},{9,10},{10,1... | collective-permute-start | bytes 776 | tf_op jit(solution)/shard_map/ppermute | solution.py:20
  54.5 6.9 %collective-permute-start.21 = (f32[1,32,128]{2,1,0:T(8,128)S(1)}, f32[1,32,128]{2,1,0:T(8,128)S(1)}, u32[]{:S(2)}, u32[]{:S(2)}) collective-permute-start(f32[1,32,128]{2,1,0:T(8,128)S(1)} %get-tuple-element.82), channel_id=1, source_target_pairs={{4,0},{8,4},{12,8},{16,12},{20,16},{24,20},{28,24},{5,1},{9,5},{13... | collective-permute-start | bytes 49160 | tf_op jit(solution)/shard_map/ppermute | solution.py:21
  56.7 6.7 %collective-permute-start.20 = (f32[1,32,128]{2,1,0:T(8,128)S(1)}, f32[1,32,128]{2,1,0:T(8,128)S(1)}, u32[]{:S(2)}, u32[]{:S(2)}) collective-permute-start(f32[1,32,128]{2,1,0:T(8,128)S(1)} %get-tuple-element.81), channel_id=1, source_target_pairs={{0,4},{4,8},{8,12},{12,16},{16,20},{20,24},{24,28},{1,5},{5,9},{9,... | collective-permute-start | bytes 49160 | tf_op jit(solution)/shard_map/ppermute | solution.py:20
  63.6 6.4 %collective-permute-start.27 = (f32[2,32,1]{2,1,0:T(8,128)S(1)}, f32[2,32,1]{2,1,0:T(8,128)S(1)}, u32[]{:S(2)}, u32[]{:S(2)}) collective-permute-start(f32[2,32,1]{2,1,0:T(8,128)S(1)} %get-tuple-element.76), channel_id=1, source_target_pairs={{1,0},{2,1},{3,2},{0,3},{5,4},{6,5},{7,6},{4,7},{9,8},{10,9},{11,1... | collective-permute-start | bytes 776 | tf_op jit(solution)/shard_map/ppermute | solution.py:21
  64.1 5.9 %collective-permute-start.26 = (f32[2,32,1]{2,1,0:T(8,128)S(1)}, f32[2,32,1]{2,1,0:T(8,128)S(1)}, u32[]{:S(2)}, u32[]{:S(2)}) collective-permute-start(f32[2,32,1]{2,1,0:T(8,128)S(1)} %get-tuple-element.75), channel_id=1, source_target_pairs={{0,1},{1,2},{2,3},{3,0},{4,5},{5,6},{6,7},{7,4},{8,9},{9,10},{10,1... | collective-permute-start | bytes 776 | tf_op jit(solution)/shard_map/ppermute | solution.py:20
  64.1 5.9 %collective-permute-start.25 = (f32[1,32,128]{2,1,0:T(8,128)S(1)}, f32[1,32,128]{2,1,0:T(8,128)S(1)}, u32[]{:S(2)}, u32[]{:S(2)}) collective-permute-start(f32[1,32,128]{2,1,0:T(8,128)S(1)} %get-tuple-element.74), channel_id=1, source_target_pairs={{4,0},{8,4},{12,8},{16,12},{20,16},{24,20},{28,24},{5,1},{9,5},{13... | collective-permute-start | bytes 49160 | tf_op jit(solution)/shard_map/ppermute | solution.py:21
  66.1 6.5 %collective-permute-start.24 = (f32[1,32,128]{2,1,0:T(8,128)S(1)}, f32[1,32,128]{2,1,0:T(8,128)S(1)}, u32[]{:S(2)}, u32[]{:S(2)}) collective-permute-start(f32[1,32,128]{2,1,0:T(8,128)S(1)} %get-tuple-element.73), channel_id=1, source_target_pairs={{0,4},{4,8},{8,12},{12,16},{16,20},{20,24},{24,28},{1,5},{5,9},{9,... | collective-permute-start | bytes 49160 | tf_op jit(solution)/shard_map/ppermute | solution.py:20
  73.2 4.0 %collective-permute-start.28 = (f32[4,1,16,64]{3,2,1,0:T(8,128)S(1)}, f32[4,1,16,64]{3,2,1,0:T(8,128)S(1)}, u32[]{:S(2)}, u32[]{:S(2)}) collective-permute-start(f32[4,1,16,64]{3,2,1,0:T(8,128)S(1)} %pad_maximum_fusion.48), channel_id=1, source_target_pairs={{0,4},{4,0},{8,12},{12,8},{16,20},{20,16},{24,28},{28,24},{1,5},{5... | collective-permute-start | bytes 49160 | tf_op jit(solution)/shard_map/ppermute | solution.py:39
  77.3 9.4 %collective-permute-start.30 = (f32[1,16,64]{2,1,0:T(8,128)S(1)}, f32[1,16,64]{2,1,0:T(8,128)S(1)}, u32[]{:S(2)}, u32[]{:S(2)}) collective-permute-start(f32[1,16,64]{2,1,0:T(8,128)S(1)} %slice_bitcast_fusion), channel_id=1, source_target_pairs={{8,0},{12,4},{16,8},{20,12},{24,16},{28,20},{9,1},{13,5},{17,9},{2... | collective-permute-start | bytes 12296 | tf_op jit(solution)/shard_map/ppermute | solution.py:29
  79.2 7.4 %collective-permute-start.29 = (f32[1,16,64]{2,1,0:T(8,128)S(1)}, f32[1,16,64]{2,1,0:T(8,128)S(1)}, u32[]{:S(2)}, u32[]{:S(2)}) collective-permute-start(f32[1,16,64]{2,1,0:T(8,128)S(1)} %slice_bitcast_fusion.1), channel_id=1, source_target_pairs={{0,8},{4,12},{8,16},{12,20},{16,24},{20,28},{1,9},{5,13},{9,17},{1... | collective-permute-start | bytes 12296 | tf_op jit(solution)/shard_map/ppermute | solution.py:29
  83.4 3.2 %collective-permute-start.31 = (f32[2,16,1]{2,1,0:T(8,128)S(1)}, f32[2,16,1]{2,1,0:T(8,128)S(1)}, u32[]{:S(2)}, u32[]{:S(2)}) collective-permute-start(f32[2,16,1]{2,1,0:T(8,128)S(1)} %get-tuple-element.110), channel_id=1, source_target_pairs={{0,1},{1,2},{2,3},{3,0},{4,5},{5,6},{6,7},{7,4},{8,9},{9,10},{10,1... | collective-permute-start | bytes 392 | tf_op jit(solution)/shard_map/ppermute | solution.py:20
  83.4 3.2 %collective-permute-start.32 = (f32[2,16,1]{2,1,0:T(8,128)S(1)}, f32[2,16,1]{2,1,0:T(8,128)S(1)}, u32[]{:S(2)}, u32[]{:S(2)}) collective-permute-start(f32[2,16,1]{2,1,0:T(8,128)S(1)} %get-tuple-element.109), channel_id=1, source_target_pairs={{1,0},{2,1},{3,2},{0,3},{5,4},{6,5},{7,6},{4,7},{9,8},{10,9},{11,1... | collective-permute-start | bytes 392 | tf_op jit(solution)/shard_map/ppermute | solution.py:21
  86.8 7.6 %collective-permute-start.36 = (f32[2,16,1]{2,1,0:T(8,128)S(1)}, f32[2,16,1]{2,1,0:T(8,128)S(1)}, u32[]{:S(2)}, u32[]{:S(2)}) collective-permute-start(f32[2,16,1]{2,1,0:T(8,128)S(1)} %get-tuple-element.108), channel_id=1, source_target_pairs={{1,0},{2,1},{3,2},{0,3},{5,4},{6,5},{7,6},{4,7},{9,8},{10,9},{11,1... | collective-permute-start | bytes 392 | tf_op jit(solution)/shard_map/ppermute | solution.py:21
  88.5 5.9 %collective-permute-start.35 = (f32[2,16,1]{2,1,0:T(8,128)S(1)}, f32[2,16,1]{2,1,0:T(8,128)S(1)}, u32[]{:S(2)}, u32[]{:S(2)}) collective-permute-start(f32[2,16,1]{2,1,0:T(8,128)S(1)} %get-tuple-element.107), channel_id=1, source_target_pairs={{0,1},{1,2},{2,3},{3,0},{4,5},{5,6},{6,7},{7,4},{8,9},{9,10},{10,1... | collective-permute-start | bytes 392 | tf_op jit(solution)/shard_map/ppermute | solution.py:20
  88.5 5.9 %collective-permute-start.33 = (f32[1,16,64]{2,1,0:T(8,128)S(1)}, f32[1,16,64]{2,1,0:T(8,128)S(1)}, u32[]{:S(2)}, u32[]{:S(2)}) collective-permute-start(f32[1,16,64]{2,1,0:T(8,128)S(1)} %get-tuple-element.105), channel_id=1, source_target_pairs={{0,8},{4,12},{8,16},{12,20},{16,24},{20,28},{1,9},{5,13},{9,17},{1... | collective-permute-start | bytes 12296 | tf_op jit(solution)/shard_map/ppermute | solution.py:29
  92.5 5.5 %collective-permute-start.34 = (f32[1,16,64]{2,1,0:T(8,128)S(1)}, f32[1,16,64]{2,1,0:T(8,128)S(1)}, u32[]{:S(2)}, u32[]{:S(2)}) collective-permute-start(f32[1,16,64]{2,1,0:T(8,128)S(1)} %get-tuple-element.106), channel_id=1, source_target_pairs={{8,0},{12,4},{16,8},{20,12},{24,16},{28,20},{9,1},{13,5},{17,9},{2... | collective-permute-start | bytes 12296 | tf_op jit(solution)/shard_map/ppermute | solution.py:29
  98.2 6.4 %collective-permute-start.40 = (f32[2,16,1]{2,1,0:T(8,128)S(1)}, f32[2,16,1]{2,1,0:T(8,128)S(1)}, u32[]{:S(2)}, u32[]{:S(2)}) collective-permute-start(f32[2,16,1]{2,1,0:T(8,128)S(1)} %get-tuple-element.102), channel_id=1, source_target_pairs={{1,0},{2,1},{3,2},{0,3},{5,4},{6,5},{7,6},{4,7},{9,8},{10,9},{11,1... | collective-permute-start | bytes 392 | tf_op jit(solution)/shard_map/ppermute | solution.py:21
  98.5 6.1 %collective-permute-start.39 = (f32[2,16,1]{2,1,0:T(8,128)S(1)}, f32[2,16,1]{2,1,0:T(8,128)S(1)}, u32[]{:S(2)}, u32[]{:S(2)}) collective-permute-start(f32[2,16,1]{2,1,0:T(8,128)S(1)} %get-tuple-element.101), channel_id=1, source_target_pairs={{0,1},{1,2},{2,3},{3,0},{4,5},{5,6},{6,7},{7,4},{8,9},{9,10},{10,1... | collective-permute-start | bytes 392 | tf_op jit(solution)/shard_map/ppermute | solution.py:20
  98.7 5.9 %collective-permute-start.37 = (f32[1,16,64]{2,1,0:T(8,128)S(1)}, f32[1,16,64]{2,1,0:T(8,128)S(1)}, u32[]{:S(2)}, u32[]{:S(2)}) collective-permute-start(f32[1,16,64]{2,1,0:T(8,128)S(1)} %get-tuple-element.99), channel_id=1, source_target_pairs={{0,8},{4,12},{8,16},{12,20},{16,24},{20,28},{1,9},{5,13},{9,17},{1... | collective-permute-start | bytes 12296 | tf_op jit(solution)/shard_map/ppermute | solution.py:29
  101.0 5.6 %collective-permute-start.38 = (f32[1,16,64]{2,1,0:T(8,128)S(1)}, f32[1,16,64]{2,1,0:T(8,128)S(1)}, u32[]{:S(2)}, u32[]{:S(2)}) collective-permute-start(f32[1,16,64]{2,1,0:T(8,128)S(1)} %get-tuple-element.100), channel_id=1, source_target_pairs={{8,0},{12,4},{16,8},{20,12},{24,16},{28,20},{9,1},{13,5},{17,9},{2... | collective-permute-start | bytes 12296 | tf_op jit(solution)/shard_map/ppermute | solution.py:29
  106.8 7.1 %collective-permute-start.43 = (f32[2,16,1]{2,1,0:T(8,128)S(1)}, f32[2,16,1]{2,1,0:T(8,128)S(1)}, u32[]{:S(2)}, u32[]{:S(2)}) collective-permute-start(f32[2,16,1]{2,1,0:T(8,128)S(1)} %get-tuple-element.95), channel_id=1, source_target_pairs={{0,1},{1,2},{2,3},{3,0},{4,5},{5,6},{6,7},{7,4},{8,9},{9,10},{10,1... | collective-permute-start | bytes 392 | tf_op jit(solution)/shard_map/ppermute | solution.py:20
  106.9 8.4 %collective-permute-start.41 = (f32[1,16,64]{2,1,0:T(8,128)S(1)}, f32[1,16,64]{2,1,0:T(8,128)S(1)}, u32[]{:S(2)}, u32[]{:S(2)}) collective-permute-start(f32[1,16,64]{2,1,0:T(8,128)S(1)} %get-tuple-element.93), channel_id=1, source_target_pairs={{0,8},{4,12},{8,16},{12,20},{16,24},{20,28},{1,9},{5,13},{9,17},{1... | collective-permute-start | bytes 12296 | tf_op jit(solution)/shard_map/ppermute | solution.py:29
  108.8 6.5 %collective-permute-start.42 = (f32[1,16,64]{2,1,0:T(8,128)S(1)}, f32[1,16,64]{2,1,0:T(8,128)S(1)}, u32[]{:S(2)}, u32[]{:S(2)}) collective-permute-start(f32[1,16,64]{2,1,0:T(8,128)S(1)} %get-tuple-element.94), channel_id=1, source_target_pairs={{8,0},{12,4},{16,8},{20,12},{24,16},{28,20},{9,1},{13,5},{17,9},{2... | collective-permute-start | bytes 12296 | tf_op jit(solution)/shard_map/ppermute | solution.py:29
  116.0 7.6 %collective-permute-start.48 = (f32[2,32,1]{2,1,0:T(8,128)S(1)}, f32[2,32,1]{2,1,0:T(8,128)S(1)}, u32[]{:S(2)}, u32[]{:S(2)}) collective-permute-start(f32[2,32,1]{2,1,0:T(8,128)S(1)} %get-tuple-element.70), channel_id=1, source_target_pairs={{1,0},{2,1},{3,2},{0,3},{5,4},{6,5},{7,6},{4,7},{9,8},{10,9},{11,1... | collective-permute-start | bytes 776 | tf_op jit(solution)/shard_map/ppermute | solution.py:21
  117.7 5.9 %collective-permute-start.47 = (f32[2,32,1]{2,1,0:T(8,128)S(1)}, f32[2,32,1]{2,1,0:T(8,128)S(1)}, u32[]{:S(2)}, u32[]{:S(2)}) collective-permute-start(f32[2,32,1]{2,1,0:T(8,128)S(1)} %get-tuple-element.69), channel_id=1, source_target_pairs={{0,1},{1,2},{2,3},{3,0},{4,5},{5,6},{6,7},{7,4},{8,9},{9,10},{10,1... | collective-permute-start | bytes 776 | tf_op jit(solution)/shard_map/ppermute | solution.py:20
  117.7 5.9 %collective-permute-start.46 = (f32[1,32,128]{2,1,0:T(8,128)S(1)}, f32[1,32,128]{2,1,0:T(8,128)S(1)}, u32[]{:S(2)}, u32[]{:S(2)}) collective-permute-start(f32[1,32,128]{2,1,0:T(8,128)S(1)} %get-tuple-element.68), channel_id=1, source_target_pairs={{4,0},{8,4},{12,8},{16,12},{20,16},{24,20},{28,24},{5,1},{9,5},{13... | collective-permute-start | bytes 49160 | tf_op jit(solution)/shard_map/ppermute | solution.py:21
  120.2 6.5 %collective-permute-start.45 = (f32[1,32,128]{2,1,0:T(8,128)S(1)}, f32[1,32,128]{2,1,0:T(8,128)S(1)}, u32[]{:S(2)}, u32[]{:S(2)}) collective-permute-start(f32[1,32,128]{2,1,0:T(8,128)S(1)} %get-tuple-element.67), channel_id=1, source_target_pairs={{0,4},{4,8},{8,12},{12,16},{16,20},{20,24},{24,28},{1,5},{5,9},{9,... | collective-permute-start | bytes 49160 | tf_op jit(solution)/shard_map/ppermute | solution.py:20
  127.0 6.4 %collective-permute-start.52 = (f32[2,32,1]{2,1,0:T(8,128)S(1)}, f32[2,32,1]{2,1,0:T(8,128)S(1)}, u32[]{:S(2)}, u32[]{:S(2)}) collective-permute-start(f32[2,32,1]{2,1,0:T(8,128)S(1)} %get-tuple-element.64), channel_id=1, source_target_pairs={{1,0},{2,1},{3,2},{0,3},{5,4},{6,5},{7,6},{4,7},{9,8},{10,9},{11,1... | collective-permute-start | bytes 776 | tf_op jit(solution)/shard_map/ppermute | solution.py:21
  127.5 5.9 %collective-permute-start.51 = (f32[2,32,1]{2,1,0:T(8,128)S(1)}, f32[2,32,1]{2,1,0:T(8,128)S(1)}, u32[]{:S(2)}, u32[]{:S(2)}) collective-permute-start(f32[2,32,1]{2,1,0:T(8,128)S(1)} %get-tuple-element.63), channel_id=1, source_target_pairs={{0,1},{1,2},{2,3},{3,0},{4,5},{5,6},{6,7},{7,4},{8,9},{9,10},{10,1... | collective-permute-start | bytes 776 | tf_op jit(solution)/shard_map/ppermute | solution.py:20
  127.5 5.9 %collective-permute-start.50 = (f32[1,32,128]{2,1,0:T(8,128)S(1)}, f32[1,32,128]{2,1,0:T(8,128)S(1)}, u32[]{:S(2)}, u32[]{:S(2)}) collective-permute-start(f32[1,32,128]{2,1,0:T(8,128)S(1)} %get-tuple-element.62), channel_id=1, source_target_pairs={{4,0},{8,4},{12,8},{16,12},{20,16},{24,20},{28,24},{5,1},{9,5},{13... | collective-permute-start | bytes 49160 | tf_op jit(solution)/shard_map/ppermute | solution.py:21
  129.5 6.5 %collective-permute-start.49 = (f32[1,32,128]{2,1,0:T(8,128)S(1)}, f32[1,32,128]{2,1,0:T(8,128)S(1)}, u32[]{:S(2)}, u32[]{:S(2)}) collective-permute-start(f32[1,32,128]{2,1,0:T(8,128)S(1)} %get-tuple-element.61), channel_id=1, source_target_pairs={{0,4},{4,8},{8,12},{12,16},{16,20},{20,24},{24,28},{1,5},{5,9},{9,... | collective-permute-start | bytes 49160 | tf_op jit(solution)/shard_map/ppermute | solution.py:20
  136.8 6.5 %collective-permute-start.56 = (f32[4,64,1]{2,1,0:T(8,128)S(1)}, f32[4,64,1]{2,1,0:T(8,128)S(1)}, u32[]{:S(2)}, u32[]{:S(2)}) collective-permute-start(f32[4,64,1]{2,1,0:T(8,128)S(1)} %get-tuple-element.32), channel_id=1, source_target_pairs={{1,0},{2,1},{3,2},{0,3},{5,4},{6,5},{7,6},{4,7},{9,8},{10,9},{11,1... | collective-permute-start | bytes 3080 | tf_op jit(solution)/shard_map/ppermute | solution.py:21
  137.4 5.9 %collective-permute-start.55 = (f32[4,64,1]{2,1,0:T(8,128)S(1)}, f32[4,64,1]{2,1,0:T(8,128)S(1)}, u32[]{:S(2)}, u32[]{:S(2)}) collective-permute-start(f32[4,64,1]{2,1,0:T(8,128)S(1)} %get-tuple-element.31), channel_id=1, source_target_pairs={{0,1},{1,2},{2,3},{3,0},{4,5},{5,6},{6,7},{7,4},{8,9},{9,10},{10,1... | collective-permute-start | bytes 3080 | tf_op jit(solution)/shard_map/ppermute | solution.py:20
  137.4 6.3 %collective-permute-start.54 = (f32[1,64,256]{2,1,0:T(8,128)S(1)}, f32[1,64,256]{2,1,0:T(8,128)S(1)}, u32[]{:S(2)}, u32[]{:S(2)}) collective-permute-start(f32[1,64,256]{2,1,0:T(8,128)S(1)} %get-tuple-element.30), channel_id=1, source_target_pairs={{4,0},{8,4},{12,8},{16,12},{20,16},{24,20},{28,24},{5,1},{9,5},{13... | collective-permute-start | bytes 196616 | tf_op jit(solution)/shard_map/ppermute | solution.py:21
  139.3 7.2 %collective-permute-start.53 = (f32[1,64,256]{2,1,0:T(8,128)S(1)}, f32[1,64,256]{2,1,0:T(8,128)S(1)}, u32[]{:S(2)}, u32[]{:S(2)}) collective-permute-start(f32[1,64,256]{2,1,0:T(8,128)S(1)} %get-tuple-element.29), channel_id=1, source_target_pairs={{0,4},{4,8},{8,12},{12,16},{16,20},{20,24},{24,28},{1,5},{5,9},{9,... | collective-permute-start | bytes 196616 | tf_op jit(solution)/shard_map/ppermute | solution.py:20
  147.1 6.6 %collective-permute-start.60 = (f32[4,64,1]{2,1,0:T(8,128)S(1)}, f32[4,64,1]{2,1,0:T(8,128)S(1)}, u32[]{:S(2)}, u32[]{:S(2)}) collective-permute-start(f32[4,64,1]{2,1,0:T(8,128)S(1)} %get-tuple-element.26), channel_id=1, source_target_pairs={{1,0},{2,1},{3,2},{0,3},{5,4},{6,5},{7,6},{4,7},{9,8},{10,9},{11,1... | collective-permute-start | bytes 3080 | tf_op jit(solution)/shard_map/ppermute | solution.py:21
  147.8 5.9 %collective-permute-start.59 = (f32[4,64,1]{2,1,0:T(8,128)S(1)}, f32[4,64,1]{2,1,0:T(8,128)S(1)}, u32[]{:S(2)}, u32[]{:S(2)}) collective-permute-start(f32[4,64,1]{2,1,0:T(8,128)S(1)} %get-tuple-element.25), channel_id=1, source_target_pairs={{0,1},{1,2},{2,3},{3,0},{4,5},{5,6},{6,7},{7,4},{8,9},{9,10},{10,1... | collective-permute-start | bytes 3080 | tf_op jit(solution)/shard_map/ppermute | solution.py:20
  147.8 6.7 %collective-permute-start.58 = (f32[1,64,256]{2,1,0:T(8,128)S(1)}, f32[1,64,256]{2,1,0:T(8,128)S(1)}, u32[]{:S(2)}, u32[]{:S(2)}) collective-permute-start(f32[1,64,256]{2,1,0:T(8,128)S(1)} %get-tuple-element.24), channel_id=1, source_target_pairs={{4,0},{8,4},{12,8},{16,12},{20,16},{24,20},{28,24},{5,1},{9,5},{13... | collective-permute-start | bytes 196616 | tf_op jit(solution)/shard_map/ppermute | solution.py:21
  149.7 7.6 %collective-permute-start.57 = (f32[1,64,256]{2,1,0:T(8,128)S(1)}, f32[1,64,256]{2,1,0:T(8,128)S(1)}, u32[]{:S(2)}, u32[]{:S(2)}) collective-permute-start(f32[1,64,256]{2,1,0:T(8,128)S(1)} %get-tuple-element.23), channel_id=1, source_target_pairs={{0,4},{4,8},{8,12},{12,16},{16,20},{20,24},{24,28},{1,5},{5,9},{9,... | collective-permute-start | bytes 196616 | tf_op jit(solution)/shard_map/ppermute | solution.py:20
  157.8 6.5 %collective-permute-start.64 = (f32[4,64,1]{2,1,0:T(8,128)S(1)}, f32[4,64,1]{2,1,0:T(8,128)S(1)}, u32[]{:S(2)}, u32[]{:S(2)}) collective-permute-start(f32[4,64,1]{2,1,0:T(8,128)S(1)} %get-tuple-element.20), channel_id=1, source_target_pairs={{1,0},{2,1},{3,2},{0,3},{5,4},{6,5},{7,6},{4,7},{9,8},{10,9},{11,1... | collective-permute-start | bytes 3080 | tf_op jit(solution)/shard_map/ppermute | solution.py:21
  158.3 6.0 %collective-permute-start.63 = (f32[4,64,1]{2,1,0:T(8,128)S(1)}, f32[4,64,1]{2,1,0:T(8,128)S(1)}, u32[]{:S(2)}, u32[]{:S(2)}) collective-permute-start(f32[4,64,1]{2,1,0:T(8,128)S(1)} %get-tuple-element.19), channel_id=1, source_target_pairs={{0,1},{1,2},{2,3},{3,0},{4,5},{5,6},{6,7},{7,4},{8,9},{9,10},{10,1... | collective-permute-start | bytes 3080 | tf_op jit(solution)/shard_map/ppermute | solution.py:20
  158.4 6.7 %collective-permute-start.62 = (f32[1,64,256]{2,1,0:T(8,128)S(1)}, f32[1,64,256]{2,1,0:T(8,128)S(1)}, u32[]{:S(2)}, u32[]{:S(2)}) collective-permute-start(f32[1,64,256]{2,1,0:T(8,128)S(1)} %get-tuple-element.18), channel_id=1, source_target_pairs={{4,0},{8,4},{12,8},{16,12},{20,16},{24,20},{28,24},{5,1},{9,5},{13... | collective-permute-start | bytes 196616 | tf_op jit(solution)/shard_map/ppermute | solution.py:21
  160.3 7.6 %collective-permute-start.61 = (f32[1,64,256]{2,1,0:T(8,128)S(1)}, f32[1,64,256]{2,1,0:T(8,128)S(1)}, u32[]{:S(2)}, u32[]{:S(2)}) collective-permute-start(f32[1,64,256]{2,1,0:T(8,128)S(1)} %get-tuple-element.17), channel_id=1, source_target_pairs={{0,4},{4,8},{8,12},{12,16},{16,20},{20,24},{24,28},{1,5},{5,9},{9,... | collective-permute-start | bytes 196616 | tf_op jit(solution)/shard_map/ppermute | solution.py:20
  (6 other events, 25.9 us)

commit v2 on v1

--- a/solution.py
+++ b/solution.py
@@ -97,7 +97,7 @@
     return (v_down, v_up, wrapped[:, :, :-2], wrapped[:, :, 2:])
 
 
-def make_weights(coef_alt, coef_inc, coef_raan, factor, alt_pair):
+def make_weights(coef_alt, coef_inc, coef_raan, factor, alt_pair, whole=False):
     alt_down, alt_up = alt_pair(coef_alt)
     w_alt_lo = factor * 0.5 * (coef_alt + alt_down)
     w_alt_hi = factor * 0.5 * (coef_alt + alt_up)
@@ -105,9 +105,13 @@
     zero_inc = jnp.zeros_like(coef_inc[:, :1])
     w_inc_lo = jnp.concatenate([zero_inc, inner_faces], 1)
     w_inc_hi = jnp.concatenate([inner_faces, zero_inc], 1)
-    wrapped = raan_ext(coef_raan)
-    w_raan_lo = factor * 0.5 * (coef_raan + wrapped[:, :, :-2])
-    w_raan_hi = factor * 0.5 * (coef_raan + wrapped[:, :, 2:])
+    if whole:
+        raan_lo, raan_hi = jnp.roll(coef_raan, 1, 2), jnp.roll(coef_raan, -1, 2)
+    else:
+        wrapped = raan_ext(coef_raan)
+        raan_lo, raan_hi = wrapped[:, :, :-2], wrapped[:, :, 2:]
+    w_raan_lo = factor * 0.5 * (coef_raan + raan_lo)
+    w_raan_hi = factor * 0.5 * (coef_raan + raan_hi)
     diagonal = 1.0 + (w_alt_lo + w_alt_hi + w_inc_lo + w_inc_hi + w_raan_lo + w_raan_hi)
     return (w_alt_lo, w_alt_hi, w_inc_lo, w_inc_hi, w_raan_lo, w_raan_hi, diagonal)
 
@@ -140,6 +144,33 @@
     return smooth(field, target, weights, near, COARSE_SWEEPS - 1)
 
 
+def gather_grid(stacked):
+    count, height, width, length = stacked.shape
+    alt_n, raan_n = lax.axis_size("alt"), lax.axis_size("raan")
+    every = lax.all_gather(stacked, ("alt", "raan"), axis=0, tiled=False)
+    every = every.reshape(alt_n, raan_n, count, height, width, length)
+    every = every.transpose(2, 0, 3, 4, 1, 5)
+    return every.reshape(count, alt_n * height, width, raan_n * length)
+
+
+def whole_weights(coef_alt, coef_inc, coef_raan, factor):
+    zero_alt = jnp.zeros_like(coef_alt[:1])
+    alt_down = jnp.concatenate([zero_alt, coef_alt[:-1]], 0)
+    alt_up = jnp.concatenate([coef_alt[1:], zero_alt], 0)
+    return make_weights(coef_alt, coef_inc, coef_raan, factor, lambda _: (alt_down, alt_up), whole=True)
+
+
+def whole_near(field):
+    zero_alt = jnp.zeros_like(field[:1])
+    v_down = jnp.concatenate([zero_alt, field[:-1]], 0)
+    v_up = jnp.concatenate([field[1:], zero_alt], 0)
+    return (v_down, v_up, jnp.roll(field, 1, 2), jnp.roll(field, -1, 2))
+
+
+def whole_apply(weights, field):
+    return apply_op(weights, field, whole_near)
+
+
 def shards(source, k_alt, k_inc, k_raan):
     weights_one = make_weights(k_alt, k_inc, k_raan, 1.0, plain_alt)
     coef_two = (coarsen(k_alt), coarsen(k_inc), coarsen(k_raan))
@@ -150,16 +181,18 @@
     correction = OMEGA * rhs_two / weights_two[6]
     correction = smooth(correction, rhs_two, weights_two, field_near, SWEEPS - 1)
     rhs_three = coarsen(rhs_two - apply_op(weights_two, correction, field_near))
-    height = rhs_three.shape[0]
-    parity = lax.axis_index("alt") % 2
-    own_part = jnp.stack((rhs_three, coef_three[0], coef_three[1], coef_three[2]))
-    theirs = from_partner(own_part, "alt", 0)
-    low_half = jnp.where(parity == 0, own_part, theirs)
-    high_half = jnp.where(parity == 0, theirs, own_part)
-    pair_block = jnp.concatenate([low_half, high_half], axis=1)
-    weights_three = make_weights(pair_block[1], pair_block[2], pair_block[3], 0.0625, fold_alt)
-    pair_result = coarse_solve(pair_block[0], weights_three, fold_near)
-    coarse_part = lax.dynamic_slice_in_dim(pair_result, parity * height, height, 0)
+    whole_coef = gather_grid(jnp.stack(coef_three))
+    weights_three = whole_weights(whole_coef[0], whole_coef[1], whole_coef[2], 0.0625)
+    whole_rhs = gather_grid(rhs_three[None])[0]
+    whole_part = OMEGA * whole_rhs / weights_three[6]
+    for _ in range(COARSE_SWEEPS - 1):
+        whole_part = whole_part + OMEGA * (whole_rhs - whole_apply(weights_three, whole_part)) / weights_three[6]
+    height, width, length = rhs_three.shape
+    coarse_part = lax.dynamic_slice(
+        whole_part,
+        (lax.axis_index("alt") * height, 0, lax.axis_index("raan") * length),
+        (height, width, length),
+    )
     correction = correction + refine(coarse_part)
     correction = smooth(correction, rhs_two, weights_two, field_near, SWEEPS)
     density = density + refine(correction)

time: 172 us -> 222 us (1.29)
  blocking collectives: 0 us -> 69 us
  starting transfers between devices: 114 us -> 85.6 us
  local copies, waits for them, and re-layouts: 3.54 us -> 11.1 us
    all_gather x0 -> x2, blocking collectives: none -> 69 us  [gather_grid(): every = lax.all_gather(stacked, ('alt', 'raan'), axis=0, tiled=False)]
    ppermute x9 -> x0, starting transfers between devices: 24.8 us -> none  [the longest x8 23.6 us: shifted(): return lax.ppermute(block, axis, route)]
    ppermute x28 -> x24, waiting for transfers between devices: 25.4 us -> 35.7 us  [with_halo(): before = lax.ppermute(last, axis, up)]
    ppermute x9 -> x0, waiting for transfers between devices: 8.36 us -> none  [the longest x8 5.63 us: shifted(): return lax.ppermute(block, axis, route)]
    ppermute x28 -> x24, starting transfers between devices: 44.9 us -> 39.2 us  [with_halo(): before = lax.ppermute(last, axis, up)]
    unnamed x10 -> x72, local copies, waits for them, and re-layouts: 0.89 us -> 4.33 us
    ppermute x28 -> x24, starting transfers between devices: 44.6 us -> 46.4 us  [with_halo(): after = lax.ppermute(leading, axis, down)]
    ppermute x28 -> x24, waiting for transfers between devices: 6.44 us -> 5.94 us  [with_halo(): after = lax.ppermute(leading, axis, down)]
  transfers between devices with their start and end apart: 65 -> 48, of which waited for: 19 -> 17; matrix products, arithmetic and copies ran while one was open for 3% -> 2% of each run, Pallas kernels for 0% -> 0%
where the time goes in v2:
time: 222 us; the launch traced here: 220 us
  starting transfers between devices  85.6 us (39%)
  blocking collectives  69 us (31%)
  waiting for transfers between devices  41.7 us (19%)
  local copies, waits for them, and re-layouts  11.1 us (5%)
  matrix products  5.74 us (3%)
  other arithmetic  5.18 us (2%)
    all_gather x2, blocking collectives, gather_grid(): every = lax.all_gather(stacked, ('alt', 'raan'), axis=0, tiled=False)  69 us
    ppermute x24, starting transfers between devices, with_halo(): after = lax.ppermute(leading, axis, down)  46.4 us
    ppermute x24, starting transfers between devices, with_halo(): before = lax.ppermute(last, axis, up)  39.2 us
    ppermute x24, waiting for transfers between devices, with_halo(): before = lax.ppermute(last, axis, up)  35.7 us
    ppermute x24, waiting for transfers between devices, with_halo(): after = lax.ppermute(leading, axis, down)  5.94 us
  transfers between devices with their start and end apart: 48, of which 17 were waited for; matrix products, arithmetic and copies ran while one was open for 2% of the time, Pallas kernels for 0%

profile of v2, /device:TPU:8, one launch (start us, length us, event | category | flops | bytes accessed | tf_op | source)
XLA Modules:
  0.0 220.1 jit_solution(10223915854470946775)
XLA Ops:
  0.6 1.1 fusion.298
  1.8 1.0 collective-permute-start.7
  2.8 3.4 %collective-permute-start.5 = (f32[1,64,256]{2,1,0:T(8,128)S(1)}, f32[1,64,256]{2,1,0:T(8,128)S(1)}, u32[]{:S(2)}, u32[]{:S(2)}) collective-permute-start(f32[1,64,256]{2,1,0:T(8,128)S(1)} %get-tuple-element.56), channel_id=1, source_target_pairs={{4,0},{8,4},{12,8},{16,12},{20,16},{24,20},{28,24},{5,1},{9,5},{13... | collective-permute-start | bytes 196616 | tf_op jit(solution)/shard_map/ppermute | solution.py:21
  6.2 2.5 %collective-permute-start.4 = (f32[1,64,256]{2,1,0:T(8,128)S(1)}, f32[1,64,256]{2,1,0:T(8,128)S(1)}, u32[]{:S(2)}, u32[]{:S(2)}) collective-permute-start(f32[1,64,256]{2,1,0:T(8,128)S(1)} %get-tuple-element.55), channel_id=1, source_target_pairs={{0,4},{4,8},{8,12},{12,16},{16,20},{20,24},{24,28},{1,5},{5,9},{9,... | collective-permute-start | bytes 196616 | tf_op jit(solution)/shard_map/ppermute | solution.py:20
  8.8 4.3 %collective-permute-start = (f32[1,64,256]{2,1,0:T(8,128)S(1)}, f32[1,64,256]{2,1,0:T(8,128)S(1)}, u32[]{:S(2)}, u32[]{:S(2)}) collective-permute-start(f32[1,64,256]{2,1,0:T(8,128)S(1)} %get-tuple-element.52), channel_id=1, source_target_pairs={{0,4},{4,8},{8,12},{12,16},{16,20},{20,24},{24,28},{1,5},{5,9},{9,... | collective-permute-start | bytes 196616 | tf_op jit(solution)/shard_map/ppermute | solution.py:20
  13.4 0.8 copy-done.4
  16.4 2.4 %collective-permute-start.1 = (f32[1,64,256]{2,1,0:T(8,128)S(1)}, f32[1,64,256]{2,1,0:T(8,128)S(1)}, u32[]{:S(2)}, u32[]{:S(2)}) collective-permute-start(f32[1,64,256]{2,1,0:T(8,128)S(1)} %get-tuple-element.51), channel_id=1, source_target_pairs={{4,0},{8,4},{12,8},{16,12},{20,16},{24,20},{28,24},{5,1},{9,5},{13... | collective-permute-start | bytes 196616 | tf_op jit(solution)/shard_map/ppermute | solution.py:21
  19.1 4.1 %collective-permute-done.2 = f32[4,64,1]{2,1,0:T(8,128)S(1)} collective-permute-done((f32[4,64,1]{2,1,0:T(8,128)S(1)}, f32[4,64,1]{2,1,0:T(8,128)S(1)}, u32[]{:S(2)}, u32[]{:S(2)}) %collective-permute-start.2) | collective-permute-done | bytes 1056 | tf_op jit(solution)/shard_map/ppermute | solution.py:20
  23.2 2.5 %collective-permute-done.3 = f32[4,64,1]{2,1,0:T(8,128)S(1)} collective-permute-done((f32[4,64,1]{2,1,0:T(8,128)S(1)}, f32[4,64,1]{2,1,0:T(8,128)S(1)}, u32[]{:S(2)}, u32[]{:S(2)}) %collective-permute-start.3) | collective-permute-done | bytes 1056 | tf_op jit(solution)/shard_map/ppermute | solution.py:21
  25.8 3.4 %collective-permute-start.16 = (f32[1,32,128]{2,1,0:T(8,128)S(1)}, f32[1,32,128]{2,1,0:T(8,128)S(1)}, u32[]{:S(2)}, u32[]{:S(2)}) collective-permute-start(f32[1,32,128]{2,1,0:T(8,128)S(1)} %get-tuple-element.116), channel_id=1, source_target_pairs={{0,4},{4,8},{8,12},{12,16},{16,20},{20,24},{24,28},{1,5},{5,9},{9,... | collective-permute-start | bytes 49160 | tf_op jit(solution)/shard_map/ppermute | solution.py:20
  29.8 1.6 collective-permute-start.11
  31.5 3.3 %collective-permute-start.9 = (f32[1,64,256]{2,1,0:T(8,128)S(1)}, f32[1,64,256]{2,1,0:T(8,128)S(1)}, u32[]{:S(2)}, u32[]{:S(2)}) collective-permute-start(f32[1,64,256]{2,1,0:T(8,128)S(1)} %get-tuple-element.46), channel_id=1, source_target_pairs={{4,0},{8,4},{12,8},{16,12},{20,16},{24,20},{28,24},{5,1},{9,5},{13... | collective-permute-start | bytes 196616 | tf_op jit(solution)/shard_map/ppermute | solution.py:21
  34.8 2.5 %collective-permute-start.8 = (f32[1,64,256]{2,1,0:T(8,128)S(1)}, f32[1,64,256]{2,1,0:T(8,128)S(1)}, u32[]{:S(2)}, u32[]{:S(2)}) collective-permute-start(f32[1,64,256]{2,1,0:T(8,128)S(1)} %get-tuple-element.45), channel_id=1, source_target_pairs={{0,4},{4,8},{8,12},{12,16},{16,20},{20,24},{24,28},{1,5},{5,9},{9,... | collective-permute-start | bytes 196616 | tf_op jit(solution)/shard_map/ppermute | solution.py:20
  37.4 0.9 collective-permute-done.9
  38.2 4.1 %collective-permute-done.8 = f32[1,64,256]{2,1,0:T(8,128)S(1)} collective-permute-done((f32[1,64,256]{2,1,0:T(8,128)S(1)}, f32[1,64,256]{2,1,0:T(8,128)S(1)}, u32[]{:S(2)}, u32[]{:S(2)}) %collective-permute-start.8) | collective-permute-done | bytes 65568 | tf_op jit(solution)/shard_map/ppermute | solution.py:20
  42.8 0.8 collective-permute-start.15
  43.6 1.9 collective-permute-start.13
  45.6 3.9 %collective-permute-start.12 = (f32[1,64,256]{2,1,0:T(8,128)S(1)}, f32[1,64,256]{2,1,0:T(8,128)S(1)}, u32[]{:S(2)}, u32[]{:S(2)}) collective-permute-start(f32[1,64,256]{2,1,0:T(8,128)S(1)} %get-tuple-element.37), channel_id=1, source_target_pairs={{0,4},{4,8},{8,12},{12,16},{16,20},{20,24},{24,28},{1,5},{5,9},{9,... | collective-permute-start | bytes 196616 | tf_op jit(solution)/shard_map/ppermute | solution.py:20
  49.5 2.8 %collective-permute-start.17 = (f32[1,32,128]{2,1,0:T(8,128)S(1)}, f32[1,32,128]{2,1,0:T(8,128)S(1)}, u32[]{:S(2)}, u32[]{:S(2)}) collective-permute-start(f32[1,32,128]{2,1,0:T(8,128)S(1)} %get-tuple-element.115), channel_id=1, source_target_pairs={{4,0},{8,4},{12,8},{16,12},{20,16},{24,20},{28,24},{5,1},{9,5},{13... | collective-permute-start | bytes 49160 | tf_op jit(solution)/shard_map/ppermute | solution.py:21
  52.8 1.4 collective-permute-start.19
  54.9 0.9 collective-permute-done.18
  55.8 0.8 bitcast_divide_fusion
  56.6 0.7 fusion.324
  57.3 0.6 fusion.323
  59.0 36.6 %all-gather.1 = f32[96,1,16,64]{3,2,1,0:T(8,128)S(1)} all-gather(f32[3,1,16,64]{3,2,1,0:T(8,128)S(1)} %pad_maximum_fusion.48), channel_id=3, replica_groups=mesh['alt'=8,'raan'=4] {'alt','raan'}, dimensions={0}, use_global_device_ids=true | all-gather | bytes 405504 | tf_op jit(solution)/shard_map/all_gather | solution.py:150
  96.4 0.7 fusion.312
  97.1 6.1 %collective-permute-start.21 = (f32[1,32,128]{2,1,0:T(8,128)}, f32[1,32,128]{2,1,0:T(8,128)}, u32[]{:S(2)}, u32[]{:S(2)}) collective-permute-start(f32[1,32,128]{2,1,0:T(8,128)} %get-tuple-element.110), channel_id=1, source_target_pairs={{4,0},{8,4},{12,8},{16,12},{20,16},{24,20},{28,24},{5,1},{9,5},{13... | collective-permute-start | bytes 49160 | tf_op jit(solution)/shard_map/ppermute | solution.py:21
  103.2 1.9 collective-permute-start.20
  105.4 0.7 copy-done.11
  106.1 0.5 collective-permute-start.22
  107.2 0.5 collective-permute-done.23
  107.7 2.0 collective-permute-done.22
  109.7 1.6 collective-permute-done.20
  111.3 0.9 fusion.173
  112.3 0.5 collective-permute-start.26
  112.8 4.5 %collective-permute-start.25 = (f32[1,32,128]{2,1,0:T(8,128)S(1)}, f32[1,32,128]{2,1,0:T(8,128)S(1)}, u32[]{:S(2)}, u32[]{:S(2)}) collective-permute-start(f32[1,32,128]{2,1,0:T(8,128)S(1)} %get-tuple-element.104), channel_id=1, source_target_pairs={{4,0},{8,4},{12,8},{16,12},{20,16},{24,20},{28,24},{5,1},{9,5},{13... | collective-permute-start | bytes 49160 | tf_op jit(solution)/shard_map/ppermute | solution.py:21
  117.3 1.9 collective-permute-start.24
  119.2 4.6 %collective-permute-done.24 = f32[1,32,128]{2,1,0:T(8,128)S(1)} collective-permute-done((f32[1,32,128]{2,1,0:T(8,128)S(1)}, f32[1,32,128]{2,1,0:T(8,128)S(1)}, u32[]{:S(2)}, u32[]{:S(2)}) %collective-permute-start.24) | collective-permute-done | bytes 16416 | tf_op jit(solution)/shard_map/ppermute | solution.py:20
  123.9 0.6 copy-done.25
  125.4 32.3 %all-gather = f32[512,64]{1,0:T(8,128)S(1)} all-gather(f32[16,64]{1,0:T(8,128)S(1)} %convolution_multiply_fusion.6), channel_id=2, replica_groups=mesh['alt'=8,'raan'=4] {'alt','raan'}, dimensions={0}, use_global_device_ids=true | all-gather | bytes 135168 | tf_op jit(solution)/shard_map/all_gather | solution.py:150
  158.1 0.6 copy-done.8
  161.4 5.6 %collective-permute-start.29 = (f32[1,32,128]{2,1,0:T(8,128)S(1)}, f32[1,32,128]{2,1,0:T(8,128)S(1)}, u32[]{:S(2)}, u32[]{:S(2)}) collective-permute-start(f32[1,32,128]{2,1,0:T(8,128)S(1)} %get-tuple-element.96), channel_id=1, source_target_pairs={{4,0},{8,4},{12,8},{16,12},{20,16},{24,20},{28,24},{5,1},{9,5},{13... | collective-permute-start | bytes 49160 | tf_op jit(solution)/shard_map/ppermute | solution.py:21
  167.1 1.9 collective-permute-start.28
  169.0 5.7 %collective-permute-done.28 = f32[1,32,128]{2,1,0:T(8,128)S(1)} collective-permute-done((f32[1,32,128]{2,1,0:T(8,128)S(1)}, f32[1,32,128]{2,1,0:T(8,128)S(1)}, u32[]{:S(2)}, u32[]{:S(2)}) %collective-permute-start.28) | collective-permute-done | bytes 16416 | tf_op jit(solution)/shard_map/ppermute | solution.py:20
  174.9 1.0 collective-permute-start.35
  176.0 3.5 %collective-permute-start.33 = (f32[1,32,128]{2,1,0:T(8,128)S(1)}, f32[1,32,128]{2,1,0:T(8,128)S(1)}, u32[]{:S(2)}, u32[]{:S(2)}) collective-permute-start(f32[1,32,128]{2,1,0:T(8,128)S(1)} %get-tuple-element.90), channel_id=1, source_target_pairs={{4,0},{8,4},{12,8},{16,12},{20,16},{24,20},{28,24},{5,1},{9,5},{13... | collective-permute-start | bytes 49160 | tf_op jit(solution)/shard_map/ppermute | solution.py:21
  179.5 2.3 %collective-permute-start.32 = (f32[1,32,128]{2,1,0:T(8,128)S(1)}, f32[1,32,128]{2,1,0:T(8,128)S(1)}, u32[]{:S(2)}, u32[]{:S(2)}) collective-permute-start(f32[1,32,128]{2,1,0:T(8,128)S(1)} %get-tuple-element.89), channel_id=1, source_target_pairs={{0,4},{4,8},{8,12},{12,16},{16,20},{20,24},{24,28},{1,5},{5,9},{9,... | collective-permute-start | bytes 49160 | tf_op jit(solution)/shard_map/ppermute | solution.py:20
  181.9 4.2 %collective-permute-done.32 = f32[1,32,128]{2,1,0:T(8,128)S(1)} collective-permute-done((f32[1,32,128]{2,1,0:T(8,128)S(1)}, f32[1,32,128]{2,1,0:T(8,128)S(1)}, u32[]{:S(2)}, u32[]{:S(2)}) %collective-permute-start.32) | collective-permute-done | bytes 16416 | tf_op jit(solution)/shard_map/ppermute | solution.py:20
  186.1 0.7 copy-done.13
  187.9 0.5 collective-permute-start.38
  188.4 1.9 collective-permute-start.37
  190.3 3.9 %collective-permute-start.36 = (f32[1,64,256]{2,1,0:T(8,128)S(1)}, f32[1,64,256]{2,1,0:T(8,128)S(1)}, u32[]{:S(2)}, u32[]{:S(2)}) collective-permute-start(f32[1,64,256]{2,1,0:T(8,128)S(1)} %get-tuple-element.33), channel_id=1, source_target_pairs={{0,4},{4,8},{8,12},{12,16},{16,20},{20,24},{24,28},{1,5},{5,9},{9,... | collective-permute-start | bytes 196616 | tf_op jit(solution)/shard_map/ppermute | solution.py:20
  194.3 0.6 collective-permute-done.37
  195.0 2.8 %collective-permute-done.36 = f32[1,64,256]{2,1,0:T(8,128)S(1)} collective-permute-done((f32[1,64,256]{2,1,0:T(8,128)S(1)}, f32[1,64,256]{2,1,0:T(8,128)S(1)}, u32[]{:S(2)}, u32[]{:S(2)}) %collective-permute-start.36) | collective-permute-done | bytes 65568 | tf_op jit(solution)/shard_map/ppermute | solution.py:20
  198.9 1.9 collective-permute-start.41
  200.8 3.9 %collective-permute-start.40 = (f32[1,64,256]{2,1,0:T(8,128)S(1)}, f32[1,64,256]{2,1,0:T(8,128)S(1)}, u32[]{:S(2)}, u32[]{:S(2)}) collective-permute-start(f32[1,64,256]{2,1,0:T(8,128)S(1)} %get-tuple-element.27), channel_id=1, source_target_pairs={{0,4},{4,8},{8,12},{12,16},{16,20},{20,24},{24,28},{1,5},{5,9},{9,... | collective-permute-start | bytes 196616 | tf_op jit(solution)/shard_map/ppermute | solution.py:20
  204.8 0.6 collective-permute-done.41
  205.4 2.8 %collective-permute-done.40 = f32[1,64,256]{2,1,0:T(8,128)S(1)} collective-permute-done((f32[1,64,256]{2,1,0:T(8,128)S(1)}, f32[1,64,256]{2,1,0:T(8,128)S(1)}, u32[]{:S(2)}, u32[]{:S(2)}) %collective-permute-start.40) | collective-permute-done | bytes 65568 | tf_op jit(solution)/shard_map/ppermute | solution.py:20
  208.8 0.7 collective-permute-start.47
  209.5 1.9 collective-permute-start.45
  211.4 3.9 %collective-permute-start.44 = (f32[1,64,256]{2,1,0:T(8,128)S(1)}, f32[1,64,256]{2,1,0:T(8,128)S(1)}, u32[]{:S(2)}, u32[]{:S(2)}) collective-permute-start(f32[1,64,256]{2,1,0:T(8,128)S(1)} %get-tuple-element.21), channel_id=1, source_target_pairs={{0,4},{4,8},{8,12},{12,16},{16,20},{20,24},{24,28},{1,5},{5,9},{9,... | collective-permute-start | bytes 196616 | tf_op jit(solution)/shard_map/ppermute | solution.py:20
  215.4 0.7 collective-permute-done.45
  216.1 2.9 %collective-permute-done.44 = f32[1,64,256]{2,1,0:T(8,128)S(1)} collective-permute-done((f32[1,64,256]{2,1,0:T(8,128)S(1)}, f32[1,64,256]{2,1,0:T(8,128)S(1)}, u32[]{:S(2)}, u32[]{:S(2)}) %collective-permute-start.44) | collective-permute-done | bytes 65568 | tf_op jit(solution)/shard_map/ppermute | solution.py:20
  219.0 1.1 fusion.10
  (215 shorter events, 14.5 us)
Async XLA Ops:
  1.7 7.0 %copy-start.1 = (f32[4,64,256]{2,1,0:T(8,128)S(1)}, f32[4,64,256]{2,1,0:T(8,128)}, u32[]{:S(2)}) copy-start(f32[4,64,256]{2,1,0:T(8,128)} %param.5) | copy-start | bytes 786436
  1.8 14.6 %collective-permute-start.7 = (f32[4,64,1]{2,1,0:T(8,128)S(1)}, f32[4,64,1]{2,1,0:T(8,128)S(1)}, u32[]{:S(2)}, u32[]{:S(2)}) collective-permute-start(f32[4,64,1]{2,1,0:T(8,128)S(1)} %get-tuple-element.58), channel_id=1, source_target_pairs={{1,0},{2,1},{3,2},{0,3},{5,4},{6,5},{7,6},{4,7},{9,8},{10,9},{11,1... | collective-permute-start | bytes 3080 | tf_op jit(solution)/shard_map/ppermute | solution.py:21
  2.7 10.4 %copy-start.3 = (f32[4,64,256]{2,1,0:T(8,128)S(1)}, f32[4,64,256]{2,1,0:T(8,128)}, u32[]{:S(2)}) copy-start(f32[4,64,256]{2,1,0:T(8,128)} %param.6) | copy-start | bytes 786436
  2.7 16.0 %collective-permute-start.6 = (f32[4,64,1]{2,1,0:T(8,128)S(1)}, f32[4,64,1]{2,1,0:T(8,128)S(1)}, u32[]{:S(2)}, u32[]{:S(2)}) collective-permute-start(f32[4,64,1]{2,1,0:T(8,128)S(1)} %get-tuple-element.57), channel_id=1, source_target_pairs={{0,1},{1,2},{2,3},{3,0},{4,5},{5,6},{6,7},{7,4},{8,9},{9,10},{10,1... | collective-permute-start | bytes 3080 | tf_op jit(solution)/shard_map/ppermute | solution.py:20
  2.8 26.4 %collective-permute-start.5 = (f32[1,64,256]{2,1,0:T(8,128)S(1)}, f32[1,64,256]{2,1,0:T(8,128)S(1)}, u32[]{:S(2)}, u32[]{:S(2)}) collective-permute-start(f32[1,64,256]{2,1,0:T(8,128)S(1)} %get-tuple-element.56), channel_id=1, source_target_pairs={{4,0},{8,4},{12,8},{16,12},{20,16},{24,20},{28,24},{5,1},{9,5},{13... | collective-permute-start | bytes 196616 | tf_op jit(solution)/shard_map/ppermute | solution.py:21
  6.2 23.0 %collective-permute-start.4 = (f32[1,64,256]{2,1,0:T(8,128)S(1)}, f32[1,64,256]{2,1,0:T(8,128)S(1)}, u32[]{:S(2)}, u32[]{:S(2)}) collective-permute-start(f32[1,64,256]{2,1,0:T(8,128)S(1)} %get-tuple-element.55), channel_id=1, source_target_pairs={{0,4},{4,8},{8,12},{12,16},{16,20},{20,24},{24,28},{1,5},{5,9},{9,... | collective-permute-start | bytes 196616 | tf_op jit(solution)/shard_map/ppermute | solution.py:20
  8.8 20.4 %collective-permute-start = (f32[1,64,256]{2,1,0:T(8,128)S(1)}, f32[1,64,256]{2,1,0:T(8,128)S(1)}, u32[]{:S(2)}, u32[]{:S(2)}) collective-permute-start(f32[1,64,256]{2,1,0:T(8,128)S(1)} %get-tuple-element.52), channel_id=1, source_target_pairs={{0,4},{4,8},{8,12},{12,16},{16,20},{20,24},{24,28},{1,5},{5,9},{9,... | collective-permute-start | bytes 196616 | tf_op jit(solution)/shard_map/ppermute | solution.py:20
  13.2 41.3 %copy-start.12 = (s32[256]{0:T(256)}, s32[256]{0:T(256)S(1)}, u32[]{:S(2)}) copy-start(s32[256]{0:T(256)S(1)} %get-tuple-element.121) | copy-start | bytes 3076
  13.3 41.3 %copy-start.14 = (s32[256]{0:T(256)}, s32[256]{0:T(256)S(1)}, u32[]{:S(2)}) copy-start(s32[256]{0:T(256)S(1)} %get-tuple-element.122) | copy-start | bytes 3076
  13.3 41.3 %copy-start.22 = (pred[256]{0:T(512)(128)(4,1)}, pred[256]{0:T(512)(128)(4,1)S(1)}, u32[]{:S(2)}) copy-start(pred[256]{0:T(512)(128)(4,1)S(1)} %compare_and_fusion.2) | copy-start | bytes 772
  13.3 42.5 %copy-start.16 = (s32[64]{0:T(128)}, s32[64]{0:T(128)S(1)}, u32[]{:S(2)}) copy-start(s32[64]{0:T(128)S(1)} %get-tuple-element.123) | copy-start | bytes 772
  13.3 42.5 %copy-start.18 = (s32[64]{0:T(128)}, s32[64]{0:T(128)S(1)}, u32[]{:S(2)}) copy-start(s32[64]{0:T(128)S(1)} %get-tuple-element.124) | copy-start | bytes 772
  13.3 42.5 %copy-start.20 = (pred[64]{0:T(512)(128)(4,1)}, pred[64]{0:T(512)(128)(4,1)S(1)}, u32[]{:S(2)}) copy-start(pred[64]{0:T(512)(128)(4,1)S(1)} %compare_and_fusion.3) | copy-start | bytes 196
  14.3 44.1 %copy-start.24 = (s32[128]{0:T(128)}, s32[128]{0:T(128)S(1)}, u32[]{:S(2)}) copy-start(s32[128]{0:T(128)S(1)} %get-tuple-element.125) | copy-start | bytes 1540
  14.3 44.1 %copy-start.26 = (s32[128]{0:T(128)}, s32[128]{0:T(128)S(1)}, u32[]{:S(2)}) copy-start(s32[128]{0:T(128)S(1)} %get-tuple-element.126) | copy-start | bytes 1540
  14.4 44.1 %copy-start.32 = (pred[128]{0:T(512)(128)(4,1)}, pred[128]{0:T(512)(128)(4,1)S(1)}, u32[]{:S(2)}) copy-start(pred[128]{0:T(512)(128)(4,1)S(1)} %compare_and_fusion) | copy-start | bytes 388
  14.4 44.3 %copy-start.28 = (s32[32]{0:T(128)}, s32[32]{0:T(128)S(1)}, u32[]{:S(2)}) copy-start(s32[32]{0:T(128)S(1)} %iota_shift-right-logical_fusion.2) | copy-start | bytes 388
  14.4 44.3 %copy-start.30 = (s32[32]{0:T(128)}, s32[32]{0:T(128)S(1)}, u32[]{:S(2)}) copy-start(s32[32]{0:T(128)S(1)} %broadcast_add_fusion.3) | copy-start | bytes 388
  16.3 42.4 %copy-start.34 = (pred[32]{0:T(512)(128)(4,1)}, pred[32]{0:T(512)(128)(4,1)S(1)}, u32[]{:S(2)}) copy-start(pred[32]{0:T(512)(128)(4,1)S(1)} %compare_and_fusion.1) | copy-start | bytes 100
  16.4 12.9 %collective-permute-start.1 = (f32[1,64,256]{2,1,0:T(8,128)S(1)}, f32[1,64,256]{2,1,0:T(8,128)S(1)}, u32[]{:S(2)}, u32[]{:S(2)}) collective-permute-start(f32[1,64,256]{2,1,0:T(8,128)S(1)} %get-tuple-element.51), channel_id=1, source_target_pairs={{4,0},{8,4},{12,8},{16,12},{20,16},{24,20},{28,24},{5,1},{9,5},{13... | collective-permute-start | bytes 196616 | tf_op jit(solution)/shard_map/ppermute | solution.py:21
  18.8 4.4 %collective-permute-start.2 = (f32[4,64,1]{2,1,0:T(8,128)S(1)}, f32[4,64,1]{2,1,0:T(8,128)S(1)}, u32[]{:S(2)}, u32[]{:S(2)}) collective-permute-start(f32[4,64,1]{2,1,0:T(8,128)S(1)} %get-tuple-element.50), channel_id=1, source_target_pairs={{0,1},{1,2},{2,3},{3,0},{4,5},{5,6},{6,7},{7,4},{8,9},{9,10},{10,1... | collective-permute-start | bytes 3080 | tf_op jit(solution)/shard_map/ppermute | solution.py:20
  23.2 2.5 %collective-permute-start.3 = (f32[4,64,1]{2,1,0:T(8,128)S(1)}, f32[4,64,1]{2,1,0:T(8,128)S(1)}, u32[]{:S(2)}, u32[]{:S(2)}) collective-permute-start(f32[4,64,1]{2,1,0:T(8,128)S(1)} %get-tuple-element.49), channel_id=1, source_target_pairs={{1,0},{2,1},{3,2},{0,3},{5,4},{6,5},{7,6},{4,7},{9,8},{10,9},{11,1... | collective-permute-start | bytes 3080 | tf_op jit(solution)/shard_map/ppermute | solution.py:21
  25.8 30.0 %collective-permute-start.16 = (f32[1,32,128]{2,1,0:T(8,128)S(1)}, f32[1,32,128]{2,1,0:T(8,128)S(1)}, u32[]{:S(2)}, u32[]{:S(2)}) collective-permute-start(f32[1,32,128]{2,1,0:T(8,128)S(1)} %get-tuple-element.116), channel_id=1, source_target_pairs={{0,4},{4,8},{8,12},{12,16},{16,20},{20,24},{24,28},{1,5},{5,9},{9,... | collective-permute-start | bytes 49160 | tf_op jit(solution)/shard_map/ppermute | solution.py:20
  29.8 7.5 %collective-permute-start.11 = (f32[4,64,1]{2,1,0:T(8,128)S(1)}, f32[4,64,1]{2,1,0:T(8,128)S(1)}, u32[]{:S(2)}, u32[]{:S(2)}) collective-permute-start(f32[4,64,1]{2,1,0:T(8,128)S(1)} %get-tuple-element.48), channel_id=1, source_target_pairs={{1,0},{2,1},{3,2},{0,3},{5,4},{6,5},{7,6},{4,7},{9,8},{10,9},{11,1... | collective-permute-start | bytes 3080 | tf_op jit(solution)/shard_map/ppermute | solution.py:21
  31.5 5.9 %collective-permute-start.10 = (f32[4,64,1]{2,1,0:T(8,128)S(1)}, f32[4,64,1]{2,1,0:T(8,128)S(1)}, u32[]{:S(2)}, u32[]{:S(2)}) collective-permute-start(f32[4,64,1]{2,1,0:T(8,128)S(1)} %get-tuple-element.47), channel_id=1, source_target_pairs={{0,1},{1,2},{2,3},{3,0},{4,5},{5,6},{6,7},{7,4},{8,9},{9,10},{10,1... | collective-permute-start | bytes 3080 | tf_op jit(solution)/shard_map/ppermute | solution.py:20
  31.5 6.8 %collective-permute-start.9 = (f32[1,64,256]{2,1,0:T(8,128)S(1)}, f32[1,64,256]{2,1,0:T(8,128)S(1)}, u32[]{:S(2)}, u32[]{:S(2)}) collective-permute-start(f32[1,64,256]{2,1,0:T(8,128)S(1)} %get-tuple-element.46), channel_id=1, source_target_pairs={{4,0},{8,4},{12,8},{16,12},{20,16},{24,20},{28,24},{5,1},{9,5},{13... | collective-permute-start | bytes 196616 | tf_op jit(solution)/shard_map/ppermute | solution.py:21
  34.8 7.6 %collective-permute-start.8 = (f32[1,64,256]{2,1,0:T(8,128)S(1)}, f32[1,64,256]{2,1,0:T(8,128)S(1)}, u32[]{:S(2)}, u32[]{:S(2)}) collective-permute-start(f32[1,64,256]{2,1,0:T(8,128)S(1)} %get-tuple-element.45), channel_id=1, source_target_pairs={{0,4},{4,8},{8,12},{12,16},{16,20},{20,24},{24,28},{1,5},{5,9},{9,... | collective-permute-start | bytes 196616 | tf_op jit(solution)/shard_map/ppermute | solution.py:20
  42.8 6.7 %collective-permute-start.15 = (f32[4,64,1]{2,1,0:T(8,128)S(1)}, f32[4,64,1]{2,1,0:T(8,128)S(1)}, u32[]{:S(2)}, u32[]{:S(2)}) collective-permute-start(f32[4,64,1]{2,1,0:T(8,128)S(1)} %get-tuple-element.42), channel_id=1, source_target_pairs={{1,0},{2,1},{3,2},{0,3},{5,4},{6,5},{7,6},{4,7},{9,8},{10,9},{11,1... | collective-permute-start | bytes 3080 | tf_op jit(solution)/shard_map/ppermute | solution.py:21
  43.6 8.7 %collective-permute-start.14 = (f32[4,64,1]{2,1,0:T(8,128)S(1)}, f32[4,64,1]{2,1,0:T(8,128)S(1)}, u32[]{:S(2)}, u32[]{:S(2)}) collective-permute-start(f32[4,64,1]{2,1,0:T(8,128)S(1)} %get-tuple-element.41), channel_id=1, source_target_pairs={{0,1},{1,2},{2,3},{3,0},{4,5},{5,6},{6,7},{7,4},{8,9},{9,10},{10,1... | collective-permute-start | bytes 3080 | tf_op jit(solution)/shard_map/ppermute | solution.py:20
  43.6 9.1 %collective-permute-start.13 = (f32[1,64,256]{2,1,0:T(8,128)S(1)}, f32[1,64,256]{2,1,0:T(8,128)S(1)}, u32[]{:S(2)}, u32[]{:S(2)}) collective-permute-start(f32[1,64,256]{2,1,0:T(8,128)S(1)} %get-tuple-element.38), channel_id=1, source_target_pairs={{4,0},{8,4},{12,8},{16,12},{20,16},{24,20},{28,24},{5,1},{9,5},{13... | collective-permute-start | bytes 196616 | tf_op jit(solution)/shard_map/ppermute | solution.py:21
  45.6 8.6 %collective-permute-start.12 = (f32[1,64,256]{2,1,0:T(8,128)S(1)}, f32[1,64,256]{2,1,0:T(8,128)S(1)}, u32[]{:S(2)}, u32[]{:S(2)}) collective-permute-start(f32[1,64,256]{2,1,0:T(8,128)S(1)} %get-tuple-element.37), channel_id=1, source_target_pairs={{0,4},{4,8},{8,12},{12,16},{16,20},{20,24},{24,28},{1,5},{5,9},{9,... | collective-permute-start | bytes 196616 | tf_op jit(solution)/shard_map/ppermute | solution.py:20
  49.5 6.2 %collective-permute-start.17 = (f32[1,32,128]{2,1,0:T(8,128)S(1)}, f32[1,32,128]{2,1,0:T(8,128)S(1)}, u32[]{:S(2)}, u32[]{:S(2)}) collective-permute-start(f32[1,32,128]{2,1,0:T(8,128)S(1)} %get-tuple-element.115), channel_id=1, source_target_pairs={{4,0},{8,4},{12,8},{16,12},{20,16},{24,20},{28,24},{5,1},{9,5},{13... | collective-permute-start | bytes 49160 | tf_op jit(solution)/shard_map/ppermute | solution.py:21
  52.4 3.4 %collective-permute-start.18 = (f32[2,32,1]{2,1,0:T(8,128)S(1)}, f32[2,32,1]{2,1,0:T(8,128)S(1)}, u32[]{:S(2)}, u32[]{:S(2)}) collective-permute-start(f32[2,32,1]{2,1,0:T(8,128)S(1)} %get-tuple-element.114), channel_id=1, source_target_pairs={{0,1},{1,2},{2,3},{3,0},{4,5},{5,6},{6,7},{7,4},{8,9},{9,10},{10,1... | collective-permute-start | bytes 776 | tf_op jit(solution)/shard_map/ppermute | solution.py:20
  52.8 3.0 %collective-permute-start.19 = (f32[2,32,1]{2,1,0:T(8,128)S(1)}, f32[2,32,1]{2,1,0:T(8,128)S(1)}, u32[]{:S(2)}, u32[]{:S(2)}) collective-permute-start(f32[2,32,1]{2,1,0:T(8,128)S(1)} %get-tuple-element.113), channel_id=1, source_target_pairs={{1,0},{2,1},{3,2},{0,3},{5,4},{6,5},{7,6},{4,7},{9,8},{10,9},{11,1... | collective-permute-start | bytes 776 | tf_op jit(solution)/shard_map/ppermute | solution.py:21
  97.1 12.6 %collective-permute-start.21 = (f32[1,32,128]{2,1,0:T(8,128)}, f32[1,32,128]{2,1,0:T(8,128)}, u32[]{:S(2)}, u32[]{:S(2)}) collective-permute-start(f32[1,32,128]{2,1,0:T(8,128)} %get-tuple-element.110), channel_id=1, source_target_pairs={{4,0},{8,4},{12,8},{16,12},{20,16},{24,20},{28,24},{5,1},{9,5},{13... | collective-permute-start | bytes 49160 | tf_op jit(solution)/shard_map/ppermute | solution.py:21
  103.2 8.1 %collective-permute-start.20 = (f32[1,32,128]{2,1,0:T(8,128)}, f32[1,32,128]{2,1,0:T(8,128)}, u32[]{:S(2)}, u32[]{:S(2)}) collective-permute-start(f32[1,32,128]{2,1,0:T(8,128)} %get-tuple-element.109), channel_id=1, source_target_pairs={{0,4},{4,8},{8,12},{12,16},{16,20},{20,24},{24,28},{1,5},{5,9},{9,... | collective-permute-start | bytes 49160 | tf_op jit(solution)/shard_map/ppermute | solution.py:20
  106.1 1.6 collective-permute-start.23
  106.1 3.6 %collective-permute-start.22 = (f32[2,32,1]{2,1,0:T(8,128)S(1)}, f32[2,32,1]{2,1,0:T(8,128)}, u32[]{:S(2)}, u32[]{:S(2)}) collective-permute-start(f32[2,32,1]{2,1,0:T(8,128)S(1)} %copy-done.10), channel_id=1, source_target_pairs={{0,1},{1,2},{2,3},{3,0},{4,5},{5,6},{6,7},{7,4},{8,9},{9,10},{10,1... | collective-permute-start | bytes 776 | tf_op jit(solution)/shard_map/ppermute | solution.py:20
  112.2 7.0 %collective-permute-start.27 = (f32[2,32,1]{2,1,0:T(8,128)S(1)}, f32[2,32,1]{2,1,0:T(8,128)S(1)}, u32[]{:S(2)}, u32[]{:S(2)}) collective-permute-start(f32[2,32,1]{2,1,0:T(8,128)S(1)} %get-tuple-element.106), channel_id=1, source_target_pairs={{1,0},{2,1},{3,2},{0,3},{5,4},{6,5},{7,6},{4,7},{9,8},{10,9},{11,1... | collective-permute-start | bytes 776 | tf_op jit(solution)/shard_map/ppermute | solution.py:21
  112.3 6.9 %collective-permute-start.26 = (f32[2,32,1]{2,1,0:T(8,128)S(1)}, f32[2,32,1]{2,1,0:T(8,128)S(1)}, u32[]{:S(2)}, u32[]{:S(2)}) collective-permute-start(f32[2,32,1]{2,1,0:T(8,128)S(1)} %get-tuple-element.105), channel_id=1, source_target_pairs={{0,1},{1,2},{2,3},{3,0},{4,5},{5,6},{6,7},{7,4},{8,9},{9,10},{10,1... | collective-permute-start | bytes 776 | tf_op jit(solution)/shard_map/ppermute | solution.py:20
  112.8 6.5 %collective-permute-start.25 = (f32[1,32,128]{2,1,0:T(8,128)S(1)}, f32[1,32,128]{2,1,0:T(8,128)S(1)}, u32[]{:S(2)}, u32[]{:S(2)}) collective-permute-start(f32[1,32,128]{2,1,0:T(8,128)S(1)} %get-tuple-element.104), channel_id=1, source_target_pairs={{4,0},{8,4},{12,8},{16,12},{20,16},{24,20},{28,24},{5,1},{9,5},{13... | collective-permute-start | bytes 49160 | tf_op jit(solution)/shard_map/ppermute | solution.py:21
  117.3 6.5 %collective-permute-start.24 = (f32[1,32,128]{2,1,0:T(8,128)S(1)}, f32[1,32,128]{2,1,0:T(8,128)S(1)}, u32[]{:S(2)}, u32[]{:S(2)}) collective-permute-start(f32[1,32,128]{2,1,0:T(8,128)S(1)} %get-tuple-element.103), channel_id=1, source_target_pairs={{0,4},{4,8},{8,12},{12,16},{16,20},{20,24},{24,28},{1,5},{5,9},{9,... | collective-permute-start | bytes 49160 | tf_op jit(solution)/shard_map/ppermute | solution.py:20
  160.9 8.1 %collective-permute-start.31 = (f32[2,32,1]{2,1,0:T(8,128)S(1)}, f32[2,32,1]{2,1,0:T(8,128)S(1)}, u32[]{:S(2)}, u32[]{:S(2)}) collective-permute-start(f32[2,32,1]{2,1,0:T(8,128)S(1)} %get-tuple-element.98), channel_id=1, source_target_pairs={{1,0},{2,1},{3,2},{0,3},{5,4},{6,5},{7,6},{4,7},{9,8},{10,9},{11,1... | collective-permute-start | bytes 776 | tf_op jit(solution)/shard_map/ppermute | solution.py:21
  160.9 8.1 %collective-permute-start.30 = (f32[2,32,1]{2,1,0:T(8,128)S(1)}, f32[2,32,1]{2,1,0:T(8,128)S(1)}, u32[]{:S(2)}, u32[]{:S(2)}) collective-permute-start(f32[2,32,1]{2,1,0:T(8,128)S(1)} %get-tuple-element.97), channel_id=1, source_target_pairs={{0,1},{1,2},{2,3},{3,0},{4,5},{5,6},{6,7},{7,4},{8,9},{9,10},{10,1... | collective-permute-start | bytes 776 | tf_op jit(solution)/shard_map/ppermute | solution.py:20
  161.4 7.6 %collective-permute-start.29 = (f32[1,32,128]{2,1,0:T(8,128)S(1)}, f32[1,32,128]{2,1,0:T(8,128)S(1)}, u32[]{:S(2)}, u32[]{:S(2)}) collective-permute-start(f32[1,32,128]{2,1,0:T(8,128)S(1)} %get-tuple-element.96), channel_id=1, source_target_pairs={{4,0},{8,4},{12,8},{16,12},{20,16},{24,20},{28,24},{5,1},{9,5},{13... | collective-permute-start | bytes 49160 | tf_op jit(solution)/shard_map/ppermute | solution.py:21
  167.1 7.7 %collective-permute-start.28 = (f32[1,32,128]{2,1,0:T(8,128)S(1)}, f32[1,32,128]{2,1,0:T(8,128)S(1)}, u32[]{:S(2)}, u32[]{:S(2)}) collective-permute-start(f32[1,32,128]{2,1,0:T(8,128)S(1)} %get-tuple-element.95), channel_id=1, source_target_pairs={{0,4},{4,8},{8,12},{12,16},{16,20},{20,24},{24,28},{1,5},{5,9},{9,... | collective-permute-start | bytes 49160 | tf_op jit(solution)/shard_map/ppermute | solution.py:20
  174.9 11.2 %copy-start.15 = (s32[256]{0:T(256)S(1)}, s32[256]{0:T(256)}, u32[]{:S(2)}) copy-start(s32[256]{0:T(256)} %copy-done.14) | copy-start | bytes 3076
  174.9 6.9 %collective-permute-start.35 = (f32[2,32,1]{2,1,0:T(8,128)S(1)}, f32[2,32,1]{2,1,0:T(8,128)S(1)}, u32[]{:S(2)}, u32[]{:S(2)}) collective-permute-start(f32[2,32,1]{2,1,0:T(8,128)S(1)} %get-tuple-element.92), channel_id=1, source_target_pairs={{1,0},{2,1},{3,2},{0,3},{5,4},{6,5},{7,6},{4,7},{9,8},{10,9},{11,1... | collective-permute-start | bytes 776 | tf_op jit(solution)/shard_map/ppermute | solution.py:21
  176.0 5.9 %collective-permute-start.34 = (f32[2,32,1]{2,1,0:T(8,128)S(1)}, f32[2,32,1]{2,1,0:T(8,128)S(1)}, u32[]{:S(2)}, u32[]{:S(2)}) collective-permute-start(f32[2,32,1]{2,1,0:T(8,128)S(1)} %get-tuple-element.91), channel_id=1, source_target_pairs={{0,1},{1,2},{2,3},{3,0},{4,5},{5,6},{6,7},{7,4},{8,9},{9,10},{10,1... | collective-permute-start | bytes 776 | tf_op jit(solution)/shard_map/ppermute | solution.py:20
  176.0 5.9 %collective-permute-start.33 = (f32[1,32,128]{2,1,0:T(8,128)S(1)}, f32[1,32,128]{2,1,0:T(8,128)S(1)}, u32[]{:S(2)}, u32[]{:S(2)}) collective-permute-start(f32[1,32,128]{2,1,0:T(8,128)S(1)} %get-tuple-element.90), channel_id=1, source_target_pairs={{4,0},{8,4},{12,8},{16,12},{20,16},{24,20},{28,24},{5,1},{9,5},{13... | collective-permute-start | bytes 49160 | tf_op jit(solution)/shard_map/ppermute | solution.py:21
  179.5 6.6 %collective-permute-start.32 = (f32[1,32,128]{2,1,0:T(8,128)S(1)}, f32[1,32,128]{2,1,0:T(8,128)S(1)}, u32[]{:S(2)}, u32[]{:S(2)}) collective-permute-start(f32[1,32,128]{2,1,0:T(8,128)S(1)} %get-tuple-element.89), channel_id=1, source_target_pairs={{0,4},{4,8},{8,12},{12,16},{16,20},{20,24},{24,28},{1,5},{5,9},{9,... | collective-permute-start | bytes 49160 | tf_op jit(solution)/shard_map/ppermute | solution.py:20
  187.8 6.5 %collective-permute-start.39 = (f32[4,64,1]{2,1,0:T(8,128)S(1)}, f32[4,64,1]{2,1,0:T(8,128)S(1)}, u32[]{:S(2)}, u32[]{:S(2)}) collective-permute-start(f32[4,64,1]{2,1,0:T(8,128)S(1)} %get-tuple-element.36), channel_id=1, source_target_pairs={{1,0},{2,1},{3,2},{0,3},{5,4},{6,5},{7,6},{4,7},{9,8},{10,9},{11,1... | collective-permute-start | bytes 3080 | tf_op jit(solution)/shard_map/ppermute | solution.py:21
  187.9 6.4 %collective-permute-start.38 = (f32[4,64,1]{2,1,0:T(8,128)S(1)}, f32[4,64,1]{2,1,0:T(8,128)S(1)}, u32[]{:S(2)}, u32[]{:S(2)}) collective-permute-start(f32[4,64,1]{2,1,0:T(8,128)S(1)} %get-tuple-element.35), channel_id=1, source_target_pairs={{0,1},{1,2},{2,3},{3,0},{4,5},{5,6},{6,7},{7,4},{8,9},{9,10},{10,1... | collective-permute-start | bytes 3080 | tf_op jit(solution)/shard_map/ppermute | solution.py:20
  188.4 6.6 %collective-permute-start.37 = (f32[1,64,256]{2,1,0:T(8,128)S(1)}, f32[1,64,256]{2,1,0:T(8,128)S(1)}, u32[]{:S(2)}, u32[]{:S(2)}) collective-permute-start(f32[1,64,256]{2,1,0:T(8,128)S(1)} %get-tuple-element.34), channel_id=1, source_target_pairs={{4,0},{8,4},{12,8},{16,12},{20,16},{24,20},{28,24},{5,1},{9,5},{13... | collective-permute-start | bytes 196616 | tf_op jit(solution)/shard_map/ppermute | solution.py:21
  190.3 7.5 %collective-permute-start.36 = (f32[1,64,256]{2,1,0:T(8,128)S(1)}, f32[1,64,256]{2,1,0:T(8,128)S(1)}, u32[]{:S(2)}, u32[]{:S(2)}) collective-permute-start(f32[1,64,256]{2,1,0:T(8,128)S(1)} %get-tuple-element.33), channel_id=1, source_target_pairs={{0,4},{4,8},{8,12},{12,16},{16,20},{20,24},{24,28},{1,5},{5,9},{9,... | collective-permute-start | bytes 196616 | tf_op jit(solution)/shard_map/ppermute | solution.py:20
  198.3 6.5 %collective-permute-start.43 = (f32[4,64,1]{2,1,0:T(8,128)S(1)}, f32[4,64,1]{2,1,0:T(8,128)S(1)}, u32[]{:S(2)}, u32[]{:S(2)}) collective-permute-start(f32[4,64,1]{2,1,0:T(8,128)S(1)} %get-tuple-element.30), channel_id=1, source_target_pairs={{1,0},{2,1},{3,2},{0,3},{5,4},{6,5},{7,6},{4,7},{9,8},{10,9},{11,1... | collective-permute-start | bytes 3080 | tf_op jit(solution)/shard_map/ppermute | solution.py:21
  198.7 6.1 %collective-permute-start.42 = (f32[4,64,1]{2,1,0:T(8,128)S(1)}, f32[4,64,1]{2,1,0:T(8,128)S(1)}, u32[]{:S(2)}, u32[]{:S(2)}) collective-permute-start(f32[4,64,1]{2,1,0:T(8,128)S(1)} %get-tuple-element.29), channel_id=1, source_target_pairs={{0,1},{1,2},{2,3},{3,0},{4,5},{5,6},{6,7},{7,4},{8,9},{9,10},{10,1... | collective-permute-start | bytes 3080 | tf_op jit(solution)/shard_map/ppermute | solution.py:20
  198.9 6.6 %collective-permute-start.41 = (f32[1,64,256]{2,1,0:T(8,128)S(1)}, f32[1,64,256]{2,1,0:T(8,128)S(1)}, u32[]{:S(2)}, u32[]{:S(2)}) collective-permute-start(f32[1,64,256]{2,1,0:T(8,128)S(1)} %get-tuple-element.28), channel_id=1, source_target_pairs={{4,0},{8,4},{12,8},{16,12},{20,16},{24,20},{28,24},{5,1},{9,5},{13... | collective-permute-start | bytes 196616 | tf_op jit(solution)/shard_map/ppermute | solution.py:21
  200.8 7.5 %collective-permute-start.40 = (f32[1,64,256]{2,1,0:T(8,128)S(1)}, f32[1,64,256]{2,1,0:T(8,128)S(1)}, u32[]{:S(2)}, u32[]{:S(2)}) collective-permute-start(f32[1,64,256]{2,1,0:T(8,128)S(1)} %get-tuple-element.27), channel_id=1, source_target_pairs={{0,4},{4,8},{8,12},{12,16},{16,20},{20,24},{24,28},{1,5},{5,9},{9,... | collective-permute-start | bytes 196616 | tf_op jit(solution)/shard_map/ppermute | solution.py:20
  208.6 10.4 %copy-start.2 = (f32[4,64,256]{2,1,0:T(8,128)}, f32[4,64,256]{2,1,0:T(8,128)S(1)}, u32[]{:S(2)}) copy-start(f32[4,64,256]{2,1,0:T(8,128)S(1)} %fusion.24) | copy-start | bytes 786436
  208.8 6.6 %collective-permute-start.47 = (f32[4,64,1]{2,1,0:T(8,128)S(1)}, f32[4,64,1]{2,1,0:T(8,128)S(1)}, u32[]{:S(2)}, u32[]{:S(2)}) collective-permute-start(f32[4,64,1]{2,1,0:T(8,128)S(1)} %get-tuple-element.24), channel_id=1, source_target_pairs={{1,0},{2,1},{3,2},{0,3},{5,4},{6,5},{7,6},{4,7},{9,8},{10,9},{11,1... | collective-permute-start | bytes 3080 | tf_op jit(solution)/shard_map/ppermute | solution.py:21
  209.5 5.9 %collective-permute-start.46 = (f32[4,64,1]{2,1,0:T(8,128)S(1)}, f32[4,64,1]{2,1,0:T(8,128)S(1)}, u32[]{:S(2)}, u32[]{:S(2)}) collective-permute-start(f32[4,64,1]{2,1,0:T(8,128)S(1)} %get-tuple-element.23), channel_id=1, source_target_pairs={{0,1},{1,2},{2,3},{3,0},{4,5},{5,6},{6,7},{7,4},{8,9},{9,10},{10,1... | collective-permute-start | bytes 3080 | tf_op jit(solution)/shard_map/ppermute | solution.py:20
  209.5 6.6 %collective-permute-start.45 = (f32[1,64,256]{2,1,0:T(8,128)S(1)}, f32[1,64,256]{2,1,0:T(8,128)S(1)}, u32[]{:S(2)}, u32[]{:S(2)}) collective-permute-start(f32[1,64,256]{2,1,0:T(8,128)S(1)} %get-tuple-element.22), channel_id=1, source_target_pairs={{4,0},{8,4},{12,8},{16,12},{20,16},{24,20},{28,24},{5,1},{9,5},{13... | collective-permute-start | bytes 196616 | tf_op jit(solution)/shard_map/ppermute | solution.py:21
  211.4 7.6 %collective-permute-start.44 = (f32[1,64,256]{2,1,0:T(8,128)S(1)}, f32[1,64,256]{2,1,0:T(8,128)S(1)}, u32[]{:S(2)}, u32[]{:S(2)}) collective-permute-start(f32[1,64,256]{2,1,0:T(8,128)S(1)} %get-tuple-element.21), channel_id=1, source_target_pairs={{0,4},{4,8},{8,12},{12,16},{16,20},{20,24},{24,28},{1,5},{5,9},{9,... | collective-permute-start | bytes 196616 | tf_op jit(solution)/shard_map/ppermute | solution.py:20
  (20 other events, 23.0 us)

commit v3 on v1

v3 whole, which is shorter than its diff:
```python
import math

import jax
import jax.numpy as jnp
from jax import lax
from jax.sharding import PartitionSpec as P

SWEEPS = 2
COARSE_SWEEPS = 4
OMEGA = 0.75
RAAN_HALO = 32
HIGH = lax.Precision.HIGHEST


def pairing(fine):
    rows = lax.broadcasted_iota(jnp.int32, (fine, fine // 2), 0) // 2
    cols = lax.broadcasted_iota(jnp.int32, (fine, fine // 2), 1)
    return (rows == cols).astype(jnp.float32)


def coarsen(values):
    depth, width, length = values.shape
    summed = values.reshape(depth // 2, 2, width, length).sum(axis=1)
    summed = jnp.matmul(summed, pairing(length), precision=HIGH)
    summed = jnp.matmul(pairing(width).T[None], summed, precision=HIGH)
    return summed * 0.125


def refine(values):
    depth, width, length = values.shape
    grown = jnp.matmul(values, pairing(2 * length).T, precision=HIGH)
    grown = jnp.matmul(pairing(2 * width)[None], grown, precision=HIGH)
    grown = jnp.broadcast_to(grown[:, None], (depth, 2, 2 * width, 2 * length))
    return grown.reshape(2 * depth, 2 * width, 2 * length)


def raan_extend(values, halo):
    count, length = lax.axis_size("raan"), values.shape[-1]
    up = [(i, (i + 1) % count) for i in range(count)]
    down = [(j, i) for i, j in up]
    before = lax.ppermute(values[..., length - halo:], "raan", up)
    after = lax.ppermute(values[..., :halo], "raan", down)
    return jnp.concatenate([before, values, after], axis=-1)


def alt_extend(items):
    count = lax.axis_size("alt")
    pieces = {}
    for index, (values, halo) in enumerate(items):
        depth = values.shape[0]
        for distance in range(1, -(-halo // depth) + 1):
            low = max(0, distance * depth - halo)
            high = min(depth, halo - (distance - 1) * depth)
            pieces.setdefault(("up", distance), []).append((index, values[low:]))
            pieces.setdefault(("down", distance), []).append((index, values[:high]))
    got = {}
    for (way, distance), parts in pieces.items():
        if way == "up":
            route = [(i, i + distance) for i in range(count) if i + distance < count]
        else:
            route = [(i, i - distance) for i in range(count) if i - distance >= 0]
        flat = jnp.concatenate([part.reshape(-1) for _, part in parts])
        moved = lax.ppermute(flat, "alt", route)
        start = 0
        for index, part in parts:
            size = part.size
            got[(index, way, distance)] = moved[start:start + size].reshape(part.shape)
            start += size
    out = []
    for index, (values, halo) in enumerate(items):
        depth = values.shape[0]
        reach = -(-halo // depth)
        below = [got[(index, "up", d)] for d in range(reach, 0, -1)]
        above = [got[(index, "down", d)] for d in range(1, reach + 1)]
        out.append(jnp.concatenate(below + [values] + above, axis=0))
    return out


def trim(values, have, want):
    cut = have - want
    return values[cut:values.shape[0] - cut] if cut else values


def lane_shifts(values):
    zero = jnp.zeros_like(values[..., :1])
    left = jnp.concatenate([zero, values[..., :-1]], axis=-1)
    right = jnp.concatenate([values[..., 1:], zero], axis=-1)
    return left, right


def make_weights(coef_alt, coef_inc, coef_raan, factor, halo):
    centre = coef_alt[1:-1]
    w_alt_lo = factor * 0.5 * (centre + coef_alt[:-2])
    w_alt_hi = factor * 0.5 * (centre + coef_alt[2:])
    inner_faces = factor * 0.5 * (coef_inc[:, :-1] + coef_inc[:, 1:])
    zero_inc = jnp.zeros_like(coef_inc[:, :1])
    w_inc_lo = jnp.concatenate([zero_inc, inner_faces], 1)
    w_inc_hi = jnp.concatenate([inner_faces, zero_inc], 1)
    raan_left, raan_right = lane_shifts(coef_raan)
    w_raan_lo = factor * 0.5 * (coef_raan + raan_left)
    w_raan_hi = factor * 0.5 * (coef_raan + raan_right)
    diagonal = 1.0 + (w_alt_lo + w_alt_hi + w_inc_lo + w_inc_hi + w_raan_lo + w_raan_hi)
    return (w_alt_lo, w_alt_hi, w_inc_lo, w_inc_hi, w_raan_lo, w_raan_hi, diagonal), halo


def apply_op(weights, field, halo):
    parts, have = weights
    w_alt_lo, w_alt_hi, w_inc_lo, w_inc_hi, w_raan_lo, w_raan_hi, diagonal = (
        trim(part, have, halo - 1) for part in parts
    )
    centre = field[1:-1]
    v_down, v_up = field[:-2], field[2:]
    zero_inc = jnp.zeros_like(centre[:, :1])
    v_prev = jnp.concatenate([zero_inc, centre[:, :-1]], 1)
    v_next = jnp.concatenate([centre[:, 1:], zero_inc], 1)
    v_left, v_right = lane_shifts(centre)
    beside = (
        w_alt_lo * v_down
        + w_alt_hi * v_up
        + w_inc_lo * v_prev
        + w_inc_hi * v_next
        + w_raan_lo * v_left
        + w_raan_hi * v_right
    )
    return diagonal * centre - beside, centre


def inside(shape, halo):
    depth = shape[0] - 2 * halo
    rows = lax.broadcasted_iota(jnp.int32, shape, 0) + lax.axis_index("alt") * depth - halo
    return (rows >= 0) & (rows < depth * lax.axis_size("alt"))


def sweep(weights, field, halo, target, target_halo):
    applied, centre = apply_op(weights, field, halo)
    diagonal = trim(weights[0][6], weights[1], halo - 1)
    updated = centre + OMEGA * (trim(target, target_halo, halo - 1) - applied) / diagonal
    return jnp.where(inside(updated.shape, halo - 1), updated, 0.0)


def first_sweep(weights, target, halo):
    diagonal = trim(weights[0][6], weights[1], halo)
    return OMEGA * target / diagonal


def shards(source, k_alt, k_inc, k_raan):
    length = source.shape[-1]
    halo_r = min(RAAN_HALO, length)
    wide = raan_extend(jnp.stack([source, k_alt, k_inc, k_raan], axis=1), halo_r)
    wide_source, wide_alt, wide_inc, wide_raan = (wide[:, i] for i in range(4))
    coef_two = [coarsen(part) for part in (wide_alt, wide_inc, wide_raan)]
    coef_three = [coarsen(part) for part in coef_two]

    first, second, two_x, three_x = alt_extend(
        [(wide[:, 0:2], 3), (wide[:, 2:4], 2), (jnp.stack(coef_two, 1), 3), (jnp.stack(coef_three, 1), 4)]
    )
    source_x, alt_x = first[:, 0], first[:, 1]
    weights_one = make_weights(alt_x, second[:, 0], second[:, 1], 1.0, 2)
    weights_two = make_weights(two_x[:, 0], trim(two_x[:, 1], 3, 2), trim(two_x[:, 2], 3, 2), 0.25, 2)
    weights_three = make_weights(
        three_x[:, 0], trim(three_x[:, 1], 4, 3), trim(three_x[:, 2], 4, 3), 0.0625, 3
    )

    density = sweep(weights_one, source_x, 3, source_x, 3)
    density = sweep(weights_one, density, 2, source_x, 3)
    applied, _ = apply_op(weights_one, density, 1)
    rhs_two = coarsen(trim(source_x, 3, 0) - applied)
    density = trim(density, 1, 0)

    (rhs_two_x,) = alt_extend([(rhs_two, 2)])
    correction = first_sweep(weights_two, rhs_two_x, 2)
    correction = sweep(weights_two, correction, 2, rhs_two_x, 2)
    applied, _ = apply_op(weights_two, correction, 1)
    rhs_three = coarsen(trim(rhs_two_x, 2, 0) - applied)
    correction = trim(correction, 1, 0)

    (rhs_three_x,) = alt_extend([(rhs_three, COARSE_SWEEPS - 1)])
    coarse_part = first_sweep(weights_three, rhs_three_x, COARSE_SWEEPS - 1)
    for halo in range(COARSE_SWEEPS - 1, 0, -1):
        coarse_part = sweep(weights_three, coarse_part, halo, rhs_three_x, COARSE_SWEEPS - 1)

    correction = correction + refine(coarse_part)
    (correction,) = alt_extend([(correction, SWEEPS)])
    for halo in range(SWEEPS, 0, -1):
        correction = sweep(weights_two, correction, halo, rhs_two_x, 2)

    density = density + refine(correction)
    (density,) = alt_extend([(density, SWEEPS + 1)])
    for halo in range(SWEEPS + 1, 1, -1):
        density = sweep(weights_one, density, halo, source_x, 3)
    applied, centre = apply_op(weights_one, density, 1)
    scaled_residual = (trim(source_x, 3, 0) - applied) / trim(weights_one[0][6], 2, 0)
    keep = slice(halo_r, halo_r + length)
    return (centre[..., keep], scaled_residual[..., keep])


def solution(mesh):
    spec = P("alt", None, "raan")
    return jax.shard_map(
        shards, mesh=mesh, in_specs=(spec,) * 4, out_specs=(spec, spec), check_vma=False
    )
```

time: 172 us -> 258 us (1.50)
  the two profiles are of different devices: /device:TPU:8 before, /device:TPU:26 now
where the time goes in v3:
time: 258 us; the launch traced here: 254 us
  local copies, waits for them, and re-layouts  105 us (41%)
  starting transfers between devices  63.7 us (25%)
  other arithmetic  36.8 us (14%)
  waiting for transfers between devices  32.5 us (13%)
  matrix products  14.1 us (5%)
    ppermute x20, starting transfers between devices, alt_extend(): moved = lax.ppermute(flat, 'alt', route)  63.2 us
    reshape x28, local copies, waits for them, and re-layouts, alt_extend(): got[index, way, distance] = moved[start:start + size].reshape(part.shape)  30.6 us
    ppermute x20, waiting for transfers between devices, alt_extend(): moved = lax.ppermute(flat, 'alt', route)  25.2 us
    unnamed x207, local copies, waits for them, and re-layouts  24.6 us
    reshape x13, local copies, waits for them, and re-layouts, alt_extend(): flat = jnp.concatenate([part.reshape(-1) for _, part in parts])  12.3 us
    slice x12, local copies, waits for them, and re-layouts, alt_extend(): got[index, way, distance] = moved[start:start + size].reshape(part.shape)  10.6 us
    dot_general x8, matrix products, coarsen(): summed = jnp.matmul(summed, pairing(length), precision=HIGH)  6.99 us
    concatenate x5, local copies, waits for them, and re-layouts, alt_extend(): out.append(jnp.concatenate(below + [values] + above, axis=0))  6.68 us
  transfers between devices with their start and end apart: 22, of which 6 were waited for; matrix products, arithmetic and copies ran while one was open for 30% of the time, Pallas kernels for 0%

profile of v3, /device:TPU:26, one launch (start us, length us, event | category | flops | bytes accessed | tf_op | source)
XLA Modules:
  0.0 254.2 jit_solution(2993740424961333737)
XLA Ops:
  9.8 5.2 %collective-permute-done.1 = f32[4,4,64,32]{3,2,0,1:T(8,128)S(1)} collective-permute-done((f32[4,4,64,32]{3,2,0,1:T(8,128)}, f32[4,4,64,32]{3,2,0,1:T(8,128)S(1)}, u32[]{:S(2)}, u32[]{:S(2)}) %collective-permute-start.1) | collective-permute-done | bytes 131104 | tf_op jit(solution)/shard_map/ppermute | solution.py:42
  14.9 2.1 collective-permute-done
  17.1 1.6 pad_maximum_fusion.1
  37.5 7.6 %collective-permute-start.15 = (f32[3840]{0:T(1024)S(1)}, f32[3840]{0:T(1024)}, u32[]{:S(2)}, u32[]{:S(2)}) collective-permute-start(f32[3840]{0:T(1024)S(1)} %reshape.264), channel_id=1, source_target_pairs={{12,0},{16,4},{20,8},{24,12},{28,16},{13,1},{17,5},{21,9},{25,13},... | collective-permute-start | bytes 46088 | tf_op jit(solution)/shard_map/ppermute | solution.py:63
  47.0 1.9 reshape.262
  51.7 2.5 pad_maximum_fusion.4
  54.1 1.9 collective-permute-start.2
  56.1 4.8 %collective-permute-start.3 = (f32[239360]{0:T(1024)}, f32[239360]{0:T(1024)}, u32[]{:S(2)}, u32[]{:S(2)}) collective-permute-start(f32[239360]{0:T(1024)} %get-tuple-element.81), channel_id=1, source_target_pairs={{4,0},{8,4},{12,8},{16,12},{20,16},{24,20},{28,24},{5,1},{9,5},{13... | collective-permute-start | bytes 2872328 | tf_op jit(solution)/shard_map/ppermute | solution.py:63
  61.8 2.4 collective-permute-start.17
  67.1 1.5 collective-permute-start.6
  68.6 1.4 reshape.293
  70.0 12.2 %collective-permute-done.17 = f32[3840]{0:T(1024)S(1)} collective-permute-done((f32[3840]{0:T(1024)S(1)}, f32[3840]{0:T(1024)S(1)}, u32[]{:S(2)}, u32[]{:S(2)}) %collective-permute-start.17) | collective-permute-done | bytes 15392 | tf_op jit(solution)/shard_map/ppermute | solution.py:63
  89.2 11.2 %collective-permute-done.3 = f32[239360]{0:T(1024)} collective-permute-done((f32[239360]{0:T(1024)}, f32[239360]{0:T(1024)}, u32[]{:S(2)}, u32[]{:S(2)}) %collective-permute-start.3) | collective-permute-done | bytes 957472 | tf_op jit(solution)/shard_map/ppermute | solution.py:63
  102.6 1.4 pad_maximum_fusion
  104.1 1.4 fusion.271
  107.9 1.7 slice.1066
  117.6 1.5 bitcast_reduce_fusion
  120.4 1.5 reshape.272
  122.0 3.5 %collective-permute-start.5 = (f32[10240]{0:T(1024)}, f32[10240]{0:T(1024)}, u32[]{:S(2)}, u32[]{:S(2)}) collective-permute-start(f32[10240]{0:T(1024)} %reshape.272), channel_id=1, source_target_pairs={{4,0},{8,4},{12,8},{16,12},{20,16},{24,20},{28,24},{5,1},{9,5},{13... | collective-permute-start | bytes 122888 | tf_op jit(solution)/shard_map/ppermute | solution.py:63
  125.5 2.9 %collective-permute-start.4 = (f32[10240]{0:T(1024)}, f32[10240]{0:T(1024)}, u32[]{:S(2)}, u32[]{:S(2)}) collective-permute-start(f32[10240]{0:T(1024)} %reshape.272), channel_id=1, source_target_pairs={{0,4},{4,8},{8,12},{12,16},{16,20},{20,24},{24,28},{1,5},{5,9},{9,... | collective-permute-start | bytes 122888 | tf_op jit(solution)/shard_map/ppermute | solution.py:63
  128.4 1.6 slice.1105
  130.0 1.7 reshape.275
  131.6 1.5 slice.1106
  133.2 1.7 reshape.276
  138.5 1.3 slice.1144
  139.8 1.4 reshape.290
  142.5 1.4 reshape.291
  143.9 1.4 constant_dynamic-update-slice_fusion.17
  145.3 1.3 constant_dynamic-update-slice_fusion.16
  146.6 1.4 constant_dynamic-update-slice_fusion.15
  147.9 1.4 constant_dynamic-update-slice_fusion.14
  149.3 1.3 constant_dynamic-update-slice_fusion.7
  152.1 1.3 constant_dynamic-update-slice_fusion.26
  154.8 1.3 constant_dynamic-update-slice_fusion.24
  156.1 1.3 constant_dynamic-update-slice_fusion.23
  158.2 1.3 constant_dynamic-update-slice_fusion.22
  159.5 1.5 reshape.274
  161.0 1.5 reshape.273
  162.5 1.7 multiply_divide_fusion
  168.0 1.3 constant_dynamic-update-slice_fusion.21
  170.6 1.9 collective-permute-start.10
  172.6 4.8 %collective-permute-start.11 = (f32[1280]{0:T(1024)}, f32[1280]{0:T(1024)}, u32[]{:S(2)}, u32[]{:S(2)}) collective-permute-start(f32[1280]{0:T(1024)} %reshape.281), channel_id=1, source_target_pairs={{4,0},{8,4},{12,8},{16,12},{20,16},{24,20},{28,24},{5,1},{9,5},{13... | collective-permute-start | bytes 15368 | tf_op jit(solution)/shard_map/ppermute | solution.py:63
  177.4 5.5 %collective-permute-start.12 = (f32[1280]{0:T(1024)}, f32[1280]{0:T(1024)}, u32[]{:S(2)}, u32[]{:S(2)}) collective-permute-start(f32[1280]{0:T(1024)} %reshape.281), channel_id=1, source_target_pairs={{8,0},{12,4},{16,8},{20,12},{24,16},{28,20},{9,1},{13,5},{17,9},{2... | collective-permute-start | bytes 15368 | tf_op jit(solution)/shard_map/ppermute | solution.py:63
  183.5 6.5 %collective-permute-start.13 = (f32[1280]{0:T(1024)}, f32[1280]{0:T(1024)}, u32[]{:S(2)}, u32[]{:S(2)}) collective-permute-start(f32[1280]{0:T(1024)} %reshape.281), channel_id=1, source_target_pairs={{12,0},{16,4},{20,8},{24,12},{28,16},{13,1},{17,5},{21,9},{25,13},... | collective-permute-start | bytes 15368 | tf_op jit(solution)/shard_map/ppermute | solution.py:63
  194.8 1.4 reshape.285
  197.4 1.4 reshape.286
  200.1 1.4 reshape.287
  201.5 1.3 constant_dynamic-update-slice_fusion
  206.5 1.6 reshape.298
  208.1 1.9 collective-permute-start.19
  210.0 4.5 %collective-permute-start.18 = (f32[10240]{0:T(1024)}, f32[10240]{0:T(1024)}, u32[]{:S(2)}, u32[]{:S(2)}) collective-permute-start(f32[10240]{0:T(1024)} %reshape.298), channel_id=1, source_target_pairs={{0,4},{4,8},{8,12},{12,16},{16,20},{20,24},{24,28},{1,5},{5,9},{9,... | collective-permute-start | bytes 122888 | tf_op jit(solution)/shard_map/ppermute | solution.py:63
  214.6 1.5 reshape.300
  217.1 1.5 reshape.299
  219.8 1.5 fusion.103
  221.5 1.4 fusion.127
  224.9 1.8 reshape.304
  226.7 1.9 collective-permute-start.21
  228.7 1.8 reshape.302
  230.5 5.0 %collective-permute-start.20 = (f32[61440]{0:T(1024)}, f32[61440]{0:T(1024)}, u32[]{:S(2)}, u32[]{:S(2)}) collective-permute-start(f32[61440]{0:T(1024)} %reshape.302), channel_id=1, source_target_pairs={{0,4},{4,8},{8,12},{12,16},{16,20},{20,24},{24,28},{1,5},{5,9},{9,... | collective-permute-start | bytes 737288 | tf_op jit(solution)/shard_map/ppermute | solution.py:63
  235.4 1.8 slice.1094
  237.2 1.8 slice.1103
  240.4 1.8 reshape.305
  242.2 1.8 reshape.303
  252.8 1.4 fusion.68
  (365 shorter events, 95.5 us)
Async XLA Ops:
  1.9 15.1 %copy-start.35 = (f32[4,64,256]{2,1,0:T(8,128)S(1)}, f32[4,64,256]{2,1,0:T(8,128)}, u32[]{:S(2)}) copy-start(f32[4,64,256]{2,1,0:T(8,128)} %param.7) | copy-start | bytes 786436
  1.9 15.1 %copy-start.36 = (f32[4,64,256]{2,1,0:T(8,128)S(1)}, f32[4,64,256]{2,1,0:T(8,128)}, u32[]{:S(2)}) copy-start(f32[4,64,256]{2,1,0:T(8,128)} %param.6) | copy-start | bytes 786436
  1.9 15.1 %copy-start.37 = (f32[4,64,256]{2,1,0:T(8,128)S(1)}, f32[4,64,256]{2,1,0:T(8,128)}, u32[]{:S(2)}) copy-start(f32[4,64,256]{2,1,0:T(8,128)} %param.5) | copy-start | bytes 786436
  2.0 15.1 %copy-start.38 = (f32[4,64,256]{2,1,0:T(8,128)S(1)}, f32[4,64,256]{2,1,0:T(8,128)}, u32[]{:S(2)}) copy-start(f32[4,64,256]{2,1,0:T(8,128)} %param.4) | copy-start | bytes 786436
  2.9 12.0 %collective-permute-start.1 = (f32[4,4,64,32]{3,2,0,1:T(8,128)}, f32[4,4,64,32]{3,2,0,1:T(8,128)S(1)}, u32[]{:S(2)}, u32[]{:S(2)}) collective-permute-start(f32[4,4,64,32]{3,2,0,1:T(8,128)} %get-tuple-element.32), channel_id=1, source_target_pairs={{1,0},{2,1},{3,2},{0,3},{5,4},{6,5},{7,6},{4,7},{9,8},{10,9},{11,1... | collective-permute-start | bytes 393224 | tf_op jit(solution)/shard_map/ppermute | solution.py:42
  2.9 14.1 %collective-permute-start = (f32[4,4,64,32]{3,2,0,1:T(8,128)S(1)}, f32[4,4,64,32]{3,2,0,1:T(8,128)}, u32[]{:S(2)}, u32[]{:S(2)}) collective-permute-start(f32[4,4,64,32]{3,2,0,1:T(8,128)S(1)} %get-tuple-element.31), channel_id=1, source_target_pairs={{0,1},{1,2},{2,3},{3,0},{4,5},{5,6},{6,7},{7,4},{8,9},{9,10},{10,1... | collective-permute-start | bytes 393224 | tf_op jit(solution)/shard_map/ppermute | solution.py:41
  4.0 24.0 %copy-start.58 = (s32[64]{0:T(128)}, s32[64]{0:T(128)S(1)}, u32[]{:S(2)}) copy-start(s32[64]{0:T(128)S(1)} %get-tuple-element.136) | copy-start | bytes 772
  4.1 24.0 %copy-start.61 = (s32[64]{0:T(128)}, s32[64]{0:T(128)S(1)}, u32[]{:S(2)}) copy-start(s32[64]{0:T(128)S(1)} %get-tuple-element.137) | copy-start | bytes 772
  4.1 24.0 %copy-start.64 = (pred[64]{0:T(512)(128)(4,1)}, pred[64]{0:T(512)(128)(4,1)S(1)}, u32[]{:S(2)}) copy-start(pred[64]{0:T(512)(128)(4,1)S(1)} %compare_and_fusion.6) | copy-start | bytes 196
  9.8 17.0 %copy-start.73 = (s32[320]{0:T(512)}, s32[320]{0:T(512)S(1)}, u32[]{:S(2)}) copy-start(s32[320]{0:T(512)S(1)} %get-tuple-element.134) | copy-start | bytes 3844
  18.7 45.5 %copy-start = (f32[4,4,64,320]{3,2,0,1:T(8,128)}, f32[4,4,64,320]{3,2,0,1:T(8,128)S(1)}, u32[]{:S(2)}) copy-start(f32[4,4,64,320]{3,2,0,1:T(8,128)S(1)} %pad_maximum_fusion.1) | copy-start | bytes 3932164
  26.0 6.6 %copy-start.39 = (f32[32,2,160]{2,0,1:T(8,128)}, f32[32,2,160]{2,0,1:T(8,128)S(1)}, u32[]{:S(2)}) copy-start(f32[32,2,160]{2,0,1:T(8,128)S(1)} %get-tuple-element.129) | copy-start | bytes 122884
  26.8 7.7 %copy-start.40 = (f32[32,2,160]{2,0,1:T(8,128)}, f32[32,2,160]{2,0,1:T(8,128)S(1)}, u32[]{:S(2)}) copy-start(f32[32,2,160]{2,0,1:T(8,128)S(1)} %get-tuple-element.131) | copy-start | bytes 122884
  26.9 3.8 %copy-start.55 = (f32[32,160]{1,0:T(8,128)S(1)}, f32[32,160]{1,0:T(8,128)}, u32[]{:S(2)}) copy-start(f32[32,160]{1,0:T(8,128)} %get-tuple-element.130) | copy-start | bytes 61444
  26.9 7.7 %copy-start.83 = (s32[32]{0:T(128)S(1)}, s32[32]{0:T(128)}, u32[]{:S(2)}) copy-start(s32[32]{0:T(128)} %get-tuple-element.140) | copy-start | bytes 388
  26.9 7.7 %copy-start.86 = (s32[32]{0:T(128)S(1)}, s32[32]{0:T(128)}, u32[]{:S(2)}) copy-start(s32[32]{0:T(128)} %get-tuple-element.141) | copy-start | bytes 388
  26.9 7.7 %copy-start.91 = (pred[32]{0:T(512)(128)(4,1)S(1)}, pred[32]{0:T(512)(128)(4,1)}, u32[]{:S(2)}) copy-start(pred[32]{0:T(512)(128)(4,1)} %compare_and_fusion.5) | copy-start | bytes 100
  26.9 19.3 %copy-start.24 = (f32[2,2,64,320]{3,2,0,1:T(8,128)S(1)}, f32[2,2,64,320]{3,2,0,1:T(8,128)}, u32[]{:S(2)}) copy-start(f32[2,2,64,320]{3,2,0,1:T(8,128)} %get-tuple-element.29) | copy-start | bytes 983044
  28.3 18.7 %copy-start.41 = (f32[32,2,160]{2,0,1:T(8,128)}, f32[32,2,160]{2,0,1:T(8,128)S(1)}, u32[]{:S(2)}) copy-start(f32[32,2,160]{2,0,1:T(8,128)S(1)} %get-tuple-element.133) | copy-start | bytes 122884
  32.6 4.9 %copy-start.48 = (f32[1,1,16,80]{3,2,1,0:T(8,128)}, f32[1,1,16,80]{3,2,1,0:T(8,128)S(1)}, u32[]{:S(2)}) copy-start(f32[1,1,16,80]{3,2,1,0:T(8,128)S(1)} %fusion.1) | copy-start | bytes 15364
  33.5 4.0 %copy-start.50 = (f32[1,1,16,80]{3,2,1,0:T(8,128)}, f32[1,1,16,80]{3,2,1,0:T(8,128)S(1)}, u32[]{:S(2)}) copy-start(f32[1,1,16,80]{3,2,1,0:T(8,128)S(1)} %fusion.2) | copy-start | bytes 15364
  34.8 14.1 %copy-start.52 = (f32[1,1,16,80]{3,2,1,0:T(8,128)}, f32[1,1,16,80]{3,2,1,0:T(8,128)S(1)}, u32[]{:S(2)}) copy-start(f32[1,1,16,80]{3,2,1,0:T(8,128)S(1)} %fusion.3) | copy-start | bytes 15364
  34.9 26.2 %collective-permute-start.16 = (f32[3840]{0:T(1024)S(1)}, f32[3840]{0:T(1024)S(1)}, u32[]{:S(2)}, u32[]{:S(2)}) collective-permute-start(f32[3840]{0:T(1024)S(1)} %reshape.264), channel_id=1, source_target_pairs={{0,16},{4,20},{8,24},{12,28},{1,17},{5,21},{9,25},{13,29},{2,18},{... | collective-permute-start | bytes 46088 | tf_op jit(solution)/shard_map/ppermute | solution.py:63
  36.2 28.8 %collective-permute-start.14 = (f32[3840]{0:T(1024)S(1)}, f32[3840]{0:T(1024)}, u32[]{:S(2)}, u32[]{:S(2)}) collective-permute-start(f32[3840]{0:T(1024)S(1)} %reshape.264), channel_id=1, source_target_pairs={{0,12},{4,16},{8,20},{12,24},{16,28},{1,13},{5,17},{9,21},{13,25},... | collective-permute-start | bytes 46088 | tf_op jit(solution)/shard_map/ppermute | solution.py:63
  37.5 29.6 %collective-permute-start.15 = (f32[3840]{0:T(1024)S(1)}, f32[3840]{0:T(1024)}, u32[]{:S(2)}, u32[]{:S(2)}) collective-permute-start(f32[3840]{0:T(1024)S(1)} %reshape.264), channel_id=1, source_target_pairs={{12,0},{16,4},{20,8},{24,12},{28,16},{13,1},{17,5},{21,9},{25,13},... | collective-permute-start | bytes 46088 | tf_op jit(solution)/shard_map/ppermute | solution.py:63
  51.6 9.3 %copy-start.46 = (f32[1,3,32,160]{3,2,0,1:T(8,128)S(1)}, f32[1,3,32,160]{3,2,0,1:T(8,128)}, u32[]{:S(2)}) copy-start(f32[1,3,32,160]{3,2,0,1:T(8,128)} %get-tuple-element.76) | copy-start | bytes 184324
  51.6 9.4 %copy-start.45 = (f32[1,3,32,160]{3,2,0,1:T(8,128)S(1)}, f32[1,3,32,160]{3,2,0,1:T(8,128)}, u32[]{:S(2)}) copy-start(f32[1,3,32,160]{3,2,0,1:T(8,128)} %get-tuple-element.77) | copy-start | bytes 184324
  54.1 33.0 %collective-permute-start.2 = (f32[239360]{0:T(1024)}, f32[239360]{0:T(1024)}, u32[]{:S(2)}, u32[]{:S(2)}) collective-permute-start(f32[239360]{0:T(1024)} %get-tuple-element.80), channel_id=1, source_target_pairs={{0,4},{4,8},{8,12},{12,16},{16,20},{20,24},{24,28},{1,5},{5,9},{9,... | collective-permute-start | bytes 2872328 | tf_op jit(solution)/shard_map/ppermute | solution.py:63
  56.1 44.4 %collective-permute-start.3 = (f32[239360]{0:T(1024)}, f32[239360]{0:T(1024)}, u32[]{:S(2)}, u32[]{:S(2)}) collective-permute-start(f32[239360]{0:T(1024)} %get-tuple-element.81), channel_id=1, source_target_pairs={{4,0},{8,4},{12,8},{16,12},{20,16},{24,20},{28,24},{5,1},{9,5},{13... | collective-permute-start | bytes 2872328 | tf_op jit(solution)/shard_map/ppermute | solution.py:63
  61.8 20.5 %collective-permute-start.17 = (f32[3840]{0:T(1024)S(1)}, f32[3840]{0:T(1024)S(1)}, u32[]{:S(2)}, u32[]{:S(2)}) collective-permute-start(f32[3840]{0:T(1024)S(1)} %reshape.264), channel_id=1, source_target_pairs={{16,0},{20,4},{24,8},{28,12},{17,1},{21,5},{25,9},{29,13},{18,2},{... | collective-permute-start | bytes 46088 | tf_op jit(solution)/shard_map/ppermute | solution.py:63
  65.0 18.5 %collective-permute-start.7 = (f32[19200]{0:T(1024)S(1)}, f32[19200]{0:T(1024)S(1)}, u32[]{:S(2)}, u32[]{:S(2)}) collective-permute-start(f32[19200]{0:T(1024)S(1)} %get-tuple-element.117), channel_id=1, source_target_pairs={{8,0},{12,4},{16,8},{20,12},{24,16},{28,20},{9,1},{13,5},{17,9},{2... | collective-permute-start | bytes 230408 | tf_op jit(solution)/shard_map/ppermute | solution.py:63
  67.1 17.2 %collective-permute-start.6 = (f32[19200]{0:T(1024)S(1)}, f32[19200]{0:T(1024)S(1)}, u32[]{:S(2)}, u32[]{:S(2)}) collective-permute-start(f32[19200]{0:T(1024)S(1)} %get-tuple-element.116), channel_id=1, source_target_pairs={{0,8},{4,12},{8,16},{12,20},{16,24},{20,28},{1,9},{5,13},{9,17},{1... | collective-permute-start | bytes 230408 | tf_op jit(solution)/shard_map/ppermute | solution.py:63
  112.0 5.0 %copy-start.1 = (f32[8,1,64,320]{3,2,0,1:T(8,128)}, f32[8,1,64,320]{3,2,0,1:T(8,128)S(1)}, u32[]{:S(2)}) copy-start(f32[8,1,64,320]{3,2,0,1:T(8,128)S(1)} %get-tuple-element.16) | copy-start | bytes 1966084
  112.0 5.0 %copy-start.3 = (f32[8,64,320]{2,1,0:T(8,128)}, f32[8,64,320]{2,1,0:T(8,128)S(1)}, u32[]{:S(2)}) copy-start(f32[8,64,320]{2,1,0:T(8,128)S(1)} %get-tuple-element.17) | copy-start | bytes 1966084
  112.0 5.0 %copy-start.6 = (f32[8,64,320]{2,1,0:T(8,128)}, f32[8,64,320]{2,1,0:T(8,128)S(1)}, u32[]{:S(2)}) copy-start(f32[8,64,320]{2,1,0:T(8,128)S(1)} %get-tuple-element.18) | copy-start | bytes 1966084
  112.0 5.0 %copy-start.10 = (f32[8,64,320]{2,1,0:T(8,128)}, f32[8,64,320]{2,1,0:T(8,128)S(1)}, u32[]{:S(2)}) copy-start(f32[8,64,320]{2,1,0:T(8,128)S(1)} %get-tuple-element.14) | copy-start | bytes 1966084
  122.0 37.6 %collective-permute-start.5 = (f32[10240]{0:T(1024)}, f32[10240]{0:T(1024)}, u32[]{:S(2)}, u32[]{:S(2)}) collective-permute-start(f32[10240]{0:T(1024)} %reshape.272), channel_id=1, source_target_pairs={{4,0},{8,4},{12,8},{16,12},{20,16},{24,20},{28,24},{5,1},{9,5},{13... | collective-permute-start | bytes 122888 | tf_op jit(solution)/shard_map/ppermute | solution.py:63
  125.5 35.5 %collective-permute-start.4 = (f32[10240]{0:T(1024)}, f32[10240]{0:T(1024)}, u32[]{:S(2)}, u32[]{:S(2)}) collective-permute-start(f32[10240]{0:T(1024)} %reshape.272), channel_id=1, source_target_pairs={{0,4},{4,8},{8,12},{12,16},{16,20},{20,24},{24,28},{1,5},{5,9},{9,... | collective-permute-start | bytes 122888 | tf_op jit(solution)/shard_map/ppermute | solution.py:63
  134.9 10.4 %copy-start.49 = (f32[1,1,16,80]{3,2,1,0:T(8,128)S(1)}, f32[1,1,16,80]{3,2,1,0:T(8,128)}, u32[]{:S(2)}) copy-start(f32[1,1,16,80]{3,2,1,0:T(8,128)} %copy-done.48) | copy-start | bytes 15364
  134.9 10.4 %copy-start.51 = (f32[1,1,16,80]{3,2,1,0:T(8,128)S(1)}, f32[1,1,16,80]{3,2,1,0:T(8,128)}, u32[]{:S(2)}) copy-start(f32[1,1,16,80]{3,2,1,0:T(8,128)} %copy-done.50) | copy-start | bytes 15364
  166.7 16.2 %collective-permute-start.8 = (f32[1280]{0:T(1024)}, f32[1280]{0:T(1024)S(1)}, u32[]{:S(2)}, u32[]{:S(2)}) collective-permute-start(f32[1280]{0:T(1024)} %reshape.281), channel_id=1, source_target_pairs={{0,12},{4,16},{8,20},{12,24},{16,28},{1,13},{5,17},{9,21},{13,25},... | collective-permute-start | bytes 15368 | tf_op jit(solution)/shard_map/ppermute | solution.py:63
  169.3 22.0 %collective-permute-start.9 = (f32[1280]{0:T(1024)}, f32[1280]{0:T(1024)}, u32[]{:S(2)}, u32[]{:S(2)}) collective-permute-start(f32[1280]{0:T(1024)} %reshape.281), channel_id=1, source_target_pairs={{0,8},{4,12},{8,16},{12,20},{16,24},{20,28},{1,9},{5,13},{9,17},{1... | collective-permute-start | bytes 15368 | tf_op jit(solution)/shard_map/ppermute | solution.py:63
  170.6 22.1 %collective-permute-start.10 = (f32[1280]{0:T(1024)}, f32[1280]{0:T(1024)}, u32[]{:S(2)}, u32[]{:S(2)}) collective-permute-start(f32[1280]{0:T(1024)} %reshape.281), channel_id=1, source_target_pairs={{0,4},{4,8},{8,12},{12,16},{16,20},{20,24},{24,28},{1,5},{5,9},{9,... | collective-permute-start | bytes 15368 | tf_op jit(solution)/shard_map/ppermute | solution.py:63
  172.6 22.2 %collective-permute-start.11 = (f32[1280]{0:T(1024)}, f32[1280]{0:T(1024)}, u32[]{:S(2)}, u32[]{:S(2)}) collective-permute-start(f32[1280]{0:T(1024)} %reshape.281), channel_id=1, source_target_pairs={{4,0},{8,4},{12,8},{16,12},{20,16},{24,20},{28,24},{5,1},{9,5},{13... | collective-permute-start | bytes 15368 | tf_op jit(solution)/shard_map/ppermute | solution.py:63
  177.4 20.1 %collective-permute-start.12 = (f32[1280]{0:T(1024)}, f32[1280]{0:T(1024)}, u32[]{:S(2)}, u32[]{:S(2)}) collective-permute-start(f32[1280]{0:T(1024)} %reshape.281), channel_id=1, source_target_pairs={{8,0},{12,4},{16,8},{20,12},{24,16},{28,20},{9,1},{13,5},{17,9},{2... | collective-permute-start | bytes 15368 | tf_op jit(solution)/shard_map/ppermute | solution.py:63
  183.5 16.6 %collective-permute-start.13 = (f32[1280]{0:T(1024)}, f32[1280]{0:T(1024)}, u32[]{:S(2)}, u32[]{:S(2)}) collective-permute-start(f32[1280]{0:T(1024)} %reshape.281), channel_id=1, source_target_pairs={{12,0},{16,4},{20,8},{24,12},{28,16},{13,1},{17,5},{21,9},{25,13},... | collective-permute-start | bytes 15368 | tf_op jit(solution)/shard_map/ppermute | solution.py:63
  201.5 3.7 %copy-start.42 = (f32[7,15,80]{2,1,0:T(8,128)S(1)}, f32[7,15,80]{2,1,0:T(8,128)}, u32[]{:S(2)}) copy-start(f32[7,15,80]{2,1,0:T(8,128)} %fusion.142) | copy-start | bytes 100804
  201.5 3.7 %copy-start.47 = (f32[1,16,80]{2,1,0:T(8,128)S(1)}, f32[1,16,80]{2,1,0:T(8,128)}, u32[]{:S(2)}) copy-start(f32[1,16,80]{2,1,0:T(8,128)} %reshape.285) | copy-start | bytes 15364
  201.5 3.7 %copy-start.82 = (pred[3]{0:T(512)(128)(4,1)S(1)}, pred[3]{0:T(512)(128)(4,1)}, u32[]{:S(2)}) copy-start(pred[3]{0:T(512)(128)(4,1)} %compare_and_fusion.1) | copy-start | bytes 13
  201.5 3.9 %copy-start.79 = (s32[160]{0:T(256)S(1)}, s32[160]{0:T(256)}, u32[]{:S(2)}) copy-start(s32[160]{0:T(256)} %get-tuple-element.138) | copy-start | bytes 1924
  201.5 3.9 %copy-start.81 = (s32[160]{0:T(256)S(1)}, s32[160]{0:T(256)}, u32[]{:S(2)}) copy-start(s32[160]{0:T(256)} %get-tuple-element.139) | copy-start | bytes 1924
  201.5 3.9 %copy-start.95 = (pred[160]{0:T(512)(128)(4,1)S(1)}, pred[160]{0:T(512)(128)(4,1)}, u32[]{:S(2)}) copy-start(pred[160]{0:T(512)(128)(4,1)} %compare_and_fusion.4) | copy-start | bytes 484
  201.5 4.1 %copy-start.85 = (s32[32]{0:T(128)S(1)}, s32[32]{0:T(128)}, u32[]{:S(2)}) copy-start(s32[32]{0:T(128)} %get-tuple-element.140) | copy-start | bytes 388
  201.5 4.2 %copy-start.88 = (s32[32]{0:T(128)S(1)}, s32[32]{0:T(128)}, u32[]{:S(2)}) copy-start(s32[32]{0:T(128)} %get-tuple-element.141) | copy-start | bytes 388
  201.5 4.2 %copy-start.93 = (pred[32]{0:T(512)(128)(4,1)S(1)}, pred[32]{0:T(512)(128)(4,1)}, u32[]{:S(2)}) copy-start(pred[32]{0:T(512)(128)(4,1)} %compare_and_fusion.5) | copy-start | bytes 100
  201.5 4.4 %copy-start.16 = (f32[4,32,160]{2,1,0:T(8,128)S(1)}, f32[4,32,160]{2,1,0:T(8,128)}, u32[]{:S(2)}) copy-start(f32[4,32,160]{2,1,0:T(8,128)} %copy-done.15) | copy-start | bytes 245764
  208.1 6.5 %collective-permute-start.19 = (f32[10240]{0:T(1024)}, f32[10240]{0:T(1024)}, u32[]{:S(2)}, u32[]{:S(2)}) collective-permute-start(f32[10240]{0:T(1024)} %reshape.298), channel_id=1, source_target_pairs={{4,0},{8,4},{12,8},{16,12},{20,16},{24,20},{28,24},{5,1},{9,5},{13... | collective-permute-start | bytes 122888 | tf_op jit(solution)/shard_map/ppermute | solution.py:63
  210.0 7.1 %collective-permute-start.18 = (f32[10240]{0:T(1024)}, f32[10240]{0:T(1024)}, u32[]{:S(2)}, u32[]{:S(2)}) collective-permute-start(f32[10240]{0:T(1024)} %reshape.298), channel_id=1, source_target_pairs={{0,4},{4,8},{8,12},{12,16},{16,20},{20,24},{24,28},{1,5},{5,9},{9,... | collective-permute-start | bytes 122888 | tf_op jit(solution)/shard_map/ppermute | solution.py:63
  219.7 3.1 %copy-start.60 = (s32[64]{0:T(128)S(1)}, s32[64]{0:T(128)}, u32[]{:S(2)}) copy-start(s32[64]{0:T(128)} %copy-done.58) | copy-start | bytes 772
  219.8 3.1 %copy-start.63 = (s32[64]{0:T(128)S(1)}, s32[64]{0:T(128)}, u32[]{:S(2)}) copy-start(s32[64]{0:T(128)} %copy-done.61) | copy-start | bytes 772
  219.8 3.4 %copy-start.9 = (f32[6,64,320]{2,1,0:T(8,128)S(1)}, f32[6,64,320]{2,1,0:T(8,128)}, u32[]{:S(2)}) copy-start(f32[6,64,320]{2,1,0:T(8,128)} %copy-done.8) | copy-start | bytes 1474564
  226.7 13.7 %collective-permute-start.21 = (f32[61440]{0:T(1024)}, f32[61440]{0:T(1024)}, u32[]{:S(2)}, u32[]{:S(2)}) collective-permute-start(f32[61440]{0:T(1024)} %reshape.304), channel_id=1, source_target_pairs={{4,0},{8,4},{12,8},{16,12},{20,16},{24,20},{28,24},{5,1},{9,5},{13... | collective-permute-start | bytes 737288 | tf_op jit(solution)/shard_map/ppermute | solution.py:63
  230.5 8.5 %copy-start.4 = (f32[8,64,320]{2,1,0:T(8,128)S(1)}, f32[8,64,320]{2,1,0:T(8,128)}, u32[]{:S(2)}) copy-start(f32[8,64,320]{2,1,0:T(8,128)} %copy-done.3) | copy-start | bytes 1966084
  230.5 11.7 %collective-permute-start.20 = (f32[61440]{0:T(1024)}, f32[61440]{0:T(1024)}, u32[]{:S(2)}, u32[]{:S(2)}) collective-permute-start(f32[61440]{0:T(1024)} %reshape.302), channel_id=1, source_target_pairs={{0,4},{4,8},{8,12},{12,16},{16,20},{20,24},{24,28},{1,5},{5,9},{9,... | collective-permute-start | bytes 737288 | tf_op jit(solution)/shard_map/ppermute | solution.py:63
  (54 other events, 74.2 us)

commit v4 on v3

--- a/solution.py
+++ b/solution.py
@@ -1,5 +1,3 @@
-import math
-
 import jax
 import jax.numpy as jnp
 from jax import lax
@@ -43,37 +41,17 @@
     return jnp.concatenate([before, values, after], axis=-1)
 
 
-def alt_extend(items):
-    count = lax.axis_size("alt")
-    pieces = {}
-    for index, (values, halo) in enumerate(items):
-        depth = values.shape[0]
-        for distance in range(1, -(-halo // depth) + 1):
-            low = max(0, distance * depth - halo)
-            high = min(depth, halo - (distance - 1) * depth)
-            pieces.setdefault(("up", distance), []).append((index, values[low:]))
-            pieces.setdefault(("down", distance), []).append((index, values[:high]))
-    got = {}
-    for (way, distance), parts in pieces.items():
-        if way == "up":
-            route = [(i, i + distance) for i in range(count) if i + distance < count]
-        else:
-            route = [(i, i - distance) for i in range(count) if i - distance >= 0]
-        flat = jnp.concatenate([part.reshape(-1) for _, part in parts])
-        moved = lax.ppermute(flat, "alt", route)
-        start = 0
-        for index, part in parts:
-            size = part.size
-            got[(index, way, distance)] = moved[start:start + size].reshape(part.shape)
-            start += size
-    out = []
-    for index, (values, halo) in enumerate(items):
-        depth = values.shape[0]
-        reach = -(-halo // depth)
-        below = [got[(index, "up", d)] for d in range(reach, 0, -1)]
-        above = [got[(index, "down", d)] for d in range(1, reach + 1)]
-        out.append(jnp.concatenate(below + [values] + above, axis=0))
-    return out
+def alt_extend(values, halo):
+    count, depth = lax.axis_size("alt"), values.shape[0]
+    below, above = [], []
+    for distance in range(1, -(-halo // depth) + 1):
+        low = max(0, distance * depth - halo)
+        high = min(depth, halo - (distance - 1) * depth)
+        up = [(i, i + distance) for i in range(count) if i + distance < count]
+        down = [(i, i - distance) for i in range(count) if i - distance >= 0]
+        below.insert(0, lax.ppermute(values[low:], "alt", up))
+        above.append(lax.ppermute(values[:high], "alt", down))
+    return jnp.concatenate(below + [values] + above, axis=0)
 
 
 def trim(values, have, want):
@@ -151,45 +129,49 @@
     coef_two = [coarsen(part) for part in (wide_alt, wide_inc, wide_raan)]
     coef_three = [coarsen(part) for part in coef_two]
 
-    first, second, two_x, three_x = alt_extend(
-        [(wide[:, 0:2], 3), (wide[:, 2:4], 2), (jnp.stack(coef_two, 1), 3), (jnp.stack(coef_three, 1), 4)]
+    first = alt_extend(wide[:, 0:2], 1)
+    source_x = first[:, 0]
+    weights_one = make_weights(first[:, 1], wide_inc, wide_raan, 1.0, 0)
+
+    density = sweep(weights_one, source_x, 1, source_x, 1)
+    density = sweep(weights_one, alt_extend(density, 1), 1, source_x, 1)
+    applied, density = apply_op(weights_one, alt_extend(density, 1), 1)
+    rhs_two = coarsen(wide_source - applied)
+
+    level_two = alt_extend(jnp.stack([rhs_two] + coef_two, 1), 3)
+    weights_two = make_weights(
+        level_two[:, 1], trim(level_two[:, 2], 3, 2), trim(level_two[:, 3], 3, 2), 0.25, 2
     )
-    source_x, alt_x = first[:, 0], first[:, 1]
-    weights_one = make_weights(alt_x, second[:, 0], second[:, 1], 1.0, 2)
-    weights_two = make_weights(two_x[:, 0], trim(two_x[:, 1], 3, 2), trim(two_x[:, 2], 3, 2), 0.25, 2)
-    weights_three = make_weights(
-        three_x[:, 0], trim(three_x[:, 1], 4, 3), trim(three_x[:, 2], 4, 3), 0.0625, 3
-    )
-
-    density = sweep(weights_one, source_x, 3, source_x, 3)
-    density = sweep(weights_one, density, 2, source_x, 3)
-    applied, _ = apply_op(weights_one, density, 1)
-    rhs_two = coarsen(trim(source_x, 3, 0) - applied)
-    density = trim(density, 1, 0)
-
-    (rhs_two_x,) = alt_extend([(rhs_two, 2)])
+    rhs_two_x = trim(level_two[:, 0], 3, 2)
     correction = first_sweep(weights_two, rhs_two_x, 2)
     correction = sweep(weights_two, correction, 2, rhs_two_x, 2)
-    applied, _ = apply_op(weights_two, correction, 1)
+    applied, correction = apply_op(weights_two, correction, 1)
     rhs_three = coarsen(trim(rhs_two_x, 2, 0) - applied)
-    correction = trim(correction, 1, 0)
 
-    (rhs_three_x,) = alt_extend([(rhs_three, COARSE_SWEEPS - 1)])
-    coarse_part = first_sweep(weights_three, rhs_three_x, COARSE_SWEEPS - 1)
-    for halo in range(COARSE_SWEEPS - 1, 0, -1):
-        coarse_part = sweep(weights_three, coarse_part, halo, rhs_three_x, COARSE_SWEEPS - 1)
+    reach = COARSE_SWEEPS - 1
+    level_three = alt_extend(jnp.stack([rhs_three] + coef_three, 1), reach + 1)
+    weights_three = make_weights(
+        level_three[:, 1],
+        trim(level_three[:, 2], reach + 1, reach),
+        trim(level_three[:, 3], reach + 1, reach),
+        0.0625,
+        reach,
+    )
+    rhs_three_x = trim(level_three[:, 0], reach + 1, reach)
+    coarse_part = first_sweep(weights_three, rhs_three_x, reach)
+    for halo in range(reach, 0, -1):
+        coarse_part = sweep(weights_three, coarse_part, halo, rhs_three_x, reach)
 
     correction = correction + refine(coarse_part)
-    (correction,) = alt_extend([(correction, SWEEPS)])
+    correction = alt_extend(correction, SWEEPS)
     for halo in range(SWEEPS, 0, -1):
         correction = sweep(weights_two, correction, halo, rhs_two_x, 2)
 
     density = density + refine(correction)
-    (density,) = alt_extend([(density, SWEEPS + 1)])
-    for halo in range(SWEEPS + 1, 1, -1):
-        density = sweep(weights_one, density, halo, source_x, 3)
-    applied, centre = apply_op(weights_one, density, 1)
-    scaled_residual = (trim(source_x, 3, 0) - applied) / trim(weights_one[0][6], 2, 0)
+    for _ in range(SWEEPS):
+        density = sweep(weights_one, alt_extend(density, 1), 1, source_x, 1)
+    applied, centre = apply_op(weights_one, alt_extend(density, 1), 1)
+    scaled_residual = (wide_source - applied) / weights_one[0][6]
     keep = slice(halo_r, halo_r + length)
     return (centre[..., keep], scaled_residual[..., keep])
 

time: 258 us -> 169 us (0.66)
  the two profiles are of different devices: /device:TPU:26 before, /device:TPU:8 now
where the time goes in v4:
time: 169 us; the launch traced here: 167 us
  starting transfers between devices  85.2 us (50%)
  waiting for transfers between devices  39 us (23%)
  other arithmetic  23.9 us (14%)
  matrix products  9.67 us (6%)
  local copies, waits for them, and re-layouts  7.08 us (4%)
  between operations  2.07 us (1%)
    ppermute x13, starting transfers between devices, alt_extend(): below.insert(0, lax.ppermute(values[low:], 'alt', up))  48.7 us
    ppermute x13, starting transfers between devices, alt_extend(): above.append(lax.ppermute(values[:high], 'alt', down))  34.8 us
    ppermute x13, waiting for transfers between devices, alt_extend(): above.append(lax.ppermute(values[:high], 'alt', down))  18.6 us
    ppermute x13, waiting for transfers between devices, alt_extend(): below.insert(0, lax.ppermute(values[low:], 'alt', up))  14.4 us
    dot_general x8, matrix products, coarsen(): summed = jnp.matmul(summed, pairing(length), precision=HIGH)  6.71 us
    ppermute x1, waiting for transfers between devices, raan_extend(): before = lax.ppermute(values[..., length - halo:], 'raan', up)  5.42 us
    select_n x8, other arithmetic, sweep(): return jnp.where(inside(updated.shape, halo - 1), updated, 0.0)  4.31 us
  transfers between devices with their start and end apart: 28, of which 20 were waited for; matrix products, arithmetic and copies ran while one was open for 14% of the time, Pallas kernels for 0%

profile of v4, /device:TPU:8, one launch (start us, length us, event | category | flops | bytes accessed | tf_op | source)
XLA Modules:
  0.0 167.0 jit_solution(9121333274621581763)
XLA Ops:
  0.6 1.3 pad_maximum_fusion.1
  2.0 1.0 fusion.277
  3.0 1.7 %collective-permute-start.1 = (f32[4,4,64,32]{3,2,0,1:T(8,128)S(1)}, f32[4,4,64,32]{3,2,0,1:T(8,128)S(1)}, u32[]{:S(2)}, u32[]{:S(2)}) collective-permute-start(f32[4,4,64,32]{3,2,0,1:T(8,128)S(1)} %get-tuple-element.32), channel_id=1, source_target_pairs={{1,0},{2,1},{3,2},{0,3},{5,4},{6,5},{7,6},{4,7},{9,8},{10,9},{11,1... | collective-permute-start | bytes 393224 | tf_op jit(solution)/shard_map/ppermute | solution.py:40
  6.4 0.6 compare_and_fusion
  7.5 0.6 iota_shift-right-logical_fusion.1
  8.7 0.6 compare_and_fusion.7
  10.3 5.4 %collective-permute-done = f32[4,4,64,32]{3,2,0,1:T(8,128)S(1)} collective-permute-done((f32[4,4,64,32]{3,2,0,1:T(8,128)}, f32[4,4,64,32]{3,2,0,1:T(8,128)S(1)}, u32[]{:S(2)}, u32[]{:S(2)}) %collective-permute-start) | collective-permute-done | bytes 131104 | tf_op jit(solution)/shard_map/ppermute | solution.py:39
  15.8 0.7 collective-permute-done.1
  16.4 1.0 pad_maximum_fusion.27
  17.4 3.3 %collective-permute-start.3 = (f32[1,2,64,320]{3,2,0,1:T(8,128)}, f32[1,2,64,320]{3,2,0,1:T(8,128)}, u32[]{:S(2)}, u32[]{:S(2)}) collective-permute-start(f32[1,2,64,320]{3,2,0,1:T(8,128)} %get-tuple-element.23), channel_id=1, source_target_pairs={{4,0},{8,4},{12,8},{16,12},{20,16},{24,20},{28,24},{5,1},{9,5},{13... | collective-permute-start | bytes 491528 | tf_op jit(solution)/shard_map/ppermute | solution.py:53
  20.7 2.5 %collective-permute-start.2 = (f32[1,2,64,320]{3,2,0,1:T(8,128)}, f32[1,2,64,320]{3,2,0,1:T(8,128)}, u32[]{:S(2)}, u32[]{:S(2)}) collective-permute-start(f32[1,2,64,320]{3,2,0,1:T(8,128)} %get-tuple-element.24), channel_id=1, source_target_pairs={{0,4},{4,8},{8,12},{12,16},{16,20},{20,24},{24,28},{1,5},{5,9},{9,... | collective-permute-start | bytes 491528 | tf_op jit(solution)/shard_map/ppermute | solution.py:52
  23.3 1.6 pad_maximum_fusion
  24.9 1.0 fusion.276
  25.9 1.9 %reduce_sum.73 = f32[2,64,320]{2,1,0:T(8,128)} reduce(f32[2,2,64,320]{3,2,1,0:T(8,128)} %bitcast.309, f32[]{:T(128)} %constant.151.clone.1), dimensions={1}, to_apply=%region_1.2 | reduce | flops 40960 | bytes 491524 | tf_op jit(solution)/shard_map/reduce_sum | solution.py:21
  27.8 0.7 reduce_sum.74
  28.6 1.4 fusion.264
  29.9 1.1 fusion.260
  31.0 1.4 fusion.262
  33.0 1.0 fusion.121
  34.0 1.0 fusion.119
  36.9 2.0 %fusion.71 = (f32[4,64,320]{2,1,0:T(8,128)}, f32[4,64,320]{2,1,0:T(8,128)S(1)}, f32[4,64,320]{2,1,0:T(8,128)S(1)}, f32[4,64,320]{2,1,0:T(8,128)S(1)}, f32[4,64,320]{2,1,0:T(8,128)S(1)}) fusion(f32[4,63,320]{2,1,0:T(8,128)S(1)} %get-tuple-element.136, f32[4,2,64,320]{3,2,0,1:T(8,128)S(1)} %slice.911, f32[1,2,64,320]{3,2,0,1:T(8,128)} %collective-permute-done.2, ...), kind=kLoop, calls=%fused_computation.106 | loop fusion | flops 1310720 | bytes 4252672 | tf_op jit(solution)/shard_map/add | solution.py:80
  39.0 1.6 fusion.75
  40.6 4.3 %collective-permute-start.4 = (f32[1,64,320]{2,1,0:T(8,128)S(1)}, f32[1,64,320]{2,1,0:T(8,128)S(1)}, u32[]{:S(2)}, u32[]{:S(2)}) collective-permute-start(f32[1,64,320]{2,1,0:T(8,128)S(1)} %get-tuple-element.59), channel_id=1, source_target_pairs={{0,4},{4,8},{8,12},{12,16},{16,20},{20,24},{24,28},{1,5},{5,9},{9,... | collective-permute-start | bytes 245768 | tf_op jit(solution)/shard_map/ppermute | solution.py:52
  45.0 2.4 %collective-permute-start.5 = (f32[1,64,320]{2,1,0:T(8,128)S(1)}, f32[1,64,320]{2,1,0:T(8,128)S(1)}, u32[]{:S(2)}, u32[]{:S(2)}) collective-permute-start(f32[1,64,320]{2,1,0:T(8,128)S(1)} %get-tuple-element.60), channel_id=1, source_target_pairs={{4,0},{8,4},{12,8},{16,12},{20,16},{24,20},{28,24},{5,1},{9,5},{13... | collective-permute-start | bytes 245768 | tf_op jit(solution)/shard_map/ppermute | solution.py:53
  47.6 0.8 collective-permute-done.4
  48.4 3.2 %collective-permute-done.5 = f32[1,64,320]{2,1,0:T(8,128)S(1)} collective-permute-done((f32[1,64,320]{2,1,0:T(8,128)S(1)}, f32[1,64,320]{2,1,0:T(8,128)S(1)}, u32[]{:S(2)}, u32[]{:S(2)}) %collective-permute-start.5) | collective-permute-done | bytes 81952 | tf_op jit(solution)/shard_map/ppermute | solution.py:53
  52.1 3.4 %collective-permute-start.6 = (f32[1,64,320]{2,1,0:T(8,128)S(1)}, f32[1,64,320]{2,1,0:T(8,128)S(1)}, u32[]{:S(2)}, u32[]{:S(2)}) collective-permute-start(f32[1,64,320]{2,1,0:T(8,128)S(1)} %get-tuple-element.53), channel_id=1, source_target_pairs={{0,4},{4,8},{8,12},{12,16},{16,20},{20,24},{24,28},{1,5},{5,9},{9,... | collective-permute-start | bytes 245768 | tf_op jit(solution)/shard_map/ppermute | solution.py:52
  55.6 3.3 %collective-permute-start.7 = (f32[1,64,320]{2,1,0:T(8,128)S(1)}, f32[1,64,320]{2,1,0:T(8,128)S(1)}, u32[]{:S(2)}, u32[]{:S(2)}) collective-permute-start(f32[1,64,320]{2,1,0:T(8,128)S(1)} %get-tuple-element.54), channel_id=1, source_target_pairs={{4,0},{8,4},{12,8},{16,12},{20,16},{24,20},{28,24},{5,1},{9,5},{13... | collective-permute-start | bytes 245768 | tf_op jit(solution)/shard_map/ppermute | solution.py:53
  59.6 2.5 %collective-permute-done.7 = f32[1,64,320]{2,1,0:T(8,128)S(1)} collective-permute-done((f32[1,64,320]{2,1,0:T(8,128)S(1)}, f32[1,64,320]{2,1,0:T(8,128)S(1)}, u32[]{:S(2)}, u32[]{:S(2)}) %collective-permute-start.7) | collective-permute-done | bytes 81952 | tf_op jit(solution)/shard_map/ppermute | solution.py:53
  63.4 4.2 %collective-permute-start.9 = (f32[2,4,32,160]{3,2,0,1:T(8,128)S(1)}, f32[2,4,32,160]{3,2,0,1:T(8,128)S(1)}, u32[]{:S(2)}, u32[]{:S(2)}) collective-permute-start(f32[2,4,32,160]{3,2,0,1:T(8,128)S(1)} %pad_maximum_fusion.15), channel_id=1, source_target_pairs={{4,0},{8,4},{12,8},{16,12},{20,16},{24,20},{28,24},{5,1},{9,5},{13... | collective-permute-start | bytes 491528 | tf_op jit(solution)/shard_map/ppermute | solution.py:53
  67.7 2.0 %collective-permute-start.8 = (f32[2,4,32,160]{3,2,0,1:T(8,128)S(1)}, f32[2,4,32,160]{3,2,0,1:T(8,128)S(1)}, u32[]{:S(2)}, u32[]{:S(2)}) collective-permute-start(f32[2,4,32,160]{3,2,0,1:T(8,128)S(1)} %pad_maximum_fusion.15), channel_id=1, source_target_pairs={{0,4},{4,8},{8,12},{12,16},{16,20},{20,24},{24,28},{1,5},{5,9},{9,... | collective-permute-start | bytes 491528 | tf_op jit(solution)/shard_map/ppermute | solution.py:52
  69.7 3.7 %collective-permute-start.10 = (f32[1,4,32,160]{3,2,0,1:T(8,128)S(1)}, f32[1,4,32,160]{3,2,0,1:T(8,128)S(1)}, u32[]{:S(2)}, u32[]{:S(2)}) collective-permute-start(f32[1,4,32,160]{3,2,0,1:T(8,128)S(1)} %get-tuple-element.71), channel_id=1, source_target_pairs={{0,8},{4,12},{8,16},{12,20},{16,24},{20,28},{1,9},{5,13},{9,17},{1... | collective-permute-start | bytes 245768 | tf_op jit(solution)/shard_map/ppermute | solution.py:52
  73.5 2.1 %collective-permute-start.11 = (f32[1,4,32,160]{3,2,0,1:T(8,128)S(1)}, f32[1,4,32,160]{3,2,0,1:T(8,128)S(1)}, u32[]{:S(2)}, u32[]{:S(2)}) collective-permute-start(f32[1,4,32,160]{3,2,0,1:T(8,128)S(1)} %get-tuple-element.72), channel_id=1, source_target_pairs={{8,0},{12,4},{16,8},{20,12},{24,16},{28,20},{9,1},{13,5},{17,9},{2... | collective-permute-start | bytes 245768 | tf_op jit(solution)/shard_map/ppermute | solution.py:53
  75.8 2.1 %collective-permute-done.8 = f32[2,4,32,160]{3,2,0,1:T(8,128)S(1)} collective-permute-done((f32[2,4,32,160]{3,2,0,1:T(8,128)S(1)}, f32[2,4,32,160]{3,2,0,1:T(8,128)S(1)}, u32[]{:S(2)}, u32[]{:S(2)}) %collective-permute-start.8) | collective-permute-done | bytes 163872 | tf_op jit(solution)/shard_map/ppermute | solution.py:52
  78.2 2.1 %collective-permute-done.11 = f32[1,4,32,160]{3,2,0,1:T(8,128)S(1)} collective-permute-done((f32[1,4,32,160]{3,2,0,1:T(8,128)S(1)}, f32[1,4,32,160]{3,2,0,1:T(8,128)S(1)}, u32[]{:S(2)}, u32[]{:S(2)}) %collective-permute-start.11) | collective-permute-done | bytes 81952 | tf_op jit(solution)/shard_map/ppermute | solution.py:53
  80.9 0.8 fusion.116
  83.0 0.6 pad_maximum_fusion.30
  83.6 3.6 %collective-permute-start.18 = (f32[1,4,16,80]{3,2,0,1:T(8,128)}, f32[1,4,16,80]{3,2,0,1:T(8,128)}, u32[]{:S(2)}, u32[]{:S(2)}) collective-permute-start(f32[1,4,16,80]{3,2,0,1:T(8,128)} %pad_maximum_fusion.30), channel_id=1, source_target_pairs={{0,16},{4,20},{8,24},{12,28},{1,17},{5,21},{9,25},{13,29},{2,18},{... | collective-permute-start | bytes 61448 | tf_op jit(solution)/shard_map/ppermute | solution.py:52
  87.6 1.4 collective-permute-start.19
  89.1 1.3 collective-permute-start.17
  90.4 3.1 %collective-permute-start.16 = (f32[1,4,16,80]{3,2,0,1:T(8,128)}, f32[1,4,16,80]{3,2,0,1:T(8,128)S(1)}, u32[]{:S(2)}, u32[]{:S(2)}) collective-permute-start(f32[1,4,16,80]{3,2,0,1:T(8,128)} %pad_maximum_fusion.30), channel_id=1, source_target_pairs={{8,0},{12,4},{16,8},{20,12},{24,16},{28,20},{9,1},{13,5},{17,9},{2... | collective-permute-start | bytes 61448 | tf_op jit(solution)/shard_map/ppermute | solution.py:53
  93.5 2.2 %collective-permute-start.15 = (f32[1,4,16,80]{3,2,0,1:T(8,128)}, f32[1,4,16,80]{3,2,0,1:T(8,128)S(1)}, u32[]{:S(2)}, u32[]{:S(2)}) collective-permute-start(f32[1,4,16,80]{3,2,0,1:T(8,128)} %pad_maximum_fusion.30), channel_id=1, source_target_pairs={{4,0},{8,4},{12,8},{16,12},{20,16},{24,20},{28,24},{5,1},{9,5},{13... | collective-permute-start | bytes 61448 | tf_op jit(solution)/shard_map/ppermute | solution.py:53
  95.7 6.1 %collective-permute-start.12 = (f32[1,4,16,80]{3,2,0,1:T(8,128)}, f32[1,4,16,80]{3,2,0,1:T(8,128)S(1)}, u32[]{:S(2)}, u32[]{:S(2)}) collective-permute-start(f32[1,4,16,80]{3,2,0,1:T(8,128)} %pad_maximum_fusion.30), channel_id=1, source_target_pairs={{0,12},{4,16},{8,20},{12,24},{16,28},{1,13},{5,17},{9,21},{13,25},... | collective-permute-start | bytes 61448 | tf_op jit(solution)/shard_map/ppermute | solution.py:52
  101.8 0.8 constant_dynamic-update-slice_fusion.13
  102.6 1.1 collective-permute-done.12
  103.7 5.0 %collective-permute-start.13 = (f32[1,4,16,80]{3,2,0,1:T(8,128)}, f32[1,4,16,80]{3,2,0,1:T(8,128)S(1)}, u32[]{:S(2)}, u32[]{:S(2)}) collective-permute-start(f32[1,4,16,80]{3,2,0,1:T(8,128)} %pad_maximum_fusion.30), channel_id=1, source_target_pairs={{0,8},{4,12},{8,16},{12,20},{16,24},{20,28},{1,9},{5,13},{9,17},{1... | collective-permute-start | bytes 61448 | tf_op jit(solution)/shard_map/ppermute | solution.py:52
  108.7 1.9 %collective-permute-done.13 = f32[1,4,16,80]{3,2,0,1:T(8,128)S(1)} collective-permute-done((f32[1,4,16,80]{3,2,0,1:T(8,128)}, f32[1,4,16,80]{3,2,0,1:T(8,128)S(1)}, u32[]{:S(2)}, u32[]{:S(2)}) %collective-permute-start.13) | collective-permute-done | bytes 20512 | tf_op jit(solution)/shard_map/ppermute | solution.py:52
  110.6 3.0 %collective-permute-start.14 = (f32[1,4,16,80]{3,2,0,1:T(8,128)}, f32[1,4,16,80]{3,2,0,1:T(8,128)S(1)}, u32[]{:S(2)}, u32[]{:S(2)}) collective-permute-start(f32[1,4,16,80]{3,2,0,1:T(8,128)} %pad_maximum_fusion.30), channel_id=1, source_target_pairs={{0,4},{4,8},{8,12},{12,16},{16,20},{20,24},{24,28},{1,5},{5,9},{9,... | collective-permute-start | bytes 61448 | tf_op jit(solution)/shard_map/ppermute | solution.py:52
  113.6 3.9 %collective-permute-done.14 = f32[1,4,16,80]{3,2,0,1:T(8,128)S(1)} collective-permute-done((f32[1,4,16,80]{3,2,0,1:T(8,128)}, f32[1,4,16,80]{3,2,0,1:T(8,128)S(1)}, u32[]{:S(2)}, u32[]{:S(2)}) %collective-permute-start.14) | collective-permute-done | bytes 20512 | tf_op jit(solution)/shard_map/ppermute | solution.py:52
  117.5 0.7 constant_dynamic-update-slice_fusion.23
  118.2 0.7 constant_dynamic-update-slice_fusion.18
  120.5 1.9 %collective-permute-start.21 = (f32[2,32,160]{2,1,0:T(8,128)S(1)}, f32[2,32,160]{2,1,0:T(8,128)S(1)}, u32[]{:S(2)}, u32[]{:S(2)}) collective-permute-start(f32[2,32,160]{2,1,0:T(8,128)S(1)} %slice_add_fusion.2), channel_id=1, source_target_pairs={{4,0},{8,4},{12,8},{16,12},{20,16},{24,20},{28,24},{5,1},{9,5},{13... | collective-permute-start | bytes 122888 | tf_op jit(solution)/shard_map/ppermute | solution.py:53
  122.4 3.9 %collective-permute-start.20 = (f32[2,32,160]{2,1,0:T(8,128)S(1)}, f32[2,32,160]{2,1,0:T(8,128)S(1)}, u32[]{:S(2)}, u32[]{:S(2)}) collective-permute-start(f32[2,32,160]{2,1,0:T(8,128)S(1)} %slice_add_fusion.2), channel_id=1, source_target_pairs={{0,4},{4,8},{8,12},{12,16},{16,20},{20,24},{24,28},{1,5},{5,9},{9,... | collective-permute-start | bytes 122888 | tf_op jit(solution)/shard_map/ppermute | solution.py:52
  126.7 2.8 %collective-permute-done.20 = f32[2,32,160]{2,1,0:T(8,128)S(1)} collective-permute-done((f32[2,32,160]{2,1,0:T(8,128)S(1)}, f32[2,32,160]{2,1,0:T(8,128)S(1)}, u32[]{:S(2)}, u32[]{:S(2)}) %collective-permute-start.20) | collective-permute-done | bytes 40992 | tf_op jit(solution)/shard_map/ppermute | solution.py:52
  131.4 3.2 %collective-permute-start.22 = (f32[1,64,320]{2,1,0:T(8,128)S(1)}, f32[1,64,320]{2,1,0:T(8,128)S(1)}, u32[]{:S(2)}, u32[]{:S(2)}) collective-permute-start(f32[1,64,320]{2,1,0:T(8,128)S(1)} %get-tuple-element.47), channel_id=1, source_target_pairs={{0,4},{4,8},{8,12},{12,16},{16,20},{20,24},{24,28},{1,5},{5,9},{9,... | collective-permute-start | bytes 245768 | tf_op jit(solution)/shard_map/ppermute | solution.py:52
  134.6 3.9 %collective-permute-start.23 = (f32[1,64,320]{2,1,0:T(8,128)S(1)}, f32[1,64,320]{2,1,0:T(8,128)S(1)}, u32[]{:S(2)}, u32[]{:S(2)}) collective-permute-start(f32[1,64,320]{2,1,0:T(8,128)S(1)} %get-tuple-element.48), channel_id=1, source_target_pairs={{4,0},{8,4},{12,8},{16,12},{20,16},{24,20},{28,24},{5,1},{9,5},{13... | collective-permute-start | bytes 245768 | tf_op jit(solution)/shard_map/ppermute | solution.py:53
  138.9 3.7 %collective-permute-done.23 = f32[1,64,320]{2,1,0:T(8,128)S(1)} collective-permute-done((f32[1,64,320]{2,1,0:T(8,128)S(1)}, f32[1,64,320]{2,1,0:T(8,128)S(1)}, u32[]{:S(2)}, u32[]{:S(2)}) %collective-permute-start.23) | collective-permute-done | bytes 81952 | tf_op jit(solution)/shard_map/ppermute | solution.py:53
  143.3 3.8 %collective-permute-start.24 = (f32[1,64,320]{2,1,0:T(8,128)S(1)}, f32[1,64,320]{2,1,0:T(8,128)S(1)}, u32[]{:S(2)}, u32[]{:S(2)}) collective-permute-start(f32[1,64,320]{2,1,0:T(8,128)S(1)} %get-tuple-element.41), channel_id=1, source_target_pairs={{0,4},{4,8},{8,12},{12,16},{16,20},{20,24},{24,28},{1,5},{5,9},{9,... | collective-permute-start | bytes 245768 | tf_op jit(solution)/shard_map/ppermute | solution.py:52
  147.1 2.9 %collective-permute-start.25 = (f32[1,64,320]{2,1,0:T(8,128)S(1)}, f32[1,64,320]{2,1,0:T(8,128)S(1)}, u32[]{:S(2)}, u32[]{:S(2)}) collective-permute-start(f32[1,64,320]{2,1,0:T(8,128)S(1)} %get-tuple-element.42), channel_id=1, source_target_pairs={{4,0},{8,4},{12,8},{16,12},{20,16},{24,20},{28,24},{5,1},{9,5},{13... | collective-permute-start | bytes 245768 | tf_op jit(solution)/shard_map/ppermute | solution.py:53
  150.7 3.3 %collective-permute-done.25 = f32[1,64,320]{2,1,0:T(8,128)S(1)} collective-permute-done((f32[1,64,320]{2,1,0:T(8,128)S(1)}, f32[1,64,320]{2,1,0:T(8,128)S(1)}, u32[]{:S(2)}, u32[]{:S(2)}) %collective-permute-start.25) | collective-permute-done | bytes 81952 | tf_op jit(solution)/shard_map/ppermute | solution.py:53
  154.6 4.1 %collective-permute-start.26 = (f32[1,64,320]{2,1,0:T(8,128)S(1)}, f32[1,64,320]{2,1,0:T(8,128)S(1)}, u32[]{:S(2)}, u32[]{:S(2)}) collective-permute-start(f32[1,64,320]{2,1,0:T(8,128)S(1)} %get-tuple-element.37), channel_id=1, source_target_pairs={{0,4},{4,8},{8,12},{12,16},{16,20},{20,24},{24,28},{1,5},{5,9},{9,... | collective-permute-start | bytes 245768 | tf_op jit(solution)/shard_map/ppermute | solution.py:52
  158.7 2.6 %collective-permute-start.27 = (f32[1,64,320]{2,1,0:T(8,128)S(1)}, f32[1,64,320]{2,1,0:T(8,128)S(1)}, u32[]{:S(2)}, u32[]{:S(2)}) collective-permute-start(f32[1,64,320]{2,1,0:T(8,128)S(1)} %get-tuple-element.38), channel_id=1, source_target_pairs={{4,0},{8,4},{12,8},{16,12},{20,16},{24,20},{28,24},{5,1},{9,5},{13... | collective-permute-start | bytes 245768 | tf_op jit(solution)/shard_map/ppermute | solution.py:53
  162.0 3.2 %collective-permute-done.27 = f32[1,64,320]{2,1,0:T(8,128)S(1)} collective-permute-done((f32[1,64,320]{2,1,0:T(8,128)S(1)}, f32[1,64,320]{2,1,0:T(8,128)S(1)}, u32[]{:S(2)}, u32[]{:S(2)}) %collective-permute-start.27) | collective-permute-done | bytes 81952 | tf_op jit(solution)/shard_map/ppermute | solution.py:53
  165.4 1.5 fusion.83
  (240 shorter events, 18.2 us)
Async XLA Ops:
  1.9 14.5 %copy-start.8 = (f32[4,64,256]{2,1,0:T(8,128)S(1)}, f32[4,64,256]{2,1,0:T(8,128)}, u32[]{:S(2)}) copy-start(f32[4,64,256]{2,1,0:T(8,128)} %param.7) | copy-start | bytes 786436
  1.9 14.5 %copy-start.9 = (f32[4,64,256]{2,1,0:T(8,128)S(1)}, f32[4,64,256]{2,1,0:T(8,128)}, u32[]{:S(2)}) copy-start(f32[4,64,256]{2,1,0:T(8,128)} %param.6) | copy-start | bytes 786436
  1.9 14.5 %copy-start.10 = (f32[4,64,256]{2,1,0:T(8,128)S(1)}, f32[4,64,256]{2,1,0:T(8,128)}, u32[]{:S(2)}) copy-start(f32[4,64,256]{2,1,0:T(8,128)} %param.5) | copy-start | bytes 786436
  2.0 14.5 %copy-start.11 = (f32[4,64,256]{2,1,0:T(8,128)S(1)}, f32[4,64,256]{2,1,0:T(8,128)}, u32[]{:S(2)}) copy-start(f32[4,64,256]{2,1,0:T(8,128)} %param.4) | copy-start | bytes 786436
  3.0 12.8 %collective-permute-start = (f32[4,4,64,32]{3,2,0,1:T(8,128)}, f32[4,4,64,32]{3,2,0,1:T(8,128)S(1)}, u32[]{:S(2)}, u32[]{:S(2)}) collective-permute-start(f32[4,4,64,32]{3,2,0,1:T(8,128)} %get-tuple-element.31), channel_id=1, source_target_pairs={{0,1},{1,2},{2,3},{3,0},{4,5},{5,6},{6,7},{7,4},{8,9},{9,10},{10,1... | collective-permute-start | bytes 393224 | tf_op jit(solution)/shard_map/ppermute | solution.py:39
  3.0 13.4 %collective-permute-start.1 = (f32[4,4,64,32]{3,2,0,1:T(8,128)S(1)}, f32[4,4,64,32]{3,2,0,1:T(8,128)S(1)}, u32[]{:S(2)}, u32[]{:S(2)}) collective-permute-start(f32[4,4,64,32]{3,2,0,1:T(8,128)S(1)} %get-tuple-element.32), channel_id=1, source_target_pairs={{1,0},{2,1},{3,2},{0,3},{5,4},{6,5},{7,6},{4,7},{9,8},{10,9},{11,1... | collective-permute-start | bytes 393224 | tf_op jit(solution)/shard_map/ppermute | solution.py:40
  5.8 26.9 %copy-start.31 = (pred[64]{0:T(512)(128)(4,1)}, pred[64]{0:T(512)(128)(4,1)S(1)}, u32[]{:S(2)}) copy-start(pred[64]{0:T(512)(128)(4,1)S(1)} %compare_and_fusion.6) | copy-start | bytes 196
  7.5 25.3 %copy-start.34 = (s32[64]{0:T(128)}, s32[64]{0:T(128)S(1)}, u32[]{:S(2)}) copy-start(s32[64]{0:T(128)S(1)} %get-tuple-element.141) | copy-start | bytes 772
  7.5 25.3 %copy-start.37 = (s32[64]{0:T(128)}, s32[64]{0:T(128)S(1)}, u32[]{:S(2)}) copy-start(s32[64]{0:T(128)S(1)} %get-tuple-element.142) | copy-start | bytes 772
  10.3 20.7 %copy-start.44 = (s32[320]{0:T(512)}, s32[320]{0:T(512)S(1)}, u32[]{:S(2)}) copy-start(s32[320]{0:T(512)S(1)} %get-tuple-element.139) | copy-start | bytes 3844
  16.4 4.3 %copy-start.14 = (f32[4,4,64,32]{3,2,0,1:T(8,128)}, f32[4,4,64,32]{3,2,0,1:T(8,128)S(1)}, u32[]{:S(2)}) copy-start(f32[4,4,64,32]{3,2,0,1:T(8,128)S(1)} %collective-permute-done.1) | copy-start | bytes 393220
  17.4 19.5 %collective-permute-start.3 = (f32[1,2,64,320]{3,2,0,1:T(8,128)}, f32[1,2,64,320]{3,2,0,1:T(8,128)}, u32[]{:S(2)}, u32[]{:S(2)}) collective-permute-start(f32[1,2,64,320]{3,2,0,1:T(8,128)} %get-tuple-element.23), channel_id=1, source_target_pairs={{4,0},{8,4},{12,8},{16,12},{20,16},{24,20},{28,24},{5,1},{9,5},{13... | collective-permute-start | bytes 491528 | tf_op jit(solution)/shard_map/ppermute | solution.py:53
  20.7 16.2 %collective-permute-start.2 = (f32[1,2,64,320]{3,2,0,1:T(8,128)}, f32[1,2,64,320]{3,2,0,1:T(8,128)}, u32[]{:S(2)}, u32[]{:S(2)}) collective-permute-start(f32[1,2,64,320]{3,2,0,1:T(8,128)} %get-tuple-element.24), channel_id=1, source_target_pairs={{0,4},{4,8},{8,12},{12,16},{16,20},{20,24},{24,28},{1,5},{5,9},{9,... | collective-permute-start | bytes 491528 | tf_op jit(solution)/shard_map/ppermute | solution.py:52
  25.9 9.4 %copy-start.2 = (f32[4,64,320]{2,1,0:T(8,128)}, f32[4,64,320]{2,1,0:T(8,128)S(1)}, u32[]{:S(2)}) copy-start(f32[4,64,320]{2,1,0:T(8,128)S(1)} %get-tuple-element.30) | copy-start | bytes 983044
  28.5 6.4 %copy-start.49 = (s32[160]{0:T(256)S(1)}, s32[160]{0:T(256)}, u32[]{:S(2)}) copy-start(s32[160]{0:T(256)} %get-tuple-element.143) | copy-start | bytes 1924
  28.5 6.4 %copy-start.52 = (s32[160]{0:T(256)S(1)}, s32[160]{0:T(256)}, u32[]{:S(2)}) copy-start(s32[160]{0:T(256)} %get-tuple-element.144) | copy-start | bytes 1924
  28.5 6.4 %copy-start.65 = (pred[160]{0:T(512)(128)(4,1)S(1)}, pred[160]{0:T(512)(128)(4,1)}, u32[]{:S(2)}) copy-start(pred[160]{0:T(512)(128)(4,1)} %compare_and_fusion) | copy-start | bytes 484
  36.9 46.0 %copy-start.27 = (f32[1,1,16,80]{3,2,0,1:T(8,128)}, f32[1,1,16,80]{3,2,0,1:T(8,128)S(1)}, u32[]{:S(2)}) copy-start(f32[1,1,16,80]{3,2,0,1:T(8,128)S(1)} %fusion.1) | copy-start | bytes 15364
  36.9 2.0 %copy-start.40 = (pred[4]{0:T(512)(128)(4,1)S(1)}, pred[4]{0:T(512)(128)(4,1)}, u32[]{:S(2)}) copy-start(pred[4]{0:T(512)(128)(4,1)} %compare_and_fusion.7) | copy-start | bytes 16
  38.9 23.1 %copy-start = (f32[4,64,320]{2,1,0:T(8,128)}, f32[4,64,320]{2,1,0:T(8,128)S(1)}, u32[]{:S(2)}) copy-start(f32[4,64,320]{2,1,0:T(8,128)S(1)} %get-tuple-element.8) | copy-start | bytes 983044
  40.6 7.8 %collective-permute-start.4 = (f32[1,64,320]{2,1,0:T(8,128)S(1)}, f32[1,64,320]{2,1,0:T(8,128)S(1)}, u32[]{:S(2)}, u32[]{:S(2)}) collective-permute-start(f32[1,64,320]{2,1,0:T(8,128)S(1)} %get-tuple-element.59), channel_id=1, source_target_pairs={{0,4},{4,8},{8,12},{12,16},{16,20},{20,24},{24,28},{1,5},{5,9},{9,... | collective-permute-start | bytes 245768 | tf_op jit(solution)/shard_map/ppermute | solution.py:52
  45.0 6.6 %collective-permute-start.5 = (f32[1,64,320]{2,1,0:T(8,128)S(1)}, f32[1,64,320]{2,1,0:T(8,128)S(1)}, u32[]{:S(2)}, u32[]{:S(2)}) collective-permute-start(f32[1,64,320]{2,1,0:T(8,128)S(1)} %get-tuple-element.60), channel_id=1, source_target_pairs={{4,0},{8,4},{12,8},{16,12},{20,16},{24,20},{28,24},{5,1},{9,5},{13... | collective-permute-start | bytes 245768 | tf_op jit(solution)/shard_map/ppermute | solution.py:53
  52.1 7.5 %collective-permute-start.6 = (f32[1,64,320]{2,1,0:T(8,128)S(1)}, f32[1,64,320]{2,1,0:T(8,128)S(1)}, u32[]{:S(2)}, u32[]{:S(2)}) collective-permute-start(f32[1,64,320]{2,1,0:T(8,128)S(1)} %get-tuple-element.53), channel_id=1, source_target_pairs={{0,4},{4,8},{8,12},{12,16},{16,20},{20,24},{24,28},{1,5},{5,9},{9,... | collective-permute-start | bytes 245768 | tf_op jit(solution)/shard_map/ppermute | solution.py:52
  55.6 6.5 %collective-permute-start.7 = (f32[1,64,320]{2,1,0:T(8,128)S(1)}, f32[1,64,320]{2,1,0:T(8,128)S(1)}, u32[]{:S(2)}, u32[]{:S(2)}) collective-permute-start(f32[1,64,320]{2,1,0:T(8,128)S(1)} %get-tuple-element.54), channel_id=1, source_target_pairs={{4,0},{8,4},{12,8},{16,12},{20,16},{24,20},{28,24},{5,1},{9,5},{13... | collective-permute-start | bytes 245768 | tf_op jit(solution)/shard_map/ppermute | solution.py:53
  63.4 18.4 %copy-start.12 = (f32[32,2,160]{2,0,1:T(8,128)}, f32[32,2,160]{2,0,1:T(8,128)S(1)}, u32[]{:S(2)}) copy-start(f32[32,2,160]{2,0,1:T(8,128)S(1)} %convolution_multiply_fusion.3) | copy-start | bytes 122884
  63.4 12.4 %collective-permute-start.9 = (f32[2,4,32,160]{3,2,0,1:T(8,128)S(1)}, f32[2,4,32,160]{3,2,0,1:T(8,128)S(1)}, u32[]{:S(2)}, u32[]{:S(2)}) collective-permute-start(f32[2,4,32,160]{3,2,0,1:T(8,128)S(1)} %pad_maximum_fusion.15), channel_id=1, source_target_pairs={{4,0},{8,4},{12,8},{16,12},{20,16},{24,20},{28,24},{5,1},{9,5},{13... | collective-permute-start | bytes 491528 | tf_op jit(solution)/shard_map/ppermute | solution.py:53
  67.7 10.3 %collective-permute-start.8 = (f32[2,4,32,160]{3,2,0,1:T(8,128)S(1)}, f32[2,4,32,160]{3,2,0,1:T(8,128)S(1)}, u32[]{:S(2)}, u32[]{:S(2)}) collective-permute-start(f32[2,4,32,160]{3,2,0,1:T(8,128)S(1)} %pad_maximum_fusion.15), channel_id=1, source_target_pairs={{0,4},{4,8},{8,12},{12,16},{16,20},{20,24},{24,28},{1,5},{5,9},{9,... | collective-permute-start | bytes 491528 | tf_op jit(solution)/shard_map/ppermute | solution.py:52
  69.7 8.5 %collective-permute-start.10 = (f32[1,4,32,160]{3,2,0,1:T(8,128)S(1)}, f32[1,4,32,160]{3,2,0,1:T(8,128)S(1)}, u32[]{:S(2)}, u32[]{:S(2)}) collective-permute-start(f32[1,4,32,160]{3,2,0,1:T(8,128)S(1)} %get-tuple-element.71), channel_id=1, source_target_pairs={{0,8},{4,12},{8,16},{12,20},{16,24},{20,28},{1,9},{5,13},{9,17},{1... | collective-permute-start | bytes 245768 | tf_op jit(solution)/shard_map/ppermute | solution.py:52
  73.5 6.9 %collective-permute-start.11 = (f32[1,4,32,160]{3,2,0,1:T(8,128)S(1)}, f32[1,4,32,160]{3,2,0,1:T(8,128)S(1)}, u32[]{:S(2)}, u32[]{:S(2)}) collective-permute-start(f32[1,4,32,160]{3,2,0,1:T(8,128)S(1)} %get-tuple-element.72), channel_id=1, source_target_pairs={{8,0},{12,4},{16,8},{20,12},{24,16},{28,20},{9,1},{13,5},{17,9},{2... | collective-permute-start | bytes 245768 | tf_op jit(solution)/shard_map/ppermute | solution.py:53
  78.2 3.7 %copy-start.4 = (f32[6,31,160]{2,1,0:T(8,128)}, f32[6,31,160]{2,1,0:T(8,128)S(1)}, u32[]{:S(2)}) copy-start(f32[6,31,160]{2,1,0:T(8,128)S(1)} %fusion.84) | copy-start | bytes 357124
  80.5 1.3 copy-start.15
  80.6 1.3 copy-start.17
  80.9 1.5 copy-start.50
  80.9 1.5 copy-start.53
  80.9 1.5 copy-start.66
  83.6 12.1 %collective-permute-start.18 = (f32[1,4,16,80]{3,2,0,1:T(8,128)}, f32[1,4,16,80]{3,2,0,1:T(8,128)}, u32[]{:S(2)}, u32[]{:S(2)}) collective-permute-start(f32[1,4,16,80]{3,2,0,1:T(8,128)} %pad_maximum_fusion.30), channel_id=1, source_target_pairs={{0,16},{4,20},{8,24},{12,28},{1,17},{5,21},{9,25},{13,29},{2,18},{... | collective-permute-start | bytes 61448 | tf_op jit(solution)/shard_map/ppermute | solution.py:52
  87.6 31.8 %copy-start.56 = (pred[5]{0:T(512)(128)(4,1)S(1)}, pred[5]{0:T(512)(128)(4,1)}, u32[]{:S(2)}) copy-start(pred[5]{0:T(512)(128)(4,1)} %compare_and_fusion.1) | copy-start | bytes 19
  87.6 31.6 %collective-permute-start.19 = (f32[1,4,16,80]{3,2,0,1:T(8,128)}, f32[1,4,16,80]{3,2,0,1:T(8,128)S(1)}, u32[]{:S(2)}, u32[]{:S(2)}) collective-permute-start(f32[1,4,16,80]{3,2,0,1:T(8,128)} %pad_maximum_fusion.30), channel_id=1, source_target_pairs={{16,0},{20,4},{24,8},{28,12},{17,1},{21,5},{25,9},{29,13},{18,2},{... | collective-permute-start | bytes 61448 | tf_op jit(solution)/shard_map/ppermute | solution.py:53
  89.1 30.0 %collective-permute-start.17 = (f32[1,4,16,80]{3,2,0,1:T(8,128)}, f32[1,4,16,80]{3,2,0,1:T(8,128)S(1)}, u32[]{:S(2)}, u32[]{:S(2)}) collective-permute-start(f32[1,4,16,80]{3,2,0,1:T(8,128)} %pad_maximum_fusion.30), channel_id=1, source_target_pairs={{12,0},{16,4},{20,8},{24,12},{28,16},{13,1},{17,5},{21,9},{25,13},... | collective-permute-start | bytes 61448 | tf_op jit(solution)/shard_map/ppermute | solution.py:53
  90.4 28.6 %collective-permute-start.16 = (f32[1,4,16,80]{3,2,0,1:T(8,128)}, f32[1,4,16,80]{3,2,0,1:T(8,128)S(1)}, u32[]{:S(2)}, u32[]{:S(2)}) collective-permute-start(f32[1,4,16,80]{3,2,0,1:T(8,128)} %pad_maximum_fusion.30), channel_id=1, source_target_pairs={{8,0},{12,4},{16,8},{20,12},{24,16},{28,20},{9,1},{13,5},{17,9},{2... | collective-permute-start | bytes 61448 | tf_op jit(solution)/shard_map/ppermute | solution.py:53
  93.5 25.5 %collective-permute-start.15 = (f32[1,4,16,80]{3,2,0,1:T(8,128)}, f32[1,4,16,80]{3,2,0,1:T(8,128)S(1)}, u32[]{:S(2)}, u32[]{:S(2)}) collective-permute-start(f32[1,4,16,80]{3,2,0,1:T(8,128)} %pad_maximum_fusion.30), channel_id=1, source_target_pairs={{4,0},{8,4},{12,8},{16,12},{20,16},{24,20},{28,24},{5,1},{9,5},{13... | collective-permute-start | bytes 61448 | tf_op jit(solution)/shard_map/ppermute | solution.py:53
  95.7 8.0 %collective-permute-start.12 = (f32[1,4,16,80]{3,2,0,1:T(8,128)}, f32[1,4,16,80]{3,2,0,1:T(8,128)S(1)}, u32[]{:S(2)}, u32[]{:S(2)}) collective-permute-start(f32[1,4,16,80]{3,2,0,1:T(8,128)} %pad_maximum_fusion.30), channel_id=1, source_target_pairs={{0,12},{4,16},{8,20},{12,24},{16,28},{1,13},{5,17},{9,21},{13,25},... | collective-permute-start | bytes 61448 | tf_op jit(solution)/shard_map/ppermute | solution.py:52
  103.7 6.9 %collective-permute-start.13 = (f32[1,4,16,80]{3,2,0,1:T(8,128)}, f32[1,4,16,80]{3,2,0,1:T(8,128)S(1)}, u32[]{:S(2)}, u32[]{:S(2)}) collective-permute-start(f32[1,4,16,80]{3,2,0,1:T(8,128)} %pad_maximum_fusion.30), channel_id=1, source_target_pairs={{0,8},{4,12},{8,16},{12,20},{16,24},{20,28},{1,9},{5,13},{9,17},{1... | collective-permute-start | bytes 61448 | tf_op jit(solution)/shard_map/ppermute | solution.py:52
  110.6 6.9 %collective-permute-start.14 = (f32[1,4,16,80]{3,2,0,1:T(8,128)}, f32[1,4,16,80]{3,2,0,1:T(8,128)S(1)}, u32[]{:S(2)}, u32[]{:S(2)}) collective-permute-start(f32[1,4,16,80]{3,2,0,1:T(8,128)} %pad_maximum_fusion.30), channel_id=1, source_target_pairs={{0,4},{4,8},{8,12},{12,16},{16,20},{20,24},{24,28},{1,5},{5,9},{9,... | collective-permute-start | bytes 61448 | tf_op jit(solution)/shard_map/ppermute | solution.py:52
  119.5 10.2 %copy-start.5 = (f32[6,31,160]{2,1,0:T(8,128)S(1)}, f32[6,31,160]{2,1,0:T(8,128)}, u32[]{:S(2)}) copy-start(f32[6,31,160]{2,1,0:T(8,128)} %copy-done.4) | copy-start | bytes 357124
  119.5 10.2 %copy-start.16 = (f32[6,32,160]{2,1,0:T(8,128)S(1)}, f32[6,32,160]{2,1,0:T(8,128)}, u32[]{:S(2)}) copy-start(f32[6,32,160]{2,1,0:T(8,128)} %copy-done.15) | copy-start | bytes 368644
  119.5 10.2 %copy-start.18 = (f32[6,1,32,160]{3,2,0,1:T(8,128)S(1)}, f32[6,1,32,160]{3,2,0,1:T(8,128)}, u32[]{:S(2)}) copy-start(f32[6,1,32,160]{3,2,0,1:T(8,128)} %copy-done.17) | copy-start | bytes 368644
  119.5 10.2 %copy-start.20 = (f32[6,1,32,160]{3,2,0,1:T(8,128)S(1)}, f32[6,1,32,160]{3,2,0,1:T(8,128)}, u32[]{:S(2)}) copy-start(f32[6,1,32,160]{3,2,0,1:T(8,128)} %copy-done.19) | copy-start | bytes 368644
  119.5 10.2 %copy-start.22 = (f32[6,32,160]{2,1,0:T(8,128)S(1)}, f32[6,32,160]{2,1,0:T(8,128)}, u32[]{:S(2)}) copy-start(f32[6,32,160]{2,1,0:T(8,128)} %copy-done.21) | copy-start | bytes 368644
  119.5 10.2 %copy-start.24 = (f32[6,32,160]{2,1,0:T(8,128)S(1)}, f32[6,32,160]{2,1,0:T(8,128)}, u32[]{:S(2)}) copy-start(f32[6,32,160]{2,1,0:T(8,128)} %copy-done.23) | copy-start | bytes 368644
  119.5 10.2 %copy-start.26 = (f32[4,32,160]{2,1,0:T(8,128)S(1)}, f32[4,32,160]{2,1,0:T(8,128)}, u32[]{:S(2)}) copy-start(f32[4,32,160]{2,1,0:T(8,128)} %get-tuple-element.16) | copy-start | bytes 245764
  119.5 10.2 %copy-start.43 = (pred[4]{0:T(512)(128)(4,1)S(1)}, pred[4]{0:T(512)(128)(4,1)}, u32[]{:S(2)}) copy-start(pred[4]{0:T(512)(128)(4,1)} %compare_and_fusion.4) | copy-start | bytes 16
  120.5 6.2 %collective-permute-start.21 = (f32[2,32,160]{2,1,0:T(8,128)S(1)}, f32[2,32,160]{2,1,0:T(8,128)S(1)}, u32[]{:S(2)}, u32[]{:S(2)}) collective-permute-start(f32[2,32,160]{2,1,0:T(8,128)S(1)} %slice_add_fusion.2), channel_id=1, source_target_pairs={{4,0},{8,4},{12,8},{16,12},{20,16},{24,20},{28,24},{5,1},{9,5},{13... | collective-permute-start | bytes 122888 | tf_op jit(solution)/shard_map/ppermute | solution.py:53
  122.4 7.1 %collective-permute-start.20 = (f32[2,32,160]{2,1,0:T(8,128)S(1)}, f32[2,32,160]{2,1,0:T(8,128)S(1)}, u32[]{:S(2)}, u32[]{:S(2)}) collective-permute-start(f32[2,32,160]{2,1,0:T(8,128)S(1)} %slice_add_fusion.2), channel_id=1, source_target_pairs={{0,4},{4,8},{8,12},{12,16},{16,20},{20,24},{24,28},{1,5},{5,9},{9,... | collective-permute-start | bytes 122888 | tf_op jit(solution)/shard_map/ppermute | solution.py:52
  131.3 11.4 %copy-start.1 = (f32[4,64,320]{2,1,0:T(8,128)S(1)}, f32[4,64,320]{2,1,0:T(8,128)}, u32[]{:S(2)}) copy-start(f32[4,64,320]{2,1,0:T(8,128)} %copy-done) | copy-start | bytes 983044
  131.3 11.3 %copy-start.41 = (pred[4]{0:T(512)(128)(4,1)S(1)}, pred[4]{0:T(512)(128)(4,1)}, u32[]{:S(2)}) copy-start(pred[4]{0:T(512)(128)(4,1)} %compare_and_fusion.7) | copy-start | bytes 16
  131.4 7.5 %collective-permute-start.22 = (f32[1,64,320]{2,1,0:T(8,128)S(1)}, f32[1,64,320]{2,1,0:T(8,128)S(1)}, u32[]{:S(2)}, u32[]{:S(2)}) collective-permute-start(f32[1,64,320]{2,1,0:T(8,128)S(1)} %get-tuple-element.47), channel_id=1, source_target_pairs={{0,4},{4,8},{8,12},{12,16},{16,20},{20,24},{24,28},{1,5},{5,9},{9,... | collective-permute-start | bytes 245768 | tf_op jit(solution)/shard_map/ppermute | solution.py:52
  134.6 8.1 %collective-permute-start.23 = (f32[1,64,320]{2,1,0:T(8,128)S(1)}, f32[1,64,320]{2,1,0:T(8,128)S(1)}, u32[]{:S(2)}, u32[]{:S(2)}) collective-permute-start(f32[1,64,320]{2,1,0:T(8,128)S(1)} %get-tuple-element.48), channel_id=1, source_target_pairs={{4,0},{8,4},{12,8},{16,12},{20,16},{24,20},{28,24},{5,1},{9,5},{13... | collective-permute-start | bytes 245768 | tf_op jit(solution)/shard_map/ppermute | solution.py:53
  143.3 7.4 %collective-permute-start.24 = (f32[1,64,320]{2,1,0:T(8,128)S(1)}, f32[1,64,320]{2,1,0:T(8,128)S(1)}, u32[]{:S(2)}, u32[]{:S(2)}) collective-permute-start(f32[1,64,320]{2,1,0:T(8,128)S(1)} %get-tuple-element.41), channel_id=1, source_target_pairs={{0,4},{4,8},{8,12},{12,16},{16,20},{20,24},{24,28},{1,5},{5,9},{9,... | collective-permute-start | bytes 245768 | tf_op jit(solution)/shard_map/ppermute | solution.py:52
  147.1 6.9 %collective-permute-start.25 = (f32[1,64,320]{2,1,0:T(8,128)S(1)}, f32[1,64,320]{2,1,0:T(8,128)S(1)}, u32[]{:S(2)}, u32[]{:S(2)}) collective-permute-start(f32[1,64,320]{2,1,0:T(8,128)S(1)} %get-tuple-element.42), channel_id=1, source_target_pairs={{4,0},{8,4},{12,8},{16,12},{20,16},{24,20},{28,24},{5,1},{9,5},{13... | collective-permute-start | bytes 245768 | tf_op jit(solution)/shard_map/ppermute | solution.py:53
  154.6 7.4 %collective-permute-start.26 = (f32[1,64,320]{2,1,0:T(8,128)S(1)}, f32[1,64,320]{2,1,0:T(8,128)S(1)}, u32[]{:S(2)}, u32[]{:S(2)}) collective-permute-start(f32[1,64,320]{2,1,0:T(8,128)S(1)} %get-tuple-element.37), channel_id=1, source_target_pairs={{0,4},{4,8},{8,12},{12,16},{16,20},{20,24},{24,28},{1,5},{5,9},{9,... | collective-permute-start | bytes 245768 | tf_op jit(solution)/shard_map/ppermute | solution.py:52
  158.7 6.5 %collective-permute-start.27 = (f32[1,64,320]{2,1,0:T(8,128)S(1)}, f32[1,64,320]{2,1,0:T(8,128)S(1)}, u32[]{:S(2)}, u32[]{:S(2)}) collective-permute-start(f32[1,64,320]{2,1,0:T(8,128)S(1)} %get-tuple-element.38), channel_id=1, source_target_pairs={{4,0},{8,4},{12,8},{16,12},{20,16},{24,20},{28,24},{5,1},{9,5},{13... | collective-permute-start | bytes 245768 | tf_op jit(solution)/shard_map/ppermute | solution.py:53
  161.5 3.9 %copy-start.3 = (f32[4,64,320]{2,1,0:T(8,128)S(1)}, f32[4,64,320]{2,1,0:T(8,128)}, u32[]{:S(2)}) copy-start(f32[4,64,320]{2,1,0:T(8,128)} %copy-done.2) | copy-start | bytes 983044
  161.5 3.9 %copy-start.25 = (f32[4,64,320]{2,1,0:T(8,128)S(1)}, f32[4,64,320]{2,1,0:T(8,128)}, u32[]{:S(2)}) copy-start(f32[4,64,320]{2,1,0:T(8,128)} %get-tuple-element.4) | copy-start | bytes 983044
  (32 other events, 29.4 us)

commit v5 on v4

--- a/solution.py
+++ b/solution.py
@@ -109,11 +109,18 @@
     return (rows >= 0) & (rows < depth * lax.axis_size("alt"))
 
 
-def sweep(weights, field, halo, target, target_halo):
+def sweep(weights, field, halo, target, target_halo, masked=True):
     applied, centre = apply_op(weights, field, halo)
     diagonal = trim(weights[0][6], weights[1], halo - 1)
     updated = centre + OMEGA * (trim(target, target_halo, halo - 1) - applied) / diagonal
+    if not masked:
+        return updated
     return jnp.where(inside(updated.shape, halo - 1), updated, 0.0)
+
+
+def pad_rows(values):
+    zero = jnp.zeros_like(values[:1])
+    return jnp.concatenate([zero, values, zero], axis=0)
 
 
 def first_sweep(weights, target, halo):
@@ -148,19 +155,14 @@
     applied, correction = apply_op(weights_two, correction, 1)
     rhs_three = coarsen(trim(rhs_two_x, 2, 0) - applied)
 
-    reach = COARSE_SWEEPS - 1
-    level_three = alt_extend(jnp.stack([rhs_three] + coef_three, 1), reach + 1)
-    weights_three = make_weights(
-        level_three[:, 1],
-        trim(level_three[:, 2], reach + 1, reach),
-        trim(level_three[:, 3], reach + 1, reach),
-        0.0625,
-        reach,
-    )
-    rhs_three_x = trim(level_three[:, 0], reach + 1, reach)
-    coarse_part = first_sweep(weights_three, rhs_three_x, reach)
-    for halo in range(reach, 0, -1):
-        coarse_part = sweep(weights_three, coarse_part, halo, rhs_three_x, reach)
+    height = rhs_three.shape[0]
+    column = lax.all_gather(jnp.stack([rhs_three] + coef_three, 1), "alt", axis=0, tiled=True)
+    weights_three = make_weights(pad_rows(column[:, 1]), column[:, 2], column[:, 3], 0.0625, 0)
+    rhs_three_x = column[:, 0]
+    coarse_part = first_sweep(weights_three, rhs_three_x, 0)
+    for _ in range(COARSE_SWEEPS - 1):
+        coarse_part = sweep(weights_three, pad_rows(coarse_part), 1, rhs_three_x, 0, masked=False)
+    coarse_part = lax.dynamic_slice_in_dim(coarse_part, lax.axis_index("alt") * height, height, 0)
 
     correction = correction + refine(coarse_part)
     correction = alt_extend(correction, SWEEPS)

time: 169 us -> 158 us (0.935)
  the two profiles are of different devices: /device:TPU:8 before, /device:TPU:0 now
where the time goes in v5:
time: 158 us; the launch traced here: 157 us
  starting transfers between devices  50.3 us (32%)
  waiting for transfers between devices  41.1 us (26%)
  blocking collectives  30.9 us (20%)
  other arithmetic  18.8 us (12%)
  matrix products  9.75 us (6%)
  local copies, waits for them, and re-layouts  4.69 us (3%)
    ppermute x9, starting transfers between devices, alt_extend(): below.insert(0, lax.ppermute(values[low:], 'alt', up))  36.2 us
    all_gather x1, blocking collectives, shards(): lax.all_gather(jnp.stack([rhs_three] + coef_three, 1), 'alt', axis=0, til...  30.9 us
    ppermute x9, waiting for transfers between devices, alt_extend(): above.append(lax.ppermute(values[:high], 'alt', down))  24.1 us
    ppermute x9, starting transfers between devices, alt_extend(): above.append(lax.ppermute(values[:high], 'alt', down))  11.6 us
    ppermute x9, waiting for transfers between devices, alt_extend(): below.insert(0, lax.ppermute(values[low:], 'alt', up))  9.3 us
    dot_general x8, matrix products, coarsen(): summed = jnp.matmul(summed, pairing(length), precision=HIGH)  6.7 us
    ppermute x1, waiting for transfers between devices, raan_extend(): before = lax.ppermute(values[..., length - halo:], 'raan', up)  5.21 us
    select_n x6, other arithmetic, sweep(): return jnp.where(inside(updated.shape, halo - 1), updated, 0.0)  3.36 us
  transfers between devices with their start and end apart: 20, of which 16 were waited for; matrix products, arithmetic and copies ran while one was open for 12% of the time, Pallas kernels for 0%

profile of v5, /device:TPU:0, one launch (start us, length us, event | category | flops | bytes accessed | tf_op | source)
XLA Modules:
  0.0 156.9 jit_solution(6809176553383007722)
XLA Ops:
  0.6 1.3 pad_maximum_fusion.1
  2.2 0.5 collective-permute-start
  2.7 2.0 %collective-permute-start.1 = (f32[4,4,64,32]{3,2,0,1:T(8,128)S(1)}, f32[4,4,64,32]{3,2,0,1:T(8,128)S(1)}, u32[]{:S(2)}, u32[]{:S(2)}) collective-permute-start(f32[4,4,64,32]{3,2,0,1:T(8,128)S(1)} %get-tuple-element.32), channel_id=1, source_target_pairs={{1,0},{2,1},{3,2},{0,3},{5,4},{6,5},{7,6},{4,7},{9,8},{10,9},{11,1... | collective-permute-start | bytes 393224 | tf_op jit(solution)/shard_map/ppermute | solution.py:40
  4.7 0.5 broadcast_add_fusion.2
  5.2 0.6 iota_shift-right-logical_fusion.2
  5.8 0.5 compare_and_fusion.1
  6.3 0.6 compare_and_fusion
  6.9 0.5 fusion.241
  7.4 0.6 iota_shift-right-logical_fusion.1
  8.0 0.6 compare_and_fusion.2
  8.6 0.6 iota_shift-right-logical_fusion
  9.2 5.2 %collective-permute-done = f32[4,4,64,32]{3,2,0,1:T(8,128)S(1)} collective-permute-done((f32[4,4,64,32]{3,2,0,1:T(8,128)S(1)}, f32[4,4,64,32]{3,2,0,1:T(8,128)S(1)}, u32[]{:S(2)}, u32[]{:S(2)}) %collective-permute-start) | collective-permute-done | bytes 131104 | tf_op jit(solution)/shard_map/ppermute | solution.py:39
  14.4 2.5 %collective-permute-done.1 = f32[4,4,64,32]{3,2,0,1:T(8,128)S(1)} collective-permute-done((f32[4,4,64,32]{3,2,0,1:T(8,128)S(1)}, f32[4,4,64,32]{3,2,0,1:T(8,128)S(1)}, u32[]{:S(2)}, u32[]{:S(2)}) %collective-permute-start.1) | collective-permute-done | bytes 131104 | tf_op jit(solution)/shard_map/ppermute | solution.py:40
  16.9 1.0 pad_maximum_fusion.27
  17.9 1.3 collective-permute-start.3
  19.2 5.2 %collective-permute-start.2 = (f32[1,2,64,320]{3,2,0,1:T(8,128)}, f32[1,2,64,320]{3,2,0,1:T(8,128)}, u32[]{:S(2)}, u32[]{:S(2)}) collective-permute-start(f32[1,2,64,320]{3,2,0,1:T(8,128)} %get-tuple-element.24), channel_id=1, source_target_pairs={{0,4},{4,8},{8,12},{12,16},{16,20},{20,24},{24,28},{1,5},{5,9},{9,... | collective-permute-start | bytes 491528 | tf_op jit(solution)/shard_map/ppermute | solution.py:52
  24.4 1.6 %pad_maximum_fusion = f32[4,4,64,320]{3,2,0,1:T(8,128)S(1)} fusion(f32[4,4,64,32]{3,2,0,1:T(8,128)} %copy-done.4, f32[4,1,64,256]{3,2,0,1:T(8,128)S(1)} %bitcast.224, f32[4,1,64,256]{3,2,0,1:T(8,128)S(1)} %bitcast.227, f32[4,1,64,256]{3,2,0,1:T(8,128)S(1)} %bitcast.230, f32[4,1,64,256]{3,2,0,1:T(8,128)S(1)} %bitcast.233, ...), kind=kLoop, calls=%fused_computation | loop fusion | flops 1638400 | bytes 2621440 | tf_op jit(solution)/shard_map/concatenate | solution.py:41
  26.1 1.0 fusion.267
  27.1 1.7 %reduce_sum.73 = f32[2,64,320]{2,1,0:T(8,128)} reduce(f32[2,2,64,320]{3,2,1,0:T(8,128)} %bitcast.252, f32[]{:T(128)} %constant.135.clone.1), dimensions={1}, to_apply=%region_1.2 | reduce | flops 40960 | bytes 491524 | tf_op jit(solution)/shard_map/reduce_sum | solution.py:21
  28.8 0.7 reduce_sum.74
  29.6 1.4 fusion.256
  30.9 1.1 fusion.252
  32.0 1.4 fusion.254
  34.0 1.0 fusion.122
  34.9 1.0 fusion.120
  37.9 1.3 fusion.72
  39.2 1.4 fusion.76
  40.7 3.7 %collective-permute-start.4 = (f32[1,64,320]{2,1,0:T(8,128)S(1)}, f32[1,64,320]{2,1,0:T(8,128)S(1)}, u32[]{:S(2)}, u32[]{:S(2)}) collective-permute-start(f32[1,64,320]{2,1,0:T(8,128)S(1)} %get-tuple-element.59), channel_id=1, source_target_pairs={{0,4},{4,8},{8,12},{12,16},{16,20},{20,24},{24,28},{1,5},{5,9},{9,... | collective-permute-start | bytes 245768 | tf_op jit(solution)/shard_map/ppermute | solution.py:52
  44.4 1.3 collective-permute-start.5
  45.8 1.0 collective-permute-done.4
  46.8 4.1 %collective-permute-done.5 = f32[1,64,320]{2,1,0:T(8,128)S(1)} collective-permute-done((f32[1,64,320]{2,1,0:T(8,128)S(1)}, f32[1,64,320]{2,1,0:T(8,128)S(1)}, u32[]{:S(2)}, u32[]{:S(2)}) %collective-permute-start.5) | collective-permute-done | bytes 81952 | tf_op jit(solution)/shard_map/ppermute | solution.py:53
  50.9 0.5 fusion.73
  51.5 3.4 %collective-permute-start.6 = (f32[1,64,320]{2,1,0:T(8,128)S(1)}, f32[1,64,320]{2,1,0:T(8,128)S(1)}, u32[]{:S(2)}, u32[]{:S(2)}) collective-permute-start(f32[1,64,320]{2,1,0:T(8,128)S(1)} %get-tuple-element.53), channel_id=1, source_target_pairs={{0,4},{4,8},{8,12},{12,16},{16,20},{20,24},{24,28},{1,5},{5,9},{9,... | collective-permute-start | bytes 245768 | tf_op jit(solution)/shard_map/ppermute | solution.py:52
  54.9 1.3 collective-permute-start.7
  56.4 0.7 collective-permute-done.6
  57.1 4.3 %collective-permute-done.7 = f32[1,64,320]{2,1,0:T(8,128)S(1)} collective-permute-done((f32[1,64,320]{2,1,0:T(8,128)S(1)}, f32[1,64,320]{2,1,0:T(8,128)S(1)}, u32[]{:S(2)}, u32[]{:S(2)}) %collective-permute-start.7) | collective-permute-done | bytes 81952 | tf_op jit(solution)/shard_map/ppermute | solution.py:53
  61.5 0.5 bitcast_reduce_fusion
  62.1 0.4 fusion.258
  62.8 1.3 collective-permute-start.9
  64.1 5.0 %collective-permute-start.8 = (f32[2,4,32,160]{3,2,0,1:T(8,128)S(1)}, f32[2,4,32,160]{3,2,0,1:T(8,128)S(1)}, u32[]{:S(2)}, u32[]{:S(2)}) collective-permute-start(f32[2,4,32,160]{3,2,0,1:T(8,128)S(1)} %pad_maximum_fusion.15), channel_id=1, source_target_pairs={{0,4},{4,8},{8,12},{12,16},{16,20},{20,24},{24,28},{1,5},{5,9},{9,... | collective-permute-start | bytes 491528 | tf_op jit(solution)/shard_map/ppermute | solution.py:52
  69.1 3.5 %collective-permute-start.10 = (f32[1,4,32,160]{3,2,0,1:T(8,128)S(1)}, f32[1,4,32,160]{3,2,0,1:T(8,128)S(1)}, u32[]{:S(2)}, u32[]{:S(2)}) collective-permute-start(f32[1,4,32,160]{3,2,0,1:T(8,128)S(1)} %get-tuple-element.75), channel_id=1, source_target_pairs={{0,8},{4,12},{8,16},{12,20},{16,24},{20,28},{1,9},{5,13},{9,17},{1... | collective-permute-start | bytes 245768 | tf_op jit(solution)/shard_map/ppermute | solution.py:52
  72.6 1.3 collective-permute-start.11
  73.9 3.2 %collective-permute-done.8 = f32[2,4,32,160]{3,2,0,1:T(8,128)S(1)} collective-permute-done((f32[2,4,32,160]{3,2,0,1:T(8,128)S(1)}, f32[2,4,32,160]{3,2,0,1:T(8,128)S(1)}, u32[]{:S(2)}, u32[]{:S(2)}) %collective-permute-start.8) | collective-permute-done | bytes 163872 | tf_op jit(solution)/shard_map/ppermute | solution.py:52
  77.3 2.1 %collective-permute-done.11 = f32[1,4,32,160]{3,2,0,1:T(8,128)S(1)} collective-permute-done((f32[1,4,32,160]{3,2,0,1:T(8,128)S(1)}, f32[1,4,32,160]{3,2,0,1:T(8,128)S(1)}, u32[]{:S(2)}, u32[]{:S(2)}) %collective-permute-start.11) | collective-permute-done | bytes 81952 | tf_op jit(solution)/shard_map/ppermute | solution.py:53
  81.1 30.9 %all_gather.3 = f32[8,4,16,80]{3,2,1,0:T(8,128)S(1)} all-gather(f32[1,4,16,80]{3,2,1,0:T(8,128)S(1)} %pad_maximum_fusion.30), channel_id=1, replica_groups=mesh['alt'=8,'raan'=4] {'alt'}, dimensions={0}, use_global_device_ids=true | all-gather | bytes 184320 | tf_op jit(solution)/shard_map/all_gather | solution.py:159
  113.4 1.3 collective-permute-start.13
  114.7 4.5 %collective-permute-start.12 = (f32[2,32,160]{2,1,0:T(8,128)S(1)}, f32[2,32,160]{2,1,0:T(8,128)S(1)}, u32[]{:S(2)}, u32[]{:S(2)}) collective-permute-start(f32[2,32,160]{2,1,0:T(8,128)S(1)} %slice_add_fusion.3), channel_id=1, source_target_pairs={{0,4},{4,8},{8,12},{12,16},{16,20},{20,24},{24,28},{1,5},{5,9},{9,... | collective-permute-start | bytes 122888 | tf_op jit(solution)/shard_map/ppermute | solution.py:52
  119.6 1.6 %collective-permute-done.12 = f32[2,32,160]{2,1,0:T(8,128)S(1)} collective-permute-done((f32[2,32,160]{2,1,0:T(8,128)S(1)}, f32[2,32,160]{2,1,0:T(8,128)S(1)}, u32[]{:S(2)}, u32[]{:S(2)}) %collective-permute-start.12) | collective-permute-done | bytes 40992 | tf_op jit(solution)/shard_map/ppermute | solution.py:52
  121.6 0.4 fusion.177
  122.5 4.3 %collective-permute-start.14 = (f32[1,64,320]{2,1,0:T(8,128)S(1)}, f32[1,64,320]{2,1,0:T(8,128)S(1)}, u32[]{:S(2)}, u32[]{:S(2)}) collective-permute-start(f32[1,64,320]{2,1,0:T(8,128)S(1)} %get-tuple-element.47), channel_id=1, source_target_pairs={{0,4},{4,8},{8,12},{12,16},{16,20},{20,24},{24,28},{1,5},{5,9},{9,... | collective-permute-start | bytes 245768 | tf_op jit(solution)/shard_map/ppermute | solution.py:52
  126.8 1.3 collective-permute-start.15
  128.3 1.4 collective-permute-done.14
  129.7 4.6 %collective-permute-done.15 = f32[1,64,320]{2,1,0:T(8,128)S(1)} collective-permute-done((f32[1,64,320]{2,1,0:T(8,128)S(1)}, f32[1,64,320]{2,1,0:T(8,128)S(1)}, u32[]{:S(2)}, u32[]{:S(2)}) %collective-permute-start.15) | collective-permute-done | bytes 81952 | tf_op jit(solution)/shard_map/ppermute | solution.py:53
  134.3 0.5 fusion.74
  134.9 3.8 %collective-permute-start.16 = (f32[1,64,320]{2,1,0:T(8,128)S(1)}, f32[1,64,320]{2,1,0:T(8,128)S(1)}, u32[]{:S(2)}, u32[]{:S(2)}) collective-permute-start(f32[1,64,320]{2,1,0:T(8,128)S(1)} %get-tuple-element.41), channel_id=1, source_target_pairs={{0,4},{4,8},{8,12},{12,16},{16,20},{20,24},{24,28},{1,5},{5,9},{9,... | collective-permute-start | bytes 245768 | tf_op jit(solution)/shard_map/ppermute | solution.py:52
  138.7 1.3 collective-permute-start.17
  140.2 0.7 collective-permute-done.16
  140.9 4.3 %collective-permute-done.17 = f32[1,64,320]{2,1,0:T(8,128)S(1)} collective-permute-done((f32[1,64,320]{2,1,0:T(8,128)S(1)}, f32[1,64,320]{2,1,0:T(8,128)S(1)}, u32[]{:S(2)}, u32[]{:S(2)}) %collective-permute-start.17) | collective-permute-done | bytes 81952 | tf_op jit(solution)/shard_map/ppermute | solution.py:53
  145.2 0.5 fusion.75
  145.8 2.8 %collective-permute-start.18 = (f32[1,64,320]{2,1,0:T(8,128)S(1)}, f32[1,64,320]{2,1,0:T(8,128)S(1)}, u32[]{:S(2)}, u32[]{:S(2)}) collective-permute-start(f32[1,64,320]{2,1,0:T(8,128)S(1)} %get-tuple-element.37), channel_id=1, source_target_pairs={{0,4},{4,8},{8,12},{12,16},{16,20},{20,24},{24,28},{1,5},{5,9},{9,... | collective-permute-start | bytes 245768 | tf_op jit(solution)/shard_map/ppermute | solution.py:52
  148.7 1.3 collective-permute-start.19
  150.1 0.7 collective-permute-done.18
  150.8 4.3 %collective-permute-done.19 = f32[1,64,320]{2,1,0:T(8,128)S(1)} collective-permute-done((f32[1,64,320]{2,1,0:T(8,128)S(1)}, f32[1,64,320]{2,1,0:T(8,128)S(1)}, u32[]{:S(2)}, u32[]{:S(2)}) %collective-permute-start.19) | collective-permute-done | bytes 81952 | tf_op jit(solution)/shard_map/ppermute | solution.py:53
  155.3 1.6 %fusion.84 = (f32[4,64,256]{2,1,0:T(8,128)}, f32[4,64,256]{2,1,0:T(8,128)}) fusion(f32[4,63,320]{2,1,0:T(8,128)S(1)} %get-tuple-element.36, f32[4,64,320]{2,1,0:T(8,128)S(1)} %get-tuple-element.30, f32[4,64,319]{2,1,0:T(8,128)S(1)} %get-tuple-element.40, f32[4,64,320]{2,1,0:T(8,128)S(1)} %get-tuple-element.8, f32[4,64,319]{2,1,0:T(8,128)S(1)} %get-tuple-element.39, ...), kind=kLoop, calls=%fused_computation.120 | loop fusion | flops 655360 | bytes 3395584 | tf_op jit(solution)/shard_map/div | solution.py:176
  (109 shorter events, 8.8 us)
Async XLA Ops:
  1.9 15.0 %copy-start = (f32[4,64,256]{2,1,0:T(8,128)S(1)}, f32[4,64,256]{2,1,0:T(8,128)}, u32[]{:S(2)}) copy-start(f32[4,64,256]{2,1,0:T(8,128)} %param.7) | copy-start | bytes 786436
  1.9 15.0 %copy-start.1 = (f32[4,64,256]{2,1,0:T(8,128)S(1)}, f32[4,64,256]{2,1,0:T(8,128)}, u32[]{:S(2)}) copy-start(f32[4,64,256]{2,1,0:T(8,128)} %param.6) | copy-start | bytes 786436
  1.9 15.0 %copy-start.2 = (f32[4,64,256]{2,1,0:T(8,128)S(1)}, f32[4,64,256]{2,1,0:T(8,128)}, u32[]{:S(2)}) copy-start(f32[4,64,256]{2,1,0:T(8,128)} %param.5) | copy-start | bytes 786436
  2.0 15.0 %copy-start.3 = (f32[4,64,256]{2,1,0:T(8,128)S(1)}, f32[4,64,256]{2,1,0:T(8,128)}, u32[]{:S(2)}) copy-start(f32[4,64,256]{2,1,0:T(8,128)} %param.4) | copy-start | bytes 786436
  2.2 12.2 %collective-permute-start = (f32[4,4,64,32]{3,2,0,1:T(8,128)S(1)}, f32[4,4,64,32]{3,2,0,1:T(8,128)S(1)}, u32[]{:S(2)}, u32[]{:S(2)}) collective-permute-start(f32[4,4,64,32]{3,2,0,1:T(8,128)S(1)} %get-tuple-element.31), channel_id=1, source_target_pairs={{0,1},{1,2},{2,3},{3,0},{4,5},{5,6},{6,7},{7,4},{8,9},{9,10},{10,1... | collective-permute-start | bytes 393224 | tf_op jit(solution)/shard_map/ppermute | solution.py:39
  2.7 14.2 %collective-permute-start.1 = (f32[4,4,64,32]{3,2,0,1:T(8,128)S(1)}, f32[4,4,64,32]{3,2,0,1:T(8,128)S(1)}, u32[]{:S(2)}, u32[]{:S(2)}) collective-permute-start(f32[4,4,64,32]{3,2,0,1:T(8,128)S(1)} %get-tuple-element.32), channel_id=1, source_target_pairs={{1,0},{2,1},{3,2},{0,3},{5,4},{6,5},{7,6},{4,7},{9,8},{10,9},{11,1... | collective-permute-start | bytes 393224 | tf_op jit(solution)/shard_map/ppermute | solution.py:40
  16.9 2.3 %copy-start.4 = (f32[4,4,64,32]{3,2,0,1:T(8,128)}, f32[4,4,64,32]{3,2,0,1:T(8,128)S(1)}, u32[]{:S(2)}) copy-start(f32[4,4,64,32]{3,2,0,1:T(8,128)S(1)} %collective-permute-done.1) | copy-start | bytes 393220
  17.9 20.0 %collective-permute-start.3 = (f32[1,2,64,320]{3,2,0,1:T(8,128)}, f32[1,2,64,320]{3,2,0,1:T(8,128)}, u32[]{:S(2)}, u32[]{:S(2)}) collective-permute-start(f32[1,2,64,320]{3,2,0,1:T(8,128)} %get-tuple-element.23), channel_id=1, source_target_pairs={{4,0},{8,4},{12,8},{16,12},{20,16},{24,20},{28,24},{5,1},{9,5},{13... | collective-permute-start | bytes 491528 | tf_op jit(solution)/shard_map/ppermute | solution.py:53
  19.2 18.7 %collective-permute-start.2 = (f32[1,2,64,320]{3,2,0,1:T(8,128)}, f32[1,2,64,320]{3,2,0,1:T(8,128)}, u32[]{:S(2)}, u32[]{:S(2)}) collective-permute-start(f32[1,2,64,320]{3,2,0,1:T(8,128)} %get-tuple-element.24), channel_id=1, source_target_pairs={{0,4},{4,8},{8,12},{12,16},{16,20},{20,24},{24,28},{1,5},{5,9},{9,... | collective-permute-start | bytes 491528 | tf_op jit(solution)/shard_map/ppermute | solution.py:52
  29.5 6.4 %copy-start.8 = (s32[160]{0:T(256)S(1)}, s32[160]{0:T(256)}, u32[]{:S(2)}) copy-start(s32[160]{0:T(256)} %get-tuple-element.122) | copy-start | bytes 1924
  29.5 6.4 %copy-start.9 = (s32[160]{0:T(256)S(1)}, s32[160]{0:T(256)}, u32[]{:S(2)}) copy-start(s32[160]{0:T(256)} %get-tuple-element.123) | copy-start | bytes 1924
  29.5 6.4 %copy-start.14 = (pred[160]{0:T(512)(128)(4,1)S(1)}, pred[160]{0:T(512)(128)(4,1)}, u32[]{:S(2)}) copy-start(pred[160]{0:T(512)(128)(4,1)} %compare_and_fusion) | copy-start | bytes 484
  36.3 0.6 copy-start.11
  36.3 0.7 copy-start.12
  36.3 0.7 copy-start.13
  40.7 6.1 %collective-permute-start.4 = (f32[1,64,320]{2,1,0:T(8,128)S(1)}, f32[1,64,320]{2,1,0:T(8,128)S(1)}, u32[]{:S(2)}, u32[]{:S(2)}) collective-permute-start(f32[1,64,320]{2,1,0:T(8,128)S(1)} %get-tuple-element.59), channel_id=1, source_target_pairs={{0,4},{4,8},{8,12},{12,16},{16,20},{20,24},{24,28},{1,5},{5,9},{9,... | collective-permute-start | bytes 245768 | tf_op jit(solution)/shard_map/ppermute | solution.py:52
  44.4 6.6 %collective-permute-start.5 = (f32[1,64,320]{2,1,0:T(8,128)S(1)}, f32[1,64,320]{2,1,0:T(8,128)S(1)}, u32[]{:S(2)}, u32[]{:S(2)}) collective-permute-start(f32[1,64,320]{2,1,0:T(8,128)S(1)} %get-tuple-element.60), channel_id=1, source_target_pairs={{4,0},{8,4},{12,8},{16,12},{20,16},{24,20},{28,24},{5,1},{9,5},{13... | collective-permute-start | bytes 245768 | tf_op jit(solution)/shard_map/ppermute | solution.py:53
  51.5 5.6 %collective-permute-start.6 = (f32[1,64,320]{2,1,0:T(8,128)S(1)}, f32[1,64,320]{2,1,0:T(8,128)S(1)}, u32[]{:S(2)}, u32[]{:S(2)}) collective-permute-start(f32[1,64,320]{2,1,0:T(8,128)S(1)} %get-tuple-element.53), channel_id=1, source_target_pairs={{0,4},{4,8},{8,12},{12,16},{16,20},{20,24},{24,28},{1,5},{5,9},{9,... | collective-permute-start | bytes 245768 | tf_op jit(solution)/shard_map/ppermute | solution.py:52
  54.9 6.5 %collective-permute-start.7 = (f32[1,64,320]{2,1,0:T(8,128)S(1)}, f32[1,64,320]{2,1,0:T(8,128)S(1)}, u32[]{:S(2)}, u32[]{:S(2)}) collective-permute-start(f32[1,64,320]{2,1,0:T(8,128)S(1)} %get-tuple-element.54), channel_id=1, source_target_pairs={{4,0},{8,4},{12,8},{16,12},{20,16},{24,20},{28,24},{5,1},{9,5},{13... | collective-permute-start | bytes 245768 | tf_op jit(solution)/shard_map/ppermute | solution.py:53
  61.5 0.7 copy-start.6
  61.5 0.7 copy-start.7
  61.5 0.7 copy-start.10
  62.8 11.1 %collective-permute-start.9 = (f32[2,4,32,160]{3,2,0,1:T(8,128)S(1)}, f32[2,4,32,160]{3,2,0,1:T(8,128)S(1)}, u32[]{:S(2)}, u32[]{:S(2)}) collective-permute-start(f32[2,4,32,160]{3,2,0,1:T(8,128)S(1)} %pad_maximum_fusion.15), channel_id=1, source_target_pairs={{4,0},{8,4},{12,8},{16,12},{20,16},{24,20},{28,24},{5,1},{9,5},{13... | collective-permute-start | bytes 491528 | tf_op jit(solution)/shard_map/ppermute | solution.py:53
  64.1 13.0 %collective-permute-start.8 = (f32[2,4,32,160]{3,2,0,1:T(8,128)S(1)}, f32[2,4,32,160]{3,2,0,1:T(8,128)S(1)}, u32[]{:S(2)}, u32[]{:S(2)}) collective-permute-start(f32[2,4,32,160]{3,2,0,1:T(8,128)S(1)} %pad_maximum_fusion.15), channel_id=1, source_target_pairs={{0,4},{4,8},{8,12},{12,16},{16,20},{20,24},{24,28},{1,5},{5,9},{9,... | collective-permute-start | bytes 491528 | tf_op jit(solution)/shard_map/ppermute | solution.py:52
  69.1 8.2 %collective-permute-start.10 = (f32[1,4,32,160]{3,2,0,1:T(8,128)S(1)}, f32[1,4,32,160]{3,2,0,1:T(8,128)S(1)}, u32[]{:S(2)}, u32[]{:S(2)}) collective-permute-start(f32[1,4,32,160]{3,2,0,1:T(8,128)S(1)} %get-tuple-element.75), channel_id=1, source_target_pairs={{0,8},{4,12},{8,16},{12,20},{16,24},{20,28},{1,9},{5,13},{9,17},{1... | collective-permute-start | bytes 245768 | tf_op jit(solution)/shard_map/ppermute | solution.py:52
  72.6 6.9 %collective-permute-start.11 = (f32[1,4,32,160]{3,2,0,1:T(8,128)S(1)}, f32[1,4,32,160]{3,2,0,1:T(8,128)S(1)}, u32[]{:S(2)}, u32[]{:S(2)}) collective-permute-start(f32[1,4,32,160]{3,2,0,1:T(8,128)S(1)} %get-tuple-element.76), channel_id=1, source_target_pairs={{8,0},{12,4},{16,8},{20,12},{24,16},{28,20},{9,1},{13,5},{17,9},{2... | collective-permute-start | bytes 245768 | tf_op jit(solution)/shard_map/ppermute | solution.py:53
  79.4 0.7 copy-start.5
  113.4 6.2 %collective-permute-start.13 = (f32[2,32,160]{2,1,0:T(8,128)S(1)}, f32[2,32,160]{2,1,0:T(8,128)S(1)}, u32[]{:S(2)}, u32[]{:S(2)}) collective-permute-start(f32[2,32,160]{2,1,0:T(8,128)S(1)} %slice_add_fusion.3), channel_id=1, source_target_pairs={{4,0},{8,4},{12,8},{16,12},{20,16},{24,20},{28,24},{5,1},{9,5},{13... | collective-permute-start | bytes 122888 | tf_op jit(solution)/shard_map/ppermute | solution.py:53
  114.7 6.4 %collective-permute-start.12 = (f32[2,32,160]{2,1,0:T(8,128)S(1)}, f32[2,32,160]{2,1,0:T(8,128)S(1)}, u32[]{:S(2)}, u32[]{:S(2)}) collective-permute-start(f32[2,32,160]{2,1,0:T(8,128)S(1)} %slice_add_fusion.3), channel_id=1, source_target_pairs={{0,4},{4,8},{8,12},{12,16},{16,20},{20,24},{24,28},{1,5},{5,9},{9,... | collective-permute-start | bytes 122888 | tf_op jit(solution)/shard_map/ppermute | solution.py:52
  122.5 7.2 %collective-permute-start.14 = (f32[1,64,320]{2,1,0:T(8,128)S(1)}, f32[1,64,320]{2,1,0:T(8,128)S(1)}, u32[]{:S(2)}, u32[]{:S(2)}) collective-permute-start(f32[1,64,320]{2,1,0:T(8,128)S(1)} %get-tuple-element.47), channel_id=1, source_target_pairs={{0,4},{4,8},{8,12},{12,16},{16,20},{20,24},{24,28},{1,5},{5,9},{9,... | collective-permute-start | bytes 245768 | tf_op jit(solution)/shard_map/ppermute | solution.py:52
  126.8 7.5 %collective-permute-start.15 = (f32[1,64,320]{2,1,0:T(8,128)S(1)}, f32[1,64,320]{2,1,0:T(8,128)S(1)}, u32[]{:S(2)}, u32[]{:S(2)}) collective-permute-start(f32[1,64,320]{2,1,0:T(8,128)S(1)} %get-tuple-element.48), channel_id=1, source_target_pairs={{4,0},{8,4},{12,8},{16,12},{20,16},{24,20},{28,24},{5,1},{9,5},{13... | collective-permute-start | bytes 245768 | tf_op jit(solution)/shard_map/ppermute | solution.py:53
  134.9 6.0 %collective-permute-start.16 = (f32[1,64,320]{2,1,0:T(8,128)S(1)}, f32[1,64,320]{2,1,0:T(8,128)S(1)}, u32[]{:S(2)}, u32[]{:S(2)}) collective-permute-start(f32[1,64,320]{2,1,0:T(8,128)S(1)} %get-tuple-element.41), channel_id=1, source_target_pairs={{0,4},{4,8},{8,12},{12,16},{16,20},{20,24},{24,28},{1,5},{5,9},{9,... | collective-permute-start | bytes 245768 | tf_op jit(solution)/shard_map/ppermute | solution.py:52
  138.7 6.5 %collective-permute-start.17 = (f32[1,64,320]{2,1,0:T(8,128)S(1)}, f32[1,64,320]{2,1,0:T(8,128)S(1)}, u32[]{:S(2)}, u32[]{:S(2)}) collective-permute-start(f32[1,64,320]{2,1,0:T(8,128)S(1)} %get-tuple-element.42), channel_id=1, source_target_pairs={{4,0},{8,4},{12,8},{16,12},{20,16},{24,20},{28,24},{5,1},{9,5},{13... | collective-permute-start | bytes 245768 | tf_op jit(solution)/shard_map/ppermute | solution.py:53
  145.8 5.0 %collective-permute-start.18 = (f32[1,64,320]{2,1,0:T(8,128)S(1)}, f32[1,64,320]{2,1,0:T(8,128)S(1)}, u32[]{:S(2)}, u32[]{:S(2)}) collective-permute-start(f32[1,64,320]{2,1,0:T(8,128)S(1)} %get-tuple-element.37), channel_id=1, source_target_pairs={{0,4},{4,8},{8,12},{12,16},{16,20},{20,24},{24,28},{1,5},{5,9},{9,... | collective-permute-start | bytes 245768 | tf_op jit(solution)/shard_map/ppermute | solution.py:52
  148.7 6.5 %collective-permute-start.19 = (f32[1,64,320]{2,1,0:T(8,128)S(1)}, f32[1,64,320]{2,1,0:T(8,128)S(1)}, u32[]{:S(2)}, u32[]{:S(2)}) collective-permute-start(f32[1,64,320]{2,1,0:T(8,128)S(1)} %get-tuple-element.38), channel_id=1, source_target_pairs={{4,0},{8,4},{12,8},{16,12},{20,16},{24,20},{28,24},{5,1},{9,5},{13... | collective-permute-start | bytes 245768 | tf_op jit(solution)/shard_map/ppermute | solution.py:53

commit v6 on v5

--- a/solution.py
+++ b/solution.py
@@ -136,13 +136,17 @@
     coef_two = [coarsen(part) for part in (wide_alt, wide_inc, wide_raan)]
     coef_three = [coarsen(part) for part in coef_two]
 
-    first = alt_extend(wide[:, 0:2], 1)
+    reach = SWEEPS + 1
+    first = alt_extend(wide, reach)
     source_x = first[:, 0]
-    weights_one = make_weights(first[:, 1], wide_inc, wide_raan, 1.0, 0)
+    weights_one = make_weights(
+        first[:, 1], trim(first[:, 2], reach, reach - 1), trim(first[:, 3], reach, reach - 1), 1.0, reach - 1
+    )
 
-    density = sweep(weights_one, source_x, 1, source_x, 1)
-    density = sweep(weights_one, alt_extend(density, 1), 1, source_x, 1)
-    applied, density = apply_op(weights_one, alt_extend(density, 1), 1)
+    density = source_x
+    for halo in range(reach, 1, -1):
+        density = sweep(weights_one, density, halo, source_x, reach)
+    applied, density = apply_op(weights_one, density, 1)
     rhs_two = coarsen(wide_source - applied)
 
     level_two = alt_extend(jnp.stack([rhs_two] + coef_two, 1), 3)
@@ -169,11 +173,11 @@
     for halo in range(SWEEPS, 0, -1):
         correction = sweep(weights_two, correction, halo, rhs_two_x, 2)
 
-    density = density + refine(correction)
-    for _ in range(SWEEPS):
-        density = sweep(weights_one, alt_extend(density, 1), 1, source_x, 1)
-    applied, centre = apply_op(weights_one, alt_extend(density, 1), 1)
-    scaled_residual = (wide_source - applied) / weights_one[0][6]
+    density = alt_extend(density + refine(correction), reach)
+    for halo in range(reach, 1, -1):
+        density = sweep(weights_one, density, halo, source_x, reach)
+    applied, centre = apply_op(weights_one, density, 1)
+    scaled_residual = (wide_source - applied) / trim(weights_one[0][6], weights_one[1], 0)
     keep = slice(halo_r, halo_r + length)
     return (centre[..., keep], scaled_residual[..., keep])
 

time: 158 us -> 169 us (1.070)
  the two profiles are of different devices: /device:TPU:0 before, /device:TPU:20 now
where the time goes in v6:
time: 169 us
  waiting for transfers between devices  59.3 us (35%)
  starting transfers between devices  34.7 us (21%)
  blocking collectives  29 us (17%)
  other arithmetic  23.6 us (14%)
  matrix products  11.8 us (7%)
  local copies, waits for them, and re-layouts  8.76 us (5%)
    ppermute x5, waiting for transfers between devices, alt_extend(): below.insert(0, lax.ppermute(values[low:], 'alt', up))  42.6 us
    all_gather x1, blocking collectives, shards(): lax.all_gather(jnp.stack([rhs_three] + coef_three, 1), 'alt', axis=0, til...  29 us
    ppermute x5, starting transfers between devices, alt_extend(): below.insert(0, lax.ppermute(values[low:], 'alt', up))  21.2 us
    ppermute x5, starting transfers between devices, alt_extend(): above.append(lax.ppermute(values[:high], 'alt', down))  11.7 us
    ppermute x5, waiting for transfers between devices, alt_extend(): above.append(lax.ppermute(values[:high], 'alt', down))  10.3 us
    dot_general x8, matrix products, coarsen(): summed = jnp.matmul(summed, pairing(length), precision=HIGH)  7.45 us
    ppermute x1, waiting for transfers between devices, raan_extend(): before = lax.ppermute(values[..., length - halo:], 'raan', up)  5.53 us
    reduce_sum x5, other arithmetic, coarsen(): summed = values.reshape(depth // 2, 2, width, length).sum(axis=1)  4.71 us
  transfers between devices with their start and end apart: 12, of which 7 were waited for; matrix products, arithmetic and copies ran while one was open for 11% of the time, Pallas kernels for 0%

profile of v6, /device:TPU:20, one launch (start us, length us, event | category | flops | bytes accessed | tf_op | source)
XLA Modules:
  0.0 168.6 jit_solution(3995734100128468338)
XLA Ops:
  0.6 1.3 pad_maximum_fusion.2
  2.2 1.7 %collective-permute-start.1 = (f32[4,4,64,32]{3,2,0,1:T(8,128)S(1)}, f32[4,4,64,32]{3,2,0,1:T(8,128)}, u32[]{:S(2)}, u32[]{:S(2)}) collective-permute-start(f32[4,4,64,32]{3,2,0,1:T(8,128)S(1)} %get-tuple-element.31), channel_id=1, source_target_pairs={{1,0},{2,1},{3,2},{0,3},{5,4},{6,5},{7,6},{4,7},{9,8},{10,9},{11,1... | collective-permute-start | bytes 393224 | tf_op jit(solution)/shard_map/ppermute | solution.py:40
  4.0 0.5 compare_and_fusion.5
  4.5 0.6 fusion.228
  5.1 0.6 iota_shift-right-logical_fusion.1
  5.7 0.6 compare_and_fusion
  6.2 0.5 broadcast_add_fusion.2
  6.8 0.5 compare_and_fusion.1
  7.3 0.6 iota_shift-right-logical_fusion.2
  7.9 0.6 compare_and_fusion.2
  8.5 0.6 iota_shift-right-logical_fusion
  9.1 5.5 %collective-permute-done = f32[4,4,64,32]{3,2,0,1:T(8,128)S(1)} collective-permute-done((f32[4,4,64,32]{3,2,0,1:T(8,128)S(1)}, f32[4,4,64,32]{3,2,0,1:T(8,128)S(1)}, u32[]{:S(2)}, u32[]{:S(2)}) %collective-permute-start) | collective-permute-done | bytes 131104 | tf_op jit(solution)/shard_map/ppermute | solution.py:39
  14.6 0.9 collective-permute-done.1
  15.5 1.6 pad_maximum_fusion.1
  17.1 1.7 %fusion.254 = (f32[3,4,64,320]{3,2,0,1:T(8,128)}, f32[3,4,64,320]{3,2,0,1:T(8,128)}) fusion(f32[4,4,64,320]{3,2,0,1:T(8,128)S(1)} %pad_maximum_fusion.1), kind=kLoop, calls=%fused_computation.376 | loop fusion | bytes 3932160 | tf_op jit(solution)/shard_map/slice | solution.py:52
  18.8 1.1 slice_bitcast_fusion.10
  20.0 3.4 %collective-permute-start.2 = (f32[3,4,64,320]{3,2,0,1:T(8,128)}, f32[3,4,64,320]{3,2,0,1:T(8,128)}, u32[]{:S(2)}, u32[]{:S(2)}) collective-permute-start(f32[3,4,64,320]{3,2,0,1:T(8,128)} %get-tuple-element.28), channel_id=1, source_target_pairs={{0,4},{4,8},{8,12},{12,16},{16,20},{20,24},{24,28},{1,5},{5,9},{9,... | collective-permute-start | bytes 2949128 | tf_op jit(solution)/shard_map/ppermute | solution.py:52
  23.4 2.4 %collective-permute-start.3 = (f32[3,4,64,320]{3,2,0,1:T(8,128)}, f32[3,4,64,320]{3,2,0,1:T(8,128)}, u32[]{:S(2)}, u32[]{:S(2)}) collective-permute-start(f32[3,4,64,320]{3,2,0,1:T(8,128)} %get-tuple-element.29), channel_id=1, source_target_pairs={{4,0},{8,4},{12,8},{16,12},{20,16},{24,20},{28,24},{5,1},{9,5},{13... | collective-permute-start | bytes 2949128 | tf_op jit(solution)/shard_map/ppermute | solution.py:53
  25.8 1.7 %reduce_sum.73 = f32[2,64,320]{2,1,0:T(8,128)} reduce(f32[2,2,64,320]{3,2,1,0:T(8,128)} %bitcast.310, f32[]{:T(128)} %constant.148.clone.1), dimensions={1}, to_apply=%region_1.2 | reduce | flops 40960 | bytes 491524 | tf_op jit(solution)/shard_map/reduce_sum | solution.py:21
  27.5 1.7 %reduce_sum.74 = f32[2,64,320]{2,1,0:T(8,128)} reduce(f32[2,2,64,320]{3,2,1,0:T(8,128)} %bitcast.309, f32[]{:T(128)} %constant.148.clone.1), dimensions={1}, to_apply=%region_2.3 | reduce | flops 40960 | bytes 491524 | tf_op jit(solution)/shard_map/reduce_sum | solution.py:21
  29.2 0.7 reduce_sum.75
  30.0 1.4 fusion.241
  31.4 1.4 fusion.239
  33.1 1.0 fusion.107
  34.1 1.0 fusion.108
  35.0 0.9 fusion
  36.0 0.9 fusion.1
  36.9 1.1 fusion.243
  38.2 1.0 fusion.109
  39.2 0.3 fusion.2
  39.5 36.8 %collective-permute-done.2 = f32[3,4,64,320]{3,2,0,1:T(8,128)} collective-permute-done((f32[3,4,64,320]{3,2,0,1:T(8,128)}, f32[3,4,64,320]{3,2,0,1:T(8,128)}, u32[]{:S(2)}, u32[]{:S(2)}) %collective-permute-start.2) | collective-permute-done | bytes 983072 | tf_op jit(solution)/shard_map/ppermute | solution.py:52
  76.2 3.3 %pad_maximum_fusion = f32[10,4,64,320]{3,2,0,1:T(8,128)S(1)} fusion(f32[3,4,64,320]{3,2,0,1:T(8,128)} %collective-permute-done.3, f32[4,4,64,32]{3,2,0,1:T(8,128)} %collective-permute-done.1, f32[4,1,64,256]{3,2,0,1:T(8,128)S(1)} %bitcast.282, f32[4,1,64,256]{3,2,0,1:T(8,128)S(1)} %bitcast.285, f32[4,1,64,256]{3,2,0,1:T(8,128)S(1)} %bitcast.288, ...), kind=kLoop, calls=%fused_computation | loop fusion | flops 5734400 | bytes 6553600 | tf_op jit(solution)/shard_map/concatenate | solution.py:54
  79.9 0.5 fusion.263
  80.5 0.7 fusion.33
  81.2 1.0 fusion.34
  82.6 0.8 fusion.56
  83.7 0.5 bitcast_reduce_fusion
  84.3 0.4 fusion.245
  85.0 4.3 %collective-permute-start.4 = (f32[2,4,32,160]{3,2,0,1:T(8,128)S(1)}, f32[2,4,32,160]{3,2,0,1:T(8,128)S(1)}, u32[]{:S(2)}, u32[]{:S(2)}) collective-permute-start(f32[2,4,32,160]{3,2,0,1:T(8,128)S(1)} %pad_maximum_fusion.5), channel_id=1, source_target_pairs={{0,4},{4,8},{8,12},{12,16},{16,20},{20,24},{24,28},{1,5},{5,9},{9,... | collective-permute-start | bytes 491528 | tf_op jit(solution)/shard_map/ppermute | solution.py:52
  89.3 1.9 %collective-permute-start.5 = (f32[2,4,32,160]{3,2,0,1:T(8,128)S(1)}, f32[2,4,32,160]{3,2,0,1:T(8,128)S(1)}, u32[]{:S(2)}, u32[]{:S(2)}) collective-permute-start(f32[2,4,32,160]{3,2,0,1:T(8,128)S(1)} %pad_maximum_fusion.5), channel_id=1, source_target_pairs={{4,0},{8,4},{12,8},{16,12},{20,16},{24,20},{28,24},{5,1},{9,5},{13... | collective-permute-start | bytes 491528 | tf_op jit(solution)/shard_map/ppermute | solution.py:53
  91.3 2.5 %collective-permute-start.6 = (f32[1,4,32,160]{3,2,0,1:T(8,128)S(1)}, f32[1,4,32,160]{3,2,0,1:T(8,128)S(1)}, u32[]{:S(2)}, u32[]{:S(2)}) collective-permute-start(f32[1,4,32,160]{3,2,0,1:T(8,128)S(1)} %get-tuple-element.69), channel_id=1, source_target_pairs={{0,8},{4,12},{8,16},{12,20},{16,24},{20,28},{1,9},{5,13},{9,17},{1... | collective-permute-start | bytes 245768 | tf_op jit(solution)/shard_map/ppermute | solution.py:52
  93.8 3.4 %collective-permute-start.7 = (f32[1,4,32,160]{3,2,0,1:T(8,128)S(1)}, f32[1,4,32,160]{3,2,0,1:T(8,128)S(1)}, u32[]{:S(2)}, u32[]{:S(2)}) collective-permute-start(f32[1,4,32,160]{3,2,0,1:T(8,128)S(1)} %get-tuple-element.70), channel_id=1, source_target_pairs={{8,0},{12,4},{16,8},{20,12},{24,16},{28,20},{9,1},{13,5},{17,9},{2... | collective-permute-start | bytes 245768 | tf_op jit(solution)/shard_map/ppermute | solution.py:53
  97.1 3.6 %collective-permute-done.4 = f32[2,4,32,160]{3,2,0,1:T(8,128)S(1)} collective-permute-done((f32[2,4,32,160]{3,2,0,1:T(8,128)S(1)}, f32[2,4,32,160]{3,2,0,1:T(8,128)S(1)}, u32[]{:S(2)}, u32[]{:S(2)}) %collective-permute-start.4) | collective-permute-done | bytes 163872 | tf_op jit(solution)/shard_map/ppermute | solution.py:52
  101.1 0.2 fusion.79
  101.4 0.3 copy-done.7
  102.4 0.3 fusion.110
  102.7 0.3 fusion.3
  103.0 29.0 %all_gather.3 = f32[8,4,16,80]{3,2,1,0:T(8,128)S(1)} all-gather(f32[1,4,16,80]{3,2,1,0:T(8,128)S(1)} %pad_maximum_fusion.18), channel_id=1, replica_groups=mesh['alt'=8,'raan'=4] {'alt'}, dimensions={0}, use_global_device_ids=true | all-gather | bytes 184320 | tf_op jit(solution)/shard_map/all_gather | solution.py:163
  133.1 0.3 fusion.197
  133.4 4.4 %collective-permute-start.8 = (f32[2,32,160]{2,1,0:T(8,128)S(1)}, f32[2,32,160]{2,1,0:T(8,128)S(1)}, u32[]{:S(2)}, u32[]{:S(2)}) collective-permute-start(f32[2,32,160]{2,1,0:T(8,128)S(1)} %slice_add_fusion.6), channel_id=1, source_target_pairs={{0,4},{4,8},{8,12},{12,16},{16,20},{20,24},{24,28},{1,5},{5,9},{9,... | collective-permute-start | bytes 122888 | tf_op jit(solution)/shard_map/ppermute | solution.py:52
  137.8 2.1 %collective-permute-start.9 = (f32[2,32,160]{2,1,0:T(8,128)S(1)}, f32[2,32,160]{2,1,0:T(8,128)S(1)}, u32[]{:S(2)}, u32[]{:S(2)}) collective-permute-start(f32[2,32,160]{2,1,0:T(8,128)S(1)} %slice_add_fusion.6), channel_id=1, source_target_pairs={{4,0},{8,4},{12,8},{16,12},{20,16},{24,20},{28,24},{5,1},{9,5},{13... | collective-permute-start | bytes 122888 | tf_op jit(solution)/shard_map/ppermute | solution.py:53
  139.9 5.0 %collective-permute-done.9 = f32[2,32,160]{2,1,0:T(8,128)S(1)} collective-permute-done((f32[2,32,160]{2,1,0:T(8,128)S(1)}, f32[2,32,160]{2,1,0:T(8,128)S(1)}, u32[]{:S(2)}, u32[]{:S(2)}) %collective-permute-start.9) | collective-permute-done | bytes 40992 | tf_op jit(solution)/shard_map/ppermute | solution.py:53
  145.4 0.4 fusion.164
  145.9 0.3 convolution_bitcast_fusion
  146.3 6.6 %collective-permute-start.10 = (f32[3,64,320]{2,1,0:T(8,128)S(1)}, f32[3,64,320]{2,1,0:T(8,128)S(1)}, u32[]{:S(2)}, u32[]{:S(2)}) collective-permute-start(f32[3,64,320]{2,1,0:T(8,128)S(1)} %get-tuple-element.63), channel_id=1, source_target_pairs={{0,4},{4,8},{8,12},{12,16},{16,20},{20,24},{24,28},{1,5},{5,9},{9,... | collective-permute-start | bytes 737288 | tf_op jit(solution)/shard_map/ppermute | solution.py:52
  152.9 1.9 %collective-permute-start.11 = (f32[3,64,320]{2,1,0:T(8,128)S(1)}, f32[3,64,320]{2,1,0:T(8,128)S(1)}, u32[]{:S(2)}, u32[]{:S(2)}) collective-permute-start(f32[3,64,320]{2,1,0:T(8,128)S(1)} %get-tuple-element.64), channel_id=1, source_target_pairs={{4,0},{8,4},{12,8},{16,12},{20,16},{24,20},{28,24},{5,1},{9,5},{13... | collective-permute-start | bytes 737288 | tf_op jit(solution)/shard_map/ppermute | solution.py:53
  154.9 2.2 %collective-permute-done.10 = f32[3,64,320]{2,1,0:T(8,128)S(1)} collective-permute-done((f32[3,64,320]{2,1,0:T(8,128)S(1)}, f32[3,64,320]{2,1,0:T(8,128)S(1)}, u32[]{:S(2)}, u32[]{:S(2)}) %collective-permute-start.10) | collective-permute-done | bytes 245792 | tf_op jit(solution)/shard_map/ppermute | solution.py:52
  157.1 5.3 %collective-permute-done.11 = f32[3,64,320]{2,1,0:T(8,128)S(1)} collective-permute-done((f32[3,64,320]{2,1,0:T(8,128)S(1)}, f32[3,64,320]{2,1,0:T(8,128)S(1)}, u32[]{:S(2)}, u32[]{:S(2)}) %collective-permute-start.11) | collective-permute-done | bytes 245792 | tf_op jit(solution)/shard_map/ppermute | solution.py:53
  162.6 0.3 fusion.257
  162.9 1.1 fusion.35
  164.3 0.9 fusion.57
  165.4 0.8 slice.964
  166.4 0.8 copy-done.4
  167.2 1.4 fusion.68
  (100 shorter events, 5.8 us)
Async XLA Ops:
  1.9 13.5 %copy-start = (f32[4,64,256]{2,1,0:T(8,128)S(1)}, f32[4,64,256]{2,1,0:T(8,128)}, u32[]{:S(2)}) copy-start(f32[4,64,256]{2,1,0:T(8,128)} %param.7) | copy-start | bytes 786436
  1.9 13.5 %copy-start.1 = (f32[4,64,256]{2,1,0:T(8,128)S(1)}, f32[4,64,256]{2,1,0:T(8,128)}, u32[]{:S(2)}) copy-start(f32[4,64,256]{2,1,0:T(8,128)} %param.6) | copy-start | bytes 786436
  1.9 13.5 %copy-start.2 = (f32[4,64,256]{2,1,0:T(8,128)S(1)}, f32[4,64,256]{2,1,0:T(8,128)}, u32[]{:S(2)}) copy-start(f32[4,64,256]{2,1,0:T(8,128)} %param.5) | copy-start | bytes 786436
  2.0 13.5 %copy-start.3 = (f32[4,64,256]{2,1,0:T(8,128)S(1)}, f32[4,64,256]{2,1,0:T(8,128)}, u32[]{:S(2)}) copy-start(f32[4,64,256]{2,1,0:T(8,128)} %param.4) | copy-start | bytes 786436
  2.2 12.4 %collective-permute-start = (f32[4,4,64,32]{3,2,0,1:T(8,128)S(1)}, f32[4,4,64,32]{3,2,0,1:T(8,128)S(1)}, u32[]{:S(2)}, u32[]{:S(2)}) collective-permute-start(f32[4,4,64,32]{3,2,0,1:T(8,128)S(1)} %get-tuple-element.30), channel_id=1, source_target_pairs={{0,1},{1,2},{2,3},{3,0},{4,5},{5,6},{6,7},{7,4},{8,9},{9,10},{10,1... | collective-permute-start | bytes 393224 | tf_op jit(solution)/shard_map/ppermute | solution.py:39
  2.2 13.2 %collective-permute-start.1 = (f32[4,4,64,32]{3,2,0,1:T(8,128)S(1)}, f32[4,4,64,32]{3,2,0,1:T(8,128)}, u32[]{:S(2)}, u32[]{:S(2)}) collective-permute-start(f32[4,4,64,32]{3,2,0,1:T(8,128)S(1)} %get-tuple-element.31), channel_id=1, source_target_pairs={{1,0},{2,1},{3,2},{0,3},{5,4},{6,5},{7,6},{4,7},{9,8},{10,9},{11,1... | collective-permute-start | bytes 393224 | tf_op jit(solution)/shard_map/ppermute | solution.py:40
  20.0 56.3 %collective-permute-start.2 = (f32[3,4,64,320]{3,2,0,1:T(8,128)}, f32[3,4,64,320]{3,2,0,1:T(8,128)}, u32[]{:S(2)}, u32[]{:S(2)}) collective-permute-start(f32[3,4,64,320]{3,2,0,1:T(8,128)} %get-tuple-element.28), channel_id=1, source_target_pairs={{0,4},{4,8},{8,12},{12,16},{16,20},{20,24},{24,28},{1,5},{5,9},{9,... | collective-permute-start | bytes 2949128 | tf_op jit(solution)/shard_map/ppermute | solution.py:52
  23.4 52.9 %collective-permute-start.3 = (f32[3,4,64,320]{3,2,0,1:T(8,128)}, f32[3,4,64,320]{3,2,0,1:T(8,128)}, u32[]{:S(2)}, u32[]{:S(2)}) collective-permute-start(f32[3,4,64,320]{3,2,0,1:T(8,128)} %get-tuple-element.29), channel_id=1, source_target_pairs={{4,0},{8,4},{12,8},{16,12},{20,16},{24,20},{28,24},{5,1},{9,5},{13... | collective-permute-start | bytes 2949128 | tf_op jit(solution)/shard_map/ppermute | solution.py:53
  29.9 6.9 %copy-start.5 = (f32[2,64,320]{2,1,0:T(8,128)S(1)}, f32[2,64,320]{2,1,0:T(8,128)}, u32[]{:S(2)}) copy-start(f32[2,64,320]{2,1,0:T(8,128)} %reduce_sum.73) | copy-start | bytes 491524
  29.9 9.2 %copy-start.13 = (s32[32]{0:T(128)S(1)}, s32[32]{0:T(128)}, u32[]{:S(2)}) copy-start(s32[32]{0:T(128)} %broadcast_add_fusion.2) | copy-start | bytes 388
  29.9 9.2 %copy-start.14 = (pred[32]{0:T(512)(128)(4,1)S(1)}, pred[32]{0:T(512)(128)(4,1)}, u32[]{:S(2)}) copy-start(pred[32]{0:T(512)(128)(4,1)} %compare_and_fusion.1) | copy-start | bytes 100
  29.9 9.2 %copy-start.15 = (s32[32]{0:T(128)S(1)}, s32[32]{0:T(128)}, u32[]{:S(2)}) copy-start(s32[32]{0:T(128)} %iota_shift-right-logical_fusion.2) | copy-start | bytes 388
  80.5 0.7 copy-start.6
  83.6 0.7 copy-start.8
  83.7 0.7 copy-start.9
  83.7 0.7 copy-start.12
  85.0 15.8 %collective-permute-start.4 = (f32[2,4,32,160]{3,2,0,1:T(8,128)S(1)}, f32[2,4,32,160]{3,2,0,1:T(8,128)S(1)}, u32[]{:S(2)}, u32[]{:S(2)}) collective-permute-start(f32[2,4,32,160]{3,2,0,1:T(8,128)S(1)} %pad_maximum_fusion.5), channel_id=1, source_target_pairs={{0,4},{4,8},{8,12},{12,16},{16,20},{20,24},{24,28},{1,5},{5,9},{9,... | collective-permute-start | bytes 491528 | tf_op jit(solution)/shard_map/ppermute | solution.py:52
  89.3 11.5 %collective-permute-start.5 = (f32[2,4,32,160]{3,2,0,1:T(8,128)S(1)}, f32[2,4,32,160]{3,2,0,1:T(8,128)S(1)}, u32[]{:S(2)}, u32[]{:S(2)}) collective-permute-start(f32[2,4,32,160]{3,2,0,1:T(8,128)S(1)} %pad_maximum_fusion.5), channel_id=1, source_target_pairs={{4,0},{8,4},{12,8},{16,12},{20,16},{24,20},{28,24},{5,1},{9,5},{13... | collective-permute-start | bytes 491528 | tf_op jit(solution)/shard_map/ppermute | solution.py:53
  91.3 9.8 %collective-permute-start.6 = (f32[1,4,32,160]{3,2,0,1:T(8,128)S(1)}, f32[1,4,32,160]{3,2,0,1:T(8,128)S(1)}, u32[]{:S(2)}, u32[]{:S(2)}) collective-permute-start(f32[1,4,32,160]{3,2,0,1:T(8,128)S(1)} %get-tuple-element.69), channel_id=1, source_target_pairs={{0,8},{4,12},{8,16},{12,20},{16,24},{20,28},{1,9},{5,13},{9,17},{1... | collective-permute-start | bytes 245768 | tf_op jit(solution)/shard_map/ppermute | solution.py:52
  93.8 7.3 %collective-permute-start.7 = (f32[1,4,32,160]{3,2,0,1:T(8,128)S(1)}, f32[1,4,32,160]{3,2,0,1:T(8,128)S(1)}, u32[]{:S(2)}, u32[]{:S(2)}) collective-permute-start(f32[1,4,32,160]{3,2,0,1:T(8,128)S(1)} %get-tuple-element.70), channel_id=1, source_target_pairs={{8,0},{12,4},{16,8},{20,12},{24,16},{28,20},{9,1},{13,5},{17,9},{2... | collective-permute-start | bytes 245768 | tf_op jit(solution)/shard_map/ppermute | solution.py:53
  101.1 0.7 copy-start.7
  101.7 0.6 copy-start.10
  101.7 0.7 copy-start.11
  101.7 0.7 copy-start.16
  133.4 6.5 %collective-permute-start.8 = (f32[2,32,160]{2,1,0:T(8,128)S(1)}, f32[2,32,160]{2,1,0:T(8,128)S(1)}, u32[]{:S(2)}, u32[]{:S(2)}) collective-permute-start(f32[2,32,160]{2,1,0:T(8,128)S(1)} %slice_add_fusion.6), channel_id=1, source_target_pairs={{0,4},{4,8},{8,12},{12,16},{16,20},{20,24},{24,28},{1,5},{5,9},{9,... | collective-permute-start | bytes 122888 | tf_op jit(solution)/shard_map/ppermute | solution.py:52
  137.8 7.2 %collective-permute-start.9 = (f32[2,32,160]{2,1,0:T(8,128)S(1)}, f32[2,32,160]{2,1,0:T(8,128)S(1)}, u32[]{:S(2)}, u32[]{:S(2)}) collective-permute-start(f32[2,32,160]{2,1,0:T(8,128)S(1)} %slice_add_fusion.6), channel_id=1, source_target_pairs={{4,0},{8,4},{12,8},{16,12},{20,16},{24,20},{28,24},{5,1},{9,5},{13... | collective-permute-start | bytes 122888 | tf_op jit(solution)/shard_map/ppermute | solution.py:53
  146.3 10.9 %collective-permute-start.10 = (f32[3,64,320]{2,1,0:T(8,128)S(1)}, f32[3,64,320]{2,1,0:T(8,128)S(1)}, u32[]{:S(2)}, u32[]{:S(2)}) collective-permute-start(f32[3,64,320]{2,1,0:T(8,128)S(1)} %get-tuple-element.63), channel_id=1, source_target_pairs={{0,4},{4,8},{8,12},{12,16},{16,20},{20,24},{24,28},{1,5},{5,9},{9,... | collective-permute-start | bytes 737288 | tf_op jit(solution)/shard_map/ppermute | solution.py:52
  152.9 9.5 %collective-permute-start.11 = (f32[3,64,320]{2,1,0:T(8,128)S(1)}, f32[3,64,320]{2,1,0:T(8,128)S(1)}, u32[]{:S(2)}, u32[]{:S(2)}) collective-permute-start(f32[3,64,320]{2,1,0:T(8,128)S(1)} %get-tuple-element.64), channel_id=1, source_target_pairs={{4,0},{8,4},{12,8},{16,12},{20,16},{24,20},{28,24},{5,1},{9,5},{13... | collective-permute-start | bytes 737288 | tf_op jit(solution)/shard_map/ppermute | solution.py:53
  166.2 1.0 copy-start.4

commit v7 on v5

--- a/solution.py
+++ b/solution.py
@@ -52,6 +52,13 @@
         below.insert(0, lax.ppermute(values[low:], "alt", up))
         above.append(lax.ppermute(values[:high], "alt", down))
     return jnp.concatenate(below + [values] + above, axis=0)
+
+
+def slot_gather(values):
+    count = lax.axis_size("alt")
+    slots = jnp.zeros((count,) + values.shape, values.dtype)
+    slots = lax.dynamic_update_index_in_dim(slots, values, lax.axis_index("alt"), 0)
+    return lax.psum(slots, "alt").reshape((count * values.shape[0],) + values.shape[1:])
 
 
 def trim(values, have, want):
@@ -156,7 +163,7 @@
     rhs_three = coarsen(trim(rhs_two_x, 2, 0) - applied)
 
     height = rhs_three.shape[0]
-    column = lax.all_gather(jnp.stack([rhs_three] + coef_three, 1), "alt", axis=0, tiled=True)
+    column = slot_gather(jnp.stack([rhs_three] + coef_three, 1))
     weights_three = make_weights(pad_rows(column[:, 1]), column[:, 2], column[:, 3], 0.0625, 0)
     rhs_three_x = column[:, 0]
     coarse_part = first_sweep(weights_three, rhs_three_x, 0)

time: 158 us -> 219 us (1.39)
  the two profiles are of different devices: /device:TPU:0 before, /device:TPU:8 now
where the time goes in v7:
time: 219 us; the launch traced here: 217 us
  waiting for transfers between devices  103 us (47%)
  starting transfers between devices  59.4 us (27%)
  other arithmetic  21.9 us (10%)
  between operations  15.2 us (7%)
  matrix products  9.7 us (4%)
  local copies, waits for them, and re-layouts  7.3 us (3%)
    psum x1, waiting for transfers between devices, slot_gather(): lax.psum(slots, 'alt')  70.2 us
    ppermute x9, starting transfers between devices, alt_extend(): above.append(lax.ppermute(values[:high], 'alt', down))  29.9 us
    ppermute x9, starting transfers between devices, alt_extend(): below.insert(0, lax.ppermute(values[low:], 'alt', up))  27.7 us
    ppermute x9, waiting for transfers between devices, alt_extend(): above.append(lax.ppermute(values[:high], 'alt', down))  17.2 us
    ppermute x9, waiting for transfers between devices, alt_extend(): below.insert(0, lax.ppermute(values[low:], 'alt', up))  8.83 us
    dot_general x8, matrix products, coarsen(): summed = jnp.matmul(summed, pairing(length), precision=HIGH)  6.74 us
    ppermute x1, waiting for transfers between devices, raan_extend(): before = lax.ppermute(values[..., length - halo:], 'raan', up)  6.14 us
  transfers between devices with their start and end apart: 21, of which 18 were waited for; matrix products, arithmetic and copies ran while one was open for 9% of the time, Pallas kernels for 0%

profile of v7, /device:TPU:8, one launch (start us, length us, event | category | flops | bytes accessed | tf_op | source)
XLA Modules:
  0.0 216.7 jit_solution(933806473245259871)
XLA Ops:
  7.2 1.3 pad_maximum_fusion.1
  8.8 1.7 collective-permute-start.1
  10.5 0.6 broadcast_add_fusion.2
  11.1 0.5 iota_shift-right-logical_fusion.2
  11.7 0.6 compare_and_fusion.1
  12.2 0.5 compare_and_fusion
  12.7 0.6 fusion.241
  13.3 0.6 iota_shift-right-logical_fusion.1
  13.9 0.5 compare_and_fusion.2
  14.4 0.6 iota_shift-right-logical_fusion
  15.0 6.1 %collective-permute-done = f32[4,4,64,32]{3,2,0,1:T(8,128)S(1)} collective-permute-done((f32[4,4,64,32]{3,2,0,1:T(8,128)S(1)}, f32[4,4,64,32]{3,2,0,1:T(8,128)S(1)}, u32[]{:S(2)}, u32[]{:S(2)}) %collective-permute-start) | collective-permute-done | bytes 131104 | tf_op jit(solution)/shard_map/ppermute | solution.py:39
  21.2 0.9 collective-permute-done.1
  22.1 1.0 pad_maximum_fusion.27
  23.0 3.3 %collective-permute-start.3 = (f32[1,2,64,320]{3,2,0,1:T(8,128)}, f32[1,2,64,320]{3,2,0,1:T(8,128)}, u32[]{:S(2)}, u32[]{:S(2)}) collective-permute-start(f32[1,2,64,320]{3,2,0,1:T(8,128)} %get-tuple-element.23), channel_id=1, source_target_pairs={{4,0},{8,4},{12,8},{16,12},{20,16},{24,20},{28,24},{5,1},{9,5},{13... | collective-permute-start | bytes 491528 | tf_op jit(solution)/shard_map/ppermute | solution.py:53
  26.3 2.5 %collective-permute-start.2 = (f32[1,2,64,320]{3,2,0,1:T(8,128)}, f32[1,2,64,320]{3,2,0,1:T(8,128)}, u32[]{:S(2)}, u32[]{:S(2)}) collective-permute-start(f32[1,2,64,320]{3,2,0,1:T(8,128)} %get-tuple-element.24), channel_id=1, source_target_pairs={{0,4},{4,8},{8,12},{12,16},{16,20},{20,24},{24,28},{1,5},{5,9},{9,... | collective-permute-start | bytes 491528 | tf_op jit(solution)/shard_map/ppermute | solution.py:52
  28.9 1.6 pad_maximum_fusion
  30.5 1.1 fusion.267
  31.6 1.9 reduce_sum.73
  33.5 0.7 reduce_sum.74
  34.2 1.4 fusion.256
  35.5 1.1 fusion.252
  36.7 1.4 fusion.254
  38.6 1.0 fusion.122
  39.6 1.0 fusion.120
  42.6 2.0 fusion.72
  44.6 1.6 fusion.76
  46.3 4.3 %collective-permute-start.4 = (f32[1,64,320]{2,1,0:T(8,128)S(1)}, f32[1,64,320]{2,1,0:T(8,128)S(1)}, u32[]{:S(2)}, u32[]{:S(2)}) collective-permute-start(f32[1,64,320]{2,1,0:T(8,128)S(1)} %get-tuple-element.59), channel_id=1, source_target_pairs={{0,4},{4,8},{8,12},{12,16},{16,20},{20,24},{24,28},{1,5},{5,9},{9,... | collective-permute-start | bytes 245768 | tf_op jit(solution)/shard_map/ppermute | solution.py:52
  50.6 2.4 %collective-permute-start.5 = (f32[1,64,320]{2,1,0:T(8,128)S(1)}, f32[1,64,320]{2,1,0:T(8,128)S(1)}, u32[]{:S(2)}, u32[]{:S(2)}) collective-permute-start(f32[1,64,320]{2,1,0:T(8,128)S(1)} %get-tuple-element.60), channel_id=1, source_target_pairs={{4,0},{8,4},{12,8},{16,12},{20,16},{24,20},{28,24},{5,1},{9,5},{13... | collective-permute-start | bytes 245768 | tf_op jit(solution)/shard_map/ppermute | solution.py:53
  53.2 0.8 collective-permute-done.4
  54.0 3.2 %collective-permute-done.5 = f32[1,64,320]{2,1,0:T(8,128)S(1)} collective-permute-done((f32[1,64,320]{2,1,0:T(8,128)S(1)}, f32[1,64,320]{2,1,0:T(8,128)S(1)}, u32[]{:S(2)}, u32[]{:S(2)}) %collective-permute-start.5) | collective-permute-done | bytes 81952 | tf_op jit(solution)/shard_map/ppermute | solution.py:53
  57.2 0.5 fusion.73
  57.8 3.4 %collective-permute-start.6 = (f32[1,64,320]{2,1,0:T(8,128)S(1)}, f32[1,64,320]{2,1,0:T(8,128)S(1)}, u32[]{:S(2)}, u32[]{:S(2)}) collective-permute-start(f32[1,64,320]{2,1,0:T(8,128)S(1)} %get-tuple-element.53), channel_id=1, source_target_pairs={{0,4},{4,8},{8,12},{12,16},{16,20},{20,24},{24,28},{1,5},{5,9},{9,... | collective-permute-start | bytes 245768 | tf_op jit(solution)/shard_map/ppermute | solution.py:52
  61.2 3.3 %collective-permute-start.7 = (f32[1,64,320]{2,1,0:T(8,128)S(1)}, f32[1,64,320]{2,1,0:T(8,128)S(1)}, u32[]{:S(2)}, u32[]{:S(2)}) collective-permute-start(f32[1,64,320]{2,1,0:T(8,128)S(1)} %get-tuple-element.54), channel_id=1, source_target_pairs={{4,0},{8,4},{12,8},{16,12},{20,16},{24,20},{28,24},{5,1},{9,5},{13... | collective-permute-start | bytes 245768 | tf_op jit(solution)/shard_map/ppermute | solution.py:53
  64.7 0.5 collective-permute-done.6
  65.2 2.5 %collective-permute-done.7 = f32[1,64,320]{2,1,0:T(8,128)S(1)} collective-permute-done((f32[1,64,320]{2,1,0:T(8,128)S(1)}, f32[1,64,320]{2,1,0:T(8,128)S(1)}, u32[]{:S(2)}, u32[]{:S(2)}) %collective-permute-start.7) | collective-permute-done | bytes 81952 | tf_op jit(solution)/shard_map/ppermute | solution.py:53
  67.7 0.5 bitcast_reduce_fusion
  69.1 4.2 %collective-permute-start.9 = (f32[2,4,32,160]{3,2,0,1:T(8,128)S(1)}, f32[2,4,32,160]{3,2,0,1:T(8,128)S(1)}, u32[]{:S(2)}, u32[]{:S(2)}) collective-permute-start(f32[2,4,32,160]{3,2,0,1:T(8,128)S(1)} %pad_maximum_fusion.15), channel_id=1, source_target_pairs={{4,0},{8,4},{12,8},{16,12},{20,16},{24,20},{28,24},{5,1},{9,5},{13... | collective-permute-start | bytes 491528 | tf_op jit(solution)/shard_map/ppermute | solution.py:53
  73.3 2.0 collective-permute-start.8
  75.4 3.7 %collective-permute-start.10 = (f32[1,4,32,160]{3,2,0,1:T(8,128)S(1)}, f32[1,4,32,160]{3,2,0,1:T(8,128)S(1)}, u32[]{:S(2)}, u32[]{:S(2)}) collective-permute-start(f32[1,4,32,160]{3,2,0,1:T(8,128)S(1)} %get-tuple-element.75), channel_id=1, source_target_pairs={{0,8},{4,12},{8,16},{12,20},{16,24},{20,28},{1,9},{5,13},{9,17},{1... | collective-permute-start | bytes 245768 | tf_op jit(solution)/shard_map/ppermute | solution.py:52
  79.1 2.1 collective-permute-start.11
  81.5 2.1 collective-permute-done.8
  83.8 2.1 collective-permute-done.11
  86.6 0.8 fusion.117
  88.6 0.7 broadcast.353
  89.4 0.6 maximum_dynamic-update-slice_fusion
  90.0 70.2 %all-reduce.74.cloned.1.call-done = f32[8,4,16,80]{3,2,1,0:T(8,128)} async-done(((f32[8,4,16,80]{3,2,1,0:T(8,128)}), f32[8,4,16,80]{3,2,1,0:T(8,128)}) %all-reduce.74.cloned.1.call-update) | async-done | bytes 163856 | tf_op jit(solution)/shard_map/psum | solution.py:61
  160.2 1.0 slice_bitcast_fusion.5
  161.3 1.0 multiply_divide_fusion
  163.6 3.0 %collective-permute-start.13 = (f32[2,32,160]{2,1,0:T(8,128)S(1)}, f32[2,32,160]{2,1,0:T(8,128)S(1)}, u32[]{:S(2)}, u32[]{:S(2)}) collective-permute-start(f32[2,32,160]{2,1,0:T(8,128)S(1)} %slice_add_fusion.3), channel_id=1, source_target_pairs={{4,0},{8,4},{12,8},{16,12},{20,16},{24,20},{28,24},{5,1},{9,5},{13... | collective-permute-start | bytes 122888 | tf_op jit(solution)/shard_map/ppermute | solution.py:53
  166.7 2.8 %collective-permute-start.12 = (f32[2,32,160]{2,1,0:T(8,128)S(1)}, f32[2,32,160]{2,1,0:T(8,128)S(1)}, u32[]{:S(2)}, u32[]{:S(2)}) collective-permute-start(f32[2,32,160]{2,1,0:T(8,128)S(1)} %slice_add_fusion.3), channel_id=1, source_target_pairs={{0,4},{4,8},{8,12},{12,16},{16,20},{20,24},{24,28},{1,5},{5,9},{9,... | collective-permute-start | bytes 122888 | tf_op jit(solution)/shard_map/ppermute | solution.py:52
  169.8 4.0 %collective-permute-done.12 = f32[2,32,160]{2,1,0:T(8,128)S(1)} collective-permute-done((f32[2,32,160]{2,1,0:T(8,128)S(1)}, f32[2,32,160]{2,1,0:T(8,128)S(1)}, u32[]{:S(2)}, u32[]{:S(2)}) %collective-permute-start.12) | collective-permute-done | bytes 40992 | tf_op jit(solution)/shard_map/ppermute | solution.py:52
  175.6 2.1 collective-permute-start.14
  177.7 4.8 %collective-permute-start.15 = (f32[1,64,320]{2,1,0:T(8,128)S(1)}, f32[1,64,320]{2,1,0:T(8,128)S(1)}, u32[]{:S(2)}, u32[]{:S(2)}) collective-permute-start(f32[1,64,320]{2,1,0:T(8,128)S(1)} %get-tuple-element.48), channel_id=1, source_target_pairs={{4,0},{8,4},{12,8},{16,12},{20,16},{24,20},{28,24},{5,1},{9,5},{13... | collective-permute-start | bytes 245768 | tf_op jit(solution)/shard_map/ppermute | solution.py:53
  182.7 0.5 collective-permute-done.14
  183.2 2.2 %collective-permute-done.15 = f32[1,64,320]{2,1,0:T(8,128)S(1)} collective-permute-done((f32[1,64,320]{2,1,0:T(8,128)S(1)}, f32[1,64,320]{2,1,0:T(8,128)S(1)}, u32[]{:S(2)}, u32[]{:S(2)}) %collective-permute-start.15) | collective-permute-done | bytes 81952 | tf_op jit(solution)/shard_map/ppermute | solution.py:53
  185.3 0.5 fusion.74
  185.9 4.8 %collective-permute-start.16 = (f32[1,64,320]{2,1,0:T(8,128)S(1)}, f32[1,64,320]{2,1,0:T(8,128)S(1)}, u32[]{:S(2)}, u32[]{:S(2)}) collective-permute-start(f32[1,64,320]{2,1,0:T(8,128)S(1)} %get-tuple-element.41), channel_id=1, source_target_pairs={{0,4},{4,8},{8,12},{12,16},{16,20},{20,24},{24,28},{1,5},{5,9},{9,... | collective-permute-start | bytes 245768 | tf_op jit(solution)/shard_map/ppermute | solution.py:52
  190.8 1.9 collective-permute-start.17
  193.3 5.0 %collective-permute-done.17 = f32[1,64,320]{2,1,0:T(8,128)S(1)} collective-permute-done((f32[1,64,320]{2,1,0:T(8,128)S(1)}, f32[1,64,320]{2,1,0:T(8,128)S(1)}, u32[]{:S(2)}, u32[]{:S(2)}) %collective-permute-start.17) | collective-permute-done | bytes 81952 | tf_op jit(solution)/shard_map/ppermute | solution.py:53
  198.3 0.5 fusion.75
  198.9 1.9 collective-permute-start.18
  200.8 4.8 %collective-permute-start.19 = (f32[1,64,320]{2,1,0:T(8,128)S(1)}, f32[1,64,320]{2,1,0:T(8,128)S(1)}, u32[]{:S(2)}, u32[]{:S(2)}) collective-permute-start(f32[1,64,320]{2,1,0:T(8,128)S(1)} %get-tuple-element.38), channel_id=1, source_target_pairs={{4,0},{8,4},{12,8},{16,12},{20,16},{24,20},{28,24},{5,1},{9,5},{13... | collective-permute-start | bytes 245768 | tf_op jit(solution)/shard_map/ppermute | solution.py:53
  206.3 1.8 collective-permute-done.19
  208.3 1.6 fusion.84
  (184 shorter events, 11.3 us)
Async XLA Ops:
  7.2 153.0 %all-reduce.74.cloned.1.call-start = ((), (), s32[]{:S(2)}) async-start(), calls=%async_computation | async-start | bytes 524288 | tf_op jit(solution)/shard_map/psum | solution.py:61
  8.5 13.5 %copy-start.8 = (f32[4,64,256]{2,1,0:T(8,128)S(1)}, f32[4,64,256]{2,1,0:T(8,128)}, u32[]{:S(2)}) copy-start(f32[4,64,256]{2,1,0:T(8,128)} %param.7) | copy-start | bytes 786436
  8.5 13.5 %copy-start.9 = (f32[4,64,256]{2,1,0:T(8,128)S(1)}, f32[4,64,256]{2,1,0:T(8,128)}, u32[]{:S(2)}) copy-start(f32[4,64,256]{2,1,0:T(8,128)} %param.6) | copy-start | bytes 786436
  8.5 13.5 %copy-start.10 = (f32[4,64,256]{2,1,0:T(8,128)S(1)}, f32[4,64,256]{2,1,0:T(8,128)}, u32[]{:S(2)}) copy-start(f32[4,64,256]{2,1,0:T(8,128)} %param.5) | copy-start | bytes 786436
  8.5 13.5 %copy-start.11 = (f32[4,64,256]{2,1,0:T(8,128)S(1)}, f32[4,64,256]{2,1,0:T(8,128)}, u32[]{:S(2)}) copy-start(f32[4,64,256]{2,1,0:T(8,128)} %param.4) | copy-start | bytes 786436
  8.7 12.4 %collective-permute-start = (f32[4,4,64,32]{3,2,0,1:T(8,128)S(1)}, f32[4,4,64,32]{3,2,0,1:T(8,128)S(1)}, u32[]{:S(2)}, u32[]{:S(2)}) collective-permute-start(f32[4,4,64,32]{3,2,0,1:T(8,128)S(1)} %get-tuple-element.31), channel_id=1, source_target_pairs={{0,1},{1,2},{2,3},{3,0},{4,5},{5,6},{6,7},{7,4},{8,9},{9,10},{10,1... | collective-permute-start | bytes 393224 | tf_op jit(solution)/shard_map/ppermute | solution.py:39
  8.8 13.2 %collective-permute-start.1 = (f32[4,4,64,32]{3,2,0,1:T(8,128)S(1)}, f32[4,4,64,32]{3,2,0,1:T(8,128)S(1)}, u32[]{:S(2)}, u32[]{:S(2)}) collective-permute-start(f32[4,4,64,32]{3,2,0,1:T(8,128)S(1)} %get-tuple-element.32), channel_id=1, source_target_pairs={{1,0},{2,1},{3,2},{0,3},{5,4},{6,5},{7,6},{4,7},{9,8},{10,9},{11,1... | collective-permute-start | bytes 393224 | tf_op jit(solution)/shard_map/ppermute | solution.py:40
  22.0 4.3 %copy-start.14 = (f32[4,4,64,32]{3,2,0,1:T(8,128)}, f32[4,4,64,32]{3,2,0,1:T(8,128)S(1)}, u32[]{:S(2)}) copy-start(f32[4,4,64,32]{3,2,0,1:T(8,128)S(1)} %collective-permute-done.1) | copy-start | bytes 393220
  23.0 19.5 %collective-permute-start.3 = (f32[1,2,64,320]{3,2,0,1:T(8,128)}, f32[1,2,64,320]{3,2,0,1:T(8,128)}, u32[]{:S(2)}, u32[]{:S(2)}) collective-permute-start(f32[1,2,64,320]{3,2,0,1:T(8,128)} %get-tuple-element.23), channel_id=1, source_target_pairs={{4,0},{8,4},{12,8},{16,12},{20,16},{24,20},{28,24},{5,1},{9,5},{13... | collective-permute-start | bytes 491528 | tf_op jit(solution)/shard_map/ppermute | solution.py:53
  26.3 16.2 %collective-permute-start.2 = (f32[1,2,64,320]{3,2,0,1:T(8,128)}, f32[1,2,64,320]{3,2,0,1:T(8,128)}, u32[]{:S(2)}, u32[]{:S(2)}) collective-permute-start(f32[1,2,64,320]{3,2,0,1:T(8,128)} %get-tuple-element.24), channel_id=1, source_target_pairs={{0,4},{4,8},{8,12},{12,16},{16,20},{20,24},{24,28},{1,5},{5,9},{9,... | collective-permute-start | bytes 491528 | tf_op jit(solution)/shard_map/ppermute | solution.py:52
  31.6 9.4 %copy-start.2 = (f32[4,64,320]{2,1,0:T(8,128)}, f32[4,64,320]{2,1,0:T(8,128)S(1)}, u32[]{:S(2)}) copy-start(f32[4,64,320]{2,1,0:T(8,128)S(1)} %get-tuple-element.30) | copy-start | bytes 983044
  34.1 6.4 %copy-start.34 = (s32[160]{0:T(256)S(1)}, s32[160]{0:T(256)}, u32[]{:S(2)}) copy-start(s32[160]{0:T(256)} %get-tuple-element.122) | copy-start | bytes 1924
  34.1 6.4 %copy-start.37 = (s32[160]{0:T(256)S(1)}, s32[160]{0:T(256)}, u32[]{:S(2)}) copy-start(s32[160]{0:T(256)} %get-tuple-element.123) | copy-start | bytes 1924
  34.1 6.4 %copy-start.48 = (pred[160]{0:T(512)(128)(4,1)S(1)}, pred[160]{0:T(512)(128)(4,1)}, u32[]{:S(2)}) copy-start(pred[160]{0:T(512)(128)(4,1)} %compare_and_fusion) | copy-start | bytes 484
  44.6 23.1 %copy-start = (f32[4,64,320]{2,1,0:T(8,128)}, f32[4,64,320]{2,1,0:T(8,128)S(1)}, u32[]{:S(2)}) copy-start(f32[4,64,320]{2,1,0:T(8,128)S(1)} %get-tuple-element.8) | copy-start | bytes 983044
  46.3 7.8 %collective-permute-start.4 = (f32[1,64,320]{2,1,0:T(8,128)S(1)}, f32[1,64,320]{2,1,0:T(8,128)S(1)}, u32[]{:S(2)}, u32[]{:S(2)}) collective-permute-start(f32[1,64,320]{2,1,0:T(8,128)S(1)} %get-tuple-element.59), channel_id=1, source_target_pairs={{0,4},{4,8},{8,12},{12,16},{16,20},{20,24},{24,28},{1,5},{5,9},{9,... | collective-permute-start | bytes 245768 | tf_op jit(solution)/shard_map/ppermute | solution.py:52
  50.6 6.6 %collective-permute-start.5 = (f32[1,64,320]{2,1,0:T(8,128)S(1)}, f32[1,64,320]{2,1,0:T(8,128)S(1)}, u32[]{:S(2)}, u32[]{:S(2)}) collective-permute-start(f32[1,64,320]{2,1,0:T(8,128)S(1)} %get-tuple-element.60), channel_id=1, source_target_pairs={{4,0},{8,4},{12,8},{16,12},{20,16},{24,20},{28,24},{5,1},{9,5},{13... | collective-permute-start | bytes 245768 | tf_op jit(solution)/shard_map/ppermute | solution.py:53
  57.8 7.5 %collective-permute-start.6 = (f32[1,64,320]{2,1,0:T(8,128)S(1)}, f32[1,64,320]{2,1,0:T(8,128)S(1)}, u32[]{:S(2)}, u32[]{:S(2)}) collective-permute-start(f32[1,64,320]{2,1,0:T(8,128)S(1)} %get-tuple-element.53), channel_id=1, source_target_pairs={{0,4},{4,8},{8,12},{12,16},{16,20},{20,24},{24,28},{1,5},{5,9},{9,... | collective-permute-start | bytes 245768 | tf_op jit(solution)/shard_map/ppermute | solution.py:52
  61.2 6.5 %collective-permute-start.7 = (f32[1,64,320]{2,1,0:T(8,128)S(1)}, f32[1,64,320]{2,1,0:T(8,128)S(1)}, u32[]{:S(2)}, u32[]{:S(2)}) collective-permute-start(f32[1,64,320]{2,1,0:T(8,128)S(1)} %get-tuple-element.54), channel_id=1, source_target_pairs={{4,0},{8,4},{12,8},{16,12},{20,16},{24,20},{28,24},{5,1},{9,5},{13... | collective-permute-start | bytes 245768 | tf_op jit(solution)/shard_map/ppermute | solution.py:53
  67.7 0.7 copy-start.32
  67.7 0.7 copy-start.40
  69.0 18.5 %copy-start.12 = (f32[32,2,160]{2,0,1:T(8,128)}, f32[32,2,160]{2,0,1:T(8,128)S(1)}, u32[]{:S(2)}) copy-start(f32[32,2,160]{2,0,1:T(8,128)S(1)} %convolution_multiply_fusion.3) | copy-start | bytes 122884
  69.1 12.4 %collective-permute-start.9 = (f32[2,4,32,160]{3,2,0,1:T(8,128)S(1)}, f32[2,4,32,160]{3,2,0,1:T(8,128)S(1)}, u32[]{:S(2)}, u32[]{:S(2)}) collective-permute-start(f32[2,4,32,160]{3,2,0,1:T(8,128)S(1)} %pad_maximum_fusion.15), channel_id=1, source_target_pairs={{4,0},{8,4},{12,8},{16,12},{20,16},{24,20},{28,24},{5,1},{9,5},{13... | collective-permute-start | bytes 491528 | tf_op jit(solution)/shard_map/ppermute | solution.py:53
  73.3 10.3 %collective-permute-start.8 = (f32[2,4,32,160]{3,2,0,1:T(8,128)S(1)}, f32[2,4,32,160]{3,2,0,1:T(8,128)S(1)}, u32[]{:S(2)}, u32[]{:S(2)}) collective-permute-start(f32[2,4,32,160]{3,2,0,1:T(8,128)S(1)} %pad_maximum_fusion.15), channel_id=1, source_target_pairs={{0,4},{4,8},{8,12},{12,16},{16,20},{20,24},{24,28},{1,5},{5,9},{9,... | collective-permute-start | bytes 491528 | tf_op jit(solution)/shard_map/ppermute | solution.py:52
  75.4 8.5 %collective-permute-start.10 = (f32[1,4,32,160]{3,2,0,1:T(8,128)S(1)}, f32[1,4,32,160]{3,2,0,1:T(8,128)S(1)}, u32[]{:S(2)}, u32[]{:S(2)}) collective-permute-start(f32[1,4,32,160]{3,2,0,1:T(8,128)S(1)} %get-tuple-element.75), channel_id=1, source_target_pairs={{0,8},{4,12},{8,16},{12,20},{16,24},{20,28},{1,9},{5,13},{9,17},{1... | collective-permute-start | bytes 245768 | tf_op jit(solution)/shard_map/ppermute | solution.py:52
  79.1 6.9 %collective-permute-start.11 = (f32[1,4,32,160]{3,2,0,1:T(8,128)S(1)}, f32[1,4,32,160]{3,2,0,1:T(8,128)S(1)}, u32[]{:S(2)}, u32[]{:S(2)}) collective-permute-start(f32[1,4,32,160]{3,2,0,1:T(8,128)S(1)} %get-tuple-element.76), channel_id=1, source_target_pairs={{8,0},{12,4},{16,8},{20,12},{24,16},{28,20},{9,1},{13,5},{17,9},{2... | collective-permute-start | bytes 245768 | tf_op jit(solution)/shard_map/ppermute | solution.py:53
  83.8 3.7 %copy-start.4 = (f32[6,31,160]{2,1,0:T(8,128)}, f32[6,31,160]{2,1,0:T(8,128)S(1)}, u32[]{:S(2)}) copy-start(f32[6,31,160]{2,1,0:T(8,128)S(1)} %fusion.85) | copy-start | bytes 357124
  86.2 1.3 copy-start.15
  86.2 1.3 copy-start.17
  86.2 1.3 copy-start.19
  86.2 1.3 copy-start.21
  86.3 1.3 copy-start.23
  86.6 1.5 copy-start.35
  86.6 1.5 copy-start.38
  86.6 1.5 copy-start.49
  160.2 2.2 %copy-start.26 = (f32[8,4,16,80]{3,2,1,0:T(8,128)S(1)}, f32[8,4,16,80]{3,2,1,0:T(8,128)}, u32[]{:S(2)}) copy-start(f32[8,4,16,80]{3,2,1,0:T(8,128)} %all-reduce.74.cloned.1.call-done) | copy-start | bytes 491524
  162.4 0.7 copy-start.39
  162.5 0.8 copy-start.43
  162.5 0.9 copy-start.45
  162.5 0.9 copy-start.47
  162.5 1.1 copy-start.7
  162.8 11.2 %copy-start.5 = (f32[6,31,160]{2,1,0:T(8,128)S(1)}, f32[6,31,160]{2,1,0:T(8,128)}, u32[]{:S(2)}) copy-start(f32[6,31,160]{2,1,0:T(8,128)} %copy-done.4) | copy-start | bytes 357124
  162.8 11.2 %copy-start.16 = (f32[6,32,160]{2,1,0:T(8,128)S(1)}, f32[6,32,160]{2,1,0:T(8,128)}, u32[]{:S(2)}) copy-start(f32[6,32,160]{2,1,0:T(8,128)} %copy-done.15) | copy-start | bytes 368644
  162.8 11.2 %copy-start.18 = (f32[6,1,32,160]{3,2,0,1:T(8,128)S(1)}, f32[6,1,32,160]{3,2,0,1:T(8,128)}, u32[]{:S(2)}) copy-start(f32[6,1,32,160]{3,2,0,1:T(8,128)} %copy-done.17) | copy-start | bytes 368644
  162.8 11.2 %copy-start.20 = (f32[6,1,32,160]{3,2,0,1:T(8,128)S(1)}, f32[6,1,32,160]{3,2,0,1:T(8,128)}, u32[]{:S(2)}) copy-start(f32[6,1,32,160]{3,2,0,1:T(8,128)} %copy-done.19) | copy-start | bytes 368644
  162.8 11.2 %copy-start.22 = (f32[6,32,160]{2,1,0:T(8,128)S(1)}, f32[6,32,160]{2,1,0:T(8,128)}, u32[]{:S(2)}) copy-start(f32[6,32,160]{2,1,0:T(8,128)} %copy-done.21) | copy-start | bytes 368644
  162.8 11.2 %copy-start.24 = (f32[6,32,160]{2,1,0:T(8,128)S(1)}, f32[6,32,160]{2,1,0:T(8,128)}, u32[]{:S(2)}) copy-start(f32[6,32,160]{2,1,0:T(8,128)} %copy-done.23) | copy-start | bytes 368644
  162.8 11.2 %copy-start.27 = (f32[4,32,160]{2,1,0:T(8,128)S(1)}, f32[4,32,160]{2,1,0:T(8,128)}, u32[]{:S(2)}) copy-start(f32[4,32,160]{2,1,0:T(8,128)} %get-tuple-element.16) | copy-start | bytes 245764
  162.8 11.2 %copy-start.29 = (pred[4]{0:T(512)(128)(4,1)S(1)}, pred[4]{0:T(512)(128)(4,1)}, u32[]{:S(2)}) copy-start(pred[4]{0:T(512)(128)(4,1)} %compare_and_fusion.2) | copy-start | bytes 16
  163.6 6.2 %collective-permute-start.13 = (f32[2,32,160]{2,1,0:T(8,128)S(1)}, f32[2,32,160]{2,1,0:T(8,128)S(1)}, u32[]{:S(2)}, u32[]{:S(2)}) collective-permute-start(f32[2,32,160]{2,1,0:T(8,128)S(1)} %slice_add_fusion.3), channel_id=1, source_target_pairs={{4,0},{8,4},{12,8},{16,12},{20,16},{24,20},{28,24},{5,1},{9,5},{13... | collective-permute-start | bytes 122888 | tf_op jit(solution)/shard_map/ppermute | solution.py:53
  166.7 7.1 %collective-permute-start.12 = (f32[2,32,160]{2,1,0:T(8,128)S(1)}, f32[2,32,160]{2,1,0:T(8,128)S(1)}, u32[]{:S(2)}, u32[]{:S(2)}) collective-permute-start(f32[2,32,160]{2,1,0:T(8,128)S(1)} %slice_add_fusion.3), channel_id=1, source_target_pairs={{0,4},{4,8},{8,12},{12,16},{16,20},{20,24},{24,28},{1,5},{5,9},{9,... | collective-permute-start | bytes 122888 | tf_op jit(solution)/shard_map/ppermute | solution.py:52
  173.9 0.8 copy-start.13
  173.9 0.8 copy-start.31
  173.9 0.8 copy-start.33
  173.9 0.8 copy-start.41
  175.5 9.8 %copy-start.1 = (f32[4,64,320]{2,1,0:T(8,128)S(1)}, f32[4,64,320]{2,1,0:T(8,128)}, u32[]{:S(2)}) copy-start(f32[4,64,320]{2,1,0:T(8,128)} %copy-done) | copy-start | bytes 983044
  175.6 7.5 %collective-permute-start.14 = (f32[1,64,320]{2,1,0:T(8,128)S(1)}, f32[1,64,320]{2,1,0:T(8,128)S(1)}, u32[]{:S(2)}, u32[]{:S(2)}) collective-permute-start(f32[1,64,320]{2,1,0:T(8,128)S(1)} %get-tuple-element.47), channel_id=1, source_target_pairs={{0,4},{4,8},{8,12},{12,16},{16,20},{20,24},{24,28},{1,5},{5,9},{9,... | collective-permute-start | bytes 245768 | tf_op jit(solution)/shard_map/ppermute | solution.py:52
  177.7 7.7 %collective-permute-start.15 = (f32[1,64,320]{2,1,0:T(8,128)S(1)}, f32[1,64,320]{2,1,0:T(8,128)S(1)}, u32[]{:S(2)}, u32[]{:S(2)}) collective-permute-start(f32[1,64,320]{2,1,0:T(8,128)S(1)} %get-tuple-element.48), channel_id=1, source_target_pairs={{4,0},{8,4},{12,8},{16,12},{20,16},{24,20},{28,24},{5,1},{9,5},{13... | collective-permute-start | bytes 245768 | tf_op jit(solution)/shard_map/ppermute | solution.py:53
  185.9 7.4 %collective-permute-start.16 = (f32[1,64,320]{2,1,0:T(8,128)S(1)}, f32[1,64,320]{2,1,0:T(8,128)S(1)}, u32[]{:S(2)}, u32[]{:S(2)}) collective-permute-start(f32[1,64,320]{2,1,0:T(8,128)S(1)} %get-tuple-element.41), channel_id=1, source_target_pairs={{0,4},{4,8},{8,12},{12,16},{16,20},{20,24},{24,28},{1,5},{5,9},{9,... | collective-permute-start | bytes 245768 | tf_op jit(solution)/shard_map/ppermute | solution.py:52
  190.8 7.6 %collective-permute-start.17 = (f32[1,64,320]{2,1,0:T(8,128)S(1)}, f32[1,64,320]{2,1,0:T(8,128)S(1)}, u32[]{:S(2)}, u32[]{:S(2)}) collective-permute-start(f32[1,64,320]{2,1,0:T(8,128)S(1)} %get-tuple-element.42), channel_id=1, source_target_pairs={{4,0},{8,4},{12,8},{16,12},{20,16},{24,20},{28,24},{5,1},{9,5},{13... | collective-permute-start | bytes 245768 | tf_op jit(solution)/shard_map/ppermute | solution.py:53
  198.9 7.4 %collective-permute-start.18 = (f32[1,64,320]{2,1,0:T(8,128)S(1)}, f32[1,64,320]{2,1,0:T(8,128)S(1)}, u32[]{:S(2)}, u32[]{:S(2)}) collective-permute-start(f32[1,64,320]{2,1,0:T(8,128)S(1)} %get-tuple-element.37), channel_id=1, source_target_pairs={{0,4},{4,8},{8,12},{12,16},{16,20},{20,24},{24,28},{1,5},{5,9},{9,... | collective-permute-start | bytes 245768 | tf_op jit(solution)/shard_map/ppermute | solution.py:52
  200.8 7.2 %collective-permute-start.19 = (f32[1,64,320]{2,1,0:T(8,128)S(1)}, f32[1,64,320]{2,1,0:T(8,128)S(1)}, u32[]{:S(2)}, u32[]{:S(2)}) collective-permute-start(f32[1,64,320]{2,1,0:T(8,128)S(1)} %get-tuple-element.38), channel_id=1, source_target_pairs={{4,0},{8,4},{12,8},{16,12},{20,16},{24,20},{28,24},{5,1},{9,5},{13... | collective-permute-start | bytes 245768 | tf_op jit(solution)/shard_map/ppermute | solution.py:53
  205.8 2.4 %copy-start.3 = (f32[4,64,320]{2,1,0:T(8,128)S(1)}, f32[4,64,320]{2,1,0:T(8,128)}, u32[]{:S(2)}) copy-start(f32[4,64,320]{2,1,0:T(8,128)} %copy-done.2) | copy-start | bytes 983044
  205.8 2.4 %copy-start.25 = (f32[4,64,320]{2,1,0:T(8,128)S(1)}, f32[4,64,320]{2,1,0:T(8,128)}, u32[]{:S(2)}) copy-start(f32[4,64,320]{2,1,0:T(8,128)} %get-tuple-element.4) | copy-start | bytes 983044
  (8 other events, 5.3 us)
Sparse Core Ops, SparseCore 0:
  90.1 69.9 all-reduce.73

commit v8 on v6

--- a/solution.py
+++ b/solution.py
@@ -131,22 +131,21 @@
 def shards(source, k_alt, k_inc, k_raan):
     length = source.shape[-1]
     halo_r = min(RAAN_HALO, length)
-    wide = raan_extend(jnp.stack([source, k_alt, k_inc, k_raan], axis=1), halo_r)
-    wide_source, wide_alt, wide_inc, wide_raan = (wide[:, i] for i in range(4))
+    wide = raan_extend(jnp.stack([k_alt, source, k_inc, k_raan], axis=1), halo_r)
+    wide_alt, wide_source, wide_inc, wide_raan = (wide[:, i] for i in range(4))
     coef_two = [coarsen(part) for part in (wide_alt, wide_inc, wide_raan)]
     coef_three = [coarsen(part) for part in coef_two]
 
     reach = SWEEPS + 1
-    first = alt_extend(wide, reach)
-    source_x = first[:, 0]
-    weights_one = make_weights(
-        first[:, 1], trim(first[:, 2], reach, reach - 1), trim(first[:, 3], reach, reach - 1), 1.0, reach - 1
-    )
+    alt_x = alt_extend(wide[:, 0], reach)
+    rest = alt_extend(wide[:, 1:4], reach - 1)
+    source_x = rest[:, 0]
+    weights_one = make_weights(alt_x, rest[:, 1], rest[:, 2], 1.0, reach - 1)
 
     density = source_x
-    for halo in range(reach, 1, -1):
-        density = sweep(weights_one, density, halo, source_x, reach)
-    applied, density = apply_op(weights_one, density, 1)
+    for halo in range(reach - 1, 0, -1):
+        density = sweep(weights_one, density, halo, source_x, reach - 1)
+    applied, density = apply_op(weights_one, alt_extend(density, 1), 1)
     rhs_two = coarsen(wide_source - applied)
 
     level_two = alt_extend(jnp.stack([rhs_two] + coef_two, 1), 3)
@@ -175,7 +174,7 @@
 
     density = alt_extend(density + refine(correction), reach)
     for halo in range(reach, 1, -1):
-        density = sweep(weights_one, density, halo, source_x, reach)
+        density = sweep(weights_one, density, halo, source_x, reach - 1)
     applied, centre = apply_op(weights_one, density, 1)
     scaled_residual = (wide_source - applied) / trim(weights_one[0][6], weights_one[1], 0)
     keep = slice(halo_r, halo_r + length)

time: 169 us -> 164 us (0.970)
  starting transfers between devices: 34.7 us -> 46.8 us
  waiting for transfers between devices: 59.3 us -> 48.9 us
  other arithmetic: 23.6 us -> 18.5 us
    ppermute x5 -> x7, waiting for transfers between devices: 42.6 us -> 25.6 us  [alt_extend(): below.insert(0, lax.ppermute(values[low:], 'alt', up))]
    ppermute x5 -> x7, starting transfers between devices: 21.2 us -> 27.3 us  [alt_extend(): below.insert(0, lax.ppermute(values[low:], 'alt', up))]
    ppermute x5 -> x7, starting transfers between devices: 11.7 us -> 17.8 us  [alt_extend(): above.append(lax.ppermute(values[:high], 'alt', down))]
    ppermute x5 -> x7, waiting for transfers between devices: 10.3 us -> 15.6 us  [alt_extend(): above.append(lax.ppermute(values[:high], 'alt', down))]
    concatenate x4 -> x5, other arithmetic: 3.42 us -> 1.43 us  [alt_extend(): return jnp.concatenate(below + [values] + above, axis=0)]
    select_n x6 -> x5, other arithmetic: 4.2 us -> 3.21 us  [sweep(): return jnp.where(inside(updated.shape, halo - 1), updated, 0.0)]
  transfers between devices with their start and end apart: 12 -> 16, of which waited for: 7 -> 9; matrix products, arithmetic and copies ran while one was open for 11% -> 10% of each run, Pallas kernels for 0% -> 0%
where the time goes in v8:
time: 164 us
  waiting for transfers between devices  48.9 us (30%)
  starting transfers between devices  46.8 us (29%)
  blocking collectives  28.3 us (17%)
  other arithmetic  18.5 us (11%)
  matrix products  10.2 us (6%)
  local copies, waits for them, and re-layouts  9.46 us (6%)
    all_gather x1, blocking collectives, shards(): lax.all_gather(jnp.stack([rhs_three] + coef_three, 1), 'alt', axis=0, til...  28.3 us
    ppermute x7, starting transfers between devices, alt_extend(): below.insert(0, lax.ppermute(values[low:], 'alt', up))  27.3 us
    ppermute x7, waiting for transfers between devices, alt_extend(): below.insert(0, lax.ppermute(values[low:], 'alt', up))  25.6 us
    ppermute x7, starting transfers between devices, alt_extend(): above.append(lax.ppermute(values[:high], 'alt', down))  17.8 us
    ppermute x7, waiting for transfers between devices, alt_extend(): above.append(lax.ppermute(values[:high], 'alt', down))  15.6 us
    ppermute x1, waiting for transfers between devices, raan_extend(): before = lax.ppermute(values[..., length - halo:], 'raan', up)  6.79 us
    dot_general x8, matrix products, coarsen(): summed = jnp.matmul(summed, pairing(length), precision=HIGH)  6.5 us
    reduce_sum x5, other arithmetic, coarsen(): summed = values.reshape(depth // 2, 2, width, length).sum(axis=1)  3.37 us
  transfers between devices with their start and end apart: 16, of which 9 were waited for; matrix products, arithmetic and copies ran while one was open for 10% of the time, Pallas kernels for 0%

profile of v8, /device:TPU:20, one launch (start us, length us, event | category | flops | bytes accessed | tf_op | source)
XLA Modules:
  0.0 163.6 jit_solution(16824221980216143316)
XLA Ops:
  0.6 1.3 pad_maximum_fusion.2
  2.2 1.7 %collective-permute-start.1 = (f32[4,4,64,32]{3,2,0,1:T(8,128)S(1)}, f32[4,4,64,32]{3,2,0,1:T(8,128)}, u32[]{:S(2)}, u32[]{:S(2)}) collective-permute-start(f32[4,4,64,32]{3,2,0,1:T(8,128)S(1)} %get-tuple-element.33), channel_id=1, source_target_pairs={{1,0},{2,1},{3,2},{0,3},{5,4},{6,5},{7,6},{4,7},{9,8},{10,9},{11,1... | collective-permute-start | bytes 393224 | tf_op jit(solution)/shard_map/ppermute | solution.py:40
  4.0 0.5 compare_and_fusion.5
  4.5 0.6 iota_shift-right-logical_fusion.1
  5.1 0.5 compare_and_fusion
  5.6 0.5 broadcast_add_fusion.2
  6.1 0.6 compare_and_fusion.1
  6.7 0.5 iota_shift-right-logical_fusion.2
  7.2 0.6 compare_and_fusion.2
  7.8 6.8 %collective-permute-done = f32[4,4,64,32]{3,2,0,1:T(8,128)S(1)} collective-permute-done((f32[4,4,64,32]{3,2,0,1:T(8,128)S(1)}, f32[4,4,64,32]{3,2,0,1:T(8,128)S(1)}, u32[]{:S(2)}, u32[]{:S(2)}) %collective-permute-start) | collective-permute-done | bytes 131104 | tf_op jit(solution)/shard_map/ppermute | solution.py:39
  14.6 0.9 collective-permute-done.1
  15.5 1.6 %pad_maximum_fusion.1 = f32[4,4,64,320]{3,2,0,1:T(8,128)S(1)} fusion(f32[4,4,64,32]{3,2,0,1:T(8,128)} %collective-permute-done.1, f32[4,1,64,256]{3,2,0,1:T(8,128)S(1)} %bitcast.250, f32[4,1,64,256]{3,2,0,1:T(8,128)S(1)} %bitcast.252, f32[4,1,64,256]{3,2,0,1:T(8,128)S(1)} %bitcast.254, f32[4,1,64,256]{3,2,0,1:T(8,128)S(1)} %bitcast.256, ...), kind=kLoop, calls=%fused_computation.1 | loop fusion | flops 1638400 | bytes 2621440 | tf_op jit(solution)/shard_map/concatenate | solution.py:41
  17.1 1.2 fusion.253
  18.3 1.2 slice_bitcast_fusion.4
  19.5 0.9 slice_bitcast_fusion.6
  20.3 3.4 %collective-permute-start.2 = (f32[2,3,64,320]{3,2,0,1:T(8,128)}, f32[2,3,64,320]{3,2,0,1:T(8,128)S(1)}, u32[]{:S(2)}, u32[]{:S(2)}) collective-permute-start(f32[2,3,64,320]{3,2,0,1:T(8,128)} %get-tuple-element.30), channel_id=1, source_target_pairs={{0,4},{4,8},{8,12},{12,16},{16,20},{20,24},{24,28},{1,5},{5,9},{9,... | collective-permute-start | bytes 1474568 | tf_op jit(solution)/shard_map/ppermute | solution.py:52
  23.8 2.4 %collective-permute-start.3 = (f32[2,3,64,320]{3,2,0,1:T(8,128)}, f32[2,3,64,320]{3,2,0,1:T(8,128)S(1)}, u32[]{:S(2)}, u32[]{:S(2)}) collective-permute-start(f32[2,3,64,320]{3,2,0,1:T(8,128)} %get-tuple-element.31), channel_id=1, source_target_pairs={{4,0},{8,4},{12,8},{16,12},{20,16},{24,20},{28,24},{5,1},{9,5},{13... | collective-permute-start | bytes 1474568 | tf_op jit(solution)/shard_map/ppermute | solution.py:53
  26.2 4.3 %collective-permute-start.4 = (f32[3,64,320]{2,1,0:T(8,128)}, f32[3,64,320]{2,1,0:T(8,128)}, u32[]{:S(2)}, u32[]{:S(2)}) collective-permute-start(f32[3,64,320]{2,1,0:T(8,128)} %get-tuple-element.28), channel_id=1, source_target_pairs={{0,4},{4,8},{8,12},{12,16},{16,20},{20,24},{24,28},{1,5},{5,9},{9,... | collective-permute-start | bytes 737288 | tf_op jit(solution)/shard_map/ppermute | solution.py:52
  30.5 1.9 %collective-permute-start.5 = (f32[3,64,320]{2,1,0:T(8,128)}, f32[3,64,320]{2,1,0:T(8,128)}, u32[]{:S(2)}, u32[]{:S(2)}) collective-permute-start(f32[3,64,320]{2,1,0:T(8,128)} %get-tuple-element.29), channel_id=1, source_target_pairs={{4,0},{8,4},{12,8},{16,12},{20,16},{24,20},{28,24},{5,1},{9,5},{13... | collective-permute-start | bytes 737288 | tf_op jit(solution)/shard_map/ppermute | solution.py:53
  32.5 1.0 reduce_sum.73
  33.5 1.7 %reduce_sum.74 = f32[2,64,320]{2,1,0:T(8,128)} reduce(f32[2,2,64,320]{3,2,1,0:T(8,128)} %bitcast.247, f32[]{:T(128)} %constant.151.clone.1), dimensions={1}, to_apply=%region_2.3 | reduce | flops 40960 | bytes 491524 | tf_op jit(solution)/shard_map/reduce_sum | solution.py:21
  35.2 0.4 fusion.242
  35.7 1.4 fusion.240
  37.5 1.1 fusion.238
  38.8 0.9 fusion.106
  39.8 0.9 fusion.107
  40.7 1.0 fusion.108
  41.7 0.9 fusion
  43.4 20.6 %collective-permute-done.4 = f32[3,64,320]{2,1,0:T(8,128)} collective-permute-done((f32[3,64,320]{2,1,0:T(8,128)}, f32[3,64,320]{2,1,0:T(8,128)}, u32[]{:S(2)}, u32[]{:S(2)}) %collective-permute-start.4) | collective-permute-done | bytes 245792 | tf_op jit(solution)/shard_map/ppermute | solution.py:52
  64.0 1.1 pad_maximum_fusion.3
  65.9 0.3 fusion.260
  66.2 0.7 add_add_fusion
  66.9 0.8 fusion.43
  68.0 0.3 copy-done.13
  68.3 0.6 fusion.257
  69.0 4.3 %collective-permute-start.6 = (f32[1,64,320]{2,1,0:T(8,128)S(1)}, f32[1,64,320]{2,1,0:T(8,128)S(1)}, u32[]{:S(2)}, u32[]{:S(2)}) collective-permute-start(f32[1,64,320]{2,1,0:T(8,128)S(1)} %get-tuple-element.67), channel_id=1, source_target_pairs={{0,4},{4,8},{8,12},{12,16},{16,20},{20,24},{24,28},{1,5},{5,9},{9,... | collective-permute-start | bytes 245768 | tf_op jit(solution)/shard_map/ppermute | solution.py:52
  73.3 1.9 %collective-permute-start.7 = (f32[1,64,320]{2,1,0:T(8,128)S(1)}, f32[1,64,320]{2,1,0:T(8,128)S(1)}, u32[]{:S(2)}, u32[]{:S(2)}) collective-permute-start(f32[1,64,320]{2,1,0:T(8,128)S(1)} %get-tuple-element.68), channel_id=1, source_target_pairs={{4,0},{8,4},{12,8},{16,12},{20,16},{24,20},{28,24},{5,1},{9,5},{13... | collective-permute-start | bytes 245768 | tf_op jit(solution)/shard_map/ppermute | solution.py:53
  75.7 5.1 %collective-permute-done.7 = f32[1,64,320]{2,1,0:T(8,128)S(1)} collective-permute-done((f32[1,64,320]{2,1,0:T(8,128)S(1)}, f32[1,64,320]{2,1,0:T(8,128)S(1)}, u32[]{:S(2)}, u32[]{:S(2)}) %collective-permute-start.7) | collective-permute-done | bytes 81952 | tf_op jit(solution)/shard_map/ppermute | solution.py:53
  80.7 0.5 bitcast_reduce_fusion
  81.4 0.4 fusion.244
  82.1 2.3 %collective-permute-start.8 = (f32[2,4,32,160]{3,2,0,1:T(8,128)S(1)}, f32[2,4,32,160]{3,2,0,1:T(8,128)S(1)}, u32[]{:S(2)}, u32[]{:S(2)}) collective-permute-start(f32[2,4,32,160]{3,2,0,1:T(8,128)S(1)} %pad_maximum_fusion.10), channel_id=1, source_target_pairs={{0,4},{4,8},{8,12},{12,16},{16,20},{20,24},{24,28},{1,5},{5,9},{9,... | collective-permute-start | bytes 491528 | tf_op jit(solution)/shard_map/ppermute | solution.py:52
  84.4 3.6 %collective-permute-start.9 = (f32[2,4,32,160]{3,2,0,1:T(8,128)S(1)}, f32[2,4,32,160]{3,2,0,1:T(8,128)S(1)}, u32[]{:S(2)}, u32[]{:S(2)}) collective-permute-start(f32[2,4,32,160]{3,2,0,1:T(8,128)S(1)} %pad_maximum_fusion.10), channel_id=1, source_target_pairs={{4,0},{8,4},{12,8},{16,12},{20,16},{24,20},{28,24},{5,1},{9,5},{13... | collective-permute-start | bytes 491528 | tf_op jit(solution)/shard_map/ppermute | solution.py:53
  88.0 1.9 %collective-permute-start.10 = (f32[1,4,32,160]{3,2,0,1:T(8,128)S(1)}, f32[1,4,32,160]{3,2,0,1:T(8,128)S(1)}, u32[]{:S(2)}, u32[]{:S(2)}) collective-permute-start(f32[1,4,32,160]{3,2,0,1:T(8,128)S(1)} %get-tuple-element.77), channel_id=1, source_target_pairs={{0,8},{4,12},{8,16},{12,20},{16,24},{20,28},{1,9},{5,13},{9,17},{1... | collective-permute-start | bytes 245768 | tf_op jit(solution)/shard_map/ppermute | solution.py:52
  89.9 3.9 %collective-permute-start.11 = (f32[1,4,32,160]{3,2,0,1:T(8,128)S(1)}, f32[1,4,32,160]{3,2,0,1:T(8,128)S(1)}, u32[]{:S(2)}, u32[]{:S(2)}) collective-permute-start(f32[1,4,32,160]{3,2,0,1:T(8,128)S(1)} %get-tuple-element.78), channel_id=1, source_target_pairs={{8,0},{12,4},{16,8},{20,12},{24,16},{28,20},{9,1},{13,5},{17,9},{2... | collective-permute-start | bytes 245768 | tf_op jit(solution)/shard_map/ppermute | solution.py:53
  93.8 2.6 %collective-permute-done.8 = f32[2,4,32,160]{3,2,0,1:T(8,128)S(1)} collective-permute-done((f32[2,4,32,160]{3,2,0,1:T(8,128)S(1)}, f32[2,4,32,160]{3,2,0,1:T(8,128)S(1)}, u32[]{:S(2)}, u32[]{:S(2)}) %collective-permute-start.8) | collective-permute-done | bytes 163872 | tf_op jit(solution)/shard_map/ppermute | solution.py:52
  97.1 0.3 copy-done.6
  98.4 0.3 fusion.3
  98.7 28.3 %all_gather.3 = f32[8,4,16,80]{3,2,1,0:T(8,128)S(1)} all-gather(f32[1,4,16,80]{3,2,1,0:T(8,128)S(1)} %pad_maximum_fusion.23), channel_id=1, replica_groups=mesh['alt'=8,'raan'=4] {'alt'}, dimensions={0}, use_global_device_ids=true | all-gather | bytes 184320 | tf_op jit(solution)/shard_map/all_gather | solution.py:162
  128.0 0.3 fusion.196
  128.3 4.4 %collective-permute-start.12 = (f32[2,32,160]{2,1,0:T(8,128)S(1)}, f32[2,32,160]{2,1,0:T(8,128)S(1)}, u32[]{:S(2)}, u32[]{:S(2)}) collective-permute-start(f32[2,32,160]{2,1,0:T(8,128)S(1)} %slice_add_fusion.6), channel_id=1, source_target_pairs={{0,4},{4,8},{8,12},{12,16},{16,20},{20,24},{24,28},{1,5},{5,9},{9,... | collective-permute-start | bytes 122888 | tf_op jit(solution)/shard_map/ppermute | solution.py:52
  132.7 1.9 %collective-permute-start.13 = (f32[2,32,160]{2,1,0:T(8,128)S(1)}, f32[2,32,160]{2,1,0:T(8,128)S(1)}, u32[]{:S(2)}, u32[]{:S(2)}) collective-permute-start(f32[2,32,160]{2,1,0:T(8,128)S(1)} %slice_add_fusion.6), channel_id=1, source_target_pairs={{4,0},{8,4},{12,8},{16,12},{20,16},{24,20},{28,24},{5,1},{9,5},{13... | collective-permute-start | bytes 122888 | tf_op jit(solution)/shard_map/ppermute | solution.py:53
  134.7 5.2 %collective-permute-done.13 = f32[2,32,160]{2,1,0:T(8,128)S(1)} collective-permute-done((f32[2,32,160]{2,1,0:T(8,128)S(1)}, f32[2,32,160]{2,1,0:T(8,128)S(1)}, u32[]{:S(2)}, u32[]{:S(2)}) %collective-permute-start.13) | collective-permute-done | bytes 40992 | tf_op jit(solution)/shard_map/ppermute | solution.py:53
  140.4 0.4 fusion.163
  140.8 0.3 convolution_bitcast_fusion
  141.2 6.6 %collective-permute-start.14 = (f32[3,64,320]{2,1,0:T(8,128)S(1)}, f32[3,64,320]{2,1,0:T(8,128)S(1)}, u32[]{:S(2)}, u32[]{:S(2)}) collective-permute-start(f32[3,64,320]{2,1,0:T(8,128)S(1)} %get-tuple-element.65), channel_id=1, source_target_pairs={{0,4},{4,8},{8,12},{12,16},{16,20},{20,24},{24,28},{1,5},{5,9},{9,... | collective-permute-start | bytes 737288 | tf_op jit(solution)/shard_map/ppermute | solution.py:52
  147.8 2.1 %collective-permute-start.15 = (f32[3,64,320]{2,1,0:T(8,128)S(1)}, f32[3,64,320]{2,1,0:T(8,128)S(1)}, u32[]{:S(2)}, u32[]{:S(2)}) collective-permute-start(f32[3,64,320]{2,1,0:T(8,128)S(1)} %get-tuple-element.66), channel_id=1, source_target_pairs={{4,0},{8,4},{12,8},{16,12},{20,16},{24,20},{28,24},{5,1},{9,5},{13... | collective-permute-start | bytes 737288 | tf_op jit(solution)/shard_map/ppermute | solution.py:53
  150.0 2.1 %collective-permute-done.14 = f32[3,64,320]{2,1,0:T(8,128)S(1)} collective-permute-done((f32[3,64,320]{2,1,0:T(8,128)S(1)}, f32[3,64,320]{2,1,0:T(8,128)S(1)}, u32[]{:S(2)}, u32[]{:S(2)}) %collective-permute-start.14) | collective-permute-done | bytes 245792 | tf_op jit(solution)/shard_map/ppermute | solution.py:52
  152.1 5.3 %collective-permute-done.15 = f32[3,64,320]{2,1,0:T(8,128)S(1)} collective-permute-done((f32[3,64,320]{2,1,0:T(8,128)S(1)}, f32[3,64,320]{2,1,0:T(8,128)S(1)}, u32[]{:S(2)}, u32[]{:S(2)}) %collective-permute-start.15) | collective-permute-done | bytes 245792 | tf_op jit(solution)/shard_map/ppermute | solution.py:53
  157.6 0.3 fusion.256
  157.8 1.1 fusion.17
  159.2 0.9 fusion.42
  160.3 0.8 slice.967
  161.4 0.8 copy-done.1
  162.2 1.4 fusion.67
  (119 shorter events, 7.4 us)
Async XLA Ops:
  1.9 13.5 %copy-start.2 = (f32[4,64,256]{2,1,0:T(8,128)S(1)}, f32[4,64,256]{2,1,0:T(8,128)}, u32[]{:S(2)}) copy-start(f32[4,64,256]{2,1,0:T(8,128)} %param.7) | copy-start | bytes 786436
  1.9 13.5 %copy-start.3 = (f32[4,64,256]{2,1,0:T(8,128)S(1)}, f32[4,64,256]{2,1,0:T(8,128)}, u32[]{:S(2)}) copy-start(f32[4,64,256]{2,1,0:T(8,128)} %param.6) | copy-start | bytes 786436
  1.9 13.5 %copy-start.4 = (f32[4,64,256]{2,1,0:T(8,128)S(1)}, f32[4,64,256]{2,1,0:T(8,128)}, u32[]{:S(2)}) copy-start(f32[4,64,256]{2,1,0:T(8,128)} %param.4) | copy-start | bytes 786436
  2.0 13.5 %copy-start.5 = (f32[4,64,256]{2,1,0:T(8,128)S(1)}, f32[4,64,256]{2,1,0:T(8,128)}, u32[]{:S(2)}) copy-start(f32[4,64,256]{2,1,0:T(8,128)} %param.5) | copy-start | bytes 786436
  2.2 12.4 %collective-permute-start = (f32[4,4,64,32]{3,2,0,1:T(8,128)S(1)}, f32[4,4,64,32]{3,2,0,1:T(8,128)S(1)}, u32[]{:S(2)}, u32[]{:S(2)}) collective-permute-start(f32[4,4,64,32]{3,2,0,1:T(8,128)S(1)} %get-tuple-element.32), channel_id=1, source_target_pairs={{0,1},{1,2},{2,3},{3,0},{4,5},{5,6},{6,7},{7,4},{8,9},{9,10},{10,1... | collective-permute-start | bytes 393224 | tf_op jit(solution)/shard_map/ppermute | solution.py:39
  2.2 13.2 %collective-permute-start.1 = (f32[4,4,64,32]{3,2,0,1:T(8,128)S(1)}, f32[4,4,64,32]{3,2,0,1:T(8,128)}, u32[]{:S(2)}, u32[]{:S(2)}) collective-permute-start(f32[4,4,64,32]{3,2,0,1:T(8,128)S(1)} %get-tuple-element.33), channel_id=1, source_target_pairs={{1,0},{2,1},{3,2},{0,3},{5,4},{6,5},{7,6},{4,7},{9,8},{10,9},{11,1... | collective-permute-start | bytes 393224 | tf_op jit(solution)/shard_map/ppermute | solution.py:40
  4.5 31.2 %copy-start.14 = (pred[320]{0:T(512)(128)(4,1)}, pred[320]{0:T(512)(128)(4,1)S(1)}, u32[]{:S(2)}) copy-start(pred[320]{0:T(512)(128)(4,1)S(1)} %fusion.227) | copy-start | bytes 964
  7.8 27.9 %copy-start.7 = (s32[320]{0:T(512)}, s32[320]{0:T(512)S(1)}, u32[]{:S(2)}) copy-start(s32[320]{0:T(512)S(1)} %get-tuple-element.117) | copy-start | bytes 3844
  7.8 27.9 %copy-start.9 = (s32[320]{0:T(512)}, s32[320]{0:T(512)S(1)}, u32[]{:S(2)}) copy-start(s32[320]{0:T(512)S(1)} %get-tuple-element.118) | copy-start | bytes 3844
  20.3 44.8 %collective-permute-start.2 = (f32[2,3,64,320]{3,2,0,1:T(8,128)}, f32[2,3,64,320]{3,2,0,1:T(8,128)S(1)}, u32[]{:S(2)}, u32[]{:S(2)}) collective-permute-start(f32[2,3,64,320]{3,2,0,1:T(8,128)} %get-tuple-element.30), channel_id=1, source_target_pairs={{0,4},{4,8},{8,12},{12,16},{16,20},{20,24},{24,28},{1,5},{5,9},{9,... | collective-permute-start | bytes 1474568 | tf_op jit(solution)/shard_map/ppermute | solution.py:52
  23.8 41.4 %collective-permute-start.3 = (f32[2,3,64,320]{3,2,0,1:T(8,128)}, f32[2,3,64,320]{3,2,0,1:T(8,128)S(1)}, u32[]{:S(2)}, u32[]{:S(2)}) collective-permute-start(f32[2,3,64,320]{3,2,0,1:T(8,128)} %get-tuple-element.31), channel_id=1, source_target_pairs={{4,0},{8,4},{12,8},{16,12},{20,16},{24,20},{28,24},{5,1},{9,5},{13... | collective-permute-start | bytes 1474568 | tf_op jit(solution)/shard_map/ppermute | solution.py:53
  26.2 37.8 %collective-permute-start.4 = (f32[3,64,320]{2,1,0:T(8,128)}, f32[3,64,320]{2,1,0:T(8,128)}, u32[]{:S(2)}, u32[]{:S(2)}) collective-permute-start(f32[3,64,320]{2,1,0:T(8,128)} %get-tuple-element.28), channel_id=1, source_target_pairs={{0,4},{4,8},{8,12},{12,16},{16,20},{20,24},{24,28},{1,5},{5,9},{9,... | collective-permute-start | bytes 737288 | tf_op jit(solution)/shard_map/ppermute | solution.py:52
  30.5 33.4 %collective-permute-start.5 = (f32[3,64,320]{2,1,0:T(8,128)}, f32[3,64,320]{2,1,0:T(8,128)}, u32[]{:S(2)}, u32[]{:S(2)}) collective-permute-start(f32[3,64,320]{2,1,0:T(8,128)} %get-tuple-element.29), channel_id=1, source_target_pairs={{4,0},{8,4},{12,8},{16,12},{20,16},{24,20},{28,24},{5,1},{9,5},{13... | collective-permute-start | bytes 737288 | tf_op jit(solution)/shard_map/ppermute | solution.py:53
  38.8 4.0 %copy-start.16 = (s32[32]{0:T(128)S(1)}, s32[32]{0:T(128)}, u32[]{:S(2)}) copy-start(s32[32]{0:T(128)} %broadcast_add_fusion.2) | copy-start | bytes 388
  38.8 4.0 %copy-start.17 = (pred[32]{0:T(512)(128)(4,1)S(1)}, pred[32]{0:T(512)(128)(4,1)}, u32[]{:S(2)}) copy-start(pred[32]{0:T(512)(128)(4,1)} %compare_and_fusion.1) | copy-start | bytes 100
  38.8 4.0 %copy-start.18 = (s32[32]{0:T(128)S(1)}, s32[32]{0:T(128)}, u32[]{:S(2)}) copy-start(s32[32]{0:T(128)} %iota_shift-right-logical_fusion.2) | copy-start | bytes 388
  40.7 23.2 %copy-start = (f32[4,64,320]{2,1,0:T(8,128)S(1)}, f32[4,64,320]{2,1,0:T(8,128)}, u32[]{:S(2)}) copy-start(f32[4,64,320]{2,1,0:T(8,128)} %get-tuple-element.24) | copy-start | bytes 983044
  67.7 0.6 copy-start.13
  69.0 6.7 %collective-permute-start.6 = (f32[1,64,320]{2,1,0:T(8,128)S(1)}, f32[1,64,320]{2,1,0:T(8,128)S(1)}, u32[]{:S(2)}, u32[]{:S(2)}) collective-permute-start(f32[1,64,320]{2,1,0:T(8,128)S(1)} %get-tuple-element.67), channel_id=1, source_target_pairs={{0,4},{4,8},{8,12},{12,16},{16,20},{20,24},{24,28},{1,5},{5,9},{9,... | collective-permute-start | bytes 245768 | tf_op jit(solution)/shard_map/ppermute | solution.py:52
  73.3 7.4 %collective-permute-start.7 = (f32[1,64,320]{2,1,0:T(8,128)S(1)}, f32[1,64,320]{2,1,0:T(8,128)S(1)}, u32[]{:S(2)}, u32[]{:S(2)}) collective-permute-start(f32[1,64,320]{2,1,0:T(8,128)S(1)} %get-tuple-element.68), channel_id=1, source_target_pairs={{4,0},{8,4},{12,8},{16,12},{20,16},{24,20},{28,24},{5,1},{9,5},{13... | collective-permute-start | bytes 245768 | tf_op jit(solution)/shard_map/ppermute | solution.py:53
  80.7 0.7 copy-start.8
  80.7 0.7 copy-start.10
  80.7 0.7 copy-start.15
  82.1 14.4 %collective-permute-start.8 = (f32[2,4,32,160]{3,2,0,1:T(8,128)S(1)}, f32[2,4,32,160]{3,2,0,1:T(8,128)S(1)}, u32[]{:S(2)}, u32[]{:S(2)}) collective-permute-start(f32[2,4,32,160]{3,2,0,1:T(8,128)S(1)} %pad_maximum_fusion.10), channel_id=1, source_target_pairs={{0,4},{4,8},{8,12},{12,16},{16,20},{20,24},{24,28},{1,5},{5,9},{9,... | collective-permute-start | bytes 491528 | tf_op jit(solution)/shard_map/ppermute | solution.py:52
  84.4 12.1 %collective-permute-start.9 = (f32[2,4,32,160]{3,2,0,1:T(8,128)S(1)}, f32[2,4,32,160]{3,2,0,1:T(8,128)S(1)}, u32[]{:S(2)}, u32[]{:S(2)}) collective-permute-start(f32[2,4,32,160]{3,2,0,1:T(8,128)S(1)} %pad_maximum_fusion.10), channel_id=1, source_target_pairs={{4,0},{8,4},{12,8},{16,12},{20,16},{24,20},{28,24},{5,1},{9,5},{13... | collective-permute-start | bytes 491528 | tf_op jit(solution)/shard_map/ppermute | solution.py:53
  88.0 8.8 %collective-permute-start.10 = (f32[1,4,32,160]{3,2,0,1:T(8,128)S(1)}, f32[1,4,32,160]{3,2,0,1:T(8,128)S(1)}, u32[]{:S(2)}, u32[]{:S(2)}) collective-permute-start(f32[1,4,32,160]{3,2,0,1:T(8,128)S(1)} %get-tuple-element.77), channel_id=1, source_target_pairs={{0,8},{4,12},{8,16},{12,20},{16,24},{20,28},{1,9},{5,13},{9,17},{1... | collective-permute-start | bytes 245768 | tf_op jit(solution)/shard_map/ppermute | solution.py:52
  89.9 6.9 %collective-permute-start.11 = (f32[1,4,32,160]{3,2,0,1:T(8,128)S(1)}, f32[1,4,32,160]{3,2,0,1:T(8,128)S(1)}, u32[]{:S(2)}, u32[]{:S(2)}) collective-permute-start(f32[1,4,32,160]{3,2,0,1:T(8,128)S(1)} %get-tuple-element.78), channel_id=1, source_target_pairs={{8,0},{12,4},{16,8},{20,12},{24,16},{28,20},{9,1},{13,5},{17,9},{2... | collective-permute-start | bytes 245768 | tf_op jit(solution)/shard_map/ppermute | solution.py:53
  96.8 0.7 copy-start.6
  97.4 0.7 copy-start.11
  97.4 0.7 copy-start.12
  97.4 0.7 copy-start.19
  128.3 6.3 %collective-permute-start.12 = (f32[2,32,160]{2,1,0:T(8,128)S(1)}, f32[2,32,160]{2,1,0:T(8,128)S(1)}, u32[]{:S(2)}, u32[]{:S(2)}) collective-permute-start(f32[2,32,160]{2,1,0:T(8,128)S(1)} %slice_add_fusion.6), channel_id=1, source_target_pairs={{0,4},{4,8},{8,12},{12,16},{16,20},{20,24},{24,28},{1,5},{5,9},{9,... | collective-permute-start | bytes 122888 | tf_op jit(solution)/shard_map/ppermute | solution.py:52
  132.7 7.2 %collective-permute-start.13 = (f32[2,32,160]{2,1,0:T(8,128)S(1)}, f32[2,32,160]{2,1,0:T(8,128)S(1)}, u32[]{:S(2)}, u32[]{:S(2)}) collective-permute-start(f32[2,32,160]{2,1,0:T(8,128)S(1)} %slice_add_fusion.6), channel_id=1, source_target_pairs={{4,0},{8,4},{12,8},{16,12},{20,16},{24,20},{28,24},{5,1},{9,5},{13... | collective-permute-start | bytes 122888 | tf_op jit(solution)/shard_map/ppermute | solution.py:53
  141.2 10.9 %collective-permute-start.14 = (f32[3,64,320]{2,1,0:T(8,128)S(1)}, f32[3,64,320]{2,1,0:T(8,128)S(1)}, u32[]{:S(2)}, u32[]{:S(2)}) collective-permute-start(f32[3,64,320]{2,1,0:T(8,128)S(1)} %get-tuple-element.65), channel_id=1, source_target_pairs={{0,4},{4,8},{8,12},{12,16},{16,20},{20,24},{24,28},{1,5},{5,9},{9,... | collective-permute-start | bytes 737288 | tf_op jit(solution)/shard_map/ppermute | solution.py:52
  147.8 9.5 %collective-permute-start.15 = (f32[3,64,320]{2,1,0:T(8,128)S(1)}, f32[3,64,320]{2,1,0:T(8,128)S(1)}, u32[]{:S(2)}, u32[]{:S(2)}) collective-permute-start(f32[3,64,320]{2,1,0:T(8,128)S(1)} %get-tuple-element.66), channel_id=1, source_target_pairs={{4,0},{8,4},{12,8},{16,12},{20,16},{24,20},{28,24},{5,1},{9,5},{13... | collective-permute-start | bytes 737288 | tf_op jit(solution)/shard_map/ppermute | solution.py:53
  161.2 1.0 copy-start.1

commit v9 on v5

--- a/solution.py
+++ b/solution.py
@@ -52,6 +52,13 @@
         below.insert(0, lax.ppermute(values[low:], "alt", up))
         above.append(lax.ppermute(values[:high], "alt", down))
     return jnp.concatenate(below + [values] + above, axis=0)
+
+
+def spread_gather(values):
+    count = lax.axis_size("alt")
+    copies = jnp.broadcast_to(values[None], (count,) + values.shape)
+    every = lax.all_to_all(copies, "alt", 0, 0)
+    return every.reshape((count * values.shape[0],) + values.shape[1:])
 
 
 def trim(values, have, want):
@@ -156,7 +163,7 @@
     rhs_three = coarsen(trim(rhs_two_x, 2, 0) - applied)
 
     height = rhs_three.shape[0]
-    column = lax.all_gather(jnp.stack([rhs_three] + coef_three, 1), "alt", axis=0, tiled=True)
+    column = spread_gather(jnp.stack([rhs_three] + coef_three, 1))
     weights_three = make_weights(pad_rows(column[:, 1]), column[:, 2], column[:, 3], 0.0625, 0)
     rhs_three_x = column[:, 0]
     coarse_part = first_sweep(weights_three, rhs_three_x, 0)

time: 158 us -> 150 us (0.949)
  blocking collectives: 30.9 us -> 0 us
  waiting for transfers between devices: 41.1 us -> 49.9 us
  starting transfers between devices: 50.3 us -> 56.7 us
  other arithmetic: 18.8 us -> 22.9 us
  local copies, waits for them, and re-layouts: 4.69 us -> 8.04 us
    all_gather x1 -> x0, blocking collectives: 30.9 us -> none  [shards(): lax.all_gather(jnp.stack([rhs_three] + coef_three, 1), 'alt', axis=0, til...]
    all_to_all x0 -> x1, waiting for transfers between devices: none -> 8.63 us  [spread_gather(): every = lax.all_to_all(copies, 'alt', 0, 0)]
    all_to_all x0 -> x1, starting transfers between devices: none -> 4.82 us  [spread_gather(): every = lax.all_to_all(copies, 'alt', 0, 0)]
    add x2, other arithmetic: 0.21 us -> 1.9 us  [sweep(): centre + OMEGA * (trim(target, target_halo, halo - 1) - applied) / diagonal]
    ppermute x9, starting transfers between devices: 36.2 us -> 37.8 us  [alt_extend(): below.insert(0, lax.ppermute(values[low:], 'alt', up))]
  transfers between devices with their start and end apart: 20 -> 21, of which waited for: 16 -> 17; matrix products, arithmetic and copies ran while one was open for 12% -> 13% of each run, Pallas kernels for 0% -> 0%
where the time goes in v9:
time: 150 us; the launch traced here: 149 us
  starting transfers between devices  56.7 us (38%)
  waiting for transfers between devices  49.9 us (33%)
  other arithmetic  22.9 us (15%)
  matrix products  9.69 us (6%)
  local copies, waits for them, and re-layouts  8.04 us (5%)
  between operations  1.76 us (1%)
    ppermute x9, starting transfers between devices, alt_extend(): below.insert(0, lax.ppermute(values[low:], 'alt', up))  37.8 us
    ppermute x9, waiting for transfers between devices, alt_extend(): above.append(lax.ppermute(values[:high], 'alt', down))  24.1 us
    ppermute x9, starting transfers between devices, alt_extend(): above.append(lax.ppermute(values[:high], 'alt', down))  11.6 us
    ppermute x9, waiting for transfers between devices, alt_extend(): below.insert(0, lax.ppermute(values[low:], 'alt', up))  9.55 us
    all_to_all x1, waiting for transfers between devices, spread_gather(): every = lax.all_to_all(copies, 'alt', 0, 0)  8.63 us
    dot_general x8, matrix products, coarsen(): summed = jnp.matmul(summed, pairing(length), precision=HIGH)  6.74 us
    ppermute x1, waiting for transfers between devices, raan_extend(): before = lax.ppermute(values[..., length - halo:], 'raan', up)  5.79 us
    all_to_all x1, starting transfers between devices, spread_gather(): every = lax.all_to_all(copies, 'alt', 0, 0)  4.82 us
  transfers between devices with their start and end apart: 21, of which 17 were waited for; matrix products, arithmetic and copies ran while one was open for 13% of the time, Pallas kernels for 0%

profile of v9, /device:TPU:0, one launch (start us, length us, event | category | flops | bytes accessed | tf_op | source)
XLA Modules:
  0.0 149.0 jit_solution(5152127417274192847)
XLA Ops:
  0.6 1.3 pad_maximum_fusion.1
  2.0 1.0 fusion.268
  3.4 1.9 %collective-permute-start.1 = (f32[4,4,64,32]{3,2,0,1:T(8,128)S(1)}, f32[4,4,64,32]{3,2,0,1:T(8,128)S(1)}, u32[]{:S(2)}, u32[]{:S(2)}) collective-permute-start(f32[4,4,64,32]{3,2,0,1:T(8,128)S(1)} %get-tuple-element.32), channel_id=1, source_target_pairs={{1,0},{2,1},{3,2},{0,3},{5,4},{6,5},{7,6},{4,7},{9,8},{10,9},{11,1... | collective-permute-start | bytes 393224 | tf_op jit(solution)/shard_map/ppermute | solution.py:40
  5.4 0.5 broadcast_add_fusion.2
  5.9 0.6 iota_shift-right-logical_fusion.2
  6.5 0.5 compare_and_fusion.1
  7.0 0.5 compare_and_fusion
  8.1 0.6 iota_shift-right-logical_fusion.1
  8.7 0.5 compare_and_fusion.2
  9.2 0.6 iota_shift-right-logical_fusion
  9.8 5.8 %collective-permute-done = f32[4,4,64,32]{3,2,0,1:T(8,128)S(1)} collective-permute-done((f32[4,4,64,32]{3,2,0,1:T(8,128)}, f32[4,4,64,32]{3,2,0,1:T(8,128)S(1)}, u32[]{:S(2)}, u32[]{:S(2)}) %collective-permute-start) | collective-permute-done | bytes 131104 | tf_op jit(solution)/shard_map/ppermute | solution.py:39
  15.6 1.9 %collective-permute-done.1 = f32[4,4,64,32]{3,2,0,1:T(8,128)S(1)} collective-permute-done((f32[4,4,64,32]{3,2,0,1:T(8,128)S(1)}, f32[4,4,64,32]{3,2,0,1:T(8,128)S(1)}, u32[]{:S(2)}, u32[]{:S(2)}) %collective-permute-start.1) | collective-permute-done | bytes 131104 | tf_op jit(solution)/shard_map/ppermute | solution.py:40
  17.5 1.0 pad_maximum_fusion.27
  18.5 1.3 collective-permute-start.3
  19.8 5.2 %collective-permute-start.2 = (f32[1,2,64,320]{3,2,0,1:T(8,128)}, f32[1,2,64,320]{3,2,0,1:T(8,128)}, u32[]{:S(2)}, u32[]{:S(2)}) collective-permute-start(f32[1,2,64,320]{3,2,0,1:T(8,128)} %get-tuple-element.24), channel_id=1, source_target_pairs={{0,4},{4,8},{8,12},{12,16},{16,20},{20,24},{24,28},{1,5},{5,9},{9,... | collective-permute-start | bytes 491528 | tf_op jit(solution)/shard_map/ppermute | solution.py:52
  25.0 1.6 %pad_maximum_fusion = f32[4,4,64,320]{3,2,0,1:T(8,128)S(1)} fusion(f32[4,4,64,32]{3,2,0,1:T(8,128)} %copy-done.14, f32[4,1,64,256]{3,2,0,1:T(8,128)S(1)} %bitcast.227, f32[4,1,64,256]{3,2,0,1:T(8,128)S(1)} %bitcast.230, f32[4,1,64,256]{3,2,0,1:T(8,128)S(1)} %bitcast.233, f32[4,1,64,256]{3,2,0,1:T(8,128)S(1)} %bitcast.236, ...), kind=kLoop, calls=%fused_computation | loop fusion | flops 1638400 | bytes 2621440 | tf_op jit(solution)/shard_map/concatenate | solution.py:41
  26.6 1.0 fusion.267
  27.7 1.9 %reduce_sum.73 = f32[2,64,320]{2,1,0:T(8,128)} reduce(f32[2,2,64,320]{3,2,1,0:T(8,128)} %bitcast.255, f32[]{:T(128)} %constant.135.clone.1), dimensions={1}, to_apply=%region_1.2 | reduce | flops 40960 | bytes 491524 | tf_op jit(solution)/shard_map/reduce_sum | solution.py:21
  29.5 0.7 reduce_sum.74
  30.3 1.4 fusion.256
  31.6 1.1 fusion.252
  32.8 1.4 fusion.254
  34.7 1.0 fusion.122
  35.7 1.0 fusion.120
  38.7 2.0 %fusion.72 = (f32[4,64,320]{2,1,0:T(8,128)}, f32[4,64,320]{2,1,0:T(8,128)S(1)}, f32[4,64,320]{2,1,0:T(8,128)S(1)}, f32[4,64,320]{2,1,0:T(8,128)S(1)}, f32[4,64,320]{2,1,0:T(8,128)S(1)}) fusion(f32[4,63,320]{2,1,0:T(8,128)S(1)} %get-tuple-element.115, f32[4,2,64,320]{3,2,0,1:T(8,128)S(1)} %slice.729, f32[1,2,64,320]{3,2,0,1:T(8,128)} %collective-permute-done.2, ...), kind=kLoop, calls=%fused_computation.107 | loop fusion | flops 1310720 | bytes 4252672 | tf_op jit(solution)/shard_map/add | solution.py:87
  40.7 1.6 %fusion.76 = f32[4,64,320]{2,1,0:T(8,128)S(1)} fusion(f32[4,64,320]{2,1,0:T(8,128)S(1)} %get-tuple-element.8, f32[4,64,319]{2,1,0:T(8,128)S(1)} %get-tuple-element.68, f32[4,64,320]{2,1,0:T(8,128)S(1)} %get-tuple-element.7, f32[4,64,319]{2,1,0:T(8,128)S(1)} %get-tuple-element.67, f32[4,63,320]{2,1,0:T(8,128)S(1)} %get-tuple-element.66, ...), kind=kLoop, calls=%fused_computation.111 | loop fusion | flops 2129920 | bytes 4570116 | tf_op jit(solution)/shard_map/jit(_where)/select_n | solution.py:125
  42.4 4.1 %collective-permute-start.4 = (f32[1,64,320]{2,1,0:T(8,128)S(1)}, f32[1,64,320]{2,1,0:T(8,128)S(1)}, u32[]{:S(2)}, u32[]{:S(2)}) collective-permute-start(f32[1,64,320]{2,1,0:T(8,128)S(1)} %get-tuple-element.59), channel_id=1, source_target_pairs={{0,4},{4,8},{8,12},{12,16},{16,20},{20,24},{24,28},{1,5},{5,9},{9,... | collective-permute-start | bytes 245768 | tf_op jit(solution)/shard_map/ppermute | solution.py:52
  46.4 1.3 collective-permute-start.5
  47.9 1.0 collective-permute-done.4
  48.9 4.1 %collective-permute-done.5 = f32[1,64,320]{2,1,0:T(8,128)S(1)} collective-permute-done((f32[1,64,320]{2,1,0:T(8,128)S(1)}, f32[1,64,320]{2,1,0:T(8,128)S(1)}, u32[]{:S(2)}, u32[]{:S(2)}) %collective-permute-start.5) | collective-permute-done | bytes 81952 | tf_op jit(solution)/shard_map/ppermute | solution.py:53
  53.6 3.4 %collective-permute-start.6 = (f32[1,64,320]{2,1,0:T(8,128)S(1)}, f32[1,64,320]{2,1,0:T(8,128)S(1)}, u32[]{:S(2)}, u32[]{:S(2)}) collective-permute-start(f32[1,64,320]{2,1,0:T(8,128)S(1)} %get-tuple-element.53), channel_id=1, source_target_pairs={{0,4},{4,8},{8,12},{12,16},{16,20},{20,24},{24,28},{1,5},{5,9},{9,... | collective-permute-start | bytes 245768 | tf_op jit(solution)/shard_map/ppermute | solution.py:52
  57.0 1.3 collective-permute-start.7
  58.5 0.7 collective-permute-done.6
  59.2 4.3 %collective-permute-done.7 = f32[1,64,320]{2,1,0:T(8,128)S(1)} collective-permute-done((f32[1,64,320]{2,1,0:T(8,128)S(1)}, f32[1,64,320]{2,1,0:T(8,128)S(1)}, u32[]{:S(2)}, u32[]{:S(2)}) %collective-permute-start.7) | collective-permute-done | bytes 81952 | tf_op jit(solution)/shard_map/ppermute | solution.py:53
  64.9 1.3 collective-permute-start.9
  66.2 5.0 %collective-permute-start.8 = (f32[2,4,32,160]{3,2,0,1:T(8,128)S(1)}, f32[2,4,32,160]{3,2,0,1:T(8,128)S(1)}, u32[]{:S(2)}, u32[]{:S(2)}) collective-permute-start(f32[2,4,32,160]{3,2,0,1:T(8,128)S(1)} %pad_maximum_fusion.15), channel_id=1, source_target_pairs={{0,4},{4,8},{8,12},{12,16},{16,20},{20,24},{24,28},{1,5},{5,9},{9,... | collective-permute-start | bytes 491528 | tf_op jit(solution)/shard_map/ppermute | solution.py:52
  71.2 3.5 %collective-permute-start.10 = (f32[1,4,32,160]{3,2,0,1:T(8,128)S(1)}, f32[1,4,32,160]{3,2,0,1:T(8,128)S(1)}, u32[]{:S(2)}, u32[]{:S(2)}) collective-permute-start(f32[1,4,32,160]{3,2,0,1:T(8,128)S(1)} %get-tuple-element.75), channel_id=1, source_target_pairs={{0,8},{4,12},{8,16},{12,20},{16,24},{20,28},{1,9},{5,13},{9,17},{1... | collective-permute-start | bytes 245768 | tf_op jit(solution)/shard_map/ppermute | solution.py:52
  74.7 1.3 collective-permute-start.11
  76.0 3.2 %collective-permute-done.8 = f32[2,4,32,160]{3,2,0,1:T(8,128)S(1)} collective-permute-done((f32[2,4,32,160]{3,2,0,1:T(8,128)S(1)}, f32[2,4,32,160]{3,2,0,1:T(8,128)S(1)}, u32[]{:S(2)}, u32[]{:S(2)}) %collective-permute-start.8) | collective-permute-done | bytes 163872 | tf_op jit(solution)/shard_map/ppermute | solution.py:52
  79.4 2.1 %collective-permute-done.11 = f32[1,4,32,160]{3,2,0,1:T(8,128)S(1)} collective-permute-done((f32[1,4,32,160]{3,2,0,1:T(8,128)S(1)}, f32[1,4,32,160]{3,2,0,1:T(8,128)S(1)}, u32[]{:S(2)}, u32[]{:S(2)}) %collective-permute-start.11) | collective-permute-done | bytes 81952 | tf_op jit(solution)/shard_map/ppermute | solution.py:53
  82.1 0.9 fusion.117
  84.2 0.7 broadcast_in_dim.42
  85.0 4.8 %all-to-all-start = ((f32[8,1,4,16,80]{4,3,2,1,0:T(8,128)}), f32[8,1,4,16,80]{4,3,2,1,0:T(8,128)}, u32[]{:S(2)}, u32[]{:S(2)}) async-start(f32[8,1,4,16,80]{4,3,2,1,0:T(8,128)} %broadcast_in_dim.42), calls=%async_computation | async-start | bytes 524288 | tf_op jit(solution)/shard_map/all_to_all | solution.py:60
  89.8 8.6 %all-to-all-done = f32[8,1,4,16,80]{4,3,2,1,0:T(8,128)} async-done(((f32[8,1,4,16,80]{4,3,2,1,0:T(8,128)}), f32[8,1,4,16,80]{4,3,2,1,0:T(8,128)}, u32[]{:S(2)}, u32[]{:S(2)}) %all-to-all-start) | async-done | bytes 163872 | tf_op jit(solution)/shard_map/all_to_all | solution.py:60
  98.4 1.0 slice_bitcast_fusion.5
  99.5 1.0 multiply_divide_fusion
  100.6 0.9 fusion.138
  101.7 0.9 fusion.150
  103.5 1.3 collective-permute-start.13
  104.8 4.5 %collective-permute-start.12 = (f32[2,32,160]{2,1,0:T(8,128)S(1)}, f32[2,32,160]{2,1,0:T(8,128)S(1)}, u32[]{:S(2)}, u32[]{:S(2)}) collective-permute-start(f32[2,32,160]{2,1,0:T(8,128)S(1)} %slice_add_fusion.3), channel_id=1, source_target_pairs={{0,4},{4,8},{8,12},{12,16},{16,20},{20,24},{24,28},{1,5},{5,9},{9,... | collective-permute-start | bytes 122888 | tf_op jit(solution)/shard_map/ppermute | solution.py:52
  109.7 1.6 %collective-permute-done.12 = f32[2,32,160]{2,1,0:T(8,128)S(1)} collective-permute-done((f32[2,32,160]{2,1,0:T(8,128)S(1)}, f32[2,32,160]{2,1,0:T(8,128)S(1)}, u32[]{:S(2)}, u32[]{:S(2)}) %collective-permute-start.12) | collective-permute-done | bytes 40992 | tf_op jit(solution)/shard_map/ppermute | solution.py:52
  113.1 4.4 %collective-permute-start.14 = (f32[1,64,320]{2,1,0:T(8,128)S(1)}, f32[1,64,320]{2,1,0:T(8,128)S(1)}, u32[]{:S(2)}, u32[]{:S(2)}) collective-permute-start(f32[1,64,320]{2,1,0:T(8,128)S(1)} %get-tuple-element.47), channel_id=1, source_target_pairs={{0,4},{4,8},{8,12},{12,16},{16,20},{20,24},{24,28},{1,5},{5,9},{9,... | collective-permute-start | bytes 245768 | tf_op jit(solution)/shard_map/ppermute | solution.py:52
  117.5 1.3 collective-permute-start.15
  119.0 1.7 %collective-permute-done.14 = f32[1,64,320]{2,1,0:T(8,128)S(1)} collective-permute-done((f32[1,64,320]{2,1,0:T(8,128)S(1)}, f32[1,64,320]{2,1,0:T(8,128)S(1)}, u32[]{:S(2)}, u32[]{:S(2)}) %collective-permute-start.14) | collective-permute-done | bytes 81952 | tf_op jit(solution)/shard_map/ppermute | solution.py:52
  120.7 4.6 %collective-permute-done.15 = f32[1,64,320]{2,1,0:T(8,128)S(1)} collective-permute-done((f32[1,64,320]{2,1,0:T(8,128)S(1)}, f32[1,64,320]{2,1,0:T(8,128)S(1)}, u32[]{:S(2)}, u32[]{:S(2)}) %collective-permute-start.15) | collective-permute-done | bytes 81952 | tf_op jit(solution)/shard_map/ppermute | solution.py:53
  125.9 4.9 %collective-permute-start.16 = (f32[1,64,320]{2,1,0:T(8,128)S(1)}, f32[1,64,320]{2,1,0:T(8,128)S(1)}, u32[]{:S(2)}, u32[]{:S(2)}) collective-permute-start(f32[1,64,320]{2,1,0:T(8,128)S(1)} %get-tuple-element.41), channel_id=1, source_target_pairs={{0,4},{4,8},{8,12},{12,16},{16,20},{20,24},{24,28},{1,5},{5,9},{9,... | collective-permute-start | bytes 245768 | tf_op jit(solution)/shard_map/ppermute | solution.py:52
  130.8 1.3 collective-permute-start.17
  132.3 0.7 collective-permute-done.16
  133.0 4.3 %collective-permute-done.17 = f32[1,64,320]{2,1,0:T(8,128)S(1)} collective-permute-done((f32[1,64,320]{2,1,0:T(8,128)S(1)}, f32[1,64,320]{2,1,0:T(8,128)S(1)}, u32[]{:S(2)}, u32[]{:S(2)}) %collective-permute-start.17) | collective-permute-done | bytes 81952 | tf_op jit(solution)/shard_map/ppermute | solution.py:53
  137.9 2.8 %collective-permute-start.18 = (f32[1,64,320]{2,1,0:T(8,128)S(1)}, f32[1,64,320]{2,1,0:T(8,128)S(1)}, u32[]{:S(2)}, u32[]{:S(2)}) collective-permute-start(f32[1,64,320]{2,1,0:T(8,128)S(1)} %get-tuple-element.37), channel_id=1, source_target_pairs={{0,4},{4,8},{8,12},{12,16},{16,20},{20,24},{24,28},{1,5},{5,9},{9,... | collective-permute-start | bytes 245768 | tf_op jit(solution)/shard_map/ppermute | solution.py:52
  140.7 1.3 collective-permute-start.19
  142.2 0.7 collective-permute-done.18
  142.9 4.3 %collective-permute-done.19 = f32[1,64,320]{2,1,0:T(8,128)S(1)} collective-permute-done((f32[1,64,320]{2,1,0:T(8,128)S(1)}, f32[1,64,320]{2,1,0:T(8,128)S(1)}, u32[]{:S(2)}, u32[]{:S(2)}) %collective-permute-start.19) | collective-permute-done | bytes 81952 | tf_op jit(solution)/shard_map/ppermute | solution.py:53
  147.4 1.5 %fusion.84 = (f32[4,64,256]{2,1,0:T(8,128)}, f32[4,64,256]{2,1,0:T(8,128)}) fusion(f32[4,63,320]{2,1,0:T(8,128)S(1)} %get-tuple-element.36, f32[4,64,320]{2,1,0:T(8,128)S(1)} %copy-done.3, f32[4,64,319]{2,1,0:T(8,128)S(1)} %get-tuple-element.40, f32[4,64,320]{2,1,0:T(8,128)S(1)} %copy-done.1, f32[4,64,319]{2,1,0:T(8,128)S(1)} %get-tuple-element.39, ...), kind=kLoop, calls=%fused_computation.120 | loop fusion | flops 655360 | bytes 3395584 | tf_op jit(solution)/shard_map/div | solution.py:183
  (181 shorter events, 12.6 us)
Async XLA Ops:
  1.9 15.6 %copy-start.8 = (f32[4,64,256]{2,1,0:T(8,128)S(1)}, f32[4,64,256]{2,1,0:T(8,128)}, u32[]{:S(2)}) copy-start(f32[4,64,256]{2,1,0:T(8,128)} %param.7) | copy-start | bytes 786436
  1.9 15.6 %copy-start.9 = (f32[4,64,256]{2,1,0:T(8,128)S(1)}, f32[4,64,256]{2,1,0:T(8,128)}, u32[]{:S(2)}) copy-start(f32[4,64,256]{2,1,0:T(8,128)} %param.6) | copy-start | bytes 786436
  1.9 15.5 %copy-start.10 = (f32[4,64,256]{2,1,0:T(8,128)S(1)}, f32[4,64,256]{2,1,0:T(8,128)}, u32[]{:S(2)}) copy-start(f32[4,64,256]{2,1,0:T(8,128)} %param.5) | copy-start | bytes 786436
  2.0 15.5 %copy-start.11 = (f32[4,64,256]{2,1,0:T(8,128)S(1)}, f32[4,64,256]{2,1,0:T(8,128)}, u32[]{:S(2)}) copy-start(f32[4,64,256]{2,1,0:T(8,128)} %param.4) | copy-start | bytes 786436
  3.0 12.6 %collective-permute-start = (f32[4,4,64,32]{3,2,0,1:T(8,128)}, f32[4,4,64,32]{3,2,0,1:T(8,128)S(1)}, u32[]{:S(2)}, u32[]{:S(2)}) collective-permute-start(f32[4,4,64,32]{3,2,0,1:T(8,128)} %get-tuple-element.31), channel_id=1, source_target_pairs={{0,1},{1,2},{2,3},{3,0},{4,5},{5,6},{6,7},{7,4},{8,9},{9,10},{10,1... | collective-permute-start | bytes 393224 | tf_op jit(solution)/shard_map/ppermute | solution.py:39
  3.4 14.0 %collective-permute-start.1 = (f32[4,4,64,32]{3,2,0,1:T(8,128)S(1)}, f32[4,4,64,32]{3,2,0,1:T(8,128)S(1)}, u32[]{:S(2)}, u32[]{:S(2)}) collective-permute-start(f32[4,4,64,32]{3,2,0,1:T(8,128)S(1)} %get-tuple-element.32), channel_id=1, source_target_pairs={{1,0},{2,1},{3,2},{0,3},{5,4},{6,5},{7,6},{4,7},{9,8},{10,9},{11,1... | collective-permute-start | bytes 393224 | tf_op jit(solution)/shard_map/ppermute | solution.py:40
  17.5 2.3 %copy-start.14 = (f32[4,4,64,32]{3,2,0,1:T(8,128)}, f32[4,4,64,32]{3,2,0,1:T(8,128)S(1)}, u32[]{:S(2)}) copy-start(f32[4,4,64,32]{3,2,0,1:T(8,128)S(1)} %collective-permute-done.1) | copy-start | bytes 393220
  18.5 20.2 %collective-permute-start.3 = (f32[1,2,64,320]{3,2,0,1:T(8,128)}, f32[1,2,64,320]{3,2,0,1:T(8,128)}, u32[]{:S(2)}, u32[]{:S(2)}) collective-permute-start(f32[1,2,64,320]{3,2,0,1:T(8,128)} %get-tuple-element.23), channel_id=1, source_target_pairs={{4,0},{8,4},{12,8},{16,12},{20,16},{24,20},{28,24},{5,1},{9,5},{13... | collective-permute-start | bytes 491528 | tf_op jit(solution)/shard_map/ppermute | solution.py:53
  19.8 18.9 %collective-permute-start.2 = (f32[1,2,64,320]{3,2,0,1:T(8,128)}, f32[1,2,64,320]{3,2,0,1:T(8,128)}, u32[]{:S(2)}, u32[]{:S(2)}) collective-permute-start(f32[1,2,64,320]{3,2,0,1:T(8,128)} %get-tuple-element.24), channel_id=1, source_target_pairs={{0,4},{4,8},{8,12},{12,16},{16,20},{20,24},{24,28},{1,5},{5,9},{9,... | collective-permute-start | bytes 491528 | tf_op jit(solution)/shard_map/ppermute | solution.py:52
  27.7 9.4 %copy-start.2 = (f32[4,64,320]{2,1,0:T(8,128)}, f32[4,64,320]{2,1,0:T(8,128)S(1)}, u32[]{:S(2)}) copy-start(f32[4,64,320]{2,1,0:T(8,128)S(1)} %get-tuple-element.30) | copy-start | bytes 983044
  30.2 6.4 %copy-start.33 = (s32[160]{0:T(256)S(1)}, s32[160]{0:T(256)}, u32[]{:S(2)}) copy-start(s32[160]{0:T(256)} %get-tuple-element.122) | copy-start | bytes 1924
  30.2 6.4 %copy-start.36 = (s32[160]{0:T(256)S(1)}, s32[160]{0:T(256)}, u32[]{:S(2)}) copy-start(s32[160]{0:T(256)} %get-tuple-element.123) | copy-start | bytes 1924
  30.2 6.4 %copy-start.47 = (pred[160]{0:T(512)(128)(4,1)S(1)}, pred[160]{0:T(512)(128)(4,1)}, u32[]{:S(2)}) copy-start(pred[160]{0:T(512)(128)(4,1)} %compare_and_fusion) | copy-start | bytes 484
  37.1 0.7 copy-start.43
  40.7 22.8 %copy-start = (f32[4,64,320]{2,1,0:T(8,128)}, f32[4,64,320]{2,1,0:T(8,128)S(1)}, u32[]{:S(2)}) copy-start(f32[4,64,320]{2,1,0:T(8,128)S(1)} %get-tuple-element.8) | copy-start | bytes 983044
  42.4 6.5 %collective-permute-start.4 = (f32[1,64,320]{2,1,0:T(8,128)S(1)}, f32[1,64,320]{2,1,0:T(8,128)S(1)}, u32[]{:S(2)}, u32[]{:S(2)}) collective-permute-start(f32[1,64,320]{2,1,0:T(8,128)S(1)} %get-tuple-element.59), channel_id=1, source_target_pairs={{0,4},{4,8},{8,12},{12,16},{16,20},{20,24},{24,28},{1,5},{5,9},{9,... | collective-permute-start | bytes 245768 | tf_op jit(solution)/shard_map/ppermute | solution.py:52
  46.4 6.6 %collective-permute-start.5 = (f32[1,64,320]{2,1,0:T(8,128)S(1)}, f32[1,64,320]{2,1,0:T(8,128)S(1)}, u32[]{:S(2)}, u32[]{:S(2)}) collective-permute-start(f32[1,64,320]{2,1,0:T(8,128)S(1)} %get-tuple-element.60), channel_id=1, source_target_pairs={{4,0},{8,4},{12,8},{16,12},{20,16},{24,20},{28,24},{5,1},{9,5},{13... | collective-permute-start | bytes 245768 | tf_op jit(solution)/shard_map/ppermute | solution.py:53
  53.6 5.6 %collective-permute-start.6 = (f32[1,64,320]{2,1,0:T(8,128)S(1)}, f32[1,64,320]{2,1,0:T(8,128)S(1)}, u32[]{:S(2)}, u32[]{:S(2)}) collective-permute-start(f32[1,64,320]{2,1,0:T(8,128)S(1)} %get-tuple-element.53), channel_id=1, source_target_pairs={{0,4},{4,8},{8,12},{12,16},{16,20},{20,24},{24,28},{1,5},{5,9},{9,... | collective-permute-start | bytes 245768 | tf_op jit(solution)/shard_map/ppermute | solution.py:52
  57.0 6.5 %collective-permute-start.7 = (f32[1,64,320]{2,1,0:T(8,128)S(1)}, f32[1,64,320]{2,1,0:T(8,128)S(1)}, u32[]{:S(2)}, u32[]{:S(2)}) collective-permute-start(f32[1,64,320]{2,1,0:T(8,128)S(1)} %get-tuple-element.54), channel_id=1, source_target_pairs={{4,0},{8,4},{12,8},{16,12},{20,16},{24,20},{28,24},{5,1},{9,5},{13... | collective-permute-start | bytes 245768 | tf_op jit(solution)/shard_map/ppermute | solution.py:53
  64.8 18.2 %copy-start.12 = (f32[32,2,160]{2,0,1:T(8,128)}, f32[32,2,160]{2,0,1:T(8,128)S(1)}, u32[]{:S(2)}) copy-start(f32[32,2,160]{2,0,1:T(8,128)S(1)} %convolution_multiply_fusion.3) | copy-start | bytes 122884
  64.9 11.1 %collective-permute-start.9 = (f32[2,4,32,160]{3,2,0,1:T(8,128)S(1)}, f32[2,4,32,160]{3,2,0,1:T(8,128)S(1)}, u32[]{:S(2)}, u32[]{:S(2)}) collective-permute-start(f32[2,4,32,160]{3,2,0,1:T(8,128)S(1)} %pad_maximum_fusion.15), channel_id=1, source_target_pairs={{4,0},{8,4},{12,8},{16,12},{20,16},{24,20},{28,24},{5,1},{9,5},{13... | collective-permute-start | bytes 491528 | tf_op jit(solution)/shard_map/ppermute | solution.py:53
  66.2 13.0 %collective-permute-start.8 = (f32[2,4,32,160]{3,2,0,1:T(8,128)S(1)}, f32[2,4,32,160]{3,2,0,1:T(8,128)S(1)}, u32[]{:S(2)}, u32[]{:S(2)}) collective-permute-start(f32[2,4,32,160]{3,2,0,1:T(8,128)S(1)} %pad_maximum_fusion.15), channel_id=1, source_target_pairs={{0,4},{4,8},{8,12},{12,16},{16,20},{20,24},{24,28},{1,5},{5,9},{9,... | collective-permute-start | bytes 491528 | tf_op jit(solution)/shard_map/ppermute | solution.py:52
  71.2 8.2 %collective-permute-start.10 = (f32[1,4,32,160]{3,2,0,1:T(8,128)S(1)}, f32[1,4,32,160]{3,2,0,1:T(8,128)S(1)}, u32[]{:S(2)}, u32[]{:S(2)}) collective-permute-start(f32[1,4,32,160]{3,2,0,1:T(8,128)S(1)} %get-tuple-element.75), channel_id=1, source_target_pairs={{0,8},{4,12},{8,16},{12,20},{16,24},{20,28},{1,9},{5,13},{9,17},{1... | collective-permute-start | bytes 245768 | tf_op jit(solution)/shard_map/ppermute | solution.py:52
  74.7 6.9 %collective-permute-start.11 = (f32[1,4,32,160]{3,2,0,1:T(8,128)S(1)}, f32[1,4,32,160]{3,2,0,1:T(8,128)S(1)}, u32[]{:S(2)}, u32[]{:S(2)}) collective-permute-start(f32[1,4,32,160]{3,2,0,1:T(8,128)S(1)} %get-tuple-element.76), channel_id=1, source_target_pairs={{8,0},{12,4},{16,8},{20,12},{24,16},{28,20},{9,1},{13,5},{17,9},{2... | collective-permute-start | bytes 245768 | tf_op jit(solution)/shard_map/ppermute | solution.py:53
  79.4 3.7 %copy-start.4 = (f32[6,31,160]{2,1,0:T(8,128)}, f32[6,31,160]{2,1,0:T(8,128)S(1)}, u32[]{:S(2)}) copy-start(f32[6,31,160]{2,1,0:T(8,128)S(1)} %fusion.85) | copy-start | bytes 357124
  81.7 1.4 copy-start.15
  81.8 1.4 copy-start.17
  81.8 1.4 copy-start.19
  81.8 1.4 copy-start.21
  81.8 1.4 copy-start.23
  82.1 1.5 %copy-start.34 = (s32[160]{0:T(256)S(1)}, s32[160]{0:T(256)}, u32[]{:S(2)}) copy-start(s32[160]{0:T(256)} %get-tuple-element.122) | copy-start | bytes 1924
  82.1 1.5 %copy-start.37 = (s32[160]{0:T(256)S(1)}, s32[160]{0:T(256)}, u32[]{:S(2)}) copy-start(s32[160]{0:T(256)} %get-tuple-element.123) | copy-start | bytes 1924
  82.1 1.5 %copy-start.48 = (pred[160]{0:T(512)(128)(4,1)S(1)}, pred[160]{0:T(512)(128)(4,1)}, u32[]{:S(2)}) copy-start(pred[160]{0:T(512)(128)(4,1)} %compare_and_fusion) | copy-start | bytes 484
  85.0 13.5 %all-to-all-start = ((f32[8,1,4,16,80]{4,3,2,1,0:T(8,128)}), f32[8,1,4,16,80]{4,3,2,1,0:T(8,128)}, u32[]{:S(2)}, u32[]{:S(2)}) async-start(f32[8,1,4,16,80]{4,3,2,1,0:T(8,128)} %broadcast_in_dim.42), calls=%async_computation | async-start | bytes 524288 | tf_op jit(solution)/shard_map/all_to_all | solution.py:60
  100.5 2.4 %copy-start.35 = (s32[160]{0:T(256)S(1)}, s32[160]{0:T(256)}, u32[]{:S(2)}) copy-start(s32[160]{0:T(256)} %get-tuple-element.122) | copy-start | bytes 1924
  100.6 2.4 %copy-start.38 = (s32[160]{0:T(256)S(1)}, s32[160]{0:T(256)}, u32[]{:S(2)}) copy-start(s32[160]{0:T(256)} %get-tuple-element.123) | copy-start | bytes 1924
  100.6 2.4 %copy-start.49 = (pred[160]{0:T(512)(128)(4,1)S(1)}, pred[160]{0:T(512)(128)(4,1)}, u32[]{:S(2)}) copy-start(pred[160]{0:T(512)(128)(4,1)} %compare_and_fusion) | copy-start | bytes 484
  101.5 1.7 %copy-start.42 = (s32[32]{0:T(128)S(1)}, s32[32]{0:T(128)}, u32[]{:S(2)}) copy-start(s32[32]{0:T(128)} %broadcast_add_fusion.2) | copy-start | bytes 388
  101.5 1.7 %copy-start.44 = (s32[32]{0:T(128)S(1)}, s32[32]{0:T(128)}, u32[]{:S(2)}) copy-start(s32[32]{0:T(128)} %iota_shift-right-logical_fusion.2) | copy-start | bytes 388
  101.5 1.7 %copy-start.46 = (pred[32]{0:T(512)(128)(4,1)S(1)}, pred[32]{0:T(512)(128)(4,1)}, u32[]{:S(2)}) copy-start(pred[32]{0:T(512)(128)(4,1)} %compare_and_fusion.1) | copy-start | bytes 100
  101.6 1.9 %copy-start.7 = (f32[4,32,160]{2,1,0:T(8,128)S(1)}, f32[4,32,160]{2,1,0:T(8,128)}, u32[]{:S(2)}) copy-start(f32[4,32,160]{2,1,0:T(8,128)} %copy-done.6) | copy-start | bytes 245764
  102.6 8.8 %copy-start.5 = (f32[6,31,160]{2,1,0:T(8,128)S(1)}, f32[6,31,160]{2,1,0:T(8,128)}, u32[]{:S(2)}) copy-start(f32[6,31,160]{2,1,0:T(8,128)} %copy-done.4) | copy-start | bytes 357124
  102.6 8.8 %copy-start.16 = (f32[6,32,160]{2,1,0:T(8,128)S(1)}, f32[6,32,160]{2,1,0:T(8,128)}, u32[]{:S(2)}) copy-start(f32[6,32,160]{2,1,0:T(8,128)} %copy-done.15) | copy-start | bytes 368644
  102.7 8.8 %copy-start.18 = (f32[6,1,32,160]{3,2,0,1:T(8,128)S(1)}, f32[6,1,32,160]{3,2,0,1:T(8,128)}, u32[]{:S(2)}) copy-start(f32[6,1,32,160]{3,2,0,1:T(8,128)} %copy-done.17) | copy-start | bytes 368644
  102.7 8.8 %copy-start.20 = (f32[6,1,32,160]{3,2,0,1:T(8,128)S(1)}, f32[6,1,32,160]{3,2,0,1:T(8,128)}, u32[]{:S(2)}) copy-start(f32[6,1,32,160]{3,2,0,1:T(8,128)} %copy-done.19) | copy-start | bytes 368644
  102.7 8.8 %copy-start.22 = (f32[6,32,160]{2,1,0:T(8,128)S(1)}, f32[6,32,160]{2,1,0:T(8,128)}, u32[]{:S(2)}) copy-start(f32[6,32,160]{2,1,0:T(8,128)} %copy-done.21) | copy-start | bytes 368644
  102.7 8.8 %copy-start.24 = (f32[6,32,160]{2,1,0:T(8,128)S(1)}, f32[6,32,160]{2,1,0:T(8,128)}, u32[]{:S(2)}) copy-start(f32[6,32,160]{2,1,0:T(8,128)} %copy-done.23) | copy-start | bytes 368644
  102.7 8.8 %copy-start.26 = (f32[4,32,160]{2,1,0:T(8,128)S(1)}, f32[4,32,160]{2,1,0:T(8,128)}, u32[]{:S(2)}) copy-start(f32[4,32,160]{2,1,0:T(8,128)} %get-tuple-element.16) | copy-start | bytes 245764
  102.7 8.8 %copy-start.28 = (pred[4]{0:T(512)(128)(4,1)S(1)}, pred[4]{0:T(512)(128)(4,1)}, u32[]{:S(2)}) copy-start(pred[4]{0:T(512)(128)(4,1)} %compare_and_fusion.2) | copy-start | bytes 16
  103.5 6.2 %collective-permute-start.13 = (f32[2,32,160]{2,1,0:T(8,128)S(1)}, f32[2,32,160]{2,1,0:T(8,128)S(1)}, u32[]{:S(2)}, u32[]{:S(2)}) collective-permute-start(f32[2,32,160]{2,1,0:T(8,128)S(1)} %slice_add_fusion.3), channel_id=1, source_target_pairs={{4,0},{8,4},{12,8},{16,12},{20,16},{24,20},{28,24},{5,1},{9,5},{13... | collective-permute-start | bytes 122888 | tf_op jit(solution)/shard_map/ppermute | solution.py:53
  104.8 6.4 %collective-permute-start.12 = (f32[2,32,160]{2,1,0:T(8,128)S(1)}, f32[2,32,160]{2,1,0:T(8,128)S(1)}, u32[]{:S(2)}, u32[]{:S(2)}) collective-permute-start(f32[2,32,160]{2,1,0:T(8,128)S(1)} %slice_add_fusion.3), channel_id=1, source_target_pairs={{0,4},{4,8},{8,12},{12,16},{16,20},{20,24},{24,28},{1,5},{5,9},{9,... | collective-permute-start | bytes 122888 | tf_op jit(solution)/shard_map/ppermute | solution.py:52
  111.4 0.8 copy-start.13
  111.4 0.8 copy-start.30
  111.4 0.8 copy-start.32
  111.4 0.8 copy-start.40
  113.0 12.2 %copy-start.1 = (f32[4,64,320]{2,1,0:T(8,128)S(1)}, f32[4,64,320]{2,1,0:T(8,128)}, u32[]{:S(2)}) copy-start(f32[4,64,320]{2,1,0:T(8,128)} %copy-done) | copy-start | bytes 983044
  113.1 7.6 %collective-permute-start.14 = (f32[1,64,320]{2,1,0:T(8,128)S(1)}, f32[1,64,320]{2,1,0:T(8,128)S(1)}, u32[]{:S(2)}, u32[]{:S(2)}) collective-permute-start(f32[1,64,320]{2,1,0:T(8,128)S(1)} %get-tuple-element.47), channel_id=1, source_target_pairs={{0,4},{4,8},{8,12},{12,16},{16,20},{20,24},{24,28},{1,5},{5,9},{9,... | collective-permute-start | bytes 245768 | tf_op jit(solution)/shard_map/ppermute | solution.py:52
  117.5 7.7 %collective-permute-start.15 = (f32[1,64,320]{2,1,0:T(8,128)S(1)}, f32[1,64,320]{2,1,0:T(8,128)S(1)}, u32[]{:S(2)}, u32[]{:S(2)}) collective-permute-start(f32[1,64,320]{2,1,0:T(8,128)S(1)} %get-tuple-element.48), channel_id=1, source_target_pairs={{4,0},{8,4},{12,8},{16,12},{20,16},{24,20},{28,24},{5,1},{9,5},{13... | collective-permute-start | bytes 245768 | tf_op jit(solution)/shard_map/ppermute | solution.py:53
  125.9 7.1 %collective-permute-start.16 = (f32[1,64,320]{2,1,0:T(8,128)S(1)}, f32[1,64,320]{2,1,0:T(8,128)S(1)}, u32[]{:S(2)}, u32[]{:S(2)}) collective-permute-start(f32[1,64,320]{2,1,0:T(8,128)S(1)} %get-tuple-element.41), channel_id=1, source_target_pairs={{0,4},{4,8},{8,12},{12,16},{16,20},{20,24},{24,28},{1,5},{5,9},{9,... | collective-permute-start | bytes 245768 | tf_op jit(solution)/shard_map/ppermute | solution.py:52
  130.8 6.5 %collective-permute-start.17 = (f32[1,64,320]{2,1,0:T(8,128)S(1)}, f32[1,64,320]{2,1,0:T(8,128)S(1)}, u32[]{:S(2)}, u32[]{:S(2)}) collective-permute-start(f32[1,64,320]{2,1,0:T(8,128)S(1)} %get-tuple-element.42), channel_id=1, source_target_pairs={{4,0},{8,4},{12,8},{16,12},{20,16},{24,20},{28,24},{5,1},{9,5},{13... | collective-permute-start | bytes 245768 | tf_op jit(solution)/shard_map/ppermute | solution.py:53
  137.9 5.0 %collective-permute-start.18 = (f32[1,64,320]{2,1,0:T(8,128)S(1)}, f32[1,64,320]{2,1,0:T(8,128)S(1)}, u32[]{:S(2)}, u32[]{:S(2)}) collective-permute-start(f32[1,64,320]{2,1,0:T(8,128)S(1)} %get-tuple-element.37), channel_id=1, source_target_pairs={{0,4},{4,8},{8,12},{12,16},{16,20},{20,24},{24,28},{1,5},{5,9},{9,... | collective-permute-start | bytes 245768 | tf_op jit(solution)/shard_map/ppermute | solution.py:52
  140.7 6.5 %collective-permute-start.19 = (f32[1,64,320]{2,1,0:T(8,128)S(1)}, f32[1,64,320]{2,1,0:T(8,128)S(1)}, u32[]{:S(2)}, u32[]{:S(2)}) collective-permute-start(f32[1,64,320]{2,1,0:T(8,128)S(1)} %get-tuple-element.38), channel_id=1, source_target_pairs={{4,0},{8,4},{12,8},{16,12},{20,16},{24,20},{28,24},{5,1},{9,5},{13... | collective-permute-start | bytes 245768 | tf_op jit(solution)/shard_map/ppermute | solution.py:53
  142.2 5.2 %copy-start.3 = (f32[4,64,320]{2,1,0:T(8,128)S(1)}, f32[4,64,320]{2,1,0:T(8,128)}, u32[]{:S(2)}) copy-start(f32[4,64,320]{2,1,0:T(8,128)} %copy-done.2) | copy-start | bytes 983044
  142.2 5.2 %copy-start.25 = (f32[4,64,320]{2,1,0:T(8,128)S(1)}, f32[4,64,320]{2,1,0:T(8,128)}, u32[]{:S(2)}) copy-start(f32[4,64,320]{2,1,0:T(8,128)} %get-tuple-element.4) | copy-start | bytes 983044
  (7 other events, 4.6 us)

commit v10 on v9

--- a/solution.py
+++ b/solution.py
@@ -152,15 +152,19 @@
     applied, density = apply_op(weights_one, alt_extend(density, 1), 1)
     rhs_two = coarsen(wide_source - applied)
 
-    level_two = alt_extend(jnp.stack([rhs_two] + coef_two, 1), 3)
+    level_two = alt_extend(jnp.stack([rhs_two] + coef_two, 1), SWEEPS + 2)
     weights_two = make_weights(
-        level_two[:, 1], trim(level_two[:, 2], 3, 2), trim(level_two[:, 3], 3, 2), 0.25, 2
+        level_two[:, 1],
+        trim(level_two[:, 2], SWEEPS + 2, SWEEPS + 1),
+        trim(level_two[:, 3], SWEEPS + 2, SWEEPS + 1),
+        0.25,
+        SWEEPS + 1,
     )
-    rhs_two_x = trim(level_two[:, 0], 3, 2)
-    correction = first_sweep(weights_two, rhs_two_x, 2)
-    correction = sweep(weights_two, correction, 2, rhs_two_x, 2)
-    applied, correction = apply_op(weights_two, correction, 1)
-    rhs_three = coarsen(trim(rhs_two_x, 2, 0) - applied)
+    rhs_two_x = trim(level_two[:, 0], SWEEPS + 2, SWEEPS + 1)
+    correction = first_sweep(weights_two, rhs_two_x, SWEEPS + 1)
+    correction = sweep(weights_two, correction, SWEEPS + 1, rhs_two_x, SWEEPS + 1)
+    applied, _ = apply_op(weights_two, trim(correction, SWEEPS, 1), 1)
+    rhs_three = coarsen(trim(rhs_two_x, SWEEPS + 1, 0) - applied)
 
     height = rhs_three.shape[0]
     column = spread_gather(jnp.stack([rhs_three] + coef_three, 1))
@@ -169,12 +173,13 @@
     coarse_part = first_sweep(weights_three, rhs_three_x, 0)
     for _ in range(COARSE_SWEEPS - 1):
         coarse_part = sweep(weights_three, pad_rows(coarse_part), 1, rhs_three_x, 0, masked=False)
-    coarse_part = lax.dynamic_slice_in_dim(coarse_part, lax.axis_index("alt") * height, height, 0)
+    reach = SWEEPS // 2
+    coarse_part = jnp.pad(coarse_part, ((reach, reach), (0, 0), (0, 0)))
+    coarse_part = lax.dynamic_slice_in_dim(coarse_part, lax.axis_index("alt") * height, height + 2 * reach, 0)
 
     correction = correction + refine(coarse_part)
-    correction = alt_extend(correction, SWEEPS)
     for halo in range(SWEEPS, 0, -1):
-        correction = sweep(weights_two, correction, halo, rhs_two_x, 2)
+        correction = sweep(weights_two, correction, halo, rhs_two_x, SWEEPS + 1)
 
     density = density + refine(correction)
     for _ in range(SWEEPS):

time: 150 us -> 144 us (0.960)
  starting transfers between devices: 56.7 us -> 50.2 us
  other arithmetic: 22.9 us -> 24.6 us
    ppermute x9 -> x8, starting transfers between devices: 37.8 us -> 30.5 us  [alt_extend(): below.insert(0, lax.ppermute(values[low:], 'alt', up))]
    all_to_all x1, starting transfers between devices: 4.82 us -> 6.86 us  [spread_gather(): every = lax.all_to_all(copies, 'alt', 0, 0)]
    ppermute x9 -> x8, waiting for transfers between devices: 9.55 us -> 7.54 us  [alt_extend(): below.insert(0, lax.ppermute(values[low:], 'alt', up))]
    and x3 -> x4, other arithmetic: 0.54 us -> 2.29 us  [inside(): return (rows >= 0) & (rows < depth * lax.axis_size('alt'))]
    ppermute x9 -> x8, waiting for transfers between devices: 24.1 us -> 25.2 us  [alt_extend(): above.append(lax.ppermute(values[:high], 'alt', down))]
    ppermute x9 -> x8, starting transfers between devices: 11.6 us -> 10.5 us  [alt_extend(): above.append(lax.ppermute(values[:high], 'alt', down))]
  transfers between devices with their start and end apart: 21 -> 19, of which waited for: 17 -> 16; matrix products, arithmetic and copies ran while one was open for 13% -> 13% of each run, Pallas kernels for 0% -> 0%
where the time goes in v10:
time: 144 us; the launch traced here: 143 us
  starting transfers between devices  50.2 us (35%)
  waiting for transfers between devices  48.6 us (34%)
  other arithmetic  24.6 us (17%)
  matrix products  9.23 us (6%)
  local copies, waits for them, and re-layouts  8.13 us (6%)
  between operations  1.91 us (1%)
    ppermute x8, starting transfers between devices, alt_extend(): below.insert(0, lax.ppermute(values[low:], 'alt', up))  30.5 us
    ppermute x8, waiting for transfers between devices, alt_extend(): above.append(lax.ppermute(values[:high], 'alt', down))  25.2 us
    ppermute x8, starting transfers between devices, alt_extend(): above.append(lax.ppermute(values[:high], 'alt', down))  10.5 us
    all_to_all x1, waiting for transfers between devices, spread_gather(): every = lax.all_to_all(copies, 'alt', 0, 0)  8.25 us
    ppermute x8, waiting for transfers between devices, alt_extend(): below.insert(0, lax.ppermute(values[low:], 'alt', up))  7.54 us
    all_to_all x1, starting transfers between devices, spread_gather(): every = lax.all_to_all(copies, 'alt', 0, 0)  6.86 us
    dot_general x8, matrix products, coarsen(): summed = jnp.matmul(summed, pairing(length), precision=HIGH)  6.71 us
    ppermute x1, waiting for transfers between devices, raan_extend(): before = lax.ppermute(values[..., length - halo:], 'raan', up)  5.78 us
  transfers between devices with their start and end apart: 19, of which 16 were waited for; matrix products, arithmetic and copies ran while one was open for 13% of the time, Pallas kernels for 0%

profile of v10, /device:TPU:0, one launch (start us, length us, event | category | flops | bytes accessed | tf_op | source)
XLA Modules:
  0.0 142.7 jit_solution(6452502570751540960)
XLA Ops:
  0.6 1.3 pad_maximum_fusion.1
  2.0 1.0 fusion.270
  3.4 1.9 %collective-permute-start.1 = (f32[4,4,64,32]{3,2,0,1:T(8,128)S(1)}, f32[4,4,64,32]{3,2,0,1:T(8,128)S(1)}, u32[]{:S(2)}, u32[]{:S(2)}) collective-permute-start(f32[4,4,64,32]{3,2,0,1:T(8,128)S(1)} %get-tuple-element.30), channel_id=1, source_target_pairs={{1,0},{2,1},{3,2},{0,3},{5,4},{6,5},{7,6},{4,7},{9,8},{10,9},{11,1... | collective-permute-start | bytes 393224 | tf_op jit(solution)/shard_map/ppermute | solution.py:40
  5.8 0.6 compare_and_fusion.1
  6.4 0.5 compare_and_fusion
  7.0 0.5 fusion.244
  7.5 0.6 iota_shift-right-logical_fusion.1
  8.1 0.5 compare_and_fusion.6
  8.6 0.6 compare_and_fusion.2
  9.2 0.6 iota_shift-right-logical_fusion
  9.8 5.8 %collective-permute-done = f32[4,4,64,32]{3,2,0,1:T(8,128)S(1)} collective-permute-done((f32[4,4,64,32]{3,2,0,1:T(8,128)}, f32[4,4,64,32]{3,2,0,1:T(8,128)S(1)}, u32[]{:S(2)}, u32[]{:S(2)}) %collective-permute-start) | collective-permute-done | bytes 131104 | tf_op jit(solution)/shard_map/ppermute | solution.py:39
  15.6 1.9 %collective-permute-done.1 = f32[4,4,64,32]{3,2,0,1:T(8,128)S(1)} collective-permute-done((f32[4,4,64,32]{3,2,0,1:T(8,128)S(1)}, f32[4,4,64,32]{3,2,0,1:T(8,128)S(1)}, u32[]{:S(2)}, u32[]{:S(2)}) %collective-permute-start.1) | collective-permute-done | bytes 131104 | tf_op jit(solution)/shard_map/ppermute | solution.py:40
  17.5 1.0 pad_maximum_fusion.26
  18.5 1.3 collective-permute-start.3
  19.8 5.2 %collective-permute-start.2 = (f32[1,2,64,320]{3,2,0,1:T(8,128)}, f32[1,2,64,320]{3,2,0,1:T(8,128)}, u32[]{:S(2)}, u32[]{:S(2)}) collective-permute-start(f32[1,2,64,320]{3,2,0,1:T(8,128)} %get-tuple-element.20), channel_id=1, source_target_pairs={{0,4},{4,8},{8,12},{12,16},{16,20},{20,24},{24,28},{1,5},{5,9},{9,... | collective-permute-start | bytes 491528 | tf_op jit(solution)/shard_map/ppermute | solution.py:52
  25.0 1.6 %pad_maximum_fusion = f32[4,4,64,320]{3,2,0,1:T(8,128)S(1)} fusion(f32[4,4,64,32]{3,2,0,1:T(8,128)} %copy-done.32, f32[4,1,64,256]{3,2,0,1:T(8,128)S(1)} %bitcast.278, f32[4,1,64,256]{3,2,0,1:T(8,128)S(1)} %bitcast.281, f32[4,1,64,256]{3,2,0,1:T(8,128)S(1)} %bitcast.284, f32[4,1,64,256]{3,2,0,1:T(8,128)S(1)} %bitcast.287, ...), kind=kLoop, calls=%fused_computation | loop fusion | flops 1638400 | bytes 2621440 | tf_op jit(solution)/shard_map/concatenate | solution.py:41
  26.6 1.0 fusion.269
  27.7 1.9 %reduce_sum.73 = f32[2,64,320]{2,1,0:T(8,128)} reduce(f32[2,2,64,320]{3,2,1,0:T(8,128)} %bitcast.290, f32[]{:T(128)} %constant.143.clone.1), dimensions={1}, to_apply=%region_1.2 | reduce | flops 40960 | bytes 491524 | tf_op jit(solution)/shard_map/reduce_sum | solution.py:21
  29.6 0.7 reduce_sum.74
  30.3 1.4 fusion.259
  31.6 1.1 fusion.255
  32.8 1.4 fusion.257
  34.7 1.0 fusion.127
  35.7 1.0 fusion.125
  38.0 2.0 %fusion.72 = (f32[4,64,320]{2,1,0:T(8,128)}, f32[4,64,320]{2,1,0:T(8,128)S(1)}, f32[4,64,320]{2,1,0:T(8,128)S(1)}, f32[4,64,320]{2,1,0:T(8,128)S(1)}, f32[4,64,320]{2,1,0:T(8,128)S(1)}) fusion(f32[4,63,320]{2,1,0:T(8,128)S(1)} %get-tuple-element.108, f32[4,2,64,320]{3,2,0,1:T(8,128)S(1)} %slice.764, f32[1,2,64,320]{3,2,0,1:T(8,128)} %collective-permute-done.2, ...), kind=kLoop, calls=%fused_computation.107 | loop fusion | flops 1310720 | bytes 4252672 | tf_op jit(solution)/shard_map/add | solution.py:87
  40.0 1.6 %fusion.76 = f32[4,64,320]{2,1,0:T(8,128)S(1)} fusion(f32[4,64,320]{2,1,0:T(8,128)S(1)} %get-tuple-element.8, f32[4,64,319]{2,1,0:T(8,128)S(1)} %get-tuple-element.64, f32[4,64,320]{2,1,0:T(8,128)S(1)} %get-tuple-element.7, f32[4,64,319]{2,1,0:T(8,128)S(1)} %get-tuple-element.63, f32[4,63,320]{2,1,0:T(8,128)S(1)} %get-tuple-element.62, ...), kind=kLoop, calls=%fused_computation.111 | loop fusion | flops 2129920 | bytes 4570116 | tf_op jit(solution)/shard_map/jit(_where)/select_n | solution.py:125
  41.7 4.1 %collective-permute-start.4 = (f32[1,64,320]{2,1,0:T(8,128)S(1)}, f32[1,64,320]{2,1,0:T(8,128)S(1)}, u32[]{:S(2)}, u32[]{:S(2)}) collective-permute-start(f32[1,64,320]{2,1,0:T(8,128)S(1)} %get-tuple-element.55), channel_id=1, source_target_pairs={{0,4},{4,8},{8,12},{12,16},{16,20},{20,24},{24,28},{1,5},{5,9},{9,... | collective-permute-start | bytes 245768 | tf_op jit(solution)/shard_map/ppermute | solution.py:52
  45.7 1.3 collective-permute-start.5
  47.2 1.0 collective-permute-done.4
  48.2 4.1 %collective-permute-done.5 = f32[1,64,320]{2,1,0:T(8,128)S(1)} collective-permute-done((f32[1,64,320]{2,1,0:T(8,128)S(1)}, f32[1,64,320]{2,1,0:T(8,128)S(1)}, u32[]{:S(2)}, u32[]{:S(2)}) %collective-permute-start.5) | collective-permute-done | bytes 81952 | tf_op jit(solution)/shard_map/ppermute | solution.py:53
  52.9 3.4 %collective-permute-start.6 = (f32[1,64,320]{2,1,0:T(8,128)S(1)}, f32[1,64,320]{2,1,0:T(8,128)S(1)}, u32[]{:S(2)}, u32[]{:S(2)}) collective-permute-start(f32[1,64,320]{2,1,0:T(8,128)S(1)} %get-tuple-element.49), channel_id=1, source_target_pairs={{0,4},{4,8},{8,12},{12,16},{16,20},{20,24},{24,28},{1,5},{5,9},{9,... | collective-permute-start | bytes 245768 | tf_op jit(solution)/shard_map/ppermute | solution.py:52
  56.3 1.3 collective-permute-start.7
  57.8 0.7 collective-permute-done.6
  58.5 4.3 %collective-permute-done.7 = f32[1,64,320]{2,1,0:T(8,128)S(1)} collective-permute-done((f32[1,64,320]{2,1,0:T(8,128)S(1)}, f32[1,64,320]{2,1,0:T(8,128)S(1)}, u32[]{:S(2)}, u32[]{:S(2)}) %collective-permute-start.7) | collective-permute-done | bytes 81952 | tf_op jit(solution)/shard_map/ppermute | solution.py:53
  64.2 3.5 %collective-permute-start.8 = (f32[2,4,32,160]{3,2,0,1:T(8,128)S(1)}, f32[2,4,32,160]{3,2,0,1:T(8,128)S(1)}, u32[]{:S(2)}, u32[]{:S(2)}) collective-permute-start(f32[2,4,32,160]{3,2,0,1:T(8,128)S(1)} %pad_maximum_fusion.25), channel_id=1, source_target_pairs={{0,8},{4,12},{8,16},{12,20},{16,24},{20,28},{1,9},{5,13},{9,17},{1... | collective-permute-start | bytes 491528 | tf_op jit(solution)/shard_map/ppermute | solution.py:52
  67.8 4.3 %collective-permute-start.9 = (f32[2,4,32,160]{3,2,0,1:T(8,128)S(1)}, f32[2,4,32,160]{3,2,0,1:T(8,128)S(1)}, u32[]{:S(2)}, u32[]{:S(2)}) collective-permute-start(f32[2,4,32,160]{3,2,0,1:T(8,128)S(1)} %pad_maximum_fusion.25), channel_id=1, source_target_pairs={{0,4},{4,8},{8,12},{12,16},{16,20},{20,24},{24,28},{1,5},{5,9},{9,... | collective-permute-start | bytes 491528 | tf_op jit(solution)/shard_map/ppermute | solution.py:52
  72.3 1.3 collective-permute-start.11
  73.6 1.3 collective-permute-start.10
  74.9 1.1 collective-permute-done.9
  76.1 5.8 %collective-permute-done.10 = f32[2,4,32,160]{3,2,0,1:T(8,128)S(1)} collective-permute-done((f32[2,4,32,160]{3,2,0,1:T(8,128)S(1)}, f32[2,4,32,160]{3,2,0,1:T(8,128)S(1)}, u32[]{:S(2)}, u32[]{:S(2)}) %collective-permute-start.10) | collective-permute-done | bytes 163872 | tf_op jit(solution)/shard_map/ppermute | solution.py:53
  81.9 0.8 collective-permute-done.11
  85.3 0.7 broadcast_in_dim.52
  86.1 6.9 %all-to-all-start = ((f32[8,1,4,16,80]{4,3,2,1,0:T(8,128)}), f32[8,1,4,16,80]{4,3,2,1,0:T(8,128)}, u32[]{:S(2)}, u32[]{:S(2)}) async-start(f32[8,1,4,16,80]{4,3,2,1,0:T(8,128)} %broadcast_in_dim.52), calls=%async_computation | async-start | bytes 524288 | tf_op jit(solution)/shard_map/all_to_all | solution.py:60
  92.9 0.6 compare_and_fusion.3
  93.5 0.6 compare_and_fusion.4
  94.1 8.3 %all-to-all-done = f32[8,1,4,16,80]{4,3,2,1,0:T(8,128)} async-done(((f32[8,1,4,16,80]{4,3,2,1,0:T(8,128)}), f32[8,1,4,16,80]{4,3,2,1,0:T(8,128)}, u32[]{:S(2)}, u32[]{:S(2)}) %all-to-all-start) | async-done | bytes 163872 | tf_op jit(solution)/shard_map/all_to_all | solution.py:60
  102.3 0.9 slice_bitcast_fusion.7
  103.4 1.0 fusion.202
  104.5 0.9 fusion.145
  105.5 0.9 fusion.157
  106.7 1.1 fusion.169
  110.3 3.2 %collective-permute-start.12 = (f32[1,64,320]{2,1,0:T(8,128)S(1)}, f32[1,64,320]{2,1,0:T(8,128)S(1)}, u32[]{:S(2)}, u32[]{:S(2)}) collective-permute-start(f32[1,64,320]{2,1,0:T(8,128)S(1)} %get-tuple-element.43), channel_id=1, source_target_pairs={{0,4},{4,8},{8,12},{12,16},{16,20},{20,24},{24,28},{1,5},{5,9},{9,... | collective-permute-start | bytes 245768 | tf_op jit(solution)/shard_map/ppermute | solution.py:52
  113.5 1.5 %collective-permute-start.13 = (f32[1,64,320]{2,1,0:T(8,128)S(1)}, f32[1,64,320]{2,1,0:T(8,128)S(1)}, u32[]{:S(2)}, u32[]{:S(2)}) collective-permute-start(f32[1,64,320]{2,1,0:T(8,128)S(1)} %get-tuple-element.44), channel_id=1, source_target_pairs={{4,0},{8,4},{12,8},{16,12},{20,16},{24,20},{28,24},{5,1},{9,5},{13... | collective-permute-start | bytes 245768 | tf_op jit(solution)/shard_map/ppermute | solution.py:53
  115.2 1.5 %collective-permute-done.12 = f32[1,64,320]{2,1,0:T(8,128)S(1)} collective-permute-done((f32[1,64,320]{2,1,0:T(8,128)S(1)}, f32[1,64,320]{2,1,0:T(8,128)S(1)}, u32[]{:S(2)}, u32[]{:S(2)}) %collective-permute-start.12) | collective-permute-done | bytes 81952 | tf_op jit(solution)/shard_map/ppermute | solution.py:52
  116.7 3.3 %collective-permute-done.13 = f32[1,64,320]{2,1,0:T(8,128)S(1)} collective-permute-done((f32[1,64,320]{2,1,0:T(8,128)S(1)}, f32[1,64,320]{2,1,0:T(8,128)S(1)}, u32[]{:S(2)}, u32[]{:S(2)}) %collective-permute-start.13) | collective-permute-done | bytes 81952 | tf_op jit(solution)/shard_map/ppermute | solution.py:53
  120.6 3.9 %collective-permute-start.14 = (f32[1,64,320]{2,1,0:T(8,128)S(1)}, f32[1,64,320]{2,1,0:T(8,128)S(1)}, u32[]{:S(2)}, u32[]{:S(2)}) collective-permute-start(f32[1,64,320]{2,1,0:T(8,128)S(1)} %get-tuple-element.37), channel_id=1, source_target_pairs={{0,4},{4,8},{8,12},{12,16},{16,20},{20,24},{24,28},{1,5},{5,9},{9,... | collective-permute-start | bytes 245768 | tf_op jit(solution)/shard_map/ppermute | solution.py:52
  124.6 1.3 collective-permute-start.15
  126.0 1.5 %collective-permute-done.14 = f32[1,64,320]{2,1,0:T(8,128)S(1)} collective-permute-done((f32[1,64,320]{2,1,0:T(8,128)S(1)}, f32[1,64,320]{2,1,0:T(8,128)S(1)}, u32[]{:S(2)}, u32[]{:S(2)}) %collective-permute-start.14) | collective-permute-done | bytes 81952 | tf_op jit(solution)/shard_map/ppermute | solution.py:52
  127.6 3.5 %collective-permute-done.15 = f32[1,64,320]{2,1,0:T(8,128)S(1)} collective-permute-done((f32[1,64,320]{2,1,0:T(8,128)S(1)}, f32[1,64,320]{2,1,0:T(8,128)S(1)}, u32[]{:S(2)}, u32[]{:S(2)}) %collective-permute-start.15) | collective-permute-done | bytes 81952 | tf_op jit(solution)/shard_map/ppermute | solution.py:53
  131.7 2.8 %collective-permute-start.16 = (f32[1,64,320]{2,1,0:T(8,128)S(1)}, f32[1,64,320]{2,1,0:T(8,128)S(1)}, u32[]{:S(2)}, u32[]{:S(2)}) collective-permute-start(f32[1,64,320]{2,1,0:T(8,128)S(1)} %get-tuple-element.33), channel_id=1, source_target_pairs={{0,4},{4,8},{8,12},{12,16},{16,20},{20,24},{24,28},{1,5},{5,9},{9,... | collective-permute-start | bytes 245768 | tf_op jit(solution)/shard_map/ppermute | solution.py:52
  134.5 1.3 collective-permute-start.17
  136.0 1.7 %collective-permute-done.16 = f32[1,64,320]{2,1,0:T(8,128)S(1)} collective-permute-done((f32[1,64,320]{2,1,0:T(8,128)S(1)}, f32[1,64,320]{2,1,0:T(8,128)S(1)}, u32[]{:S(2)}, u32[]{:S(2)}) %collective-permute-start.16) | collective-permute-done | bytes 81952 | tf_op jit(solution)/shard_map/ppermute | solution.py:52
  137.7 3.3 %collective-permute-done.17 = f32[1,64,320]{2,1,0:T(8,128)S(1)} collective-permute-done((f32[1,64,320]{2,1,0:T(8,128)S(1)}, f32[1,64,320]{2,1,0:T(8,128)S(1)}, u32[]{:S(2)}, u32[]{:S(2)}) %collective-permute-start.17) | collective-permute-done | bytes 81952 | tf_op jit(solution)/shard_map/ppermute | solution.py:53
  141.2 1.5 %fusion.84 = (f32[4,64,256]{2,1,0:T(8,128)}, f32[4,64,256]{2,1,0:T(8,128)}) fusion(f32[4,63,320]{2,1,0:T(8,128)S(1)} %get-tuple-element.32, f32[4,64,320]{2,1,0:T(8,128)S(1)} %copy-done.5, f32[4,64,319]{2,1,0:T(8,128)S(1)} %get-tuple-element.36, f32[4,64,320]{2,1,0:T(8,128)S(1)} %copy-done.1, f32[4,64,319]{2,1,0:T(8,128)S(1)} %get-tuple-element.35, ...), kind=kLoop, calls=%fused_computation.120 | loop fusion | flops 655360 | bytes 3395584 | tf_op jit(solution)/shard_map/div | solution.py:188
  (194 shorter events, 12.3 us)
Async XLA Ops:
  1.9 15.6 %copy-start.28 = (f32[4,64,256]{2,1,0:T(8,128)S(1)}, f32[4,64,256]{2,1,0:T(8,128)}, u32[]{:S(2)}) copy-start(f32[4,64,256]{2,1,0:T(8,128)} %param.7) | copy-start | bytes 786436
  1.9 15.5 %copy-start.29 = (f32[4,64,256]{2,1,0:T(8,128)S(1)}, f32[4,64,256]{2,1,0:T(8,128)}, u32[]{:S(2)}) copy-start(f32[4,64,256]{2,1,0:T(8,128)} %param.6) | copy-start | bytes 786436
  1.9 15.5 %copy-start.30 = (f32[4,64,256]{2,1,0:T(8,128)S(1)}, f32[4,64,256]{2,1,0:T(8,128)}, u32[]{:S(2)}) copy-start(f32[4,64,256]{2,1,0:T(8,128)} %param.5) | copy-start | bytes 786436
  2.0 15.5 %copy-start.31 = (f32[4,64,256]{2,1,0:T(8,128)S(1)}, f32[4,64,256]{2,1,0:T(8,128)}, u32[]{:S(2)}) copy-start(f32[4,64,256]{2,1,0:T(8,128)} %param.4) | copy-start | bytes 786436
  3.0 12.6 %collective-permute-start = (f32[4,4,64,32]{3,2,0,1:T(8,128)}, f32[4,4,64,32]{3,2,0,1:T(8,128)S(1)}, u32[]{:S(2)}, u32[]{:S(2)}) collective-permute-start(f32[4,4,64,32]{3,2,0,1:T(8,128)} %get-tuple-element.29), channel_id=1, source_target_pairs={{0,1},{1,2},{2,3},{3,0},{4,5},{5,6},{6,7},{7,4},{8,9},{9,10},{10,1... | collective-permute-start | bytes 393224 | tf_op jit(solution)/shard_map/ppermute | solution.py:39
  3.4 14.0 %collective-permute-start.1 = (f32[4,4,64,32]{3,2,0,1:T(8,128)S(1)}, f32[4,4,64,32]{3,2,0,1:T(8,128)S(1)}, u32[]{:S(2)}, u32[]{:S(2)}) collective-permute-start(f32[4,4,64,32]{3,2,0,1:T(8,128)S(1)} %get-tuple-element.30), channel_id=1, source_target_pairs={{1,0},{2,1},{3,2},{0,3},{5,4},{6,5},{7,6},{4,7},{9,8},{10,9},{11,1... | collective-permute-start | bytes 393224 | tf_op jit(solution)/shard_map/ppermute | solution.py:40
  17.5 2.3 %copy-start.32 = (f32[4,4,64,32]{3,2,0,1:T(8,128)}, f32[4,4,64,32]{3,2,0,1:T(8,128)S(1)}, u32[]{:S(2)}) copy-start(f32[4,4,64,32]{3,2,0,1:T(8,128)S(1)} %collective-permute-done.1) | copy-start | bytes 393220
  18.5 19.5 %collective-permute-start.3 = (f32[1,2,64,320]{3,2,0,1:T(8,128)}, f32[1,2,64,320]{3,2,0,1:T(8,128)}, u32[]{:S(2)}, u32[]{:S(2)}) collective-permute-start(f32[1,2,64,320]{3,2,0,1:T(8,128)} %get-tuple-element.19), channel_id=1, source_target_pairs={{4,0},{8,4},{12,8},{16,12},{20,16},{24,20},{28,24},{5,1},{9,5},{13... | collective-permute-start | bytes 491528 | tf_op jit(solution)/shard_map/ppermute | solution.py:53
  19.8 18.2 %collective-permute-start.2 = (f32[1,2,64,320]{3,2,0,1:T(8,128)}, f32[1,2,64,320]{3,2,0,1:T(8,128)}, u32[]{:S(2)}, u32[]{:S(2)}) collective-permute-start(f32[1,2,64,320]{3,2,0,1:T(8,128)} %get-tuple-element.20), channel_id=1, source_target_pairs={{0,4},{4,8},{8,12},{12,16},{16,20},{20,24},{24,28},{1,5},{5,9},{9,... | collective-permute-start | bytes 491528 | tf_op jit(solution)/shard_map/ppermute | solution.py:52
  27.7 9.1 %copy-start.4 = (f32[4,64,320]{2,1,0:T(8,128)}, f32[4,64,320]{2,1,0:T(8,128)S(1)}, u32[]{:S(2)}) copy-start(f32[4,64,320]{2,1,0:T(8,128)S(1)} %get-tuple-element.26) | copy-start | bytes 983044
  34.3 49.2 %copy-start.22 = (f32[32,2,160]{2,0,1:T(8,128)}, f32[32,2,160]{2,0,1:T(8,128)S(1)}, u32[]{:S(2)}) copy-start(f32[32,2,160]{2,0,1:T(8,128)S(1)} %get-tuple-element.107) | copy-start | bytes 122884
  34.5 49.0 %copy-start.24 = (f32[32,2,160]{2,0,1:T(8,128)}, f32[32,2,160]{2,0,1:T(8,128)S(1)}, u32[]{:S(2)}) copy-start(f32[32,2,160]{2,0,1:T(8,128)S(1)} %get-tuple-element.105) | copy-start | bytes 122884
  34.7 48.8 %copy-start.26 = (f32[32,2,160]{2,0,1:T(8,128)}, f32[32,2,160]{2,0,1:T(8,128)S(1)}, u32[]{:S(2)}) copy-start(f32[32,2,160]{2,0,1:T(8,128)S(1)} %get-tuple-element.103) | copy-start | bytes 122884
  37.1 0.7 copy-start.36
  37.1 0.7 copy-start.38
  38.0 2.0 %copy-start.40 = (pred[4]{0:T(512)(128)(4,1)S(1)}, pred[4]{0:T(512)(128)(4,1)}, u32[]{:S(2)}) copy-start(pred[4]{0:T(512)(128)(4,1)} %compare_and_fusion.6) | copy-start | bytes 16
  40.0 22.8 %copy-start = (f32[4,64,320]{2,1,0:T(8,128)}, f32[4,64,320]{2,1,0:T(8,128)S(1)}, u32[]{:S(2)}) copy-start(f32[4,64,320]{2,1,0:T(8,128)S(1)} %get-tuple-element.8) | copy-start | bytes 983044
  41.7 6.5 %collective-permute-start.4 = (f32[1,64,320]{2,1,0:T(8,128)S(1)}, f32[1,64,320]{2,1,0:T(8,128)S(1)}, u32[]{:S(2)}, u32[]{:S(2)}) collective-permute-start(f32[1,64,320]{2,1,0:T(8,128)S(1)} %get-tuple-element.55), channel_id=1, source_target_pairs={{0,4},{4,8},{8,12},{12,16},{16,20},{20,24},{24,28},{1,5},{5,9},{9,... | collective-permute-start | bytes 245768 | tf_op jit(solution)/shard_map/ppermute | solution.py:52
  45.7 6.6 %collective-permute-start.5 = (f32[1,64,320]{2,1,0:T(8,128)S(1)}, f32[1,64,320]{2,1,0:T(8,128)S(1)}, u32[]{:S(2)}, u32[]{:S(2)}) collective-permute-start(f32[1,64,320]{2,1,0:T(8,128)S(1)} %get-tuple-element.56), channel_id=1, source_target_pairs={{4,0},{8,4},{12,8},{16,12},{20,16},{24,20},{28,24},{5,1},{9,5},{13... | collective-permute-start | bytes 245768 | tf_op jit(solution)/shard_map/ppermute | solution.py:53
  52.9 5.6 %collective-permute-start.6 = (f32[1,64,320]{2,1,0:T(8,128)S(1)}, f32[1,64,320]{2,1,0:T(8,128)S(1)}, u32[]{:S(2)}, u32[]{:S(2)}) collective-permute-start(f32[1,64,320]{2,1,0:T(8,128)S(1)} %get-tuple-element.49), channel_id=1, source_target_pairs={{0,4},{4,8},{8,12},{12,16},{16,20},{20,24},{24,28},{1,5},{5,9},{9,... | collective-permute-start | bytes 245768 | tf_op jit(solution)/shard_map/ppermute | solution.py:52
  56.3 6.5 %collective-permute-start.7 = (f32[1,64,320]{2,1,0:T(8,128)S(1)}, f32[1,64,320]{2,1,0:T(8,128)S(1)}, u32[]{:S(2)}, u32[]{:S(2)}) collective-permute-start(f32[1,64,320]{2,1,0:T(8,128)S(1)} %get-tuple-element.50), channel_id=1, source_target_pairs={{4,0},{8,4},{12,8},{16,12},{20,16},{24,20},{28,24},{5,1},{9,5},{13... | collective-permute-start | bytes 245768 | tf_op jit(solution)/shard_map/ppermute | solution.py:53
  64.2 20.2 %copy-start.6 = (f32[32,2,160]{2,0,1:T(8,128)}, f32[32,2,160]{2,0,1:T(8,128)S(1)}, u32[]{:S(2)}) copy-start(f32[32,2,160]{2,0,1:T(8,128)S(1)} %convolution_multiply_fusion.3) | copy-start | bytes 122884
  64.2 10.7 %collective-permute-start.8 = (f32[2,4,32,160]{3,2,0,1:T(8,128)S(1)}, f32[2,4,32,160]{3,2,0,1:T(8,128)S(1)}, u32[]{:S(2)}, u32[]{:S(2)}) collective-permute-start(f32[2,4,32,160]{3,2,0,1:T(8,128)S(1)} %pad_maximum_fusion.25), channel_id=1, source_target_pairs={{0,8},{4,12},{8,16},{12,20},{16,24},{20,28},{1,9},{5,13},{9,17},{1... | collective-permute-start | bytes 491528 | tf_op jit(solution)/shard_map/ppermute | solution.py:52
  67.8 8.2 %collective-permute-start.9 = (f32[2,4,32,160]{3,2,0,1:T(8,128)S(1)}, f32[2,4,32,160]{3,2,0,1:T(8,128)S(1)}, u32[]{:S(2)}, u32[]{:S(2)}) collective-permute-start(f32[2,4,32,160]{3,2,0,1:T(8,128)S(1)} %pad_maximum_fusion.25), channel_id=1, source_target_pairs={{0,4},{4,8},{8,12},{12,16},{16,20},{20,24},{24,28},{1,5},{5,9},{9,... | collective-permute-start | bytes 491528 | tf_op jit(solution)/shard_map/ppermute | solution.py:52
  72.3 10.4 %collective-permute-start.11 = (f32[2,4,32,160]{3,2,0,1:T(8,128)S(1)}, f32[2,4,32,160]{3,2,0,1:T(8,128)S(1)}, u32[]{:S(2)}, u32[]{:S(2)}) collective-permute-start(f32[2,4,32,160]{3,2,0,1:T(8,128)S(1)} %pad_maximum_fusion.25), channel_id=1, source_target_pairs={{8,0},{12,4},{16,8},{20,12},{24,16},{28,20},{9,1},{13,5},{17,9},{2... | collective-permute-start | bytes 491528 | tf_op jit(solution)/shard_map/ppermute | solution.py:53
  73.6 8.3 %collective-permute-start.10 = (f32[2,4,32,160]{3,2,0,1:T(8,128)S(1)}, f32[2,4,32,160]{3,2,0,1:T(8,128)S(1)}, u32[]{:S(2)}, u32[]{:S(2)}) collective-permute-start(f32[2,4,32,160]{3,2,0,1:T(8,128)S(1)} %pad_maximum_fusion.25), channel_id=1, source_target_pairs={{4,0},{8,4},{12,8},{16,12},{20,16},{24,20},{28,24},{5,1},{9,5},{13... | collective-permute-start | bytes 491528 | tf_op jit(solution)/shard_map/ppermute | solution.py:53
  76.0 7.6 %copy-start.8 = (f32[2,4,32,160]{3,2,0,1:T(8,128)}, f32[2,4,32,160]{3,2,0,1:T(8,128)S(1)}, u32[]{:S(2)}) copy-start(f32[2,4,32,160]{3,2,0,1:T(8,128)S(1)} %collective-permute-done.9) | copy-start | bytes 491524
  81.9 1.7 %copy-start.10 = (f32[2,4,32,160]{3,2,0,1:T(8,128)}, f32[2,4,32,160]{3,2,0,1:T(8,128)S(1)}, u32[]{:S(2)}) copy-start(f32[2,4,32,160]{3,2,0,1:T(8,128)S(1)} %collective-permute-done.10) | copy-start | bytes 491524
  82.8 1.5 %copy-start.2 = (f32[8,31,160]{2,1,0:T(8,128)}, f32[8,31,160]{2,1,0:T(8,128)S(1)}, u32[]{:S(2)}) copy-start(f32[8,31,160]{2,1,0:T(8,128)S(1)} %fusion.85) | copy-start | bytes 476164
  83.2 1.2 copy-start.14
  83.2 1.2 copy-start.16
  83.2 1.2 copy-start.18
  83.2 1.2 copy-start.20
  83.2 1.2 copy-start.33
  86.1 16.3 %all-to-all-start = ((f32[8,1,4,16,80]{4,3,2,1,0:T(8,128)}), f32[8,1,4,16,80]{4,3,2,1,0:T(8,128)}, u32[]{:S(2)}, u32[]{:S(2)}) async-start(f32[8,1,4,16,80]{4,3,2,1,0:T(8,128)} %broadcast_in_dim.52), calls=%async_computation | async-start | bytes 524288 | tf_op jit(solution)/shard_map/all_to_all | solution.py:60
  104.4 3.4 %copy-start.47 = (s32[160]{0:T(256)S(1)}, s32[160]{0:T(256)}, u32[]{:S(2)}) copy-start(s32[160]{0:T(256)} %get-tuple-element.115) | copy-start | bytes 1924
  104.5 3.4 %copy-start.49 = (s32[160]{0:T(256)S(1)}, s32[160]{0:T(256)}, u32[]{:S(2)}) copy-start(s32[160]{0:T(256)} %get-tuple-element.116) | copy-start | bytes 1924
  104.5 3.4 %copy-start.56 = (pred[160]{0:T(512)(128)(4,1)S(1)}, pred[160]{0:T(512)(128)(4,1)}, u32[]{:S(2)}) copy-start(pred[160]{0:T(512)(128)(4,1)} %compare_and_fusion) | copy-start | bytes 484
  105.4 2.7 %copy-start.37 = (s32[32]{0:T(128)S(1)}, s32[32]{0:T(128)}, u32[]{:S(2)}) copy-start(s32[32]{0:T(128)} %iota_shift-right-logical_fusion.2) | copy-start | bytes 388
  105.4 2.7 %copy-start.39 = (pred[32]{0:T(512)(128)(4,1)S(1)}, pred[32]{0:T(512)(128)(4,1)}, u32[]{:S(2)}) copy-start(pred[32]{0:T(512)(128)(4,1)} %compare_and_fusion.1) | copy-start | bytes 100
  105.4 3.0 %copy-start.13 = (f32[6,32,160]{2,1,0:T(8,128)S(1)}, f32[6,32,160]{2,1,0:T(8,128)}, u32[]{:S(2)}) copy-start(f32[6,32,160]{2,1,0:T(8,128)} %copy-done.12) | copy-start | bytes 368644
  106.5 2.1 %copy-start.3 = (f32[8,31,160]{2,1,0:T(8,128)S(1)}, f32[8,31,160]{2,1,0:T(8,128)}, u32[]{:S(2)}) copy-start(f32[8,31,160]{2,1,0:T(8,128)} %copy-done.2) | copy-start | bytes 476164
  106.5 2.1 %copy-start.7 = (f32[32,2,160]{2,0,1:T(8,128)S(1)}, f32[32,2,160]{2,0,1:T(8,128)}, u32[]{:S(2)}) copy-start(f32[32,2,160]{2,0,1:T(8,128)} %copy-done.6) | copy-start | bytes 122884
  106.5 2.1 %copy-start.9 = (f32[2,4,32,160]{3,2,0,1:T(8,128)S(1)}, f32[2,4,32,160]{3,2,0,1:T(8,128)}, u32[]{:S(2)}) copy-start(f32[2,4,32,160]{3,2,0,1:T(8,128)} %copy-done.8) | copy-start | bytes 491524
  106.5 2.1 %copy-start.11 = (f32[2,4,32,160]{3,2,0,1:T(8,128)S(1)}, f32[2,4,32,160]{3,2,0,1:T(8,128)}, u32[]{:S(2)}) copy-start(f32[2,4,32,160]{3,2,0,1:T(8,128)} %copy-done.10) | copy-start | bytes 491524
  106.5 2.1 %copy-start.15 = (f32[8,1,32,160]{3,2,0,1:T(8,128)S(1)}, f32[8,1,32,160]{3,2,0,1:T(8,128)}, u32[]{:S(2)}) copy-start(f32[8,1,32,160]{3,2,0,1:T(8,128)} %copy-done.14) | copy-start | bytes 491524
  106.5 2.1 %copy-start.17 = (f32[8,1,32,160]{3,2,0,1:T(8,128)S(1)}, f32[8,1,32,160]{3,2,0,1:T(8,128)}, u32[]{:S(2)}) copy-start(f32[8,1,32,160]{3,2,0,1:T(8,128)} %copy-done.16) | copy-start | bytes 491524
  106.6 2.1 %copy-start.19 = (f32[8,32,160]{2,1,0:T(8,128)S(1)}, f32[8,32,160]{2,1,0:T(8,128)}, u32[]{:S(2)}) copy-start(f32[8,32,160]{2,1,0:T(8,128)} %copy-done.18) | copy-start | bytes 491524
  106.6 2.1 %copy-start.21 = (f32[8,32,160]{2,1,0:T(8,128)S(1)}, f32[8,32,160]{2,1,0:T(8,128)}, u32[]{:S(2)}) copy-start(f32[8,32,160]{2,1,0:T(8,128)} %copy-done.20) | copy-start | bytes 491524
  106.6 2.1 %copy-start.23 = (f32[32,2,160]{2,0,1:T(8,128)S(1)}, f32[32,2,160]{2,0,1:T(8,128)}, u32[]{:S(2)}) copy-start(f32[32,2,160]{2,0,1:T(8,128)} %copy-done.22) | copy-start | bytes 122884
  106.6 2.1 %copy-start.25 = (f32[32,2,160]{2,0,1:T(8,128)S(1)}, f32[32,2,160]{2,0,1:T(8,128)}, u32[]{:S(2)}) copy-start(f32[32,2,160]{2,0,1:T(8,128)} %copy-done.24) | copy-start | bytes 122884
  106.6 2.1 %copy-start.27 = (f32[32,2,160]{2,0,1:T(8,128)S(1)}, f32[32,2,160]{2,0,1:T(8,128)}, u32[]{:S(2)}) copy-start(f32[32,2,160]{2,0,1:T(8,128)} %copy-done.26) | copy-start | bytes 122884
  106.6 2.1 %copy-start.34 = (f32[8,32,160]{2,1,0:T(8,128)S(1)}, f32[8,32,160]{2,1,0:T(8,128)}, u32[]{:S(2)}) copy-start(f32[8,32,160]{2,1,0:T(8,128)} %copy-done.33) | copy-start | bytes 491524
  106.6 2.1 %copy-start.53 = (pred[4]{0:T(512)(128)(4,1)S(1)}, pred[4]{0:T(512)(128)(4,1)}, u32[]{:S(2)}) copy-start(pred[4]{0:T(512)(128)(4,1)} %compare_and_fusion.3) | copy-start | bytes 16
  110.2 9.8 %copy-start.1 = (f32[4,64,320]{2,1,0:T(8,128)S(1)}, f32[4,64,320]{2,1,0:T(8,128)}, u32[]{:S(2)}) copy-start(f32[4,64,320]{2,1,0:T(8,128)} %copy-done) | copy-start | bytes 983044
  110.2 9.8 %copy-start.41 = (pred[4]{0:T(512)(128)(4,1)S(1)}, pred[4]{0:T(512)(128)(4,1)}, u32[]{:S(2)}) copy-start(pred[4]{0:T(512)(128)(4,1)} %compare_and_fusion.6) | copy-start | bytes 16
  110.3 6.4 %collective-permute-start.12 = (f32[1,64,320]{2,1,0:T(8,128)S(1)}, f32[1,64,320]{2,1,0:T(8,128)S(1)}, u32[]{:S(2)}, u32[]{:S(2)}) collective-permute-start(f32[1,64,320]{2,1,0:T(8,128)S(1)} %get-tuple-element.43), channel_id=1, source_target_pairs={{0,4},{4,8},{8,12},{12,16},{16,20},{20,24},{24,28},{1,5},{5,9},{9,... | collective-permute-start | bytes 245768 | tf_op jit(solution)/shard_map/ppermute | solution.py:52
  113.5 6.5 %collective-permute-start.13 = (f32[1,64,320]{2,1,0:T(8,128)S(1)}, f32[1,64,320]{2,1,0:T(8,128)S(1)}, u32[]{:S(2)}, u32[]{:S(2)}) collective-permute-start(f32[1,64,320]{2,1,0:T(8,128)S(1)} %get-tuple-element.44), channel_id=1, source_target_pairs={{4,0},{8,4},{12,8},{16,12},{20,16},{24,20},{28,24},{5,1},{9,5},{13... | collective-permute-start | bytes 245768 | tf_op jit(solution)/shard_map/ppermute | solution.py:53
  120.6 6.9 %collective-permute-start.14 = (f32[1,64,320]{2,1,0:T(8,128)S(1)}, f32[1,64,320]{2,1,0:T(8,128)S(1)}, u32[]{:S(2)}, u32[]{:S(2)}) collective-permute-start(f32[1,64,320]{2,1,0:T(8,128)S(1)} %get-tuple-element.37), channel_id=1, source_target_pairs={{0,4},{4,8},{8,12},{12,16},{16,20},{20,24},{24,28},{1,5},{5,9},{9,... | collective-permute-start | bytes 245768 | tf_op jit(solution)/shard_map/ppermute | solution.py:52
  124.6 6.5 %collective-permute-start.15 = (f32[1,64,320]{2,1,0:T(8,128)S(1)}, f32[1,64,320]{2,1,0:T(8,128)S(1)}, u32[]{:S(2)}, u32[]{:S(2)}) collective-permute-start(f32[1,64,320]{2,1,0:T(8,128)S(1)} %get-tuple-element.38), channel_id=1, source_target_pairs={{4,0},{8,4},{12,8},{16,12},{20,16},{24,20},{28,24},{5,1},{9,5},{13... | collective-permute-start | bytes 245768 | tf_op jit(solution)/shard_map/ppermute | solution.py:53
  131.7 6.0 %collective-permute-start.16 = (f32[1,64,320]{2,1,0:T(8,128)S(1)}, f32[1,64,320]{2,1,0:T(8,128)S(1)}, u32[]{:S(2)}, u32[]{:S(2)}) collective-permute-start(f32[1,64,320]{2,1,0:T(8,128)S(1)} %get-tuple-element.33), channel_id=1, source_target_pairs={{0,4},{4,8},{8,12},{12,16},{16,20},{20,24},{24,28},{1,5},{5,9},{9,... | collective-permute-start | bytes 245768 | tf_op jit(solution)/shard_map/ppermute | solution.py:52
  134.5 6.5 %collective-permute-start.17 = (f32[1,64,320]{2,1,0:T(8,128)S(1)}, f32[1,64,320]{2,1,0:T(8,128)S(1)}, u32[]{:S(2)}, u32[]{:S(2)}) collective-permute-start(f32[1,64,320]{2,1,0:T(8,128)S(1)} %get-tuple-element.34), channel_id=1, source_target_pairs={{4,0},{8,4},{12,8},{16,12},{20,16},{24,20},{28,24},{5,1},{9,5},{13... | collective-permute-start | bytes 245768 | tf_op jit(solution)/shard_map/ppermute | solution.py:53
  136.0 5.2 %copy-start.5 = (f32[4,64,320]{2,1,0:T(8,128)S(1)}, f32[4,64,320]{2,1,0:T(8,128)}, u32[]{:S(2)}) copy-start(f32[4,64,320]{2,1,0:T(8,128)} %copy-done.4) | copy-start | bytes 983044
  136.0 5.2 %copy-start.35 = (f32[4,64,320]{2,1,0:T(8,128)S(1)}, f32[4,64,320]{2,1,0:T(8,128)}, u32[]{:S(2)}) copy-start(f32[4,64,320]{2,1,0:T(8,128)} %get-tuple-element.4) | copy-start | bytes 983044
  (12 other events, 8.1 us)

commit v11 on v10

--- a/solution.py
+++ b/solution.py
@@ -130,6 +130,35 @@
     return jnp.concatenate([zero, values, zero], axis=0)
 
 
+def split_sweep(weights, field, target, target_halo):
+    parts, have = weights
+    depth = field.shape[0] - 2
+    cuts = [0, 1, depth - 1, depth] if depth >= 3 else [0, depth]
+    rows = []
+    for low, high in zip(cuts[:-1], cuts[1:]):
+        w_alt_lo, w_alt_hi, w_inc_lo, w_inc_hi, w_raan_lo, w_raan_hi, diagonal = (
+            trim(part, have, 0)[low:high] for part in parts
+        )
+        centre = field[low + 1:high + 1]
+        v_down, v_up = field[low:high], field[low + 2:high + 2]
+        zero_inc = jnp.zeros_like(centre[:, :1])
+        v_prev = jnp.concatenate([zero_inc, centre[:, :-1]], 1)
+        v_next = jnp.concatenate([centre[:, 1:], zero_inc], 1)
+        v_left, v_right = lane_shifts(centre)
+        beside = (
+            w_alt_lo * v_down
+            + w_alt_hi * v_up
+            + w_inc_lo * v_prev
+            + w_inc_hi * v_next
+            + w_raan_lo * v_left
+            + w_raan_hi * v_right
+        )
+        applied = diagonal * centre - beside
+        aim = trim(target, target_halo, 0)[low:high]
+        rows.append(centre + OMEGA * (aim - applied) / diagonal)
+    return jnp.concatenate(rows, axis=0)
+
+
 def first_sweep(weights, target, halo):
     diagonal = trim(weights[0][6], weights[1], halo)
     return OMEGA * target / diagonal
@@ -147,8 +176,8 @@
     source_x = first[:, 0]
     weights_one = make_weights(first[:, 1], wide_inc, wide_raan, 1.0, 0)
 
-    density = sweep(weights_one, source_x, 1, source_x, 1)
-    density = sweep(weights_one, alt_extend(density, 1), 1, source_x, 1)
+    density = split_sweep(weights_one, source_x, source_x, 1)
+    density = split_sweep(weights_one, alt_extend(density, 1), source_x, 1)
     applied, density = apply_op(weights_one, alt_extend(density, 1), 1)
     rhs_two = coarsen(wide_source - applied)
 
@@ -183,7 +212,7 @@
 
     density = density + refine(correction)
     for _ in range(SWEEPS):
-        density = sweep(weights_one, alt_extend(density, 1), 1, source_x, 1)
+        density = split_sweep(weights_one, alt_extend(density, 1), source_x, 1)
     applied, centre = apply_op(weights_one, alt_extend(density, 1), 1)
     scaled_residual = (wide_source - applied) / weights_one[0][6]
     keep = slice(halo_r, halo_r + length)

time: 144 us -> 144 us (level)
  the two profiles are of different devices: /device:TPU:0 before, /device:TPU:8 now
where the time goes in v11:
time: 144 us; the launch traced here: 141 us
  starting transfers between devices  55.4 us (38%)
  waiting for transfers between devices  40.3 us (28%)
  other arithmetic  20.6 us (14%)
  local copies, waits for them, and re-layouts  13.2 us (9%)
  matrix products  8.97 us (6%)
  between operations  2.43 us (2%)
    ppermute x8, starting transfers between devices, alt_extend(): below.insert(0, lax.ppermute(values[low:], 'alt', up))  27.2 us
    ppermute x8, starting transfers between devices, alt_extend(): above.append(lax.ppermute(values[:high], 'alt', down))  20.9 us
    ppermute x8, waiting for transfers between devices, alt_extend(): above.append(lax.ppermute(values[:high], 'alt', down))  14.6 us
    ppermute x8, waiting for transfers between devices, alt_extend(): below.insert(0, lax.ppermute(values[low:], 'alt', up))  12.9 us
    ppermute x1, waiting for transfers between devices, raan_extend(): before = lax.ppermute(values[..., length - halo:], 'raan', up)  6.74 us
    dot_general x8, matrix products, coarsen(): summed = jnp.matmul(summed, pairing(length), precision=HIGH)  6.46 us
    all_to_all x1, starting transfers between devices, spread_gather(): every = lax.all_to_all(copies, 'alt', 0, 0)  5.55 us
    all_to_all x1, waiting for transfers between devices, spread_gather(): every = lax.all_to_all(copies, 'alt', 0, 0)  5.2 us
  transfers between devices with their start and end apart: 19, of which 13 were waited for; matrix products, arithmetic and copies ran while one was open for 12% of the time, Pallas kernels for 0%

profile of v11, /device:TPU:8, one launch (start us, length us, event | category | flops | bytes accessed | tf_op | source)
XLA Modules:
  0.0 140.9 jit_solution(15344265000995655392)
XLA Ops:
  0.6 1.3 pad_maximum_fusion.1
  2.2 1.7 %collective-permute-start.1 = (f32[4,4,64,32]{3,2,0,1:T(8,128)S(1)}, f32[4,4,64,32]{3,2,0,1:T(8,128)S(1)}, u32[]{:S(2)}, u32[]{:S(2)}) collective-permute-start(f32[4,4,64,32]{3,2,0,1:T(8,128)S(1)} %get-tuple-element.32), channel_id=1, source_target_pairs={{1,0},{2,1},{3,2},{0,3},{5,4},{6,5},{7,6},{4,7},{9,8},{10,9},{11,1... | collective-permute-start | bytes 393224 | tf_op jit(solution)/shard_map/ppermute | solution.py:40
  4.0 0.5 iota_shift-right-logical_fusion.2
  5.0 0.5 compare_and_fusion
  5.5 0.5 fusion.320
  6.1 0.6 iota_shift-right-logical_fusion.1
  6.7 0.6 compare_and_fusion.2
  7.3 0.6 iota_shift-right-logical_fusion
  7.8 6.7 %collective-permute-done = f32[4,4,64,32]{3,2,0,1:T(8,128)S(1)} collective-permute-done((f32[4,4,64,32]{3,2,0,1:T(8,128)S(1)}, f32[4,4,64,32]{3,2,0,1:T(8,128)S(1)}, u32[]{:S(2)}, u32[]{:S(2)}) %collective-permute-start) | collective-permute-done | bytes 131104 | tf_op jit(solution)/shard_map/ppermute | solution.py:39
  14.6 0.9 collective-permute-done.1
  15.6 0.8 fusion.377
  16.4 0.7 fusion.376
  17.1 0.7 fusion.381
  17.9 0.7 fusion.380
  18.6 0.6 pad_maximum_fusion
  19.2 0.8 fusion.366
  20.0 0.8 fusion.367
  20.8 0.8 slice_bitcast_fusion.11
  21.6 1.0 slice_bitcast_fusion
  22.6 3.4 %collective-permute-start.2 = (f32[1,2,64,320]{3,2,1,0:T(8,128)}, f32[1,2,64,320]{3,2,1,0:T(8,128)}, u32[]{:S(2)}, u32[]{:S(2)}) collective-permute-start(f32[1,2,64,320]{3,2,1,0:T(8,128)} %get-tuple-element.27), channel_id=1, source_target_pairs={{0,4},{4,8},{8,12},{12,16},{16,20},{20,24},{24,28},{1,5},{5,9},{9,... | collective-permute-start | bytes 491528 | tf_op jit(solution)/shard_map/ppermute | solution.py:52
  26.0 3.3 %collective-permute-start.3 = (f32[1,2,64,320]{3,2,1,0:T(8,128)}, f32[1,2,64,320]{3,2,1,0:T(8,128)}, u32[]{:S(2)}, u32[]{:S(2)}) collective-permute-start(f32[1,2,64,320]{3,2,1,0:T(8,128)} %get-tuple-element.28), channel_id=1, source_target_pairs={{4,0},{8,4},{12,8},{16,12},{20,16},{24,20},{28,24},{5,1},{9,5},{13... | collective-permute-start | bytes 491528 | tf_op jit(solution)/shard_map/ppermute | solution.py:53
  29.3 0.7 reduce_sum.75
  30.1 1.4 fusion.331
  31.5 1.1 fusion.335
  32.6 1.1 fusion.333
  34.3 1.0 fusion.201
  35.3 0.9 fusion.203
  37.0 0.5 collective-permute-done.3
  37.6 1.4 fusion.22
  39.3 1.1 fusion.198
  40.4 2.6 %collective-permute-start.5 = (f32[1,64,320]{2,1,0:T(8,128)S(1)}, f32[1,64,320]{2,1,0:T(8,128)S(1)}, u32[]{:S(2)}, u32[]{:S(2)}) collective-permute-start(f32[1,64,320]{2,1,0:T(8,128)S(1)} %fusion.198), channel_id=1, source_target_pairs={{4,0},{8,4},{12,8},{16,12},{20,16},{24,20},{28,24},{5,1},{9,5},{13... | collective-permute-start | bytes 245768 | tf_op jit(solution)/shard_map/ppermute | solution.py:53
  43.2 1.1 fusion.186
  44.3 3.3 %collective-permute-start.4 = (f32[1,64,320]{2,1,0:T(8,128)S(1)}, f32[1,64,320]{2,1,0:T(8,128)S(1)}, u32[]{:S(2)}, u32[]{:S(2)}) collective-permute-start(f32[1,64,320]{2,1,0:T(8,128)S(1)} %fusion.186), channel_id=1, source_target_pairs={{0,4},{4,8},{8,12},{12,16},{16,20},{20,24},{24,28},{1,5},{5,9},{9,... | collective-permute-start | bytes 245768 | tf_op jit(solution)/shard_map/ppermute | solution.py:52
  48.4 3.4 %collective-permute-done.4 = f32[1,64,320]{2,1,0:T(8,128)S(1)} collective-permute-done((f32[1,64,320]{2,1,0:T(8,128)S(1)}, f32[1,64,320]{2,1,0:T(8,128)S(1)}, u32[]{:S(2)}, u32[]{:S(2)}) %collective-permute-start.4) | collective-permute-done | bytes 81952 | tf_op jit(solution)/shard_map/ppermute | solution.py:52
  51.9 1.9 %collective-permute-start.7 = (f32[1,64,320]{2,1,0:T(8,128)S(1)}, f32[1,64,320]{2,1,0:T(8,128)S(1)}, u32[]{:S(2)}, u32[]{:S(2)}) collective-permute-start(f32[1,64,320]{2,1,0:T(8,128)S(1)} %fusion.175), channel_id=1, source_target_pairs={{4,0},{8,4},{12,8},{16,12},{20,16},{24,20},{28,24},{5,1},{9,5},{13... | collective-permute-start | bytes 245768 | tf_op jit(solution)/shard_map/ppermute | solution.py:53
  54.0 3.9 %collective-permute-start.6 = (f32[1,64,320]{2,1,0:T(8,128)S(1)}, f32[1,64,320]{2,1,0:T(8,128)S(1)}, u32[]{:S(2)}, u32[]{:S(2)}) collective-permute-start(f32[1,64,320]{2,1,0:T(8,128)S(1)} %fusion.165), channel_id=1, source_target_pairs={{0,4},{4,8},{8,12},{12,16},{16,20},{20,24},{24,28},{1,5},{5,9},{9,... | collective-permute-start | bytes 245768 | tf_op jit(solution)/shard_map/ppermute | solution.py:52
  58.4 3.0 %collective-permute-done.6 = f32[1,64,320]{2,1,0:T(8,128)S(1)} collective-permute-done((f32[1,64,320]{2,1,0:T(8,128)S(1)}, f32[1,64,320]{2,1,0:T(8,128)S(1)}, u32[]{:S(2)}, u32[]{:S(2)}) %collective-permute-start.6) | collective-permute-done | bytes 81952 | tf_op jit(solution)/shard_map/ppermute | solution.py:52
  62.8 3.8 %collective-permute-start.8 = (f32[2,4,32,160]{3,2,0,1:T(8,128)S(1)}, f32[2,4,32,160]{3,2,0,1:T(8,128)S(1)}, u32[]{:S(2)}, u32[]{:S(2)}) collective-permute-start(f32[2,4,32,160]{3,2,0,1:T(8,128)S(1)} %pad_maximum_fusion.17), channel_id=1, source_target_pairs={{0,8},{4,12},{8,16},{12,20},{16,24},{20,28},{1,9},{5,13},{9,17},{1... | collective-permute-start | bytes 491528 | tf_op jit(solution)/shard_map/ppermute | solution.py:52
  66.7 2.5 %collective-permute-start.9 = (f32[2,4,32,160]{3,2,0,1:T(8,128)S(1)}, f32[2,4,32,160]{3,2,0,1:T(8,128)S(1)}, u32[]{:S(2)}, u32[]{:S(2)}) collective-permute-start(f32[2,4,32,160]{3,2,0,1:T(8,128)S(1)} %pad_maximum_fusion.17), channel_id=1, source_target_pairs={{0,4},{4,8},{8,12},{12,16},{16,20},{20,24},{24,28},{1,5},{5,9},{9,... | collective-permute-start | bytes 491528 | tf_op jit(solution)/shard_map/ppermute | solution.py:52
  69.4 2.6 %collective-permute-start.11 = (f32[2,4,32,160]{3,2,0,1:T(8,128)S(1)}, f32[2,4,32,160]{3,2,0,1:T(8,128)S(1)}, u32[]{:S(2)}, u32[]{:S(2)}) collective-permute-start(f32[2,4,32,160]{3,2,0,1:T(8,128)S(1)} %pad_maximum_fusion.17), channel_id=1, source_target_pairs={{8,0},{12,4},{16,8},{20,12},{24,16},{28,20},{9,1},{13,5},{17,9},{2... | collective-permute-start | bytes 491528 | tf_op jit(solution)/shard_map/ppermute | solution.py:53
  71.9 2.9 %collective-permute-start.10 = (f32[2,4,32,160]{3,2,0,1:T(8,128)S(1)}, f32[2,4,32,160]{3,2,0,1:T(8,128)S(1)}, u32[]{:S(2)}, u32[]{:S(2)}) collective-permute-start(f32[2,4,32,160]{3,2,0,1:T(8,128)S(1)} %pad_maximum_fusion.17), channel_id=1, source_target_pairs={{4,0},{8,4},{12,8},{16,12},{20,16},{24,20},{28,24},{5,1},{9,5},{13... | collective-permute-start | bytes 491528 | tf_op jit(solution)/shard_map/ppermute | solution.py:53
  74.9 2.4 %collective-permute-done.9 = f32[2,4,32,160]{3,2,0,1:T(8,128)S(1)} collective-permute-done((f32[2,4,32,160]{3,2,0,1:T(8,128)S(1)}, f32[2,4,32,160]{3,2,0,1:T(8,128)S(1)}, u32[]{:S(2)}, u32[]{:S(2)}) %collective-permute-start.9) | collective-permute-done | bytes 163872 | tf_op jit(solution)/shard_map/ppermute | solution.py:52
  77.4 5.3 %collective-permute-done.10 = f32[2,4,32,160]{3,2,0,1:T(8,128)S(1)} collective-permute-done((f32[2,4,32,160]{3,2,0,1:T(8,128)S(1)}, f32[2,4,32,160]{3,2,0,1:T(8,128)S(1)}, u32[]{:S(2)}, u32[]{:S(2)}) %collective-permute-start.10) | collective-permute-done | bytes 163872 | tf_op jit(solution)/shard_map/ppermute | solution.py:53
  85.3 0.7 broadcast_in_dim.20
  86.1 5.6 %all-to-all-start = ((f32[8,1,4,16,80]{4,3,2,1,0:T(8,128)}), f32[8,1,4,16,80]{4,3,2,1,0:T(8,128)}, u32[]{:S(2)}, u32[]{:S(2)}) async-start(f32[8,1,4,16,80]{4,3,2,1,0:T(8,128)} %broadcast_in_dim.20), calls=%async_computation | async-start | bytes 524288 | tf_op jit(solution)/shard_map/all_to_all | solution.py:60
  91.6 0.5 compare_and_fusion.3
  92.1 0.6 compare_and_fusion.4
  92.7 5.2 %all-to-all-done = f32[8,1,4,16,80]{4,3,2,1,0:T(8,128)} async-done(((f32[8,1,4,16,80]{4,3,2,1,0:T(8,128)}), f32[8,1,4,16,80]{4,3,2,1,0:T(8,128)}, u32[]{:S(2)}, u32[]{:S(2)}) %all-to-all-start) | async-done | bytes 163872 | tf_op jit(solution)/shard_map/all_to_all | solution.py:60
  97.9 0.9 slice_bitcast_fusion.20
  98.9 1.0 fusion.278
  100.1 0.9 fusion.221
  101.1 0.9 fusion.233
  102.3 1.1 fusion.245
  106.1 0.7 copy-done.3
  107.2 3.5 %collective-permute-start.12 = (f32[1,64,320]{2,1,0:T(8,128)S(1)}, f32[1,64,320]{2,1,0:T(8,128)S(1)}, u32[]{:S(2)}, u32[]{:S(2)}) collective-permute-start(f32[1,64,320]{2,1,0:T(8,128)S(1)} %slice.1291), channel_id=1, source_target_pairs={{0,4},{4,8},{8,12},{12,16},{16,20},{20,24},{24,28},{1,5},{5,9},{9,... | collective-permute-start | bytes 245768 | tf_op jit(solution)/shard_map/ppermute | solution.py:52
  110.8 4.0 %collective-permute-done.12 = f32[1,64,320]{2,1,0:T(8,128)S(1)} collective-permute-done((f32[1,64,320]{2,1,0:T(8,128)S(1)}, f32[1,64,320]{2,1,0:T(8,128)S(1)}, u32[]{:S(2)}, u32[]{:S(2)}) %collective-permute-start.12) | collective-permute-done | bytes 81952 | tf_op jit(solution)/shard_map/ppermute | solution.py:52
  114.9 2.5 %collective-permute-start.15 = (f32[1,64,320]{2,1,0:T(8,128)S(1)}, f32[1,64,320]{2,1,0:T(8,128)S(1)}, u32[]{:S(2)}, u32[]{:S(2)}) collective-permute-start(f32[1,64,320]{2,1,0:T(8,128)S(1)} %get-tuple-element.37), channel_id=1, source_target_pairs={{4,0},{8,4},{12,8},{16,12},{20,16},{24,20},{28,24},{5,1},{9,5},{13... | collective-permute-start | bytes 245768 | tf_op jit(solution)/shard_map/ppermute | solution.py:53
  117.4 1.9 %collective-permute-start.13 = (f32[1,64,320]{2,1,0:T(8,128)S(1)}, f32[1,64,320]{2,1,0:T(8,128)S(1)}, u32[]{:S(2)}, u32[]{:S(2)}) collective-permute-start(f32[1,64,320]{2,1,0:T(8,128)S(1)} %get-tuple-element.38), channel_id=1, source_target_pairs={{4,0},{8,4},{12,8},{16,12},{20,16},{24,20},{28,24},{5,1},{9,5},{13... | collective-permute-start | bytes 245768 | tf_op jit(solution)/shard_map/ppermute | solution.py:53
  119.4 5.6 %collective-permute-done.13 = f32[1,64,320]{2,1,0:T(8,128)S(1)} collective-permute-done((f32[1,64,320]{2,1,0:T(8,128)S(1)}, f32[1,64,320]{2,1,0:T(8,128)S(1)}, u32[]{:S(2)}, u32[]{:S(2)}) %collective-permute-start.13) | collective-permute-done | bytes 81952 | tf_op jit(solution)/shard_map/ppermute | solution.py:53
  125.1 3.3 %collective-permute-start.14 = (f32[1,64,320]{2,1,0:T(8,128)S(1)}, f32[1,64,320]{2,1,0:T(8,128)S(1)}, u32[]{:S(2)}, u32[]{:S(2)}) collective-permute-start(f32[1,64,320]{2,1,0:T(8,128)S(1)} %fusion.145), channel_id=1, source_target_pairs={{0,4},{4,8},{8,12},{12,16},{16,20},{20,24},{24,28},{1,5},{5,9},{9,... | collective-permute-start | bytes 245768 | tf_op jit(solution)/shard_map/ppermute | solution.py:52
  128.7 3.4 %collective-permute-start.16 = (f32[1,64,320]{2,1,0:T(8,128)S(1)}, f32[1,64,320]{2,1,0:T(8,128)S(1)}, u32[]{:S(2)}, u32[]{:S(2)}) collective-permute-start(f32[1,64,320]{2,1,0:T(8,128)S(1)} %fusion.125), channel_id=1, source_target_pairs={{0,4},{4,8},{8,12},{12,16},{16,20},{20,24},{24,28},{1,5},{5,9},{9,... | collective-permute-start | bytes 245768 | tf_op jit(solution)/shard_map/ppermute | solution.py:52
  132.7 3.2 %collective-permute-start.17 = (f32[1,64,320]{2,1,0:T(8,128)S(1)}, f32[1,64,320]{2,1,0:T(8,128)S(1)}, u32[]{:S(2)}, u32[]{:S(2)}) collective-permute-start(f32[1,64,320]{2,1,0:T(8,128)S(1)} %fusion.135), channel_id=1, source_target_pairs={{4,0},{8,4},{12,8},{16,12},{20,16},{24,20},{28,24},{5,1},{9,5},{13... | collective-permute-start | bytes 245768 | tf_op jit(solution)/shard_map/ppermute | solution.py:53
  136.2 3.0 %collective-permute-done.17 = f32[1,64,320]{2,1,0:T(8,128)S(1)} collective-permute-done((f32[1,64,320]{2,1,0:T(8,128)S(1)}, f32[1,64,320]{2,1,0:T(8,128)S(1)}, u32[]{:S(2)}, u32[]{:S(2)}) %collective-permute-start.17) | collective-permute-done | bytes 81952 | tf_op jit(solution)/shard_map/ppermute | solution.py:53
  139.4 1.6 %fusion.30 = (f32[4,64,256]{2,1,0:T(8,128)}, f32[4,64,256]{2,1,0:T(8,128)}) fusion(f32[4,63,320]{2,1,0:T(8,128)S(1)} %fusion.4, f32[4,63,320]{2,1,0:T(8,128)S(1)} %get-tuple-element.34, f32[4,64,320]{2,1,0:T(8,128)S(1)} %copy-done.53, f32[4,64,319]{2,1,0:T(8,128)S(1)} %get-tuple-element.36, f32[4,64,320]{2,1,0:T(8,128)S(1)} %get-tuple-element.18, ...), kind=kLoop, calls=%fused_computation.66 | loop fusion | flops 655360 | bytes 3395584 | tf_op jit(solution)/shard_map/div | solution.py:217
  (272 shorter events, 12.9 us)
Async XLA Ops:
  1.9 13.5 %copy-start.14 = (f32[4,64,256]{2,1,0:T(8,128)S(1)}, f32[4,64,256]{2,1,0:T(8,128)}, u32[]{:S(2)}) copy-start(f32[4,64,256]{2,1,0:T(8,128)} %param.7) | copy-start | bytes 786436
  1.9 13.5 %copy-start.16 = (f32[4,64,256]{2,1,0:T(8,128)S(1)}, f32[4,64,256]{2,1,0:T(8,128)}, u32[]{:S(2)}) copy-start(f32[4,64,256]{2,1,0:T(8,128)} %param.6) | copy-start | bytes 786436
  1.9 13.5 %copy-start.18 = (f32[4,64,256]{2,1,0:T(8,128)S(1)}, f32[4,64,256]{2,1,0:T(8,128)}, u32[]{:S(2)}) copy-start(f32[4,64,256]{2,1,0:T(8,128)} %param.5) | copy-start | bytes 786436
  2.0 13.5 %copy-start.20 = (f32[4,64,256]{2,1,0:T(8,128)S(1)}, f32[4,64,256]{2,1,0:T(8,128)}, u32[]{:S(2)}) copy-start(f32[4,64,256]{2,1,0:T(8,128)} %param.4) | copy-start | bytes 786436
  2.2 12.4 %collective-permute-start = (f32[4,4,64,32]{3,2,0,1:T(8,128)S(1)}, f32[4,4,64,32]{3,2,0,1:T(8,128)S(1)}, u32[]{:S(2)}, u32[]{:S(2)}) collective-permute-start(f32[4,4,64,32]{3,2,0,1:T(8,128)S(1)} %get-tuple-element.31), channel_id=1, source_target_pairs={{0,1},{1,2},{2,3},{3,0},{4,5},{5,6},{6,7},{7,4},{8,9},{9,10},{10,1... | collective-permute-start | bytes 393224 | tf_op jit(solution)/shard_map/ppermute | solution.py:39
  2.2 13.2 %collective-permute-start.1 = (f32[4,4,64,32]{3,2,0,1:T(8,128)S(1)}, f32[4,4,64,32]{3,2,0,1:T(8,128)S(1)}, u32[]{:S(2)}, u32[]{:S(2)}) collective-permute-start(f32[4,4,64,32]{3,2,0,1:T(8,128)S(1)} %get-tuple-element.32), channel_id=1, source_target_pairs={{1,0},{2,1},{3,2},{0,3},{5,4},{6,5},{7,6},{4,7},{9,8},{10,9},{11,1... | collective-permute-start | bytes 393224 | tf_op jit(solution)/shard_map/ppermute | solution.py:40
  7.8 10.7 %copy-start.21 = (f32[4,64,256]{2,1,0:T(8,128)S(1)}, f32[4,64,256]{2,1,0:T(8,128)}, u32[]{:S(2)}) copy-start(f32[4,64,256]{2,1,0:T(8,128)} %param.4) | copy-start | bytes 786436
  14.6 4.0 %copy-start.4 = (f32[4,4,64,32]{3,2,0,1:T(8,128)}, f32[4,4,64,32]{3,2,0,1:T(8,128)S(1)}, u32[]{:S(2)}) copy-start(f32[4,4,64,32]{3,2,0,1:T(8,128)S(1)} %collective-permute-done) | copy-start | bytes 393220
  15.5 3.1 %copy-start.6 = (f32[4,4,64,32]{3,2,0,1:T(8,128)}, f32[4,4,64,32]{3,2,0,1:T(8,128)S(1)}, u32[]{:S(2)}) copy-start(f32[4,4,64,32]{3,2,0,1:T(8,128)S(1)} %collective-permute-done.1) | copy-start | bytes 393220
  15.6 2.2 %copy-start.8 = (f32[1,64,320]{2,1,0:T(8,128)}, f32[1,64,320]{2,1,0:T(8,128)S(1)}, u32[]{:S(2)}) copy-start(f32[1,64,320]{2,1,0:T(8,128)S(1)} %get-tuple-element.19) | copy-start | bytes 245764
  15.6 2.2 %copy-start.11 = (f32[1,64,320]{2,1,0:T(8,128)}, f32[1,64,320]{2,1,0:T(8,128)S(1)}, u32[]{:S(2)}) copy-start(f32[1,64,320]{2,1,0:T(8,128)S(1)} %get-tuple-element.20) | copy-start | bytes 245764
  22.6 14.4 %collective-permute-start.2 = (f32[1,2,64,320]{3,2,1,0:T(8,128)}, f32[1,2,64,320]{3,2,1,0:T(8,128)}, u32[]{:S(2)}, u32[]{:S(2)}) collective-permute-start(f32[1,2,64,320]{3,2,1,0:T(8,128)} %get-tuple-element.27), channel_id=1, source_target_pairs={{0,4},{4,8},{8,12},{12,16},{16,20},{20,24},{24,28},{1,5},{5,9},{9,... | collective-permute-start | bytes 491528 | tf_op jit(solution)/shard_map/ppermute | solution.py:52
  26.0 11.5 %collective-permute-start.3 = (f32[1,2,64,320]{3,2,1,0:T(8,128)}, f32[1,2,64,320]{3,2,1,0:T(8,128)}, u32[]{:S(2)}, u32[]{:S(2)}) collective-permute-start(f32[1,2,64,320]{3,2,1,0:T(8,128)} %get-tuple-element.28), channel_id=1, source_target_pairs={{4,0},{8,4},{12,8},{16,12},{20,16},{24,20},{28,24},{5,1},{9,5},{13... | collective-permute-start | bytes 491528 | tf_op jit(solution)/shard_map/ppermute | solution.py:53
  33.9 49.6 %copy-start.41 = (f32[32,2,160]{2,0,1:T(8,128)}, f32[32,2,160]{2,0,1:T(8,128)S(1)}, u32[]{:S(2)}) copy-start(f32[32,2,160]{2,0,1:T(8,128)S(1)} %get-tuple-element.129) | copy-start | bytes 122884
  34.1 49.4 %copy-start.43 = (f32[32,2,160]{2,0,1:T(8,128)}, f32[32,2,160]{2,0,1:T(8,128)S(1)}, u32[]{:S(2)}) copy-start(f32[32,2,160]{2,0,1:T(8,128)S(1)} %get-tuple-element.131) | copy-start | bytes 122884
  34.3 49.3 %copy-start.45 = (f32[32,2,160]{2,0,1:T(8,128)}, f32[32,2,160]{2,0,1:T(8,128)S(1)}, u32[]{:S(2)}) copy-start(f32[32,2,160]{2,0,1:T(8,128)S(1)} %get-tuple-element.133) | copy-start | bytes 122884
  34.3 2.2 %copy-start.74 = (s32[160]{0:T(256)S(1)}, s32[160]{0:T(256)}, u32[]{:S(2)}) copy-start(s32[160]{0:T(256)} %get-tuple-element.138) | copy-start | bytes 1924
  34.3 2.2 %copy-start.76 = (s32[160]{0:T(256)S(1)}, s32[160]{0:T(256)}, u32[]{:S(2)}) copy-start(s32[160]{0:T(256)} %get-tuple-element.139) | copy-start | bytes 1924
  34.3 2.2 %copy-start.83 = (pred[160]{0:T(512)(128)(4,1)S(1)}, pred[160]{0:T(512)(128)(4,1)}, u32[]{:S(2)}) copy-start(pred[160]{0:T(512)(128)(4,1)} %compare_and_fusion) | copy-start | bytes 484
  39.0 14.8 %copy-start.2 = (f32[4,64,320]{2,1,0:T(8,128)}, f32[4,64,320]{2,1,0:T(8,128)S(1)}, u32[]{:S(2)}) copy-start(f32[4,64,320]{2,1,0:T(8,128)S(1)} %get-tuple-element.14) | copy-start | bytes 983044
  39.3 3.8 %copy-start.12 = (f32[1,64,320]{2,1,0:T(8,128)S(1)}, f32[1,64,320]{2,1,0:T(8,128)}, u32[]{:S(2)}) copy-start(f32[1,64,320]{2,1,0:T(8,128)} %copy-done.11) | copy-start | bytes 245764
  39.3 3.8 %copy-start.58 = (f32[1,64,319]{2,1,0:T(8,128)S(1)}, f32[1,64,319]{2,1,0:T(8,128)}, u32[]{:S(2)}) copy-start(f32[1,64,319]{2,1,0:T(8,128)} %get-tuple-element.112) | copy-start | bytes 244996
  39.3 3.8 %copy-start.59 = (f32[1,64,319]{2,1,0:T(8,128)S(1)}, f32[1,64,319]{2,1,0:T(8,128)}, u32[]{:S(2)}) copy-start(f32[1,64,319]{2,1,0:T(8,128)} %get-tuple-element.113) | copy-start | bytes 244996
  39.3 3.8 %copy-start.60 = (f32[1,63,320]{2,1,0:T(8,128)S(1)}, f32[1,63,320]{2,1,0:T(8,128)}, u32[]{:S(2)}) copy-start(f32[1,63,320]{2,1,0:T(8,128)} %get-tuple-element.110) | copy-start | bytes 241924
  39.3 3.8 %copy-start.61 = (f32[1,63,320]{2,1,0:T(8,128)S(1)}, f32[1,63,320]{2,1,0:T(8,128)}, u32[]{:S(2)}) copy-start(f32[1,63,320]{2,1,0:T(8,128)} %get-tuple-element.111) | copy-start | bytes 241924
  40.4 13.4 %collective-permute-start.5 = (f32[1,64,320]{2,1,0:T(8,128)S(1)}, f32[1,64,320]{2,1,0:T(8,128)S(1)}, u32[]{:S(2)}, u32[]{:S(2)}) collective-permute-start(f32[1,64,320]{2,1,0:T(8,128)S(1)} %fusion.198), channel_id=1, source_target_pairs={{4,0},{8,4},{12,8},{16,12},{20,16},{24,20},{28,24},{5,1},{9,5},{13... | collective-permute-start | bytes 245768 | tf_op jit(solution)/shard_map/ppermute | solution.py:53
  43.1 4.6 %copy-start.54 = (f32[2,63,320]{2,1,0:T(8,128)S(1)}, f32[2,63,320]{2,1,0:T(8,128)}, u32[]{:S(2)}) copy-start(f32[2,63,320]{2,1,0:T(8,128)} %get-tuple-element.82) | copy-start | bytes 483844
  43.1 4.6 %copy-start.55 = (f32[2,63,320]{2,1,0:T(8,128)S(1)}, f32[2,63,320]{2,1,0:T(8,128)}, u32[]{:S(2)}) copy-start(f32[2,63,320]{2,1,0:T(8,128)} %get-tuple-element.83) | copy-start | bytes 483844
  43.2 4.6 %copy-start.56 = (f32[2,64,319]{2,1,0:T(8,128)S(1)}, f32[2,64,319]{2,1,0:T(8,128)}, u32[]{:S(2)}) copy-start(f32[2,64,319]{2,1,0:T(8,128)} %get-tuple-element.84) | copy-start | bytes 489988
  43.2 4.6 %copy-start.57 = (f32[2,64,319]{2,1,0:T(8,128)S(1)}, f32[2,64,319]{2,1,0:T(8,128)}, u32[]{:S(2)}) copy-start(f32[2,64,319]{2,1,0:T(8,128)} %get-tuple-element.85) | copy-start | bytes 489988
  44.3 7.5 %collective-permute-start.4 = (f32[1,64,320]{2,1,0:T(8,128)S(1)}, f32[1,64,320]{2,1,0:T(8,128)S(1)}, u32[]{:S(2)}, u32[]{:S(2)}) collective-permute-start(f32[1,64,320]{2,1,0:T(8,128)S(1)} %fusion.186), channel_id=1, source_target_pairs={{0,4},{4,8},{8,12},{12,16},{16,20},{20,24},{24,28},{1,5},{5,9},{9,... | collective-permute-start | bytes 245768 | tf_op jit(solution)/shard_map/ppermute | solution.py:52
  48.4 13.0 %copy-start.39 = (f32[2,64,320]{2,1,0:T(8,128)}, f32[2,64,320]{2,1,0:T(8,128)S(1)}, u32[]{:S(2)}) copy-start(f32[2,64,320]{2,1,0:T(8,128)S(1)} %fusion.87) | copy-start | bytes 491524
  51.9 9.5 %copy-start.49 = (f32[1,64,320]{2,1,0:T(8,128)}, f32[1,64,320]{2,1,0:T(8,128)S(1)}, u32[]{:S(2)}) copy-start(f32[1,64,320]{2,1,0:T(8,128)S(1)} %fusion.175) | copy-start | bytes 245764
  51.9 6.5 %collective-permute-start.7 = (f32[1,64,320]{2,1,0:T(8,128)S(1)}, f32[1,64,320]{2,1,0:T(8,128)S(1)}, u32[]{:S(2)}, u32[]{:S(2)}) collective-permute-start(f32[1,64,320]{2,1,0:T(8,128)S(1)} %fusion.175), channel_id=1, source_target_pairs={{4,0},{8,4},{12,8},{16,12},{20,16},{24,20},{28,24},{5,1},{9,5},{13... | collective-permute-start | bytes 245768 | tf_op jit(solution)/shard_map/ppermute | solution.py:53
  54.0 7.4 %copy-start.51 = (f32[1,64,320]{2,1,0:T(8,128)}, f32[1,64,320]{2,1,0:T(8,128)S(1)}, u32[]{:S(2)}) copy-start(f32[1,64,320]{2,1,0:T(8,128)S(1)} %fusion.165) | copy-start | bytes 245764
  54.0 7.4 %collective-permute-start.6 = (f32[1,64,320]{2,1,0:T(8,128)S(1)}, f32[1,64,320]{2,1,0:T(8,128)S(1)}, u32[]{:S(2)}, u32[]{:S(2)}) collective-permute-start(f32[1,64,320]{2,1,0:T(8,128)S(1)} %fusion.165), channel_id=1, source_target_pairs={{0,4},{4,8},{8,12},{12,16},{16,20},{20,24},{24,28},{1,5},{5,9},{9,... | collective-permute-start | bytes 245768 | tf_op jit(solution)/shard_map/ppermute | solution.py:52
  62.7 21.6 %copy-start.23 = (f32[32,2,160]{2,0,1:T(8,128)}, f32[32,2,160]{2,0,1:T(8,128)S(1)}, u32[]{:S(2)}) copy-start(f32[32,2,160]{2,0,1:T(8,128)S(1)} %convolution_multiply_fusion.3) | copy-start | bytes 122884
  62.8 12.1 %collective-permute-start.8 = (f32[2,4,32,160]{3,2,0,1:T(8,128)S(1)}, f32[2,4,32,160]{3,2,0,1:T(8,128)S(1)}, u32[]{:S(2)}, u32[]{:S(2)}) collective-permute-start(f32[2,4,32,160]{3,2,0,1:T(8,128)S(1)} %pad_maximum_fusion.17), channel_id=1, source_target_pairs={{0,8},{4,12},{8,16},{12,20},{16,24},{20,28},{1,9},{5,13},{9,17},{1... | collective-permute-start | bytes 491528 | tf_op jit(solution)/shard_map/ppermute | solution.py:52
  66.7 10.6 %collective-permute-start.9 = (f32[2,4,32,160]{3,2,0,1:T(8,128)S(1)}, f32[2,4,32,160]{3,2,0,1:T(8,128)S(1)}, u32[]{:S(2)}, u32[]{:S(2)}) collective-permute-start(f32[2,4,32,160]{3,2,0,1:T(8,128)S(1)} %pad_maximum_fusion.17), channel_id=1, source_target_pairs={{0,4},{4,8},{8,12},{12,16},{16,20},{20,24},{24,28},{1,5},{5,9},{9,... | collective-permute-start | bytes 491528 | tf_op jit(solution)/shard_map/ppermute | solution.py:52
  69.4 13.3 %collective-permute-start.11 = (f32[2,4,32,160]{3,2,0,1:T(8,128)S(1)}, f32[2,4,32,160]{3,2,0,1:T(8,128)S(1)}, u32[]{:S(2)}, u32[]{:S(2)}) collective-permute-start(f32[2,4,32,160]{3,2,0,1:T(8,128)S(1)} %pad_maximum_fusion.17), channel_id=1, source_target_pairs={{8,0},{12,4},{16,8},{20,12},{24,16},{28,20},{9,1},{13,5},{17,9},{2... | collective-permute-start | bytes 491528 | tf_op jit(solution)/shard_map/ppermute | solution.py:53
  71.9 10.7 %collective-permute-start.10 = (f32[2,4,32,160]{3,2,0,1:T(8,128)S(1)}, f32[2,4,32,160]{3,2,0,1:T(8,128)S(1)}, u32[]{:S(2)}, u32[]{:S(2)}) collective-permute-start(f32[2,4,32,160]{3,2,0,1:T(8,128)S(1)} %pad_maximum_fusion.17), channel_id=1, source_target_pairs={{4,0},{8,4},{12,8},{16,12},{20,16},{24,20},{28,24},{5,1},{9,5},{13... | collective-permute-start | bytes 491528 | tf_op jit(solution)/shard_map/ppermute | solution.py:53
  77.3 6.2 %copy-start.25 = (f32[2,4,32,160]{3,2,0,1:T(8,128)}, f32[2,4,32,160]{3,2,0,1:T(8,128)S(1)}, u32[]{:S(2)}) copy-start(f32[2,4,32,160]{3,2,0,1:T(8,128)S(1)} %collective-permute-done.9) | copy-start | bytes 491524
  86.1 11.9 %all-to-all-start = ((f32[8,1,4,16,80]{4,3,2,1,0:T(8,128)}), f32[8,1,4,16,80]{4,3,2,1,0:T(8,128)}, u32[]{:S(2)}, u32[]{:S(2)}) async-start(f32[8,1,4,16,80]{4,3,2,1,0:T(8,128)} %broadcast_in_dim.20), calls=%async_computation | async-start | bytes 524288 | tf_op jit(solution)/shard_map/all_to_all | solution.py:60
  100.0 3.4 %copy-start.75 = (s32[160]{0:T(256)S(1)}, s32[160]{0:T(256)}, u32[]{:S(2)}) copy-start(s32[160]{0:T(256)} %get-tuple-element.138) | copy-start | bytes 1924
  100.0 3.4 %copy-start.77 = (s32[160]{0:T(256)S(1)}, s32[160]{0:T(256)}, u32[]{:S(2)}) copy-start(s32[160]{0:T(256)} %get-tuple-element.139) | copy-start | bytes 1924
  100.0 3.4 %copy-start.84 = (pred[160]{0:T(512)(128)(4,1)S(1)}, pred[160]{0:T(512)(128)(4,1)}, u32[]{:S(2)}) copy-start(pred[160]{0:T(512)(128)(4,1)} %compare_and_fusion) | copy-start | bytes 484
  101.0 2.7 %copy-start.67 = (s32[32]{0:T(128)S(1)}, s32[32]{0:T(128)}, u32[]{:S(2)}) copy-start(s32[32]{0:T(128)} %iota_shift-right-logical_fusion.2) | copy-start | bytes 388
  101.0 2.7 %copy-start.69 = (pred[32]{0:T(512)(128)(4,1)S(1)}, pred[32]{0:T(512)(128)(4,1)}, u32[]{:S(2)}) copy-start(pred[32]{0:T(512)(128)(4,1)} %compare_and_fusion.1) | copy-start | bytes 100
  101.0 3.0 %copy-start.30 = (f32[6,32,160]{2,1,0:T(8,128)S(1)}, f32[6,32,160]{2,1,0:T(8,128)}, u32[]{:S(2)}) copy-start(f32[6,32,160]{2,1,0:T(8,128)} %copy-done.29) | copy-start | bytes 368644
  102.1 2.1 %copy-start.1 = (f32[8,31,160]{2,1,0:T(8,128)S(1)}, f32[8,31,160]{2,1,0:T(8,128)}, u32[]{:S(2)}) copy-start(f32[8,31,160]{2,1,0:T(8,128)} %copy-done) | copy-start | bytes 476164
  102.1 2.1 %copy-start.24 = (f32[32,2,160]{2,0,1:T(8,128)S(1)}, f32[32,2,160]{2,0,1:T(8,128)}, u32[]{:S(2)}) copy-start(f32[32,2,160]{2,0,1:T(8,128)} %copy-done.23) | copy-start | bytes 122884
  102.1 2.1 %copy-start.26 = (f32[2,4,32,160]{3,2,0,1:T(8,128)S(1)}, f32[2,4,32,160]{3,2,0,1:T(8,128)}, u32[]{:S(2)}) copy-start(f32[2,4,32,160]{3,2,0,1:T(8,128)} %copy-done.25) | copy-start | bytes 491524
  102.1 2.1 %copy-start.28 = (f32[2,4,32,160]{3,2,0,1:T(8,128)S(1)}, f32[2,4,32,160]{3,2,0,1:T(8,128)}, u32[]{:S(2)}) copy-start(f32[2,4,32,160]{3,2,0,1:T(8,128)} %copy-done.27) | copy-start | bytes 491524
  102.1 2.1 %copy-start.32 = (f32[8,1,32,160]{3,2,0,1:T(8,128)S(1)}, f32[8,1,32,160]{3,2,0,1:T(8,128)}, u32[]{:S(2)}) copy-start(f32[8,1,32,160]{3,2,0,1:T(8,128)} %copy-done.31) | copy-start | bytes 491524
  102.1 2.1 %copy-start.34 = (f32[8,1,32,160]{3,2,0,1:T(8,128)S(1)}, f32[8,1,32,160]{3,2,0,1:T(8,128)}, u32[]{:S(2)}) copy-start(f32[8,1,32,160]{3,2,0,1:T(8,128)} %copy-done.33) | copy-start | bytes 491524
  107.0 7.7 %copy-start.10 = (f32[1,64,320]{2,1,0:T(8,128)S(1)}, f32[1,64,320]{2,1,0:T(8,128)}, u32[]{:S(2)}) copy-start(f32[1,64,320]{2,1,0:T(8,128)} %copy-done.8) | copy-start | bytes 245764
  107.2 17.8 %copy-start.13 = (f32[1,64,320]{2,1,0:T(8,128)S(1)}, f32[1,64,320]{2,1,0:T(8,128)}, u32[]{:S(2)}) copy-start(f32[1,64,320]{2,1,0:T(8,128)} %copy-done.11) | copy-start | bytes 245764
  107.2 7.5 %collective-permute-start.12 = (f32[1,64,320]{2,1,0:T(8,128)S(1)}, f32[1,64,320]{2,1,0:T(8,128)S(1)}, u32[]{:S(2)}, u32[]{:S(2)}) collective-permute-start(f32[1,64,320]{2,1,0:T(8,128)S(1)} %slice.1291), channel_id=1, source_target_pairs={{0,4},{4,8},{8,12},{12,16},{16,20},{20,24},{24,28},{1,5},{5,9},{9,... | collective-permute-start | bytes 245768 | tf_op jit(solution)/shard_map/ppermute | solution.py:52
  114.9 13.7 %collective-permute-start.15 = (f32[1,64,320]{2,1,0:T(8,128)S(1)}, f32[1,64,320]{2,1,0:T(8,128)S(1)}, u32[]{:S(2)}, u32[]{:S(2)}) collective-permute-start(f32[1,64,320]{2,1,0:T(8,128)S(1)} %get-tuple-element.37), channel_id=1, source_target_pairs={{4,0},{8,4},{12,8},{16,12},{20,16},{24,20},{28,24},{5,1},{9,5},{13... | collective-permute-start | bytes 245768 | tf_op jit(solution)/shard_map/ppermute | solution.py:53
  117.4 7.6 %collective-permute-start.13 = (f32[1,64,320]{2,1,0:T(8,128)S(1)}, f32[1,64,320]{2,1,0:T(8,128)S(1)}, u32[]{:S(2)}, u32[]{:S(2)}) collective-permute-start(f32[1,64,320]{2,1,0:T(8,128)S(1)} %get-tuple-element.38), channel_id=1, source_target_pairs={{4,0},{8,4},{12,8},{16,12},{20,16},{24,20},{28,24},{5,1},{9,5},{13... | collective-permute-start | bytes 245768 | tf_op jit(solution)/shard_map/ppermute | solution.py:53
  125.1 7.4 %collective-permute-start.14 = (f32[1,64,320]{2,1,0:T(8,128)S(1)}, f32[1,64,320]{2,1,0:T(8,128)S(1)}, u32[]{:S(2)}, u32[]{:S(2)}) collective-permute-start(f32[1,64,320]{2,1,0:T(8,128)S(1)} %fusion.145), channel_id=1, source_target_pairs={{0,4},{4,8},{8,12},{12,16},{16,20},{20,24},{24,28},{1,5},{5,9},{9,... | collective-permute-start | bytes 245768 | tf_op jit(solution)/shard_map/ppermute | solution.py:52
  128.7 7.5 %collective-permute-start.16 = (f32[1,64,320]{2,1,0:T(8,128)S(1)}, f32[1,64,320]{2,1,0:T(8,128)S(1)}, u32[]{:S(2)}, u32[]{:S(2)}) collective-permute-start(f32[1,64,320]{2,1,0:T(8,128)S(1)} %fusion.125), channel_id=1, source_target_pairs={{0,4},{4,8},{8,12},{12,16},{16,20},{20,24},{24,28},{1,5},{5,9},{9,... | collective-permute-start | bytes 245768 | tf_op jit(solution)/shard_map/ppermute | solution.py:52
  132.7 6.5 %collective-permute-start.17 = (f32[1,64,320]{2,1,0:T(8,128)S(1)}, f32[1,64,320]{2,1,0:T(8,128)S(1)}, u32[]{:S(2)}, u32[]{:S(2)}) collective-permute-start(f32[1,64,320]{2,1,0:T(8,128)S(1)} %fusion.135), channel_id=1, source_target_pairs={{4,0},{8,4},{12,8},{16,12},{20,16},{24,20},{28,24},{5,1},{9,5},{13... | collective-permute-start | bytes 245768 | tf_op jit(solution)/shard_map/ppermute | solution.py:53
  136.2 3.2 %copy-start.53 = (f32[4,64,320]{2,1,0:T(8,128)S(1)}, f32[4,64,320]{2,1,0:T(8,128)}, u32[]{:S(2)}) copy-start(f32[4,64,320]{2,1,0:T(8,128)} %get-tuple-element.21) | copy-start | bytes 983044
  (40 other events, 53.9 us)

commit v12 on v11

--- a/solution.py
+++ b/solution.py
@@ -169,8 +169,7 @@
     halo_r = min(RAAN_HALO, length)
     wide = raan_extend(jnp.stack([source, k_alt, k_inc, k_raan], axis=1), halo_r)
     wide_source, wide_alt, wide_inc, wide_raan = (wide[:, i] for i in range(4))
-    coef_two = [coarsen(part) for part in (wide_alt, wide_inc, wide_raan)]
-    coef_three = [coarsen(part) for part in coef_two]
+    coef_column = spread_gather(jnp.stack([coarsen(part) for part in (wide_alt, wide_inc, wide_raan)], 1))
 
     first = alt_extend(wide[:, 0:2], 1)
     source_x = first[:, 0]
@@ -181,34 +180,25 @@
     applied, density = apply_op(weights_one, alt_extend(density, 1), 1)
     rhs_two = coarsen(wide_source - applied)
 
-    level_two = alt_extend(jnp.stack([rhs_two] + coef_two, 1), SWEEPS + 2)
-    weights_two = make_weights(
-        level_two[:, 1],
-        trim(level_two[:, 2], SWEEPS + 2, SWEEPS + 1),
-        trim(level_two[:, 3], SWEEPS + 2, SWEEPS + 1),
-        0.25,
-        SWEEPS + 1,
-    )
-    rhs_two_x = trim(level_two[:, 0], SWEEPS + 2, SWEEPS + 1)
-    correction = first_sweep(weights_two, rhs_two_x, SWEEPS + 1)
-    correction = sweep(weights_two, correction, SWEEPS + 1, rhs_two_x, SWEEPS + 1)
-    applied, _ = apply_op(weights_two, trim(correction, SWEEPS, 1), 1)
-    rhs_three = coarsen(trim(rhs_two_x, SWEEPS + 1, 0) - applied)
-
-    height = rhs_three.shape[0]
-    column = spread_gather(jnp.stack([rhs_three] + coef_three, 1))
-    weights_three = make_weights(pad_rows(column[:, 1]), column[:, 2], column[:, 3], 0.0625, 0)
-    rhs_three_x = column[:, 0]
+    height = rhs_two.shape[0]
+    rhs_two_x = spread_gather(rhs_two)
+    weights_two = make_weights(pad_rows(coef_column[:, 0]), coef_column[:, 1], coef_column[:, 2], 0.25, 0)
+    correction = first_sweep(weights_two, rhs_two_x, 0)
+    for _ in range(SWEEPS - 1):
+        correction = sweep(weights_two, pad_rows(correction), 1, rhs_two_x, 0, masked=False)
+    applied, _ = apply_op(weights_two, pad_rows(correction), 1)
+    rhs_three_x = coarsen(rhs_two_x - applied)
+
+    coef_three = [coarsen(coef_column[:, i]) for i in range(3)]
+    weights_three = make_weights(pad_rows(coef_three[0]), coef_three[1], coef_three[2], 0.0625, 0)
     coarse_part = first_sweep(weights_three, rhs_three_x, 0)
     for _ in range(COARSE_SWEEPS - 1):
         coarse_part = sweep(weights_three, pad_rows(coarse_part), 1, rhs_three_x, 0, masked=False)
-    reach = SWEEPS // 2
-    coarse_part = jnp.pad(coarse_part, ((reach, reach), (0, 0), (0, 0)))
-    coarse_part = lax.dynamic_slice_in_dim(coarse_part, lax.axis_index("alt") * height, height + 2 * reach, 0)
 
     correction = correction + refine(coarse_part)
-    for halo in range(SWEEPS, 0, -1):
-        correction = sweep(weights_two, correction, halo, rhs_two_x, SWEEPS + 1)
+    for _ in range(SWEEPS):
+        correction = sweep(weights_two, pad_rows(correction), 1, rhs_two_x, 0, masked=False)
+    correction = lax.dynamic_slice_in_dim(correction, lax.axis_index("alt") * height, height, 0)
 
     density = density + refine(correction)
     for _ in range(SWEEPS):

time: 144 us -> 169 us (1.17)
  waiting for transfers between devices: 40.3 us -> 55.9 us
  local copies, waits for them, and re-layouts: 13.2 us -> 19.1 us
  other arithmetic: 20.6 us -> 26 us
    ppermute x8 -> x6, waiting for transfers between devices: 12.9 us -> 29.1 us  [alt_extend(): below.insert(0, lax.ppermute(values[low:], 'alt', up))]
    all_to_all x1 -> x2, starting transfers between devices: 5.55 us -> 12.9 us  [spread_gather(): every = lax.all_to_all(copies, 'alt', 0, 0)]
    ppermute x8 -> x6, waiting for transfers between devices: 14.6 us -> 7.97 us  [alt_extend(): above.append(lax.ppermute(values[:high], 'alt', down))]
    reduce_sum x5 -> x8, other arithmetic: 1.37 us -> 6.56 us  [coarsen(): summed = values.reshape(depth // 2, 2, width, length).sum(axis=1)]
    ppermute x8 -> x6, starting transfers between devices: 27.2 us -> 22.3 us  [alt_extend(): below.insert(0, lax.ppermute(values[low:], 'alt', up))]
    ppermute x1, waiting for transfers between devices: 6.74 us -> 10.7 us  [raan_extend(): before = lax.ppermute(values[..., length - halo:], 'raan', up)]
    ppermute x8 -> x6, starting transfers between devices: 20.9 us -> 17.1 us  [alt_extend(): above.append(lax.ppermute(values[:high], 'alt', down))]
    add x2, other arithmetic: 1.61 us -> 3.63 us  [make_weights(): 1.0 + (w_alt_lo + w_alt_hi + w_inc_lo + w_inc_hi + w_raan_lo + w_raan_hi)]
  transfers between devices with their start and end apart: 19 -> 16, of which waited for: 13 -> 10; matrix products, arithmetic and copies ran while one was open for 12% -> 14% of each run, Pallas kernels for 0% -> 0%
where the time goes in v12:
time: 169 us; the launch traced here: 166 us
  waiting for transfers between devices  55.9 us (33%)
  starting transfers between devices  54 us (32%)
  other arithmetic  26 us (15%)
  local copies, waits for them, and re-layouts  19.1 us (11%)
  matrix products  9.04 us (5%)
  between operations  1.89 us (1%)
    ppermute x6, waiting for transfers between devices, alt_extend(): below.insert(0, lax.ppermute(values[low:], 'alt', up))  29.1 us
    ppermute x6, starting transfers between devices, alt_extend(): below.insert(0, lax.ppermute(values[low:], 'alt', up))  22.3 us
    ppermute x6, starting transfers between devices, alt_extend(): above.append(lax.ppermute(values[:high], 'alt', down))  17.1 us
    all_to_all x2, starting transfers between devices, spread_gather(): every = lax.all_to_all(copies, 'alt', 0, 0)  12.9 us
    ppermute x1, waiting for transfers between devices, raan_extend(): before = lax.ppermute(values[..., length - halo:], 'raan', up)  10.7 us
    ppermute x6, waiting for transfers between devices, alt_extend(): above.append(lax.ppermute(values[:high], 'alt', down))  7.97 us
    all_to_all x2, waiting for transfers between devices, spread_gather(): every = lax.all_to_all(copies, 'alt', 0, 0)  7.15 us
    reduce_sum x8, other arithmetic, coarsen(): summed = values.reshape(depth // 2, 2, width, length).sum(axis=1)  6.56 us
  transfers between devices with their start and end apart: 16, of which 10 were waited for; matrix products, arithmetic and copies ran while one was open for 14% of the time, Pallas kernels for 0%

profile of v12, /device:TPU:8, one launch (start us, length us, event | category | flops | bytes accessed | tf_op | source)
XLA Modules:
  0.0 166.0 jit_solution(11975229443016491631)
XLA Ops:
  0.6 1.3 pad_maximum_fusion.1
  2.0 1.1 fusion.317
  3.1 1.7 %collective-permute-start.1 = (f32[4,4,64,32]{3,2,0,1:T(8,128)}, f32[4,4,64,32]{3,2,0,1:T(8,128)S(1)}, u32[]{:S(2)}, u32[]{:S(2)}) collective-permute-start(f32[4,4,64,32]{3,2,0,1:T(8,128)} %get-tuple-element.36), channel_id=1, source_target_pairs={{1,0},{2,1},{3,2},{0,3},{5,4},{6,5},{7,6},{4,7},{9,8},{10,9},{11,1... | collective-permute-start | bytes 393224 | tf_op jit(solution)/shard_map/ppermute | solution.py:40
  4.9 10.7 %collective-permute-done = f32[4,4,64,32]{3,2,0,1:T(8,128)S(1)} collective-permute-done((f32[4,4,64,32]{3,2,0,1:T(8,128)}, f32[4,4,64,32]{3,2,0,1:T(8,128)S(1)}, u32[]{:S(2)}, u32[]{:S(2)}) %collective-permute-start) | collective-permute-done | bytes 131104 | tf_op jit(solution)/shard_map/ppermute | solution.py:39
  15.7 1.0 collective-permute-done.1
  16.8 0.7 fusion.349
  17.6 0.7 fusion.348
  18.3 1.6 pad_maximum_fusion
  19.9 0.8 fusion.340
  20.7 0.8 fusion.341
  21.5 0.8 slice_bitcast_fusion.7
  22.3 1.1 slice_bitcast_fusion
  23.4 0.7 fusion.353
  24.2 3.4 %collective-permute-start.2 = (f32[1,2,64,320]{3,2,1,0:T(8,128)}, f32[1,2,64,320]{3,2,1,0:T(8,128)}, u32[]{:S(2)}, u32[]{:S(2)}) collective-permute-start(f32[1,2,64,320]{3,2,1,0:T(8,128)} %get-tuple-element.33), channel_id=1, source_target_pairs={{0,4},{4,8},{8,12},{12,16},{16,20},{20,24},{24,28},{1,5},{5,9},{9,... | collective-permute-start | bytes 491528 | tf_op jit(solution)/shard_map/ppermute | solution.py:52
  27.6 3.3 %collective-permute-start.3 = (f32[1,2,64,320]{3,2,1,0:T(8,128)}, f32[1,2,64,320]{3,2,1,0:T(8,128)}, u32[]{:S(2)}, u32[]{:S(2)}) collective-permute-start(f32[1,2,64,320]{3,2,1,0:T(8,128)} %get-tuple-element.34), channel_id=1, source_target_pairs={{4,0},{8,4},{12,8},{16,12},{20,16},{24,20},{28,24},{5,1},{9,5},{13... | collective-permute-start | bytes 491528 | tf_op jit(solution)/shard_map/ppermute | solution.py:53
  30.9 1.7 %reduce_sum.75 = f32[2,64,320]{2,1,0:T(8,128)} reduce(f32[2,2,64,320]{3,2,1,0:T(8,128)} %bitcast.371, f32[]{:T(128)} %constant.122.clone.1), dimensions={1}, to_apply=%region_3.4 | reduce | flops 40960 | bytes 491524 | tf_op jit(solution)/shard_map/reduce_sum | solution.py:21
  32.6 1.7 %reduce_sum.74 = f32[2,64,320]{2,1,0:T(8,128)} reduce(f32[2,2,64,320]{3,2,1,0:T(8,128)} %bitcast.370, f32[]{:T(128)} %constant.122.clone.1), dimensions={1}, to_apply=%region_2.3 | reduce | flops 40960 | bytes 491524 | tf_op jit(solution)/shard_map/reduce_sum | solution.py:21
  34.3 0.7 reduce_sum.73
  35.1 1.2 fusion.302
  36.3 1.2 fusion.306
  37.9 1.2 fusion.304
  39.4 1.0 fusion.335
  40.4 1.4 broadcast_in_dim.9
  41.8 6.1 %all-to-all-start.1 = ((f32[8,2,3,32,160]{4,3,1,2,0:T(8,128)}), f32[8,2,3,32,160]{4,3,1,2,0:T(8,128)}, u32[]{:S(2)}, u32[]{:S(2)}) async-start(f32[8,2,3,32,160]{4,3,1,2,0:T(8,128)} %broadcast_in_dim.9), calls=%async_computation.1 | async-start | bytes 3145728 | tf_op jit(solution)/shard_map/all_to_all | solution.py:60
  48.0 1.6 fusion.69
  49.8 1.4 fusion.206
  51.1 3.4 %collective-permute-start.5 = (f32[1,64,320]{2,1,0:T(8,128)S(1)}, f32[1,64,320]{2,1,0:T(8,128)S(1)}, u32[]{:S(2)}, u32[]{:S(2)}) collective-permute-start(f32[1,64,320]{2,1,0:T(8,128)S(1)} %fusion.206), channel_id=1, source_target_pairs={{4,0},{8,4},{12,8},{16,12},{20,16},{24,20},{28,24},{5,1},{9,5},{13... | collective-permute-start | bytes 245768 | tf_op jit(solution)/shard_map/ppermute | solution.py:53
  54.7 1.1 fusion.194
  55.8 2.5 %collective-permute-start.4 = (f32[1,64,320]{2,1,0:T(8,128)S(1)}, f32[1,64,320]{2,1,0:T(8,128)S(1)}, u32[]{:S(2)}, u32[]{:S(2)}) collective-permute-start(f32[1,64,320]{2,1,0:T(8,128)S(1)} %fusion.194), channel_id=1, source_target_pairs={{0,4},{4,8},{8,12},{12,16},{16,20},{20,24},{24,28},{1,5},{5,9},{9,... | collective-permute-start | bytes 245768 | tf_op jit(solution)/shard_map/ppermute | solution.py:52
  59.1 19.2 %collective-permute-done.4 = f32[1,64,320]{2,1,0:T(8,128)S(1)} collective-permute-done((f32[1,64,320]{2,1,0:T(8,128)S(1)}, f32[1,64,320]{2,1,0:T(8,128)S(1)}, u32[]{:S(2)}, u32[]{:S(2)}) %collective-permute-start.4) | collective-permute-done | bytes 81952 | tf_op jit(solution)/shard_map/ppermute | solution.py:52
  78.5 1.9 %collective-permute-start.7 = (f32[1,64,320]{2,1,0:T(8,128)S(1)}, f32[1,64,320]{2,1,0:T(8,128)S(1)}, u32[]{:S(2)}, u32[]{:S(2)}) collective-permute-start(f32[1,64,320]{2,1,0:T(8,128)S(1)} %fusion.183), channel_id=1, source_target_pairs={{4,0},{8,4},{12,8},{16,12},{20,16},{24,20},{28,24},{5,1},{9,5},{13... | collective-permute-start | bytes 245768 | tf_op jit(solution)/shard_map/ppermute | solution.py:53
  80.6 9.0 %collective-permute-start.6 = (f32[1,64,320]{2,1,0:T(8,128)S(1)}, f32[1,64,320]{2,1,0:T(8,128)S(1)}, u32[]{:S(2)}, u32[]{:S(2)}) collective-permute-start(f32[1,64,320]{2,1,0:T(8,128)S(1)} %fusion.173), channel_id=1, source_target_pairs={{0,4},{4,8},{8,12},{12,16},{16,20},{20,24},{24,28},{1,5},{5,9},{9,... | collective-permute-start | bytes 245768 | tf_op jit(solution)/shard_map/ppermute | solution.py:52
  89.8 0.6 collective-permute-done.7
  90.4 3.0 %collective-permute-done.6 = f32[1,64,320]{2,1,0:T(8,128)S(1)} collective-permute-done((f32[1,64,320]{2,1,0:T(8,128)S(1)}, f32[1,64,320]{2,1,0:T(8,128)S(1)}, u32[]{:S(2)}, u32[]{:S(2)}) %collective-permute-start.6) | collective-permute-done | bytes 81952 | tf_op jit(solution)/shard_map/ppermute | solution.py:52
  93.5 0.5 bitcast_reduce_fusion.4
  94.5 0.8 broadcast_in_dim.8
  95.3 6.8 %all-to-all-start = ((f32[8,2,32,160]{3,2,1,0:T(8,128)}), f32[8,2,32,160]{3,2,1,0:T(8,128)}, u32[]{:S(2)}, u32[]{:S(2)}) async-start(f32[8,2,32,160]{3,2,1,0:T(8,128)} %broadcast_in_dim.8), calls=%async_computation | async-start | bytes 1048576 | tf_op jit(solution)/shard_map/all_to_all | solution.py:60
  102.2 1.5 copy.24
  103.7 1.3 fusion.316
  105.2 2.0 %broadcast_add_fusion = (f32[16,32,160]{2,1,0:T(8,128)}, f32[16,32,160]{2,1,0:T(8,128)}, f32[16,32,160]{2,1,0:T(8,128)}, f32[16,32,160]{2,1,0:T(8,128)}, f32[16,32,160]{2,1,0:T(8,128)}) fusion(f32[16,31,160]{2,1,0:T(8,128)S(1)} %fusion.50, f32[16,32,160]{2,1,0:T(8,128)S(1)} %get-tuple-element.29, f32[16,32,159]{2,1,0:T(8,128)S(1)} %get-tuple-element.54, ...), kind=kLoop, calls=%fused_computation.134 | loop fusion | flops 1146880 | bytes 3262464 | tf_op jit(solution)/shard_map/add | solution.py:87
  107.3 7.1 %all-to-all-done = f32[8,2,32,160]{3,2,1,0:T(8,128)} async-done(((f32[8,2,32,160]{3,2,1,0:T(8,128)}), f32[8,2,32,160]{3,2,1,0:T(8,128)}, u32[]{:S(2)}, u32[]{:S(2)}) %all-to-all-start) | async-done | bytes 327712 | tf_op jit(solution)/shard_map/all_to_all | solution.py:60
  114.4 2.0 %add_divide_fusion = f32[16,32,160]{2,1,0:T(8,128)S(1)} fusion(f32[8,2,32,160]{3,2,1,0:T(8,128)} %all-to-all-done, f32[16,32,160]{2,1,0:T(8,128)} %get-tuple-element.8, f32[16,32,160]{2,1,0:T(8,128)} %get-tuple-element.7, f32[16,31,160]{2,1,0:T(8,128)S(1)} %fusion.50, f32[16,32,160]{2,1,0:T(8,128)} %get-tuple-element.6, f32[16,32,160]{2,1,0:T(8,128)} %get-tuple-element.5), kind=kLoop, calls=%fused_computation.79 | loop fusion | flops 655360 | bytes 2283520 | tf_op jit(solution)/shard_map/div | solution.py:164
  116.8 0.8 copy-done
  118.0 1.8 %fusion.21 = f32[16,32,160]{2,1,0:T(8,128)S(1)} fusion(f32[16,32,160]{2,1,0:T(8,128)S(1)} %add_divide_fusion, f32[16,32,160]{2,1,0:T(8,128)S(1)} %copy-done.1, f32[16,32,160]{2,1,0:T(8,128)S(1)} %copy-done, f32[16,32,160]{2,1,0:T(8,128)S(1)} %copy-done.3, f32[16,32,159]{2,1,0:T(8,128)S(1)} %get-tuple-element.52, f32[16,32,160]{2,1,0:T(8,128)S(1)} %copy-done.2, ...), kind=kLoop, calls=%fused_computation.42 | loop fusion | flops 1884160 | bytes 3897344 | tf_op jit(solution)/shard_map/add | solution.py:122
  120.1 0.8 copy-done.24
  121.0 0.4 fusion.293
  121.7 0.4 fusion.295
  122.3 0.4 fusion.297
  122.9 1.8 %bitcast_reduce_fusion.3 = f32[8,32,160]{2,1,0:T(8,128)S(1)} fusion(f32[16,32,160]{2,1,0:T(8,128)S(1)} %copy-done.3, f32[16,32,159]{2,1,0:T(8,128)S(1)} %get-tuple-element.48, f32[16,32,160]{2,1,0:T(8,128)S(1)} %copy-done.2, f32[16,32,159]{2,1,0:T(8,128)S(1)} %get-tuple-element.47, f32[16,31,160]{2,1,0:T(8,128)S(1)} %get-tuple-element.46, ...), kind=kLoop, calls=%fused_computation.77 | loop fusion | flops 1679360 | bytes 3733504 | tf_op jit(solution)/shard_map/reduce_sum | solution.py:21
  126.8 1.8 %fusion.42 = f32[16,32,160]{2,1,0:T(8,128)S(1)} fusion(f32[16,32,160]{2,1,0:T(8,128)S(1)} %bitcast_add_fusion, f32[16,32,160]{2,1,0:T(8,128)S(1)} %copy-done.1, f32[16,32,160]{2,1,0:T(8,128)S(1)} %copy-done, f32[16,32,160]{2,1,0:T(8,128)S(1)} %copy-done.3, f32[16,32,159]{2,1,0:T(8,128)S(1)} %get-tuple-element.44, f32[16,32,160]{2,1,0:T(8,128)S(1)} %copy-done.2, ...), kind=kLoop, calls=%fused_computation.63 | loop fusion | flops 1884160 | bytes 3897344 | tf_op jit(solution)/shard_map/add | solution.py:122
  129.0 0.5 fusion.48
  129.5 1.1 fusion.252
  131.4 0.6 copy-done.5
  132.7 1.9 %collective-permute-start.8 = (f32[1,64,320]{2,1,0:T(8,128)S(1)}, f32[1,64,320]{2,1,0:T(8,128)S(1)}, u32[]{:S(2)}, u32[]{:S(2)}) collective-permute-start(f32[1,64,320]{2,1,0:T(8,128)S(1)} %slice.1049), channel_id=1, source_target_pairs={{0,4},{4,8},{8,12},{12,16},{16,20},{20,24},{24,28},{1,5},{5,9},{9,... | collective-permute-start | bytes 245768 | tf_op jit(solution)/shard_map/ppermute | solution.py:52
  134.6 5.4 %collective-permute-done.8 = f32[1,64,320]{2,1,0:T(8,128)S(1)} collective-permute-done((f32[1,64,320]{2,1,0:T(8,128)S(1)}, f32[1,64,320]{2,1,0:T(8,128)S(1)}, u32[]{:S(2)}, u32[]{:S(2)}) %collective-permute-start.8) | collective-permute-done | bytes 81952 | tf_op jit(solution)/shard_map/ppermute | solution.py:52
  140.2 3.2 %collective-permute-start.11 = (f32[1,64,320]{2,1,0:T(8,128)S(1)}, f32[1,64,320]{2,1,0:T(8,128)S(1)}, u32[]{:S(2)}, u32[]{:S(2)}) collective-permute-start(f32[1,64,320]{2,1,0:T(8,128)S(1)} %get-tuple-element.59), channel_id=1, source_target_pairs={{4,0},{8,4},{12,8},{16,12},{20,16},{24,20},{28,24},{5,1},{9,5},{13... | collective-permute-start | bytes 245768 | tf_op jit(solution)/shard_map/ppermute | solution.py:53
  143.5 1.9 %collective-permute-start.9 = (f32[1,64,320]{2,1,0:T(8,128)S(1)}, f32[1,64,320]{2,1,0:T(8,128)S(1)}, u32[]{:S(2)}, u32[]{:S(2)}) collective-permute-start(f32[1,64,320]{2,1,0:T(8,128)S(1)} %get-tuple-element.60), channel_id=1, source_target_pairs={{4,0},{8,4},{12,8},{16,12},{20,16},{24,20},{28,24},{5,1},{9,5},{13... | collective-permute-start | bytes 245768 | tf_op jit(solution)/shard_map/ppermute | solution.py:53
  145.4 4.6 %collective-permute-done.9 = f32[1,64,320]{2,1,0:T(8,128)S(1)} collective-permute-done((f32[1,64,320]{2,1,0:T(8,128)S(1)}, f32[1,64,320]{2,1,0:T(8,128)S(1)}, u32[]{:S(2)}, u32[]{:S(2)}) %collective-permute-start.9) | collective-permute-done | bytes 81952 | tf_op jit(solution)/shard_map/ppermute | solution.py:53
  150.1 3.6 %collective-permute-start.10 = (f32[1,64,320]{2,1,0:T(8,128)S(1)}, f32[1,64,320]{2,1,0:T(8,128)S(1)}, u32[]{:S(2)}, u32[]{:S(2)}) collective-permute-start(f32[1,64,320]{2,1,0:T(8,128)S(1)} %fusion.153), channel_id=1, source_target_pairs={{0,4},{4,8},{8,12},{12,16},{16,20},{20,24},{24,28},{1,5},{5,9},{9,... | collective-permute-start | bytes 245768 | tf_op jit(solution)/shard_map/ppermute | solution.py:52
  153.9 1.9 %collective-permute-start.12 = (f32[1,64,320]{2,1,0:T(8,128)S(1)}, f32[1,64,320]{2,1,0:T(8,128)S(1)}, u32[]{:S(2)}, u32[]{:S(2)}) collective-permute-start(f32[1,64,320]{2,1,0:T(8,128)S(1)} %fusion.133), channel_id=1, source_target_pairs={{0,4},{4,8},{8,12},{12,16},{16,20},{20,24},{24,28},{1,5},{5,9},{9,... | collective-permute-start | bytes 245768 | tf_op jit(solution)/shard_map/ppermute | solution.py:52
  156.1 1.4 collective-permute-done.10
  157.7 3.4 %collective-permute-start.13 = (f32[1,64,320]{2,1,0:T(8,128)S(1)}, f32[1,64,320]{2,1,0:T(8,128)S(1)}, u32[]{:S(2)}, u32[]{:S(2)}) collective-permute-start(f32[1,64,320]{2,1,0:T(8,128)S(1)} %fusion.143), channel_id=1, source_target_pairs={{4,0},{8,4},{12,8},{16,12},{20,16},{24,20},{28,24},{5,1},{9,5},{13... | collective-permute-start | bytes 245768 | tf_op jit(solution)/shard_map/ppermute | solution.py:53
  161.4 2.8 %collective-permute-done.13 = f32[1,64,320]{2,1,0:T(8,128)S(1)} collective-permute-done((f32[1,64,320]{2,1,0:T(8,128)S(1)}, f32[1,64,320]{2,1,0:T(8,128)S(1)}, u32[]{:S(2)}, u32[]{:S(2)}) %collective-permute-start.13) | collective-permute-done | bytes 81952 | tf_op jit(solution)/shard_map/ppermute | solution.py:53
  164.4 1.6 fusion.76
  (170 shorter events, 10.1 us)
Async XLA Ops:
  1.9 14.7 %copy-start.12 = (f32[4,64,256]{2,1,0:T(8,128)S(1)}, f32[4,64,256]{2,1,0:T(8,128)}, u32[]{:S(2)}) copy-start(f32[4,64,256]{2,1,0:T(8,128)} %param.7) | copy-start | bytes 786436
  1.9 14.7 %copy-start.14 = (f32[4,64,256]{2,1,0:T(8,128)S(1)}, f32[4,64,256]{2,1,0:T(8,128)}, u32[]{:S(2)}) copy-start(f32[4,64,256]{2,1,0:T(8,128)} %param.6) | copy-start | bytes 786436
  1.9 14.7 %copy-start.16 = (f32[4,64,256]{2,1,0:T(8,128)S(1)}, f32[4,64,256]{2,1,0:T(8,128)}, u32[]{:S(2)}) copy-start(f32[4,64,256]{2,1,0:T(8,128)} %param.5) | copy-start | bytes 786436
  2.0 14.7 %copy-start.18 = (f32[4,64,256]{2,1,0:T(8,128)S(1)}, f32[4,64,256]{2,1,0:T(8,128)}, u32[]{:S(2)}) copy-start(f32[4,64,256]{2,1,0:T(8,128)} %param.4) | copy-start | bytes 786436
  3.1 12.6 %collective-permute-start = (f32[4,4,64,32]{3,2,0,1:T(8,128)}, f32[4,4,64,32]{3,2,0,1:T(8,128)S(1)}, u32[]{:S(2)}, u32[]{:S(2)}) collective-permute-start(f32[4,4,64,32]{3,2,0,1:T(8,128)} %get-tuple-element.35), channel_id=1, source_target_pairs={{0,1},{1,2},{2,3},{3,0},{4,5},{5,6},{6,7},{7,4},{8,9},{9,10},{10,1... | collective-permute-start | bytes 393224 | tf_op jit(solution)/shard_map/ppermute | solution.py:39
  3.1 13.5 %collective-permute-start.1 = (f32[4,4,64,32]{3,2,0,1:T(8,128)}, f32[4,4,64,32]{3,2,0,1:T(8,128)S(1)}, u32[]{:S(2)}, u32[]{:S(2)}) collective-permute-start(f32[4,4,64,32]{3,2,0,1:T(8,128)} %get-tuple-element.36), channel_id=1, source_target_pairs={{1,0},{2,1},{3,2},{0,3},{5,4},{6,5},{7,6},{4,7},{9,8},{10,9},{11,1... | collective-permute-start | bytes 393224 | tf_op jit(solution)/shard_map/ppermute | solution.py:40
  16.7 3.2 %copy-start.10 = (f32[4,4,64,32]{3,2,0,1:T(8,128)}, f32[4,4,64,32]{3,2,0,1:T(8,128)S(1)}, u32[]{:S(2)}) copy-start(f32[4,4,64,32]{3,2,0,1:T(8,128)S(1)} %collective-permute-done.1) | copy-start | bytes 393220
  24.2 23.7 %collective-permute-start.2 = (f32[1,2,64,320]{3,2,1,0:T(8,128)}, f32[1,2,64,320]{3,2,1,0:T(8,128)}, u32[]{:S(2)}, u32[]{:S(2)}) collective-permute-start(f32[1,2,64,320]{3,2,1,0:T(8,128)} %get-tuple-element.33), channel_id=1, source_target_pairs={{0,4},{4,8},{8,12},{12,16},{16,20},{20,24},{24,28},{1,5},{5,9},{9,... | collective-permute-start | bytes 491528 | tf_op jit(solution)/shard_map/ppermute | solution.py:52
  27.6 20.3 %collective-permute-start.3 = (f32[1,2,64,320]{3,2,1,0:T(8,128)}, f32[1,2,64,320]{3,2,1,0:T(8,128)}, u32[]{:S(2)}, u32[]{:S(2)}) collective-permute-start(f32[1,2,64,320]{3,2,1,0:T(8,128)} %get-tuple-element.34), channel_id=1, source_target_pairs={{4,0},{8,4},{12,8},{16,12},{20,16},{24,20},{28,24},{5,1},{9,5},{13... | collective-permute-start | bytes 491528 | tf_op jit(solution)/shard_map/ppermute | solution.py:53
  41.8 52.7 %all-to-all-start.1 = ((f32[8,2,3,32,160]{4,3,1,2,0:T(8,128)}), f32[8,2,3,32,160]{4,3,1,2,0:T(8,128)}, u32[]{:S(2)}, u32[]{:S(2)}) async-start(f32[8,2,3,32,160]{4,3,1,2,0:T(8,128)} %broadcast_in_dim.9), calls=%async_computation.1 | async-start | bytes 3145728 | tf_op jit(solution)/shard_map/all_to_all | solution.py:60
  47.9 1.8 %copy-start.11 = (f32[4,4,64,32]{3,2,0,1:T(8,128)S(1)}, f32[4,4,64,32]{3,2,0,1:T(8,128)}, u32[]{:S(2)}) copy-start(f32[4,4,64,32]{3,2,0,1:T(8,128)} %copy-done.10) | copy-start | bytes 393220
  47.9 1.8 %copy-start.13 = (f32[4,64,256]{2,1,0:T(8,128)S(1)}, f32[4,64,256]{2,1,0:T(8,128)}, u32[]{:S(2)}) copy-start(f32[4,64,256]{2,1,0:T(8,128)} %param.7) | copy-start | bytes 786436
  47.9 1.8 %copy-start.15 = (f32[4,64,256]{2,1,0:T(8,128)S(1)}, f32[4,64,256]{2,1,0:T(8,128)}, u32[]{:S(2)}) copy-start(f32[4,64,256]{2,1,0:T(8,128)} %param.6) | copy-start | bytes 786436
  47.9 1.7 %copy-start.17 = (f32[4,64,256]{2,1,0:T(8,128)S(1)}, f32[4,64,256]{2,1,0:T(8,128)}, u32[]{:S(2)}) copy-start(f32[4,64,256]{2,1,0:T(8,128)} %param.5) | copy-start | bytes 786436
  47.9 1.7 %copy-start.19 = (f32[4,64,256]{2,1,0:T(8,128)S(1)}, f32[4,64,256]{2,1,0:T(8,128)}, u32[]{:S(2)}) copy-start(f32[4,64,256]{2,1,0:T(8,128)} %param.4) | copy-start | bytes 786436
  48.0 1.7 %copy-start.34 = (f32[1,64,319]{2,1,0:T(8,128)S(1)}, f32[1,64,319]{2,1,0:T(8,128)}, u32[]{:S(2)}) copy-start(f32[1,64,319]{2,1,0:T(8,128)} %get-tuple-element.105) | copy-start | bytes 244996
  48.0 1.7 %copy-start.35 = (f32[1,64,319]{2,1,0:T(8,128)S(1)}, f32[1,64,319]{2,1,0:T(8,128)}, u32[]{:S(2)}) copy-start(f32[1,64,319]{2,1,0:T(8,128)} %get-tuple-element.106) | copy-start | bytes 244996
  48.0 1.7 %copy-start.36 = (f32[1,63,320]{2,1,0:T(8,128)S(1)}, f32[1,63,320]{2,1,0:T(8,128)}, u32[]{:S(2)}) copy-start(f32[1,63,320]{2,1,0:T(8,128)} %get-tuple-element.103) | copy-start | bytes 241924
  48.0 1.7 %copy-start.37 = (f32[1,63,320]{2,1,0:T(8,128)S(1)}, f32[1,63,320]{2,1,0:T(8,128)}, u32[]{:S(2)}) copy-start(f32[1,63,320]{2,1,0:T(8,128)} %get-tuple-element.104) | copy-start | bytes 241924
  49.6 30.8 %copy-start.8 = (f32[4,64,320]{2,1,0:T(8,128)}, f32[4,64,320]{2,1,0:T(8,128)S(1)}, u32[]{:S(2)}) copy-start(f32[4,64,320]{2,1,0:T(8,128)S(1)} %get-tuple-element.14) | copy-start | bytes 983044
  49.6 43.8 %copy-start.4 = (f32[4,64,320]{2,1,0:T(8,128)}, f32[4,64,320]{2,1,0:T(8,128)S(1)}, u32[]{:S(2)}) copy-start(f32[4,64,320]{2,1,0:T(8,128)S(1)} %get-tuple-element.15) | copy-start | bytes 983044
  49.6 43.8 %copy-start.6 = (f32[4,64,320]{2,1,0:T(8,128)}, f32[4,64,320]{2,1,0:T(8,128)S(1)}, u32[]{:S(2)}) copy-start(f32[4,64,320]{2,1,0:T(8,128)S(1)} %get-tuple-element.18) | copy-start | bytes 983044
  49.7 4.9 %copy-start.38 = (f32[1,64,319]{2,1,0:T(8,128)S(1)}, f32[1,64,319]{2,1,0:T(8,128)}, u32[]{:S(2)}) copy-start(f32[1,64,319]{2,1,0:T(8,128)} %get-tuple-element.113) | copy-start | bytes 244996
  49.7 4.9 %copy-start.39 = (f32[1,64,319]{2,1,0:T(8,128)S(1)}, f32[1,64,319]{2,1,0:T(8,128)}, u32[]{:S(2)}) copy-start(f32[1,64,319]{2,1,0:T(8,128)} %get-tuple-element.114) | copy-start | bytes 244996
  51.1 29.3 %collective-permute-start.5 = (f32[1,64,320]{2,1,0:T(8,128)S(1)}, f32[1,64,320]{2,1,0:T(8,128)S(1)}, u32[]{:S(2)}, u32[]{:S(2)}) collective-permute-start(f32[1,64,320]{2,1,0:T(8,128)S(1)} %fusion.206), channel_id=1, source_target_pairs={{4,0},{8,4},{12,8},{16,12},{20,16},{24,20},{28,24},{5,1},{9,5},{13... | collective-permute-start | bytes 245768 | tf_op jit(solution)/shard_map/ppermute | solution.py:53
  54.6 3.7 %copy-start.30 = (f32[2,63,320]{2,1,0:T(8,128)S(1)}, f32[2,63,320]{2,1,0:T(8,128)}, u32[]{:S(2)}) copy-start(f32[2,63,320]{2,1,0:T(8,128)} %get-tuple-element.87) | copy-start | bytes 483844
  54.6 3.7 %copy-start.31 = (f32[2,63,320]{2,1,0:T(8,128)S(1)}, f32[2,63,320]{2,1,0:T(8,128)}, u32[]{:S(2)}) copy-start(f32[2,63,320]{2,1,0:T(8,128)} %get-tuple-element.88) | copy-start | bytes 483844
  54.7 3.7 %copy-start.32 = (f32[2,64,319]{2,1,0:T(8,128)S(1)}, f32[2,64,319]{2,1,0:T(8,128)}, u32[]{:S(2)}) copy-start(f32[2,64,319]{2,1,0:T(8,128)} %get-tuple-element.89) | copy-start | bytes 489988
  54.7 3.7 %copy-start.33 = (f32[2,64,319]{2,1,0:T(8,128)S(1)}, f32[2,64,319]{2,1,0:T(8,128)}, u32[]{:S(2)}) copy-start(f32[2,64,319]{2,1,0:T(8,128)} %get-tuple-element.90) | copy-start | bytes 489988
  55.8 22.5 %collective-permute-start.4 = (f32[1,64,320]{2,1,0:T(8,128)S(1)}, f32[1,64,320]{2,1,0:T(8,128)S(1)}, u32[]{:S(2)}, u32[]{:S(2)}) collective-permute-start(f32[1,64,320]{2,1,0:T(8,128)S(1)} %fusion.194), channel_id=1, source_target_pairs={{0,4},{4,8},{8,12},{12,16},{16,20},{20,24},{24,28},{1,5},{5,9},{9,... | collective-permute-start | bytes 245768 | tf_op jit(solution)/shard_map/ppermute | solution.py:52
  59.1 34.4 %copy-start.20 = (f32[2,64,320]{2,1,0:T(8,128)}, f32[2,64,320]{2,1,0:T(8,128)S(1)}, u32[]{:S(2)}) copy-start(f32[2,64,320]{2,1,0:T(8,128)S(1)} %fusion.110) | copy-start | bytes 491524
  78.4 15.0 %copy-start.25 = (f32[1,64,320]{2,1,0:T(8,128)}, f32[1,64,320]{2,1,0:T(8,128)S(1)}, u32[]{:S(2)}) copy-start(f32[1,64,320]{2,1,0:T(8,128)S(1)} %fusion.183) | copy-start | bytes 245764
  78.5 12.0 %collective-permute-start.7 = (f32[1,64,320]{2,1,0:T(8,128)S(1)}, f32[1,64,320]{2,1,0:T(8,128)S(1)}, u32[]{:S(2)}, u32[]{:S(2)}) collective-permute-start(f32[1,64,320]{2,1,0:T(8,128)S(1)} %fusion.183), channel_id=1, source_target_pairs={{4,0},{8,4},{12,8},{16,12},{20,16},{24,20},{28,24},{5,1},{9,5},{13... | collective-permute-start | bytes 245768 | tf_op jit(solution)/shard_map/ppermute | solution.py:53
  80.5 12.9 %copy-start.27 = (f32[1,64,320]{2,1,0:T(8,128)}, f32[1,64,320]{2,1,0:T(8,128)S(1)}, u32[]{:S(2)}) copy-start(f32[1,64,320]{2,1,0:T(8,128)S(1)} %fusion.173) | copy-start | bytes 245764
  80.6 12.9 %collective-permute-start.6 = (f32[1,64,320]{2,1,0:T(8,128)S(1)}, f32[1,64,320]{2,1,0:T(8,128)S(1)}, u32[]{:S(2)}, u32[]{:S(2)}) collective-permute-start(f32[1,64,320]{2,1,0:T(8,128)S(1)} %fusion.173), channel_id=1, source_target_pairs={{0,4},{4,8},{8,12},{12,16},{16,20},{20,24},{24,28},{1,5},{5,9},{9,... | collective-permute-start | bytes 245768 | tf_op jit(solution)/shard_map/ppermute | solution.py:52
  95.3 19.1 %all-to-all-start = ((f32[8,2,32,160]{3,2,1,0:T(8,128)}), f32[8,2,32,160]{3,2,1,0:T(8,128)}, u32[]{:S(2)}, u32[]{:S(2)}) async-start(f32[8,2,32,160]{3,2,1,0:T(8,128)} %broadcast_in_dim.8), calls=%async_computation | async-start | bytes 1048576 | tf_op jit(solution)/shard_map/all_to_all | solution.py:60
  116.5 1.0 copy-start
  116.5 1.2 copy-start.1
  116.5 1.3 copy-start.2
  116.5 1.5 copy-start.3
  119.9 1.0 copy-start.24
  119.9 1.7 %copy-start.23 = (f32[16,1,32,160]{3,2,1,0:T(8,128)S(1)}, f32[16,1,32,160]{3,2,1,0:T(8,128)}, u32[]{:S(2)}) copy-start(f32[16,1,32,160]{3,2,1,0:T(8,128)} %get-tuple-element.31) | copy-start | bytes 983044
  120.9 1.3 copy-start.22
  129.0 2.0 %copy-start.21 = (f32[2,64,320]{2,1,0:T(8,128)S(1)}, f32[2,64,320]{2,1,0:T(8,128)}, u32[]{:S(2)}) copy-start(f32[2,64,320]{2,1,0:T(8,128)} %copy-done.20) | copy-start | bytes 491524
  129.0 2.0 %copy-start.26 = (f32[1,64,320]{2,1,0:T(8,128)S(1)}, f32[1,64,320]{2,1,0:T(8,128)}, u32[]{:S(2)}) copy-start(f32[1,64,320]{2,1,0:T(8,128)} %copy-done.25) | copy-start | bytes 245764
  129.0 2.0 %copy-start.28 = (f32[1,64,320]{2,1,0:T(8,128)S(1)}, f32[1,64,320]{2,1,0:T(8,128)}, u32[]{:S(2)}) copy-start(f32[1,64,320]{2,1,0:T(8,128)} %copy-done.27) | copy-start | bytes 245764
  131.0 1.0 copy-start.5
  131.0 1.1 copy-start.7
  131.0 1.2 copy-start.9
  132.7 7.4 %collective-permute-start.8 = (f32[1,64,320]{2,1,0:T(8,128)S(1)}, f32[1,64,320]{2,1,0:T(8,128)S(1)}, u32[]{:S(2)}, u32[]{:S(2)}) collective-permute-start(f32[1,64,320]{2,1,0:T(8,128)S(1)} %slice.1049), channel_id=1, source_target_pairs={{0,4},{4,8},{8,12},{12,16},{16,20},{20,24},{24,28},{1,5},{5,9},{9,... | collective-permute-start | bytes 245768 | tf_op jit(solution)/shard_map/ppermute | solution.py:52
  140.2 13.6 %collective-permute-start.11 = (f32[1,64,320]{2,1,0:T(8,128)S(1)}, f32[1,64,320]{2,1,0:T(8,128)S(1)}, u32[]{:S(2)}, u32[]{:S(2)}) collective-permute-start(f32[1,64,320]{2,1,0:T(8,128)S(1)} %get-tuple-element.59), channel_id=1, source_target_pairs={{4,0},{8,4},{12,8},{16,12},{20,16},{24,20},{28,24},{5,1},{9,5},{13... | collective-permute-start | bytes 245768 | tf_op jit(solution)/shard_map/ppermute | solution.py:53
  143.5 6.5 %collective-permute-start.9 = (f32[1,64,320]{2,1,0:T(8,128)S(1)}, f32[1,64,320]{2,1,0:T(8,128)S(1)}, u32[]{:S(2)}, u32[]{:S(2)}) collective-permute-start(f32[1,64,320]{2,1,0:T(8,128)S(1)} %get-tuple-element.60), channel_id=1, source_target_pairs={{4,0},{8,4},{12,8},{16,12},{20,16},{24,20},{28,24},{5,1},{9,5},{13... | collective-permute-start | bytes 245768 | tf_op jit(solution)/shard_map/ppermute | solution.py:53
  150.1 7.5 %collective-permute-start.10 = (f32[1,64,320]{2,1,0:T(8,128)S(1)}, f32[1,64,320]{2,1,0:T(8,128)S(1)}, u32[]{:S(2)}, u32[]{:S(2)}) collective-permute-start(f32[1,64,320]{2,1,0:T(8,128)S(1)} %fusion.153), channel_id=1, source_target_pairs={{0,4},{4,8},{8,12},{12,16},{16,20},{20,24},{24,28},{1,5},{5,9},{9,... | collective-permute-start | bytes 245768 | tf_op jit(solution)/shard_map/ppermute | solution.py:52
  153.9 7.5 %collective-permute-start.12 = (f32[1,64,320]{2,1,0:T(8,128)S(1)}, f32[1,64,320]{2,1,0:T(8,128)S(1)}, u32[]{:S(2)}, u32[]{:S(2)}) collective-permute-start(f32[1,64,320]{2,1,0:T(8,128)S(1)} %fusion.133), channel_id=1, source_target_pairs={{0,4},{4,8},{8,12},{12,16},{16,20},{20,24},{24,28},{1,5},{5,9},{9,... | collective-permute-start | bytes 245768 | tf_op jit(solution)/shard_map/ppermute | solution.py:52
  157.7 6.5 %collective-permute-start.13 = (f32[1,64,320]{2,1,0:T(8,128)S(1)}, f32[1,64,320]{2,1,0:T(8,128)S(1)}, u32[]{:S(2)}, u32[]{:S(2)}) collective-permute-start(f32[1,64,320]{2,1,0:T(8,128)S(1)} %fusion.143), channel_id=1, source_target_pairs={{4,0},{8,4},{12,8},{16,12},{20,16},{24,20},{28,24},{5,1},{9,5},{13... | collective-permute-start | bytes 245768 | tf_op jit(solution)/shard_map/ppermute | solution.py:53
  161.4 3.0 %copy-start.29 = (f32[4,64,320]{2,1,0:T(8,128)S(1)}, f32[4,64,320]{2,1,0:T(8,128)}, u32[]{:S(2)}) copy-start(f32[4,64,320]{2,1,0:T(8,128)} %get-tuple-element.21) | copy-start | bytes 983044

commit v13 on v11

--- a/solution.py
+++ b/solution.py
@@ -36,8 +36,10 @@
     count, length = lax.axis_size("raan"), values.shape[-1]
     up = [(i, (i + 1) % count) for i in range(count)]
     down = [(j, i) for i, j in up]
-    before = lax.ppermute(values[..., length - halo:], "raan", up)
-    after = lax.ppermute(values[..., :halo], "raan", down)
+    edge = values[..., :halo].shape
+    dense = edge[:-2] + (edge[-2] * halo // 128, 128) if edge[-2] * halo % 128 == 0 else edge
+    before = lax.ppermute(values[..., length - halo:].reshape(dense), "raan", up).reshape(edge)
+    after = lax.ppermute(values[..., :halo].reshape(dense), "raan", down).reshape(edge)
     return jnp.concatenate([before, values, after], axis=-1)
 
 

time: 144 us -> 136 us (0.944)
  waiting for transfers between devices: 40.3 us -> 33.5 us
    ppermute x2, waiting for transfers between devices: 7.6 us -> 0.7 us  [the longest x1 0.7 us: raan_extend(): lax.ppermute(values[..., length - halo:].reshape(dense), 'raan', up)]
    ppermute x8, waiting for transfers between devices: 14.6 us -> 16.2 us  [alt_extend(): above.append(lax.ppermute(values[:high], 'alt', down))]
    unnamed x174 -> x180, local copies, waits for them, and re-layouts: 3.27 us -> 3.28 us
  transfers between devices with their start and end apart: 19 -> 19, of which waited for: 13 -> 12; matrix products, arithmetic and copies ran while one was open for 12% -> 12% of each run, Pallas kernels for 0% -> 0%
where the time goes in v13:
time: 136 us; the launch traced here: 133 us
  starting transfers between devices  55 us (40%)
  waiting for transfers between devices  33.5 us (25%)
  other arithmetic  20.7 us (15%)
  local copies, waits for them, and re-layouts  13.9 us (10%)
  matrix products  7.58 us (6%)
  between operations  2.54 us (2%)
    ppermute x8, starting transfers between devices, alt_extend(): below.insert(0, lax.ppermute(values[low:], 'alt', up))  27.5 us
    ppermute x8, starting transfers between devices, alt_extend(): above.append(lax.ppermute(values[:high], 'alt', down))  20.8 us
    ppermute x8, waiting for transfers between devices, alt_extend(): above.append(lax.ppermute(values[:high], 'alt', down))  16.2 us
    ppermute x8, waiting for transfers between devices, alt_extend(): below.insert(0, lax.ppermute(values[low:], 'alt', up))  11.5 us
    all_to_all x1, starting transfers between devices, spread_gather(): every = lax.all_to_all(copies, 'alt', 0, 0)  5.7 us
    all_to_all x1, waiting for transfers between devices, spread_gather(): every = lax.all_to_all(copies, 'alt', 0, 0)  5.2 us
    dot_general x8, matrix products, coarsen(): summed = jnp.matmul(summed, pairing(length), precision=HIGH)  5.07 us
    add x12, other arithmetic, split_sweep(): rows.append(centre + OMEGA * (aim - applied) / diagonal)  4.03 us
  transfers between devices with their start and end apart: 19, of which 12 were waited for; matrix products, arithmetic and copies ran while one was open for 12% of the time, Pallas kernels for 0%

profile of v13, /device:TPU:8, one launch (start us, length us, event | category | flops | bytes accessed | tf_op | source)
XLA Modules:
  0.0 133.2 jit_solution(12532425509692154384)
XLA Ops:
  0.6 1.3 pad_maximum_fusion.1
  2.4 1.0 collective-permute-start.1
  3.6 0.5 iota_shift-right-logical_fusion.2
  4.1 0.6 compare_and_fusion.1
  4.7 0.5 compare_and_fusion
  5.2 0.5 fusion.320
  5.8 0.6 iota_shift-right-logical_fusion.1
  6.4 0.6 compare_and_fusion.2
  7.0 0.6 iota_shift-right-logical_fusion
  7.6 0.7 collective-permute-done
  8.9 0.8 fusion.377
  9.6 0.7 fusion.376
  10.3 0.7 fusion.381
  11.0 0.7 fusion.380
  11.7 0.6 pad_maximum_fusion
  12.4 0.8 fusion.366
  13.2 0.8 fusion.367
  14.0 0.8 slice_bitcast_fusion.11
  14.7 1.0 slice_bitcast_fusion
  15.8 3.4 %collective-permute-start.2 = (f32[1,2,64,320]{3,2,1,0:T(8,128)}, f32[1,2,64,320]{3,2,1,0:T(8,128)}, u32[]{:S(2)}, u32[]{:S(2)}) collective-permute-start(f32[1,2,64,320]{3,2,1,0:T(8,128)} %get-tuple-element.27), channel_id=1, source_target_pairs={{0,4},{4,8},{8,12},{12,16},{16,20},{20,24},{24,28},{1,5},{5,9},{9,... | collective-permute-start | bytes 491528 | tf_op jit(solution)/shard_map/ppermute | solution.py:54
  19.2 3.3 %collective-permute-start.3 = (f32[1,2,64,320]{3,2,1,0:T(8,128)}, f32[1,2,64,320]{3,2,1,0:T(8,128)}, u32[]{:S(2)}, u32[]{:S(2)}) collective-permute-start(f32[1,2,64,320]{3,2,1,0:T(8,128)} %get-tuple-element.28), channel_id=1, source_target_pairs={{4,0},{8,4},{12,8},{16,12},{20,16},{24,20},{28,24},{5,1},{9,5},{13... | collective-permute-start | bytes 491528 | tf_op jit(solution)/shard_map/ppermute | solution.py:55
  22.5 0.7 reduce_sum.75
  23.3 1.4 %fusion.331 = f32[2,64,160]{2,1,0:T(8,128)S(1)} fusion(f32[2,64,320]{2,1,0:T(8,128)} %reduce_sum.75, s32[320]{0:T(512)} %get-tuple-element.134, s32[320]{0:T(512)} %get-tuple-element.135, pred[320]{0:T(512)(128)(4,1)} %fusion.320), kind=kOutput, calls=%fused_computation.493 | convolution fusion | flops 78745600 | bytes 248640 | tf_op jit(solution)/shard_map/dot_general | solution.py:22
  24.7 1.1 fusion.335
  25.8 1.1 fusion.333
  28.8 1.1 collective-permute-done.3
  29.9 1.4 %fusion.22 = (f32[4,64,320]{2,1,0:T(8,128)S(1)}, f32[4,64,320]{2,1,0:T(8,128)S(1)}, f32[4,1,64,320]{3,2,1,0:T(8,128)S(1)}, f32[4,1,64,320]{3,2,1,0:T(8,128)S(1)}, f32[4,64,320]{2,1,0:T(8,128)S(1)}) fusion(f32[4,63,320]{2,1,0:T(8,128)S(1)} %fusion.4, f32[4,64,319]{2,1,0:T(8,128)S(1)} %get-tuple-element.56, f32[4,4,64,320]{3,2,0,1:T(8,128)S(1)} %pad_maximum_fusion, ...), kind=kLoop, calls=%fused_computation.47 | loop fusion | flops 1310720 | bytes 4252672 | tf_op jit(solution)/shard_map/add | solution.py:89
  31.6 1.1 fusion.198
  32.7 2.4 %collective-permute-start.5 = (f32[1,64,320]{2,1,0:T(8,128)S(1)}, f32[1,64,320]{2,1,0:T(8,128)S(1)}, u32[]{:S(2)}, u32[]{:S(2)}) collective-permute-start(f32[1,64,320]{2,1,0:T(8,128)S(1)} %fusion.198), channel_id=1, source_target_pairs={{4,0},{8,4},{12,8},{16,12},{20,16},{24,20},{28,24},{5,1},{9,5},{13... | collective-permute-start | bytes 245768 | tf_op jit(solution)/shard_map/ppermute | solution.py:55
  35.4 1.1 fusion.186
  36.5 3.4 %collective-permute-start.4 = (f32[1,64,320]{2,1,0:T(8,128)S(1)}, f32[1,64,320]{2,1,0:T(8,128)S(1)}, u32[]{:S(2)}, u32[]{:S(2)}) collective-permute-start(f32[1,64,320]{2,1,0:T(8,128)S(1)} %fusion.186), channel_id=1, source_target_pairs={{0,4},{4,8},{8,12},{12,16},{16,20},{20,24},{24,28},{1,5},{5,9},{9,... | collective-permute-start | bytes 245768 | tf_op jit(solution)/shard_map/ppermute | solution.py:54
  40.7 3.2 %collective-permute-done.4 = f32[1,64,320]{2,1,0:T(8,128)S(1)} collective-permute-done((f32[1,64,320]{2,1,0:T(8,128)S(1)}, f32[1,64,320]{2,1,0:T(8,128)S(1)}, u32[]{:S(2)}, u32[]{:S(2)}) %collective-permute-start.4) | collective-permute-done | bytes 81952 | tf_op jit(solution)/shard_map/ppermute | solution.py:54
  44.0 1.9 %collective-permute-start.7 = (f32[1,64,320]{2,1,0:T(8,128)S(1)}, f32[1,64,320]{2,1,0:T(8,128)S(1)}, u32[]{:S(2)}, u32[]{:S(2)}) collective-permute-start(f32[1,64,320]{2,1,0:T(8,128)S(1)} %fusion.175), channel_id=1, source_target_pairs={{4,0},{8,4},{12,8},{16,12},{20,16},{24,20},{28,24},{5,1},{9,5},{13... | collective-permute-start | bytes 245768 | tf_op jit(solution)/shard_map/ppermute | solution.py:55
  46.1 3.9 %collective-permute-start.6 = (f32[1,64,320]{2,1,0:T(8,128)S(1)}, f32[1,64,320]{2,1,0:T(8,128)S(1)}, u32[]{:S(2)}, u32[]{:S(2)}) collective-permute-start(f32[1,64,320]{2,1,0:T(8,128)S(1)} %fusion.165), channel_id=1, source_target_pairs={{0,4},{4,8},{8,12},{12,16},{16,20},{20,24},{24,28},{1,5},{5,9},{9,... | collective-permute-start | bytes 245768 | tf_op jit(solution)/shard_map/ppermute | solution.py:54
  50.3 1.3 collective-permute-done.7
  51.6 1.9 %collective-permute-done.6 = f32[1,64,320]{2,1,0:T(8,128)S(1)} collective-permute-done((f32[1,64,320]{2,1,0:T(8,128)S(1)}, f32[1,64,320]{2,1,0:T(8,128)S(1)}, u32[]{:S(2)}, u32[]{:S(2)}) %collective-permute-start.6) | collective-permute-done | bytes 81952 | tf_op jit(solution)/shard_map/ppermute | solution.py:54
  53.6 0.5 bitcast_reduce_fusion
  54.9 4.0 %collective-permute-start.8 = (f32[2,4,32,160]{3,2,0,1:T(8,128)S(1)}, f32[2,4,32,160]{3,2,0,1:T(8,128)S(1)}, u32[]{:S(2)}, u32[]{:S(2)}) collective-permute-start(f32[2,4,32,160]{3,2,0,1:T(8,128)S(1)} %pad_maximum_fusion.17), channel_id=1, source_target_pairs={{0,8},{4,12},{8,16},{12,20},{16,24},{20,28},{1,9},{5,13},{9,17},{1... | collective-permute-start | bytes 491528 | tf_op jit(solution)/shard_map/ppermute | solution.py:54
  59.0 2.5 %collective-permute-start.9 = (f32[2,4,32,160]{3,2,0,1:T(8,128)S(1)}, f32[2,4,32,160]{3,2,0,1:T(8,128)S(1)}, u32[]{:S(2)}, u32[]{:S(2)}) collective-permute-start(f32[2,4,32,160]{3,2,0,1:T(8,128)S(1)} %pad_maximum_fusion.17), channel_id=1, source_target_pairs={{0,4},{4,8},{8,12},{12,16},{16,20},{20,24},{24,28},{1,5},{5,9},{9,... | collective-permute-start | bytes 491528 | tf_op jit(solution)/shard_map/ppermute | solution.py:54
  61.7 2.4 %collective-permute-start.11 = (f32[2,4,32,160]{3,2,0,1:T(8,128)S(1)}, f32[2,4,32,160]{3,2,0,1:T(8,128)S(1)}, u32[]{:S(2)}, u32[]{:S(2)}) collective-permute-start(f32[2,4,32,160]{3,2,0,1:T(8,128)S(1)} %pad_maximum_fusion.17), channel_id=1, source_target_pairs={{8,0},{12,4},{16,8},{20,12},{24,16},{28,20},{9,1},{13,5},{17,9},{2... | collective-permute-start | bytes 491528 | tf_op jit(solution)/shard_map/ppermute | solution.py:55
  64.1 3.1 %collective-permute-start.10 = (f32[2,4,32,160]{3,2,0,1:T(8,128)S(1)}, f32[2,4,32,160]{3,2,0,1:T(8,128)S(1)}, u32[]{:S(2)}, u32[]{:S(2)}) collective-permute-start(f32[2,4,32,160]{3,2,0,1:T(8,128)S(1)} %pad_maximum_fusion.17), channel_id=1, source_target_pairs={{4,0},{8,4},{12,8},{16,12},{20,16},{24,20},{28,24},{5,1},{9,5},{13... | collective-permute-start | bytes 491528 | tf_op jit(solution)/shard_map/ppermute | solution.py:55
  67.2 2.2 %collective-permute-done.9 = f32[2,4,32,160]{3,2,0,1:T(8,128)S(1)} collective-permute-done((f32[2,4,32,160]{3,2,0,1:T(8,128)S(1)}, f32[2,4,32,160]{3,2,0,1:T(8,128)S(1)}, u32[]{:S(2)}, u32[]{:S(2)}) %collective-permute-start.9) | collective-permute-done | bytes 163872 | tf_op jit(solution)/shard_map/ppermute | solution.py:54
  69.5 5.2 %collective-permute-done.10 = f32[2,4,32,160]{3,2,0,1:T(8,128)S(1)} collective-permute-done((f32[2,4,32,160]{3,2,0,1:T(8,128)S(1)}, f32[2,4,32,160]{3,2,0,1:T(8,128)S(1)}, u32[]{:S(2)}, u32[]{:S(2)}) %collective-permute-start.10) | collective-permute-done | bytes 163872 | tf_op jit(solution)/shard_map/ppermute | solution.py:55
  77.5 0.7 broadcast_in_dim.20
  78.2 5.7 %all-to-all-start = ((f32[8,1,4,16,80]{4,3,2,1,0:T(8,128)}), f32[8,1,4,16,80]{4,3,2,1,0:T(8,128)}, u32[]{:S(2)}, u32[]{:S(2)}) async-start(f32[8,1,4,16,80]{4,3,2,1,0:T(8,128)} %broadcast_in_dim.20), calls=%async_computation | async-start | bytes 524288 | tf_op jit(solution)/shard_map/all_to_all | solution.py:62
  83.9 0.5 compare_and_fusion.3
  84.4 0.6 compare_and_fusion.4
  85.0 5.2 %all-to-all-done = f32[8,1,4,16,80]{4,3,2,1,0:T(8,128)} async-done(((f32[8,1,4,16,80]{4,3,2,1,0:T(8,128)}), f32[8,1,4,16,80]{4,3,2,1,0:T(8,128)}, u32[]{:S(2)}, u32[]{:S(2)}) %all-to-all-start) | async-done | bytes 163872 | tf_op jit(solution)/shard_map/all_to_all | solution.py:62
  90.2 0.9 slice_bitcast_fusion.20
  91.2 1.0 fusion.278
  92.4 0.9 fusion.221
  93.4 0.9 fusion.233
  94.6 1.1 fusion.245
  98.4 0.7 copy-done.7
  99.5 3.5 %collective-permute-start.12 = (f32[1,64,320]{2,1,0:T(8,128)S(1)}, f32[1,64,320]{2,1,0:T(8,128)S(1)}, u32[]{:S(2)}, u32[]{:S(2)}) collective-permute-start(f32[1,64,320]{2,1,0:T(8,128)S(1)} %slice.1291), channel_id=1, source_target_pairs={{0,4},{4,8},{8,12},{12,16},{16,20},{20,24},{24,28},{1,5},{5,9},{9,... | collective-permute-start | bytes 245768 | tf_op jit(solution)/shard_map/ppermute | solution.py:54
  103.0 4.0 %collective-permute-done.12 = f32[1,64,320]{2,1,0:T(8,128)S(1)} collective-permute-done((f32[1,64,320]{2,1,0:T(8,128)S(1)}, f32[1,64,320]{2,1,0:T(8,128)S(1)}, u32[]{:S(2)}, u32[]{:S(2)}) %collective-permute-start.12) | collective-permute-done | bytes 81952 | tf_op jit(solution)/shard_map/ppermute | solution.py:54
  107.2 2.5 %collective-permute-start.15 = (f32[1,64,320]{2,1,0:T(8,128)S(1)}, f32[1,64,320]{2,1,0:T(8,128)S(1)}, u32[]{:S(2)}, u32[]{:S(2)}) collective-permute-start(f32[1,64,320]{2,1,0:T(8,128)S(1)} %get-tuple-element.37), channel_id=1, source_target_pairs={{4,0},{8,4},{12,8},{16,12},{20,16},{24,20},{28,24},{5,1},{9,5},{13... | collective-permute-start | bytes 245768 | tf_op jit(solution)/shard_map/ppermute | solution.py:55
  109.7 1.9 %collective-permute-start.13 = (f32[1,64,320]{2,1,0:T(8,128)S(1)}, f32[1,64,320]{2,1,0:T(8,128)S(1)}, u32[]{:S(2)}, u32[]{:S(2)}) collective-permute-start(f32[1,64,320]{2,1,0:T(8,128)S(1)} %get-tuple-element.38), channel_id=1, source_target_pairs={{4,0},{8,4},{12,8},{16,12},{20,16},{24,20},{28,24},{5,1},{9,5},{13... | collective-permute-start | bytes 245768 | tf_op jit(solution)/shard_map/ppermute | solution.py:55
  111.7 5.6 %collective-permute-done.13 = f32[1,64,320]{2,1,0:T(8,128)S(1)} collective-permute-done((f32[1,64,320]{2,1,0:T(8,128)S(1)}, f32[1,64,320]{2,1,0:T(8,128)S(1)}, u32[]{:S(2)}, u32[]{:S(2)}) %collective-permute-start.13) | collective-permute-done | bytes 81952 | tf_op jit(solution)/shard_map/ppermute | solution.py:55
  117.4 3.3 %collective-permute-start.14 = (f32[1,64,320]{2,1,0:T(8,128)S(1)}, f32[1,64,320]{2,1,0:T(8,128)S(1)}, u32[]{:S(2)}, u32[]{:S(2)}) collective-permute-start(f32[1,64,320]{2,1,0:T(8,128)S(1)} %fusion.145), channel_id=1, source_target_pairs={{0,4},{4,8},{8,12},{12,16},{16,20},{20,24},{24,28},{1,5},{5,9},{9,... | collective-permute-start | bytes 245768 | tf_op jit(solution)/shard_map/ppermute | solution.py:54
  121.0 3.4 %collective-permute-start.16 = (f32[1,64,320]{2,1,0:T(8,128)S(1)}, f32[1,64,320]{2,1,0:T(8,128)S(1)}, u32[]{:S(2)}, u32[]{:S(2)}) collective-permute-start(f32[1,64,320]{2,1,0:T(8,128)S(1)} %fusion.125), channel_id=1, source_target_pairs={{0,4},{4,8},{8,12},{12,16},{16,20},{20,24},{24,28},{1,5},{5,9},{9,... | collective-permute-start | bytes 245768 | tf_op jit(solution)/shard_map/ppermute | solution.py:54
  125.0 3.2 %collective-permute-start.17 = (f32[1,64,320]{2,1,0:T(8,128)S(1)}, f32[1,64,320]{2,1,0:T(8,128)S(1)}, u32[]{:S(2)}, u32[]{:S(2)}) collective-permute-start(f32[1,64,320]{2,1,0:T(8,128)S(1)} %fusion.135), channel_id=1, source_target_pairs={{4,0},{8,4},{12,8},{16,12},{20,16},{24,20},{28,24},{5,1},{9,5},{13... | collective-permute-start | bytes 245768 | tf_op jit(solution)/shard_map/ppermute | solution.py:55
  128.5 3.0 %collective-permute-done.17 = f32[1,64,320]{2,1,0:T(8,128)S(1)} collective-permute-done((f32[1,64,320]{2,1,0:T(8,128)S(1)}, f32[1,64,320]{2,1,0:T(8,128)S(1)}, u32[]{:S(2)}, u32[]{:S(2)}) %collective-permute-start.17) | collective-permute-done | bytes 81952 | tf_op jit(solution)/shard_map/ppermute | solution.py:55
  131.7 1.6 %fusion.30 = (f32[4,64,256]{2,1,0:T(8,128)}, f32[4,64,256]{2,1,0:T(8,128)}) fusion(f32[4,63,320]{2,1,0:T(8,128)S(1)} %fusion.4, f32[4,63,320]{2,1,0:T(8,128)S(1)} %get-tuple-element.34, f32[4,64,320]{2,1,0:T(8,128)S(1)} %copy-done.53, f32[4,64,319]{2,1,0:T(8,128)S(1)} %get-tuple-element.36, f32[4,64,320]{2,1,0:T(8,128)S(1)} %get-tuple-element.18, ...), kind=kLoop, calls=%fused_computation.66 | loop fusion | flops 655360 | bytes 3395584 | tf_op jit(solution)/shard_map/div | solution.py:219
  (284 shorter events, 13.0 us)
Async XLA Ops:
  2.1 6.5 %copy-start.14 = (f32[4,64,256]{2,1,0:T(8,128)S(1)}, f32[4,64,256]{2,1,0:T(8,128)}, u32[]{:S(2)}) copy-start(f32[4,64,256]{2,1,0:T(8,128)} %param.7) | copy-start | bytes 786436
  2.1 6.5 %copy-start.16 = (f32[4,64,256]{2,1,0:T(8,128)S(1)}, f32[4,64,256]{2,1,0:T(8,128)}, u32[]{:S(2)}) copy-start(f32[4,64,256]{2,1,0:T(8,128)} %param.6) | copy-start | bytes 786436
  2.1 6.5 %copy-start.18 = (f32[4,64,256]{2,1,0:T(8,128)S(1)}, f32[4,64,256]{2,1,0:T(8,128)}, u32[]{:S(2)}) copy-start(f32[4,64,256]{2,1,0:T(8,128)} %param.5) | copy-start | bytes 786436
  2.2 6.5 %copy-start.20 = (f32[4,64,256]{2,1,0:T(8,128)S(1)}, f32[4,64,256]{2,1,0:T(8,128)}, u32[]{:S(2)}) copy-start(f32[4,64,256]{2,1,0:T(8,128)} %param.4) | copy-start | bytes 786436
  2.4 6.1 %collective-permute-start.1 = (f32[4,4,16,128]{3,2,1,0:T(8,128)S(1)}, f32[4,4,16,128]{3,2,1,0:T(8,128)S(1)}, u32[]{:S(2)}, u32[]{:S(2)}) collective-permute-start(f32[4,4,16,128]{3,2,1,0:T(8,128)S(1)} %copy.29), channel_id=1, source_target_pairs={{1,0},{2,1},{3,2},{0,3},{5,4},{6,5},{7,6},{4,7},{9,8},{10,9},{11,1... | collective-permute-start | bytes 393224 | tf_op jit(solution)/shard_map/ppermute | solution.py:42
  3.5 4.7 %collective-permute-start = (f32[4,4,16,128]{3,2,1,0:T(8,128)S(1)}, f32[4,4,16,128]{3,2,1,0:T(8,128)S(1)}, u32[]{:S(2)}, u32[]{:S(2)}) collective-permute-start(f32[4,4,16,128]{3,2,1,0:T(8,128)S(1)} %copy.28), channel_id=1, source_target_pairs={{0,1},{1,2},{2,3},{3,0},{4,5},{5,6},{6,7},{7,4},{8,9},{9,10},{10,1... | collective-permute-start | bytes 393224 | tf_op jit(solution)/shard_map/ppermute | solution.py:41
  8.4 3.3 %copy-start = (f32[4,4,64,32]{3,2,1,0:T(8,128)}, f32[4,4,64,32]{3,2,1,0:T(8,128)S(1)}, u32[]{:S(2)}) copy-start(f32[4,4,64,32]{3,2,1,0:T(8,128)S(1)} %reshape.119) | copy-start | bytes 393220
  8.7 3.0 %copy-start.2 = (f32[4,4,64,32]{3,2,1,0:T(8,128)}, f32[4,4,64,32]{3,2,1,0:T(8,128)S(1)}, u32[]{:S(2)}) copy-start(f32[4,4,64,32]{3,2,1,0:T(8,128)S(1)} %reshape.121) | copy-start | bytes 393220
  8.7 3.0 %copy-start.21 = (f32[4,64,256]{2,1,0:T(8,128)S(1)}, f32[4,64,256]{2,1,0:T(8,128)}, u32[]{:S(2)}) copy-start(f32[4,64,256]{2,1,0:T(8,128)} %param.4) | copy-start | bytes 786436
  8.8 2.2 %copy-start.8 = (f32[1,64,320]{2,1,0:T(8,128)}, f32[1,64,320]{2,1,0:T(8,128)S(1)}, u32[]{:S(2)}) copy-start(f32[1,64,320]{2,1,0:T(8,128)S(1)} %get-tuple-element.19) | copy-start | bytes 245764
  8.8 2.2 %copy-start.11 = (f32[1,64,320]{2,1,0:T(8,128)}, f32[1,64,320]{2,1,0:T(8,128)S(1)}, u32[]{:S(2)}) copy-start(f32[1,64,320]{2,1,0:T(8,128)S(1)} %get-tuple-element.20) | copy-start | bytes 245764
  15.8 13.0 %collective-permute-start.2 = (f32[1,2,64,320]{3,2,1,0:T(8,128)}, f32[1,2,64,320]{3,2,1,0:T(8,128)}, u32[]{:S(2)}, u32[]{:S(2)}) collective-permute-start(f32[1,2,64,320]{3,2,1,0:T(8,128)} %get-tuple-element.27), channel_id=1, source_target_pairs={{0,4},{4,8},{8,12},{12,16},{16,20},{20,24},{24,28},{1,5},{5,9},{9,... | collective-permute-start | bytes 491528 | tf_op jit(solution)/shard_map/ppermute | solution.py:54
  19.2 10.7 %collective-permute-start.3 = (f32[1,2,64,320]{3,2,1,0:T(8,128)}, f32[1,2,64,320]{3,2,1,0:T(8,128)}, u32[]{:S(2)}, u32[]{:S(2)}) collective-permute-start(f32[1,2,64,320]{3,2,1,0:T(8,128)} %get-tuple-element.28), channel_id=1, source_target_pairs={{4,0},{8,4},{12,8},{16,12},{20,16},{24,20},{28,24},{5,1},{9,5},{13... | collective-permute-start | bytes 491528 | tf_op jit(solution)/shard_map/ppermute | solution.py:55
  23.2 4.3 %copy-start.74 = (s32[160]{0:T(256)S(1)}, s32[160]{0:T(256)}, u32[]{:S(2)}) copy-start(s32[160]{0:T(256)} %get-tuple-element.138) | copy-start | bytes 1924
  23.2 4.3 %copy-start.77 = (s32[160]{0:T(256)S(1)}, s32[160]{0:T(256)}, u32[]{:S(2)}) copy-start(s32[160]{0:T(256)} %get-tuple-element.139) | copy-start | bytes 1924
  23.2 4.3 %copy-start.85 = (pred[160]{0:T(512)(128)(4,1)S(1)}, pred[160]{0:T(512)(128)(4,1)}, u32[]{:S(2)}) copy-start(pred[160]{0:T(512)(128)(4,1)} %compare_and_fusion) | copy-start | bytes 484
  27.1 48.6 %copy-start.41 = (f32[32,2,160]{2,0,1:T(8,128)}, f32[32,2,160]{2,0,1:T(8,128)S(1)}, u32[]{:S(2)}) copy-start(f32[32,2,160]{2,0,1:T(8,128)S(1)} %get-tuple-element.129) | copy-start | bytes 122884
  27.3 48.4 %copy-start.43 = (f32[32,2,160]{2,0,1:T(8,128)}, f32[32,2,160]{2,0,1:T(8,128)S(1)}, u32[]{:S(2)}) copy-start(f32[32,2,160]{2,0,1:T(8,128)S(1)} %get-tuple-element.131) | copy-start | bytes 122884
  27.5 48.2 %copy-start.45 = (f32[32,2,160]{2,0,1:T(8,128)}, f32[32,2,160]{2,0,1:T(8,128)S(1)}, u32[]{:S(2)}) copy-start(f32[32,2,160]{2,0,1:T(8,128)S(1)} %get-tuple-element.133) | copy-start | bytes 122884
  31.3 14.7 %copy-start.6 = (f32[4,64,320]{2,1,0:T(8,128)}, f32[4,64,320]{2,1,0:T(8,128)S(1)}, u32[]{:S(2)}) copy-start(f32[4,64,320]{2,1,0:T(8,128)S(1)} %get-tuple-element.14) | copy-start | bytes 983044
  31.6 3.7 %copy-start.12 = (f32[1,64,320]{2,1,0:T(8,128)S(1)}, f32[1,64,320]{2,1,0:T(8,128)}, u32[]{:S(2)}) copy-start(f32[1,64,320]{2,1,0:T(8,128)} %copy-done.11) | copy-start | bytes 245764
  31.6 3.7 %copy-start.58 = (f32[1,64,319]{2,1,0:T(8,128)S(1)}, f32[1,64,319]{2,1,0:T(8,128)}, u32[]{:S(2)}) copy-start(f32[1,64,319]{2,1,0:T(8,128)} %get-tuple-element.112) | copy-start | bytes 244996
  31.6 3.7 %copy-start.59 = (f32[1,64,319]{2,1,0:T(8,128)S(1)}, f32[1,64,319]{2,1,0:T(8,128)}, u32[]{:S(2)}) copy-start(f32[1,64,319]{2,1,0:T(8,128)} %get-tuple-element.113) | copy-start | bytes 244996
  31.6 3.7 %copy-start.60 = (f32[1,63,320]{2,1,0:T(8,128)S(1)}, f32[1,63,320]{2,1,0:T(8,128)}, u32[]{:S(2)}) copy-start(f32[1,63,320]{2,1,0:T(8,128)} %get-tuple-element.110) | copy-start | bytes 241924
  31.6 3.7 %copy-start.61 = (f32[1,63,320]{2,1,0:T(8,128)S(1)}, f32[1,63,320]{2,1,0:T(8,128)}, u32[]{:S(2)}) copy-start(f32[1,63,320]{2,1,0:T(8,128)} %get-tuple-element.111) | copy-start | bytes 241924
  32.7 13.2 %collective-permute-start.5 = (f32[1,64,320]{2,1,0:T(8,128)S(1)}, f32[1,64,320]{2,1,0:T(8,128)S(1)}, u32[]{:S(2)}, u32[]{:S(2)}) collective-permute-start(f32[1,64,320]{2,1,0:T(8,128)S(1)} %fusion.198), channel_id=1, source_target_pairs={{4,0},{8,4},{12,8},{16,12},{20,16},{24,20},{28,24},{5,1},{9,5},{13... | collective-permute-start | bytes 245768 | tf_op jit(solution)/shard_map/ppermute | solution.py:55
  35.3 4.7 %copy-start.54 = (f32[2,63,320]{2,1,0:T(8,128)S(1)}, f32[2,63,320]{2,1,0:T(8,128)}, u32[]{:S(2)}) copy-start(f32[2,63,320]{2,1,0:T(8,128)} %get-tuple-element.82) | copy-start | bytes 483844
  35.3 4.7 %copy-start.55 = (f32[2,63,320]{2,1,0:T(8,128)S(1)}, f32[2,63,320]{2,1,0:T(8,128)}, u32[]{:S(2)}) copy-start(f32[2,63,320]{2,1,0:T(8,128)} %get-tuple-element.83) | copy-start | bytes 483844
  35.3 4.7 %copy-start.56 = (f32[2,64,319]{2,1,0:T(8,128)S(1)}, f32[2,64,319]{2,1,0:T(8,128)}, u32[]{:S(2)}) copy-start(f32[2,64,319]{2,1,0:T(8,128)} %get-tuple-element.84) | copy-start | bytes 489988
  35.4 4.7 %copy-start.57 = (f32[2,64,319]{2,1,0:T(8,128)S(1)}, f32[2,64,319]{2,1,0:T(8,128)}, u32[]{:S(2)}) copy-start(f32[2,64,319]{2,1,0:T(8,128)} %get-tuple-element.85) | copy-start | bytes 489988
  36.5 7.4 %collective-permute-start.4 = (f32[1,64,320]{2,1,0:T(8,128)S(1)}, f32[1,64,320]{2,1,0:T(8,128)S(1)}, u32[]{:S(2)}, u32[]{:S(2)}) collective-permute-start(f32[1,64,320]{2,1,0:T(8,128)S(1)} %fusion.186), channel_id=1, source_target_pairs={{0,4},{4,8},{8,12},{12,16},{16,20},{20,24},{24,28},{1,5},{5,9},{9,... | collective-permute-start | bytes 245768 | tf_op jit(solution)/shard_map/ppermute | solution.py:54
  40.7 12.9 %copy-start.39 = (f32[2,64,320]{2,1,0:T(8,128)}, f32[2,64,320]{2,1,0:T(8,128)S(1)}, u32[]{:S(2)}) copy-start(f32[2,64,320]{2,1,0:T(8,128)S(1)} %fusion.87) | copy-start | bytes 491524
  44.0 9.5 %copy-start.49 = (f32[1,64,320]{2,1,0:T(8,128)}, f32[1,64,320]{2,1,0:T(8,128)S(1)}, u32[]{:S(2)}) copy-start(f32[1,64,320]{2,1,0:T(8,128)S(1)} %fusion.175) | copy-start | bytes 245764
  44.0 7.6 %collective-permute-start.7 = (f32[1,64,320]{2,1,0:T(8,128)S(1)}, f32[1,64,320]{2,1,0:T(8,128)S(1)}, u32[]{:S(2)}, u32[]{:S(2)}) collective-permute-start(f32[1,64,320]{2,1,0:T(8,128)S(1)} %fusion.175), channel_id=1, source_target_pairs={{4,0},{8,4},{12,8},{16,12},{20,16},{24,20},{28,24},{5,1},{9,5},{13... | collective-permute-start | bytes 245768 | tf_op jit(solution)/shard_map/ppermute | solution.py:55
  46.1 7.4 %copy-start.51 = (f32[1,64,320]{2,1,0:T(8,128)}, f32[1,64,320]{2,1,0:T(8,128)S(1)}, u32[]{:S(2)}) copy-start(f32[1,64,320]{2,1,0:T(8,128)S(1)} %fusion.165) | copy-start | bytes 245764
  46.1 7.4 %collective-permute-start.6 = (f32[1,64,320]{2,1,0:T(8,128)S(1)}, f32[1,64,320]{2,1,0:T(8,128)S(1)}, u32[]{:S(2)}, u32[]{:S(2)}) collective-permute-start(f32[1,64,320]{2,1,0:T(8,128)S(1)} %fusion.165), channel_id=1, source_target_pairs={{0,4},{4,8},{8,12},{12,16},{16,20},{20,24},{24,28},{1,5},{5,9},{9,... | collective-permute-start | bytes 245768 | tf_op jit(solution)/shard_map/ppermute | solution.py:54
  54.9 21.6 %copy-start.23 = (f32[32,2,160]{2,0,1:T(8,128)}, f32[32,2,160]{2,0,1:T(8,128)S(1)}, u32[]{:S(2)}) copy-start(f32[32,2,160]{2,0,1:T(8,128)S(1)} %convolution_multiply_fusion.3) | copy-start | bytes 122884
  54.9 12.3 %collective-permute-start.8 = (f32[2,4,32,160]{3,2,0,1:T(8,128)S(1)}, f32[2,4,32,160]{3,2,0,1:T(8,128)S(1)}, u32[]{:S(2)}, u32[]{:S(2)}) collective-permute-start(f32[2,4,32,160]{3,2,0,1:T(8,128)S(1)} %pad_maximum_fusion.17), channel_id=1, source_target_pairs={{0,8},{4,12},{8,16},{12,20},{16,24},{20,28},{1,9},{5,13},{9,17},{1... | collective-permute-start | bytes 491528 | tf_op jit(solution)/shard_map/ppermute | solution.py:54
  59.0 10.4 %collective-permute-start.9 = (f32[2,4,32,160]{3,2,0,1:T(8,128)S(1)}, f32[2,4,32,160]{3,2,0,1:T(8,128)S(1)}, u32[]{:S(2)}, u32[]{:S(2)}) collective-permute-start(f32[2,4,32,160]{3,2,0,1:T(8,128)S(1)} %pad_maximum_fusion.17), channel_id=1, source_target_pairs={{0,4},{4,8},{8,12},{12,16},{16,20},{20,24},{24,28},{1,5},{5,9},{9,... | collective-permute-start | bytes 491528 | tf_op jit(solution)/shard_map/ppermute | solution.py:54
  61.7 13.1 %collective-permute-start.11 = (f32[2,4,32,160]{3,2,0,1:T(8,128)S(1)}, f32[2,4,32,160]{3,2,0,1:T(8,128)S(1)}, u32[]{:S(2)}, u32[]{:S(2)}) collective-permute-start(f32[2,4,32,160]{3,2,0,1:T(8,128)S(1)} %pad_maximum_fusion.17), channel_id=1, source_target_pairs={{8,0},{12,4},{16,8},{20,12},{24,16},{28,20},{9,1},{13,5},{17,9},{2... | collective-permute-start | bytes 491528 | tf_op jit(solution)/shard_map/ppermute | solution.py:55
  64.1 10.7 %collective-permute-start.10 = (f32[2,4,32,160]{3,2,0,1:T(8,128)S(1)}, f32[2,4,32,160]{3,2,0,1:T(8,128)S(1)}, u32[]{:S(2)}, u32[]{:S(2)}) collective-permute-start(f32[2,4,32,160]{3,2,0,1:T(8,128)S(1)} %pad_maximum_fusion.17), channel_id=1, source_target_pairs={{4,0},{8,4},{12,8},{16,12},{20,16},{24,20},{28,24},{5,1},{9,5},{13... | collective-permute-start | bytes 491528 | tf_op jit(solution)/shard_map/ppermute | solution.py:55
  69.5 6.2 %copy-start.25 = (f32[2,4,32,160]{3,2,0,1:T(8,128)}, f32[2,4,32,160]{3,2,0,1:T(8,128)S(1)}, u32[]{:S(2)}) copy-start(f32[2,4,32,160]{3,2,0,1:T(8,128)S(1)} %collective-permute-done.9) | copy-start | bytes 491524
  78.2 12.0 %all-to-all-start = ((f32[8,1,4,16,80]{4,3,2,1,0:T(8,128)}), f32[8,1,4,16,80]{4,3,2,1,0:T(8,128)}, u32[]{:S(2)}, u32[]{:S(2)}) async-start(f32[8,1,4,16,80]{4,3,2,1,0:T(8,128)} %broadcast_in_dim.20), calls=%async_computation | async-start | bytes 524288 | tf_op jit(solution)/shard_map/all_to_all | solution.py:62
  92.3 3.4 %copy-start.76 = (s32[160]{0:T(256)S(1)}, s32[160]{0:T(256)}, u32[]{:S(2)}) copy-start(s32[160]{0:T(256)} %get-tuple-element.138) | copy-start | bytes 1924
  92.3 3.4 %copy-start.79 = (s32[160]{0:T(256)S(1)}, s32[160]{0:T(256)}, u32[]{:S(2)}) copy-start(s32[160]{0:T(256)} %get-tuple-element.139) | copy-start | bytes 1924
  92.3 3.4 %copy-start.87 = (pred[160]{0:T(512)(128)(4,1)S(1)}, pred[160]{0:T(512)(128)(4,1)}, u32[]{:S(2)}) copy-start(pred[160]{0:T(512)(128)(4,1)} %compare_and_fusion) | copy-start | bytes 484
  93.3 2.7 %copy-start.67 = (s32[32]{0:T(128)S(1)}, s32[32]{0:T(128)}, u32[]{:S(2)}) copy-start(s32[32]{0:T(128)} %iota_shift-right-logical_fusion.2) | copy-start | bytes 388
  93.3 2.7 %copy-start.69 = (pred[32]{0:T(512)(128)(4,1)S(1)}, pred[32]{0:T(512)(128)(4,1)}, u32[]{:S(2)}) copy-start(pred[32]{0:T(512)(128)(4,1)} %compare_and_fusion.1) | copy-start | bytes 100
  93.3 3.0 %copy-start.30 = (f32[6,32,160]{2,1,0:T(8,128)S(1)}, f32[6,32,160]{2,1,0:T(8,128)}, u32[]{:S(2)}) copy-start(f32[6,32,160]{2,1,0:T(8,128)} %copy-done.29) | copy-start | bytes 368644
  94.4 2.1 %copy-start.5 = (f32[8,31,160]{2,1,0:T(8,128)S(1)}, f32[8,31,160]{2,1,0:T(8,128)}, u32[]{:S(2)}) copy-start(f32[8,31,160]{2,1,0:T(8,128)} %copy-done.4) | copy-start | bytes 476164
  94.4 2.1 %copy-start.24 = (f32[32,2,160]{2,0,1:T(8,128)S(1)}, f32[32,2,160]{2,0,1:T(8,128)}, u32[]{:S(2)}) copy-start(f32[32,2,160]{2,0,1:T(8,128)} %copy-done.23) | copy-start | bytes 122884
  94.4 2.1 %copy-start.26 = (f32[2,4,32,160]{3,2,0,1:T(8,128)S(1)}, f32[2,4,32,160]{3,2,0,1:T(8,128)}, u32[]{:S(2)}) copy-start(f32[2,4,32,160]{3,2,0,1:T(8,128)} %copy-done.25) | copy-start | bytes 491524
  94.4 2.1 %copy-start.28 = (f32[2,4,32,160]{3,2,0,1:T(8,128)S(1)}, f32[2,4,32,160]{3,2,0,1:T(8,128)}, u32[]{:S(2)}) copy-start(f32[2,4,32,160]{3,2,0,1:T(8,128)} %copy-done.27) | copy-start | bytes 491524
  94.4 2.1 %copy-start.32 = (f32[8,1,32,160]{3,2,0,1:T(8,128)S(1)}, f32[8,1,32,160]{3,2,0,1:T(8,128)}, u32[]{:S(2)}) copy-start(f32[8,1,32,160]{3,2,0,1:T(8,128)} %copy-done.31) | copy-start | bytes 491524
  94.4 2.1 %copy-start.34 = (f32[8,1,32,160]{3,2,0,1:T(8,128)S(1)}, f32[8,1,32,160]{3,2,0,1:T(8,128)}, u32[]{:S(2)}) copy-start(f32[8,1,32,160]{3,2,0,1:T(8,128)} %copy-done.33) | copy-start | bytes 491524
  99.3 7.7 %copy-start.10 = (f32[1,64,320]{2,1,0:T(8,128)S(1)}, f32[1,64,320]{2,1,0:T(8,128)}, u32[]{:S(2)}) copy-start(f32[1,64,320]{2,1,0:T(8,128)} %copy-done.8) | copy-start | bytes 245764
  99.5 17.8 %copy-start.13 = (f32[1,64,320]{2,1,0:T(8,128)S(1)}, f32[1,64,320]{2,1,0:T(8,128)}, u32[]{:S(2)}) copy-start(f32[1,64,320]{2,1,0:T(8,128)} %copy-done.11) | copy-start | bytes 245764
  99.5 7.5 %collective-permute-start.12 = (f32[1,64,320]{2,1,0:T(8,128)S(1)}, f32[1,64,320]{2,1,0:T(8,128)S(1)}, u32[]{:S(2)}, u32[]{:S(2)}) collective-permute-start(f32[1,64,320]{2,1,0:T(8,128)S(1)} %slice.1291), channel_id=1, source_target_pairs={{0,4},{4,8},{8,12},{12,16},{16,20},{20,24},{24,28},{1,5},{5,9},{9,... | collective-permute-start | bytes 245768 | tf_op jit(solution)/shard_map/ppermute | solution.py:54
  107.2 13.7 %collective-permute-start.15 = (f32[1,64,320]{2,1,0:T(8,128)S(1)}, f32[1,64,320]{2,1,0:T(8,128)S(1)}, u32[]{:S(2)}, u32[]{:S(2)}) collective-permute-start(f32[1,64,320]{2,1,0:T(8,128)S(1)} %get-tuple-element.37), channel_id=1, source_target_pairs={{4,0},{8,4},{12,8},{16,12},{20,16},{24,20},{28,24},{5,1},{9,5},{13... | collective-permute-start | bytes 245768 | tf_op jit(solution)/shard_map/ppermute | solution.py:55
  109.7 7.6 %collective-permute-start.13 = (f32[1,64,320]{2,1,0:T(8,128)S(1)}, f32[1,64,320]{2,1,0:T(8,128)S(1)}, u32[]{:S(2)}, u32[]{:S(2)}) collective-permute-start(f32[1,64,320]{2,1,0:T(8,128)S(1)} %get-tuple-element.38), channel_id=1, source_target_pairs={{4,0},{8,4},{12,8},{16,12},{20,16},{24,20},{28,24},{5,1},{9,5},{13... | collective-permute-start | bytes 245768 | tf_op jit(solution)/shard_map/ppermute | solution.py:55
  117.4 7.4 %collective-permute-start.14 = (f32[1,64,320]{2,1,0:T(8,128)S(1)}, f32[1,64,320]{2,1,0:T(8,128)S(1)}, u32[]{:S(2)}, u32[]{:S(2)}) collective-permute-start(f32[1,64,320]{2,1,0:T(8,128)S(1)} %fusion.145), channel_id=1, source_target_pairs={{0,4},{4,8},{8,12},{12,16},{16,20},{20,24},{24,28},{1,5},{5,9},{9,... | collective-permute-start | bytes 245768 | tf_op jit(solution)/shard_map/ppermute | solution.py:54
  121.0 7.5 %collective-permute-start.16 = (f32[1,64,320]{2,1,0:T(8,128)S(1)}, f32[1,64,320]{2,1,0:T(8,128)S(1)}, u32[]{:S(2)}, u32[]{:S(2)}) collective-permute-start(f32[1,64,320]{2,1,0:T(8,128)S(1)} %fusion.125), channel_id=1, source_target_pairs={{0,4},{4,8},{8,12},{12,16},{16,20},{20,24},{24,28},{1,5},{5,9},{9,... | collective-permute-start | bytes 245768 | tf_op jit(solution)/shard_map/ppermute | solution.py:54
  125.0 6.5 %collective-permute-start.17 = (f32[1,64,320]{2,1,0:T(8,128)S(1)}, f32[1,64,320]{2,1,0:T(8,128)S(1)}, u32[]{:S(2)}, u32[]{:S(2)}) collective-permute-start(f32[1,64,320]{2,1,0:T(8,128)S(1)} %fusion.135), channel_id=1, source_target_pairs={{4,0},{8,4},{12,8},{16,12},{20,16},{24,20},{28,24},{5,1},{9,5},{13... | collective-permute-start | bytes 245768 | tf_op jit(solution)/shard_map/ppermute | solution.py:55
  128.5 3.2 %copy-start.53 = (f32[4,64,320]{2,1,0:T(8,128)S(1)}, f32[4,64,320]{2,1,0:T(8,128)}, u32[]{:S(2)}) copy-start(f32[4,64,320]{2,1,0:T(8,128)} %get-tuple-element.21) | copy-start | bytes 983044
  (43 other events, 54.8 us)

commit v14 on v13

--- a/solution.py
+++ b/solution.py
@@ -43,6 +43,18 @@
     return jnp.concatenate([before, values, after], axis=-1)
 
 
+def packed(values):
+    lanes, inner = values.shape[-1], values[0].size
+    padded = -(-lanes // 128) * 128
+    if lanes % 128 and 4 * (padded - lanes) >= padded and inner % 1024 == 0:
+        return values.reshape(values.shape[0], inner // 128, 128)
+    return values
+
+
+def send(values, axis, route):
+    return lax.ppermute(packed(values), axis, route).reshape(values.shape)
+
+
 def alt_extend(values, halo):
     count, depth = lax.axis_size("alt"), values.shape[0]
     below, above = [], []
@@ -51,14 +63,15 @@
         high = min(depth, halo - (distance - 1) * depth)
         up = [(i, i + distance) for i in range(count) if i + distance < count]
         down = [(i, i - distance) for i in range(count) if i - distance >= 0]
-        below.insert(0, lax.ppermute(values[low:], "alt", up))
-        above.append(lax.ppermute(values[:high], "alt", down))
+        below.insert(0, send(values[low:], "alt", up))
+        above.append(send(values[:high], "alt", down))
     return jnp.concatenate(below + [values] + above, axis=0)
 
 
 def spread_gather(values):
     count = lax.axis_size("alt")
-    copies = jnp.broadcast_to(values[None], (count,) + values.shape)
+    dense = packed(values)
+    copies = jnp.broadcast_to(dense[None], (count,) + dense.shape)
     every = lax.all_to_all(copies, "alt", 0, 0)
     return every.reshape((count * values.shape[0],) + values.shape[1:])
 

time: 136 us -> 159 us (1.17)
  the two profiles are of different devices: /device:TPU:8 before, /device:TPU:0 now
where the time goes in v14:
time: 159 us; the launch traced here: 157 us
  starting transfers between devices  58.5 us (37%)
  local copies, waits for them, and re-layouts  35.4 us (22%)
  waiting for transfers between devices  25.6 us (16%)
  other arithmetic  22.7 us (14%)
  matrix products  12.4 us (8%)
  between operations  2.59 us (2%)
    ppermute x16, starting transfers between devices, send(): return lax.ppermute(packed(values), axis, route).reshape(values.shape)  48.7 us
    ppermute x16, waiting for transfers between devices, send(): return lax.ppermute(packed(values), axis, route).reshape(values.shape)  17.4 us
    reshape x8, local copies, waits for them, and re-layouts, send(): return lax.ppermute(packed(values), axis, route).reshape(values.shape)  14.1 us
    all_to_all x1, waiting for transfers between devices, spread_gather(): every = lax.all_to_all(copies, 'alt', 0, 0)  7.65 us
    all_to_all x1, starting transfers between devices, spread_gather(): every = lax.all_to_all(copies, 'alt', 0, 0)  7.27 us
    dot_general x8, matrix products, coarsen(): summed = jnp.matmul(summed, pairing(length), precision=HIGH)  6.33 us
    add x12, other arithmetic, split_sweep(): rows.append(centre + OMEGA * (aim - applied) / diagonal)  4.03 us
    slice x20, local copies, waits for them, and re-layouts, lane_shifts(): left = jnp.concatenate([zero, values[..., :-1]], axis=-1)  4.03 us
  transfers between devices with their start and end apart: 19, of which 9 were waited for; matrix products, arithmetic and copies ran while one was open for 19% of the time, Pallas kernels for 0%

profile of v14, /device:TPU:0, one launch (start us, length us, event | category | flops | bytes accessed | tf_op | source)
XLA Modules:
  0.0 157.2 jit_solution(15874549199379374616)
XLA Ops:
  0.6 1.3 pad_maximum_fusion.1
  2.4 2.4 %collective-permute-start.1 = (f32[4,4,16,128]{3,2,1,0:T(8,128)S(1)}, f32[4,4,16,128]{3,2,1,0:T(8,128)S(1)}, u32[]{:S(2)}, u32[]{:S(2)}) collective-permute-start(f32[4,4,16,128]{3,2,1,0:T(8,128)S(1)} %copy.42), channel_id=1, source_target_pairs={{1,0},{2,1},{3,2},{0,3},{5,4},{6,5},{7,6},{4,7},{9,8},{10,9},{11,1... | collective-permute-start | bytes 393224 | tf_op jit(solution)/shard_map/ppermute | solution.py:42
  10.3 0.8 fusion.381
  11.8 0.7 fusion.385
  13.8 0.8 fusion.370
  14.6 0.8 fusion.371
  15.4 0.8 slice_bitcast_fusion.11
  16.2 1.0 slice_bitcast_fusion
  17.2 4.1 %collective-permute-start.2 = (f32[1,2,64,320]{3,2,1,0:T(8,128)}, f32[1,2,64,320]{3,2,1,0:T(8,128)}, u32[]{:S(2)}, u32[]{:S(2)}) collective-permute-start(f32[1,2,64,320]{3,2,1,0:T(8,128)} %get-tuple-element.27), channel_id=1, source_target_pairs={{0,4},{4,8},{8,12},{12,16},{16,20},{20,24},{24,28},{1,5},{5,9},{9,... | collective-permute-start | bytes 491528 | tf_op jit(solution)/shard_map/ppermute | solution.py:55
  21.3 1.3 collective-permute-start.3
  23.4 1.4 fusion.331
  24.7 1.1 fusion.335
  25.8 1.1 fusion.333
  27.9 0.9 fusion.203
  29.0 0.9 fusion.202
  30.2 1.4 fusion.22
  31.9 1.1 fusion.198
  33.0 1.3 collective-permute-start.5
  34.5 1.1 fusion.186
  35.6 5.2 %collective-permute-start.4 = (f32[1,64,320]{2,1,0:T(8,128)S(1)}, f32[1,64,320]{2,1,0:T(8,128)S(1)}, u32[]{:S(2)}, u32[]{:S(2)}) collective-permute-start(f32[1,64,320]{2,1,0:T(8,128)S(1)} %fusion.186), channel_id=1, source_target_pairs={{0,4},{4,8},{8,12},{12,16},{16,20},{20,24},{24,28},{1,5},{5,9},{9,... | collective-permute-start | bytes 245768 | tf_op jit(solution)/shard_map/ppermute | solution.py:55
  41.6 1.4 collective-permute-done.4
  43.1 1.3 collective-permute-start.7
  44.6 5.5 %collective-permute-start.6 = (f32[1,64,320]{2,1,0:T(8,128)S(1)}, f32[1,64,320]{2,1,0:T(8,128)S(1)}, u32[]{:S(2)}, u32[]{:S(2)}) collective-permute-start(f32[1,64,320]{2,1,0:T(8,128)S(1)} %fusion.165), channel_id=1, source_target_pairs={{0,4},{4,8},{8,12},{12,16},{16,20},{20,24},{24,28},{1,5},{5,9},{9,... | collective-permute-start | bytes 245768 | tf_op jit(solution)/shard_map/ppermute | solution.py:55
  50.5 1.9 %collective-permute-done.6 = f32[1,64,320]{2,1,0:T(8,128)S(1)} collective-permute-done((f32[1,64,320]{2,1,0:T(8,128)S(1)}, f32[1,64,320]{2,1,0:T(8,128)S(1)}, u32[]{:S(2)}, u32[]{:S(2)}) %collective-permute-start.6) | collective-permute-done | bytes 81952 | tf_op jit(solution)/shard_map/ppermute | solution.py:55
  53.6 0.8 convolution_multiply_fusion.3
  54.4 0.9 pad_maximum_fusion.17
  56.0 1.8 %reshape.141 = f32[2,160,128]{2,1,0:T(8,128)} reshape(f32[2,4,32,160]{3,2,1,0:T(8,128)} %copy.25) | data formatting | bytes 327680 | tf_op jit(solution)/shard_map/reshape | solution.py:50
  57.8 7.5 %collective-permute-start.8 = (f32[2,160,128]{2,1,0:T(8,128)}, f32[2,160,128]{2,1,0:T(8,128)}, u32[]{:S(2)}, u32[]{:S(2)}) collective-permute-start(f32[2,160,128]{2,1,0:T(8,128)} %reshape.141), channel_id=1, source_target_pairs={{0,8},{4,12},{8,16},{12,20},{16,24},{20,28},{1,9},{5,13},{9,17},{1... | collective-permute-start | bytes 491528 | tf_op jit(solution)/shard_map/ppermute | solution.py:55
  65.3 0.9 fusion.2
  66.2 1.5 fusion.1
  67.7 1.3 collective-permute-start.11
  69.0 1.3 collective-permute-start.10
  70.3 5.2 %collective-permute-start.9 = (f32[2,160,128]{2,1,0:T(8,128)}, f32[2,160,128]{2,1,0:T(8,128)}, u32[]{:S(2)}, u32[]{:S(2)}) collective-permute-start(f32[2,160,128]{2,1,0:T(8,128)} %reshape.141), channel_id=1, source_target_pairs={{0,4},{4,8},{8,12},{12,16},{16,20},{20,24},{24,28},{1,5},{5,9},{9,... | collective-permute-start | bytes 491528 | tf_op jit(solution)/shard_map/ppermute | solution.py:55
  75.5 1.8 %reshape.142 = f32[2,4,32,160]{3,2,1,0:T(8,128)} reshape(f32[2,160,128]{2,1,0:T(8,128)} %collective-permute-done.8) | data formatting | bytes 327680 | tf_op jit(solution)/shard_map/reshape | solution.py:55
  77.2 1.8 %fusion.358 = (f32[2,4,32,160]{3,2,0,1:T(8,128)}, f32[10,4,32,160]{3,2,0,1:T(8,128)}) fusion(f32[2,4,32,160]{3,2,1,0:T(8,128)} %reshape.142), kind=kLoop, calls=%fused_computation.510 | loop fusion | bytes 688128 | tf_op jit(solution)/shard_map/reshape | solution.py:55
  79.0 1.8 %reshape.143 = f32[2,4,32,160]{3,2,1,0:T(8,128)} reshape(f32[2,160,128]{2,1,0:T(8,128)} %collective-permute-done.9) | data formatting | bytes 327680 | tf_op jit(solution)/shard_map/reshape | solution.py:55
  80.8 1.8 %fusion.359 = (f32[2,4,32,160]{3,2,0,1:T(8,128)}, f32[10,4,32,160]{3,2,0,1:T(8,128)}) fusion(f32[2,4,32,160]{3,2,1,0:T(8,128)} %reshape.143, f32[10,4,32,160]{3,2,0,1:T(8,128)} %get-tuple-element.67), kind=kLoop, calls=%fused_computation.511 | loop fusion | bytes 786432 | tf_op jit(solution)/shard_map/reshape | solution.py:55
  82.6 1.7 %constant_dynamic-update-slice_fusion.2 = f32[10,4,32,160]{3,2,0,1:T(8,128)} fusion(f32[10,4,32,160]{3,2,0,1:T(8,128)} %get-tuple-element.69, f32[2,1,32,160]{3,2,0,1:T(8,128)} %bitcast.448, f32[2,1,32,160]{3,2,0,1:T(8,128)} %bitcast.453, f32[2,1,32,160]{3,2,0,1:T(8,128)} %bitcast.458, f32[2,1,32,160]{3,2,0,1:T(8,128)} %bitcast.28), kind=kLoop, calls=%fused_computation.442 | loop fusion | flops 122880 | bytes 524288
  84.3 1.8 %reshape.144 = f32[2,4,32,160]{3,2,1,0:T(8,128)} reshape(f32[2,160,128]{2,1,0:T(8,128)} %collective-permute-done.10) | data formatting | bytes 327680 | tf_op jit(solution)/shard_map/reshape | solution.py:55
  86.0 1.8 %fusion.360 = (f32[2,4,32,160]{3,2,0,1:T(8,128)}, f32[10,4,32,160]{3,2,0,1:T(8,128)}) fusion(f32[2,4,32,160]{3,2,1,0:T(8,128)} %reshape.144, f32[10,4,32,160]{3,2,0,1:T(8,128)} %constant_dynamic-update-slice_fusion.2), kind=kLoop, calls=%fused_computation.512 | loop fusion | bytes 786432 | tf_op jit(solution)/shard_map/reshape | solution.py:55
  87.8 1.8 %reshape.145 = f32[2,4,32,160]{3,2,1,0:T(8,128)} reshape(f32[2,160,128]{2,1,0:T(8,128)} %collective-permute-done.11) | data formatting | bytes 327680 | tf_op jit(solution)/shard_map/reshape | solution.py:55
  89.6 1.7 %fusion.361 = (f32[2,4,32,160]{3,2,0,1:T(8,128)S(1)}, f32[10,4,32,160]{3,2,0,1:T(8,128)}) fusion(f32[2,4,32,160]{3,2,1,0:T(8,128)} %reshape.145, f32[10,4,32,160]{3,2,0,1:T(8,128)} %get-tuple-element.71), kind=kLoop, calls=%fused_computation.513 | loop fusion | bytes 688128 | tf_op jit(solution)/shard_map/reshape | solution.py:55
  91.3 1.2 slice_bitcast_fusion.1
  93.9 1.1 fusion.101
  95.3 0.9 fusion.265
  97.3 1.4 broadcast_in_dim.19
  98.8 1.4 broadcast_in_dim.21
  100.2 7.3 %all-to-all-start = ((f32[8,1,40,128]{3,2,1,0:T(8,128)}), f32[8,1,40,128]{3,2,1,0:T(8,128)}, u32[]{:S(2)}, u32[]{:S(2)}) async-start(f32[8,1,40,128]{3,2,1,0:T(8,128)} %broadcast_in_dim.21), calls=%async_computation | async-start | bytes 327680 | tf_op jit(solution)/shard_map/all_to_all | solution.py:75
  107.5 7.6 %all-to-all-done = f32[8,1,40,128]{3,2,1,0:T(8,128)} async-done(((f32[8,1,40,128]{3,2,1,0:T(8,128)}), f32[8,1,40,128]{3,2,1,0:T(8,128)}, u32[]{:S(2)}, u32[]{:S(2)}) %all-to-all-start) | async-done | bytes 163872 | tf_op jit(solution)/shard_map/all_to_all | solution.py:75
  115.1 1.8 %reshape.146 = f32[8,4,16,80]{3,2,1,0:T(8,128)} reshape(f32[8,1,40,128]{3,2,1,0:T(8,128)} %all-to-all-done) | data formatting | bytes 327680 | tf_op jit(solution)/shard_map/reshape | solution.py:76
  116.9 1.0 slice_bitcast_fusion.20
  117.9 1.0 fusion.278
  121.0 1.0 fusion.115
  122.2 1.3 fusion.266
  125.3 2.2 %collective-permute-start.12 = (f32[1,64,320]{2,1,0:T(8,128)S(1)}, f32[1,64,320]{2,1,0:T(8,128)S(1)}, u32[]{:S(2)}, u32[]{:S(2)}) collective-permute-start(f32[1,64,320]{2,1,0:T(8,128)S(1)} %slice.1291), channel_id=1, source_target_pairs={{0,4},{4,8},{8,12},{12,16},{16,20},{20,24},{24,28},{1,5},{5,9},{9,... | collective-permute-start | bytes 245768 | tf_op jit(solution)/shard_map/ppermute | solution.py:55
  127.5 2.8 %collective-permute-done.12 = f32[1,64,320]{2,1,0:T(8,128)S(1)} collective-permute-done((f32[1,64,320]{2,1,0:T(8,128)S(1)}, f32[1,64,320]{2,1,0:T(8,128)S(1)}, u32[]{:S(2)}, u32[]{:S(2)}) %collective-permute-start.12) | collective-permute-done | bytes 81952 | tf_op jit(solution)/shard_map/ppermute | solution.py:55
  130.5 1.3 collective-permute-start.15
  131.9 1.3 collective-permute-start.13
  133.2 6.2 %collective-permute-done.13 = f32[1,64,320]{2,1,0:T(8,128)S(1)} collective-permute-done((f32[1,64,320]{2,1,0:T(8,128)S(1)}, f32[1,64,320]{2,1,0:T(8,128)S(1)}, u32[]{:S(2)}, u32[]{:S(2)}) %collective-permute-start.13) | collective-permute-done | bytes 81952 | tf_op jit(solution)/shard_map/ppermute | solution.py:55
  139.5 4.9 %collective-permute-start.14 = (f32[1,64,320]{2,1,0:T(8,128)S(1)}, f32[1,64,320]{2,1,0:T(8,128)S(1)}, u32[]{:S(2)}, u32[]{:S(2)}) collective-permute-start(f32[1,64,320]{2,1,0:T(8,128)S(1)} %fusion.145), channel_id=1, source_target_pairs={{0,4},{4,8},{8,12},{12,16},{16,20},{20,24},{24,28},{1,5},{5,9},{9,... | collective-permute-start | bytes 245768 | tf_op jit(solution)/shard_map/ppermute | solution.py:55
  144.7 3.9 %collective-permute-start.16 = (f32[1,64,320]{2,1,0:T(8,128)S(1)}, f32[1,64,320]{2,1,0:T(8,128)S(1)}, u32[]{:S(2)}, u32[]{:S(2)}) collective-permute-start(f32[1,64,320]{2,1,0:T(8,128)S(1)} %fusion.125), channel_id=1, source_target_pairs={{0,4},{4,8},{8,12},{12,16},{16,20},{20,24},{24,28},{1,5},{5,9},{9,... | collective-permute-start | bytes 245768 | tf_op jit(solution)/shard_map/ppermute | solution.py:55
  149.0 1.3 collective-permute-start.17
  150.7 4.7 %collective-permute-done.17 = f32[1,64,320]{2,1,0:T(8,128)S(1)} collective-permute-done((f32[1,64,320]{2,1,0:T(8,128)S(1)}, f32[1,64,320]{2,1,0:T(8,128)S(1)}, u32[]{:S(2)}, u32[]{:S(2)}) %collective-permute-start.17) | collective-permute-done | bytes 81952 | tf_op jit(solution)/shard_map/ppermute | solution.py:55
  155.7 1.6 fusion.30
  (323 shorter events, 21.2 us)
Async XLA Ops:
  2.1 8.0 %copy-start.14 = (f32[4,64,256]{2,1,0:T(8,128)S(1)}, f32[4,64,256]{2,1,0:T(8,128)}, u32[]{:S(2)}) copy-start(f32[4,64,256]{2,1,0:T(8,128)} %param.7) | copy-start | bytes 786436
  2.1 8.0 %copy-start.16 = (f32[4,64,256]{2,1,0:T(8,128)S(1)}, f32[4,64,256]{2,1,0:T(8,128)}, u32[]{:S(2)}) copy-start(f32[4,64,256]{2,1,0:T(8,128)} %param.6) | copy-start | bytes 786436
  2.1 8.0 %copy-start.18 = (f32[4,64,256]{2,1,0:T(8,128)S(1)}, f32[4,64,256]{2,1,0:T(8,128)}, u32[]{:S(2)}) copy-start(f32[4,64,256]{2,1,0:T(8,128)} %param.5) | copy-start | bytes 786436
  2.2 8.0 %copy-start.20 = (f32[4,64,256]{2,1,0:T(8,128)S(1)}, f32[4,64,256]{2,1,0:T(8,128)}, u32[]{:S(2)}) copy-start(f32[4,64,256]{2,1,0:T(8,128)} %param.4) | copy-start | bytes 786436
  2.4 7.5 %collective-permute-start.1 = (f32[4,4,16,128]{3,2,1,0:T(8,128)S(1)}, f32[4,4,16,128]{3,2,1,0:T(8,128)S(1)}, u32[]{:S(2)}, u32[]{:S(2)}) collective-permute-start(f32[4,4,16,128]{3,2,1,0:T(8,128)S(1)} %copy.42), channel_id=1, source_target_pairs={{1,0},{2,1},{3,2},{0,3},{5,4},{6,5},{7,6},{4,7},{9,8},{10,9},{11,1... | collective-permute-start | bytes 393224 | tf_op jit(solution)/shard_map/ppermute | solution.py:42
  5.0 4.7 %collective-permute-start = (f32[4,4,16,128]{3,2,1,0:T(8,128)S(1)}, f32[4,4,16,128]{3,2,1,0:T(8,128)S(1)}, u32[]{:S(2)}, u32[]{:S(2)}) collective-permute-start(f32[4,4,16,128]{3,2,1,0:T(8,128)S(1)} %copy.41), channel_id=1, source_target_pairs={{0,1},{1,2},{2,3},{3,0},{4,5},{5,6},{6,7},{7,4},{8,9},{9,10},{10,1... | collective-permute-start | bytes 393224 | tf_op jit(solution)/shard_map/ppermute | solution.py:41
  5.1 48.5 %copy-start.71 = (pred[64]{0:T(512)(128)(4,1)}, pred[64]{0:T(512)(128)(4,1)S(1)}, u32[]{:S(2)}) copy-start(pred[64]{0:T(512)(128)(4,1)S(1)} %compare_and_fusion.5) | copy-start | bytes 196
  6.9 20.5 %copy-start.75 = (s32[64]{0:T(128)}, s32[64]{0:T(128)S(1)}, u32[]{:S(2)}) copy-start(s32[64]{0:T(128)S(1)} %get-tuple-element.145) | copy-start | bytes 772
  6.9 46.7 %copy-start.73 = (s32[64]{0:T(128)}, s32[64]{0:T(128)S(1)}, u32[]{:S(2)}) copy-start(s32[64]{0:T(128)S(1)} %get-tuple-element.144) | copy-start | bytes 772
  9.1 16.7 %copy-start.87 = (s32[320]{0:T(512)}, s32[320]{0:T(512)S(1)}, u32[]{:S(2)}) copy-start(s32[320]{0:T(512)S(1)} %get-tuple-element.142) | copy-start | bytes 3844
  9.9 3.3 %copy-start = (f32[4,4,64,32]{3,2,1,0:T(8,128)}, f32[4,4,64,32]{3,2,1,0:T(8,128)S(1)}, u32[]{:S(2)}) copy-start(f32[4,4,64,32]{3,2,1,0:T(8,128)S(1)} %reshape.137) | copy-start | bytes 393220
  10.1 3.1 %copy-start.2 = (f32[4,4,64,32]{3,2,1,0:T(8,128)}, f32[4,4,64,32]{3,2,1,0:T(8,128)S(1)}, u32[]{:S(2)}) copy-start(f32[4,4,64,32]{3,2,1,0:T(8,128)S(1)} %reshape.139) | copy-start | bytes 393220
  10.1 3.1 %copy-start.21 = (f32[4,64,256]{2,1,0:T(8,128)S(1)}, f32[4,64,256]{2,1,0:T(8,128)}, u32[]{:S(2)}) copy-start(f32[4,64,256]{2,1,0:T(8,128)} %param.4) | copy-start | bytes 786436
  10.3 2.2 %copy-start.8 = (f32[1,64,320]{2,1,0:T(8,128)}, f32[1,64,320]{2,1,0:T(8,128)S(1)}, u32[]{:S(2)}) copy-start(f32[1,64,320]{2,1,0:T(8,128)S(1)} %get-tuple-element.19) | copy-start | bytes 245764
  10.3 2.2 %copy-start.11 = (f32[1,64,320]{2,1,0:T(8,128)}, f32[1,64,320]{2,1,0:T(8,128)S(1)}, u32[]{:S(2)}) copy-start(f32[1,64,320]{2,1,0:T(8,128)S(1)} %get-tuple-element.20) | copy-start | bytes 245764
  17.2 12.9 %collective-permute-start.2 = (f32[1,2,64,320]{3,2,1,0:T(8,128)}, f32[1,2,64,320]{3,2,1,0:T(8,128)}, u32[]{:S(2)}, u32[]{:S(2)}) collective-permute-start(f32[1,2,64,320]{3,2,1,0:T(8,128)} %get-tuple-element.27), channel_id=1, source_target_pairs={{0,4},{4,8},{8,12},{12,16},{16,20},{20,24},{24,28},{1,5},{5,9},{9,... | collective-permute-start | bytes 491528 | tf_op jit(solution)/shard_map/ppermute | solution.py:55
  21.3 8.8 %collective-permute-start.3 = (f32[1,2,64,320]{3,2,1,0:T(8,128)}, f32[1,2,64,320]{3,2,1,0:T(8,128)}, u32[]{:S(2)}, u32[]{:S(2)}) collective-permute-start(f32[1,2,64,320]{3,2,1,0:T(8,128)} %get-tuple-element.28), channel_id=1, source_target_pairs={{4,0},{8,4},{12,8},{16,12},{20,16},{24,20},{28,24},{5,1},{9,5},{13... | collective-permute-start | bytes 491528 | tf_op jit(solution)/shard_map/ppermute | solution.py:55
  23.3 4.3 %copy-start.92 = (s32[160]{0:T(256)S(1)}, s32[160]{0:T(256)}, u32[]{:S(2)}) copy-start(s32[160]{0:T(256)} %get-tuple-element.146) | copy-start | bytes 1924
  23.3 4.3 %copy-start.95 = (s32[160]{0:T(256)S(1)}, s32[160]{0:T(256)}, u32[]{:S(2)}) copy-start(s32[160]{0:T(256)} %get-tuple-element.147) | copy-start | bytes 1924
  23.3 4.3 %copy-start.101 = (pred[160]{0:T(512)(128)(4,1)S(1)}, pred[160]{0:T(512)(128)(4,1)}, u32[]{:S(2)}) copy-start(pred[160]{0:T(512)(128)(4,1)} %compare_and_fusion) | copy-start | bytes 484
  27.2 27.2 %copy-start.39 = (f32[32,2,160]{2,0,1:T(8,128)}, f32[32,2,160]{2,0,1:T(8,128)S(1)}, u32[]{:S(2)}) copy-start(f32[32,2,160]{2,0,1:T(8,128)S(1)} %get-tuple-element.137) | copy-start | bytes 122884
  27.4 27.0 %copy-start.42 = (f32[32,2,160]{2,0,1:T(8,128)}, f32[32,2,160]{2,0,1:T(8,128)S(1)}, u32[]{:S(2)}) copy-start(f32[32,2,160]{2,0,1:T(8,128)S(1)} %get-tuple-element.139) | copy-start | bytes 122884
  27.6 26.8 %copy-start.45 = (f32[32,2,160]{2,0,1:T(8,128)}, f32[32,2,160]{2,0,1:T(8,128)S(1)}, u32[]{:S(2)}) copy-start(f32[32,2,160]{2,0,1:T(8,128)S(1)} %get-tuple-element.141) | copy-start | bytes 122884
  27.9 2.1 %copy-start.78 = (pred[32]{0:T(512)(128)(4,1)S(1)}, pred[32]{0:T(512)(128)(4,1)}, u32[]{:S(2)}) copy-start(pred[32]{0:T(512)(128)(4,1)} %compare_and_fusion.1) | copy-start | bytes 100
  27.9 2.0 %copy-start.81 = (s32[32]{0:T(128)S(1)}, s32[32]{0:T(128)}, u32[]{:S(2)}) copy-start(s32[32]{0:T(128)} %get-tuple-element.148) | copy-start | bytes 388
  27.9 2.0 %copy-start.84 = (s32[32]{0:T(128)S(1)}, s32[32]{0:T(128)}, u32[]{:S(2)}) copy-start(s32[32]{0:T(128)} %get-tuple-element.149) | copy-start | bytes 388
  31.6 12.9 %copy-start.6 = (f32[4,64,320]{2,1,0:T(8,128)}, f32[4,64,320]{2,1,0:T(8,128)S(1)}, u32[]{:S(2)}) copy-start(f32[4,64,320]{2,1,0:T(8,128)S(1)} %get-tuple-element.14) | copy-start | bytes 983044
  31.8 2.5 %copy-start.12 = (f32[1,64,320]{2,1,0:T(8,128)S(1)}, f32[1,64,320]{2,1,0:T(8,128)}, u32[]{:S(2)}) copy-start(f32[1,64,320]{2,1,0:T(8,128)} %copy-done.11) | copy-start | bytes 245764
  31.9 2.6 %copy-start.62 = (f32[1,64,319]{2,1,0:T(8,128)S(1)}, f32[1,64,319]{2,1,0:T(8,128)}, u32[]{:S(2)}) copy-start(f32[1,64,319]{2,1,0:T(8,128)} %get-tuple-element.120) | copy-start | bytes 244996
  31.9 2.6 %copy-start.63 = (f32[1,64,319]{2,1,0:T(8,128)S(1)}, f32[1,64,319]{2,1,0:T(8,128)}, u32[]{:S(2)}) copy-start(f32[1,64,319]{2,1,0:T(8,128)} %get-tuple-element.121) | copy-start | bytes 244996
  31.9 2.6 %copy-start.64 = (f32[1,63,320]{2,1,0:T(8,128)S(1)}, f32[1,63,320]{2,1,0:T(8,128)}, u32[]{:S(2)}) copy-start(f32[1,63,320]{2,1,0:T(8,128)} %get-tuple-element.118) | copy-start | bytes 241924
  31.9 2.6 %copy-start.65 = (f32[1,63,320]{2,1,0:T(8,128)S(1)}, f32[1,63,320]{2,1,0:T(8,128)}, u32[]{:S(2)}) copy-start(f32[1,63,320]{2,1,0:T(8,128)} %get-tuple-element.119) | copy-start | bytes 241924
  33.0 11.4 %collective-permute-start.5 = (f32[1,64,320]{2,1,0:T(8,128)S(1)}, f32[1,64,320]{2,1,0:T(8,128)S(1)}, u32[]{:S(2)}, u32[]{:S(2)}) collective-permute-start(f32[1,64,320]{2,1,0:T(8,128)S(1)} %fusion.198), channel_id=1, source_target_pairs={{4,0},{8,4},{12,8},{16,12},{20,16},{24,20},{28,24},{5,1},{9,5},{13... | collective-permute-start | bytes 245768 | tf_op jit(solution)/shard_map/ppermute | solution.py:55
  34.4 6.4 %copy-start.58 = (f32[2,63,320]{2,1,0:T(8,128)S(1)}, f32[2,63,320]{2,1,0:T(8,128)}, u32[]{:S(2)}) copy-start(f32[2,63,320]{2,1,0:T(8,128)} %get-tuple-element.90) | copy-start | bytes 483844
  34.5 6.4 %copy-start.59 = (f32[2,63,320]{2,1,0:T(8,128)S(1)}, f32[2,63,320]{2,1,0:T(8,128)}, u32[]{:S(2)}) copy-start(f32[2,63,320]{2,1,0:T(8,128)} %get-tuple-element.91) | copy-start | bytes 483844
  34.5 6.4 %copy-start.60 = (f32[2,64,319]{2,1,0:T(8,128)S(1)}, f32[2,64,319]{2,1,0:T(8,128)}, u32[]{:S(2)}) copy-start(f32[2,64,319]{2,1,0:T(8,128)} %get-tuple-element.92) | copy-start | bytes 489988
  34.5 6.4 %copy-start.61 = (f32[2,64,319]{2,1,0:T(8,128)S(1)}, f32[2,64,319]{2,1,0:T(8,128)}, u32[]{:S(2)}) copy-start(f32[2,64,319]{2,1,0:T(8,128)} %get-tuple-element.93) | copy-start | bytes 489988
  35.6 7.4 %collective-permute-start.4 = (f32[1,64,320]{2,1,0:T(8,128)S(1)}, f32[1,64,320]{2,1,0:T(8,128)S(1)}, u32[]{:S(2)}, u32[]{:S(2)}) collective-permute-start(f32[1,64,320]{2,1,0:T(8,128)S(1)} %fusion.186), channel_id=1, source_target_pairs={{0,4},{4,8},{8,12},{12,16},{16,20},{20,24},{24,28},{1,5},{5,9},{9,... | collective-permute-start | bytes 245768 | tf_op jit(solution)/shard_map/ppermute | solution.py:55
  41.6 10.8 %copy-start.37 = (f32[2,64,320]{2,1,0:T(8,128)}, f32[2,64,320]{2,1,0:T(8,128)S(1)}, u32[]{:S(2)}) copy-start(f32[2,64,320]{2,1,0:T(8,128)S(1)} %fusion.87) | copy-start | bytes 491524
  43.1 9.3 %copy-start.52 = (f32[1,64,320]{2,1,0:T(8,128)}, f32[1,64,320]{2,1,0:T(8,128)S(1)}, u32[]{:S(2)}) copy-start(f32[1,64,320]{2,1,0:T(8,128)S(1)} %fusion.175) | copy-start | bytes 245764
  43.1 7.4 %collective-permute-start.7 = (f32[1,64,320]{2,1,0:T(8,128)S(1)}, f32[1,64,320]{2,1,0:T(8,128)S(1)}, u32[]{:S(2)}, u32[]{:S(2)}) collective-permute-start(f32[1,64,320]{2,1,0:T(8,128)S(1)} %fusion.175), channel_id=1, source_target_pairs={{4,0},{8,4},{12,8},{16,12},{20,16},{24,20},{28,24},{5,1},{9,5},{13... | collective-permute-start | bytes 245768 | tf_op jit(solution)/shard_map/ppermute | solution.py:55
  44.6 7.8 %copy-start.54 = (f32[1,64,320]{2,1,0:T(8,128)}, f32[1,64,320]{2,1,0:T(8,128)S(1)}, u32[]{:S(2)}) copy-start(f32[1,64,320]{2,1,0:T(8,128)S(1)} %fusion.165) | copy-start | bytes 245764
  44.6 7.8 %collective-permute-start.6 = (f32[1,64,320]{2,1,0:T(8,128)S(1)}, f32[1,64,320]{2,1,0:T(8,128)S(1)}, u32[]{:S(2)}, u32[]{:S(2)}) collective-permute-start(f32[1,64,320]{2,1,0:T(8,128)S(1)} %fusion.165), channel_id=1, source_target_pairs={{0,4},{4,8},{8,12},{12,16},{16,20},{20,24},{24,28},{1,5},{5,9},{9,... | collective-permute-start | bytes 245768 | tf_op jit(solution)/shard_map/ppermute | solution.py:55
  57.8 17.7 %collective-permute-start.8 = (f32[2,160,128]{2,1,0:T(8,128)}, f32[2,160,128]{2,1,0:T(8,128)}, u32[]{:S(2)}, u32[]{:S(2)}) collective-permute-start(f32[2,160,128]{2,1,0:T(8,128)} %reshape.141), channel_id=1, source_target_pairs={{0,8},{4,12},{8,16},{12,20},{16,24},{20,28},{1,9},{5,13},{9,17},{1... | collective-permute-start | bytes 491528 | tf_op jit(solution)/shard_map/ppermute | solution.py:55
  67.7 20.2 %collective-permute-start.11 = (f32[2,160,128]{2,1,0:T(8,128)}, f32[2,160,128]{2,1,0:T(8,128)}, u32[]{:S(2)}, u32[]{:S(2)}) collective-permute-start(f32[2,160,128]{2,1,0:T(8,128)} %reshape.141), channel_id=1, source_target_pairs={{8,0},{12,4},{16,8},{20,12},{24,16},{28,20},{9,1},{13,5},{17,9},{2... | collective-permute-start | bytes 491528 | tf_op jit(solution)/shard_map/ppermute | solution.py:55
  69.0 15.3 %collective-permute-start.10 = (f32[2,160,128]{2,1,0:T(8,128)}, f32[2,160,128]{2,1,0:T(8,128)}, u32[]{:S(2)}, u32[]{:S(2)}) collective-permute-start(f32[2,160,128]{2,1,0:T(8,128)} %reshape.141), channel_id=1, source_target_pairs={{4,0},{8,4},{12,8},{16,12},{20,16},{24,20},{28,24},{5,1},{9,5},{13... | collective-permute-start | bytes 491528 | tf_op jit(solution)/shard_map/ppermute | solution.py:55
  70.3 8.8 %collective-permute-start.9 = (f32[2,160,128]{2,1,0:T(8,128)}, f32[2,160,128]{2,1,0:T(8,128)}, u32[]{:S(2)}, u32[]{:S(2)}) collective-permute-start(f32[2,160,128]{2,1,0:T(8,128)} %reshape.141), channel_id=1, source_target_pairs={{0,4},{4,8},{8,12},{12,16},{16,20},{20,24},{24,28},{1,5},{5,9},{9,... | collective-permute-start | bytes 491528 | tf_op jit(solution)/shard_map/ppermute | solution.py:55
  92.6 2.6 %copy-start.4 = (f32[8,31,160]{2,1,0:T(8,128)}, f32[8,31,160]{2,1,0:T(8,128)S(1)}, u32[]{:S(2)}) copy-start(f32[8,31,160]{2,1,0:T(8,128)S(1)} %fusion.31) | copy-start | bytes 476164
  93.3 2.0 %copy-start.29 = (f32[8,1,32,160]{3,2,0,1:T(8,128)}, f32[8,1,32,160]{3,2,0,1:T(8,128)S(1)}, u32[]{:S(2)}) copy-start(f32[8,1,32,160]{3,2,0,1:T(8,128)S(1)} %get-tuple-element.10) | copy-start | bytes 491524
  93.3 2.0 %copy-start.31 = (f32[8,1,32,160]{3,2,0,1:T(8,128)}, f32[8,1,32,160]{3,2,0,1:T(8,128)S(1)}, u32[]{:S(2)}) copy-start(f32[8,1,32,160]{3,2,0,1:T(8,128)S(1)} %get-tuple-element.11) | copy-start | bytes 491524
  100.2 14.9 %all-to-all-start = ((f32[8,1,40,128]{3,2,1,0:T(8,128)}), f32[8,1,40,128]{3,2,1,0:T(8,128)}, u32[]{:S(2)}, u32[]{:S(2)}) async-start(f32[8,1,40,128]{3,2,1,0:T(8,128)} %broadcast_in_dim.21), calls=%async_computation | async-start | bytes 327680 | tf_op jit(solution)/shard_map/all_to_all | solution.py:75
  116.9 2.2 %copy-start.48 = (f32[8,4,16,80]{3,2,1,0:T(8,128)S(1)}, f32[8,4,16,80]{3,2,1,0:T(8,128)}, u32[]{:S(2)}) copy-start(f32[8,4,16,80]{3,2,1,0:T(8,128)} %reshape.146) | copy-start | bytes 491524
  121.0 2.5 %copy-start.72 = (pred[64]{0:T(512)(128)(4,1)S(1)}, pred[64]{0:T(512)(128)(4,1)}, u32[]{:S(2)}) copy-start(pred[64]{0:T(512)(128)(4,1)} %copy-done.71) | copy-start | bytes 196
  121.0 2.5 %copy-start.74 = (s32[64]{0:T(128)S(1)}, s32[64]{0:T(128)}, u32[]{:S(2)}) copy-start(s32[64]{0:T(128)} %copy-done.73) | copy-start | bytes 772
  121.0 2.5 %copy-start.77 = (s32[64]{0:T(128)S(1)}, s32[64]{0:T(128)}, u32[]{:S(2)}) copy-start(s32[64]{0:T(128)} %copy-done.75) | copy-start | bytes 772
  125.2 5.2 %copy-start.10 = (f32[1,64,320]{2,1,0:T(8,128)S(1)}, f32[1,64,320]{2,1,0:T(8,128)}, u32[]{:S(2)}) copy-start(f32[1,64,320]{2,1,0:T(8,128)} %copy-done.8) | copy-start | bytes 245764
  125.3 14.1 %copy-start.13 = (f32[1,64,320]{2,1,0:T(8,128)S(1)}, f32[1,64,320]{2,1,0:T(8,128)}, u32[]{:S(2)}) copy-start(f32[1,64,320]{2,1,0:T(8,128)} %copy-done.11) | copy-start | bytes 245764
  125.3 5.0 %collective-permute-start.12 = (f32[1,64,320]{2,1,0:T(8,128)S(1)}, f32[1,64,320]{2,1,0:T(8,128)S(1)}, u32[]{:S(2)}, u32[]{:S(2)}) collective-permute-start(f32[1,64,320]{2,1,0:T(8,128)S(1)} %slice.1291), channel_id=1, source_target_pairs={{0,4},{4,8},{8,12},{12,16},{16,20},{20,24},{24,28},{1,5},{5,9},{9,... | collective-permute-start | bytes 245768 | tf_op jit(solution)/shard_map/ppermute | solution.py:55
  130.5 14.0 %collective-permute-start.15 = (f32[1,64,320]{2,1,0:T(8,128)S(1)}, f32[1,64,320]{2,1,0:T(8,128)S(1)}, u32[]{:S(2)}, u32[]{:S(2)}) collective-permute-start(f32[1,64,320]{2,1,0:T(8,128)S(1)} %get-tuple-element.37), channel_id=1, source_target_pairs={{4,0},{8,4},{12,8},{16,12},{20,16},{24,20},{28,24},{5,1},{9,5},{13... | collective-permute-start | bytes 245768 | tf_op jit(solution)/shard_map/ppermute | solution.py:55
  131.9 7.5 %collective-permute-start.13 = (f32[1,64,320]{2,1,0:T(8,128)S(1)}, f32[1,64,320]{2,1,0:T(8,128)S(1)}, u32[]{:S(2)}, u32[]{:S(2)}) collective-permute-start(f32[1,64,320]{2,1,0:T(8,128)S(1)} %get-tuple-element.38), channel_id=1, source_target_pairs={{4,0},{8,4},{12,8},{16,12},{20,16},{24,20},{28,24},{5,1},{9,5},{13... | collective-permute-start | bytes 245768 | tf_op jit(solution)/shard_map/ppermute | solution.py:55
  139.5 9.3 %collective-permute-start.14 = (f32[1,64,320]{2,1,0:T(8,128)S(1)}, f32[1,64,320]{2,1,0:T(8,128)S(1)}, u32[]{:S(2)}, u32[]{:S(2)}) collective-permute-start(f32[1,64,320]{2,1,0:T(8,128)S(1)} %fusion.145), channel_id=1, source_target_pairs={{0,4},{4,8},{8,12},{12,16},{16,20},{20,24},{24,28},{1,5},{5,9},{9,... | collective-permute-start | bytes 245768 | tf_op jit(solution)/shard_map/ppermute | solution.py:55
  144.7 6.1 %collective-permute-start.16 = (f32[1,64,320]{2,1,0:T(8,128)S(1)}, f32[1,64,320]{2,1,0:T(8,128)S(1)}, u32[]{:S(2)}, u32[]{:S(2)}) collective-permute-start(f32[1,64,320]{2,1,0:T(8,128)S(1)} %fusion.125), channel_id=1, source_target_pairs={{0,4},{4,8},{8,12},{12,16},{16,20},{20,24},{24,28},{1,5},{5,9},{9,... | collective-permute-start | bytes 245768 | tf_op jit(solution)/shard_map/ppermute | solution.py:55
  149.0 6.5 %collective-permute-start.17 = (f32[1,64,320]{2,1,0:T(8,128)S(1)}, f32[1,64,320]{2,1,0:T(8,128)S(1)}, u32[]{:S(2)}, u32[]{:S(2)}) collective-permute-start(f32[1,64,320]{2,1,0:T(8,128)S(1)} %fusion.135), channel_id=1, source_target_pairs={{4,0},{8,4},{12,8},{16,12},{20,16},{24,20},{28,24},{5,1},{9,5},{13... | collective-permute-start | bytes 245768 | tf_op jit(solution)/shard_map/ppermute | solution.py:55
  150.5 5.1 %copy-start.56 = (f32[4,64,320]{2,1,0:T(8,128)S(1)}, f32[4,64,320]{2,1,0:T(8,128)}, u32[]{:S(2)}) copy-start(f32[4,64,320]{2,1,0:T(8,128)} %get-tuple-element.21) | copy-start | bytes 983044
  (59 other events, 78.5 us)

commit v15 on v13

--- a/solution.py
+++ b/solution.py
@@ -174,6 +174,15 @@
     coef_two = [coarsen(part) for part in (wide_alt, wide_inc, wide_raan)]
     coef_three = [coarsen(part) for part in coef_two]
 
+    coef_two_x = alt_extend(jnp.stack(coef_two, 1), SWEEPS + 2)
+    weights_two = make_weights(
+        coef_two_x[:, 0],
+        trim(coef_two_x[:, 1], SWEEPS + 2, SWEEPS + 1),
+        trim(coef_two_x[:, 2], SWEEPS + 2, SWEEPS + 1),
+        0.25,
+        SWEEPS + 1,
+    )
+
     first = alt_extend(wide[:, 0:2], 1)
     source_x = first[:, 0]
     weights_one = make_weights(first[:, 1], wide_inc, wide_raan, 1.0, 0)
@@ -183,15 +192,7 @@
     applied, density = apply_op(weights_one, alt_extend(density, 1), 1)
     rhs_two = coarsen(wide_source - applied)
 
-    level_two = alt_extend(jnp.stack([rhs_two] + coef_two, 1), SWEEPS + 2)
-    weights_two = make_weights(
-        level_two[:, 1],
-        trim(level_two[:, 2], SWEEPS + 2, SWEEPS + 1),
-        trim(level_two[:, 3], SWEEPS + 2, SWEEPS + 1),
-        0.25,
-        SWEEPS + 1,
-    )
-    rhs_two_x = trim(level_two[:, 0], SWEEPS + 2, SWEEPS + 1)
+    rhs_two_x = alt_extend(rhs_two, SWEEPS + 1)
     correction = first_sweep(weights_two, rhs_two_x, SWEEPS + 1)
     correction = sweep(weights_two, correction, SWEEPS + 1, rhs_two_x, SWEEPS + 1)
     applied, _ = apply_op(weights_two, trim(correction, SWEEPS, 1), 1)

time: 136 us -> 151 us (1.11)
  starting transfers between devices: 55 us -> 68.5 us
  local copies, waits for them, and re-layouts: 13.9 us -> 16.8 us
    ppermute x8 -> x10, starting transfers between devices: 27.5 us -> 36.4 us  [alt_extend(): below.insert(0, lax.ppermute(values[low:], 'alt', up))]
    ppermute x8 -> x10, starting transfers between devices: 20.8 us -> 26.1 us  [alt_extend(): above.append(lax.ppermute(values[:high], 'alt', down))]
    ppermute x8 -> x10, waiting for transfers between devices: 16.2 us -> 19.3 us  [alt_extend(): above.append(lax.ppermute(values[:high], 'alt', down))]
    unnamed x180 -> x174, local copies, waits for them, and re-layouts: 3.28 us -> 6.21 us
    add x12, other arithmetic: 4.03 us -> 2.18 us  [split_sweep(): rows.append(centre + OMEGA * (aim - applied) / diagonal)]
    all_to_all x1, waiting for transfers between devices: 5.2 us -> 3.5 us  [spread_gather(): every = lax.all_to_all(copies, 'alt', 0, 0)]
    concatenate x0 -> x1, other arithmetic: none -> 1.59 us  [alt_extend(): return jnp.concatenate(below + [values] + above, axis=0)]
    all_to_all x1, starting transfers between devices: 5.7 us -> 4.19 us  [spread_gather(): every = lax.all_to_all(copies, 'alt', 0, 0)]
  transfers between devices with their start and end apart: 19 -> 23, of which waited for: 12 -> 13; matrix products, arithmetic and copies ran while one was open for 12% -> 7% of each run, Pallas kernels for 0% -> 0%
where the time goes in v15:
time: 151 us; the launch traced here: 149 us
  starting transfers between devices  68.5 us (45%)
  waiting for transfers between devices  33 us (22%)
  other arithmetic  20.4 us (14%)
  local copies, waits for them, and re-layouts  16.8 us (11%)
  matrix products  7.63 us (5%)
  between operations  2.44 us (2%)
    ppermute x10, starting transfers between devices, alt_extend(): below.insert(0, lax.ppermute(values[low:], 'alt', up))  36.4 us
    ppermute x10, starting transfers between devices, alt_extend(): above.append(lax.ppermute(values[:high], 'alt', down))  26.1 us
    ppermute x10, waiting for transfers between devices, alt_extend(): above.append(lax.ppermute(values[:high], 'alt', down))  19.3 us
    ppermute x10, waiting for transfers between devices, alt_extend(): below.insert(0, lax.ppermute(values[low:], 'alt', up))  10.2 us
    unnamed x174, local copies, waits for them, and re-layouts  6.21 us
    dot_general x8, matrix products, coarsen(): summed = jnp.matmul(summed, pairing(length), precision=HIGH)  5.09 us
    all_to_all x1, starting transfers between devices, spread_gather(): every = lax.all_to_all(copies, 'alt', 0, 0)  4.19 us
    slice x20, local copies, waits for them, and re-layouts, lane_shifts(): left = jnp.concatenate([zero, values[..., :-1]], axis=-1)  4.01 us
  transfers between devices with their start and end apart: 23, of which 13 were waited for; matrix products, arithmetic and copies ran while one was open for 7% of the time, Pallas kernels for 0%

profile of v15, /device:TPU:8, one launch (start us, length us, event | category | flops | bytes accessed | tf_op | source)
XLA Modules:
  0.0 148.8 jit_solution(497428172581116039)
XLA Ops:
  0.6 1.3 pad_maximum_fusion.1
  2.6 1.8 %collective-permute-start.1 = (f32[4,4,16,128]{3,2,1,0:T(8,128)S(1)}, f32[4,4,16,128]{3,2,1,0:T(8,128)S(1)}, u32[]{:S(2)}, u32[]{:S(2)}) collective-permute-start(f32[4,4,16,128]{3,2,1,0:T(8,128)S(1)} %copy.29), channel_id=1, source_target_pairs={{1,0},{2,1},{3,2},{0,3},{5,4},{6,5},{7,6},{4,7},{9,8},{10,9},{11,1... | collective-permute-start | bytes 393224 | tf_op jit(solution)/shard_map/ppermute | solution.py:42
  4.4 0.5 fusion.318
  4.9 0.6 iota_shift-right-logical_fusion.1
  6.0 0.6 broadcast_add_fusion.2
  7.1 0.6 compare_and_fusion.2
  7.7 0.6 iota_shift-right-logical_fusion
  8.7 1.8 %pad_maximum_fusion = f32[4,4,64,320]{3,2,0,1:T(8,128)S(1)} fusion(f32[4,1,64,256]{3,2,0,1:T(8,128)S(1)} %bitcast.402, f32[4,1,64,256]{3,2,0,1:T(8,128)S(1)} %bitcast.407, f32[4,1,64,256]{3,2,0,1:T(8,128)S(1)} %bitcast.412, f32[4,1,64,256]{3,2,0,1:T(8,128)} %bitcast.417, f32[4,4,64,32]{3,2,1,0:T(8,128)S(1)} %reshape.112, f32[4,4,64,32]{3,2,1,0:T(8,128)S(1)} %reshape.114), kind=kLoop, calls=%fused_computation | loop fusion | flops 1638400 | bytes 2621440 | tf_op jit(solution)/shard_map/concatenate | solution.py:43
  10.7 1.0 slice_bitcast_fusion
  11.7 0.8 slice_bitcast_fusion.11
  12.5 0.7 fusion.380
  13.2 0.7 fusion.379
  13.9 0.8 fusion.366
  14.8 0.8 fusion.365
  15.5 0.7 fusion.376
  16.3 0.7 fusion.375
  17.0 0.7 reduce_sum.75
  17.7 1.4 fusion.329
  19.1 1.1 fusion.331
  20.6 1.1 fusion.333
  22.0 3.6 %collective-permute-start.12 = (f32[2,3,32,160]{3,2,0,1:T(8,128)S(1)}, f32[2,3,32,160]{3,2,0,1:T(8,128)S(1)}, u32[]{:S(2)}, u32[]{:S(2)}) collective-permute-start(f32[2,3,32,160]{3,2,0,1:T(8,128)S(1)} %pad_maximum_fusion.19), channel_id=1, source_target_pairs={{0,8},{4,12},{8,16},{12,20},{16,24},{20,28},{1,9},{5,13},{9,17},{1... | collective-permute-start | bytes 368648 | tf_op jit(solution)/shard_map/ppermute | solution.py:54
  25.6 3.4 %collective-permute-start.13 = (f32[2,3,32,160]{3,2,0,1:T(8,128)S(1)}, f32[2,3,32,160]{3,2,0,1:T(8,128)S(1)}, u32[]{:S(2)}, u32[]{:S(2)}) collective-permute-start(f32[2,3,32,160]{3,2,0,1:T(8,128)S(1)} %pad_maximum_fusion.19), channel_id=1, source_target_pairs={{0,4},{4,8},{8,12},{12,16},{16,20},{20,24},{24,28},{1,5},{5,9},{9,... | collective-permute-start | bytes 368648 | tf_op jit(solution)/shard_map/ppermute | solution.py:54
  29.1 3.3 %collective-permute-start.14 = (f32[2,3,32,160]{3,2,0,1:T(8,128)S(1)}, f32[2,3,32,160]{3,2,0,1:T(8,128)S(1)}, u32[]{:S(2)}, u32[]{:S(2)}) collective-permute-start(f32[2,3,32,160]{3,2,0,1:T(8,128)S(1)} %pad_maximum_fusion.19), channel_id=1, source_target_pairs={{4,0},{8,4},{12,8},{16,12},{20,16},{24,20},{28,24},{5,1},{9,5},{13... | collective-permute-start | bytes 368648 | tf_op jit(solution)/shard_map/ppermute | solution.py:55
  32.4 1.9 %collective-permute-start.15 = (f32[2,3,32,160]{3,2,0,1:T(8,128)S(1)}, f32[2,3,32,160]{3,2,0,1:T(8,128)S(1)}, u32[]{:S(2)}, u32[]{:S(2)}) collective-permute-start(f32[2,3,32,160]{3,2,0,1:T(8,128)S(1)} %pad_maximum_fusion.19), channel_id=1, source_target_pairs={{8,0},{12,4},{16,8},{20,12},{24,16},{28,20},{9,1},{13,5},{17,9},{2... | collective-permute-start | bytes 368648 | tf_op jit(solution)/shard_map/ppermute | solution.py:55
  34.6 1.9 %collective-permute-start.3 = (f32[1,2,64,320]{3,2,1,0:T(8,128)S(1)}, f32[1,2,64,320]{3,2,1,0:T(8,128)S(1)}, u32[]{:S(2)}, u32[]{:S(2)}) collective-permute-start(f32[1,2,64,320]{3,2,1,0:T(8,128)S(1)} %copy-done.63), channel_id=1, source_target_pairs={{4,0},{8,4},{12,8},{16,12},{20,16},{24,20},{28,24},{5,1},{9,5},{13... | collective-permute-start | bytes 491528 | tf_op jit(solution)/shard_map/ppermute | solution.py:55
  37.8 3.9 %collective-permute-start.2 = (f32[1,2,64,320]{3,2,1,0:T(8,128)S(1)}, f32[1,2,64,320]{3,2,1,0:T(8,128)S(1)}, u32[]{:S(2)}, u32[]{:S(2)}) collective-permute-start(f32[1,2,64,320]{3,2,1,0:T(8,128)S(1)} %copy-done.62), channel_id=1, source_target_pairs={{0,4},{4,8},{8,12},{12,16},{16,20},{20,24},{24,28},{1,5},{5,9},{9,... | collective-permute-start | bytes 491528 | tf_op jit(solution)/shard_map/ppermute | solution.py:54
  41.9 2.0 %collective-permute-done.15 = f32[2,3,32,160]{3,2,0,1:T(8,128)S(1)} collective-permute-done((f32[2,3,32,160]{3,2,0,1:T(8,128)S(1)}, f32[2,3,32,160]{3,2,0,1:T(8,128)S(1)}, u32[]{:S(2)}, u32[]{:S(2)}) %collective-permute-start.15) | collective-permute-done | bytes 122912 | tf_op jit(solution)/shard_map/ppermute | solution.py:55
  44.2 4.6 %collective-permute-done.3 = f32[1,2,64,320]{3,2,1,0:T(8,128)S(1)} collective-permute-done((f32[1,2,64,320]{3,2,1,0:T(8,128)S(1)}, f32[1,2,64,320]{3,2,1,0:T(8,128)S(1)}, u32[]{:S(2)}, u32[]{:S(2)}) %collective-permute-start.3) | collective-permute-done | bytes 163872 | tf_op jit(solution)/shard_map/ppermute | solution.py:55
  49.3 0.7 copy-done.1
  51.0 0.6 copy-done.47
  53.2 2.9 %collective-permute-start.5 = (f32[1,64,320]{2,1,0:T(8,128)S(1)}, f32[1,64,320]{2,1,0:T(8,128)S(1)}, u32[]{:S(2)}, u32[]{:S(2)}) collective-permute-start(f32[1,64,320]{2,1,0:T(8,128)S(1)} %fusion.196), channel_id=1, source_target_pairs={{4,0},{8,4},{12,8},{16,12},{20,16},{24,20},{28,24},{5,1},{9,5},{13... | collective-permute-start | bytes 245768 | tf_op jit(solution)/shard_map/ppermute | solution.py:55
  56.2 3.4 %collective-permute-start.4 = (f32[1,64,320]{2,1,0:T(8,128)S(1)}, f32[1,64,320]{2,1,0:T(8,128)S(1)}, u32[]{:S(2)}, u32[]{:S(2)}) collective-permute-start(f32[1,64,320]{2,1,0:T(8,128)S(1)} %fusion.184), channel_id=1, source_target_pairs={{0,4},{4,8},{8,12},{12,16},{16,20},{20,24},{24,28},{1,5},{5,9},{9,... | collective-permute-start | bytes 245768 | tf_op jit(solution)/shard_map/ppermute | solution.py:54
  59.9 3.7 %collective-permute-done.4 = f32[1,64,320]{2,1,0:T(8,128)S(1)} collective-permute-done((f32[1,64,320]{2,1,0:T(8,128)S(1)}, f32[1,64,320]{2,1,0:T(8,128)S(1)}, u32[]{:S(2)}, u32[]{:S(2)}) %collective-permute-start.4) | collective-permute-done | bytes 81952 | tf_op jit(solution)/shard_map/ppermute | solution.py:54
  63.8 1.9 %collective-permute-start.7 = (f32[1,64,320]{2,1,0:T(8,128)S(1)}, f32[1,64,320]{2,1,0:T(8,128)S(1)}, u32[]{:S(2)}, u32[]{:S(2)}) collective-permute-start(f32[1,64,320]{2,1,0:T(8,128)S(1)} %fusion.173), channel_id=1, source_target_pairs={{4,0},{8,4},{12,8},{16,12},{20,16},{24,20},{28,24},{5,1},{9,5},{13... | collective-permute-start | bytes 245768 | tf_op jit(solution)/shard_map/ppermute | solution.py:55
  65.9 3.9 %collective-permute-start.6 = (f32[1,64,320]{2,1,0:T(8,128)S(1)}, f32[1,64,320]{2,1,0:T(8,128)S(1)}, u32[]{:S(2)}, u32[]{:S(2)}) collective-permute-start(f32[1,64,320]{2,1,0:T(8,128)S(1)} %fusion.163), channel_id=1, source_target_pairs={{0,4},{4,8},{8,12},{12,16},{16,20},{20,24},{24,28},{1,5},{5,9},{9,... | collective-permute-start | bytes 245768 | tf_op jit(solution)/shard_map/ppermute | solution.py:54
  70.1 1.2 collective-permute-done.7
  71.3 2.0 %collective-permute-done.6 = f32[1,64,320]{2,1,0:T(8,128)S(1)} collective-permute-done((f32[1,64,320]{2,1,0:T(8,128)S(1)}, f32[1,64,320]{2,1,0:T(8,128)S(1)}, u32[]{:S(2)}, u32[]{:S(2)}) %collective-permute-start.6) | collective-permute-done | bytes 81952 | tf_op jit(solution)/shard_map/ppermute | solution.py:54
  74.6 4.8 %collective-permute-start.8 = (f32[1,32,160]{2,1,0:T(8,128)S(1)}, f32[1,32,160]{2,1,0:T(8,128)S(1)}, u32[]{:S(2)}, u32[]{:S(2)}) collective-permute-start(f32[1,32,160]{2,1,0:T(8,128)S(1)} %get-tuple-element.130), channel_id=1, source_target_pairs={{0,8},{4,12},{8,16},{12,20},{16,24},{20,28},{1,9},{5,13},{9,17},{1... | collective-permute-start | bytes 61448 | tf_op jit(solution)/shard_map/ppermute | solution.py:54
  79.5 3.0 %collective-permute-start.9 = (f32[2,32,160]{2,1,0:T(8,128)S(1)}, f32[2,32,160]{2,1,0:T(8,128)S(1)}, u32[]{:S(2)}, u32[]{:S(2)}) collective-permute-start(f32[2,32,160]{2,1,0:T(8,128)S(1)} %fusion), channel_id=1, source_target_pairs={{0,4},{4,8},{8,12},{12,16},{16,20},{20,24},{24,28},{1,5},{5,9},{9,... | collective-permute-start | bytes 122888 | tf_op jit(solution)/shard_map/ppermute | solution.py:54
  82.6 3.7 %collective-permute-start.10 = (f32[2,32,160]{2,1,0:T(8,128)S(1)}, f32[2,32,160]{2,1,0:T(8,128)S(1)}, u32[]{:S(2)}, u32[]{:S(2)}) collective-permute-start(f32[2,32,160]{2,1,0:T(8,128)S(1)} %fusion), channel_id=1, source_target_pairs={{4,0},{8,4},{12,8},{16,12},{20,16},{24,20},{28,24},{5,1},{9,5},{13... | collective-permute-start | bytes 122888 | tf_op jit(solution)/shard_map/ppermute | solution.py:55
  86.3 1.9 %collective-permute-start.11 = (f32[1,32,160]{2,1,0:T(8,128)S(1)}, f32[1,32,160]{2,1,0:T(8,128)S(1)}, u32[]{:S(2)}, u32[]{:S(2)}) collective-permute-start(f32[1,32,160]{2,1,0:T(8,128)S(1)} %get-tuple-element.129), channel_id=1, source_target_pairs={{8,0},{12,4},{16,8},{20,12},{24,16},{28,20},{9,1},{13,5},{17,9},{2... | collective-permute-start | bytes 61448 | tf_op jit(solution)/shard_map/ppermute | solution.py:55
  88.7 3.4 %collective-permute-done.11 = f32[1,32,160]{2,1,0:T(8,128)S(1)} collective-permute-done((f32[1,32,160]{2,1,0:T(8,128)S(1)}, f32[1,32,160]{2,1,0:T(8,128)S(1)}, u32[]{:S(2)}, u32[]{:S(2)}) %collective-permute-start.11) | collective-permute-done | bytes 20512 | tf_op jit(solution)/shard_map/ppermute | solution.py:55
  94.5 0.7 broadcast_in_dim.20
  95.3 4.2 %all-to-all-start = ((f32[8,1,4,16,80]{4,3,2,1,0:T(8,128)}), f32[8,1,4,16,80]{4,3,2,1,0:T(8,128)}, u32[]{:S(2)}, u32[]{:S(2)}) async-start(f32[8,1,4,16,80]{4,3,2,1,0:T(8,128)} %broadcast_in_dim.20), calls=%async_computation | async-start | bytes 524288 | tf_op jit(solution)/shard_map/all_to_all | solution.py:62
  99.5 0.6 compare_and_fusion.3
  100.1 0.6 compare_and_fusion.4
  100.6 1.6 %pad_maximum_fusion.20 = f32[6,32,160]{2,1,0:T(8,128)} fusion(f32[2,32,160]{2,1,0:T(8,128)} %copy-done.52, f32[2,32,160]{2,1,0:T(8,128)} %copy-done.24, f32[2,32,160]{2,1,0:T(8,128)} %copy-done.51), kind=kLoop, calls=%fused_computation.180 | loop fusion | flops 61440 | bytes 245760 | tf_op jit(solution)/shard_map/concatenate | solution.py:56
  102.2 3.5 %all-to-all-done = f32[8,1,4,16,80]{4,3,2,1,0:T(8,128)} async-done(((f32[8,1,4,16,80]{4,3,2,1,0:T(8,128)}), f32[8,1,4,16,80]{4,3,2,1,0:T(8,128)}, u32[]{:S(2)}, u32[]{:S(2)}) %all-to-all-start) | async-done | bytes 163872 | tf_op jit(solution)/shard_map/all_to_all | solution.py:62
  105.7 0.9 slice_bitcast_fusion.20
  106.8 1.0 fusion.276
  107.9 0.9 fusion.219
  109.0 0.9 fusion.231
  110.1 1.0 fusion.243
  113.9 0.7 copy-done.5
  114.9 3.5 %collective-permute-start.16 = (f32[1,64,320]{2,1,0:T(8,128)S(1)}, f32[1,64,320]{2,1,0:T(8,128)S(1)}, u32[]{:S(2)}, u32[]{:S(2)}) collective-permute-start(f32[1,64,320]{2,1,0:T(8,128)S(1)} %slice.1276), channel_id=1, source_target_pairs={{0,4},{4,8},{8,12},{12,16},{16,20},{20,24},{24,28},{1,5},{5,9},{9,... | collective-permute-start | bytes 245768 | tf_op jit(solution)/shard_map/ppermute | solution.py:54
  118.5 4.1 %collective-permute-done.16 = f32[1,64,320]{2,1,0:T(8,128)S(1)} collective-permute-done((f32[1,64,320]{2,1,0:T(8,128)S(1)}, f32[1,64,320]{2,1,0:T(8,128)S(1)}, u32[]{:S(2)}, u32[]{:S(2)}) %collective-permute-start.16) | collective-permute-done | bytes 81952 | tf_op jit(solution)/shard_map/ppermute | solution.py:54
  122.7 3.4 %collective-permute-start.19 = (f32[1,64,320]{2,1,0:T(8,128)S(1)}, f32[1,64,320]{2,1,0:T(8,128)S(1)}, u32[]{:S(2)}, u32[]{:S(2)}) collective-permute-start(f32[1,64,320]{2,1,0:T(8,128)S(1)} %get-tuple-element.38), channel_id=1, source_target_pairs={{4,0},{8,4},{12,8},{16,12},{20,16},{24,20},{28,24},{5,1},{9,5},{13... | collective-permute-start | bytes 245768 | tf_op jit(solution)/shard_map/ppermute | solution.py:55
  126.2 1.9 %collective-permute-start.17 = (f32[1,64,320]{2,1,0:T(8,128)S(1)}, f32[1,64,320]{2,1,0:T(8,128)S(1)}, u32[]{:S(2)}, u32[]{:S(2)}) collective-permute-start(f32[1,64,320]{2,1,0:T(8,128)S(1)} %get-tuple-element.39), channel_id=1, source_target_pairs={{4,0},{8,4},{12,8},{16,12},{20,16},{24,20},{28,24},{5,1},{9,5},{13... | collective-permute-start | bytes 245768 | tf_op jit(solution)/shard_map/ppermute | solution.py:55
  128.2 4.6 %collective-permute-done.17 = f32[1,64,320]{2,1,0:T(8,128)S(1)} collective-permute-done((f32[1,64,320]{2,1,0:T(8,128)S(1)}, f32[1,64,320]{2,1,0:T(8,128)S(1)}, u32[]{:S(2)}, u32[]{:S(2)}) %collective-permute-start.17) | collective-permute-done | bytes 81952 | tf_op jit(solution)/shard_map/ppermute | solution.py:55
  133.0 3.4 %collective-permute-start.18 = (f32[1,64,320]{2,1,0:T(8,128)S(1)}, f32[1,64,320]{2,1,0:T(8,128)S(1)}, u32[]{:S(2)}, u32[]{:S(2)}) collective-permute-start(f32[1,64,320]{2,1,0:T(8,128)S(1)} %fusion.143), channel_id=1, source_target_pairs={{0,4},{4,8},{8,12},{12,16},{16,20},{20,24},{24,28},{1,5},{5,9},{9,... | collective-permute-start | bytes 245768 | tf_op jit(solution)/shard_map/ppermute | solution.py:54
  136.5 3.4 %collective-permute-start.20 = (f32[1,64,320]{2,1,0:T(8,128)S(1)}, f32[1,64,320]{2,1,0:T(8,128)S(1)}, u32[]{:S(2)}, u32[]{:S(2)}) collective-permute-start(f32[1,64,320]{2,1,0:T(8,128)S(1)} %fusion.123), channel_id=1, source_target_pairs={{0,4},{4,8},{8,12},{12,16},{16,20},{20,24},{24,28},{1,5},{5,9},{9,... | collective-permute-start | bytes 245768 | tf_op jit(solution)/shard_map/ppermute | solution.py:54
  140.6 3.1 %collective-permute-start.21 = (f32[1,64,320]{2,1,0:T(8,128)S(1)}, f32[1,64,320]{2,1,0:T(8,128)S(1)}, u32[]{:S(2)}, u32[]{:S(2)}) collective-permute-start(f32[1,64,320]{2,1,0:T(8,128)S(1)} %fusion.133), channel_id=1, source_target_pairs={{4,0},{8,4},{12,8},{16,12},{20,16},{24,20},{28,24},{5,1},{9,5},{13... | collective-permute-start | bytes 245768 | tf_op jit(solution)/shard_map/ppermute | solution.py:55
  144.0 3.1 %collective-permute-done.21 = f32[1,64,320]{2,1,0:T(8,128)S(1)} collective-permute-done((f32[1,64,320]{2,1,0:T(8,128)S(1)}, f32[1,64,320]{2,1,0:T(8,128)S(1)}, u32[]{:S(2)}, u32[]{:S(2)}) %collective-permute-start.21) | collective-permute-done | bytes 81952 | tf_op jit(solution)/shard_map/ppermute | solution.py:55
  147.2 1.6 %fusion.31 = (f32[4,64,256]{2,1,0:T(8,128)}, f32[4,64,256]{2,1,0:T(8,128)}) fusion(f32[4,63,320]{2,1,0:T(8,128)S(1)} %fusion.5, f32[4,63,320]{2,1,0:T(8,128)S(1)} %get-tuple-element.35, f32[4,64,320]{2,1,0:T(8,128)S(1)} %copy-done.42, f32[4,64,319]{2,1,0:T(8,128)S(1)} %get-tuple-element.37, f32[4,64,320]{2,1,0:T(8,128)S(1)} %get-tuple-element.19, ...), kind=kLoop, calls=%fused_computation.67 | loop fusion | flops 655360 | bytes 3395584 | tf_op jit(solution)/shard_map/div | solution.py:220
  (288 shorter events, 17.5 us)
Async XLA Ops:
  2.1 6.6 %copy-start.14 = (f32[4,64,256]{2,1,0:T(8,128)S(1)}, f32[4,64,256]{2,1,0:T(8,128)}, u32[]{:S(2)}) copy-start(f32[4,64,256]{2,1,0:T(8,128)} %param.7) | copy-start | bytes 786436
  2.1 6.6 %copy-start.16 = (f32[4,64,256]{2,1,0:T(8,128)S(1)}, f32[4,64,256]{2,1,0:T(8,128)}, u32[]{:S(2)}) copy-start(f32[4,64,256]{2,1,0:T(8,128)} %param.6) | copy-start | bytes 786436
  2.1 6.6 %copy-start.18 = (f32[4,64,256]{2,1,0:T(8,128)S(1)}, f32[4,64,256]{2,1,0:T(8,128)}, u32[]{:S(2)}) copy-start(f32[4,64,256]{2,1,0:T(8,128)} %param.5) | copy-start | bytes 786436
  2.3 6.0 %collective-permute-start = (f32[4,4,16,128]{3,2,1,0:T(8,128)S(1)}, f32[4,4,16,128]{3,2,1,0:T(8,128)S(1)}, u32[]{:S(2)}, u32[]{:S(2)}) collective-permute-start(f32[4,4,16,128]{3,2,1,0:T(8,128)S(1)} %copy.28), channel_id=1, source_target_pairs={{0,1},{1,2},{2,3},{3,0},{4,5},{5,6},{6,7},{7,4},{8,9},{9,10},{10,1... | collective-permute-start | bytes 393224 | tf_op jit(solution)/shard_map/ppermute | solution.py:41
  2.6 5.9 %collective-permute-start.1 = (f32[4,4,16,128]{3,2,1,0:T(8,128)S(1)}, f32[4,4,16,128]{3,2,1,0:T(8,128)S(1)}, u32[]{:S(2)}, u32[]{:S(2)}) collective-permute-start(f32[4,4,16,128]{3,2,1,0:T(8,128)S(1)} %copy.29), channel_id=1, source_target_pairs={{1,0},{2,1},{3,2},{0,3},{5,4},{6,5},{7,6},{4,7},{9,8},{10,9},{11,1... | collective-permute-start | bytes 393224 | tf_op jit(solution)/shard_map/ppermute | solution.py:42
  10.7 2.6 %copy-start.11 = (f32[1,64,320]{2,1,0:T(8,128)}, f32[1,64,320]{2,1,0:T(8,128)S(1)}, u32[]{:S(2)}) copy-start(f32[1,64,320]{2,1,0:T(8,128)S(1)} %get-tuple-element.21) | copy-start | bytes 245764
  10.7 5.6 %copy-start.8 = (f32[1,64,320]{2,1,0:T(8,128)}, f32[1,64,320]{2,1,0:T(8,128)S(1)}, u32[]{:S(2)}) copy-start(f32[1,64,320]{2,1,0:T(8,128)S(1)} %get-tuple-element.20) | copy-start | bytes 245764
  20.4 21.4 %copy-start.43 = (f32[32,2,160]{2,0,1:T(8,128)}, f32[32,2,160]{2,0,1:T(8,128)S(1)}, u32[]{:S(2)}) copy-start(f32[32,2,160]{2,0,1:T(8,128)S(1)} %get-tuple-element.132) | copy-start | bytes 122884
  20.6 21.3 %copy-start.45 = (f32[32,2,160]{2,0,1:T(8,128)}, f32[32,2,160]{2,0,1:T(8,128)S(1)}, u32[]{:S(2)}) copy-start(f32[32,2,160]{2,0,1:T(8,128)S(1)} %get-tuple-element.134) | copy-start | bytes 122884
  21.9 12.7 %copy-start.63 = (f32[1,2,64,320]{3,2,1,0:T(8,128)S(1)}, f32[1,2,64,320]{3,2,1,0:T(8,128)}, u32[]{:S(2)}) copy-start(f32[1,2,64,320]{3,2,1,0:T(8,128)} %get-tuple-element.29) | copy-start | bytes 491524
  21.9 14.6 %copy-start.72 = (s32[160]{0:T(256)S(1)}, s32[160]{0:T(256)}, u32[]{:S(2)}) copy-start(s32[160]{0:T(256)} %get-tuple-element.141) | copy-start | bytes 1924
  22.0 14.6 %copy-start.74 = (s32[160]{0:T(256)S(1)}, s32[160]{0:T(256)}, u32[]{:S(2)}) copy-start(s32[160]{0:T(256)} %get-tuple-element.142) | copy-start | bytes 1924
  22.0 14.6 %copy-start.81 = (pred[160]{0:T(512)(128)(4,1)S(1)}, pred[160]{0:T(512)(128)(4,1)}, u32[]{:S(2)}) copy-start(pred[160]{0:T(512)(128)(4,1)} %compare_and_fusion) | copy-start | bytes 484
  22.0 15.8 %collective-permute-start.12 = (f32[2,3,32,160]{3,2,0,1:T(8,128)S(1)}, f32[2,3,32,160]{3,2,0,1:T(8,128)S(1)}, u32[]{:S(2)}, u32[]{:S(2)}) collective-permute-start(f32[2,3,32,160]{3,2,0,1:T(8,128)S(1)} %pad_maximum_fusion.19), channel_id=1, source_target_pairs={{0,8},{4,12},{8,16},{12,20},{16,24},{20,28},{1,9},{5,13},{9,17},{1... | collective-permute-start | bytes 368648 | tf_op jit(solution)/shard_map/ppermute | solution.py:54
  25.6 16.2 %collective-permute-start.13 = (f32[2,3,32,160]{3,2,0,1:T(8,128)S(1)}, f32[2,3,32,160]{3,2,0,1:T(8,128)S(1)}, u32[]{:S(2)}, u32[]{:S(2)}) collective-permute-start(f32[2,3,32,160]{3,2,0,1:T(8,128)S(1)} %pad_maximum_fusion.19), channel_id=1, source_target_pairs={{0,4},{4,8},{8,12},{12,16},{16,20},{20,24},{24,28},{1,5},{5,9},{9,... | collective-permute-start | bytes 368648 | tf_op jit(solution)/shard_map/ppermute | solution.py:54
  29.1 12.8 %collective-permute-start.14 = (f32[2,3,32,160]{3,2,0,1:T(8,128)S(1)}, f32[2,3,32,160]{3,2,0,1:T(8,128)S(1)}, u32[]{:S(2)}, u32[]{:S(2)}) collective-permute-start(f32[2,3,32,160]{3,2,0,1:T(8,128)S(1)} %pad_maximum_fusion.19), channel_id=1, source_target_pairs={{4,0},{8,4},{12,8},{16,12},{20,16},{24,20},{28,24},{5,1},{9,5},{13... | collective-permute-start | bytes 368648 | tf_op jit(solution)/shard_map/ppermute | solution.py:55
  32.4 11.6 %collective-permute-start.15 = (f32[2,3,32,160]{3,2,0,1:T(8,128)S(1)}, f32[2,3,32,160]{3,2,0,1:T(8,128)S(1)}, u32[]{:S(2)}, u32[]{:S(2)}) collective-permute-start(f32[2,3,32,160]{3,2,0,1:T(8,128)S(1)} %pad_maximum_fusion.19), channel_id=1, source_target_pairs={{8,0},{12,4},{16,8},{20,12},{24,16},{28,20},{9,1},{13,5},{17,9},{2... | collective-permute-start | bytes 368648 | tf_op jit(solution)/shard_map/ppermute | solution.py:55
  34.3 3.1 %copy-start.64 = (s32[32]{0:T(128)S(1)}, s32[32]{0:T(128)}, u32[]{:S(2)}) copy-start(s32[32]{0:T(128)} %broadcast_add_fusion.2) | copy-start | bytes 388
  34.3 3.1 %copy-start.66 = (pred[32]{0:T(512)(128)(4,1)S(1)}, pred[32]{0:T(512)(128)(4,1)}, u32[]{:S(2)}) copy-start(pred[32]{0:T(512)(128)(4,1)} %compare_and_fusion.1) | copy-start | bytes 100
  34.3 3.5 %copy-start.62 = (f32[1,2,64,320]{3,2,1,0:T(8,128)S(1)}, f32[1,2,64,320]{3,2,1,0:T(8,128)}, u32[]{:S(2)}) copy-start(f32[1,2,64,320]{3,2,1,0:T(8,128)} %get-tuple-element.28) | copy-start | bytes 491524
  34.6 14.2 %collective-permute-start.3 = (f32[1,2,64,320]{3,2,1,0:T(8,128)S(1)}, f32[1,2,64,320]{3,2,1,0:T(8,128)S(1)}, u32[]{:S(2)}, u32[]{:S(2)}) collective-permute-start(f32[1,2,64,320]{3,2,1,0:T(8,128)S(1)} %copy-done.63), channel_id=1, source_target_pairs={{4,0},{8,4},{12,8},{16,12},{20,16},{24,20},{28,24},{5,1},{9,5},{13... | collective-permute-start | bytes 491528 | tf_op jit(solution)/shard_map/ppermute | solution.py:55
  37.8 11.1 %collective-permute-start.2 = (f32[1,2,64,320]{3,2,1,0:T(8,128)S(1)}, f32[1,2,64,320]{3,2,1,0:T(8,128)S(1)}, u32[]{:S(2)}, u32[]{:S(2)}) collective-permute-start(f32[1,2,64,320]{3,2,1,0:T(8,128)S(1)} %copy-done.62), channel_id=1, source_target_pairs={{0,4},{4,8},{8,12},{12,16},{16,20},{20,24},{24,28},{1,5},{5,9},{9,... | collective-permute-start | bytes 491528 | tf_op jit(solution)/shard_map/ppermute | solution.py:54
  49.3 16.4 %copy-start.4 = (f32[4,64,320]{2,1,0:T(8,128)}, f32[4,64,320]{2,1,0:T(8,128)S(1)}, u32[]{:S(2)}) copy-start(f32[4,64,320]{2,1,0:T(8,128)S(1)} %get-tuple-element.15) | copy-start | bytes 983044
  53.2 12.5 %collective-permute-start.5 = (f32[1,64,320]{2,1,0:T(8,128)S(1)}, f32[1,64,320]{2,1,0:T(8,128)S(1)}, u32[]{:S(2)}, u32[]{:S(2)}) collective-permute-start(f32[1,64,320]{2,1,0:T(8,128)S(1)} %fusion.196), channel_id=1, source_target_pairs={{4,0},{8,4},{12,8},{16,12},{20,16},{24,20},{28,24},{5,1},{9,5},{13... | collective-permute-start | bytes 245768 | tf_op jit(solution)/shard_map/ppermute | solution.py:55
  56.2 7.4 %collective-permute-start.4 = (f32[1,64,320]{2,1,0:T(8,128)S(1)}, f32[1,64,320]{2,1,0:T(8,128)S(1)}, u32[]{:S(2)}, u32[]{:S(2)}) collective-permute-start(f32[1,64,320]{2,1,0:T(8,128)S(1)} %fusion.184), channel_id=1, source_target_pairs={{0,4},{4,8},{8,12},{12,16},{16,20},{20,24},{24,28},{1,5},{5,9},{9,... | collective-permute-start | bytes 245768 | tf_op jit(solution)/shard_map/ppermute | solution.py:54
  59.9 13.4 %copy-start.26 = (f32[2,64,320]{2,1,0:T(8,128)}, f32[2,64,320]{2,1,0:T(8,128)S(1)}, u32[]{:S(2)}) copy-start(f32[2,64,320]{2,1,0:T(8,128)S(1)} %fusion.86) | copy-start | bytes 491524
  63.8 9.5 %copy-start.38 = (f32[1,64,320]{2,1,0:T(8,128)}, f32[1,64,320]{2,1,0:T(8,128)S(1)}, u32[]{:S(2)}) copy-start(f32[1,64,320]{2,1,0:T(8,128)S(1)} %fusion.173) | copy-start | bytes 245764
  63.8 7.6 %collective-permute-start.7 = (f32[1,64,320]{2,1,0:T(8,128)S(1)}, f32[1,64,320]{2,1,0:T(8,128)S(1)}, u32[]{:S(2)}, u32[]{:S(2)}) collective-permute-start(f32[1,64,320]{2,1,0:T(8,128)S(1)} %fusion.173), channel_id=1, source_target_pairs={{4,0},{8,4},{12,8},{16,12},{20,16},{24,20},{28,24},{5,1},{9,5},{13... | collective-permute-start | bytes 245768 | tf_op jit(solution)/shard_map/ppermute | solution.py:55
  65.9 7.4 %copy-start.40 = (f32[1,64,320]{2,1,0:T(8,128)}, f32[1,64,320]{2,1,0:T(8,128)S(1)}, u32[]{:S(2)}) copy-start(f32[1,64,320]{2,1,0:T(8,128)S(1)} %fusion.163) | copy-start | bytes 245764
  65.9 7.4 %collective-permute-start.6 = (f32[1,64,320]{2,1,0:T(8,128)S(1)}, f32[1,64,320]{2,1,0:T(8,128)S(1)}, u32[]{:S(2)}, u32[]{:S(2)}) collective-permute-start(f32[1,64,320]{2,1,0:T(8,128)S(1)} %fusion.163), channel_id=1, source_target_pairs={{0,4},{4,8},{8,12},{12,16},{16,20},{20,24},{24,28},{1,5},{5,9},{9,... | collective-permute-start | bytes 245768 | tf_op jit(solution)/shard_map/ppermute | solution.py:54
  74.0 18.1 %copy-start.44 = (f32[32,2,160]{2,0,1:T(8,128)S(1)}, f32[32,2,160]{2,0,1:T(8,128)}, u32[]{:S(2)}) copy-start(f32[32,2,160]{2,0,1:T(8,128)} %copy-done.43) | copy-start | bytes 122884
  74.0 18.1 %copy-start.46 = (f32[32,2,160]{2,0,1:T(8,128)S(1)}, f32[32,2,160]{2,0,1:T(8,128)}, u32[]{:S(2)}) copy-start(f32[32,2,160]{2,0,1:T(8,128)} %copy-done.45) | copy-start | bytes 122884
  74.6 18.9 %copy-start.24 = (f32[2,32,160]{2,1,0:T(8,128)}, f32[2,32,160]{2,1,0:T(8,128)S(1)}, u32[]{:S(2)}) copy-start(f32[2,32,160]{2,1,0:T(8,128)S(1)} %fusion) | copy-start | bytes 122884
  74.6 13.6 %collective-permute-start.8 = (f32[1,32,160]{2,1,0:T(8,128)S(1)}, f32[1,32,160]{2,1,0:T(8,128)S(1)}, u32[]{:S(2)}, u32[]{:S(2)}) collective-permute-start(f32[1,32,160]{2,1,0:T(8,128)S(1)} %get-tuple-element.130), channel_id=1, source_target_pairs={{0,8},{4,12},{8,16},{12,20},{16,24},{20,28},{1,9},{5,13},{9,17},{1... | collective-permute-start | bytes 61448 | tf_op jit(solution)/shard_map/ppermute | solution.py:54
  79.5 14.0 %copy-start.6 = (f32[8,31,160]{2,1,0:T(8,128)}, f32[8,31,160]{2,1,0:T(8,128)S(1)}, u32[]{:S(2)}) copy-start(f32[8,31,160]{2,1,0:T(8,128)S(1)} %fusion.32) | copy-start | bytes 476164
  79.5 8.7 %collective-permute-start.9 = (f32[2,32,160]{2,1,0:T(8,128)S(1)}, f32[2,32,160]{2,1,0:T(8,128)S(1)}, u32[]{:S(2)}, u32[]{:S(2)}) collective-permute-start(f32[2,32,160]{2,1,0:T(8,128)S(1)} %fusion), channel_id=1, source_target_pairs={{0,4},{4,8},{8,12},{12,16},{16,20},{20,24},{24,28},{1,5},{5,9},{9,... | collective-permute-start | bytes 122888 | tf_op jit(solution)/shard_map/ppermute | solution.py:54
  82.6 6.2 %collective-permute-start.10 = (f32[2,32,160]{2,1,0:T(8,128)S(1)}, f32[2,32,160]{2,1,0:T(8,128)S(1)}, u32[]{:S(2)}, u32[]{:S(2)}) collective-permute-start(f32[2,32,160]{2,1,0:T(8,128)S(1)} %fusion), channel_id=1, source_target_pairs={{4,0},{8,4},{12,8},{16,12},{20,16},{24,20},{28,24},{5,1},{9,5},{13... | collective-permute-start | bytes 122888 | tf_op jit(solution)/shard_map/ppermute | solution.py:55
  86.3 5.8 %collective-permute-start.11 = (f32[1,32,160]{2,1,0:T(8,128)S(1)}, f32[1,32,160]{2,1,0:T(8,128)S(1)}, u32[]{:S(2)}, u32[]{:S(2)}) collective-permute-start(f32[1,32,160]{2,1,0:T(8,128)S(1)} %get-tuple-element.129), channel_id=1, source_target_pairs={{8,0},{12,4},{16,8},{20,12},{24,16},{28,20},{9,1},{13,5},{17,9},{2... | collective-permute-start | bytes 61448 | tf_op jit(solution)/shard_map/ppermute | solution.py:55
  88.2 4.3 %copy-start.51 = (f32[2,32,160]{2,1,0:T(8,128)}, f32[2,32,160]{2,1,0:T(8,128)S(1)}, u32[]{:S(2)}) copy-start(f32[2,32,160]{2,1,0:T(8,128)S(1)} %collective-permute-done.9) | copy-start | bytes 122884
  88.7 3.9 %copy-start.52 = (f32[2,32,160]{2,1,0:T(8,128)}, f32[2,32,160]{2,1,0:T(8,128)S(1)}, u32[]{:S(2)}) copy-start(f32[2,32,160]{2,1,0:T(8,128)S(1)} %collective-permute-done.10) | copy-start | bytes 122884
  95.3 10.5 %all-to-all-start = ((f32[8,1,4,16,80]{4,3,2,1,0:T(8,128)}), f32[8,1,4,16,80]{4,3,2,1,0:T(8,128)}, u32[]{:S(2)}, u32[]{:S(2)}) async-start(f32[8,1,4,16,80]{4,3,2,1,0:T(8,128)} %broadcast_in_dim.20), calls=%async_computation | async-start | bytes 524288 | tf_op jit(solution)/shard_map/all_to_all | solution.py:62
  107.8 3.3 %copy-start.73 = (s32[160]{0:T(256)S(1)}, s32[160]{0:T(256)}, u32[]{:S(2)}) copy-start(s32[160]{0:T(256)} %get-tuple-element.141) | copy-start | bytes 1924
  107.9 3.3 %copy-start.75 = (s32[160]{0:T(256)S(1)}, s32[160]{0:T(256)}, u32[]{:S(2)}) copy-start(s32[160]{0:T(256)} %get-tuple-element.142) | copy-start | bytes 1924
  107.9 3.3 %copy-start.82 = (pred[160]{0:T(512)(128)(4,1)S(1)}, pred[160]{0:T(512)(128)(4,1)}, u32[]{:S(2)}) copy-start(pred[160]{0:T(512)(128)(4,1)} %compare_and_fusion) | copy-start | bytes 484
  108.8 2.7 %copy-start.65 = (s32[32]{0:T(128)S(1)}, s32[32]{0:T(128)}, u32[]{:S(2)}) copy-start(s32[32]{0:T(128)} %broadcast_add_fusion.2) | copy-start | bytes 388
  108.8 2.7 %copy-start.67 = (pred[32]{0:T(512)(128)(4,1)S(1)}, pred[32]{0:T(512)(128)(4,1)}, u32[]{:S(2)}) copy-start(pred[32]{0:T(512)(128)(4,1)} %compare_and_fusion.1) | copy-start | bytes 100
  108.8 2.9 %copy-start.23 = (f32[6,32,160]{2,1,0:T(8,128)S(1)}, f32[6,32,160]{2,1,0:T(8,128)}, u32[]{:S(2)}) copy-start(f32[6,32,160]{2,1,0:T(8,128)} %copy-done.22) | copy-start | bytes 368644
  109.9 2.1 %copy-start.7 = (f32[8,31,160]{2,1,0:T(8,128)S(1)}, f32[8,31,160]{2,1,0:T(8,128)}, u32[]{:S(2)}) copy-start(f32[8,31,160]{2,1,0:T(8,128)} %copy-done.6) | copy-start | bytes 476164
  109.9 2.1 %copy-start.29 = (f32[8,32,160]{2,1,0:T(8,128)S(1)}, f32[8,32,160]{2,1,0:T(8,128)}, u32[]{:S(2)}) copy-start(f32[8,32,160]{2,1,0:T(8,128)} %copy-done.28) | copy-start | bytes 491524
  109.9 2.1 %copy-start.31 = (f32[8,1,32,160]{3,2,0,1:T(8,128)S(1)}, f32[8,1,32,160]{3,2,0,1:T(8,128)}, u32[]{:S(2)}) copy-start(f32[8,1,32,160]{3,2,0,1:T(8,128)} %copy-done.30) | copy-start | bytes 491524
  109.9 2.1 %copy-start.33 = (f32[8,1,32,160]{3,2,0,1:T(8,128)S(1)}, f32[8,1,32,160]{3,2,0,1:T(8,128)}, u32[]{:S(2)}) copy-start(f32[8,1,32,160]{3,2,0,1:T(8,128)} %copy-done.32) | copy-start | bytes 491524
  109.9 2.1 %copy-start.35 = (f32[8,32,160]{2,1,0:T(8,128)S(1)}, f32[8,32,160]{2,1,0:T(8,128)}, u32[]{:S(2)}) copy-start(f32[8,32,160]{2,1,0:T(8,128)} %copy-done.34) | copy-start | bytes 491524
  110.0 2.1 %copy-start.37 = (f32[8,32,160]{2,1,0:T(8,128)S(1)}, f32[8,32,160]{2,1,0:T(8,128)}, u32[]{:S(2)}) copy-start(f32[8,32,160]{2,1,0:T(8,128)} %copy-done.36) | copy-start | bytes 491524
  110.0 2.1 %copy-start.53 = (f32[6,32,160]{2,1,0:T(8,128)S(1)}, f32[6,32,160]{2,1,0:T(8,128)}, u32[]{:S(2)}) copy-start(f32[6,32,160]{2,1,0:T(8,128)} %pad_maximum_fusion.20) | copy-start | bytes 368644
  110.0 2.1 %copy-start.80 = (pred[4]{0:T(512)(128)(4,1)S(1)}, pred[4]{0:T(512)(128)(4,1)}, u32[]{:S(2)}) copy-start(pred[4]{0:T(512)(128)(4,1)} %compare_and_fusion.3) | copy-start | bytes 16
  114.8 7.8 %copy-start.10 = (f32[1,64,320]{2,1,0:T(8,128)S(1)}, f32[1,64,320]{2,1,0:T(8,128)}, u32[]{:S(2)}) copy-start(f32[1,64,320]{2,1,0:T(8,128)} %copy-done.8) | copy-start | bytes 245764
  114.9 17.8 %copy-start.13 = (f32[1,64,320]{2,1,0:T(8,128)S(1)}, f32[1,64,320]{2,1,0:T(8,128)}, u32[]{:S(2)}) copy-start(f32[1,64,320]{2,1,0:T(8,128)} %copy-done.11) | copy-start | bytes 245764
  114.9 7.6 %collective-permute-start.16 = (f32[1,64,320]{2,1,0:T(8,128)S(1)}, f32[1,64,320]{2,1,0:T(8,128)S(1)}, u32[]{:S(2)}, u32[]{:S(2)}) collective-permute-start(f32[1,64,320]{2,1,0:T(8,128)S(1)} %slice.1276), channel_id=1, source_target_pairs={{0,4},{4,8},{8,12},{12,16},{16,20},{20,24},{24,28},{1,5},{5,9},{9,... | collective-permute-start | bytes 245768 | tf_op jit(solution)/shard_map/ppermute | solution.py:54
  122.7 13.7 %collective-permute-start.19 = (f32[1,64,320]{2,1,0:T(8,128)S(1)}, f32[1,64,320]{2,1,0:T(8,128)S(1)}, u32[]{:S(2)}, u32[]{:S(2)}) collective-permute-start(f32[1,64,320]{2,1,0:T(8,128)S(1)} %get-tuple-element.38), channel_id=1, source_target_pairs={{4,0},{8,4},{12,8},{16,12},{20,16},{24,20},{28,24},{5,1},{9,5},{13... | collective-permute-start | bytes 245768 | tf_op jit(solution)/shard_map/ppermute | solution.py:55
  126.2 6.5 %collective-permute-start.17 = (f32[1,64,320]{2,1,0:T(8,128)S(1)}, f32[1,64,320]{2,1,0:T(8,128)S(1)}, u32[]{:S(2)}, u32[]{:S(2)}) collective-permute-start(f32[1,64,320]{2,1,0:T(8,128)S(1)} %get-tuple-element.39), channel_id=1, source_target_pairs={{4,0},{8,4},{12,8},{16,12},{20,16},{24,20},{28,24},{5,1},{9,5},{13... | collective-permute-start | bytes 245768 | tf_op jit(solution)/shard_map/ppermute | solution.py:55
  133.0 7.4 %collective-permute-start.18 = (f32[1,64,320]{2,1,0:T(8,128)S(1)}, f32[1,64,320]{2,1,0:T(8,128)S(1)}, u32[]{:S(2)}, u32[]{:S(2)}) collective-permute-start(f32[1,64,320]{2,1,0:T(8,128)S(1)} %fusion.143), channel_id=1, source_target_pairs={{0,4},{4,8},{8,12},{12,16},{16,20},{20,24},{24,28},{1,5},{5,9},{9,... | collective-permute-start | bytes 245768 | tf_op jit(solution)/shard_map/ppermute | solution.py:54
  136.5 7.5 %collective-permute-start.20 = (f32[1,64,320]{2,1,0:T(8,128)S(1)}, f32[1,64,320]{2,1,0:T(8,128)S(1)}, u32[]{:S(2)}, u32[]{:S(2)}) collective-permute-start(f32[1,64,320]{2,1,0:T(8,128)S(1)} %fusion.123), channel_id=1, source_target_pairs={{0,4},{4,8},{8,12},{12,16},{16,20},{20,24},{24,28},{1,5},{5,9},{9,... | collective-permute-start | bytes 245768 | tf_op jit(solution)/shard_map/ppermute | solution.py:54
  140.6 6.5 %collective-permute-start.21 = (f32[1,64,320]{2,1,0:T(8,128)S(1)}, f32[1,64,320]{2,1,0:T(8,128)S(1)}, u32[]{:S(2)}, u32[]{:S(2)}) collective-permute-start(f32[1,64,320]{2,1,0:T(8,128)S(1)} %fusion.133), channel_id=1, source_target_pairs={{4,0},{8,4},{12,8},{16,12},{20,16},{24,20},{28,24},{5,1},{9,5},{13... | collective-permute-start | bytes 245768 | tf_op jit(solution)/shard_map/ppermute | solution.py:55
  144.0 3.3 %copy-start.42 = (f32[4,64,320]{2,1,0:T(8,128)S(1)}, f32[4,64,320]{2,1,0:T(8,128)}, u32[]{:S(2)}) copy-start(f32[4,64,320]{2,1,0:T(8,128)} %get-tuple-element.22) | copy-start | bytes 983044
  (42 other events, 49.8 us)

commit v16 on v13

--- a/solution.py
+++ b/solution.py
@@ -174,12 +174,13 @@
     coef_two = [coarsen(part) for part in (wide_alt, wide_inc, wide_raan)]
     coef_three = [coarsen(part) for part in coef_two]
 
-    first = alt_extend(wide[:, 0:2], 1)
+    first = alt_extend(wide[:, 0:2], 2)
+    rest = alt_extend(wide[:, 2:4], 1)
     source_x = first[:, 0]
-    weights_one = make_weights(first[:, 1], wide_inc, wide_raan, 1.0, 0)
-
-    density = split_sweep(weights_one, source_x, source_x, 1)
-    density = split_sweep(weights_one, alt_extend(density, 1), source_x, 1)
+    weights_one = make_weights(first[:, 1], rest[:, 0], rest[:, 1], 1.0, 1)
+
+    density = sweep(weights_one, source_x, 2, source_x, 2)
+    density = split_sweep(weights_one, density, source_x, 2)
     applied, density = apply_op(weights_one, alt_extend(density, 1), 1)
     rhs_two = coarsen(wide_source - applied)
 
@@ -212,11 +213,11 @@
     for halo in range(SWEEPS, 0, -1):
         correction = sweep(weights_two, correction, halo, rhs_two_x, SWEEPS + 1)
 
-    density = density + refine(correction)
-    for _ in range(SWEEPS):
-        density = split_sweep(weights_one, alt_extend(density, 1), source_x, 1)
+    density = alt_extend(density + refine(correction), 2)
+    density = sweep(weights_one, density, 2, source_x, 2)
+    density = split_sweep(weights_one, density, source_x, 2)
     applied, centre = apply_op(weights_one, alt_extend(density, 1), 1)
-    scaled_residual = (wide_source - applied) / weights_one[0][6]
+    scaled_residual = (wide_source - applied) / trim(weights_one[0][6], weights_one[1], 0)
     keep = slice(halo_r, halo_r + length)
     return (centre[..., keep], scaled_residual[..., keep])
 

time: 136 us -> 140 us (1.029)
  other arithmetic: 20.7 us -> 27.2 us
  matrix products: 7.58 us -> 13.5 us
  starting transfers between devices: 55 us -> 50.7 us
  waiting for transfers between devices: 33.5 us -> 29.9 us
    ppermute x8 -> x7, starting transfers between devices: 27.5 us -> 20.8 us  [alt_extend(): below.insert(0, lax.ppermute(values[low:], 'alt', up))]
    ppermute x8 -> x7, waiting for transfers between devices: 16.2 us -> 11.9 us  [alt_extend(): above.append(lax.ppermute(values[:high], 'alt', down))]
    select_n x2 -> x4, other arithmetic: 0.49 us -> 3.58 us  [sweep(): return jnp.where(inside(updated.shape, halo - 1), updated, 0.0)]
    dot_general x8, matrix products: 1.23 us -> 4.32 us  [coarsen(): summed = jnp.matmul(pairing(width).T[None], summed, precision=HIGH)]
    ppermute x8 -> x7, starting transfers between devices: 20.8 us -> 23.7 us  [alt_extend(): above.append(lax.ppermute(values[:high], 'alt', down))]
    dot_general x8, matrix products: 5.07 us -> 7.92 us  [coarsen(): summed = jnp.matmul(summed, pairing(length), precision=HIGH)]
    unnamed x180 -> x151, local copies, waits for them, and re-layouts: 3.28 us -> 5.76 us
    slice x11 -> x4, local copies, waits for them, and re-layouts: 2.33 us -> 0.12 us  [split_sweep(): v_prev = jnp.concatenate([zero_inc, centre[:, :-1]], 1)]
  transfers between devices with their start and end apart: 19 -> 17, of which waited for: 12 -> 10; matrix products, arithmetic and copies ran while one was open for 12% -> 16% of each run, Pallas kernels for 0% -> 0%
where the time goes in v16:
time: 140 us; the launch traced here: 139 us
  starting transfers between devices  50.7 us (36%)
  waiting for transfers between devices  29.9 us (21%)
  other arithmetic  27.2 us (19%)
  local copies, waits for them, and re-layouts  15 us (11%)
  matrix products  13.5 us (10%)
  between operations  2.26 us (2%)
    ppermute x7, starting transfers between devices, alt_extend(): above.append(lax.ppermute(values[:high], 'alt', down))  23.7 us
    ppermute x7, starting transfers between devices, alt_extend(): below.insert(0, lax.ppermute(values[low:], 'alt', up))  20.8 us
    ppermute x7, waiting for transfers between devices, alt_extend(): below.insert(0, lax.ppermute(values[low:], 'alt', up))  12.7 us
    ppermute x7, waiting for transfers between devices, alt_extend(): above.append(lax.ppermute(values[:high], 'alt', down))  11.9 us
    dot_general x8, matrix products, coarsen(): summed = jnp.matmul(summed, pairing(length), precision=HIGH)  7.92 us
    unnamed x151, local copies, waits for them, and re-layouts  5.76 us
    all_to_all x1, waiting for transfers between devices, spread_gather(): every = lax.all_to_all(copies, 'alt', 0, 0)  5.29 us
    all_to_all x1, starting transfers between devices, spread_gather(): every = lax.all_to_all(copies, 'alt', 0, 0)  4.38 us
  transfers between devices with their start and end apart: 17, of which 10 were waited for; matrix products, arithmetic and copies ran while one was open for 16% of the time, Pallas kernels for 0%

profile of v16, /device:TPU:8, one launch (start us, length us, event | category | flops | bytes accessed | tf_op | source)
XLA Modules:
  0.0 138.6 jit_solution(6444585045374355338)
XLA Ops:
  0.6 1.3 pad_maximum_fusion.2
  2.6 1.8 %collective-permute-start.1 = (f32[4,4,16,128]{3,2,1,0:T(8,128)S(1)}, f32[4,4,16,128]{3,2,1,0:T(8,128)S(1)}, u32[]{:S(2)}, u32[]{:S(2)}) collective-permute-start(f32[4,4,16,128]{3,2,1,0:T(8,128)S(1)} %copy.23), channel_id=1, source_target_pairs={{1,0},{2,1},{3,2},{0,3},{5,4},{6,5},{7,6},{4,7},{9,8},{10,9},{11,1... | collective-permute-start | bytes 393224 | tf_op jit(solution)/shard_map/ppermute | solution.py:42
  4.9 0.6 iota_shift-right-logical_fusion.1
  9.2 1.7 %pad_maximum_fusion = f32[4,4,64,320]{3,2,0,1:T(8,128)S(1)} fusion(f32[4,1,64,256]{3,2,0,1:T(8,128)S(1)} %bitcast.371, f32[4,1,64,256]{3,2,0,1:T(8,128)S(1)} %bitcast.375, f32[4,1,64,256]{3,2,0,1:T(8,128)S(1)} %bitcast.379, f32[4,1,64,256]{3,2,0,1:T(8,128)} %bitcast.383, f32[4,4,64,32]{3,2,1,0:T(8,128)S(1)} %reshape.115, f32[4,4,64,32]{3,2,1,0:T(8,128)S(1)} %reshape.117), kind=kLoop, calls=%fused_computation | loop fusion | flops 1638400 | bytes 2621440 | tf_op jit(solution)/shard_map/concatenate | solution.py:43
  11.0 1.0 fusion.304
  12.0 0.8 fusion.303
  12.8 1.0 fusion.305
  13.8 0.9 fusion.302
  14.7 3.4 %collective-permute-start.4 = (f32[1,2,64,320]{3,2,0,1:T(8,128)}, f32[1,2,64,320]{3,2,0,1:T(8,128)}, u32[]{:S(2)}, u32[]{:S(2)}) collective-permute-start(f32[1,2,64,320]{3,2,0,1:T(8,128)} %get-tuple-element.27), channel_id=1, source_target_pairs={{0,4},{4,8},{8,12},{12,16},{16,20},{20,24},{24,28},{1,5},{5,9},{9,... | collective-permute-start | bytes 491528 | tf_op jit(solution)/shard_map/ppermute | solution.py:54
  18.1 3.3 %collective-permute-start.5 = (f32[1,2,64,320]{3,2,0,1:T(8,128)}, f32[1,2,64,320]{3,2,0,1:T(8,128)}, u32[]{:S(2)}, u32[]{:S(2)}) collective-permute-start(f32[1,2,64,320]{3,2,0,1:T(8,128)} %get-tuple-element.28), channel_id=1, source_target_pairs={{4,0},{8,4},{12,8},{16,12},{20,16},{24,20},{28,24},{5,1},{9,5},{13... | collective-permute-start | bytes 491528 | tf_op jit(solution)/shard_map/ppermute | solution.py:55
  21.5 2.5 %collective-permute-start.2 = (f32[2,2,64,320]{3,2,0,1:T(8,128)}, f32[2,2,64,320]{3,2,0,1:T(8,128)}, u32[]{:S(2)}, u32[]{:S(2)}) collective-permute-start(f32[2,2,64,320]{3,2,0,1:T(8,128)} %get-tuple-element.31), channel_id=1, source_target_pairs={{0,4},{4,8},{8,12},{12,16},{16,20},{20,24},{24,28},{1,5},{5,9},{9,... | collective-permute-start | bytes 983048 | tf_op jit(solution)/shard_map/ppermute | solution.py:54
  24.0 4.2 %collective-permute-start.3 = (f32[2,2,64,320]{3,2,0,1:T(8,128)}, f32[2,2,64,320]{3,2,0,1:T(8,128)}, u32[]{:S(2)}, u32[]{:S(2)}) collective-permute-start(f32[2,2,64,320]{3,2,0,1:T(8,128)} %get-tuple-element.32), channel_id=1, source_target_pairs={{4,0},{8,4},{12,8},{16,12},{20,16},{24,20},{28,24},{5,1},{9,5},{13... | collective-permute-start | bytes 983048 | tf_op jit(solution)/shard_map/ppermute | solution.py:55
  28.2 0.7 reduce_sum.73
  28.9 0.7 reduce_sum.74
  29.6 1.4 fusion.292
  31.0 1.4 %fusion.290 = f32[2,64,160]{2,1,0:T(8,128)S(1)} fusion(f32[2,64,320]{2,1,0:T(8,128)} %reduce_sum.74, s32[320]{0:T(512)} %get-tuple-element.126, s32[320]{0:T(512)} %get-tuple-element.127, pred[320]{0:T(512)(128)(4,1)} %fusion.277), kind=kOutput, calls=%fused_computation.460 | convolution fusion | flops 78745600 | bytes 248640 | tf_op jit(solution)/shard_map/dot_general | solution.py:22
  32.4 1.4 %bitcast_reduce_fusion.3 = (f32[32,160]{1,0:T(8,128)}, f32[32,2,160]{2,0,1:T(8,128)}) fusion(f32[2,64,160]{2,1,0:T(8,128)S(1)} %fusion.292, s32[64]{0:T(128)S(1)} %get-tuple-element.128, s32[64]{0:T(128)S(1)} %get-tuple-element.129, pred[64]{0:T(512)(128)(4,1)S(1)} %compare_and_fusion.5), kind=kOutput, calls=%fused_computation.367 | convolution fusion | flops 7883776 | bytes 143936 | tf_op jit(solution)/shard_map/dot_general | solution.py:23
  33.9 1.4 %bitcast_reduce_fusion.2 = (f32[32,160]{1,0:T(8,128)}, f32[32,2,160]{2,0,1:T(8,128)}) fusion(f32[2,64,160]{2,1,0:T(8,128)S(1)} %fusion.290, s32[64]{0:T(128)S(1)} %get-tuple-element.128, s32[64]{0:T(128)S(1)} %get-tuple-element.129, pred[64]{0:T(512)(128)(4,1)S(1)} %compare_and_fusion.5), kind=kOutput, calls=%fused_computation.366 | convolution fusion | flops 7883776 | bytes 143936 | tf_op jit(solution)/shard_map/dot_general | solution.py:23
  35.3 0.7 reduce_sum.75
  36.0 1.4 fusion.288
  37.5 1.0 fusion.158
  38.5 1.1 fusion.159
  39.6 1.1 fusion.160
  40.6 0.8 fusion
  41.4 1.1 pad_maximum_fusion.1
  42.9 0.8 collective-permute-done.2
  43.7 1.9 %collective-permute-done.3 = f32[2,2,64,320]{3,2,0,1:T(8,128)} collective-permute-done((f32[2,2,64,320]{3,2,0,1:T(8,128)}, f32[2,2,64,320]{3,2,0,1:T(8,128)}, u32[]{:S(2)}, u32[]{:S(2)}) %collective-permute-start.3) | collective-permute-done | bytes 327712 | tf_op jit(solution)/shard_map/ppermute | solution.py:55
  45.6 1.0 maximum_bitcast_fusion
  46.9 0.9 copy-done.9
  47.8 1.6 %fusion.41 = (f32[6,64,320]{2,1,0:T(8,128)S(1)}, f32[6,1,64,320]{3,2,1,0:T(8,128)S(1)}, f32[6,1,64,320]{3,2,1,0:T(8,128)S(1)}, f32[6,64,320]{2,1,0:T(8,128)S(1)}, f32[6,64,320]{2,1,0:T(8,128)S(1)}) fusion(f32[6,63,320]{2,1,0:T(8,128)S(1)} %fusion.26, f32[4,2,64,320]{3,2,0,1:T(8,128)S(1)} %copy-done.9, f32[2,2,64,320]{3,2,0,1:T(8,128)} %collective-permute-done.2, ...), kind=kLoop, calls=%fused_computation.70 | loop fusion | flops 2211840 | bytes 5723648 | tf_op jit(solution)/shard_map/add | solution.py:89
  49.4 2.2 %fusion.42 = f32[6,64,320]{2,1,0:T(8,128)S(1)} fusion(f32[6,64,320]{2,1,0:T(8,128)S(1)} %maximum_bitcast_fusion, f32[6,64,320]{2,1,0:T(8,128)S(1)} %get-tuple-element.22, f32[6,64,319]{2,1,0:T(8,128)S(1)} %get-tuple-element.72, f32[6,64,320]{2,1,0:T(8,128)S(1)} %get-tuple-element.21, f32[6,64,319]{2,1,0:T(8,128)S(1)} %get-tuple-element.71, ...), kind=kLoop, calls=%fused_computation.73 | loop fusion | flops 3194880 | bytes 6691334 | tf_op jit(solution)/shard_map/jit(_where)/select_n | solution.py:127
  52.1 0.7 copy-done.11
  53.2 0.8 fusion.156
  54.0 2.4 %collective-permute-start.7 = (f32[1,64,320]{2,1,0:T(8,128)S(1)}, f32[1,64,320]{2,1,0:T(8,128)S(1)}, u32[]{:S(2)}, u32[]{:S(2)}) collective-permute-start(f32[1,64,320]{2,1,0:T(8,128)S(1)} %get-tuple-element.14), channel_id=1, source_target_pairs={{4,0},{8,4},{12,8},{16,12},{20,16},{24,20},{28,24},{5,1},{9,5},{13... | collective-permute-start | bytes 245768 | tf_op jit(solution)/shard_map/ppermute | solution.py:55
  56.4 0.8 fusion.146
  57.2 3.4 %collective-permute-start.6 = (f32[1,64,320]{2,1,0:T(8,128)S(1)}, f32[1,64,320]{2,1,0:T(8,128)S(1)}, u32[]{:S(2)}, u32[]{:S(2)}) collective-permute-start(f32[1,64,320]{2,1,0:T(8,128)S(1)} %get-tuple-element.16), channel_id=1, source_target_pairs={{0,4},{4,8},{8,12},{12,16},{16,20},{20,24},{24,28},{1,5},{5,9},{9,... | collective-permute-start | bytes 245768 | tf_op jit(solution)/shard_map/ppermute | solution.py:54
  61.2 3.4 %collective-permute-done.6 = f32[1,64,320]{2,1,0:T(8,128)S(1)} collective-permute-done((f32[1,64,320]{2,1,0:T(8,128)S(1)}, f32[1,64,320]{2,1,0:T(8,128)S(1)}, u32[]{:S(2)}, u32[]{:S(2)}) %collective-permute-start.6) | collective-permute-done | bytes 81952 | tf_op jit(solution)/shard_map/ppermute | solution.py:54
  66.0 3.5 %collective-permute-start.8 = (f32[2,4,32,160]{3,2,0,1:T(8,128)S(1)}, f32[2,4,32,160]{3,2,0,1:T(8,128)S(1)}, u32[]{:S(2)}, u32[]{:S(2)}) collective-permute-start(f32[2,4,32,160]{3,2,0,1:T(8,128)S(1)} %pad_maximum_fusion.21), channel_id=1, source_target_pairs={{0,8},{4,12},{8,16},{12,20},{16,24},{20,28},{1,9},{5,13},{9,17},{1... | collective-permute-start | bytes 491528 | tf_op jit(solution)/shard_map/ppermute | solution.py:54
  69.6 2.5 %collective-permute-start.9 = (f32[2,4,32,160]{3,2,0,1:T(8,128)S(1)}, f32[2,4,32,160]{3,2,0,1:T(8,128)S(1)}, u32[]{:S(2)}, u32[]{:S(2)}) collective-permute-start(f32[2,4,32,160]{3,2,0,1:T(8,128)S(1)} %pad_maximum_fusion.21), channel_id=1, source_target_pairs={{0,4},{4,8},{8,12},{12,16},{16,20},{20,24},{24,28},{1,5},{5,9},{9,... | collective-permute-start | bytes 491528 | tf_op jit(solution)/shard_map/ppermute | solution.py:54
  72.3 4.2 %collective-permute-start.10 = (f32[2,4,32,160]{3,2,0,1:T(8,128)S(1)}, f32[2,4,32,160]{3,2,0,1:T(8,128)S(1)}, u32[]{:S(2)}, u32[]{:S(2)}) collective-permute-start(f32[2,4,32,160]{3,2,0,1:T(8,128)S(1)} %pad_maximum_fusion.21), channel_id=1, source_target_pairs={{4,0},{8,4},{12,8},{16,12},{20,16},{24,20},{28,24},{5,1},{9,5},{13... | collective-permute-start | bytes 491528 | tf_op jit(solution)/shard_map/ppermute | solution.py:55
  76.5 1.9 %collective-permute-start.11 = (f32[2,4,32,160]{3,2,0,1:T(8,128)S(1)}, f32[2,4,32,160]{3,2,0,1:T(8,128)S(1)}, u32[]{:S(2)}, u32[]{:S(2)}) collective-permute-start(f32[2,4,32,160]{3,2,0,1:T(8,128)S(1)} %pad_maximum_fusion.21), channel_id=1, source_target_pairs={{8,0},{12,4},{16,8},{20,12},{24,16},{28,20},{9,1},{13,5},{17,9},{2... | collective-permute-start | bytes 491528 | tf_op jit(solution)/shard_map/ppermute | solution.py:55
  78.5 2.0 %collective-permute-done.9 = f32[2,4,32,160]{3,2,0,1:T(8,128)S(1)} collective-permute-done((f32[2,4,32,160]{3,2,0,1:T(8,128)S(1)}, f32[2,4,32,160]{3,2,0,1:T(8,128)S(1)}, u32[]{:S(2)}, u32[]{:S(2)}) %collective-permute-start.9) | collective-permute-done | bytes 163872 | tf_op jit(solution)/shard_map/ppermute | solution.py:54
  80.5 5.2 %collective-permute-done.10 = f32[2,4,32,160]{3,2,0,1:T(8,128)S(1)} collective-permute-done((f32[2,4,32,160]{3,2,0,1:T(8,128)S(1)}, f32[2,4,32,160]{3,2,0,1:T(8,128)S(1)}, u32[]{:S(2)}, u32[]{:S(2)}) %collective-permute-start.10) | collective-permute-done | bytes 163872 | tf_op jit(solution)/shard_map/ppermute | solution.py:55
  85.8 2.2 %collective-permute-done.11 = f32[2,4,32,160]{3,2,0,1:T(8,128)S(1)} collective-permute-done((f32[2,4,32,160]{3,2,0,1:T(8,128)S(1)}, f32[2,4,32,160]{3,2,0,1:T(8,128)S(1)}, u32[]{:S(2)}, u32[]{:S(2)}) %collective-permute-start.11) | collective-permute-done | bytes 163872 | tf_op jit(solution)/shard_map/ppermute | solution.py:55
  90.7 0.7 broadcast_in_dim.28
  91.4 4.4 %all-to-all-start = ((f32[8,1,4,16,80]{4,3,2,1,0:T(8,128)}), f32[8,1,4,16,80]{4,3,2,1,0:T(8,128)}, u32[]{:S(2)}, u32[]{:S(2)}) async-start(f32[8,1,4,16,80]{4,3,2,1,0:T(8,128)} %broadcast_in_dim.28), calls=%async_computation | async-start | bytes 524288 | tf_op jit(solution)/shard_map/all_to_all | solution.py:62
  96.9 5.3 %all-to-all-done = f32[8,1,4,16,80]{4,3,2,1,0:T(8,128)} async-done(((f32[8,1,4,16,80]{4,3,2,1,0:T(8,128)}), f32[8,1,4,16,80]{4,3,2,1,0:T(8,128)}, u32[]{:S(2)}, u32[]{:S(2)}) %all-to-all-start) | async-done | bytes 163872 | tf_op jit(solution)/shard_map/all_to_all | solution.py:62
  102.2 0.9 slice_bitcast_fusion.18
  103.2 1.0 fusion.235
  104.3 0.9 fusion.178
  105.4 0.9 fusion.190
  106.5 1.1 fusion.202
  110.0 3.5 %collective-permute-start.12 = (f32[2,64,320]{2,1,0:T(8,128)S(1)}, f32[2,64,320]{2,1,0:T(8,128)S(1)}, u32[]{:S(2)}, u32[]{:S(2)}) collective-permute-start(f32[2,64,320]{2,1,0:T(8,128)S(1)} %get-tuple-element.79), channel_id=1, source_target_pairs={{0,4},{4,8},{8,12},{12,16},{16,20},{20,24},{24,28},{1,5},{5,9},{9,... | collective-permute-start | bytes 491528 | tf_op jit(solution)/shard_map/ppermute | solution.py:54
  113.6 3.4 %collective-permute-start.13 = (f32[2,64,320]{2,1,0:T(8,128)S(1)}, f32[2,64,320]{2,1,0:T(8,128)S(1)}, u32[]{:S(2)}, u32[]{:S(2)}) collective-permute-start(f32[2,64,320]{2,1,0:T(8,128)S(1)} %get-tuple-element.80), channel_id=1, source_target_pairs={{4,0},{8,4},{12,8},{16,12},{20,16},{24,20},{28,24},{5,1},{9,5},{13... | collective-permute-start | bytes 491528 | tf_op jit(solution)/shard_map/ppermute | solution.py:55
  117.1 1.6 %collective-permute-done.12 = f32[2,64,320]{2,1,0:T(8,128)S(1)} collective-permute-done((f32[2,64,320]{2,1,0:T(8,128)S(1)}, f32[2,64,320]{2,1,0:T(8,128)S(1)}, u32[]{:S(2)}, u32[]{:S(2)}) %collective-permute-start.12) | collective-permute-done | bytes 163872 | tf_op jit(solution)/shard_map/ppermute | solution.py:54
  118.6 2.5 %collective-permute-done.13 = f32[2,64,320]{2,1,0:T(8,128)S(1)} collective-permute-done((f32[2,64,320]{2,1,0:T(8,128)S(1)}, f32[2,64,320]{2,1,0:T(8,128)S(1)}, u32[]{:S(2)}, u32[]{:S(2)}) %collective-permute-start.13) | collective-permute-done | bytes 163872 | tf_op jit(solution)/shard_map/ppermute | solution.py:55
  121.5 0.8 copy-done.1
  122.3 0.8 fusion.43
  123.5 0.6 copy-done.51
  124.2 4.3 %collective-permute-start.15 = (f32[1,64,320]{2,1,0:T(8,128)S(1)}, f32[1,64,320]{2,1,0:T(8,128)S(1)}, u32[]{:S(2)}, u32[]{:S(2)}) collective-permute-start(f32[1,64,320]{2,1,0:T(8,128)S(1)} %fusion.136), channel_id=1, source_target_pairs={{4,0},{8,4},{12,8},{16,12},{20,16},{24,20},{28,24},{5,1},{9,5},{13... | collective-permute-start | bytes 245768 | tf_op jit(solution)/shard_map/ppermute | solution.py:55
  128.7 1.9 %collective-permute-start.14 = (f32[1,64,320]{2,1,0:T(8,128)S(1)}, f32[1,64,320]{2,1,0:T(8,128)S(1)}, u32[]{:S(2)}, u32[]{:S(2)}) collective-permute-start(f32[1,64,320]{2,1,0:T(8,128)S(1)} %fusion.126), channel_id=1, source_target_pairs={{0,4},{4,8},{8,12},{12,16},{16,20},{20,24},{24,28},{1,5},{5,9},{9,... | collective-permute-start | bytes 245768 | tf_op jit(solution)/shard_map/ppermute | solution.py:54
  131.1 4.9 %collective-permute-done.14 = f32[1,64,320]{2,1,0:T(8,128)S(1)} collective-permute-done((f32[1,64,320]{2,1,0:T(8,128)S(1)}, f32[1,64,320]{2,1,0:T(8,128)S(1)}, u32[]{:S(2)}, u32[]{:S(2)}) %collective-permute-start.14) | collective-permute-done | bytes 81952 | tf_op jit(solution)/shard_map/ppermute | solution.py:54
  136.3 0.8 copy-done.50
  137.1 1.5 %fusion.54 = (f32[4,64,256]{2,1,0:T(8,128)}, f32[4,64,256]{2,1,0:T(8,128)}) fusion(f32[4,64,320]{2,1,0:T(8,128)S(1)} %copy-done.50, f32[4,64,319]{2,1,0:T(8,128)S(1)} %get-tuple-element.78, f32[4,64,320]{2,1,0:T(8,128)S(1)} %slice.1224, f32[4,64,319]{2,1,0:T(8,128)S(1)} %get-tuple-element.77, f32[4,64,320]{2,1,0:T(8,128)S(1)} %slice.1222, ...), kind=kLoop, calls=%fused_computation.107 | loop fusion | flops 589824 | bytes 3012608 | tf_op jit(solution)/shard_map/div | solution.py:220
  (246 shorter events, 16.3 us)
Async XLA Ops:
  2.3 6.9 %copy-start.16 = (f32[4,64,256]{2,1,0:T(8,128)S(1)}, f32[4,64,256]{2,1,0:T(8,128)}, u32[]{:S(2)}) copy-start(f32[4,64,256]{2,1,0:T(8,128)} %param.7) | copy-start | bytes 786436
  2.3 6.9 %copy-start.18 = (f32[4,64,256]{2,1,0:T(8,128)S(1)}, f32[4,64,256]{2,1,0:T(8,128)}, u32[]{:S(2)}) copy-start(f32[4,64,256]{2,1,0:T(8,128)} %param.6) | copy-start | bytes 786436
  2.3 6.9 %copy-start.20 = (f32[4,64,256]{2,1,0:T(8,128)S(1)}, f32[4,64,256]{2,1,0:T(8,128)}, u32[]{:S(2)}) copy-start(f32[4,64,256]{2,1,0:T(8,128)} %param.5) | copy-start | bytes 786436
  2.4 6.5 %collective-permute-start = (f32[4,4,16,128]{3,2,1,0:T(8,128)S(1)}, f32[4,4,16,128]{3,2,1,0:T(8,128)S(1)}, u32[]{:S(2)}, u32[]{:S(2)}) collective-permute-start(f32[4,4,16,128]{3,2,1,0:T(8,128)S(1)} %copy.22), channel_id=1, source_target_pairs={{0,1},{1,2},{2,3},{3,0},{4,5},{5,6},{6,7},{7,4},{8,9},{9,10},{10,1... | collective-permute-start | bytes 393224 | tf_op jit(solution)/shard_map/ppermute | solution.py:41
  2.6 6.4 %collective-permute-start.1 = (f32[4,4,16,128]{3,2,1,0:T(8,128)S(1)}, f32[4,4,16,128]{3,2,1,0:T(8,128)S(1)}, u32[]{:S(2)}, u32[]{:S(2)}) collective-permute-start(f32[4,4,16,128]{3,2,1,0:T(8,128)S(1)} %copy.23), channel_id=1, source_target_pairs={{1,0},{2,1},{3,2},{0,3},{5,4},{6,5},{7,6},{4,7},{9,8},{10,9},{11,1... | collective-permute-start | bytes 393224 | tf_op jit(solution)/shard_map/ppermute | solution.py:42
  9.0 2.0 %copy-start.10 = (f32[4,4,64,32]{3,2,1,0:T(8,128)}, f32[4,4,64,32]{3,2,1,0:T(8,128)S(1)}, u32[]{:S(2)}) copy-start(f32[4,4,64,32]{3,2,1,0:T(8,128)S(1)} %reshape.115) | copy-start | bytes 393220
  9.2 1.8 %copy-start.12 = (f32[4,4,64,32]{3,2,1,0:T(8,128)}, f32[4,4,64,32]{3,2,1,0:T(8,128)S(1)}, u32[]{:S(2)}) copy-start(f32[4,4,64,32]{3,2,1,0:T(8,128)S(1)} %reshape.117) | copy-start | bytes 393220
  12.0 33.6 %copy-start.8 = (f32[4,2,64,320]{3,2,0,1:T(8,128)}, f32[4,2,64,320]{3,2,0,1:T(8,128)S(1)}, u32[]{:S(2)}) copy-start(f32[4,2,64,320]{3,2,0,1:T(8,128)S(1)} %get-tuple-element.30) | copy-start | bytes 1966084
  14.7 26.7 %collective-permute-start.4 = (f32[1,2,64,320]{3,2,0,1:T(8,128)}, f32[1,2,64,320]{3,2,0,1:T(8,128)}, u32[]{:S(2)}, u32[]{:S(2)}) collective-permute-start(f32[1,2,64,320]{3,2,0,1:T(8,128)} %get-tuple-element.27), channel_id=1, source_target_pairs={{0,4},{4,8},{8,12},{12,16},{16,20},{20,24},{24,28},{1,5},{5,9},{9,... | collective-permute-start | bytes 491528 | tf_op jit(solution)/shard_map/ppermute | solution.py:54
  18.1 23.2 %collective-permute-start.5 = (f32[1,2,64,320]{3,2,0,1:T(8,128)}, f32[1,2,64,320]{3,2,0,1:T(8,128)}, u32[]{:S(2)}, u32[]{:S(2)}) collective-permute-start(f32[1,2,64,320]{3,2,0,1:T(8,128)} %get-tuple-element.28), channel_id=1, source_target_pairs={{4,0},{8,4},{12,8},{16,12},{20,16},{24,20},{28,24},{5,1},{9,5},{13... | collective-permute-start | bytes 491528 | tf_op jit(solution)/shard_map/ppermute | solution.py:55
  21.5 22.2 %collective-permute-start.2 = (f32[2,2,64,320]{3,2,0,1:T(8,128)}, f32[2,2,64,320]{3,2,0,1:T(8,128)}, u32[]{:S(2)}, u32[]{:S(2)}) collective-permute-start(f32[2,2,64,320]{3,2,0,1:T(8,128)} %get-tuple-element.31), channel_id=1, source_target_pairs={{0,4},{4,8},{8,12},{12,16},{16,20},{20,24},{24,28},{1,5},{5,9},{9,... | collective-permute-start | bytes 983048 | tf_op jit(solution)/shard_map/ppermute | solution.py:54
  24.0 21.6 %collective-permute-start.3 = (f32[2,2,64,320]{3,2,0,1:T(8,128)}, f32[2,2,64,320]{3,2,0,1:T(8,128)}, u32[]{:S(2)}, u32[]{:S(2)}) collective-permute-start(f32[2,2,64,320]{3,2,0,1:T(8,128)} %get-tuple-element.32), channel_id=1, source_target_pairs={{4,0},{8,4},{12,8},{16,12},{20,16},{24,20},{28,24},{5,1},{9,5},{13... | collective-permute-start | bytes 983048 | tf_op jit(solution)/shard_map/ppermute | solution.py:55
  31.0 10.4 %copy-start.37 = (f32[4,2,64,320]{3,2,0,1:T(8,128)S(1)}, f32[4,2,64,320]{3,2,0,1:T(8,128)}, u32[]{:S(2)}) copy-start(f32[4,2,64,320]{3,2,0,1:T(8,128)} %get-tuple-element.29) | copy-start | bytes 1966084
  37.5 51.4 %copy-start.42 = (f32[32,2,160]{2,0,1:T(8,128)}, f32[32,2,160]{2,0,1:T(8,128)S(1)}, u32[]{:S(2)}) copy-start(f32[32,2,160]{2,0,1:T(8,128)S(1)} %get-tuple-element.121) | copy-start | bytes 122884
  47.8 1.6 %copy-start.61 = (pred[6]{0:T(512)(128)(4,1)S(1)}, pred[6]{0:T(512)(128)(4,1)}, u32[]{:S(2)}) copy-start(pred[6]{0:T(512)(128)(4,1)} %compare_and_fusion.6) | copy-start | bytes 22
  49.4 15.2 %copy-start = (f32[6,1,64,320]{3,2,1,0:T(8,128)}, f32[6,1,64,320]{3,2,1,0:T(8,128)S(1)}, u32[]{:S(2)}) copy-start(f32[6,1,64,320]{3,2,1,0:T(8,128)S(1)} %get-tuple-element.20) | copy-start | bytes 1474564
  49.4 15.2 %copy-start.2 = (f32[6,64,320]{2,1,0:T(8,128)}, f32[6,64,320]{2,1,0:T(8,128)S(1)}, u32[]{:S(2)}) copy-start(f32[6,64,320]{2,1,0:T(8,128)S(1)} %get-tuple-element.21) | copy-start | bytes 1474564
  49.4 15.2 %copy-start.4 = (f32[6,64,320]{2,1,0:T(8,128)}, f32[6,64,320]{2,1,0:T(8,128)S(1)}, u32[]{:S(2)}) copy-start(f32[6,64,320]{2,1,0:T(8,128)S(1)} %get-tuple-element.22) | copy-start | bytes 1474564
  49.4 15.2 %copy-start.14 = (f32[6,64,320]{2,1,0:T(8,128)}, f32[6,64,320]{2,1,0:T(8,128)S(1)}, u32[]{:S(2)}) copy-start(f32[6,64,320]{2,1,0:T(8,128)S(1)} %get-tuple-element.18) | copy-start | bytes 1474564
  51.7 1.2 copy-start.17
  51.8 1.3 copy-start.19
  51.8 1.4 %copy-start.21 = (f32[4,64,256]{2,1,0:T(8,128)S(1)}, f32[4,64,256]{2,1,0:T(8,128)}, u32[]{:S(2)}) copy-start(f32[4,64,256]{2,1,0:T(8,128)} %param.5) | copy-start | bytes 786436
  51.8 1.5 %copy-start.22 = (f32[4,64,256]{2,1,0:T(8,128)S(1)}, f32[4,64,256]{2,1,0:T(8,128)}, u32[]{:S(2)}) copy-start(f32[4,64,256]{2,1,0:T(8,128)} %param.4) | copy-start | bytes 786436
  54.0 10.6 %copy-start.46 = (f32[1,64,320]{2,1,0:T(8,128)}, f32[1,64,320]{2,1,0:T(8,128)S(1)}, u32[]{:S(2)}) copy-start(f32[1,64,320]{2,1,0:T(8,128)S(1)} %get-tuple-element.14) | copy-start | bytes 245764
  54.0 7.1 %collective-permute-start.7 = (f32[1,64,320]{2,1,0:T(8,128)S(1)}, f32[1,64,320]{2,1,0:T(8,128)S(1)}, u32[]{:S(2)}, u32[]{:S(2)}) collective-permute-start(f32[1,64,320]{2,1,0:T(8,128)S(1)} %get-tuple-element.14), channel_id=1, source_target_pairs={{4,0},{8,4},{12,8},{16,12},{20,16},{24,20},{28,24},{5,1},{9,5},{13... | collective-permute-start | bytes 245768 | tf_op jit(solution)/shard_map/ppermute | solution.py:55
  57.2 7.4 %copy-start.48 = (f32[1,64,320]{2,1,0:T(8,128)}, f32[1,64,320]{2,1,0:T(8,128)S(1)}, u32[]{:S(2)}) copy-start(f32[1,64,320]{2,1,0:T(8,128)S(1)} %get-tuple-element.16) | copy-start | bytes 245764
  57.2 7.4 %collective-permute-start.6 = (f32[1,64,320]{2,1,0:T(8,128)S(1)}, f32[1,64,320]{2,1,0:T(8,128)S(1)}, u32[]{:S(2)}, u32[]{:S(2)}) collective-permute-start(f32[1,64,320]{2,1,0:T(8,128)S(1)} %get-tuple-element.16), channel_id=1, source_target_pairs={{0,4},{4,8},{8,12},{12,16},{16,20},{20,24},{24,28},{1,5},{5,9},{9,... | collective-permute-start | bytes 245768 | tf_op jit(solution)/shard_map/ppermute | solution.py:54
  60.9 3.8 %copy-start.38 = (f32[2,64,320]{2,1,0:T(8,128)}, f32[2,64,320]{2,1,0:T(8,128)S(1)}, u32[]{:S(2)}) copy-start(f32[2,64,320]{2,1,0:T(8,128)S(1)} %fusion.101) | copy-start | bytes 491524
  64.7 1.3 copy-start.40
  64.7 1.3 copy-start.41
  64.7 4.8 %copy-start.53 = (pred[32]{0:T(512)(128)(4,1)S(1)}, pred[32]{0:T(512)(128)(4,1)}, u32[]{:S(2)}) copy-start(pred[32]{0:T(512)(128)(4,1)} %compare_and_fusion.1) | copy-start | bytes 100
  64.7 4.8 %copy-start.55 = (s32[32]{0:T(128)S(1)}, s32[32]{0:T(128)}, u32[]{:S(2)}) copy-start(s32[32]{0:T(128)} %iota_shift-right-logical_fusion.2) | copy-start | bytes 388
  66.0 12.4 %collective-permute-start.8 = (f32[2,4,32,160]{3,2,0,1:T(8,128)S(1)}, f32[2,4,32,160]{3,2,0,1:T(8,128)S(1)}, u32[]{:S(2)}, u32[]{:S(2)}) collective-permute-start(f32[2,4,32,160]{3,2,0,1:T(8,128)S(1)} %pad_maximum_fusion.21), channel_id=1, source_target_pairs={{0,8},{4,12},{8,16},{12,20},{16,24},{20,28},{1,9},{5,13},{9,17},{1... | collective-permute-start | bytes 491528 | tf_op jit(solution)/shard_map/ppermute | solution.py:54
  69.6 10.8 %collective-permute-start.9 = (f32[2,4,32,160]{3,2,0,1:T(8,128)S(1)}, f32[2,4,32,160]{3,2,0,1:T(8,128)S(1)}, u32[]{:S(2)}, u32[]{:S(2)}) collective-permute-start(f32[2,4,32,160]{3,2,0,1:T(8,128)S(1)} %pad_maximum_fusion.21), channel_id=1, source_target_pairs={{0,4},{4,8},{8,12},{12,16},{16,20},{20,24},{24,28},{1,5},{5,9},{9,... | collective-permute-start | bytes 491528 | tf_op jit(solution)/shard_map/ppermute | solution.py:54
  72.3 13.5 %collective-permute-start.10 = (f32[2,4,32,160]{3,2,0,1:T(8,128)S(1)}, f32[2,4,32,160]{3,2,0,1:T(8,128)S(1)}, u32[]{:S(2)}, u32[]{:S(2)}) collective-permute-start(f32[2,4,32,160]{3,2,0,1:T(8,128)S(1)} %pad_maximum_fusion.21), channel_id=1, source_target_pairs={{4,0},{8,4},{12,8},{16,12},{20,16},{24,20},{28,24},{5,1},{9,5},{13... | collective-permute-start | bytes 491528 | tf_op jit(solution)/shard_map/ppermute | solution.py:55
  76.5 11.5 %collective-permute-start.11 = (f32[2,4,32,160]{3,2,0,1:T(8,128)S(1)}, f32[2,4,32,160]{3,2,0,1:T(8,128)S(1)}, u32[]{:S(2)}, u32[]{:S(2)}) collective-permute-start(f32[2,4,32,160]{3,2,0,1:T(8,128)S(1)} %pad_maximum_fusion.21), channel_id=1, source_target_pairs={{8,0},{12,4},{16,8},{20,12},{24,16},{28,20},{9,1},{13,5},{17,9},{2... | collective-permute-start | bytes 491528 | tf_op jit(solution)/shard_map/ppermute | solution.py:55
  80.5 8.5 %copy-start.23 = (f32[2,4,32,160]{3,2,0,1:T(8,128)}, f32[2,4,32,160]{3,2,0,1:T(8,128)S(1)}, u32[]{:S(2)}) copy-start(f32[2,4,32,160]{3,2,0,1:T(8,128)S(1)} %collective-permute-done.9) | copy-start | bytes 491524
  85.8 3.2 %copy-start.25 = (f32[2,4,32,160]{3,2,0,1:T(8,128)}, f32[2,4,32,160]{3,2,0,1:T(8,128)S(1)}, u32[]{:S(2)}) copy-start(f32[2,4,32,160]{3,2,0,1:T(8,128)S(1)} %collective-permute-done.10) | copy-start | bytes 491524
  88.3 1.4 %copy-start.6 = (f32[8,31,160]{2,1,0:T(8,128)}, f32[8,31,160]{2,1,0:T(8,128)S(1)}, u32[]{:S(2)}) copy-start(f32[8,31,160]{2,1,0:T(8,128)S(1)} %fusion.58) | copy-start | bytes 476164
  91.4 10.7 %all-to-all-start = ((f32[8,1,4,16,80]{4,3,2,1,0:T(8,128)}), f32[8,1,4,16,80]{4,3,2,1,0:T(8,128)}, u32[]{:S(2)}, u32[]{:S(2)}) async-start(f32[8,1,4,16,80]{4,3,2,1,0:T(8,128)} %broadcast_in_dim.28), calls=%async_computation | async-start | bytes 524288 | tf_op jit(solution)/shard_map/all_to_all | solution.py:62
  105.2 2.4 %copy-start.64 = (s32[160]{0:T(256)S(1)}, s32[160]{0:T(256)}, u32[]{:S(2)}) copy-start(s32[160]{0:T(256)} %get-tuple-element.130) | copy-start | bytes 1924
  105.2 2.4 %copy-start.66 = (s32[160]{0:T(256)S(1)}, s32[160]{0:T(256)}, u32[]{:S(2)}) copy-start(s32[160]{0:T(256)} %get-tuple-element.131) | copy-start | bytes 1924
  105.2 2.4 %copy-start.73 = (pred[160]{0:T(512)(128)(4,1)S(1)}, pred[160]{0:T(512)(128)(4,1)}, u32[]{:S(2)}) copy-start(pred[160]{0:T(512)(128)(4,1)} %compare_and_fusion) | copy-start | bytes 484
  105.3 2.7 %copy-start.54 = (pred[32]{0:T(512)(128)(4,1)S(1)}, pred[32]{0:T(512)(128)(4,1)}, u32[]{:S(2)}) copy-start(pred[32]{0:T(512)(128)(4,1)} %compare_and_fusion.1) | copy-start | bytes 100
  105.3 2.7 %copy-start.56 = (s32[32]{0:T(128)S(1)}, s32[32]{0:T(128)}, u32[]{:S(2)}) copy-start(s32[32]{0:T(128)} %iota_shift-right-logical_fusion.2) | copy-start | bytes 388
  105.3 2.9 %copy-start.28 = (f32[6,32,160]{2,1,0:T(8,128)S(1)}, f32[6,32,160]{2,1,0:T(8,128)}, u32[]{:S(2)}) copy-start(f32[6,32,160]{2,1,0:T(8,128)} %copy-done.27) | copy-start | bytes 368644
  106.4 2.0 %copy-start.7 = (f32[8,31,160]{2,1,0:T(8,128)S(1)}, f32[8,31,160]{2,1,0:T(8,128)}, u32[]{:S(2)}) copy-start(f32[8,31,160]{2,1,0:T(8,128)} %copy-done.6) | copy-start | bytes 476164
  106.4 2.0 %copy-start.24 = (f32[2,4,32,160]{3,2,0,1:T(8,128)S(1)}, f32[2,4,32,160]{3,2,0,1:T(8,128)}, u32[]{:S(2)}) copy-start(f32[2,4,32,160]{3,2,0,1:T(8,128)} %copy-done.23) | copy-start | bytes 491524
  106.4 2.0 %copy-start.26 = (f32[2,4,32,160]{3,2,0,1:T(8,128)S(1)}, f32[2,4,32,160]{3,2,0,1:T(8,128)}, u32[]{:S(2)}) copy-start(f32[2,4,32,160]{3,2,0,1:T(8,128)} %copy-done.25) | copy-start | bytes 491524
  106.4 2.0 %copy-start.30 = (f32[8,1,32,160]{3,2,0,1:T(8,128)S(1)}, f32[8,1,32,160]{3,2,0,1:T(8,128)}, u32[]{:S(2)}) copy-start(f32[8,1,32,160]{3,2,0,1:T(8,128)} %copy-done.29) | copy-start | bytes 491524
  106.5 2.0 %copy-start.32 = (f32[8,1,32,160]{3,2,0,1:T(8,128)S(1)}, f32[8,1,32,160]{3,2,0,1:T(8,128)}, u32[]{:S(2)}) copy-start(f32[8,1,32,160]{3,2,0,1:T(8,128)} %copy-done.31) | copy-start | bytes 491524
  106.5 2.0 %copy-start.34 = (f32[8,32,160]{2,1,0:T(8,128)S(1)}, f32[8,32,160]{2,1,0:T(8,128)}, u32[]{:S(2)}) copy-start(f32[8,32,160]{2,1,0:T(8,128)} %copy-done.33) | copy-start | bytes 491524
  106.5 2.0 %copy-start.36 = (f32[8,32,160]{2,1,0:T(8,128)S(1)}, f32[8,32,160]{2,1,0:T(8,128)}, u32[]{:S(2)}) copy-start(f32[8,32,160]{2,1,0:T(8,128)} %copy-done.35) | copy-start | bytes 491524
  106.5 2.0 %copy-start.43 = (f32[32,2,160]{2,0,1:T(8,128)S(1)}, f32[32,2,160]{2,0,1:T(8,128)}, u32[]{:S(2)}) copy-start(f32[32,2,160]{2,0,1:T(8,128)} %copy-done.42) | copy-start | bytes 122884
  106.5 2.0 %copy-start.45 = (f32[8,32,160]{2,1,0:T(8,128)S(1)}, f32[8,32,160]{2,1,0:T(8,128)}, u32[]{:S(2)}) copy-start(f32[8,32,160]{2,1,0:T(8,128)} %copy-done.44) | copy-start | bytes 491524
  106.5 2.0 %copy-start.70 = (pred[4]{0:T(512)(128)(4,1)S(1)}, pred[4]{0:T(512)(128)(4,1)}, u32[]{:S(2)}) copy-start(pred[4]{0:T(512)(128)(4,1)} %compare_and_fusion.3) | copy-start | bytes 16
  109.2 7.8 %copy-start.15 = (f32[6,64,320]{2,1,0:T(8,128)S(1)}, f32[6,64,320]{2,1,0:T(8,128)}, u32[]{:S(2)}) copy-start(f32[6,64,320]{2,1,0:T(8,128)} %copy-done.14) | copy-start | bytes 1474564
  109.9 7.0 %copy-start.3 = (f32[6,64,320]{2,1,0:T(8,128)S(1)}, f32[6,64,320]{2,1,0:T(8,128)}, u32[]{:S(2)}) copy-start(f32[6,64,320]{2,1,0:T(8,128)} %copy-done.2) | copy-start | bytes 1474564
  110.0 7.0 %copy-start.5 = (f32[6,64,320]{2,1,0:T(8,128)S(1)}, f32[6,64,320]{2,1,0:T(8,128)}, u32[]{:S(2)}) copy-start(f32[6,64,320]{2,1,0:T(8,128)} %copy-done.4) | copy-start | bytes 1474564
  110.0 8.6 %collective-permute-start.12 = (f32[2,64,320]{2,1,0:T(8,128)S(1)}, f32[2,64,320]{2,1,0:T(8,128)S(1)}, u32[]{:S(2)}, u32[]{:S(2)}) collective-permute-start(f32[2,64,320]{2,1,0:T(8,128)S(1)} %get-tuple-element.79), channel_id=1, source_target_pairs={{0,4},{4,8},{8,12},{12,16},{16,20},{20,24},{24,28},{1,5},{5,9},{9,... | collective-permute-start | bytes 491528 | tf_op jit(solution)/shard_map/ppermute | solution.py:54
  113.6 7.6 %collective-permute-start.13 = (f32[2,64,320]{2,1,0:T(8,128)S(1)}, f32[2,64,320]{2,1,0:T(8,128)S(1)}, u32[]{:S(2)}, u32[]{:S(2)}) collective-permute-start(f32[2,64,320]{2,1,0:T(8,128)S(1)} %get-tuple-element.80), channel_id=1, source_target_pairs={{4,0},{8,4},{12,8},{16,12},{20,16},{24,20},{28,24},{5,1},{9,5},{13... | collective-permute-start | bytes 491528 | tf_op jit(solution)/shard_map/ppermute | solution.py:55
  123.4 5.1 %copy-start.52 = (f32[1,64,320]{2,1,0:T(8,128)S(1)}, f32[1,64,320]{2,1,0:T(8,128)}, u32[]{:S(2)}) copy-start(f32[1,64,320]{2,1,0:T(8,128)} %get-tuple-element.17) | copy-start | bytes 245764
  124.2 6.9 %collective-permute-start.15 = (f32[1,64,320]{2,1,0:T(8,128)S(1)}, f32[1,64,320]{2,1,0:T(8,128)S(1)}, u32[]{:S(2)}, u32[]{:S(2)}) collective-permute-start(f32[1,64,320]{2,1,0:T(8,128)S(1)} %fusion.136), channel_id=1, source_target_pairs={{4,0},{8,4},{12,8},{16,12},{20,16},{24,20},{28,24},{5,1},{9,5},{13... | collective-permute-start | bytes 245768 | tf_op jit(solution)/shard_map/ppermute | solution.py:55
  128.7 7.4 %collective-permute-start.14 = (f32[1,64,320]{2,1,0:T(8,128)S(1)}, f32[1,64,320]{2,1,0:T(8,128)S(1)}, u32[]{:S(2)}, u32[]{:S(2)}) collective-permute-start(f32[1,64,320]{2,1,0:T(8,128)S(1)} %fusion.126), channel_id=1, source_target_pairs={{0,4},{4,8},{8,12},{12,16},{16,20},{20,24},{24,28},{1,5},{5,9},{9,... | collective-permute-start | bytes 245768 | tf_op jit(solution)/shard_map/ppermute | solution.py:54
  (27 other events, 24.6 us)

commit v17 on v13

--- a/solution.py
+++ b/solution.py
@@ -169,12 +169,17 @@
 def shards(source, k_alt, k_inc, k_raan):
     length = source.shape[-1]
     halo_r = min(RAAN_HALO, length)
-    wide = raan_extend(jnp.stack([source, k_alt, k_inc, k_raan], axis=1), halo_r)
+    raw = jnp.stack([source, k_alt, k_inc, k_raan], axis=1)
+    count = lax.axis_size("alt")
+    below = lax.ppermute(raw[-1:, 0:2], "alt", [(i, i + 1) for i in range(count - 1)])
+    above = lax.ppermute(raw[:1, 0:2], "alt", [(i + 1, i) for i in range(count - 1)])
+    wide = raan_extend(raw, halo_r)
+    edges = raan_extend(jnp.concatenate([below, above], axis=0), halo_r)
     wide_source, wide_alt, wide_inc, wide_raan = (wide[:, i] for i in range(4))
     coef_two = [coarsen(part) for part in (wide_alt, wide_inc, wide_raan)]
     coef_three = [coarsen(part) for part in coef_two]
 
-    first = alt_extend(wide[:, 0:2], 1)
+    first = jnp.concatenate([edges[:1], wide[:, 0:2], edges[1:]], axis=0)
     source_x = first[:, 0]
     weights_one = make_weights(first[:, 1], wide_inc, wide_raan, 1.0, 0)
 

time: 136 us -> 147 us (1.081)
  local copies, waits for them, and re-layouts: 13.9 us -> 19.9 us
  waiting for transfers between devices: 33.5 us -> 38.2 us
  starting transfers between devices: 55 us -> 53.4 us
  matrix products: 7.58 us -> 9.1 us
    ppermute x8 -> x7, starting transfers between devices: 27.5 us -> 20.7 us  [alt_extend(): below.insert(0, lax.ppermute(values[low:], 'alt', up))]
    ppermute x8 -> x7, waiting for transfers between devices: 11.5 us -> 17.7 us  [alt_extend(): below.insert(0, lax.ppermute(values[low:], 'alt', up))]
    ppermute x0 -> x2, starting transfers between devices: none -> 5.83 us  [the longest x1 3.3 us: shards(): lax.ppermute(raw[:1, 0:2], 'alt', [(i + 1, i) for i in range(count - 1)])]
    ppermute x8 -> x7, waiting for transfers between devices: 16.2 us -> 12.9 us  [alt_extend(): above.append(lax.ppermute(values[:high], 'alt', down))]
    dot_general x8, matrix products: 1.23 us -> 3.1 us  [coarsen(): summed = jnp.matmul(pairing(width).T[None], summed, precision=HIGH)]
    add x12, other arithmetic: 4.03 us -> 2.15 us  [split_sweep(): rows.append(centre + OMEGA * (aim - applied) / diagonal)]
    all_to_all x1, waiting for transfers between devices: 5.2 us -> 6.94 us  [spread_gather(): every = lax.all_to_all(copies, 'alt', 0, 0)]
    another operation x1 -> x2, other arithmetic: 1.28 us -> 2.97 us  [shards(): raw = jnp.stack([source, k_alt, k_inc, k_raan], axis=1)]
  transfers between devices with their start and end apart: 19 -> 21, of which waited for: 12 -> 11; matrix products, arithmetic and copies ran while one was open for 12% -> 18% of each run, Pallas kernels for 0% -> 0%
where the time goes in v17:
time: 147 us; the launch traced here: 144 us
  starting transfers between devices  53.4 us (36%)
  waiting for transfers between devices  38.2 us (26%)
  other arithmetic  20.7 us (14%)
  local copies, waits for them, and re-layouts  19.9 us (14%)
  matrix products  9.1 us (6%)
  between operations  2.75 us (2%)
    ppermute x7, starting transfers between devices, alt_extend(): below.insert(0, lax.ppermute(values[low:], 'alt', up))  20.7 us
    ppermute x7, starting transfers between devices, alt_extend(): above.append(lax.ppermute(values[:high], 'alt', down))  20 us
    ppermute x7, waiting for transfers between devices, alt_extend(): below.insert(0, lax.ppermute(values[low:], 'alt', up))  17.7 us
    ppermute x7, waiting for transfers between devices, alt_extend(): above.append(lax.ppermute(values[:high], 'alt', down))  12.9 us
    all_to_all x1, waiting for transfers between devices, spread_gather(): every = lax.all_to_all(copies, 'alt', 0, 0)  6.94 us
    all_to_all x1, starting transfers between devices, spread_gather(): every = lax.all_to_all(copies, 'alt', 0, 0)  5.36 us
    dot_general x8, matrix products, coarsen(): summed = jnp.matmul(summed, pairing(length), precision=HIGH)  4.71 us
    slice x20, local copies, waits for them, and re-layouts, lane_shifts(): left = jnp.concatenate([zero, values[..., :-1]], axis=-1)  4.03 us
  transfers between devices with their start and end apart: 21, of which 11 were waited for; matrix products, arithmetic and copies ran while one was open for 18% of the time, Pallas kernels for 0%

profile of v17, /device:TPU:8, one launch (start us, length us, event | category | flops | bytes accessed | tf_op | source)
XLA Modules:
  0.0 144.0 jit_solution(9252301826585899327)
XLA Ops:
  0.6 1.7 %pad_maximum_fusion.28 = (f32[1,2,64,256]{3,2,1,0:T(8,128)}, f32[1,2,64,256]{3,2,1,0:T(8,128)}) fusion(f32[4,1,64,256]{3,2,1,0:T(8,128)} %bitcast.437, f32[4,1,64,256]{3,2,1,0:T(8,128)} %bitcast.443), kind=kLoop, calls=%fused_computation.212 | loop fusion | flops 65536 | bytes 786432 | tf_op jit(solution)/shard_map/stack | solution.py:172
  2.3 3.3 %collective-permute-start.3 = (f32[1,2,64,256]{3,2,1,0:T(8,128)}, f32[1,2,64,256]{3,2,1,0:T(8,128)}, u32[]{:S(2)}, u32[]{:S(2)}) collective-permute-start(f32[1,2,64,256]{3,2,1,0:T(8,128)} %get-tuple-element.31), channel_id=1, source_target_pairs={{4,0},{8,4},{12,8},{16,12},{20,16},{24,20},{28,24},{5,1},{9,5},{13... | collective-permute-start | bytes 393224 | tf_op jit(solution)/shard_map/ppermute | solution.py:175
  5.6 2.5 %collective-permute-start.2 = (f32[1,2,64,256]{3,2,1,0:T(8,128)}, f32[1,2,64,256]{3,2,1,0:T(8,128)}, u32[]{:S(2)}, u32[]{:S(2)}) collective-permute-start(f32[1,2,64,256]{3,2,1,0:T(8,128)} %get-tuple-element.32), channel_id=1, source_target_pairs={{0,4},{4,8},{8,12},{12,16},{16,20},{20,24},{24,28},{1,5},{5,9},{9,... | collective-permute-start | bytes 393224 | tf_op jit(solution)/shard_map/ppermute | solution.py:174
  8.2 1.3 pad_maximum_fusion.1
  11.2 0.6 iota_shift-right-logical_fusion.2
  13.4 0.6 iota_shift-right-logical_fusion.1
  14.5 0.6 iota_shift-right-logical_fusion
  15.1 0.7 collective-permute-done
  16.4 0.8 fusion.379
  17.2 0.7 fusion.378
  17.8 0.6 pad_maximum_fusion
  18.5 0.8 fusion.368
  19.4 0.8 fusion.369
  20.2 1.2 slice_bitcast_fusion
  21.4 0.7 fusion.383
  22.1 0.7 fusion.382
  22.8 0.9 constant_dynamic-update-slice_fusion.1
  23.7 0.9 constant_dynamic-update-slice_fusion
  24.6 0.7 fusion.359
  25.4 1.6 %reshape.134 = f32[2,2,16,128]{3,2,1,0:T(8,128)} reshape(f32[2,2,64,32]{3,2,1,0:T(8,128)} %get-tuple-element.68) | data formatting | bytes 65536 | tf_op jit(solution)/shard_map/reshape | solution.py:41
  27.0 0.7 reshape.136
  27.7 0.9 collective-permute-start.5
  28.8 1.1 fusion.335
  30.4 0.8 bitcast_reduce_fusion.6
  31.2 0.8 bitcast_reduce_fusion.4
  32.3 0.9 fusion.201
  33.6 0.8 bitcast_reduce_fusion.5
  34.4 0.9 fusion.202
  35.3 1.0 fusion.354
  36.9 0.7 slice-done
  37.9 1.6 %fusion.22 = (f32[4,64,320]{2,1,0:T(8,128)S(1)}, f32[4,64,320]{2,1,0:T(8,128)S(1)}, f32[4,1,64,320]{3,2,1,0:T(8,128)S(1)}, f32[4,1,64,320]{3,2,1,0:T(8,128)S(1)}, f32[4,64,320]{2,1,0:T(8,128)S(1)}) fusion(f32[4,63,320]{2,1,0:T(8,128)S(1)} %fusion.4, f32[4,64,319]{2,1,0:T(8,128)S(1)} %copy-done.52, f32[4,4,64,320]{3,2,1,0:T(8,128)} %copy-done, ...), kind=kLoop, calls=%fused_computation.51 | loop fusion | flops 1310720 | bytes 4252672 | tf_op jit(solution)/shard_map/add | solution.py:89
  39.9 4.3 %collective-permute-start.7 = (f32[1,64,320]{2,1,0:T(8,128)S(1)}, f32[1,64,320]{2,1,0:T(8,128)S(1)}, u32[]{:S(2)}, u32[]{:S(2)}) collective-permute-start(f32[1,64,320]{2,1,0:T(8,128)S(1)} %fusion.198), channel_id=1, source_target_pairs={{4,0},{8,4},{12,8},{16,12},{20,16},{24,20},{28,24},{5,1},{9,5},{13... | collective-permute-start | bytes 245768 | tf_op jit(solution)/shard_map/ppermute | solution.py:55
  44.6 2.2 %collective-permute-start.6 = (f32[1,64,320]{2,1,0:T(8,128)S(1)}, f32[1,64,320]{2,1,0:T(8,128)S(1)}, u32[]{:S(2)}, u32[]{:S(2)}) collective-permute-start(f32[1,64,320]{2,1,0:T(8,128)S(1)} %fusion.186), channel_id=1, source_target_pairs={{0,4},{4,8},{8,12},{12,16},{16,20},{20,24},{24,28},{1,5},{5,9},{9,... | collective-permute-start | bytes 245768 | tf_op jit(solution)/shard_map/ppermute | solution.py:54
  47.7 5.6 %collective-permute-done.6 = f32[1,64,320]{2,1,0:T(8,128)S(1)} collective-permute-done((f32[1,64,320]{2,1,0:T(8,128)S(1)}, f32[1,64,320]{2,1,0:T(8,128)S(1)}, u32[]{:S(2)}, u32[]{:S(2)}) %collective-permute-start.6) | collective-permute-done | bytes 81952 | tf_op jit(solution)/shard_map/ppermute | solution.py:54
  53.4 1.9 %collective-permute-start.9 = (f32[1,64,320]{2,1,0:T(8,128)S(1)}, f32[1,64,320]{2,1,0:T(8,128)S(1)}, u32[]{:S(2)}, u32[]{:S(2)}) collective-permute-start(f32[1,64,320]{2,1,0:T(8,128)S(1)} %fusion.175), channel_id=1, source_target_pairs={{4,0},{8,4},{12,8},{16,12},{20,16},{24,20},{28,24},{5,1},{9,5},{13... | collective-permute-start | bytes 245768 | tf_op jit(solution)/shard_map/ppermute | solution.py:55
  55.5 3.9 %collective-permute-start.8 = (f32[1,64,320]{2,1,0:T(8,128)S(1)}, f32[1,64,320]{2,1,0:T(8,128)S(1)}, u32[]{:S(2)}, u32[]{:S(2)}) collective-permute-start(f32[1,64,320]{2,1,0:T(8,128)S(1)} %fusion.165), channel_id=1, source_target_pairs={{0,4},{4,8},{8,12},{12,16},{16,20},{20,24},{24,28},{1,5},{5,9},{9,... | collective-permute-start | bytes 245768 | tf_op jit(solution)/shard_map/ppermute | solution.py:54
  60.1 3.0 %collective-permute-done.8 = f32[1,64,320]{2,1,0:T(8,128)S(1)} collective-permute-done((f32[1,64,320]{2,1,0:T(8,128)S(1)}, f32[1,64,320]{2,1,0:T(8,128)S(1)}, u32[]{:S(2)}, u32[]{:S(2)}) %collective-permute-start.8) | collective-permute-done | bytes 81952 | tf_op jit(solution)/shard_map/ppermute | solution.py:54
  64.5 3.5 %collective-permute-start.10 = (f32[2,4,32,160]{3,2,0,1:T(8,128)S(1)}, f32[2,4,32,160]{3,2,0,1:T(8,128)S(1)}, u32[]{:S(2)}, u32[]{:S(2)}) collective-permute-start(f32[2,4,32,160]{3,2,0,1:T(8,128)S(1)} %pad_maximum_fusion.18), channel_id=1, source_target_pairs={{0,8},{4,12},{8,16},{12,20},{16,24},{20,28},{1,9},{5,13},{9,17},{1... | collective-permute-start | bytes 491528 | tf_op jit(solution)/shard_map/ppermute | solution.py:54
  68.1 2.8 %collective-permute-start.11 = (f32[2,4,32,160]{3,2,0,1:T(8,128)S(1)}, f32[2,4,32,160]{3,2,0,1:T(8,128)S(1)}, u32[]{:S(2)}, u32[]{:S(2)}) collective-permute-start(f32[2,4,32,160]{3,2,0,1:T(8,128)S(1)} %pad_maximum_fusion.18), channel_id=1, source_target_pairs={{0,4},{4,8},{8,12},{12,16},{16,20},{20,24},{24,28},{1,5},{5,9},{9,... | collective-permute-start | bytes 491528 | tf_op jit(solution)/shard_map/ppermute | solution.py:54
  71.1 2.4 %collective-permute-start.13 = (f32[2,4,32,160]{3,2,0,1:T(8,128)S(1)}, f32[2,4,32,160]{3,2,0,1:T(8,128)S(1)}, u32[]{:S(2)}, u32[]{:S(2)}) collective-permute-start(f32[2,4,32,160]{3,2,0,1:T(8,128)S(1)} %pad_maximum_fusion.18), channel_id=1, source_target_pairs={{8,0},{12,4},{16,8},{20,12},{24,16},{28,20},{9,1},{13,5},{17,9},{2... | collective-permute-start | bytes 491528 | tf_op jit(solution)/shard_map/ppermute | solution.py:55
  73.5 2.8 %collective-permute-start.12 = (f32[2,4,32,160]{3,2,0,1:T(8,128)S(1)}, f32[2,4,32,160]{3,2,0,1:T(8,128)S(1)}, u32[]{:S(2)}, u32[]{:S(2)}) collective-permute-start(f32[2,4,32,160]{3,2,0,1:T(8,128)S(1)} %pad_maximum_fusion.18), channel_id=1, source_target_pairs={{4,0},{8,4},{12,8},{16,12},{20,16},{24,20},{28,24},{5,1},{9,5},{13... | collective-permute-start | bytes 491528 | tf_op jit(solution)/shard_map/ppermute | solution.py:55
  76.4 3.0 %collective-permute-done.11 = f32[2,4,32,160]{3,2,0,1:T(8,128)S(1)} collective-permute-done((f32[2,4,32,160]{3,2,0,1:T(8,128)S(1)}, f32[2,4,32,160]{3,2,0,1:T(8,128)S(1)}, u32[]{:S(2)}, u32[]{:S(2)}) %collective-permute-start.11) | collective-permute-done | bytes 163872 | tf_op jit(solution)/shard_map/ppermute | solution.py:54
  79.4 5.5 %collective-permute-done.12 = f32[2,4,32,160]{3,2,0,1:T(8,128)S(1)} collective-permute-done((f32[2,4,32,160]{3,2,0,1:T(8,128)S(1)}, f32[2,4,32,160]{3,2,0,1:T(8,128)S(1)}, u32[]{:S(2)}, u32[]{:S(2)}) %collective-permute-start.12) | collective-permute-done | bytes 163872 | tf_op jit(solution)/shard_map/ppermute | solution.py:55
  87.5 0.7 broadcast_in_dim.20
  88.2 5.4 %all-to-all-start = ((f32[8,1,4,16,80]{4,3,2,1,0:T(8,128)}), f32[8,1,4,16,80]{4,3,2,1,0:T(8,128)}, u32[]{:S(2)}, u32[]{:S(2)}) async-start(f32[8,1,4,16,80]{4,3,2,1,0:T(8,128)} %broadcast_in_dim.20), calls=%async_computation | async-start | bytes 524288 | tf_op jit(solution)/shard_map/all_to_all | solution.py:62
  93.6 0.6 compare_and_fusion.3
  94.7 6.9 %all-to-all-done = f32[8,1,4,16,80]{4,3,2,1,0:T(8,128)} async-done(((f32[8,1,4,16,80]{4,3,2,1,0:T(8,128)}), f32[8,1,4,16,80]{4,3,2,1,0:T(8,128)}, u32[]{:S(2)}, u32[]{:S(2)}) %all-to-all-start) | async-done | bytes 163872 | tf_op jit(solution)/shard_map/all_to_all | solution.py:62
  101.6 0.9 slice_bitcast_fusion.18
  102.7 1.0 fusion.278
  103.8 0.9 fusion.221
  104.9 0.9 fusion.233
  106.0 1.1 fusion.245
  109.9 0.7 copy-done.9
  110.9 2.5 %collective-permute-start.14 = (f32[1,64,320]{2,1,0:T(8,128)S(1)}, f32[1,64,320]{2,1,0:T(8,128)S(1)}, u32[]{:S(2)}, u32[]{:S(2)}) collective-permute-start(f32[1,64,320]{2,1,0:T(8,128)S(1)} %slice.1311), channel_id=1, source_target_pairs={{0,4},{4,8},{8,12},{12,16},{16,20},{20,24},{24,28},{1,5},{5,9},{9,... | collective-permute-start | bytes 245768 | tf_op jit(solution)/shard_map/ppermute | solution.py:54
  113.4 5.0 %collective-permute-done.14 = f32[1,64,320]{2,1,0:T(8,128)S(1)} collective-permute-done((f32[1,64,320]{2,1,0:T(8,128)S(1)}, f32[1,64,320]{2,1,0:T(8,128)S(1)}, u32[]{:S(2)}, u32[]{:S(2)}) %collective-permute-start.14) | collective-permute-done | bytes 81952 | tf_op jit(solution)/shard_map/ppermute | solution.py:54
  118.6 2.8 %collective-permute-start.17 = (f32[1,64,320]{2,1,0:T(8,128)S(1)}, f32[1,64,320]{2,1,0:T(8,128)S(1)}, u32[]{:S(2)}, u32[]{:S(2)}) collective-permute-start(f32[1,64,320]{2,1,0:T(8,128)S(1)} %get-tuple-element.37), channel_id=1, source_target_pairs={{4,0},{8,4},{12,8},{16,12},{20,16},{24,20},{28,24},{5,1},{9,5},{13... | collective-permute-start | bytes 245768 | tf_op jit(solution)/shard_map/ppermute | solution.py:55
  121.5 1.9 %collective-permute-start.15 = (f32[1,64,320]{2,1,0:T(8,128)S(1)}, f32[1,64,320]{2,1,0:T(8,128)S(1)}, u32[]{:S(2)}, u32[]{:S(2)}) collective-permute-start(f32[1,64,320]{2,1,0:T(8,128)S(1)} %get-tuple-element.38), channel_id=1, source_target_pairs={{4,0},{8,4},{12,8},{16,12},{20,16},{24,20},{28,24},{5,1},{9,5},{13... | collective-permute-start | bytes 245768 | tf_op jit(solution)/shard_map/ppermute | solution.py:55
  123.5 4.6 %collective-permute-done.15 = f32[1,64,320]{2,1,0:T(8,128)S(1)} collective-permute-done((f32[1,64,320]{2,1,0:T(8,128)S(1)}, f32[1,64,320]{2,1,0:T(8,128)S(1)}, u32[]{:S(2)}, u32[]{:S(2)}) %collective-permute-start.15) | collective-permute-done | bytes 81952 | tf_op jit(solution)/shard_map/ppermute | solution.py:55
  128.2 3.9 %collective-permute-start.16 = (f32[1,64,320]{2,1,0:T(8,128)S(1)}, f32[1,64,320]{2,1,0:T(8,128)S(1)}, u32[]{:S(2)}, u32[]{:S(2)}) collective-permute-start(f32[1,64,320]{2,1,0:T(8,128)S(1)} %fusion.145), channel_id=1, source_target_pairs={{0,4},{4,8},{8,12},{12,16},{16,20},{20,24},{24,28},{1,5},{5,9},{9,... | collective-permute-start | bytes 245768 | tf_op jit(solution)/shard_map/ppermute | solution.py:54
  132.4 1.9 %collective-permute-start.18 = (f32[1,64,320]{2,1,0:T(8,128)S(1)}, f32[1,64,320]{2,1,0:T(8,128)S(1)}, u32[]{:S(2)}, u32[]{:S(2)}) collective-permute-start(f32[1,64,320]{2,1,0:T(8,128)S(1)} %fusion.125), channel_id=1, source_target_pairs={{0,4},{4,8},{8,12},{12,16},{16,20},{20,24},{24,28},{1,5},{5,9},{9,... | collective-permute-start | bytes 245768 | tf_op jit(solution)/shard_map/ppermute | solution.py:54
  134.6 1.1 collective-permute-done.16
  135.8 3.8 %collective-permute-start.19 = (f32[1,64,320]{2,1,0:T(8,128)S(1)}, f32[1,64,320]{2,1,0:T(8,128)S(1)}, u32[]{:S(2)}, u32[]{:S(2)}) collective-permute-start(f32[1,64,320]{2,1,0:T(8,128)S(1)} %fusion.135), channel_id=1, source_target_pairs={{4,0},{8,4},{12,8},{16,12},{20,16},{24,20},{28,24},{5,1},{9,5},{13... | collective-permute-start | bytes 245768 | tf_op jit(solution)/shard_map/ppermute | solution.py:55
  139.8 2.5 %collective-permute-done.19 = f32[1,64,320]{2,1,0:T(8,128)S(1)} collective-permute-done((f32[1,64,320]{2,1,0:T(8,128)S(1)}, f32[1,64,320]{2,1,0:T(8,128)S(1)}, u32[]{:S(2)}, u32[]{:S(2)}) %collective-permute-start.19) | collective-permute-done | bytes 81952 | tf_op jit(solution)/shard_map/ppermute | solution.py:55
  142.5 1.6 %fusion.30 = (f32[4,64,256]{2,1,0:T(8,128)}, f32[4,64,256]{2,1,0:T(8,128)}) fusion(f32[4,63,320]{2,1,0:T(8,128)S(1)} %fusion.4, f32[4,63,320]{2,1,0:T(8,128)S(1)} %get-tuple-element.34, f32[4,64,320]{2,1,0:T(8,128)S(1)} %copy-done.58, f32[4,64,319]{2,1,0:T(8,128)S(1)} %get-tuple-element.36, f32[4,64,320]{2,1,0:T(8,128)S(1)} %get-tuple-element.18, ...), kind=kLoop, calls=%fused_computation.70 | loop fusion | flops 655360 | bytes 3395584 | tf_op jit(solution)/shard_map/div | solution.py:224
  (332 shorter events, 17.9 us)
Async XLA Ops:
  2.3 21.4 %collective-permute-start.3 = (f32[1,2,64,256]{3,2,1,0:T(8,128)}, f32[1,2,64,256]{3,2,1,0:T(8,128)}, u32[]{:S(2)}, u32[]{:S(2)}) collective-permute-start(f32[1,2,64,256]{3,2,1,0:T(8,128)} %get-tuple-element.31), channel_id=1, source_target_pairs={{4,0},{8,4},{12,8},{16,12},{20,16},{24,20},{28,24},{5,1},{9,5},{13... | collective-permute-start | bytes 393224 | tf_op jit(solution)/shard_map/ppermute | solution.py:175
  5.6 17.2 %collective-permute-start.2 = (f32[1,2,64,256]{3,2,1,0:T(8,128)}, f32[1,2,64,256]{3,2,1,0:T(8,128)}, u32[]{:S(2)}, u32[]{:S(2)}) collective-permute-start(f32[1,2,64,256]{3,2,1,0:T(8,128)} %get-tuple-element.32), channel_id=1, source_target_pairs={{0,4},{4,8},{8,12},{12,16},{16,20},{20,24},{24,28},{1,5},{5,9},{9,... | collective-permute-start | bytes 393224 | tf_op jit(solution)/shard_map/ppermute | solution.py:174
  9.7 6.5 %copy-start.10 = (f32[4,64,256]{2,1,0:T(8,128)S(1)}, f32[4,64,256]{2,1,0:T(8,128)}, u32[]{:S(2)}) copy-start(f32[4,64,256]{2,1,0:T(8,128)} %param.5) | copy-start | bytes 786436
  9.7 6.5 %copy-start.12 = (f32[4,64,256]{2,1,0:T(8,128)S(1)}, f32[4,64,256]{2,1,0:T(8,128)}, u32[]{:S(2)}) copy-start(f32[4,64,256]{2,1,0:T(8,128)} %param.4) | copy-start | bytes 786436
  9.7 6.5 %copy-start.20 = (f32[4,64,256]{2,1,0:T(8,128)S(1)}, f32[4,64,256]{2,1,0:T(8,128)}, u32[]{:S(2)}) copy-start(f32[4,64,256]{2,1,0:T(8,128)} %param.7) | copy-start | bytes 786436
  9.7 6.5 %copy-start.22 = (f32[4,64,256]{2,1,0:T(8,128)S(1)}, f32[4,64,256]{2,1,0:T(8,128)}, u32[]{:S(2)}) copy-start(f32[4,64,256]{2,1,0:T(8,128)} %param.6) | copy-start | bytes 786436
  9.9 6.1 %collective-permute-start.1 = (f32[4,4,16,128]{3,2,1,0:T(8,128)S(1)}, f32[4,4,16,128]{3,2,1,0:T(8,128)S(1)}, u32[]{:S(2)}, u32[]{:S(2)}) collective-permute-start(f32[4,4,16,128]{3,2,1,0:T(8,128)S(1)} %reshape.132), channel_id=1, source_target_pairs={{1,0},{2,1},{3,2},{0,3},{5,4},{6,5},{7,6},{4,7},{9,8},{10,9},{11,1... | collective-permute-start | bytes 393224 | tf_op jit(solution)/shard_map/ppermute | solution.py:42
  10.5 5.3 %collective-permute-start = (f32[4,4,16,128]{3,2,1,0:T(8,128)S(1)}, f32[4,4,16,128]{3,2,1,0:T(8,128)S(1)}, u32[]{:S(2)}, u32[]{:S(2)}) collective-permute-start(f32[4,4,16,128]{3,2,1,0:T(8,128)S(1)} %reshape.130), channel_id=1, source_target_pairs={{0,1},{1,2},{2,3},{3,0},{4,5},{5,6},{6,7},{7,4},{8,9},{9,10},{10,1... | collective-permute-start | bytes 393224 | tf_op jit(solution)/shard_map/ppermute | solution.py:41
  13.4 20.2 %copy-start.73 = (s32[64]{0:T(128)}, s32[64]{0:T(128)S(1)}, u32[]{:S(2)}) copy-start(s32[64]{0:T(128)S(1)} %get-tuple-element.143) | copy-start | bytes 772
  15.1 18.1 %copy-start.85 = (s32[320]{0:T(512)}, s32[320]{0:T(512)S(1)}, u32[]{:S(2)}) copy-start(s32[320]{0:T(512)S(1)} %get-tuple-element.140) | copy-start | bytes 3844
  16.4 5.7 %copy-start.17 = (f32[1,64,320]{2,1,0:T(8,128)}, f32[1,64,320]{2,1,0:T(8,128)S(1)}, u32[]{:S(2)}) copy-start(f32[1,64,320]{2,1,0:T(8,128)S(1)} %get-tuple-element.20) | copy-start | bytes 245764
  18.5 18.0 %copy-start = (f32[4,4,64,320]{3,2,1,0:T(8,128)}, f32[4,4,64,320]{3,2,1,0:T(8,128)S(1)}, u32[]{:S(2)}) copy-start(f32[4,4,64,320]{3,2,1,0:T(8,128)S(1)} %pad_maximum_fusion) | copy-start | bytes 3932164
  27.7 8.9 %collective-permute-start.5 = (f32[2,2,16,128]{3,2,1,0:T(8,128)}, f32[2,2,16,128]{3,2,1,0:T(8,128)S(1)}, u32[]{:S(2)}, u32[]{:S(2)}) collective-permute-start(f32[2,2,16,128]{3,2,1,0:T(8,128)} %reshape.136), channel_id=1, source_target_pairs={{1,0},{2,1},{3,2},{0,3},{5,4},{6,5},{7,6},{4,7},{9,8},{10,9},{11,1... | collective-permute-start | bytes 98312 | tf_op jit(solution)/shard_map/ppermute | solution.py:42
  28.6 7.9 %collective-permute-start.4 = (f32[2,2,16,128]{3,2,1,0:T(8,128)}, f32[2,2,16,128]{3,2,1,0:T(8,128)S(1)}, u32[]{:S(2)}, u32[]{:S(2)}) collective-permute-start(f32[2,2,16,128]{3,2,1,0:T(8,128)} %reshape.134), channel_id=1, source_target_pairs={{0,1},{1,2},{2,3},{3,0},{4,5},{5,6},{6,7},{7,4},{8,9},{9,10},{10,1... | collective-permute-start | bytes 98312 | tf_op jit(solution)/shard_map/ppermute | solution.py:41
  28.6 3.4 %copy-start.91 = (s32[160]{0:T(256)S(1)}, s32[160]{0:T(256)}, u32[]{:S(2)}) copy-start(s32[160]{0:T(256)} %get-tuple-element.144) | copy-start | bytes 1924
  28.6 3.4 %copy-start.94 = (s32[160]{0:T(256)S(1)}, s32[160]{0:T(256)}, u32[]{:S(2)}) copy-start(s32[160]{0:T(256)} %get-tuple-element.145) | copy-start | bytes 1924
  28.6 3.4 %copy-start.103 = (pred[160]{0:T(512)(128)(4,1)S(1)}, pred[160]{0:T(512)(128)(4,1)}, u32[]{:S(2)}) copy-start(pred[160]{0:T(512)(128)(4,1)} %compare_and_fusion) | copy-start | bytes 484
  30.3 6.0 %copy-start.76 = (s32[32]{0:T(128)S(1)}, s32[32]{0:T(128)}, u32[]{:S(2)}) copy-start(s32[32]{0:T(128)} %broadcast_add_fusion.2) | copy-start | bytes 388
  30.4 6.0 %copy-start.79 = (s32[32]{0:T(128)S(1)}, s32[32]{0:T(128)}, u32[]{:S(2)}) copy-start(s32[32]{0:T(128)} %iota_shift-right-logical_fusion.2) | copy-start | bytes 388
  30.4 6.0 %copy-start.82 = (pred[32]{0:T(512)(128)(4,1)S(1)}, pred[32]{0:T(512)(128)(4,1)}, u32[]{:S(2)}) copy-start(pred[32]{0:T(512)(128)(4,1)} %compare_and_fusion.1) | copy-start | bytes 100
  39.5 15.9 %copy-start.8 = (f32[4,64,320]{2,1,0:T(8,128)}, f32[4,64,320]{2,1,0:T(8,128)S(1)}, u32[]{:S(2)}) copy-start(f32[4,64,320]{2,1,0:T(8,128)S(1)} %get-tuple-element.14) | copy-start | bytes 983044
  39.7 4.7 %copy-start.18 = (f32[1,64,320]{2,1,0:T(8,128)S(1)}, f32[1,64,320]{2,1,0:T(8,128)}, u32[]{:S(2)}) copy-start(f32[1,64,320]{2,1,0:T(8,128)} %copy-done.17) | copy-start | bytes 245764
  39.7 4.7 %copy-start.67 = (f32[1,64,319]{2,1,0:T(8,128)S(1)}, f32[1,64,319]{2,1,0:T(8,128)}, u32[]{:S(2)}) copy-start(f32[1,64,319]{2,1,0:T(8,128)} %get-tuple-element.116) | copy-start | bytes 244996
  39.7 4.7 %copy-start.68 = (f32[1,64,319]{2,1,0:T(8,128)S(1)}, f32[1,64,319]{2,1,0:T(8,128)}, u32[]{:S(2)}) copy-start(f32[1,64,319]{2,1,0:T(8,128)} %get-tuple-element.117) | copy-start | bytes 244996
  39.7 4.7 %copy-start.69 = (f32[1,63,320]{2,1,0:T(8,128)S(1)}, f32[1,63,320]{2,1,0:T(8,128)}, u32[]{:S(2)}) copy-start(f32[1,63,320]{2,1,0:T(8,128)} %get-tuple-element.114) | copy-start | bytes 241924
  39.7 4.7 %copy-start.70 = (f32[1,63,320]{2,1,0:T(8,128)S(1)}, f32[1,63,320]{2,1,0:T(8,128)}, u32[]{:S(2)}) copy-start(f32[1,63,320]{2,1,0:T(8,128)} %get-tuple-element.115) | copy-start | bytes 241924
  39.9 15.4 %collective-permute-start.7 = (f32[1,64,320]{2,1,0:T(8,128)S(1)}, f32[1,64,320]{2,1,0:T(8,128)S(1)}, u32[]{:S(2)}, u32[]{:S(2)}) collective-permute-start(f32[1,64,320]{2,1,0:T(8,128)S(1)} %fusion.198), channel_id=1, source_target_pairs={{4,0},{8,4},{12,8},{16,12},{20,16},{24,20},{28,24},{5,1},{9,5},{13... | collective-permute-start | bytes 245768 | tf_op jit(solution)/shard_map/ppermute | solution.py:55
  44.4 2.5 %copy-start.1 = (f32[4,4,64,320]{3,2,1,0:T(8,128)S(1)}, f32[4,4,64,320]{3,2,1,0:T(8,128)}, u32[]{:S(2)}) copy-start(f32[4,4,64,320]{3,2,1,0:T(8,128)} %copy-done) | copy-start | bytes 3932164
  44.4 2.5 %copy-start.59 = (f32[2,63,320]{2,1,0:T(8,128)S(1)}, f32[2,63,320]{2,1,0:T(8,128)}, u32[]{:S(2)}) copy-start(f32[2,63,320]{2,1,0:T(8,128)} %get-tuple-element.86) | copy-start | bytes 483844
  44.4 2.5 %copy-start.60 = (f32[2,63,320]{2,1,0:T(8,128)S(1)}, f32[2,63,320]{2,1,0:T(8,128)}, u32[]{:S(2)}) copy-start(f32[2,63,320]{2,1,0:T(8,128)} %get-tuple-element.87) | copy-start | bytes 483844
  44.6 8.6 %collective-permute-start.6 = (f32[1,64,320]{2,1,0:T(8,128)S(1)}, f32[1,64,320]{2,1,0:T(8,128)S(1)}, u32[]{:S(2)}, u32[]{:S(2)}) collective-permute-start(f32[1,64,320]{2,1,0:T(8,128)S(1)} %fusion.186), channel_id=1, source_target_pairs={{0,4},{4,8},{8,12},{12,16},{16,20},{20,24},{24,28},{1,5},{5,9},{9,... | collective-permute-start | bytes 245768 | tf_op jit(solution)/shard_map/ppermute | solution.py:54
  47.6 15.5 %copy-start.41 = (f32[2,64,320]{2,1,0:T(8,128)}, f32[2,64,320]{2,1,0:T(8,128)S(1)}, u32[]{:S(2)}) copy-start(f32[2,64,320]{2,1,0:T(8,128)S(1)} %fusion.87) | copy-start | bytes 491524
  53.4 9.7 %copy-start.53 = (f32[1,64,320]{2,1,0:T(8,128)}, f32[1,64,320]{2,1,0:T(8,128)S(1)}, u32[]{:S(2)}) copy-start(f32[1,64,320]{2,1,0:T(8,128)S(1)} %fusion.175) | copy-start | bytes 245764
  53.4 6.7 %collective-permute-start.9 = (f32[1,64,320]{2,1,0:T(8,128)S(1)}, f32[1,64,320]{2,1,0:T(8,128)S(1)}, u32[]{:S(2)}, u32[]{:S(2)}) collective-permute-start(f32[1,64,320]{2,1,0:T(8,128)S(1)} %fusion.175), channel_id=1, source_target_pairs={{4,0},{8,4},{12,8},{16,12},{20,16},{24,20},{28,24},{5,1},{9,5},{13... | collective-permute-start | bytes 245768 | tf_op jit(solution)/shard_map/ppermute | solution.py:55
  55.5 7.6 %copy-start.55 = (f32[1,64,320]{2,1,0:T(8,128)}, f32[1,64,320]{2,1,0:T(8,128)S(1)}, u32[]{:S(2)}) copy-start(f32[1,64,320]{2,1,0:T(8,128)S(1)} %fusion.165) | copy-start | bytes 245764
  55.5 7.6 %collective-permute-start.8 = (f32[1,64,320]{2,1,0:T(8,128)S(1)}, f32[1,64,320]{2,1,0:T(8,128)S(1)}, u32[]{:S(2)}, u32[]{:S(2)}) collective-permute-start(f32[1,64,320]{2,1,0:T(8,128)S(1)} %fusion.165), channel_id=1, source_target_pairs={{0,4},{4,8},{8,12},{12,16},{16,20},{20,24},{24,28},{1,5},{5,9},{9,... | collective-permute-start | bytes 245768 | tf_op jit(solution)/shard_map/ppermute | solution.py:54
  63.2 4.8 %copy-start.71 = (f32[32,80]{1,0:T(8,128)S(1)}, f32[32,80]{1,0:T(8,128)}, u32[]{:S(2)}) copy-start(f32[32,80]{1,0:T(8,128)} %fusion.201) | copy-start | bytes 30724
  63.2 4.8 %copy-start.77 = (s32[32]{0:T(128)S(1)}, s32[32]{0:T(128)}, u32[]{:S(2)}) copy-start(s32[32]{0:T(128)} %broadcast_add_fusion.2) | copy-start | bytes 388
  63.2 4.8 %copy-start.80 = (s32[32]{0:T(128)S(1)}, s32[32]{0:T(128)}, u32[]{:S(2)}) copy-start(s32[32]{0:T(128)} %iota_shift-right-logical_fusion.2) | copy-start | bytes 388
  63.2 4.8 %copy-start.83 = (pred[32]{0:T(512)(128)(4,1)S(1)}, pred[32]{0:T(512)(128)(4,1)}, u32[]{:S(2)}) copy-start(pred[32]{0:T(512)(128)(4,1)} %compare_and_fusion.1) | copy-start | bytes 100
  63.2 7.8 %copy-start.72 = (f32[32,80]{1,0:T(8,128)S(1)}, f32[32,80]{1,0:T(8,128)}, u32[]{:S(2)}) copy-start(f32[32,80]{1,0:T(8,128)} %fusion.202) | copy-start | bytes 30724
  64.4 22.1 %copy-start.25 = (f32[32,2,160]{2,0,1:T(8,128)}, f32[32,2,160]{2,0,1:T(8,128)S(1)}, u32[]{:S(2)}) copy-start(f32[32,2,160]{2,0,1:T(8,128)S(1)} %convolution_multiply_fusion.3) | copy-start | bytes 122884
  64.5 11.8 %collective-permute-start.10 = (f32[2,4,32,160]{3,2,0,1:T(8,128)S(1)}, f32[2,4,32,160]{3,2,0,1:T(8,128)S(1)}, u32[]{:S(2)}, u32[]{:S(2)}) collective-permute-start(f32[2,4,32,160]{3,2,0,1:T(8,128)S(1)} %pad_maximum_fusion.18), channel_id=1, source_target_pairs={{0,8},{4,12},{8,16},{12,20},{16,24},{20,28},{1,9},{5,13},{9,17},{1... | collective-permute-start | bytes 491528 | tf_op jit(solution)/shard_map/ppermute | solution.py:54
  68.1 11.2 %collective-permute-start.11 = (f32[2,4,32,160]{3,2,0,1:T(8,128)S(1)}, f32[2,4,32,160]{3,2,0,1:T(8,128)S(1)}, u32[]{:S(2)}, u32[]{:S(2)}) collective-permute-start(f32[2,4,32,160]{3,2,0,1:T(8,128)S(1)} %pad_maximum_fusion.18), channel_id=1, source_target_pairs={{0,4},{4,8},{8,12},{12,16},{16,20},{20,24},{24,28},{1,5},{5,9},{9,... | collective-permute-start | bytes 491528 | tf_op jit(solution)/shard_map/ppermute | solution.py:54
  71.1 13.8 %collective-permute-start.13 = (f32[2,4,32,160]{3,2,0,1:T(8,128)S(1)}, f32[2,4,32,160]{3,2,0,1:T(8,128)S(1)}, u32[]{:S(2)}, u32[]{:S(2)}) collective-permute-start(f32[2,4,32,160]{3,2,0,1:T(8,128)S(1)} %pad_maximum_fusion.18), channel_id=1, source_target_pairs={{8,0},{12,4},{16,8},{20,12},{24,16},{28,20},{9,1},{13,5},{17,9},{2... | collective-permute-start | bytes 491528 | tf_op jit(solution)/shard_map/ppermute | solution.py:55
  73.5 11.4 %collective-permute-start.12 = (f32[2,4,32,160]{3,2,0,1:T(8,128)S(1)}, f32[2,4,32,160]{3,2,0,1:T(8,128)S(1)}, u32[]{:S(2)}, u32[]{:S(2)}) collective-permute-start(f32[2,4,32,160]{3,2,0,1:T(8,128)S(1)} %pad_maximum_fusion.18), channel_id=1, source_target_pairs={{4,0},{8,4},{12,8},{16,12},{20,16},{24,20},{28,24},{5,1},{9,5},{13... | collective-permute-start | bytes 491528 | tf_op jit(solution)/shard_map/ppermute | solution.py:55
  79.4 6.4 %copy-start.27 = (f32[2,4,32,160]{3,2,0,1:T(8,128)}, f32[2,4,32,160]{3,2,0,1:T(8,128)S(1)}, u32[]{:S(2)}) copy-start(f32[2,4,32,160]{3,2,0,1:T(8,128)S(1)} %collective-permute-done.11) | copy-start | bytes 491524
  88.2 13.4 %all-to-all-start = ((f32[8,1,4,16,80]{4,3,2,1,0:T(8,128)}), f32[8,1,4,16,80]{4,3,2,1,0:T(8,128)}, u32[]{:S(2)}, u32[]{:S(2)}) async-start(f32[8,1,4,16,80]{4,3,2,1,0:T(8,128)} %broadcast_in_dim.20), calls=%async_computation | async-start | bytes 524288 | tf_op jit(solution)/shard_map/all_to_all | solution.py:62
  103.8 3.4 %copy-start.93 = (s32[160]{0:T(256)S(1)}, s32[160]{0:T(256)}, u32[]{:S(2)}) copy-start(s32[160]{0:T(256)} %get-tuple-element.144) | copy-start | bytes 1924
  103.8 3.4 %copy-start.96 = (s32[160]{0:T(256)S(1)}, s32[160]{0:T(256)}, u32[]{:S(2)}) copy-start(s32[160]{0:T(256)} %get-tuple-element.145) | copy-start | bytes 1924
  103.8 3.4 %copy-start.105 = (pred[160]{0:T(512)(128)(4,1)S(1)}, pred[160]{0:T(512)(128)(4,1)}, u32[]{:S(2)}) copy-start(pred[160]{0:T(512)(128)(4,1)} %compare_and_fusion) | copy-start | bytes 484
  104.7 2.7 %copy-start.78 = (s32[32]{0:T(128)S(1)}, s32[32]{0:T(128)}, u32[]{:S(2)}) copy-start(s32[32]{0:T(128)} %broadcast_add_fusion.2) | copy-start | bytes 388
  104.7 2.7 %copy-start.81 = (s32[32]{0:T(128)S(1)}, s32[32]{0:T(128)}, u32[]{:S(2)}) copy-start(s32[32]{0:T(128)} %iota_shift-right-logical_fusion.2) | copy-start | bytes 388
  104.7 2.7 %copy-start.84 = (pred[32]{0:T(512)(128)(4,1)S(1)}, pred[32]{0:T(512)(128)(4,1)}, u32[]{:S(2)}) copy-start(pred[32]{0:T(512)(128)(4,1)} %compare_and_fusion.1) | copy-start | bytes 100
  104.8 3.0 %copy-start.32 = (f32[6,32,160]{2,1,0:T(8,128)S(1)}, f32[6,32,160]{2,1,0:T(8,128)}, u32[]{:S(2)}) copy-start(f32[6,32,160]{2,1,0:T(8,128)} %copy-done.31) | copy-start | bytes 368644
  110.8 7.7 %copy-start.16 = (f32[1,64,320]{2,1,0:T(8,128)S(1)}, f32[1,64,320]{2,1,0:T(8,128)}, u32[]{:S(2)}) copy-start(f32[1,64,320]{2,1,0:T(8,128)} %copy-done.14) | copy-start | bytes 245764
  110.9 17.1 %copy-start.19 = (f32[1,64,320]{2,1,0:T(8,128)S(1)}, f32[1,64,320]{2,1,0:T(8,128)}, u32[]{:S(2)}) copy-start(f32[1,64,320]{2,1,0:T(8,128)} %copy-done.17) | copy-start | bytes 245764
  110.9 7.5 %collective-permute-start.14 = (f32[1,64,320]{2,1,0:T(8,128)S(1)}, f32[1,64,320]{2,1,0:T(8,128)S(1)}, u32[]{:S(2)}, u32[]{:S(2)}) collective-permute-start(f32[1,64,320]{2,1,0:T(8,128)S(1)} %slice.1311), channel_id=1, source_target_pairs={{0,4},{4,8},{8,12},{12,16},{16,20},{20,24},{24,28},{1,5},{5,9},{9,... | collective-permute-start | bytes 245768 | tf_op jit(solution)/shard_map/ppermute | solution.py:54
  118.6 13.6 %collective-permute-start.17 = (f32[1,64,320]{2,1,0:T(8,128)S(1)}, f32[1,64,320]{2,1,0:T(8,128)S(1)}, u32[]{:S(2)}, u32[]{:S(2)}) collective-permute-start(f32[1,64,320]{2,1,0:T(8,128)S(1)} %get-tuple-element.37), channel_id=1, source_target_pairs={{4,0},{8,4},{12,8},{16,12},{20,16},{24,20},{28,24},{5,1},{9,5},{13... | collective-permute-start | bytes 245768 | tf_op jit(solution)/shard_map/ppermute | solution.py:55
  121.5 6.5 %collective-permute-start.15 = (f32[1,64,320]{2,1,0:T(8,128)S(1)}, f32[1,64,320]{2,1,0:T(8,128)S(1)}, u32[]{:S(2)}, u32[]{:S(2)}) collective-permute-start(f32[1,64,320]{2,1,0:T(8,128)S(1)} %get-tuple-element.38), channel_id=1, source_target_pairs={{4,0},{8,4},{12,8},{16,12},{20,16},{24,20},{28,24},{5,1},{9,5},{13... | collective-permute-start | bytes 245768 | tf_op jit(solution)/shard_map/ppermute | solution.py:55
  128.2 7.5 %collective-permute-start.16 = (f32[1,64,320]{2,1,0:T(8,128)S(1)}, f32[1,64,320]{2,1,0:T(8,128)S(1)}, u32[]{:S(2)}, u32[]{:S(2)}) collective-permute-start(f32[1,64,320]{2,1,0:T(8,128)S(1)} %fusion.145), channel_id=1, source_target_pairs={{0,4},{4,8},{8,12},{12,16},{16,20},{20,24},{24,28},{1,5},{5,9},{9,... | collective-permute-start | bytes 245768 | tf_op jit(solution)/shard_map/ppermute | solution.py:54
  132.4 7.5 %collective-permute-start.18 = (f32[1,64,320]{2,1,0:T(8,128)S(1)}, f32[1,64,320]{2,1,0:T(8,128)S(1)}, u32[]{:S(2)}, u32[]{:S(2)}) collective-permute-start(f32[1,64,320]{2,1,0:T(8,128)S(1)} %fusion.125), channel_id=1, source_target_pairs={{0,4},{4,8},{8,12},{12,16},{16,20},{20,24},{24,28},{1,5},{5,9},{9,... | collective-permute-start | bytes 245768 | tf_op jit(solution)/shard_map/ppermute | solution.py:54
  135.8 6.5 %collective-permute-start.19 = (f32[1,64,320]{2,1,0:T(8,128)S(1)}, f32[1,64,320]{2,1,0:T(8,128)S(1)}, u32[]{:S(2)}, u32[]{:S(2)}) collective-permute-start(f32[1,64,320]{2,1,0:T(8,128)S(1)} %fusion.135), channel_id=1, source_target_pairs={{4,0},{8,4},{12,8},{16,12},{20,16},{24,20},{28,24},{5,1},{9,5},{13... | collective-permute-start | bytes 245768 | tf_op jit(solution)/shard_map/ppermute | solution.py:55
  139.8 2.6 %copy-start.58 = (f32[4,64,320]{2,1,0:T(8,128)S(1)}, f32[4,64,320]{2,1,0:T(8,128)}, u32[]{:S(2)}) copy-start(f32[4,64,320]{2,1,0:T(8,128)} %get-tuple-element.21) | copy-start | bytes 983044
  (64 other events, 93.4 us)

commit v18 on v13

--- a/solution.py
+++ b/solution.py
@@ -180,22 +180,24 @@
 
     density = split_sweep(weights_one, source_x, source_x, 1)
     density = split_sweep(weights_one, alt_extend(density, 1), source_x, 1)
-    applied, density = apply_op(weights_one, alt_extend(density, 1), 1)
+    density_x = alt_extend(density, 1)
+    applied, density = apply_op(weights_one, density_x, 1)
     rhs_two = coarsen(wide_source - applied)
 
-    level_two = alt_extend(jnp.stack([rhs_two] + coef_two, 1), SWEEPS + 2)
+    wide_two = SWEEPS + 3
+    level_two = alt_extend(jnp.stack([rhs_two] + coef_two, 1), wide_two)
     weights_two = make_weights(
         level_two[:, 1],
-        trim(level_two[:, 2], SWEEPS + 2, SWEEPS + 1),
-        trim(level_two[:, 3], SWEEPS + 2, SWEEPS + 1),
+        trim(level_two[:, 2], wide_two, wide_two - 1),
+        trim(level_two[:, 3], wide_two, wide_two - 1),
         0.25,
-        SWEEPS + 1,
-    )
-    rhs_two_x = trim(level_two[:, 0], SWEEPS + 2, SWEEPS + 1)
-    correction = first_sweep(weights_two, rhs_two_x, SWEEPS + 1)
-    correction = sweep(weights_two, correction, SWEEPS + 1, rhs_two_x, SWEEPS + 1)
-    applied, _ = apply_op(weights_two, trim(correction, SWEEPS, 1), 1)
-    rhs_three = coarsen(trim(rhs_two_x, SWEEPS + 1, 0) - applied)
+        wide_two - 1,
+    )
+    rhs_two_x = trim(level_two[:, 0], wide_two, wide_two - 1)
+    correction = first_sweep(weights_two, rhs_two_x, wide_two - 1)
+    correction = sweep(weights_two, correction, wide_two - 1, rhs_two_x, wide_two - 1)
+    applied, _ = apply_op(weights_two, trim(correction, wide_two - 2, 1), 1)
+    rhs_three = coarsen(trim(rhs_two_x, wide_two - 1, 0) - applied)
 
     height = rhs_three.shape[0]
     column = spread_gather(jnp.stack([rhs_three] + coef_three, 1))
@@ -204,17 +206,17 @@
     coarse_part = first_sweep(weights_three, rhs_three_x, 0)
     for _ in range(COARSE_SWEEPS - 1):
         coarse_part = sweep(weights_three, pad_rows(coarse_part), 1, rhs_three_x, 0, masked=False)
-    reach = SWEEPS // 2
+    reach = SWEEPS
     coarse_part = jnp.pad(coarse_part, ((reach, reach), (0, 0), (0, 0)))
     coarse_part = lax.dynamic_slice_in_dim(coarse_part, lax.axis_index("alt") * height, height + 2 * reach, 0)
 
-    correction = correction + refine(coarse_part)
-    for halo in range(SWEEPS, 0, -1):
-        correction = sweep(weights_two, correction, halo, rhs_two_x, SWEEPS + 1)
-
-    density = density + refine(correction)
-    for _ in range(SWEEPS):
-        density = split_sweep(weights_one, alt_extend(density, 1), source_x, 1)
+    correction = correction + trim(refine(coarse_part), 2 * reach, wide_two - 2)
+    for halo in range(wide_two - 2, 1, -1):
+        correction = sweep(weights_two, correction, halo, rhs_two_x, wide_two - 1)
+
+    density = density_x + trim(refine(correction), 2, 1)
+    density = split_sweep(weights_one, density, source_x, 1)
+    density = split_sweep(weights_one, alt_extend(density, 1), source_x, 1)
     applied, centre = apply_op(weights_one, alt_extend(density, 1), 1)
     scaled_residual = (wide_source - applied) / weights_one[0][6]
     keep = slice(halo_r, halo_r + length)

time: 136 us -> 132 us (0.971); the launches traced: 133 us -> 131 us
  waiting for transfers between devices: 33.5 us -> 29.1 us
  starting transfers between devices: 55 us -> 58.5 us
  local copies, waits for them, and re-layouts: 13.9 us -> 16.1 us
  matrix products: 7.58 us -> 5.54 us
  other arithmetic: 20.7 us -> 19.2 us
    ppermute x8, waiting for transfers between devices: 16.2 us -> 7.53 us  [alt_extend(): above.append(lax.ppermute(values[:high], 'alt', down))]
    ppermute x8, waiting for transfers between devices: 11.5 us -> 18.2 us  [alt_extend(): below.insert(0, lax.ppermute(values[low:], 'alt', up))]
    unnamed x180 -> x138, local copies, waits for them, and re-layouts: 3.28 us -> 7.99 us
    ppermute x8, starting transfers between devices: 20.8 us -> 25.4 us  [alt_extend(): above.append(lax.ppermute(values[:high], 'alt', down))]
    all_to_all x1, waiting for transfers between devices: 5.2 us -> 2.65 us  [spread_gather(): every = lax.all_to_all(copies, 'alt', 0, 0)]
    dot_general x8, matrix products: 5.07 us -> 2.81 us  [coarsen(): summed = jnp.matmul(summed, pairing(length), precision=HIGH)]
    add x12 -> x10, other arithmetic: 4.03 us -> 1.8 us  [split_sweep(): rows.append(centre + OMEGA * (aim - applied) / diagonal)]
    slice x11, local copies, waits for them, and re-layouts: 2.33 us -> 0.24 us  [split_sweep(): v_prev = jnp.concatenate([zero_inc, centre[:, :-1]], 1)]
  transfers between devices with their start and end apart: 19 -> 19, of which waited for: 12 -> 10; matrix products, arithmetic and copies ran while one was open for 12% -> 12% of each run, Pallas kernels for 0% -> 0%
where the time goes in v18:
time: 132 us; the launch traced here: 131 us
  starting transfers between devices  58.5 us (44%)
  waiting for transfers between devices  29.1 us (22%)
  other arithmetic  19.2 us (15%)
  local copies, waits for them, and re-layouts  16.1 us (12%)
  matrix products  5.54 us (4%)
  between operations  2.27 us (2%)
    ppermute x8, starting transfers between devices, alt_extend(): below.insert(0, lax.ppermute(values[low:], 'alt', up))  26.9 us
    ppermute x8, starting transfers between devices, alt_extend(): above.append(lax.ppermute(values[:high], 'alt', down))  25.4 us
    ppermute x8, waiting for transfers between devices, alt_extend(): below.insert(0, lax.ppermute(values[low:], 'alt', up))  18.2 us
    unnamed x138, local copies, waits for them, and re-layouts  7.99 us
    ppermute x8, waiting for transfers between devices, alt_extend(): above.append(lax.ppermute(values[:high], 'alt', down))  7.53 us
    all_to_all x1, starting transfers between devices, spread_gather(): every = lax.all_to_all(copies, 'alt', 0, 0)  5.22 us
    add x3, other arithmetic, sweep(): centre + OMEGA * (trim(target, target_halo, halo - 1) - applied) / diagonal  2.88 us
    dot_general x8, matrix products, coarsen(): summed = jnp.matmul(summed, pairing(length), precision=HIGH)  2.81 us
  transfers between devices with their start and end apart: 19, of which 10 were waited for; matrix products, arithmetic and copies ran while one was open for 12% of the time, Pallas kernels for 0%

profile of v18, /device:TPU:8, one launch (start us, length us, event | category | flops | bytes accessed | tf_op | source)
XLA Modules:
  0.0 130.8 jit_solution(4886110387399141907)
XLA Ops:
  0.6 1.3 pad_maximum_fusion.1
  2.3 1.0 collective-permute-start.1
  3.6 0.6 compare_and_fusion
  4.2 0.5 fusion.308
  4.7 0.6 iota_shift-right-logical_fusion.3
  5.3 0.6 iota_shift-right-logical_fusion.1
  5.8 0.5 compare_and_fusion.2
  6.4 0.5 compare_and_fusion.3
  6.9 0.6 iota_shift-right-logical_fusion
  7.5 0.8 collective-permute-done
  9.8 0.6 pad_maximum_fusion
  10.6 0.9 slice_bitcast_fusion
  11.5 3.4 %collective-permute-start.2 = (f32[1,2,64,320]{3,2,1,0:T(8,128)S(1)}, f32[1,2,64,320]{3,2,1,0:T(8,128)S(1)}, u32[]{:S(2)}, u32[]{:S(2)}) collective-permute-start(f32[1,2,64,320]{3,2,1,0:T(8,128)S(1)} %get-tuple-element.32), channel_id=1, source_target_pairs={{0,4},{4,8},{8,12},{12,16},{16,20},{20,24},{24,28},{1,5},{5,9},{9,... | collective-permute-start | bytes 491528 | tf_op jit(solution)/shard_map/ppermute | solution.py:54
  15.0 3.3 %collective-permute-start.3 = (f32[1,2,64,320]{3,2,1,0:T(8,128)S(1)}, f32[1,2,64,320]{3,2,1,0:T(8,128)S(1)}, u32[]{:S(2)}, u32[]{:S(2)}) collective-permute-start(f32[1,2,64,320]{3,2,1,0:T(8,128)S(1)} %get-tuple-element.33), channel_id=1, source_target_pairs={{4,0},{8,4},{12,8},{16,12},{20,16},{24,20},{28,24},{5,1},{9,5},{13... | collective-permute-start | bytes 491528 | tf_op jit(solution)/shard_map/ppermute | solution.py:55
  18.5 0.4 copy-done.51
  19.0 0.4 fusion.324
  19.4 0.4 fusion.320
  20.9 0.5 fusion.322
  22.2 3.0 %collective-permute-done.3 = f32[1,2,64,320]{3,2,1,0:T(8,128)S(1)} collective-permute-done((f32[1,2,64,320]{3,2,1,0:T(8,128)S(1)}, f32[1,2,64,320]{3,2,1,0:T(8,128)S(1)}, u32[]{:S(2)}, u32[]{:S(2)}) %collective-permute-start.3) | collective-permute-done | bytes 163872 | tf_op jit(solution)/shard_map/ppermute | solution.py:55
  25.6 0.7 copy-done.1
  27.0 2.5 %collective-permute-start.6 = (f32[1,64,320]{2,1,0:T(8,128)S(1)}, f32[1,64,320]{2,1,0:T(8,128)S(1)}, u32[]{:S(2)}, u32[]{:S(2)}) collective-permute-start(f32[1,64,320]{2,1,0:T(8,128)S(1)} %fusion.209), channel_id=1, source_target_pairs={{0,4},{4,8},{8,12},{12,16},{16,20},{20,24},{24,28},{1,5},{5,9},{9,... | collective-permute-start | bytes 245768 | tf_op jit(solution)/shard_map/ppermute | solution.py:54
  30.2 4.2 %collective-permute-start.4 = (f32[1,64,320]{2,1,0:T(8,128)S(1)}, f32[1,64,320]{2,1,0:T(8,128)S(1)}, u32[]{:S(2)}, u32[]{:S(2)}) collective-permute-start(f32[1,64,320]{2,1,0:T(8,128)S(1)} %fusion.187), channel_id=1, source_target_pairs={{4,0},{8,4},{12,8},{16,12},{20,16},{24,20},{28,24},{5,1},{9,5},{13... | collective-permute-start | bytes 245768 | tf_op jit(solution)/shard_map/ppermute | solution.py:55
  34.5 2.7 %collective-permute-done.4 = f32[1,64,320]{2,1,0:T(8,128)S(1)} collective-permute-done((f32[1,64,320]{2,1,0:T(8,128)S(1)}, f32[1,64,320]{2,1,0:T(8,128)S(1)}, u32[]{:S(2)}, u32[]{:S(2)}) %collective-permute-start.4) | collective-permute-done | bytes 81952 | tf_op jit(solution)/shard_map/ppermute | solution.py:55
  37.4 4.7 %collective-permute-start.5 = (f32[1,64,320]{2,1,0:T(8,128)S(1)}, f32[1,64,320]{2,1,0:T(8,128)S(1)}, u32[]{:S(2)}, u32[]{:S(2)}) collective-permute-start(f32[1,64,320]{2,1,0:T(8,128)S(1)} %fusion.198), channel_id=1, source_target_pairs={{0,4},{4,8},{8,12},{12,16},{16,20},{20,24},{24,28},{1,5},{5,9},{9,... | collective-permute-start | bytes 245768 | tf_op jit(solution)/shard_map/ppermute | solution.py:54
  42.1 2.7 %collective-permute-done.5 = f32[1,64,320]{2,1,0:T(8,128)S(1)} collective-permute-done((f32[1,64,320]{2,1,0:T(8,128)S(1)}, f32[1,64,320]{2,1,0:T(8,128)S(1)}, u32[]{:S(2)}, u32[]{:S(2)}) %collective-permute-start.5) | collective-permute-done | bytes 81952 | tf_op jit(solution)/shard_map/ppermute | solution.py:54
  44.8 0.7 constant_dynamic-update-slice_fusion.4
  45.5 0.8 constant_dynamic-update-slice_fusion.3
  46.2 3.7 %collective-permute-start.7 = (f32[1,64,320]{2,1,0:T(8,128)S(1)}, f32[1,64,320]{2,1,0:T(8,128)S(1)}, u32[]{:S(2)}, u32[]{:S(2)}) collective-permute-start(f32[1,64,320]{2,1,0:T(8,128)S(1)} %get-tuple-element.18), channel_id=1, source_target_pairs={{4,0},{8,4},{12,8},{16,12},{20,16},{24,20},{28,24},{5,1},{9,5},{13... | collective-permute-start | bytes 245768 | tf_op jit(solution)/shard_map/ppermute | solution.py:55
  49.9 0.9 constant_dynamic-update-slice_fusion.2
  51.1 1.6 %collective-permute-done.7 = f32[1,64,320]{2,1,0:T(8,128)S(1)} collective-permute-done((f32[1,64,320]{2,1,0:T(8,128)S(1)}, f32[1,64,320]{2,1,0:T(8,128)S(1)}, u32[]{:S(2)}, u32[]{:S(2)}) %collective-permute-start.7) | collective-permute-done | bytes 81952 | tf_op jit(solution)/shard_map/ppermute | solution.py:55
  52.7 0.5 bitcast_reduce_fusion.3
  53.2 0.4 fusion.326
  53.9 3.5 %collective-permute-start.8 = (f32[2,4,32,160]{3,2,0,1:T(8,128)S(1)}, f32[2,4,32,160]{3,2,0,1:T(8,128)S(1)}, u32[]{:S(2)}, u32[]{:S(2)}) collective-permute-start(f32[2,4,32,160]{3,2,0,1:T(8,128)S(1)} %pad_maximum_fusion.6), channel_id=1, source_target_pairs={{0,8},{4,12},{8,16},{12,20},{16,24},{20,28},{1,9},{5,13},{9,17},{1... | collective-permute-start | bytes 491528 | tf_op jit(solution)/shard_map/ppermute | solution.py:54
  57.4 4.2 %collective-permute-start.12 = (f32[1,4,32,160]{3,2,0,1:T(8,128)S(1)}, f32[1,4,32,160]{3,2,0,1:T(8,128)S(1)}, u32[]{:S(2)}, u32[]{:S(2)}) collective-permute-start(f32[1,4,32,160]{3,2,0,1:T(8,128)S(1)} %get-tuple-element.92), channel_id=1, source_target_pairs={{0,12},{4,16},{8,20},{12,24},{16,28},{1,13},{5,17},{9,21},{13,25},... | collective-permute-start | bytes 245768 | tf_op jit(solution)/shard_map/ppermute | solution.py:54
  61.7 3.9 %collective-permute-start.11 = (f32[2,4,32,160]{3,2,0,1:T(8,128)S(1)}, f32[2,4,32,160]{3,2,0,1:T(8,128)S(1)}, u32[]{:S(2)}, u32[]{:S(2)}) collective-permute-start(f32[2,4,32,160]{3,2,0,1:T(8,128)S(1)} %pad_maximum_fusion.6), channel_id=1, source_target_pairs={{8,0},{12,4},{16,8},{20,12},{24,16},{28,20},{9,1},{13,5},{17,9},{2... | collective-permute-start | bytes 491528 | tf_op jit(solution)/shard_map/ppermute | solution.py:55
  65.7 1.9 %collective-permute-start.10 = (f32[2,4,32,160]{3,2,0,1:T(8,128)S(1)}, f32[2,4,32,160]{3,2,0,1:T(8,128)S(1)}, u32[]{:S(2)}, u32[]{:S(2)}) collective-permute-start(f32[2,4,32,160]{3,2,0,1:T(8,128)S(1)} %pad_maximum_fusion.6), channel_id=1, source_target_pairs={{4,0},{8,4},{12,8},{16,12},{20,16},{24,20},{28,24},{5,1},{9,5},{13... | collective-permute-start | bytes 491528 | tf_op jit(solution)/shard_map/ppermute | solution.py:55
  67.6 3.9 %collective-permute-start.9 = (f32[2,4,32,160]{3,2,0,1:T(8,128)S(1)}, f32[2,4,32,160]{3,2,0,1:T(8,128)S(1)}, u32[]{:S(2)}, u32[]{:S(2)}) collective-permute-start(f32[2,4,32,160]{3,2,0,1:T(8,128)S(1)} %pad_maximum_fusion.6), channel_id=1, source_target_pairs={{0,4},{4,8},{8,12},{12,16},{16,20},{20,24},{24,28},{1,5},{5,9},{9,... | collective-permute-start | bytes 491528 | tf_op jit(solution)/shard_map/ppermute | solution.py:54
  71.5 1.3 collective-permute-start.13
  72.9 6.8 %collective-permute-done.9 = f32[2,4,32,160]{3,2,0,1:T(8,128)S(1)} collective-permute-done((f32[2,4,32,160]{3,2,0,1:T(8,128)S(1)}, f32[2,4,32,160]{3,2,0,1:T(8,128)S(1)}, u32[]{:S(2)}, u32[]{:S(2)}) %collective-permute-start.9) | collective-permute-done | bytes 163872 | tf_op jit(solution)/shard_map/ppermute | solution.py:54
  80.0 0.4 copy-done.36
  80.9 0.4 fusion.28
  81.6 0.5 copy-done.61
  82.7 0.4 copy-done.20
  83.6 0.7 broadcast_in_dim.20
  84.3 5.2 %all-to-all-start = ((f32[8,1,4,16,80]{4,3,2,1,0:T(8,128)}), f32[8,1,4,16,80]{4,3,2,1,0:T(8,128)}, u32[]{:S(2)}, u32[]{:S(2)}) async-start(f32[8,1,4,16,80]{4,3,2,1,0:T(8,128)} %broadcast_in_dim.20), calls=%async_computation | async-start | bytes 524288 | tf_op jit(solution)/shard_map/all_to_all | solution.py:62
  89.5 0.6 compare_and_fusion.4
  90.1 1.5 %constant_dynamic-update-slice_fusion.1 = f32[6,64,320]{2,1,0:T(8,128)} fusion(f32[6,64,320]{2,1,0:T(8,128)} %get-tuple-element.15, f32[1,64,320]{2,1,0:T(8,128)} %copy-done.44), kind=kLoop, calls=%fused_computation.412 | loop fusion | bytes 196608
  91.7 1.5 %constant_dynamic-update-slice_fusion = f32[6,64,320]{2,1,0:T(8,128)} fusion(f32[6,64,320]{2,1,0:T(8,128)} %constant_dynamic-update-slice_fusion.1, f32[1,64,320]{2,1,0:T(8,128)} %copy-done.46), kind=kLoop, calls=%fused_computation.411 | loop fusion | bytes 196608 | tf_op jit(solution)/shard_map/concatenate | solution.py:56
  93.2 2.6 %all-to-all-done = f32[8,1,4,16,80]{4,3,2,1,0:T(8,128)} async-done(((f32[8,1,4,16,80]{4,3,2,1,0:T(8,128)}), f32[8,1,4,16,80]{4,3,2,1,0:T(8,128)}, u32[]{:S(2)}, u32[]{:S(2)}) %all-to-all-start) | async-done | bytes 163872 | tf_op jit(solution)/shard_map/all_to_all | solution.py:62
  95.9 0.9 slice_bitcast_fusion.21
  96.9 1.0 fusion.270
  98.0 0.9 fusion.232
  99.1 1.0 fusion.244
  100.1 0.9 fusion.256
  102.1 0.6 copy-done.7
  104.1 0.5 fusion.124
  105.1 1.2 slice_add_fusion
  106.6 3.4 %collective-permute-start.15 = (f32[1,64,320]{2,1,0:T(8,128)S(1)}, f32[1,64,320]{2,1,0:T(8,128)S(1)}, u32[]{:S(2)}, u32[]{:S(2)}) collective-permute-start(f32[1,64,320]{2,1,0:T(8,128)S(1)} %fusion.166), channel_id=1, source_target_pairs={{4,0},{8,4},{12,8},{16,12},{20,16},{24,20},{28,24},{5,1},{9,5},{13... | collective-permute-start | bytes 245768 | tf_op jit(solution)/shard_map/ppermute | solution.py:55
  110.3 2.5 %collective-permute-start.14 = (f32[1,64,320]{2,1,0:T(8,128)S(1)}, f32[1,64,320]{2,1,0:T(8,128)S(1)}, u32[]{:S(2)}, u32[]{:S(2)}) collective-permute-start(f32[1,64,320]{2,1,0:T(8,128)S(1)} %fusion.156), channel_id=1, source_target_pairs={{0,4},{4,8},{8,12},{12,16},{16,20},{20,24},{24,28},{1,5},{5,9},{9,... | collective-permute-start | bytes 245768 | tf_op jit(solution)/shard_map/ppermute | solution.py:54
  113.7 4.0 %collective-permute-done.14 = f32[1,64,320]{2,1,0:T(8,128)S(1)} collective-permute-done((f32[1,64,320]{2,1,0:T(8,128)S(1)}, f32[1,64,320]{2,1,0:T(8,128)S(1)}, u32[]{:S(2)}, u32[]{:S(2)}) %collective-permute-start.14) | collective-permute-done | bytes 81952 | tf_op jit(solution)/shard_map/ppermute | solution.py:54
  117.8 3.7 %collective-permute-start.17 = (f32[1,64,320]{2,1,0:T(8,128)S(1)}, f32[1,64,320]{2,1,0:T(8,128)S(1)}, u32[]{:S(2)}, u32[]{:S(2)}) collective-permute-start(f32[1,64,320]{2,1,0:T(8,128)S(1)} %fusion.146), channel_id=1, source_target_pairs={{4,0},{8,4},{12,8},{16,12},{20,16},{24,20},{28,24},{5,1},{9,5},{13... | collective-permute-start | bytes 245768 | tf_op jit(solution)/shard_map/ppermute | solution.py:55
  121.6 2.2 %collective-permute-start.16 = (f32[1,64,320]{2,1,0:T(8,128)S(1)}, f32[1,64,320]{2,1,0:T(8,128)S(1)}, u32[]{:S(2)}, u32[]{:S(2)}) collective-permute-start(f32[1,64,320]{2,1,0:T(8,128)S(1)} %fusion.136), channel_id=1, source_target_pairs={{0,4},{4,8},{8,12},{12,16},{16,20},{20,24},{24,28},{1,5},{5,9},{9,... | collective-permute-start | bytes 245768 | tf_op jit(solution)/shard_map/ppermute | solution.py:54
  124.3 4.7 %collective-permute-done.16 = f32[1,64,320]{2,1,0:T(8,128)S(1)} collective-permute-done((f32[1,64,320]{2,1,0:T(8,128)S(1)}, f32[1,64,320]{2,1,0:T(8,128)S(1)}, u32[]{:S(2)}, u32[]{:S(2)}) %collective-permute-start.16) | collective-permute-done | bytes 81952 | tf_op jit(solution)/shard_map/ppermute | solution.py:54
  129.2 1.6 %fusion.40 = (f32[4,64,256]{2,1,0:T(8,128)}, f32[4,64,256]{2,1,0:T(8,128)}) fusion(f32[4,63,320]{2,1,0:T(8,128)S(1)} %fusion.4, f32[4,63,320]{2,1,0:T(8,128)S(1)} %get-tuple-element.51, f32[4,64,320]{2,1,0:T(8,128)S(1)} %copy-done.45, f32[4,64,319]{2,1,0:T(8,128)S(1)} %get-tuple-element.53, f32[4,64,320]{2,1,0:T(8,128)S(1)} %get-tuple-element.21, ...), kind=kLoop, calls=%fused_computation.88 | loop fusion | flops 655360 | bytes 3395584 | tf_op jit(solution)/shard_map/div | solution.py:221
  (242 shorter events, 13.9 us)
Async XLA Ops:
  2.1 6.5 %copy-start.12 = (f32[4,64,256]{2,1,0:T(8,128)S(1)}, f32[4,64,256]{2,1,0:T(8,128)}, u32[]{:S(2)}) copy-start(f32[4,64,256]{2,1,0:T(8,128)} %param.7) | copy-start | bytes 786436
  2.1 6.5 %copy-start.14 = (f32[4,64,256]{2,1,0:T(8,128)S(1)}, f32[4,64,256]{2,1,0:T(8,128)}, u32[]{:S(2)}) copy-start(f32[4,64,256]{2,1,0:T(8,128)} %param.6) | copy-start | bytes 786436
  2.2 6.5 %copy-start.16 = (f32[4,64,256]{2,1,0:T(8,128)S(1)}, f32[4,64,256]{2,1,0:T(8,128)}, u32[]{:S(2)}) copy-start(f32[4,64,256]{2,1,0:T(8,128)} %param.5) | copy-start | bytes 786436
  2.2 6.5 %copy-start.18 = (f32[4,64,256]{2,1,0:T(8,128)S(1)}, f32[4,64,256]{2,1,0:T(8,128)}, u32[]{:S(2)}) copy-start(f32[4,64,256]{2,1,0:T(8,128)} %param.4) | copy-start | bytes 786436
  2.3 6.1 %collective-permute-start.1 = (f32[4,4,16,128]{3,2,1,0:T(8,128)S(1)}, f32[4,4,16,128]{3,2,1,0:T(8,128)S(1)}, u32[]{:S(2)}, u32[]{:S(2)}) collective-permute-start(f32[4,4,16,128]{3,2,1,0:T(8,128)S(1)} %reshape.123), channel_id=1, source_target_pairs={{1,0},{2,1},{3,2},{0,3},{5,4},{6,5},{7,6},{4,7},{9,8},{10,9},{11,1... | collective-permute-start | bytes 393224 | tf_op jit(solution)/shard_map/ppermute | solution.py:42
  3.5 4.7 %collective-permute-start = (f32[4,4,16,128]{3,2,1,0:T(8,128)S(1)}, f32[4,4,16,128]{3,2,1,0:T(8,128)S(1)}, u32[]{:S(2)}, u32[]{:S(2)}) collective-permute-start(f32[4,4,16,128]{3,2,1,0:T(8,128)S(1)} %reshape.121), channel_id=1, source_target_pairs={{0,1},{1,2},{2,3},{3,0},{4,5},{5,6},{6,7},{7,4},{8,9},{9,10},{10,1... | collective-permute-start | bytes 393224 | tf_op jit(solution)/shard_map/ppermute | solution.py:41
  8.8 28.4 %copy-start.10 = (f32[1,64,320]{2,1,0:T(8,128)}, f32[1,64,320]{2,1,0:T(8,128)S(1)}, u32[]{:S(2)}) copy-start(f32[1,64,320]{2,1,0:T(8,128)S(1)} %get-tuple-element.25) | copy-start | bytes 245764
  8.8 36.6 %copy-start.8 = (f32[1,64,320]{2,1,0:T(8,128)}, f32[1,64,320]{2,1,0:T(8,128)S(1)}, u32[]{:S(2)}) copy-start(f32[1,64,320]{2,1,0:T(8,128)S(1)} %get-tuple-element.24) | copy-start | bytes 245764
  11.5 10.7 %collective-permute-start.2 = (f32[1,2,64,320]{3,2,1,0:T(8,128)S(1)}, f32[1,2,64,320]{3,2,1,0:T(8,128)S(1)}, u32[]{:S(2)}, u32[]{:S(2)}) collective-permute-start(f32[1,2,64,320]{3,2,1,0:T(8,128)S(1)} %get-tuple-element.32), channel_id=1, source_target_pairs={{0,4},{4,8},{8,12},{12,16},{16,20},{20,24},{24,28},{1,5},{5,9},{9,... | collective-permute-start | bytes 491528 | tf_op jit(solution)/shard_map/ppermute | solution.py:54
  15.0 10.3 %collective-permute-start.3 = (f32[1,2,64,320]{3,2,1,0:T(8,128)S(1)}, f32[1,2,64,320]{3,2,1,0:T(8,128)S(1)}, u32[]{:S(2)}, u32[]{:S(2)}) collective-permute-start(f32[1,2,64,320]{3,2,1,0:T(8,128)S(1)} %get-tuple-element.33), channel_id=1, source_target_pairs={{4,0},{8,4},{12,8},{16,12},{20,16},{24,20},{28,24},{5,1},{9,5},{13... | collective-permute-start | bytes 491528 | tf_op jit(solution)/shard_map/ppermute | solution.py:55
  18.3 1.5 %copy-start.47 = (s32[64]{0:T(128)S(1)}, s32[64]{0:T(128)}, u32[]{:S(2)}) copy-start(s32[64]{0:T(128)} %get-tuple-element.158) | copy-start | bytes 772
  18.4 1.5 %copy-start.49 = (s32[64]{0:T(128)S(1)}, s32[64]{0:T(128)}, u32[]{:S(2)}) copy-start(s32[64]{0:T(128)} %get-tuple-element.159) | copy-start | bytes 772
  18.4 1.8 %copy-start.55 = (s32[160]{0:T(256)S(1)}, s32[160]{0:T(256)}, u32[]{:S(2)}) copy-start(s32[160]{0:T(256)} %get-tuple-element.160) | copy-start | bytes 1924
  18.4 1.8 %copy-start.57 = (s32[160]{0:T(256)S(1)}, s32[160]{0:T(256)}, u32[]{:S(2)}) copy-start(s32[160]{0:T(256)} %get-tuple-element.161) | copy-start | bytes 1924
  18.4 1.8 %copy-start.64 = (pred[160]{0:T(512)(128)(4,1)S(1)}, pred[160]{0:T(512)(128)(4,1)}, u32[]{:S(2)}) copy-start(pred[160]{0:T(512)(128)(4,1)} %compare_and_fusion) | copy-start | bytes 484
  20.1 59.8 %copy-start.38 = (f32[32,2,160]{2,0,1:T(8,128)}, f32[32,2,160]{2,0,1:T(8,128)S(1)}, u32[]{:S(2)}) copy-start(f32[32,2,160]{2,0,1:T(8,128)S(1)} %get-tuple-element.153) | copy-start | bytes 122884
  20.3 59.6 %copy-start.40 = (f32[32,2,160]{2,0,1:T(8,128)}, f32[32,2,160]{2,0,1:T(8,128)S(1)}, u32[]{:S(2)}) copy-start(f32[32,2,160]{2,0,1:T(8,128)S(1)} %get-tuple-element.149) | copy-start | bytes 122884
  21.5 58.4 %copy-start.42 = (f32[32,2,160]{2,0,1:T(8,128)}, f32[32,2,160]{2,0,1:T(8,128)S(1)}, u32[]{:S(2)}) copy-start(f32[32,2,160]{2,0,1:T(8,128)S(1)} %get-tuple-element.151) | copy-start | bytes 122884
  25.2 1.4 %copy-start.13 = (f32[4,64,256]{2,1,0:T(8,128)S(1)}, f32[4,64,256]{2,1,0:T(8,128)}, u32[]{:S(2)}) copy-start(f32[4,64,256]{2,1,0:T(8,128)} %param.7) | copy-start | bytes 786436
  25.2 1.5 %copy-start.15 = (f32[4,64,256]{2,1,0:T(8,128)S(1)}, f32[4,64,256]{2,1,0:T(8,128)}, u32[]{:S(2)}) copy-start(f32[4,64,256]{2,1,0:T(8,128)} %param.6) | copy-start | bytes 786436
  25.2 1.6 %copy-start.17 = (f32[4,64,256]{2,1,0:T(8,128)S(1)}, f32[4,64,256]{2,1,0:T(8,128)}, u32[]{:S(2)}) copy-start(f32[4,64,256]{2,1,0:T(8,128)} %param.5) | copy-start | bytes 786436
  25.6 24.4 %copy-start.4 = (f32[4,64,320]{2,1,0:T(8,128)}, f32[4,64,320]{2,1,0:T(8,128)S(1)}, u32[]{:S(2)}) copy-start(f32[4,64,320]{2,1,0:T(8,128)S(1)} %get-tuple-element.19) | copy-start | bytes 983044
  27.0 18.5 %collective-permute-start.6 = (f32[1,64,320]{2,1,0:T(8,128)S(1)}, f32[1,64,320]{2,1,0:T(8,128)S(1)}, u32[]{:S(2)}, u32[]{:S(2)}) collective-permute-start(f32[1,64,320]{2,1,0:T(8,128)S(1)} %fusion.209), channel_id=1, source_target_pairs={{0,4},{4,8},{8,12},{12,16},{16,20},{20,24},{24,28},{1,5},{5,9},{9,... | collective-permute-start | bytes 245768 | tf_op jit(solution)/shard_map/ppermute | solution.py:54
  30.2 7.0 %collective-permute-start.4 = (f32[1,64,320]{2,1,0:T(8,128)S(1)}, f32[1,64,320]{2,1,0:T(8,128)S(1)}, u32[]{:S(2)}, u32[]{:S(2)}) collective-permute-start(f32[1,64,320]{2,1,0:T(8,128)S(1)} %fusion.187), channel_id=1, source_target_pairs={{4,0},{8,4},{12,8},{16,12},{20,16},{24,20},{28,24},{5,1},{9,5},{13... | collective-permute-start | bytes 245768 | tf_op jit(solution)/shard_map/ppermute | solution.py:55
  37.4 15.3 %copy-start.44 = (f32[1,64,320]{2,1,0:T(8,128)}, f32[1,64,320]{2,1,0:T(8,128)S(1)}, u32[]{:S(2)}) copy-start(f32[1,64,320]{2,1,0:T(8,128)S(1)} %fusion.198) | copy-start | bytes 245764
  37.4 7.4 %collective-permute-start.5 = (f32[1,64,320]{2,1,0:T(8,128)S(1)}, f32[1,64,320]{2,1,0:T(8,128)S(1)}, u32[]{:S(2)}, u32[]{:S(2)}) collective-permute-start(f32[1,64,320]{2,1,0:T(8,128)S(1)} %fusion.198), channel_id=1, source_target_pairs={{0,4},{4,8},{8,12},{12,16},{16,20},{20,24},{24,28},{1,5},{5,9},{9,... | collective-permute-start | bytes 245768 | tf_op jit(solution)/shard_map/ppermute | solution.py:54
  46.2 6.5 %collective-permute-start.7 = (f32[1,64,320]{2,1,0:T(8,128)S(1)}, f32[1,64,320]{2,1,0:T(8,128)S(1)}, u32[]{:S(2)}, u32[]{:S(2)}) collective-permute-start(f32[1,64,320]{2,1,0:T(8,128)S(1)} %get-tuple-element.18), channel_id=1, source_target_pairs={{4,0},{8,4},{12,8},{16,12},{20,16},{24,20},{28,24},{5,1},{9,5},{13... | collective-permute-start | bytes 245768 | tf_op jit(solution)/shard_map/ppermute | solution.py:55
  52.7 27.1 %copy-start.46 = (f32[1,64,320]{2,1,0:T(8,128)}, f32[1,64,320]{2,1,0:T(8,128)S(1)}, u32[]{:S(2)}) copy-start(f32[1,64,320]{2,1,0:T(8,128)S(1)} %collective-permute-done.7) | copy-start | bytes 245764
  53.9 28.7 %copy-start.32 = (f32[32,2,160]{2,0,1:T(8,128)}, f32[32,2,160]{2,0,1:T(8,128)S(1)}, u32[]{:S(2)}) copy-start(f32[32,2,160]{2,0,1:T(8,128)S(1)} %convolution_multiply_fusion.3) | copy-start | bytes 122884
  53.9 18.9 %collective-permute-start.8 = (f32[2,4,32,160]{3,2,0,1:T(8,128)S(1)}, f32[2,4,32,160]{3,2,0,1:T(8,128)S(1)}, u32[]{:S(2)}, u32[]{:S(2)}) collective-permute-start(f32[2,4,32,160]{3,2,0,1:T(8,128)S(1)} %pad_maximum_fusion.6), channel_id=1, source_target_pairs={{0,8},{4,12},{8,16},{12,20},{16,24},{20,28},{1,9},{5,13},{9,17},{1... | collective-permute-start | bytes 491528 | tf_op jit(solution)/shard_map/ppermute | solution.py:54
  57.4 14.1 %collective-permute-start.12 = (f32[1,4,32,160]{3,2,0,1:T(8,128)S(1)}, f32[1,4,32,160]{3,2,0,1:T(8,128)S(1)}, u32[]{:S(2)}, u32[]{:S(2)}) collective-permute-start(f32[1,4,32,160]{3,2,0,1:T(8,128)S(1)} %get-tuple-element.92), channel_id=1, source_target_pairs={{0,12},{4,16},{8,20},{12,24},{16,28},{1,13},{5,17},{9,21},{13,25},... | collective-permute-start | bytes 245768 | tf_op jit(solution)/shard_map/ppermute | solution.py:54
  61.7 18.7 %collective-permute-start.11 = (f32[2,4,32,160]{3,2,0,1:T(8,128)S(1)}, f32[2,4,32,160]{3,2,0,1:T(8,128)S(1)}, u32[]{:S(2)}, u32[]{:S(2)}) collective-permute-start(f32[2,4,32,160]{3,2,0,1:T(8,128)S(1)} %pad_maximum_fusion.6), channel_id=1, source_target_pairs={{8,0},{12,4},{16,8},{20,12},{24,16},{28,20},{9,1},{13,5},{17,9},{2... | collective-permute-start | bytes 491528 | tf_op jit(solution)/shard_map/ppermute | solution.py:55
  65.7 14.3 %collective-permute-start.10 = (f32[2,4,32,160]{3,2,0,1:T(8,128)S(1)}, f32[2,4,32,160]{3,2,0,1:T(8,128)S(1)}, u32[]{:S(2)}, u32[]{:S(2)}) collective-permute-start(f32[2,4,32,160]{3,2,0,1:T(8,128)S(1)} %pad_maximum_fusion.6), channel_id=1, source_target_pairs={{4,0},{8,4},{12,8},{16,12},{20,16},{24,20},{28,24},{5,1},{9,5},{13... | collective-permute-start | bytes 491528 | tf_op jit(solution)/shard_map/ppermute | solution.py:55
  67.6 12.2 %collective-permute-start.9 = (f32[2,4,32,160]{3,2,0,1:T(8,128)S(1)}, f32[2,4,32,160]{3,2,0,1:T(8,128)S(1)}, u32[]{:S(2)}, u32[]{:S(2)}) collective-permute-start(f32[2,4,32,160]{3,2,0,1:T(8,128)S(1)} %pad_maximum_fusion.6), channel_id=1, source_target_pairs={{0,4},{4,8},{8,12},{12,16},{16,20},{20,24},{24,28},{1,5},{5,9},{9,... | collective-permute-start | bytes 491528 | tf_op jit(solution)/shard_map/ppermute | solution.py:54
  71.5 9.3 %collective-permute-start.13 = (f32[1,4,32,160]{3,2,0,1:T(8,128)S(1)}, f32[1,4,32,160]{3,2,0,1:T(8,128)S(1)}, u32[]{:S(2)}, u32[]{:S(2)}) collective-permute-start(f32[1,4,32,160]{3,2,0,1:T(8,128)S(1)} %get-tuple-element.93), channel_id=1, source_target_pairs={{12,0},{16,4},{20,8},{24,12},{28,16},{13,1},{17,5},{21,9},{25,13},... | collective-permute-start | bytes 245768 | tf_op jit(solution)/shard_map/ppermute | solution.py:55
  80.9 1.7 %copy-start.6 = (f32[10,31,160]{2,1,0:T(8,128)}, f32[10,31,160]{2,1,0:T(8,128)S(1)}, u32[]{:S(2)}) copy-start(f32[10,31,160]{2,1,0:T(8,128)S(1)} %fusion.24) | copy-start | bytes 595204
  81.3 1.3 copy-start.22
  81.3 1.3 copy-start.24
  81.3 1.3 copy-start.26
  81.3 1.3 copy-start.28
  81.4 1.3 copy-start.30
  84.3 11.5 %all-to-all-start = ((f32[8,1,4,16,80]{4,3,2,1,0:T(8,128)}), f32[8,1,4,16,80]{4,3,2,1,0:T(8,128)}, u32[]{:S(2)}, u32[]{:S(2)}) async-start(f32[8,1,4,16,80]{4,3,2,1,0:T(8,128)} %broadcast_in_dim.20), calls=%async_computation | async-start | bytes 524288 | tf_op jit(solution)/shard_map/all_to_all | solution.py:62
  98.9 2.2 %copy-start.56 = (s32[160]{0:T(256)S(1)}, s32[160]{0:T(256)}, u32[]{:S(2)}) copy-start(s32[160]{0:T(256)} %get-tuple-element.160) | copy-start | bytes 1924
  98.9 2.2 %copy-start.58 = (s32[160]{0:T(256)S(1)}, s32[160]{0:T(256)}, u32[]{:S(2)}) copy-start(s32[160]{0:T(256)} %get-tuple-element.161) | copy-start | bytes 1924
  98.9 2.2 %copy-start.65 = (pred[160]{0:T(512)(128)(4,1)S(1)}, pred[160]{0:T(512)(128)(4,1)}, u32[]{:S(2)}) copy-start(pred[160]{0:T(512)(128)(4,1)} %compare_and_fusion) | copy-start | bytes 484
  99.0 2.8 %copy-start.21 = (f32[8,32,160]{2,1,0:T(8,128)S(1)}, f32[8,32,160]{2,1,0:T(8,128)}, u32[]{:S(2)}) copy-start(f32[8,32,160]{2,1,0:T(8,128)} %copy-done.20) | copy-start | bytes 491524
  101.8 1.2 copy-start.27
  101.8 1.3 %copy-start.29 = (f32[10,32,160]{2,1,0:T(8,128)S(1)}, f32[10,32,160]{2,1,0:T(8,128)}, u32[]{:S(2)}) copy-start(f32[10,32,160]{2,1,0:T(8,128)} %copy-done.28) | copy-start | bytes 614404
  101.8 1.4 %copy-start.31 = (f32[10,32,160]{2,1,0:T(8,128)S(1)}, f32[10,32,160]{2,1,0:T(8,128)}, u32[]{:S(2)}) copy-start(f32[10,32,160]{2,1,0:T(8,128)} %copy-done.30) | copy-start | bytes 614404
  101.8 1.4 %copy-start.33 = (f32[32,2,160]{2,0,1:T(8,128)S(1)}, f32[32,2,160]{2,0,1:T(8,128)}, u32[]{:S(2)}) copy-start(f32[32,2,160]{2,0,1:T(8,128)} %copy-done.32) | copy-start | bytes 122884
  101.8 1.5 %copy-start.35 = (f32[2,4,32,160]{3,2,0,1:T(8,128)S(1)}, f32[2,4,32,160]{3,2,0,1:T(8,128)}, u32[]{:S(2)}) copy-start(f32[2,4,32,160]{3,2,0,1:T(8,128)} %copy-done.34) | copy-start | bytes 491524
  101.8 1.6 %copy-start.37 = (f32[2,4,32,160]{3,2,0,1:T(8,128)S(1)}, f32[2,4,32,160]{3,2,0,1:T(8,128)}, u32[]{:S(2)}) copy-start(f32[2,4,32,160]{3,2,0,1:T(8,128)} %copy-done.36) | copy-start | bytes 491524
  101.8 1.6 %copy-start.39 = (f32[32,2,160]{2,0,1:T(8,128)S(1)}, f32[32,2,160]{2,0,1:T(8,128)}, u32[]{:S(2)}) copy-start(f32[32,2,160]{2,0,1:T(8,128)} %copy-done.38) | copy-start | bytes 122884
  101.8 1.6 %copy-start.41 = (f32[32,2,160]{2,0,1:T(8,128)S(1)}, f32[32,2,160]{2,0,1:T(8,128)}, u32[]{:S(2)}) copy-start(f32[32,2,160]{2,0,1:T(8,128)} %copy-done.40) | copy-start | bytes 122884
  101.8 1.6 %copy-start.43 = (f32[32,2,160]{2,0,1:T(8,128)S(1)}, f32[32,2,160]{2,0,1:T(8,128)}, u32[]{:S(2)}) copy-start(f32[32,2,160]{2,0,1:T(8,128)} %copy-done.42) | copy-start | bytes 122884
  101.9 1.6 %copy-start.63 = (pred[6]{0:T(512)(128)(4,1)S(1)}, pred[6]{0:T(512)(128)(4,1)}, u32[]{:S(2)}) copy-start(pred[6]{0:T(512)(128)(4,1)} %compare_and_fusion.3) | copy-start | bytes 22
  105.1 1.4 %copy-start.5 = (f32[4,64,320]{2,1,0:T(8,128)S(1)}, f32[4,64,320]{2,1,0:T(8,128)}, u32[]{:S(2)}) copy-start(f32[4,64,320]{2,1,0:T(8,128)} %copy-done.4) | copy-start | bytes 983044
  105.1 1.4 %copy-start.9 = (f32[1,64,320]{2,1,0:T(8,128)S(1)}, f32[1,64,320]{2,1,0:T(8,128)}, u32[]{:S(2)}) copy-start(f32[1,64,320]{2,1,0:T(8,128)} %copy-done.8) | copy-start | bytes 245764
  106.5 3.7 %copy-start.11 = (f32[1,64,320]{2,1,0:T(8,128)S(1)}, f32[1,64,320]{2,1,0:T(8,128)}, u32[]{:S(2)}) copy-start(f32[1,64,320]{2,1,0:T(8,128)} %copy-done.10) | copy-start | bytes 245764
  106.6 14.9 %collective-permute-start.15 = (f32[1,64,320]{2,1,0:T(8,128)S(1)}, f32[1,64,320]{2,1,0:T(8,128)S(1)}, u32[]{:S(2)}, u32[]{:S(2)}) collective-permute-start(f32[1,64,320]{2,1,0:T(8,128)S(1)} %fusion.166), channel_id=1, source_target_pairs={{4,0},{8,4},{12,8},{16,12},{20,16},{24,20},{28,24},{5,1},{9,5},{13... | collective-permute-start | bytes 245768 | tf_op jit(solution)/shard_map/ppermute | solution.py:55
  110.3 7.4 %collective-permute-start.14 = (f32[1,64,320]{2,1,0:T(8,128)S(1)}, f32[1,64,320]{2,1,0:T(8,128)S(1)}, u32[]{:S(2)}, u32[]{:S(2)}) collective-permute-start(f32[1,64,320]{2,1,0:T(8,128)S(1)} %fusion.156), channel_id=1, source_target_pairs={{0,4},{4,8},{8,12},{12,16},{16,20},{20,24},{24,28},{1,5},{5,9},{9,... | collective-permute-start | bytes 245768 | tf_op jit(solution)/shard_map/ppermute | solution.py:54
  117.8 6.5 %collective-permute-start.17 = (f32[1,64,320]{2,1,0:T(8,128)S(1)}, f32[1,64,320]{2,1,0:T(8,128)S(1)}, u32[]{:S(2)}, u32[]{:S(2)}) collective-permute-start(f32[1,64,320]{2,1,0:T(8,128)S(1)} %fusion.146), channel_id=1, source_target_pairs={{4,0},{8,4},{12,8},{16,12},{20,16},{24,20},{28,24},{5,1},{9,5},{13... | collective-permute-start | bytes 245768 | tf_op jit(solution)/shard_map/ppermute | solution.py:55
  121.6 7.4 %collective-permute-start.16 = (f32[1,64,320]{2,1,0:T(8,128)S(1)}, f32[1,64,320]{2,1,0:T(8,128)S(1)}, u32[]{:S(2)}, u32[]{:S(2)}) collective-permute-start(f32[1,64,320]{2,1,0:T(8,128)S(1)} %fusion.136), channel_id=1, source_target_pairs={{0,4},{4,8},{8,12},{12,16},{16,20},{20,24},{24,28},{1,5},{5,9},{9,... | collective-permute-start | bytes 245768 | tf_op jit(solution)/shard_map/ppermute | solution.py:54
  124.1 5.1 %copy-start.45 = (f32[4,64,320]{2,1,0:T(8,128)S(1)}, f32[4,64,320]{2,1,0:T(8,128)}, u32[]{:S(2)}) copy-start(f32[4,64,320]{2,1,0:T(8,128)} %get-tuple-element.26) | copy-start | bytes 983044
  (21 other events, 17.2 us)

commit v19 on v18

--- a/solution.py
+++ b/solution.py
@@ -54,6 +54,17 @@
         below.insert(0, lax.ppermute(values[low:], "alt", up))
         above.append(lax.ppermute(values[:high], "alt", down))
     return jnp.concatenate(below + [values] + above, axis=0)
+
+
+def alt_row(values, offset):
+    count, depth = lax.axis_size("alt"), values.shape[0]
+    distance = -(-offset // depth)
+    up = [(i, i + distance) for i in range(count) if i + distance < count]
+    down = [(i, i - distance) for i in range(count) if i - distance >= 0]
+    index = distance * depth - offset
+    below = lax.ppermute(values[index:index + 1], "alt", up)
+    above = lax.ppermute(values[depth - 1 - index:depth - index], "alt", down)
+    return below, above
 
 
 def spread_gather(values):
@@ -185,15 +196,16 @@
     rhs_two = coarsen(wide_source - applied)
 
     wide_two = SWEEPS + 3
-    level_two = alt_extend(jnp.stack([rhs_two] + coef_two, 1), wide_two)
+    level_two = alt_extend(jnp.stack([rhs_two] + coef_two, 1), wide_two - 1)
+    far_below, far_above = alt_row(coef_two[0], wide_two)
     weights_two = make_weights(
-        level_two[:, 1],
-        trim(level_two[:, 2], wide_two, wide_two - 1),
-        trim(level_two[:, 3], wide_two, wide_two - 1),
+        jnp.concatenate([far_below, level_two[:, 1], far_above], axis=0),
+        level_two[:, 2],
+        level_two[:, 3],
         0.25,
         wide_two - 1,
     )
-    rhs_two_x = trim(level_two[:, 0], wide_two, wide_two - 1)
+    rhs_two_x = level_two[:, 0]
     correction = first_sweep(weights_two, rhs_two_x, wide_two - 1)
     correction = sweep(weights_two, correction, wide_two - 1, rhs_two_x, wide_two - 1)
     applied, _ = apply_op(weights_two, trim(correction, wide_two - 2, 1), 1)

time: 132 us -> 129 us (0.977)
  starting transfers between devices: 58.5 us -> 55.8 us
    ppermute x8 -> x7, starting transfers between devices: 25.4 us -> 19.1 us  [alt_extend(): above.append(lax.ppermute(values[:high], 'alt', down))]
    ppermute x8 -> x7, waiting for transfers between devices: 7.53 us -> 12.8 us  [alt_extend(): above.append(lax.ppermute(values[:high], 'alt', down))]
    ppermute x0 -> x2, starting transfers between devices: none -> 4.83 us  [the longest x1 3.54 us: alt_row(): below = lax.ppermute(values[index:index + 1], 'alt', up)]
    ppermute x8 -> x7, waiting for transfers between devices: 18.2 us -> 13.8 us  [alt_extend(): below.insert(0, lax.ppermute(values[low:], 'alt', up))]
    unnamed x138 -> x137, local copies, waits for them, and re-layouts: 7.99 us -> 6.94 us
    ppermute x8 -> x7, starting transfers between devices: 26.9 us -> 25.9 us  [alt_extend(): below.insert(0, lax.ppermute(values[low:], 'alt', up))]
  transfers between devices with their start and end apart: 19 -> 19, of which waited for: 10 -> 9; matrix products, arithmetic and copies ran while one was open for 12% -> 14% of each run, Pallas kernels for 0% -> 0%
where the time goes in v19:
time: 129 us; the launch traced here: 128 us
  starting transfers between devices  55.8 us (43%)
  waiting for transfers between devices  30.1 us (23%)
  other arithmetic  19 us (15%)
  local copies, waits for them, and re-layouts  15.1 us (12%)
  matrix products  5.54 us (4%)
  between operations  2.29 us (2%)
    ppermute x7, starting transfers between devices, alt_extend(): below.insert(0, lax.ppermute(values[low:], 'alt', up))  25.9 us
    ppermute x7, starting transfers between devices, alt_extend(): above.append(lax.ppermute(values[:high], 'alt', down))  19.1 us
    ppermute x7, waiting for transfers between devices, alt_extend(): below.insert(0, lax.ppermute(values[low:], 'alt', up))  13.8 us
    ppermute x7, waiting for transfers between devices, alt_extend(): above.append(lax.ppermute(values[:high], 'alt', down))  12.8 us
    unnamed x137, local copies, waits for them, and re-layouts  6.94 us
    all_to_all x1, starting transfers between devices, spread_gather(): every = lax.all_to_all(copies, 'alt', 0, 0)  4.85 us
    ppermute x1, starting transfers between devices, alt_row(): below = lax.ppermute(values[index:index + 1], 'alt', up)  3.54 us
    add x3, other arithmetic, sweep(): centre + OMEGA * (trim(target, target_halo, halo - 1) - applied) / diagonal  2.88 us
  transfers between devices with their start and end apart: 19, of which 9 were waited for; matrix products, arithmetic and copies ran while one was open for 14% of the time, Pallas kernels for 0%

profile of v19, /device:TPU:8, one launch (start us, length us, event | category | flops | bytes accessed | tf_op | source)
XLA Modules:
  0.0 127.8 jit_solution(583902495839636057)
XLA Ops:
  0.6 1.3 %pad_maximum_fusion.1 = f32[4,4,64,256]{3,2,1,0:T(8,128)S(1)} fusion(f32[4,1,64,256]{3,2,1,0:T(8,128)} %bitcast.399, f32[4,1,64,256]{3,2,1,0:T(8,128)} %bitcast.404, f32[4,1,64,256]{3,2,1,0:T(8,128)} %bitcast.409, f32[4,1,64,256]{3,2,1,0:T(8,128)} %bitcast.414), kind=kLoop, calls=%fused_computation.15 | loop fusion | flops 786432 | bytes 2097152 | tf_op jit(solution)/shard_map/stack | solution.py:183
  2.3 1.0 collective-permute-start.1
  3.6 0.5 compare_and_fusion
  4.1 0.5 fusion.306
  4.7 0.5 iota_shift-right-logical_fusion.3
  5.2 0.6 iota_shift-right-logical_fusion.1
  5.8 0.5 compare_and_fusion.2
  6.3 0.6 compare_and_fusion.3
  6.9 0.6 iota_shift-right-logical_fusion
  7.5 0.7 collective-permute-done
  9.4 0.4 copy-done.19
  9.8 0.6 pad_maximum_fusion
  10.7 0.9 slice_bitcast_fusion
  11.6 3.4 %collective-permute-start.2 = (f32[1,2,64,320]{3,2,1,0:T(8,128)S(1)}, f32[1,2,64,320]{3,2,1,0:T(8,128)S(1)}, u32[]{:S(2)}, u32[]{:S(2)}) collective-permute-start(f32[1,2,64,320]{3,2,1,0:T(8,128)S(1)} %get-tuple-element.32), channel_id=1, source_target_pairs={{0,4},{4,8},{8,12},{12,16},{16,20},{20,24},{24,28},{1,5},{5,9},{9,... | collective-permute-start | bytes 491528 | tf_op jit(solution)/shard_map/ppermute | solution.py:54
  15.0 3.3 %collective-permute-start.3 = (f32[1,2,64,320]{3,2,1,0:T(8,128)S(1)}, f32[1,2,64,320]{3,2,1,0:T(8,128)S(1)}, u32[]{:S(2)}, u32[]{:S(2)}) collective-permute-start(f32[1,2,64,320]{3,2,1,0:T(8,128)S(1)} %get-tuple-element.33), channel_id=1, source_target_pairs={{4,0},{8,4},{12,8},{16,12},{20,16},{24,20},{28,24},{5,1},{9,5},{13... | collective-permute-start | bytes 491528 | tf_op jit(solution)/shard_map/ppermute | solution.py:55
  18.4 0.4 fusion.322
  19.1 3.5 %collective-permute-start.12 = (f32[1,32,160]{2,1,0:T(8,128)S(1)}, f32[1,32,160]{2,1,0:T(8,128)S(1)}, u32[]{:S(2)}, u32[]{:S(2)}) collective-permute-start(f32[1,32,160]{2,1,0:T(8,128)S(1)} %get-tuple-element.132), channel_id=1, source_target_pairs={{0,12},{4,16},{8,20},{12,24},{16,28},{1,13},{5,17},{9,21},{13,25},... | collective-permute-start | bytes 61448 | tf_op jit(solution)/shard_map/ppermute | solution.py:65
  22.6 1.3 %collective-permute-start.13 = (f32[1,32,160]{2,1,0:T(8,128)S(1)}, f32[1,32,160]{2,1,0:T(8,128)S(1)}, u32[]{:S(2)}, u32[]{:S(2)}) collective-permute-start(f32[1,32,160]{2,1,0:T(8,128)S(1)} %get-tuple-element.133), channel_id=1, source_target_pairs={{12,0},{16,4},{20,8},{24,12},{28,16},{13,1},{17,5},{21,9},{25,13},... | collective-permute-start | bytes 61448 | tf_op jit(solution)/shard_map/ppermute | solution.py:66
  24.1 0.4 fusion.318
  25.3 0.4 fusion.320
  26.9 0.7 copy-done.1
  28.3 5.0 %collective-permute-start.6 = (f32[1,64,320]{2,1,0:T(8,128)S(1)}, f32[1,64,320]{2,1,0:T(8,128)S(1)}, u32[]{:S(2)}, u32[]{:S(2)}) collective-permute-start(f32[1,64,320]{2,1,0:T(8,128)S(1)} %fusion.207), channel_id=1, source_target_pairs={{0,4},{4,8},{8,12},{12,16},{16,20},{20,24},{24,28},{1,5},{5,9},{9,... | collective-permute-start | bytes 245768 | tf_op jit(solution)/shard_map/ppermute | solution.py:54
  34.0 1.9 %collective-permute-start.4 = (f32[1,64,320]{2,1,0:T(8,128)S(1)}, f32[1,64,320]{2,1,0:T(8,128)S(1)}, u32[]{:S(2)}, u32[]{:S(2)}) collective-permute-start(f32[1,64,320]{2,1,0:T(8,128)S(1)} %fusion.185), channel_id=1, source_target_pairs={{4,0},{8,4},{12,8},{16,12},{20,16},{24,20},{28,24},{5,1},{9,5},{13... | collective-permute-start | bytes 245768 | tf_op jit(solution)/shard_map/ppermute | solution.py:55
  36.0 5.3 %collective-permute-done.4 = f32[1,64,320]{2,1,0:T(8,128)S(1)} collective-permute-done((f32[1,64,320]{2,1,0:T(8,128)S(1)}, f32[1,64,320]{2,1,0:T(8,128)S(1)}, u32[]{:S(2)}, u32[]{:S(2)}) %collective-permute-start.4) | collective-permute-done | bytes 81952 | tf_op jit(solution)/shard_map/ppermute | solution.py:55
  41.4 4.8 %collective-permute-start.5 = (f32[1,64,320]{2,1,0:T(8,128)S(1)}, f32[1,64,320]{2,1,0:T(8,128)S(1)}, u32[]{:S(2)}, u32[]{:S(2)}) collective-permute-start(f32[1,64,320]{2,1,0:T(8,128)S(1)} %fusion.196), channel_id=1, source_target_pairs={{0,4},{4,8},{8,12},{12,16},{16,20},{20,24},{24,28},{1,5},{5,9},{9,... | collective-permute-start | bytes 245768 | tf_op jit(solution)/shard_map/ppermute | solution.py:54
  46.3 2.6 %collective-permute-done.5 = f32[1,64,320]{2,1,0:T(8,128)S(1)} collective-permute-done((f32[1,64,320]{2,1,0:T(8,128)S(1)}, f32[1,64,320]{2,1,0:T(8,128)S(1)}, u32[]{:S(2)}, u32[]{:S(2)}) %collective-permute-start.5) | collective-permute-done | bytes 81952 | tf_op jit(solution)/shard_map/ppermute | solution.py:54
  48.8 0.6 constant_dynamic-update-slice_fusion.4
  49.5 0.8 constant_dynamic-update-slice_fusion.3
  50.2 1.9 %collective-permute-start.7 = (f32[1,64,320]{2,1,0:T(8,128)S(1)}, f32[1,64,320]{2,1,0:T(8,128)S(1)}, u32[]{:S(2)}, u32[]{:S(2)}) collective-permute-start(f32[1,64,320]{2,1,0:T(8,128)S(1)} %get-tuple-element.18), channel_id=1, source_target_pairs={{4,0},{8,4},{12,8},{16,12},{20,16},{24,20},{28,24},{5,1},{9,5},{13... | collective-permute-start | bytes 245768 | tf_op jit(solution)/shard_map/ppermute | solution.py:55
  52.1 0.9 constant_dynamic-update-slice_fusion.2
  53.3 3.4 %collective-permute-done.7 = f32[1,64,320]{2,1,0:T(8,128)S(1)} collective-permute-done((f32[1,64,320]{2,1,0:T(8,128)S(1)}, f32[1,64,320]{2,1,0:T(8,128)S(1)}, u32[]{:S(2)}, u32[]{:S(2)}) %collective-permute-start.7) | collective-permute-done | bytes 81952 | tf_op jit(solution)/shard_map/ppermute | solution.py:55
  56.7 0.5 bitcast_reduce_fusion.3
  57.2 0.4 fusion.324
  57.9 3.5 %collective-permute-start.8 = (f32[2,4,32,160]{3,2,0,1:T(8,128)S(1)}, f32[2,4,32,160]{3,2,0,1:T(8,128)S(1)}, u32[]{:S(2)}, u32[]{:S(2)}) collective-permute-start(f32[2,4,32,160]{3,2,0,1:T(8,128)S(1)} %pad_maximum_fusion.8), channel_id=1, source_target_pairs={{0,8},{4,12},{8,16},{12,20},{16,24},{20,28},{1,9},{5,13},{9,17},{1... | collective-permute-start | bytes 491528 | tf_op jit(solution)/shard_map/ppermute | solution.py:54
  61.5 4.8 %collective-permute-start.9 = (f32[2,4,32,160]{3,2,0,1:T(8,128)S(1)}, f32[2,4,32,160]{3,2,0,1:T(8,128)S(1)}, u32[]{:S(2)}, u32[]{:S(2)}) collective-permute-start(f32[2,4,32,160]{3,2,0,1:T(8,128)S(1)} %pad_maximum_fusion.8), channel_id=1, source_target_pairs={{0,4},{4,8},{8,12},{12,16},{16,20},{20,24},{24,28},{1,5},{5,9},{9,... | collective-permute-start | bytes 491528 | tf_op jit(solution)/shard_map/ppermute | solution.py:54
  66.4 2.4 %collective-permute-start.11 = (f32[2,4,32,160]{3,2,0,1:T(8,128)S(1)}, f32[2,4,32,160]{3,2,0,1:T(8,128)S(1)}, u32[]{:S(2)}, u32[]{:S(2)}) collective-permute-start(f32[2,4,32,160]{3,2,0,1:T(8,128)S(1)} %pad_maximum_fusion.8), channel_id=1, source_target_pairs={{8,0},{12,4},{16,8},{20,12},{24,16},{28,20},{9,1},{13,5},{17,9},{2... | collective-permute-start | bytes 491528 | tf_op jit(solution)/shard_map/ppermute | solution.py:55
  68.8 1.9 %collective-permute-start.10 = (f32[2,4,32,160]{3,2,0,1:T(8,128)S(1)}, f32[2,4,32,160]{3,2,0,1:T(8,128)S(1)}, u32[]{:S(2)}, u32[]{:S(2)}) collective-permute-start(f32[2,4,32,160]{3,2,0,1:T(8,128)S(1)} %pad_maximum_fusion.8), channel_id=1, source_target_pairs={{4,0},{8,4},{12,8},{16,12},{20,16},{24,20},{28,24},{5,1},{9,5},{13... | collective-permute-start | bytes 491528 | tf_op jit(solution)/shard_map/ppermute | solution.py:55
  70.8 2.1 %collective-permute-done.9 = f32[2,4,32,160]{3,2,0,1:T(8,128)S(1)} collective-permute-done((f32[2,4,32,160]{3,2,0,1:T(8,128)S(1)}, f32[2,4,32,160]{3,2,0,1:T(8,128)S(1)}, u32[]{:S(2)}, u32[]{:S(2)}) %collective-permute-start.9) | collective-permute-done | bytes 163872 | tf_op jit(solution)/shard_map/ppermute | solution.py:54
  72.9 4.2 %collective-permute-done.10 = f32[2,4,32,160]{3,2,0,1:T(8,128)S(1)} collective-permute-done((f32[2,4,32,160]{3,2,0,1:T(8,128)S(1)}, f32[2,4,32,160]{3,2,0,1:T(8,128)S(1)}, u32[]{:S(2)}, u32[]{:S(2)}) %collective-permute-start.10) | collective-permute-done | bytes 163872 | tf_op jit(solution)/shard_map/ppermute | solution.py:55
  77.9 0.4 fusion.30
  78.6 0.5 copy-done.61
  79.1 0.4 fusion.49
  79.7 0.4 copy-done.20
  80.6 0.7 broadcast_in_dim.20
  81.3 4.8 %all-to-all-start = ((f32[8,1,4,16,80]{4,3,2,1,0:T(8,128)}), f32[8,1,4,16,80]{4,3,2,1,0:T(8,128)}, u32[]{:S(2)}, u32[]{:S(2)}) async-start(f32[8,1,4,16,80]{4,3,2,1,0:T(8,128)} %broadcast_in_dim.20), calls=%async_computation | async-start | bytes 524288 | tf_op jit(solution)/shard_map/all_to_all | solution.py:73
  86.2 0.5 compare_and_fusion.4
  86.7 1.5 %constant_dynamic-update-slice_fusion.1 = f32[6,64,320]{2,1,0:T(8,128)} fusion(f32[6,64,320]{2,1,0:T(8,128)} %get-tuple-element.15, f32[1,64,320]{2,1,0:T(8,128)} %copy-done.44), kind=kLoop, calls=%fused_computation.418 | loop fusion | bytes 196608
  88.2 1.5 %constant_dynamic-update-slice_fusion = f32[6,64,320]{2,1,0:T(8,128)} fusion(f32[6,64,320]{2,1,0:T(8,128)} %constant_dynamic-update-slice_fusion.1, f32[1,64,320]{2,1,0:T(8,128)} %copy-done.46), kind=kLoop, calls=%fused_computation.417 | loop fusion | bytes 196608 | tf_op jit(solution)/shard_map/concatenate | solution.py:56
  89.7 2.7 %all-to-all-done = f32[8,1,4,16,80]{4,3,2,1,0:T(8,128)} async-done(((f32[8,1,4,16,80]{4,3,2,1,0:T(8,128)}), f32[8,1,4,16,80]{4,3,2,1,0:T(8,128)}, u32[]{:S(2)}, u32[]{:S(2)}) %all-to-all-start) | async-done | bytes 163872 | tf_op jit(solution)/shard_map/all_to_all | solution.py:73
  92.5 0.9 slice_bitcast_fusion.16
  93.5 1.0 fusion.268
  94.6 0.9 fusion.230
  95.7 1.0 fusion.242
  96.8 0.9 fusion.254
  100.5 0.5 fusion.122
  101.0 0.4 convolution_bitcast_fusion
  101.5 1.2 slice_add_fusion
  103.0 3.4 %collective-permute-start.15 = (f32[1,64,320]{2,1,0:T(8,128)S(1)}, f32[1,64,320]{2,1,0:T(8,128)S(1)}, u32[]{:S(2)}, u32[]{:S(2)}) collective-permute-start(f32[1,64,320]{2,1,0:T(8,128)S(1)} %fusion.164), channel_id=1, source_target_pairs={{4,0},{8,4},{12,8},{16,12},{20,16},{24,20},{28,24},{5,1},{9,5},{13... | collective-permute-start | bytes 245768 | tf_op jit(solution)/shard_map/ppermute | solution.py:55
  106.6 2.5 %collective-permute-start.14 = (f32[1,64,320]{2,1,0:T(8,128)S(1)}, f32[1,64,320]{2,1,0:T(8,128)S(1)}, u32[]{:S(2)}, u32[]{:S(2)}) collective-permute-start(f32[1,64,320]{2,1,0:T(8,128)S(1)} %fusion.154), channel_id=1, source_target_pairs={{0,4},{4,8},{8,12},{12,16},{16,20},{20,24},{24,28},{1,5},{5,9},{9,... | collective-permute-start | bytes 245768 | tf_op jit(solution)/shard_map/ppermute | solution.py:54
  110.0 4.0 %collective-permute-done.14 = f32[1,64,320]{2,1,0:T(8,128)S(1)} collective-permute-done((f32[1,64,320]{2,1,0:T(8,128)S(1)}, f32[1,64,320]{2,1,0:T(8,128)S(1)}, u32[]{:S(2)}, u32[]{:S(2)}) %collective-permute-start.14) | collective-permute-done | bytes 81952 | tf_op jit(solution)/shard_map/ppermute | solution.py:54
  114.2 4.3 %collective-permute-start.17 = (f32[1,64,320]{2,1,0:T(8,128)S(1)}, f32[1,64,320]{2,1,0:T(8,128)S(1)}, u32[]{:S(2)}, u32[]{:S(2)}) collective-permute-start(f32[1,64,320]{2,1,0:T(8,128)S(1)} %fusion.144), channel_id=1, source_target_pairs={{4,0},{8,4},{12,8},{16,12},{20,16},{24,20},{28,24},{5,1},{9,5},{13... | collective-permute-start | bytes 245768 | tf_op jit(solution)/shard_map/ppermute | solution.py:55
  118.6 1.9 %collective-permute-start.16 = (f32[1,64,320]{2,1,0:T(8,128)S(1)}, f32[1,64,320]{2,1,0:T(8,128)S(1)}, u32[]{:S(2)}, u32[]{:S(2)}) collective-permute-start(f32[1,64,320]{2,1,0:T(8,128)S(1)} %fusion.134), channel_id=1, source_target_pairs={{0,4},{4,8},{8,12},{12,16},{16,20},{20,24},{24,28},{1,5},{5,9},{9,... | collective-permute-start | bytes 245768 | tf_op jit(solution)/shard_map/ppermute | solution.py:54
  120.9 5.2 %collective-permute-done.16 = f32[1,64,320]{2,1,0:T(8,128)S(1)} collective-permute-done((f32[1,64,320]{2,1,0:T(8,128)S(1)}, f32[1,64,320]{2,1,0:T(8,128)S(1)}, u32[]{:S(2)}, u32[]{:S(2)}) %collective-permute-start.16) | collective-permute-done | bytes 81952 | tf_op jit(solution)/shard_map/ppermute | solution.py:54
  126.2 1.6 %fusion.38 = (f32[4,64,256]{2,1,0:T(8,128)}, f32[4,64,256]{2,1,0:T(8,128)}) fusion(f32[4,63,320]{2,1,0:T(8,128)S(1)} %fusion.4, f32[4,63,320]{2,1,0:T(8,128)S(1)} %get-tuple-element.52, f32[4,64,320]{2,1,0:T(8,128)S(1)} %copy-done.45, f32[4,64,319]{2,1,0:T(8,128)S(1)} %get-tuple-element.54, f32[4,64,320]{2,1,0:T(8,128)S(1)} %get-tuple-element.21, ...), kind=kLoop, calls=%fused_computation.87 | loop fusion | flops 655360 | bytes 3395584 | tf_op jit(solution)/shard_map/div | solution.py:233
  (240 shorter events, 13.0 us)
Async XLA Ops:
  2.1 6.5 %copy-start.12 = (f32[4,64,256]{2,1,0:T(8,128)S(1)}, f32[4,64,256]{2,1,0:T(8,128)}, u32[]{:S(2)}) copy-start(f32[4,64,256]{2,1,0:T(8,128)} %param.7) | copy-start | bytes 786436
  2.1 6.5 %copy-start.14 = (f32[4,64,256]{2,1,0:T(8,128)S(1)}, f32[4,64,256]{2,1,0:T(8,128)}, u32[]{:S(2)}) copy-start(f32[4,64,256]{2,1,0:T(8,128)} %param.6) | copy-start | bytes 786436
  2.2 6.5 %copy-start.16 = (f32[4,64,256]{2,1,0:T(8,128)S(1)}, f32[4,64,256]{2,1,0:T(8,128)}, u32[]{:S(2)}) copy-start(f32[4,64,256]{2,1,0:T(8,128)} %param.5) | copy-start | bytes 786436
  2.2 6.5 %copy-start.18 = (f32[4,64,256]{2,1,0:T(8,128)S(1)}, f32[4,64,256]{2,1,0:T(8,128)}, u32[]{:S(2)}) copy-start(f32[4,64,256]{2,1,0:T(8,128)} %param.4) | copy-start | bytes 786436
  2.3 6.1 %collective-permute-start.1 = (f32[4,4,16,128]{3,2,1,0:T(8,128)S(1)}, f32[4,4,16,128]{3,2,1,0:T(8,128)S(1)}, u32[]{:S(2)}, u32[]{:S(2)}) collective-permute-start(f32[4,4,16,128]{3,2,1,0:T(8,128)S(1)} %reshape.102), channel_id=1, source_target_pairs={{1,0},{2,1},{3,2},{0,3},{5,4},{6,5},{7,6},{4,7},{9,8},{10,9},{11,1... | collective-permute-start | bytes 393224 | tf_op jit(solution)/shard_map/ppermute | solution.py:42
  3.5 4.7 %collective-permute-start = (f32[4,4,16,128]{3,2,1,0:T(8,128)S(1)}, f32[4,4,16,128]{3,2,1,0:T(8,128)S(1)}, u32[]{:S(2)}, u32[]{:S(2)}) collective-permute-start(f32[4,4,16,128]{3,2,1,0:T(8,128)S(1)} %reshape.100), channel_id=1, source_target_pairs={{0,1},{1,2},{2,3},{3,0},{4,5},{5,6},{6,7},{7,4},{8,9},{9,10},{10,1... | collective-permute-start | bytes 393224 | tf_op jit(solution)/shard_map/ppermute | solution.py:41
  8.8 32.4 %copy-start.10 = (f32[1,64,320]{2,1,0:T(8,128)}, f32[1,64,320]{2,1,0:T(8,128)S(1)}, u32[]{:S(2)}) copy-start(f32[1,64,320]{2,1,0:T(8,128)S(1)} %get-tuple-element.25) | copy-start | bytes 245764
  8.8 40.6 %copy-start.8 = (f32[1,64,320]{2,1,0:T(8,128)}, f32[1,64,320]{2,1,0:T(8,128)S(1)}, u32[]{:S(2)}) copy-start(f32[1,64,320]{2,1,0:T(8,128)S(1)} %get-tuple-element.24) | copy-start | bytes 245764
  10.6 7.7 %copy-start.51 = (s32[320]{0:T(512)S(1)}, s32[320]{0:T(512)}, u32[]{:S(2)}) copy-start(s32[320]{0:T(512)} %get-tuple-element.142) | copy-start | bytes 3844
  10.6 7.7 %copy-start.53 = (s32[320]{0:T(512)S(1)}, s32[320]{0:T(512)}, u32[]{:S(2)}) copy-start(s32[320]{0:T(512)} %get-tuple-element.143) | copy-start | bytes 3844
  10.7 7.7 %copy-start.59 = (pred[320]{0:T(512)(128)(4,1)S(1)}, pred[320]{0:T(512)(128)(4,1)}, u32[]{:S(2)}) copy-start(pred[320]{0:T(512)(128)(4,1)} %fusion.306) | copy-start | bytes 964
  10.7 8.2 %copy-start.47 = (s32[64]{0:T(128)S(1)}, s32[64]{0:T(128)}, u32[]{:S(2)}) copy-start(s32[64]{0:T(128)} %get-tuple-element.144) | copy-start | bytes 772
  10.7 8.2 %copy-start.49 = (s32[64]{0:T(128)S(1)}, s32[64]{0:T(128)}, u32[]{:S(2)}) copy-start(s32[64]{0:T(128)} %get-tuple-element.145) | copy-start | bytes 772
  11.6 14.9 %collective-permute-start.2 = (f32[1,2,64,320]{3,2,1,0:T(8,128)S(1)}, f32[1,2,64,320]{3,2,1,0:T(8,128)S(1)}, u32[]{:S(2)}, u32[]{:S(2)}) collective-permute-start(f32[1,2,64,320]{3,2,1,0:T(8,128)S(1)} %get-tuple-element.32), channel_id=1, source_target_pairs={{0,4},{4,8},{8,12},{12,16},{16,20},{20,24},{24,28},{1,5},{5,9},{9,... | collective-permute-start | bytes 491528 | tf_op jit(solution)/shard_map/ppermute | solution.py:54
  15.0 11.5 %collective-permute-start.3 = (f32[1,2,64,320]{3,2,1,0:T(8,128)S(1)}, f32[1,2,64,320]{3,2,1,0:T(8,128)S(1)}, u32[]{:S(2)}, u32[]{:S(2)}) collective-permute-start(f32[1,2,64,320]{3,2,1,0:T(8,128)S(1)} %get-tuple-element.33), channel_id=1, source_target_pairs={{4,0},{8,4},{12,8},{16,12},{20,16},{24,20},{28,24},{5,1},{9,5},{13... | collective-permute-start | bytes 491528 | tf_op jit(solution)/shard_map/ppermute | solution.py:55
  19.0 53.8 %copy-start.32 = (f32[32,2,160]{2,0,1:T(8,128)}, f32[32,2,160]{2,0,1:T(8,128)S(1)}, u32[]{:S(2)}) copy-start(f32[32,2,160]{2,0,1:T(8,128)S(1)} %get-tuple-element.139) | copy-start | bytes 122884
  19.1 5.7 %copy-start.55 = (s32[160]{0:T(256)S(1)}, s32[160]{0:T(256)}, u32[]{:S(2)}) copy-start(s32[160]{0:T(256)} %get-tuple-element.146) | copy-start | bytes 1924
  19.1 5.7 %copy-start.57 = (s32[160]{0:T(256)S(1)}, s32[160]{0:T(256)}, u32[]{:S(2)}) copy-start(s32[160]{0:T(256)} %get-tuple-element.147) | copy-start | bytes 1924
  19.1 5.7 %copy-start.64 = (pred[160]{0:T(512)(128)(4,1)S(1)}, pred[160]{0:T(512)(128)(4,1)}, u32[]{:S(2)}) copy-start(pred[160]{0:T(512)(128)(4,1)} %compare_and_fusion) | copy-start | bytes 484
  19.1 58.8 %collective-permute-start.12 = (f32[1,32,160]{2,1,0:T(8,128)S(1)}, f32[1,32,160]{2,1,0:T(8,128)S(1)}, u32[]{:S(2)}, u32[]{:S(2)}) collective-permute-start(f32[1,32,160]{2,1,0:T(8,128)S(1)} %get-tuple-element.132), channel_id=1, source_target_pairs={{0,12},{4,16},{8,20},{12,24},{16,28},{1,13},{5,17},{9,21},{13,25},... | collective-permute-start | bytes 61448 | tf_op jit(solution)/shard_map/ppermute | solution.py:65
  22.6 55.2 %collective-permute-start.13 = (f32[1,32,160]{2,1,0:T(8,128)S(1)}, f32[1,32,160]{2,1,0:T(8,128)S(1)}, u32[]{:S(2)}, u32[]{:S(2)}) collective-permute-start(f32[1,32,160]{2,1,0:T(8,128)S(1)} %get-tuple-element.133), channel_id=1, source_target_pairs={{12,0},{16,4},{20,8},{24,12},{28,16},{13,1},{17,5},{21,9},{25,13},... | collective-permute-start | bytes 61448 | tf_op jit(solution)/shard_map/ppermute | solution.py:66
  24.7 48.2 %copy-start.40 = (f32[32,2,160]{2,0,1:T(8,128)}, f32[32,2,160]{2,0,1:T(8,128)S(1)}, u32[]{:S(2)}) copy-start(f32[32,2,160]{2,0,1:T(8,128)S(1)} %get-tuple-element.135) | copy-start | bytes 122884
  25.9 47.0 %copy-start.42 = (f32[32,2,160]{2,0,1:T(8,128)}, f32[32,2,160]{2,0,1:T(8,128)S(1)}, u32[]{:S(2)}) copy-start(f32[32,2,160]{2,0,1:T(8,128)S(1)} %get-tuple-element.137) | copy-start | bytes 122884
  26.6 1.3 %copy-start.13 = (f32[4,64,256]{2,1,0:T(8,128)S(1)}, f32[4,64,256]{2,1,0:T(8,128)}, u32[]{:S(2)}) copy-start(f32[4,64,256]{2,1,0:T(8,128)} %param.7) | copy-start | bytes 786436
  26.6 1.5 %copy-start.15 = (f32[4,64,256]{2,1,0:T(8,128)S(1)}, f32[4,64,256]{2,1,0:T(8,128)}, u32[]{:S(2)}) copy-start(f32[4,64,256]{2,1,0:T(8,128)} %param.6) | copy-start | bytes 786436
  26.6 1.5 %copy-start.17 = (f32[4,64,256]{2,1,0:T(8,128)S(1)}, f32[4,64,256]{2,1,0:T(8,128)}, u32[]{:S(2)}) copy-start(f32[4,64,256]{2,1,0:T(8,128)} %param.5) | copy-start | bytes 786436
  26.9 25.2 %copy-start.4 = (f32[4,64,320]{2,1,0:T(8,128)}, f32[4,64,320]{2,1,0:T(8,128)S(1)}, u32[]{:S(2)}) copy-start(f32[4,64,320]{2,1,0:T(8,128)S(1)} %get-tuple-element.19) | copy-start | bytes 983044
  28.3 21.1 %collective-permute-start.6 = (f32[1,64,320]{2,1,0:T(8,128)S(1)}, f32[1,64,320]{2,1,0:T(8,128)S(1)}, u32[]{:S(2)}, u32[]{:S(2)}) collective-permute-start(f32[1,64,320]{2,1,0:T(8,128)S(1)} %fusion.207), channel_id=1, source_target_pairs={{0,4},{4,8},{8,12},{12,16},{16,20},{20,24},{24,28},{1,5},{5,9},{9,... | collective-permute-start | bytes 245768 | tf_op jit(solution)/shard_map/ppermute | solution.py:54
  34.0 7.3 %collective-permute-start.4 = (f32[1,64,320]{2,1,0:T(8,128)S(1)}, f32[1,64,320]{2,1,0:T(8,128)S(1)}, u32[]{:S(2)}, u32[]{:S(2)}) collective-permute-start(f32[1,64,320]{2,1,0:T(8,128)S(1)} %fusion.185), channel_id=1, source_target_pairs={{4,0},{8,4},{12,8},{16,12},{20,16},{24,20},{28,24},{5,1},{9,5},{13... | collective-permute-start | bytes 245768 | tf_op jit(solution)/shard_map/ppermute | solution.py:55
  41.4 15.3 %copy-start.44 = (f32[1,64,320]{2,1,0:T(8,128)}, f32[1,64,320]{2,1,0:T(8,128)S(1)}, u32[]{:S(2)}) copy-start(f32[1,64,320]{2,1,0:T(8,128)S(1)} %fusion.196) | copy-start | bytes 245764
  41.4 7.4 %collective-permute-start.5 = (f32[1,64,320]{2,1,0:T(8,128)S(1)}, f32[1,64,320]{2,1,0:T(8,128)S(1)}, u32[]{:S(2)}, u32[]{:S(2)}) collective-permute-start(f32[1,64,320]{2,1,0:T(8,128)S(1)} %fusion.196), channel_id=1, source_target_pairs={{0,4},{4,8},{8,12},{12,16},{16,20},{20,24},{24,28},{1,5},{5,9},{9,... | collective-permute-start | bytes 245768 | tf_op jit(solution)/shard_map/ppermute | solution.py:54
  50.2 6.5 %collective-permute-start.7 = (f32[1,64,320]{2,1,0:T(8,128)S(1)}, f32[1,64,320]{2,1,0:T(8,128)S(1)}, u32[]{:S(2)}, u32[]{:S(2)}) collective-permute-start(f32[1,64,320]{2,1,0:T(8,128)S(1)} %get-tuple-element.18), channel_id=1, source_target_pairs={{4,0},{8,4},{12,8},{16,12},{20,16},{24,20},{28,24},{5,1},{9,5},{13... | collective-permute-start | bytes 245768 | tf_op jit(solution)/shard_map/ppermute | solution.py:55
  56.7 20.6 %copy-start.46 = (f32[1,64,320]{2,1,0:T(8,128)}, f32[1,64,320]{2,1,0:T(8,128)S(1)}, u32[]{:S(2)}) copy-start(f32[1,64,320]{2,1,0:T(8,128)S(1)} %collective-permute-done.7) | copy-start | bytes 245764
  57.8 21.7 %copy-start.34 = (f32[32,2,160]{2,0,1:T(8,128)}, f32[32,2,160]{2,0,1:T(8,128)S(1)}, u32[]{:S(2)}) copy-start(f32[32,2,160]{2,0,1:T(8,128)S(1)} %convolution_multiply_fusion.3) | copy-start | bytes 122884
  57.9 11.0 %collective-permute-start.8 = (f32[2,4,32,160]{3,2,0,1:T(8,128)S(1)}, f32[2,4,32,160]{3,2,0,1:T(8,128)S(1)}, u32[]{:S(2)}, u32[]{:S(2)}) collective-permute-start(f32[2,4,32,160]{3,2,0,1:T(8,128)S(1)} %pad_maximum_fusion.8), channel_id=1, source_target_pairs={{0,8},{4,12},{8,16},{12,20},{16,24},{20,28},{1,9},{5,13},{9,17},{1... | collective-permute-start | bytes 491528 | tf_op jit(solution)/shard_map/ppermute | solution.py:54
  61.5 11.4 %collective-permute-start.9 = (f32[2,4,32,160]{3,2,0,1:T(8,128)S(1)}, f32[2,4,32,160]{3,2,0,1:T(8,128)S(1)}, u32[]{:S(2)}, u32[]{:S(2)}) collective-permute-start(f32[2,4,32,160]{3,2,0,1:T(8,128)S(1)} %pad_maximum_fusion.8), channel_id=1, source_target_pairs={{0,4},{4,8},{8,12},{12,16},{16,20},{20,24},{24,28},{1,5},{5,9},{9,... | collective-permute-start | bytes 491528 | tf_op jit(solution)/shard_map/ppermute | solution.py:54
  66.4 10.7 %collective-permute-start.11 = (f32[2,4,32,160]{3,2,0,1:T(8,128)S(1)}, f32[2,4,32,160]{3,2,0,1:T(8,128)S(1)}, u32[]{:S(2)}, u32[]{:S(2)}) collective-permute-start(f32[2,4,32,160]{3,2,0,1:T(8,128)S(1)} %pad_maximum_fusion.8), channel_id=1, source_target_pairs={{8,0},{12,4},{16,8},{20,12},{24,16},{28,20},{9,1},{13,5},{17,9},{2... | collective-permute-start | bytes 491528 | tf_op jit(solution)/shard_map/ppermute | solution.py:55
  68.8 8.3 %collective-permute-start.10 = (f32[2,4,32,160]{3,2,0,1:T(8,128)S(1)}, f32[2,4,32,160]{3,2,0,1:T(8,128)S(1)}, u32[]{:S(2)}, u32[]{:S(2)}) collective-permute-start(f32[2,4,32,160]{3,2,0,1:T(8,128)S(1)} %pad_maximum_fusion.8), channel_id=1, source_target_pairs={{4,0},{8,4},{12,8},{16,12},{20,16},{24,20},{28,24},{5,1},{9,5},{13... | collective-permute-start | bytes 491528 | tf_op jit(solution)/shard_map/ppermute | solution.py:55
  72.9 4.4 %copy-start.36 = (f32[2,4,32,160]{3,2,0,1:T(8,128)}, f32[2,4,32,160]{3,2,0,1:T(8,128)S(1)}, u32[]{:S(2)}) copy-start(f32[2,4,32,160]{3,2,0,1:T(8,128)S(1)} %collective-permute-done.9) | copy-start | bytes 491524
  77.9 1.7 %copy-start.6 = (f32[10,31,160]{2,1,0:T(8,128)}, f32[10,31,160]{2,1,0:T(8,128)S(1)}, u32[]{:S(2)}) copy-start(f32[10,31,160]{2,1,0:T(8,128)S(1)} %fusion.24) | copy-start | bytes 595204
  78.3 1.3 copy-start.22
  78.3 1.3 copy-start.24
  81.3 11.2 %all-to-all-start = ((f32[8,1,4,16,80]{4,3,2,1,0:T(8,128)}), f32[8,1,4,16,80]{4,3,2,1,0:T(8,128)}, u32[]{:S(2)}, u32[]{:S(2)}) async-start(f32[8,1,4,16,80]{4,3,2,1,0:T(8,128)} %broadcast_in_dim.20), calls=%async_computation | async-start | bytes 524288 | tf_op jit(solution)/shard_map/all_to_all | solution.py:73
  94.6 3.1 %copy-start.56 = (s32[160]{0:T(256)S(1)}, s32[160]{0:T(256)}, u32[]{:S(2)}) copy-start(s32[160]{0:T(256)} %get-tuple-element.146) | copy-start | bytes 1924
  94.6 3.1 %copy-start.58 = (s32[160]{0:T(256)S(1)}, s32[160]{0:T(256)}, u32[]{:S(2)}) copy-start(s32[160]{0:T(256)} %get-tuple-element.147) | copy-start | bytes 1924
  94.6 3.1 %copy-start.65 = (pred[160]{0:T(512)(128)(4,1)S(1)}, pred[160]{0:T(512)(128)(4,1)}, u32[]{:S(2)}) copy-start(pred[160]{0:T(512)(128)(4,1)} %compare_and_fusion) | copy-start | bytes 484
  95.7 2.9 %copy-start.21 = (f32[8,32,160]{2,1,0:T(8,128)S(1)}, f32[8,32,160]{2,1,0:T(8,128)}, u32[]{:S(2)}) copy-start(f32[8,32,160]{2,1,0:T(8,128)} %copy-done.20) | copy-start | bytes 491524
  98.1 1.3 %copy-start.29 = (f32[10,32,160]{2,1,0:T(8,128)S(1)}, f32[10,32,160]{2,1,0:T(8,128)}, u32[]{:S(2)}) copy-start(f32[10,32,160]{2,1,0:T(8,128)} %copy-done.28) | copy-start | bytes 614404
  98.1 1.4 %copy-start.31 = (f32[10,32,160]{2,1,0:T(8,128)S(1)}, f32[10,32,160]{2,1,0:T(8,128)}, u32[]{:S(2)}) copy-start(f32[10,32,160]{2,1,0:T(8,128)} %copy-done.30) | copy-start | bytes 614404
  98.1 1.4 %copy-start.33 = (f32[32,2,160]{2,0,1:T(8,128)S(1)}, f32[32,2,160]{2,0,1:T(8,128)}, u32[]{:S(2)}) copy-start(f32[32,2,160]{2,0,1:T(8,128)} %copy-done.32) | copy-start | bytes 122884
  98.1 1.4 %copy-start.35 = (f32[32,2,160]{2,0,1:T(8,128)S(1)}, f32[32,2,160]{2,0,1:T(8,128)}, u32[]{:S(2)}) copy-start(f32[32,2,160]{2,0,1:T(8,128)} %copy-done.34) | copy-start | bytes 122884
  98.1 1.5 %copy-start.37 = (f32[2,4,32,160]{3,2,0,1:T(8,128)S(1)}, f32[2,4,32,160]{3,2,0,1:T(8,128)}, u32[]{:S(2)}) copy-start(f32[2,4,32,160]{3,2,0,1:T(8,128)} %copy-done.36) | copy-start | bytes 491524
  98.2 1.6 %copy-start.39 = (f32[2,4,32,160]{3,2,0,1:T(8,128)S(1)}, f32[2,4,32,160]{3,2,0,1:T(8,128)}, u32[]{:S(2)}) copy-start(f32[2,4,32,160]{3,2,0,1:T(8,128)} %copy-done.38) | copy-start | bytes 491524
  98.2 1.6 %copy-start.41 = (f32[32,2,160]{2,0,1:T(8,128)S(1)}, f32[32,2,160]{2,0,1:T(8,128)}, u32[]{:S(2)}) copy-start(f32[32,2,160]{2,0,1:T(8,128)} %copy-done.40) | copy-start | bytes 122884
  98.2 1.6 %copy-start.43 = (f32[32,2,160]{2,0,1:T(8,128)S(1)}, f32[32,2,160]{2,0,1:T(8,128)}, u32[]{:S(2)}) copy-start(f32[32,2,160]{2,0,1:T(8,128)} %copy-done.42) | copy-start | bytes 122884
  98.2 1.6 %copy-start.63 = (pred[6]{0:T(512)(128)(4,1)S(1)}, pred[6]{0:T(512)(128)(4,1)}, u32[]{:S(2)}) copy-start(pred[6]{0:T(512)(128)(4,1)} %compare_and_fusion.3) | copy-start | bytes 22
  101.4 1.4 %copy-start.5 = (f32[4,64,320]{2,1,0:T(8,128)S(1)}, f32[4,64,320]{2,1,0:T(8,128)}, u32[]{:S(2)}) copy-start(f32[4,64,320]{2,1,0:T(8,128)} %copy-done.4) | copy-start | bytes 983044
  101.4 1.4 %copy-start.9 = (f32[1,64,320]{2,1,0:T(8,128)S(1)}, f32[1,64,320]{2,1,0:T(8,128)}, u32[]{:S(2)}) copy-start(f32[1,64,320]{2,1,0:T(8,128)} %copy-done.8) | copy-start | bytes 245764
  102.8 3.7 %copy-start.11 = (f32[1,64,320]{2,1,0:T(8,128)S(1)}, f32[1,64,320]{2,1,0:T(8,128)}, u32[]{:S(2)}) copy-start(f32[1,64,320]{2,1,0:T(8,128)} %copy-done.10) | copy-start | bytes 245764
  103.0 15.5 %collective-permute-start.15 = (f32[1,64,320]{2,1,0:T(8,128)S(1)}, f32[1,64,320]{2,1,0:T(8,128)S(1)}, u32[]{:S(2)}, u32[]{:S(2)}) collective-permute-start(f32[1,64,320]{2,1,0:T(8,128)S(1)} %fusion.164), channel_id=1, source_target_pairs={{4,0},{8,4},{12,8},{16,12},{20,16},{24,20},{28,24},{5,1},{9,5},{13... | collective-permute-start | bytes 245768 | tf_op jit(solution)/shard_map/ppermute | solution.py:55
  106.6 7.4 %collective-permute-start.14 = (f32[1,64,320]{2,1,0:T(8,128)S(1)}, f32[1,64,320]{2,1,0:T(8,128)S(1)}, u32[]{:S(2)}, u32[]{:S(2)}) collective-permute-start(f32[1,64,320]{2,1,0:T(8,128)S(1)} %fusion.154), channel_id=1, source_target_pairs={{0,4},{4,8},{8,12},{12,16},{16,20},{20,24},{24,28},{1,5},{5,9},{9,... | collective-permute-start | bytes 245768 | tf_op jit(solution)/shard_map/ppermute | solution.py:54
  114.2 6.7 %collective-permute-start.17 = (f32[1,64,320]{2,1,0:T(8,128)S(1)}, f32[1,64,320]{2,1,0:T(8,128)S(1)}, u32[]{:S(2)}, u32[]{:S(2)}) collective-permute-start(f32[1,64,320]{2,1,0:T(8,128)S(1)} %fusion.144), channel_id=1, source_target_pairs={{4,0},{8,4},{12,8},{16,12},{20,16},{24,20},{28,24},{5,1},{9,5},{13... | collective-permute-start | bytes 245768 | tf_op jit(solution)/shard_map/ppermute | solution.py:55
  118.6 7.4 %collective-permute-start.16 = (f32[1,64,320]{2,1,0:T(8,128)S(1)}, f32[1,64,320]{2,1,0:T(8,128)S(1)}, u32[]{:S(2)}, u32[]{:S(2)}) collective-permute-start(f32[1,64,320]{2,1,0:T(8,128)S(1)} %fusion.134), channel_id=1, source_target_pairs={{0,4},{4,8},{8,12},{12,16},{16,20},{20,24},{24,28},{1,5},{5,9},{9,... | collective-permute-start | bytes 245768 | tf_op jit(solution)/shard_map/ppermute | solution.py:54
  120.8 5.4 %copy-start.45 = (f32[4,64,320]{2,1,0:T(8,128)S(1)}, f32[4,64,320]{2,1,0:T(8,128)}, u32[]{:S(2)}) copy-start(f32[4,64,320]{2,1,0:T(8,128)} %get-tuple-element.26) | copy-start | bytes 983044
  (21 other events, 19.8 us)

commit v20 on v19

--- a/solution.py
+++ b/solution.py
@@ -196,16 +196,18 @@
     rhs_two = coarsen(wide_source - applied)
 
     wide_two = SWEEPS + 3
-    level_two = alt_extend(jnp.stack([rhs_two] + coef_two, 1), wide_two - 1)
+    lanes = rhs_two.shape[-1]
+    level_two = alt_extend(jnp.concatenate([rhs_two] + coef_two, axis=-1), wide_two - 1)
+    level_two = [level_two[..., i * lanes:(i + 1) * lanes] for i in range(4)]
     far_below, far_above = alt_row(coef_two[0], wide_two)
     weights_two = make_weights(
-        jnp.concatenate([far_below, level_two[:, 1], far_above], axis=0),
-        level_two[:, 2],
-        level_two[:, 3],
+        jnp.concatenate([far_below, level_two[1], far_above], axis=0),
+        level_two[2],
+        level_two[3],
         0.25,
         wide_two - 1,
     )
-    rhs_two_x = level_two[:, 0]
+    rhs_two_x = level_two[0]
     correction = first_sweep(weights_two, rhs_two_x, wide_two - 1)
     correction = sweep(weights_two, correction, wide_two - 1, rhs_two_x, wide_two - 1)
     applied, _ = apply_op(weights_two, trim(correction, wide_two - 2, 1), 1)

time: 129 us -> 127 us (0.984)
  waiting for transfers between devices: 30.1 us -> 28.8 us
    ppermute x7, waiting for transfers between devices: 13.8 us -> 11.3 us  [alt_extend(): below.insert(0, lax.ppermute(values[low:], 'alt', up))]
    unnamed x137 -> x138, local copies, waits for them, and re-layouts: 6.94 us -> 6.54 us
  transfers between devices with their start and end apart: 19 -> 19, of which waited for: 9 -> 9; matrix products, arithmetic and copies ran while one was open for 14% -> 15% of each run, Pallas kernels for 0% -> 0%
where the time goes in v20:
time: 127 us; the launch traced here: 126 us
  starting transfers between devices  55.1 us (43%)
  waiting for transfers between devices  28.8 us (23%)
  other arithmetic  19.4 us (15%)
  local copies, waits for them, and re-layouts  14.8 us (12%)
  matrix products  5.56 us (4%)
  between operations  2.3 us (2%)
    ppermute x7, starting transfers between devices, alt_extend(): below.insert(0, lax.ppermute(values[low:], 'alt', up))  26.1 us
    ppermute x7, starting transfers between devices, alt_extend(): above.append(lax.ppermute(values[:high], 'alt', down))  18.5 us
    ppermute x7, waiting for transfers between devices, alt_extend(): above.append(lax.ppermute(values[:high], 'alt', down))  14.1 us
    ppermute x7, waiting for transfers between devices, alt_extend(): below.insert(0, lax.ppermute(values[low:], 'alt', up))  11.3 us
    unnamed x138, local copies, waits for them, and re-layouts  6.54 us
    all_to_all x1, starting transfers between devices, spread_gather(): every = lax.all_to_all(copies, 'alt', 0, 0)  4.65 us
    ppermute x1, starting transfers between devices, alt_row(): below = lax.ppermute(values[index:index + 1], 'alt', up)  3.54 us
    add x3, other arithmetic, sweep(): centre + OMEGA * (trim(target, target_halo, halo - 1) - applied) / diagonal  2.88 us
  transfers between devices with their start and end apart: 19, of which 9 were waited for; matrix products, arithmetic and copies ran while one was open for 15% of the time, Pallas kernels for 0%

profile of v20, /device:TPU:8, one launch (start us, length us, event | category | flops | bytes accessed | tf_op | source)
XLA Modules:
  0.0 126.0 jit_solution(11755056452349856587)
XLA Ops:
  0.6 1.3 %pad_maximum_fusion.1 = f32[4,4,64,256]{3,2,1,0:T(8,128)S(1)} fusion(f32[4,1,64,256]{3,2,1,0:T(8,128)} %bitcast.354, f32[4,1,64,256]{3,2,1,0:T(8,128)} %bitcast.359, f32[4,1,64,256]{3,2,1,0:T(8,128)} %bitcast.364, f32[4,1,64,256]{3,2,1,0:T(8,128)} %bitcast.369), kind=kLoop, calls=%fused_computation.19 | loop fusion | flops 786432 | bytes 2097152 | tf_op jit(solution)/shard_map/stack | solution.py:183
  2.3 1.0 collective-permute-start.1
  3.6 0.5 compare_and_fusion
  4.1 0.5 fusion.308
  4.6 0.6 iota_shift-right-logical_fusion.3
  5.2 0.6 iota_shift-right-logical_fusion.1
  5.8 0.5 compare_and_fusion.2
  6.3 0.6 compare_and_fusion.3
  6.9 0.6 iota_shift-right-logical_fusion
  7.5 0.7 collective-permute-done
  9.4 0.4 copy-done.19
  9.8 0.6 pad_maximum_fusion
  10.7 0.9 slice_bitcast_fusion
  11.6 3.4 %collective-permute-start.2 = (f32[1,2,64,320]{3,2,1,0:T(8,128)S(1)}, f32[1,2,64,320]{3,2,1,0:T(8,128)S(1)}, u32[]{:S(2)}, u32[]{:S(2)}) collective-permute-start(f32[1,2,64,320]{3,2,1,0:T(8,128)S(1)} %get-tuple-element.32), channel_id=1, source_target_pairs={{0,4},{4,8},{8,12},{12,16},{16,20},{20,24},{24,28},{1,5},{5,9},{9,... | collective-permute-start | bytes 491528 | tf_op jit(solution)/shard_map/ppermute | solution.py:54
  15.0 3.3 %collective-permute-start.3 = (f32[1,2,64,320]{3,2,1,0:T(8,128)S(1)}, f32[1,2,64,320]{3,2,1,0:T(8,128)S(1)}, u32[]{:S(2)}, u32[]{:S(2)}) collective-permute-start(f32[1,2,64,320]{3,2,1,0:T(8,128)S(1)} %get-tuple-element.33), channel_id=1, source_target_pairs={{4,0},{8,4},{12,8},{16,12},{20,16},{24,20},{28,24},{5,1},{9,5},{13... | collective-permute-start | bytes 491528 | tf_op jit(solution)/shard_map/ppermute | solution.py:55
  18.4 0.4 fusion.324
  19.1 3.5 %collective-permute-start.12 = (f32[1,32,160]{2,1,0:T(8,128)S(1)}, f32[1,32,160]{2,1,0:T(8,128)S(1)}, u32[]{:S(2)}, u32[]{:S(2)}) collective-permute-start(f32[1,32,160]{2,1,0:T(8,128)S(1)} %get-tuple-element.129), channel_id=1, source_target_pairs={{0,12},{4,16},{8,20},{12,24},{16,28},{1,13},{5,17},{9,21},{13,25},... | collective-permute-start | bytes 61448 | tf_op jit(solution)/shard_map/ppermute | solution.py:65
  22.7 1.3 %collective-permute-start.13 = (f32[1,32,160]{2,1,0:T(8,128)S(1)}, f32[1,32,160]{2,1,0:T(8,128)S(1)}, u32[]{:S(2)}, u32[]{:S(2)}) collective-permute-start(f32[1,32,160]{2,1,0:T(8,128)S(1)} %get-tuple-element.130), channel_id=1, source_target_pairs={{12,0},{16,4},{20,8},{24,12},{28,16},{13,1},{17,5},{21,9},{25,13},... | collective-permute-start | bytes 61448 | tf_op jit(solution)/shard_map/ppermute | solution.py:66
  24.1 0.4 fusion.320
  25.3 0.5 fusion.322
  26.9 0.7 copy-done.1
  28.3 5.0 %collective-permute-start.6 = (f32[1,64,320]{2,1,0:T(8,128)S(1)}, f32[1,64,320]{2,1,0:T(8,128)S(1)}, u32[]{:S(2)}, u32[]{:S(2)}) collective-permute-start(f32[1,64,320]{2,1,0:T(8,128)S(1)} %fusion.209), channel_id=1, source_target_pairs={{0,4},{4,8},{8,12},{12,16},{16,20},{20,24},{24,28},{1,5},{5,9},{9,... | collective-permute-start | bytes 245768 | tf_op jit(solution)/shard_map/ppermute | solution.py:54
  34.0 1.9 %collective-permute-start.4 = (f32[1,64,320]{2,1,0:T(8,128)S(1)}, f32[1,64,320]{2,1,0:T(8,128)S(1)}, u32[]{:S(2)}, u32[]{:S(2)}) collective-permute-start(f32[1,64,320]{2,1,0:T(8,128)S(1)} %fusion.187), channel_id=1, source_target_pairs={{4,0},{8,4},{12,8},{16,12},{20,16},{24,20},{28,24},{5,1},{9,5},{13... | collective-permute-start | bytes 245768 | tf_op jit(solution)/shard_map/ppermute | solution.py:55
  36.0 5.3 %collective-permute-done.4 = f32[1,64,320]{2,1,0:T(8,128)S(1)} collective-permute-done((f32[1,64,320]{2,1,0:T(8,128)S(1)}, f32[1,64,320]{2,1,0:T(8,128)S(1)}, u32[]{:S(2)}, u32[]{:S(2)}) %collective-permute-start.4) | collective-permute-done | bytes 81952 | tf_op jit(solution)/shard_map/ppermute | solution.py:55
  41.4 4.8 %collective-permute-start.5 = (f32[1,64,320]{2,1,0:T(8,128)S(1)}, f32[1,64,320]{2,1,0:T(8,128)S(1)}, u32[]{:S(2)}, u32[]{:S(2)}) collective-permute-start(f32[1,64,320]{2,1,0:T(8,128)S(1)} %fusion.198), channel_id=1, source_target_pairs={{0,4},{4,8},{8,12},{12,16},{16,20},{20,24},{24,28},{1,5},{5,9},{9,... | collective-permute-start | bytes 245768 | tf_op jit(solution)/shard_map/ppermute | solution.py:54
  46.3 2.6 %collective-permute-done.5 = f32[1,64,320]{2,1,0:T(8,128)S(1)} collective-permute-done((f32[1,64,320]{2,1,0:T(8,128)S(1)}, f32[1,64,320]{2,1,0:T(8,128)S(1)}, u32[]{:S(2)}, u32[]{:S(2)}) %collective-permute-start.5) | collective-permute-done | bytes 81952 | tf_op jit(solution)/shard_map/ppermute | solution.py:54
  48.8 0.6 constant_dynamic-update-slice_fusion.4
  49.5 0.8 constant_dynamic-update-slice_fusion.3
  50.3 1.9 %collective-permute-start.7 = (f32[1,64,320]{2,1,0:T(8,128)S(1)}, f32[1,64,320]{2,1,0:T(8,128)S(1)}, u32[]{:S(2)}, u32[]{:S(2)}) collective-permute-start(f32[1,64,320]{2,1,0:T(8,128)S(1)} %get-tuple-element.18), channel_id=1, source_target_pairs={{4,0},{8,4},{12,8},{16,12},{20,16},{24,20},{28,24},{5,1},{9,5},{13... | collective-permute-start | bytes 245768 | tf_op jit(solution)/shard_map/ppermute | solution.py:55
  52.2 0.9 constant_dynamic-update-slice_fusion.2
  53.4 3.4 %collective-permute-done.7 = f32[1,64,320]{2,1,0:T(8,128)S(1)} collective-permute-done((f32[1,64,320]{2,1,0:T(8,128)S(1)}, f32[1,64,320]{2,1,0:T(8,128)S(1)}, u32[]{:S(2)}, u32[]{:S(2)}) %collective-permute-start.7) | collective-permute-done | bytes 81952 | tf_op jit(solution)/shard_map/ppermute | solution.py:55
  56.8 0.5 bitcast_reduce_fusion.3
  57.3 0.4 fusion.326
  58.1 3.5 %collective-permute-start.8 = (f32[2,32,640]{2,1,0:T(8,128)S(1)}, f32[2,32,640]{2,1,0:T(8,128)S(1)}, u32[]{:S(2)}, u32[]{:S(2)}) collective-permute-start(f32[2,32,640]{2,1,0:T(8,128)S(1)} %pad_maximum_fusion.12), channel_id=1, source_target_pairs={{0,8},{4,12},{8,16},{12,20},{16,24},{20,28},{1,9},{5,13},{9,17},{1... | collective-permute-start | bytes 491528 | tf_op jit(solution)/shard_map/ppermute | solution.py:54
  61.7 4.8 %collective-permute-start.9 = (f32[2,32,640]{2,1,0:T(8,128)S(1)}, f32[2,32,640]{2,1,0:T(8,128)S(1)}, u32[]{:S(2)}, u32[]{:S(2)}) collective-permute-start(f32[2,32,640]{2,1,0:T(8,128)S(1)} %pad_maximum_fusion.12), channel_id=1, source_target_pairs={{0,4},{4,8},{8,12},{12,16},{16,20},{20,24},{24,28},{1,5},{5,9},{9,... | collective-permute-start | bytes 491528 | tf_op jit(solution)/shard_map/ppermute | solution.py:54
  66.7 2.4 %collective-permute-start.11 = (f32[2,32,640]{2,1,0:T(8,128)S(1)}, f32[2,32,640]{2,1,0:T(8,128)S(1)}, u32[]{:S(2)}, u32[]{:S(2)}) collective-permute-start(f32[2,32,640]{2,1,0:T(8,128)S(1)} %pad_maximum_fusion.12), channel_id=1, source_target_pairs={{8,0},{12,4},{16,8},{20,12},{24,16},{28,20},{9,1},{13,5},{17,9},{2... | collective-permute-start | bytes 491528 | tf_op jit(solution)/shard_map/ppermute | solution.py:55
  69.1 1.9 %collective-permute-start.10 = (f32[2,32,640]{2,1,0:T(8,128)S(1)}, f32[2,32,640]{2,1,0:T(8,128)S(1)}, u32[]{:S(2)}, u32[]{:S(2)}) collective-permute-start(f32[2,32,640]{2,1,0:T(8,128)S(1)} %pad_maximum_fusion.12), channel_id=1, source_target_pairs={{4,0},{8,4},{12,8},{16,12},{20,16},{24,20},{28,24},{5,1},{9,5},{13... | collective-permute-start | bytes 491528 | tf_op jit(solution)/shard_map/ppermute | solution.py:55
  71.1 5.2 %collective-permute-done.10 = f32[2,32,640]{2,1,0:T(8,128)S(1)} collective-permute-done((f32[2,32,640]{2,1,0:T(8,128)S(1)}, f32[2,32,640]{2,1,0:T(8,128)S(1)}, u32[]{:S(2)}, u32[]{:S(2)}) %collective-permute-start.10) | collective-permute-done | bytes 163872 | tf_op jit(solution)/shard_map/ppermute | solution.py:55
  77.0 0.3 fusion.33
  77.6 0.5 copy-done.62
  78.1 0.4 fusion.52
  78.8 0.4 copy-done.20
  79.6 0.7 broadcast_in_dim.20
  80.4 4.6 %all-to-all-start = ((f32[8,1,4,16,80]{4,3,2,1,0:T(8,128)}), f32[8,1,4,16,80]{4,3,2,1,0:T(8,128)}, u32[]{:S(2)}, u32[]{:S(2)}) async-start(f32[8,1,4,16,80]{4,3,2,1,0:T(8,128)} %broadcast_in_dim.20), calls=%async_computation | async-start | bytes 524288 | tf_op jit(solution)/shard_map/all_to_all | solution.py:73
  85.0 0.6 compare_and_fusion.4
  85.6 1.5 %constant_dynamic-update-slice_fusion.1 = f32[6,64,320]{2,1,0:T(8,128)} fusion(f32[6,64,320]{2,1,0:T(8,128)} %get-tuple-element.15, f32[1,64,320]{2,1,0:T(8,128)} %copy-done.36), kind=kLoop, calls=%fused_computation.413 | loop fusion | bytes 196608
  87.1 1.5 %constant_dynamic-update-slice_fusion = f32[6,64,320]{2,1,0:T(8,128)} fusion(f32[6,64,320]{2,1,0:T(8,128)} %constant_dynamic-update-slice_fusion.1, f32[1,64,320]{2,1,0:T(8,128)} %copy-done.46), kind=kLoop, calls=%fused_computation.412 | loop fusion | bytes 196608 | tf_op jit(solution)/shard_map/concatenate | solution.py:56
  88.7 2.7 %all-to-all-done = f32[8,1,4,16,80]{4,3,2,1,0:T(8,128)} async-done(((f32[8,1,4,16,80]{4,3,2,1,0:T(8,128)}), f32[8,1,4,16,80]{4,3,2,1,0:T(8,128)}, u32[]{:S(2)}, u32[]{:S(2)}) %all-to-all-start) | async-done | bytes 163872 | tf_op jit(solution)/shard_map/all_to_all | solution.py:73
  91.3 0.9 slice_bitcast_fusion.12
  92.3 1.0 fusion.270
  93.5 0.9 fusion.232
  94.5 1.0 fusion.244
  95.6 0.9 fusion.256
  96.6 0.3 fusion.216
  99.2 0.5 fusion.124
  99.8 0.4 convolution_bitcast_fusion
  100.2 1.2 slice_add_fusion
  101.7 3.4 %collective-permute-start.15 = (f32[1,64,320]{2,1,0:T(8,128)S(1)}, f32[1,64,320]{2,1,0:T(8,128)S(1)}, u32[]{:S(2)}, u32[]{:S(2)}) collective-permute-start(f32[1,64,320]{2,1,0:T(8,128)S(1)} %fusion.166), channel_id=1, source_target_pairs={{4,0},{8,4},{12,8},{16,12},{20,16},{24,20},{28,24},{5,1},{9,5},{13... | collective-permute-start | bytes 245768 | tf_op jit(solution)/shard_map/ppermute | solution.py:55
  105.4 2.5 %collective-permute-start.14 = (f32[1,64,320]{2,1,0:T(8,128)S(1)}, f32[1,64,320]{2,1,0:T(8,128)S(1)}, u32[]{:S(2)}, u32[]{:S(2)}) collective-permute-start(f32[1,64,320]{2,1,0:T(8,128)S(1)} %fusion.156), channel_id=1, source_target_pairs={{0,4},{4,8},{8,12},{12,16},{16,20},{20,24},{24,28},{1,5},{5,9},{9,... | collective-permute-start | bytes 245768 | tf_op jit(solution)/shard_map/ppermute | solution.py:54
  108.8 4.0 %collective-permute-done.14 = f32[1,64,320]{2,1,0:T(8,128)S(1)} collective-permute-done((f32[1,64,320]{2,1,0:T(8,128)S(1)}, f32[1,64,320]{2,1,0:T(8,128)S(1)}, u32[]{:S(2)}, u32[]{:S(2)}) %collective-permute-start.14) | collective-permute-done | bytes 81952 | tf_op jit(solution)/shard_map/ppermute | solution.py:54
  112.9 3.7 %collective-permute-start.17 = (f32[1,64,320]{2,1,0:T(8,128)S(1)}, f32[1,64,320]{2,1,0:T(8,128)S(1)}, u32[]{:S(2)}, u32[]{:S(2)}) collective-permute-start(f32[1,64,320]{2,1,0:T(8,128)S(1)} %fusion.146), channel_id=1, source_target_pairs={{4,0},{8,4},{12,8},{16,12},{20,16},{24,20},{28,24},{5,1},{9,5},{13... | collective-permute-start | bytes 245768 | tf_op jit(solution)/shard_map/ppermute | solution.py:55
  116.8 2.1 %collective-permute-start.16 = (f32[1,64,320]{2,1,0:T(8,128)S(1)}, f32[1,64,320]{2,1,0:T(8,128)S(1)}, u32[]{:S(2)}, u32[]{:S(2)}) collective-permute-start(f32[1,64,320]{2,1,0:T(8,128)S(1)} %fusion.136), channel_id=1, source_target_pairs={{0,4},{4,8},{8,12},{12,16},{16,20},{20,24},{24,28},{1,5},{5,9},{9,... | collective-permute-start | bytes 245768 | tf_op jit(solution)/shard_map/ppermute | solution.py:54
  119.4 4.8 %collective-permute-done.16 = f32[1,64,320]{2,1,0:T(8,128)S(1)} collective-permute-done((f32[1,64,320]{2,1,0:T(8,128)S(1)}, f32[1,64,320]{2,1,0:T(8,128)S(1)}, u32[]{:S(2)}, u32[]{:S(2)}) %collective-permute-start.16) | collective-permute-done | bytes 81952 | tf_op jit(solution)/shard_map/ppermute | solution.py:54
  124.4 1.6 %fusion.41 = (f32[4,64,256]{2,1,0:T(8,128)}, f32[4,64,256]{2,1,0:T(8,128)}) fusion(f32[4,63,320]{2,1,0:T(8,128)S(1)} %fusion.8, f32[4,63,320]{2,1,0:T(8,128)S(1)} %get-tuple-element.51, f32[4,64,320]{2,1,0:T(8,128)S(1)} %copy-done.41, f32[4,64,319]{2,1,0:T(8,128)S(1)} %get-tuple-element.53, f32[4,64,320]{2,1,0:T(8,128)S(1)} %get-tuple-element.21, ...), kind=kLoop, calls=%fused_computation.87 | loop fusion | flops 655360 | bytes 3395584 | tf_op jit(solution)/shard_map/div | solution.py:235
  (240 shorter events, 12.9 us)
Async XLA Ops:
  2.1 6.5 %copy-start.12 = (f32[4,64,256]{2,1,0:T(8,128)S(1)}, f32[4,64,256]{2,1,0:T(8,128)}, u32[]{:S(2)}) copy-start(f32[4,64,256]{2,1,0:T(8,128)} %param.7) | copy-start | bytes 786436
  2.1 6.5 %copy-start.14 = (f32[4,64,256]{2,1,0:T(8,128)S(1)}, f32[4,64,256]{2,1,0:T(8,128)}, u32[]{:S(2)}) copy-start(f32[4,64,256]{2,1,0:T(8,128)} %param.6) | copy-start | bytes 786436
  2.2 6.5 %copy-start.16 = (f32[4,64,256]{2,1,0:T(8,128)S(1)}, f32[4,64,256]{2,1,0:T(8,128)}, u32[]{:S(2)}) copy-start(f32[4,64,256]{2,1,0:T(8,128)} %param.5) | copy-start | bytes 786436
  2.2 6.5 %copy-start.18 = (f32[4,64,256]{2,1,0:T(8,128)S(1)}, f32[4,64,256]{2,1,0:T(8,128)}, u32[]{:S(2)}) copy-start(f32[4,64,256]{2,1,0:T(8,128)} %param.4) | copy-start | bytes 786436
  2.3 6.1 %collective-permute-start.1 = (f32[4,4,16,128]{3,2,1,0:T(8,128)S(1)}, f32[4,4,16,128]{3,2,1,0:T(8,128)S(1)}, u32[]{:S(2)}, u32[]{:S(2)}) collective-permute-start(f32[4,4,16,128]{3,2,1,0:T(8,128)S(1)} %reshape.95), channel_id=1, source_target_pairs={{1,0},{2,1},{3,2},{0,3},{5,4},{6,5},{7,6},{4,7},{9,8},{10,9},{11,1... | collective-permute-start | bytes 393224 | tf_op jit(solution)/shard_map/ppermute | solution.py:42
  3.5 4.7 %collective-permute-start = (f32[4,4,16,128]{3,2,1,0:T(8,128)S(1)}, f32[4,4,16,128]{3,2,1,0:T(8,128)S(1)}, u32[]{:S(2)}, u32[]{:S(2)}) collective-permute-start(f32[4,4,16,128]{3,2,1,0:T(8,128)S(1)} %reshape.93), channel_id=1, source_target_pairs={{0,1},{1,2},{2,3},{3,0},{4,5},{5,6},{6,7},{7,4},{8,9},{9,10},{10,1... | collective-permute-start | bytes 393224 | tf_op jit(solution)/shard_map/ppermute | solution.py:41
  8.8 32.5 %copy-start.10 = (f32[1,64,320]{2,1,0:T(8,128)}, f32[1,64,320]{2,1,0:T(8,128)S(1)}, u32[]{:S(2)}) copy-start(f32[1,64,320]{2,1,0:T(8,128)S(1)} %get-tuple-element.25) | copy-start | bytes 245764
  8.8 40.7 %copy-start.8 = (f32[1,64,320]{2,1,0:T(8,128)}, f32[1,64,320]{2,1,0:T(8,128)S(1)}, u32[]{:S(2)}) copy-start(f32[1,64,320]{2,1,0:T(8,128)S(1)} %get-tuple-element.24) | copy-start | bytes 245764
  10.6 7.7 %copy-start.51 = (s32[320]{0:T(512)S(1)}, s32[320]{0:T(512)}, u32[]{:S(2)}) copy-start(s32[320]{0:T(512)} %get-tuple-element.139) | copy-start | bytes 3844
  10.6 7.7 %copy-start.53 = (s32[320]{0:T(512)S(1)}, s32[320]{0:T(512)}, u32[]{:S(2)}) copy-start(s32[320]{0:T(512)} %get-tuple-element.140) | copy-start | bytes 3844
  10.7 7.7 %copy-start.59 = (pred[320]{0:T(512)(128)(4,1)S(1)}, pred[320]{0:T(512)(128)(4,1)}, u32[]{:S(2)}) copy-start(pred[320]{0:T(512)(128)(4,1)} %fusion.308) | copy-start | bytes 964
  10.7 8.2 %copy-start.47 = (s32[64]{0:T(128)S(1)}, s32[64]{0:T(128)}, u32[]{:S(2)}) copy-start(s32[64]{0:T(128)} %get-tuple-element.141) | copy-start | bytes 772
  10.7 8.2 %copy-start.49 = (s32[64]{0:T(128)S(1)}, s32[64]{0:T(128)}, u32[]{:S(2)}) copy-start(s32[64]{0:T(128)} %get-tuple-element.142) | copy-start | bytes 772
  11.6 14.9 %collective-permute-start.2 = (f32[1,2,64,320]{3,2,1,0:T(8,128)S(1)}, f32[1,2,64,320]{3,2,1,0:T(8,128)S(1)}, u32[]{:S(2)}, u32[]{:S(2)}) collective-permute-start(f32[1,2,64,320]{3,2,1,0:T(8,128)S(1)} %get-tuple-element.32), channel_id=1, source_target_pairs={{0,4},{4,8},{8,12},{12,16},{16,20},{20,24},{24,28},{1,5},{5,9},{9,... | collective-permute-start | bytes 491528 | tf_op jit(solution)/shard_map/ppermute | solution.py:54
  15.0 11.5 %collective-permute-start.3 = (f32[1,2,64,320]{3,2,1,0:T(8,128)S(1)}, f32[1,2,64,320]{3,2,1,0:T(8,128)S(1)}, u32[]{:S(2)}, u32[]{:S(2)}) collective-permute-start(f32[1,2,64,320]{3,2,1,0:T(8,128)S(1)} %get-tuple-element.33), channel_id=1, source_target_pairs={{4,0},{8,4},{12,8},{16,12},{20,16},{24,20},{28,24},{5,1},{9,5},{13... | collective-permute-start | bytes 491528 | tf_op jit(solution)/shard_map/ppermute | solution.py:55
  19.1 38.9 %copy-start.34 = (f32[2,32,160]{2,1,0:T(8,128)}, f32[2,32,160]{2,1,0:T(8,128)S(1)}, u32[]{:S(2)}) copy-start(f32[2,32,160]{2,1,0:T(8,128)S(1)} %get-tuple-element.136) | copy-start | bytes 122884
  19.1 5.7 %copy-start.55 = (s32[160]{0:T(256)S(1)}, s32[160]{0:T(256)}, u32[]{:S(2)}) copy-start(s32[160]{0:T(256)} %get-tuple-element.143) | copy-start | bytes 1924
  19.1 5.7 %copy-start.57 = (s32[160]{0:T(256)S(1)}, s32[160]{0:T(256)}, u32[]{:S(2)}) copy-start(s32[160]{0:T(256)} %get-tuple-element.144) | copy-start | bytes 1924
  19.1 5.7 %copy-start.64 = (pred[160]{0:T(512)(128)(4,1)S(1)}, pred[160]{0:T(512)(128)(4,1)}, u32[]{:S(2)}) copy-start(pred[160]{0:T(512)(128)(4,1)} %compare_and_fusion) | copy-start | bytes 484
  19.1 57.9 %collective-permute-start.12 = (f32[1,32,160]{2,1,0:T(8,128)S(1)}, f32[1,32,160]{2,1,0:T(8,128)S(1)}, u32[]{:S(2)}, u32[]{:S(2)}) collective-permute-start(f32[1,32,160]{2,1,0:T(8,128)S(1)} %get-tuple-element.129), channel_id=1, source_target_pairs={{0,12},{4,16},{8,20},{12,24},{16,28},{1,13},{5,17},{9,21},{13,25},... | collective-permute-start | bytes 61448 | tf_op jit(solution)/shard_map/ppermute | solution.py:65
  22.7 54.3 %collective-permute-start.13 = (f32[1,32,160]{2,1,0:T(8,128)S(1)}, f32[1,32,160]{2,1,0:T(8,128)S(1)}, u32[]{:S(2)}, u32[]{:S(2)}) collective-permute-start(f32[1,32,160]{2,1,0:T(8,128)S(1)} %get-tuple-element.130), channel_id=1, source_target_pairs={{12,0},{16,4},{20,8},{24,12},{28,16},{13,1},{17,5},{21,9},{25,13},... | collective-permute-start | bytes 61448 | tf_op jit(solution)/shard_map/ppermute | solution.py:66
  24.7 33.2 %copy-start.42 = (f32[2,32,160]{2,1,0:T(8,128)}, f32[2,32,160]{2,1,0:T(8,128)S(1)}, u32[]{:S(2)}) copy-start(f32[2,32,160]{2,1,0:T(8,128)S(1)} %get-tuple-element.132) | copy-start | bytes 122884
  25.9 32.0 %copy-start.44 = (f32[2,32,160]{2,1,0:T(8,128)}, f32[2,32,160]{2,1,0:T(8,128)S(1)}, u32[]{:S(2)}) copy-start(f32[2,32,160]{2,1,0:T(8,128)S(1)} %get-tuple-element.134) | copy-start | bytes 122884
  26.6 1.3 %copy-start.13 = (f32[4,64,256]{2,1,0:T(8,128)S(1)}, f32[4,64,256]{2,1,0:T(8,128)}, u32[]{:S(2)}) copy-start(f32[4,64,256]{2,1,0:T(8,128)} %param.7) | copy-start | bytes 786436
  26.6 1.5 %copy-start.15 = (f32[4,64,256]{2,1,0:T(8,128)S(1)}, f32[4,64,256]{2,1,0:T(8,128)}, u32[]{:S(2)}) copy-start(f32[4,64,256]{2,1,0:T(8,128)} %param.6) | copy-start | bytes 786436
  26.6 1.5 %copy-start.17 = (f32[4,64,256]{2,1,0:T(8,128)S(1)}, f32[4,64,256]{2,1,0:T(8,128)}, u32[]{:S(2)}) copy-start(f32[4,64,256]{2,1,0:T(8,128)} %param.5) | copy-start | bytes 786436
  26.9 25.3 %copy-start.4 = (f32[4,64,320]{2,1,0:T(8,128)}, f32[4,64,320]{2,1,0:T(8,128)S(1)}, u32[]{:S(2)}) copy-start(f32[4,64,320]{2,1,0:T(8,128)S(1)} %get-tuple-element.19) | copy-start | bytes 983044
  28.3 21.2 %collective-permute-start.6 = (f32[1,64,320]{2,1,0:T(8,128)S(1)}, f32[1,64,320]{2,1,0:T(8,128)S(1)}, u32[]{:S(2)}, u32[]{:S(2)}) collective-permute-start(f32[1,64,320]{2,1,0:T(8,128)S(1)} %fusion.209), channel_id=1, source_target_pairs={{0,4},{4,8},{8,12},{12,16},{16,20},{20,24},{24,28},{1,5},{5,9},{9,... | collective-permute-start | bytes 245768 | tf_op jit(solution)/shard_map/ppermute | solution.py:54
  34.0 7.3 %collective-permute-start.4 = (f32[1,64,320]{2,1,0:T(8,128)S(1)}, f32[1,64,320]{2,1,0:T(8,128)S(1)}, u32[]{:S(2)}, u32[]{:S(2)}) collective-permute-start(f32[1,64,320]{2,1,0:T(8,128)S(1)} %fusion.187), channel_id=1, source_target_pairs={{4,0},{8,4},{12,8},{16,12},{20,16},{24,20},{28,24},{5,1},{9,5},{13... | collective-permute-start | bytes 245768 | tf_op jit(solution)/shard_map/ppermute | solution.py:55
  41.4 15.4 %copy-start.36 = (f32[1,64,320]{2,1,0:T(8,128)}, f32[1,64,320]{2,1,0:T(8,128)S(1)}, u32[]{:S(2)}) copy-start(f32[1,64,320]{2,1,0:T(8,128)S(1)} %fusion.198) | copy-start | bytes 245764
  41.4 7.4 %collective-permute-start.5 = (f32[1,64,320]{2,1,0:T(8,128)S(1)}, f32[1,64,320]{2,1,0:T(8,128)S(1)}, u32[]{:S(2)}, u32[]{:S(2)}) collective-permute-start(f32[1,64,320]{2,1,0:T(8,128)S(1)} %fusion.198), channel_id=1, source_target_pairs={{0,4},{4,8},{8,12},{12,16},{16,20},{20,24},{24,28},{1,5},{5,9},{9,... | collective-permute-start | bytes 245768 | tf_op jit(solution)/shard_map/ppermute | solution.py:54
  50.3 6.5 %collective-permute-start.7 = (f32[1,64,320]{2,1,0:T(8,128)S(1)}, f32[1,64,320]{2,1,0:T(8,128)S(1)}, u32[]{:S(2)}, u32[]{:S(2)}) collective-permute-start(f32[1,64,320]{2,1,0:T(8,128)S(1)} %get-tuple-element.18), channel_id=1, source_target_pairs={{4,0},{8,4},{12,8},{16,12},{20,16},{24,20},{28,24},{5,1},{9,5},{13... | collective-permute-start | bytes 245768 | tf_op jit(solution)/shard_map/ppermute | solution.py:55
  56.8 20.0 %copy-start.46 = (f32[1,64,320]{2,1,0:T(8,128)}, f32[1,64,320]{2,1,0:T(8,128)S(1)}, u32[]{:S(2)}) copy-start(f32[1,64,320]{2,1,0:T(8,128)S(1)} %collective-permute-done.7) | copy-start | bytes 245764
  57.9 20.7 %copy-start.32 = (f32[2,32,160]{2,1,0:T(8,128)}, f32[2,32,160]{2,1,0:T(8,128)S(1)}, u32[]{:S(2)}) copy-start(f32[2,32,160]{2,1,0:T(8,128)S(1)} %fusion.3) | copy-start | bytes 122884
  58.1 10.9 %collective-permute-start.8 = (f32[2,32,640]{2,1,0:T(8,128)S(1)}, f32[2,32,640]{2,1,0:T(8,128)S(1)}, u32[]{:S(2)}, u32[]{:S(2)}) collective-permute-start(f32[2,32,640]{2,1,0:T(8,128)S(1)} %pad_maximum_fusion.12), channel_id=1, source_target_pairs={{0,8},{4,12},{8,16},{12,20},{16,24},{20,28},{1,9},{5,13},{9,17},{1... | collective-permute-start | bytes 491528 | tf_op jit(solution)/shard_map/ppermute | solution.py:54
  61.7 9.3 %collective-permute-start.9 = (f32[2,32,640]{2,1,0:T(8,128)S(1)}, f32[2,32,640]{2,1,0:T(8,128)S(1)}, u32[]{:S(2)}, u32[]{:S(2)}) collective-permute-start(f32[2,32,640]{2,1,0:T(8,128)S(1)} %pad_maximum_fusion.12), channel_id=1, source_target_pairs={{0,4},{4,8},{8,12},{12,16},{16,20},{20,24},{24,28},{1,5},{5,9},{9,... | collective-permute-start | bytes 491528 | tf_op jit(solution)/shard_map/ppermute | solution.py:54
  66.7 9.6 %collective-permute-start.11 = (f32[2,32,640]{2,1,0:T(8,128)S(1)}, f32[2,32,640]{2,1,0:T(8,128)S(1)}, u32[]{:S(2)}, u32[]{:S(2)}) collective-permute-start(f32[2,32,640]{2,1,0:T(8,128)S(1)} %pad_maximum_fusion.12), channel_id=1, source_target_pairs={{8,0},{12,4},{16,8},{20,12},{24,16},{28,20},{9,1},{13,5},{17,9},{2... | collective-permute-start | bytes 491528 | tf_op jit(solution)/shard_map/ppermute | solution.py:55
  69.1 7.2 %collective-permute-start.10 = (f32[2,32,640]{2,1,0:T(8,128)S(1)}, f32[2,32,640]{2,1,0:T(8,128)S(1)}, u32[]{:S(2)}, u32[]{:S(2)}) collective-permute-start(f32[2,32,640]{2,1,0:T(8,128)S(1)} %pad_maximum_fusion.12), channel_id=1, source_target_pairs={{4,0},{8,4},{12,8},{16,12},{20,16},{24,20},{28,24},{5,1},{9,5},{13... | collective-permute-start | bytes 491528 | tf_op jit(solution)/shard_map/ppermute | solution.py:55
  71.0 5.8 %copy-start.37 = (f32[2,32,640]{2,1,0:T(8,128)}, f32[2,32,640]{2,1,0:T(8,128)S(1)}, u32[]{:S(2)}) copy-start(f32[2,32,640]{2,1,0:T(8,128)S(1)} %collective-permute-done.9) | copy-start | bytes 491524
  76.8 1.8 %copy-start.6 = (f32[10,31,160]{2,1,0:T(8,128)}, f32[10,31,160]{2,1,0:T(8,128)S(1)}, u32[]{:S(2)}) copy-start(f32[10,31,160]{2,1,0:T(8,128)S(1)} %fusion.28) | copy-start | bytes 595204
  77.4 1.3 %copy-start.22 = (f32[10,32,160]{2,1,0:T(8,128)}, f32[10,32,160]{2,1,0:T(8,128)S(1)}, u32[]{:S(2)}) copy-start(f32[10,32,160]{2,1,0:T(8,128)S(1)} %get-tuple-element.10) | copy-start | bytes 614404
  77.4 1.3 %copy-start.24 = (f32[10,32,160]{2,1,0:T(8,128)}, f32[10,32,160]{2,1,0:T(8,128)S(1)}, u32[]{:S(2)}) copy-start(f32[10,32,160]{2,1,0:T(8,128)S(1)} %get-tuple-element.11) | copy-start | bytes 614404
  80.4 11.0 %all-to-all-start = ((f32[8,1,4,16,80]{4,3,2,1,0:T(8,128)}), f32[8,1,4,16,80]{4,3,2,1,0:T(8,128)}, u32[]{:S(2)}, u32[]{:S(2)}) async-start(f32[8,1,4,16,80]{4,3,2,1,0:T(8,128)} %broadcast_in_dim.20), calls=%async_computation | async-start | bytes 524288 | tf_op jit(solution)/shard_map/all_to_all | solution.py:73
  93.4 3.1 %copy-start.56 = (s32[160]{0:T(256)S(1)}, s32[160]{0:T(256)}, u32[]{:S(2)}) copy-start(s32[160]{0:T(256)} %get-tuple-element.143) | copy-start | bytes 1924
  93.4 3.1 %copy-start.58 = (s32[160]{0:T(256)S(1)}, s32[160]{0:T(256)}, u32[]{:S(2)}) copy-start(s32[160]{0:T(256)} %get-tuple-element.144) | copy-start | bytes 1924
  93.4 3.1 %copy-start.65 = (pred[160]{0:T(512)(128)(4,1)S(1)}, pred[160]{0:T(512)(128)(4,1)}, u32[]{:S(2)}) copy-start(pred[160]{0:T(512)(128)(4,1)} %compare_and_fusion) | copy-start | bytes 484
  94.5 2.9 %copy-start.21 = (f32[8,32,160]{2,1,0:T(8,128)S(1)}, f32[8,32,160]{2,1,0:T(8,128)}, u32[]{:S(2)}) copy-start(f32[8,32,160]{2,1,0:T(8,128)} %copy-done.20) | copy-start | bytes 491524
  96.9 1.3 %copy-start.29 = (f32[10,32,160]{2,1,0:T(8,128)S(1)}, f32[10,32,160]{2,1,0:T(8,128)}, u32[]{:S(2)}) copy-start(f32[10,32,160]{2,1,0:T(8,128)} %copy-done.28) | copy-start | bytes 614404
  97.0 1.4 %copy-start.31 = (f32[10,32,160]{2,1,0:T(8,128)S(1)}, f32[10,32,160]{2,1,0:T(8,128)}, u32[]{:S(2)}) copy-start(f32[10,32,160]{2,1,0:T(8,128)} %copy-done.30) | copy-start | bytes 614404
  97.0 1.4 %copy-start.33 = (f32[2,32,160]{2,1,0:T(8,128)S(1)}, f32[2,32,160]{2,1,0:T(8,128)}, u32[]{:S(2)}) copy-start(f32[2,32,160]{2,1,0:T(8,128)} %copy-done.32) | copy-start | bytes 122884
  97.0 1.4 %copy-start.35 = (f32[2,32,160]{2,1,0:T(8,128)S(1)}, f32[2,32,160]{2,1,0:T(8,128)}, u32[]{:S(2)}) copy-start(f32[2,32,160]{2,1,0:T(8,128)} %copy-done.34) | copy-start | bytes 122884
  97.0 1.5 %copy-start.38 = (f32[2,32,640]{2,1,0:T(8,128)S(1)}, f32[2,32,640]{2,1,0:T(8,128)}, u32[]{:S(2)}) copy-start(f32[2,32,640]{2,1,0:T(8,128)} %copy-done.37) | copy-start | bytes 491524
  97.0 1.5 %copy-start.40 = (f32[2,32,640]{2,1,0:T(8,128)S(1)}, f32[2,32,640]{2,1,0:T(8,128)}, u32[]{:S(2)}) copy-start(f32[2,32,640]{2,1,0:T(8,128)} %copy-done.39) | copy-start | bytes 491524
  97.0 1.5 %copy-start.43 = (f32[2,32,160]{2,1,0:T(8,128)S(1)}, f32[2,32,160]{2,1,0:T(8,128)}, u32[]{:S(2)}) copy-start(f32[2,32,160]{2,1,0:T(8,128)} %copy-done.42) | copy-start | bytes 122884
  97.0 1.5 %copy-start.45 = (f32[2,32,160]{2,1,0:T(8,128)S(1)}, f32[2,32,160]{2,1,0:T(8,128)}, u32[]{:S(2)}) copy-start(f32[2,32,160]{2,1,0:T(8,128)} %copy-done.44) | copy-start | bytes 122884
  97.0 1.5 %copy-start.61 = (pred[6]{0:T(512)(128)(4,1)S(1)}, pred[6]{0:T(512)(128)(4,1)}, u32[]{:S(2)}) copy-start(pred[6]{0:T(512)(128)(4,1)} %compare_and_fusion.3) | copy-start | bytes 22
  100.2 1.4 %copy-start.5 = (f32[4,64,320]{2,1,0:T(8,128)S(1)}, f32[4,64,320]{2,1,0:T(8,128)}, u32[]{:S(2)}) copy-start(f32[4,64,320]{2,1,0:T(8,128)} %copy-done.4) | copy-start | bytes 983044
  100.2 1.4 %copy-start.9 = (f32[1,64,320]{2,1,0:T(8,128)S(1)}, f32[1,64,320]{2,1,0:T(8,128)}, u32[]{:S(2)}) copy-start(f32[1,64,320]{2,1,0:T(8,128)} %copy-done.8) | copy-start | bytes 245764
  101.5 3.7 %copy-start.11 = (f32[1,64,320]{2,1,0:T(8,128)S(1)}, f32[1,64,320]{2,1,0:T(8,128)}, u32[]{:S(2)}) copy-start(f32[1,64,320]{2,1,0:T(8,128)} %copy-done.10) | copy-start | bytes 245764
  101.7 14.9 %collective-permute-start.15 = (f32[1,64,320]{2,1,0:T(8,128)S(1)}, f32[1,64,320]{2,1,0:T(8,128)S(1)}, u32[]{:S(2)}, u32[]{:S(2)}) collective-permute-start(f32[1,64,320]{2,1,0:T(8,128)S(1)} %fusion.166), channel_id=1, source_target_pairs={{4,0},{8,4},{12,8},{16,12},{20,16},{24,20},{28,24},{5,1},{9,5},{13... | collective-permute-start | bytes 245768 | tf_op jit(solution)/shard_map/ppermute | solution.py:55
  105.4 7.4 %collective-permute-start.14 = (f32[1,64,320]{2,1,0:T(8,128)S(1)}, f32[1,64,320]{2,1,0:T(8,128)S(1)}, u32[]{:S(2)}, u32[]{:S(2)}) collective-permute-start(f32[1,64,320]{2,1,0:T(8,128)S(1)} %fusion.156), channel_id=1, source_target_pairs={{0,4},{4,8},{8,12},{12,16},{16,20},{20,24},{24,28},{1,5},{5,9},{9,... | collective-permute-start | bytes 245768 | tf_op jit(solution)/shard_map/ppermute | solution.py:54
  112.9 6.5 %collective-permute-start.17 = (f32[1,64,320]{2,1,0:T(8,128)S(1)}, f32[1,64,320]{2,1,0:T(8,128)S(1)}, u32[]{:S(2)}, u32[]{:S(2)}) collective-permute-start(f32[1,64,320]{2,1,0:T(8,128)S(1)} %fusion.146), channel_id=1, source_target_pairs={{4,0},{8,4},{12,8},{16,12},{20,16},{24,20},{28,24},{5,1},{9,5},{13... | collective-permute-start | bytes 245768 | tf_op jit(solution)/shard_map/ppermute | solution.py:55
  116.8 7.4 %collective-permute-start.16 = (f32[1,64,320]{2,1,0:T(8,128)S(1)}, f32[1,64,320]{2,1,0:T(8,128)S(1)}, u32[]{:S(2)}, u32[]{:S(2)}) collective-permute-start(f32[1,64,320]{2,1,0:T(8,128)S(1)} %fusion.136), channel_id=1, source_target_pairs={{0,4},{4,8},{8,12},{12,16},{16,20},{20,24},{24,28},{1,5},{5,9},{9,... | collective-permute-start | bytes 245768 | tf_op jit(solution)/shard_map/ppermute | solution.py:54
  119.2 5.2 %copy-start.41 = (f32[4,64,320]{2,1,0:T(8,128)S(1)}, f32[4,64,320]{2,1,0:T(8,128)}, u32[]{:S(2)}) copy-start(f32[4,64,320]{2,1,0:T(8,128)} %get-tuple-element.26) | copy-start | bytes 983044
  (21 other events, 19.8 us)

commit v21 on v20

--- a/solution.py
+++ b/solution.py
@@ -214,9 +214,11 @@
     rhs_three = coarsen(trim(rhs_two_x, wide_two - 1, 0) - applied)
 
     height = rhs_three.shape[0]
-    column = spread_gather(jnp.stack([rhs_three] + coef_three, 1))
-    weights_three = make_weights(pad_rows(column[:, 1]), column[:, 2], column[:, 3], 0.0625, 0)
-    rhs_three_x = column[:, 0]
+    lanes = rhs_three.shape[-1]
+    column = spread_gather(jnp.concatenate([rhs_three] + coef_three, axis=-1))
+    column = [column[..., i * lanes:(i + 1) * lanes] for i in range(4)]
+    weights_three = make_weights(pad_rows(column[1]), column[2], column[3], 0.0625, 0)
+    rhs_three_x = column[0]
     coarse_part = first_sweep(weights_three, rhs_three_x, 0)
     for _ in range(COARSE_SWEEPS - 1):
         coarse_part = sweep(weights_three, pad_rows(coarse_part), 1, rhs_three_x, 0, masked=False)

time: 127 us -> 129 us (1.016)
  no operation moved by 1% of the time
where the time goes in v21:
time: 129 us; the launch traced here: 128 us
  starting transfers between devices  55.1 us (43%)
  waiting for transfers between devices  28.5 us (22%)
  other arithmetic  20.5 us (16%)
  local copies, waits for them, and re-layouts  15.8 us (12%)
  matrix products  5.55 us (4%)
  between operations  2.3 us (2%)
    ppermute x7, starting transfers between devices, alt_extend(): below.insert(0, lax.ppermute(values[low:], 'alt', up))  25.9 us
    ppermute x7, starting transfers between devices, alt_extend(): above.append(lax.ppermute(values[:high], 'alt', down))  18.7 us
    ppermute x7, waiting for transfers between devices, alt_extend(): above.append(lax.ppermute(values[:high], 'alt', down))  14.1 us
    ppermute x7, waiting for transfers between devices, alt_extend(): below.insert(0, lax.ppermute(values[low:], 'alt', up))  11.5 us
    unnamed x138, local copies, waits for them, and re-layouts  6.52 us
    all_to_all x1, starting transfers between devices, spread_gather(): every = lax.all_to_all(copies, 'alt', 0, 0)  4.65 us
    ppermute x1, starting transfers between devices, alt_row(): below = lax.ppermute(values[index:index + 1], 'alt', up)  3.54 us
    add x3, other arithmetic, sweep(): centre + OMEGA * (trim(target, target_halo, halo - 1) - applied) / diagonal  2.87 us
  transfers between devices with their start and end apart: 19, of which 9 were waited for; matrix products, arithmetic and copies ran while one was open for 15% of the time, Pallas kernels for 0%

profile of v21, /device:TPU:8, one launch (start us, length us, event | category | flops | bytes accessed | tf_op | source)
XLA Modules:
  0.0 127.8 jit_solution(16640915223785302984)
XLA Ops:
  0.6 1.3 %pad_maximum_fusion.1 = f32[4,4,64,256]{3,2,1,0:T(8,128)S(1)} fusion(f32[4,1,64,256]{3,2,1,0:T(8,128)} %bitcast.326, f32[4,1,64,256]{3,2,1,0:T(8,128)} %bitcast.331, f32[4,1,64,256]{3,2,1,0:T(8,128)} %bitcast.336, f32[4,1,64,256]{3,2,1,0:T(8,128)} %bitcast.341), kind=kLoop, calls=%fused_computation.19 | loop fusion | flops 786432 | bytes 2097152 | tf_op jit(solution)/shard_map/stack | solution.py:183
  2.3 1.0 collective-permute-start.1
  3.6 0.6 compare_and_fusion
  4.2 0.5 fusion.308
  4.7 0.6 iota_shift-right-logical_fusion.3
  5.3 0.6 iota_shift-right-logical_fusion.1
  5.9 0.5 compare_and_fusion.2
  6.4 0.6 compare_and_fusion.3
  7.0 0.6 iota_shift-right-logical_fusion
  7.6 0.7 collective-permute-done
  9.4 0.4 copy-done.19
  9.8 0.6 pad_maximum_fusion
  10.7 0.9 slice_bitcast_fusion
  11.6 3.4 %collective-permute-start.2 = (f32[1,2,64,320]{3,2,1,0:T(8,128)S(1)}, f32[1,2,64,320]{3,2,1,0:T(8,128)S(1)}, u32[]{:S(2)}, u32[]{:S(2)}) collective-permute-start(f32[1,2,64,320]{3,2,1,0:T(8,128)S(1)} %get-tuple-element.32), channel_id=1, source_target_pairs={{0,4},{4,8},{8,12},{12,16},{16,20},{20,24},{24,28},{1,5},{5,9},{9,... | collective-permute-start | bytes 491528 | tf_op jit(solution)/shard_map/ppermute | solution.py:54
  15.0 3.3 %collective-permute-start.3 = (f32[1,2,64,320]{3,2,1,0:T(8,128)S(1)}, f32[1,2,64,320]{3,2,1,0:T(8,128)S(1)}, u32[]{:S(2)}, u32[]{:S(2)}) collective-permute-start(f32[1,2,64,320]{3,2,1,0:T(8,128)S(1)} %get-tuple-element.33), channel_id=1, source_target_pairs={{4,0},{8,4},{12,8},{16,12},{20,16},{24,20},{28,24},{5,1},{9,5},{13... | collective-permute-start | bytes 491528 | tf_op jit(solution)/shard_map/ppermute | solution.py:55
  18.4 0.4 fusion.324
  19.1 3.5 %collective-permute-start.12 = (f32[1,32,160]{2,1,0:T(8,128)S(1)}, f32[1,32,160]{2,1,0:T(8,128)S(1)}, u32[]{:S(2)}, u32[]{:S(2)}) collective-permute-start(f32[1,32,160]{2,1,0:T(8,128)S(1)} %get-tuple-element.126), channel_id=1, source_target_pairs={{0,12},{4,16},{8,20},{12,24},{16,28},{1,13},{5,17},{9,21},{13,25},... | collective-permute-start | bytes 61448 | tf_op jit(solution)/shard_map/ppermute | solution.py:65
  22.6 1.3 %collective-permute-start.13 = (f32[1,32,160]{2,1,0:T(8,128)S(1)}, f32[1,32,160]{2,1,0:T(8,128)S(1)}, u32[]{:S(2)}, u32[]{:S(2)}) collective-permute-start(f32[1,32,160]{2,1,0:T(8,128)S(1)} %get-tuple-element.127), channel_id=1, source_target_pairs={{12,0},{16,4},{20,8},{24,12},{28,16},{13,1},{17,5},{21,9},{25,13},... | collective-permute-start | bytes 61448 | tf_op jit(solution)/shard_map/ppermute | solution.py:66
  24.1 0.4 fusion.320
  25.3 0.5 fusion.322
  26.9 0.7 copy-done.1
  28.3 5.0 %collective-permute-start.6 = (f32[1,64,320]{2,1,0:T(8,128)S(1)}, f32[1,64,320]{2,1,0:T(8,128)S(1)}, u32[]{:S(2)}, u32[]{:S(2)}) collective-permute-start(f32[1,64,320]{2,1,0:T(8,128)S(1)} %fusion.209), channel_id=1, source_target_pairs={{0,4},{4,8},{8,12},{12,16},{16,20},{20,24},{24,28},{1,5},{5,9},{9,... | collective-permute-start | bytes 245768 | tf_op jit(solution)/shard_map/ppermute | solution.py:54
  34.0 1.9 %collective-permute-start.4 = (f32[1,64,320]{2,1,0:T(8,128)S(1)}, f32[1,64,320]{2,1,0:T(8,128)S(1)}, u32[]{:S(2)}, u32[]{:S(2)}) collective-permute-start(f32[1,64,320]{2,1,0:T(8,128)S(1)} %fusion.187), channel_id=1, source_target_pairs={{4,0},{8,4},{12,8},{16,12},{20,16},{24,20},{28,24},{5,1},{9,5},{13... | collective-permute-start | bytes 245768 | tf_op jit(solution)/shard_map/ppermute | solution.py:55
  36.0 5.3 %collective-permute-done.4 = f32[1,64,320]{2,1,0:T(8,128)S(1)} collective-permute-done((f32[1,64,320]{2,1,0:T(8,128)S(1)}, f32[1,64,320]{2,1,0:T(8,128)S(1)}, u32[]{:S(2)}, u32[]{:S(2)}) %collective-permute-start.4) | collective-permute-done | bytes 81952 | tf_op jit(solution)/shard_map/ppermute | solution.py:55
  41.4 4.8 %collective-permute-start.5 = (f32[1,64,320]{2,1,0:T(8,128)S(1)}, f32[1,64,320]{2,1,0:T(8,128)S(1)}, u32[]{:S(2)}, u32[]{:S(2)}) collective-permute-start(f32[1,64,320]{2,1,0:T(8,128)S(1)} %fusion.198), channel_id=1, source_target_pairs={{0,4},{4,8},{8,12},{12,16},{16,20},{20,24},{24,28},{1,5},{5,9},{9,... | collective-permute-start | bytes 245768 | tf_op jit(solution)/shard_map/ppermute | solution.py:54
  46.3 2.6 %collective-permute-done.5 = f32[1,64,320]{2,1,0:T(8,128)S(1)} collective-permute-done((f32[1,64,320]{2,1,0:T(8,128)S(1)}, f32[1,64,320]{2,1,0:T(8,128)S(1)}, u32[]{:S(2)}, u32[]{:S(2)}) %collective-permute-start.5) | collective-permute-done | bytes 81952 | tf_op jit(solution)/shard_map/ppermute | solution.py:54
  48.8 0.6 constant_dynamic-update-slice_fusion.4
  49.5 0.8 constant_dynamic-update-slice_fusion.3
  50.2 1.9 %collective-permute-start.7 = (f32[1,64,320]{2,1,0:T(8,128)S(1)}, f32[1,64,320]{2,1,0:T(8,128)S(1)}, u32[]{:S(2)}, u32[]{:S(2)}) collective-permute-start(f32[1,64,320]{2,1,0:T(8,128)S(1)} %get-tuple-element.18), channel_id=1, source_target_pairs={{4,0},{8,4},{12,8},{16,12},{20,16},{24,20},{28,24},{5,1},{9,5},{13... | collective-permute-start | bytes 245768 | tf_op jit(solution)/shard_map/ppermute | solution.py:55
  52.2 0.9 constant_dynamic-update-slice_fusion.2
  53.4 3.4 %collective-permute-done.7 = f32[1,64,320]{2,1,0:T(8,128)S(1)} collective-permute-done((f32[1,64,320]{2,1,0:T(8,128)S(1)}, f32[1,64,320]{2,1,0:T(8,128)S(1)}, u32[]{:S(2)}, u32[]{:S(2)}) %collective-permute-start.7) | collective-permute-done | bytes 81952 | tf_op jit(solution)/shard_map/ppermute | solution.py:55
  56.7 0.5 bitcast_reduce_fusion.3
  57.3 0.4 fusion.326
  58.1 3.5 %collective-permute-start.8 = (f32[2,32,640]{2,1,0:T(8,128)S(1)}, f32[2,32,640]{2,1,0:T(8,128)S(1)}, u32[]{:S(2)}, u32[]{:S(2)}) collective-permute-start(f32[2,32,640]{2,1,0:T(8,128)S(1)} %pad_maximum_fusion.12), channel_id=1, source_target_pairs={{0,8},{4,12},{8,16},{12,20},{16,24},{20,28},{1,9},{5,13},{9,17},{1... | collective-permute-start | bytes 491528 | tf_op jit(solution)/shard_map/ppermute | solution.py:54
  61.7 4.8 %collective-permute-start.9 = (f32[2,32,640]{2,1,0:T(8,128)S(1)}, f32[2,32,640]{2,1,0:T(8,128)S(1)}, u32[]{:S(2)}, u32[]{:S(2)}) collective-permute-start(f32[2,32,640]{2,1,0:T(8,128)S(1)} %pad_maximum_fusion.12), channel_id=1, source_target_pairs={{0,4},{4,8},{8,12},{12,16},{16,20},{20,24},{24,28},{1,5},{5,9},{9,... | collective-permute-start | bytes 491528 | tf_op jit(solution)/shard_map/ppermute | solution.py:54
  66.6 2.4 %collective-permute-start.11 = (f32[2,32,640]{2,1,0:T(8,128)S(1)}, f32[2,32,640]{2,1,0:T(8,128)S(1)}, u32[]{:S(2)}, u32[]{:S(2)}) collective-permute-start(f32[2,32,640]{2,1,0:T(8,128)S(1)} %pad_maximum_fusion.12), channel_id=1, source_target_pairs={{8,0},{12,4},{16,8},{20,12},{24,16},{28,20},{9,1},{13,5},{17,9},{2... | collective-permute-start | bytes 491528 | tf_op jit(solution)/shard_map/ppermute | solution.py:55
  69.0 1.9 %collective-permute-start.10 = (f32[2,32,640]{2,1,0:T(8,128)S(1)}, f32[2,32,640]{2,1,0:T(8,128)S(1)}, u32[]{:S(2)}, u32[]{:S(2)}) collective-permute-start(f32[2,32,640]{2,1,0:T(8,128)S(1)} %pad_maximum_fusion.12), channel_id=1, source_target_pairs={{4,0},{8,4},{12,8},{16,12},{20,16},{24,20},{28,24},{5,1},{9,5},{13... | collective-permute-start | bytes 491528 | tf_op jit(solution)/shard_map/ppermute | solution.py:55
  71.0 5.2 %collective-permute-done.10 = f32[2,32,640]{2,1,0:T(8,128)S(1)} collective-permute-done((f32[2,32,640]{2,1,0:T(8,128)S(1)}, f32[2,32,640]{2,1,0:T(8,128)S(1)}, u32[]{:S(2)}, u32[]{:S(2)}) %collective-permute-start.10) | collective-permute-done | bytes 163872 | tf_op jit(solution)/shard_map/ppermute | solution.py:55
  77.6 0.5 copy-done.62
  78.1 0.4 fusion.52
  78.7 0.4 copy-done.20
  79.7 0.7 broadcast_in_dim.20
  80.4 4.6 %all-to-all-start = ((f32[8,1,16,320]{3,2,1,0:T(8,128)}), f32[8,1,16,320]{3,2,1,0:T(8,128)}, u32[]{:S(2)}, u32[]{:S(2)}) async-start(f32[8,1,16,320]{3,2,1,0:T(8,128)} %broadcast_in_dim.20), calls=%async_computation | async-start | bytes 393216 | tf_op jit(solution)/shard_map/all_to_all | solution.py:73
  85.0 0.5 compare_and_fusion.4
  85.5 1.5 %constant_dynamic-update-slice_fusion.1 = f32[6,64,320]{2,1,0:T(8,128)} fusion(f32[6,64,320]{2,1,0:T(8,128)} %get-tuple-element.15, f32[1,64,320]{2,1,0:T(8,128)} %copy-done.36), kind=kLoop, calls=%fused_computation.409 | loop fusion | bytes 196608
  87.1 1.5 %constant_dynamic-update-slice_fusion = f32[6,64,320]{2,1,0:T(8,128)} fusion(f32[6,64,320]{2,1,0:T(8,128)} %constant_dynamic-update-slice_fusion.1, f32[1,64,320]{2,1,0:T(8,128)} %copy-done.46), kind=kLoop, calls=%fused_computation.408 | loop fusion | bytes 196608 | tf_op jit(solution)/shard_map/concatenate | solution.py:56
  88.6 2.2 %all-to-all-done = f32[8,1,16,320]{3,2,1,0:T(8,128)} async-done(((f32[8,1,16,320]{3,2,1,0:T(8,128)}), f32[8,1,16,320]{3,2,1,0:T(8,128)}, u32[]{:S(2)}, u32[]{:S(2)}) %all-to-all-start) | async-done | bytes 163872 | tf_op jit(solution)/shard_map/all_to_all | solution.py:73
  90.8 1.0 fusion.266
  91.8 1.0 slice.1248
  92.8 1.1 fusion.358
  93.9 1.1 fusion.270
  95.1 0.9 fusion.232
  96.1 1.0 fusion.244
  97.2 0.9 fusion.256
  100.9 0.5 fusion.124
  101.4 0.4 convolution_bitcast_fusion
  101.9 1.2 slice_add_fusion
  103.4 3.5 %collective-permute-start.15 = (f32[1,64,320]{2,1,0:T(8,128)S(1)}, f32[1,64,320]{2,1,0:T(8,128)S(1)}, u32[]{:S(2)}, u32[]{:S(2)}) collective-permute-start(f32[1,64,320]{2,1,0:T(8,128)S(1)} %fusion.166), channel_id=1, source_target_pairs={{4,0},{8,4},{12,8},{16,12},{20,16},{24,20},{28,24},{5,1},{9,5},{13... | collective-permute-start | bytes 245768 | tf_op jit(solution)/shard_map/ppermute | solution.py:55
  107.1 2.4 %collective-permute-start.14 = (f32[1,64,320]{2,1,0:T(8,128)S(1)}, f32[1,64,320]{2,1,0:T(8,128)S(1)}, u32[]{:S(2)}, u32[]{:S(2)}) collective-permute-start(f32[1,64,320]{2,1,0:T(8,128)S(1)} %fusion.156), channel_id=1, source_target_pairs={{0,4},{4,8},{8,12},{12,16},{16,20},{20,24},{24,28},{1,5},{5,9},{9,... | collective-permute-start | bytes 245768 | tf_op jit(solution)/shard_map/ppermute | solution.py:54
  110.4 4.1 %collective-permute-done.14 = f32[1,64,320]{2,1,0:T(8,128)S(1)} collective-permute-done((f32[1,64,320]{2,1,0:T(8,128)S(1)}, f32[1,64,320]{2,1,0:T(8,128)S(1)}, u32[]{:S(2)}, u32[]{:S(2)}) %collective-permute-start.14) | collective-permute-done | bytes 81952 | tf_op jit(solution)/shard_map/ppermute | solution.py:54
  114.7 3.8 %collective-permute-start.17 = (f32[1,64,320]{2,1,0:T(8,128)S(1)}, f32[1,64,320]{2,1,0:T(8,128)S(1)}, u32[]{:S(2)}, u32[]{:S(2)}) collective-permute-start(f32[1,64,320]{2,1,0:T(8,128)S(1)} %fusion.146), channel_id=1, source_target_pairs={{4,0},{8,4},{12,8},{16,12},{20,16},{24,20},{28,24},{5,1},{9,5},{13... | collective-permute-start | bytes 245768 | tf_op jit(solution)/shard_map/ppermute | solution.py:55
  118.6 2.0 %collective-permute-start.16 = (f32[1,64,320]{2,1,0:T(8,128)S(1)}, f32[1,64,320]{2,1,0:T(8,128)S(1)}, u32[]{:S(2)}, u32[]{:S(2)}) collective-permute-start(f32[1,64,320]{2,1,0:T(8,128)S(1)} %fusion.136), channel_id=1, source_target_pairs={{0,4},{4,8},{8,12},{12,16},{16,20},{20,24},{24,28},{1,5},{5,9},{9,... | collective-permute-start | bytes 245768 | tf_op jit(solution)/shard_map/ppermute | solution.py:54
  121.2 4.9 %collective-permute-done.16 = f32[1,64,320]{2,1,0:T(8,128)S(1)} collective-permute-done((f32[1,64,320]{2,1,0:T(8,128)S(1)}, f32[1,64,320]{2,1,0:T(8,128)S(1)}, u32[]{:S(2)}, u32[]{:S(2)}) %collective-permute-start.16) | collective-permute-done | bytes 81952 | tf_op jit(solution)/shard_map/ppermute | solution.py:54
  126.2 1.6 %fusion.41 = (f32[4,64,256]{2,1,0:T(8,128)}, f32[4,64,256]{2,1,0:T(8,128)}) fusion(f32[4,63,320]{2,1,0:T(8,128)S(1)} %fusion.8, f32[4,63,320]{2,1,0:T(8,128)S(1)} %get-tuple-element.51, f32[4,64,320]{2,1,0:T(8,128)S(1)} %copy-done.41, f32[4,64,319]{2,1,0:T(8,128)S(1)} %get-tuple-element.53, f32[4,64,320]{2,1,0:T(8,128)S(1)} %get-tuple-element.21, ...), kind=kLoop, calls=%fused_computation.87 | loop fusion | flops 655360 | bytes 3395584 | tf_op jit(solution)/shard_map/div | solution.py:237
  (240 shorter events, 13.5 us)
Async XLA Ops:
  2.1 6.5 %copy-start.12 = (f32[4,64,256]{2,1,0:T(8,128)S(1)}, f32[4,64,256]{2,1,0:T(8,128)}, u32[]{:S(2)}) copy-start(f32[4,64,256]{2,1,0:T(8,128)} %param.7) | copy-start | bytes 786436
  2.1 6.5 %copy-start.14 = (f32[4,64,256]{2,1,0:T(8,128)S(1)}, f32[4,64,256]{2,1,0:T(8,128)}, u32[]{:S(2)}) copy-start(f32[4,64,256]{2,1,0:T(8,128)} %param.6) | copy-start | bytes 786436
  2.2 6.5 %copy-start.16 = (f32[4,64,256]{2,1,0:T(8,128)S(1)}, f32[4,64,256]{2,1,0:T(8,128)}, u32[]{:S(2)}) copy-start(f32[4,64,256]{2,1,0:T(8,128)} %param.5) | copy-start | bytes 786436
  2.2 6.5 %copy-start.18 = (f32[4,64,256]{2,1,0:T(8,128)S(1)}, f32[4,64,256]{2,1,0:T(8,128)}, u32[]{:S(2)}) copy-start(f32[4,64,256]{2,1,0:T(8,128)} %param.4) | copy-start | bytes 786436
  2.3 6.1 %collective-permute-start.1 = (f32[4,4,16,128]{3,2,1,0:T(8,128)S(1)}, f32[4,4,16,128]{3,2,1,0:T(8,128)S(1)}, u32[]{:S(2)}, u32[]{:S(2)}) collective-permute-start(f32[4,4,16,128]{3,2,1,0:T(8,128)S(1)} %reshape.91), channel_id=1, source_target_pairs={{1,0},{2,1},{3,2},{0,3},{5,4},{6,5},{7,6},{4,7},{9,8},{10,9},{11,1... | collective-permute-start | bytes 393224 | tf_op jit(solution)/shard_map/ppermute | solution.py:42
  3.5 4.7 %collective-permute-start = (f32[4,4,16,128]{3,2,1,0:T(8,128)S(1)}, f32[4,4,16,128]{3,2,1,0:T(8,128)S(1)}, u32[]{:S(2)}, u32[]{:S(2)}) collective-permute-start(f32[4,4,16,128]{3,2,1,0:T(8,128)S(1)} %reshape.89), channel_id=1, source_target_pairs={{0,1},{1,2},{2,3},{3,0},{4,5},{5,6},{6,7},{7,4},{8,9},{9,10},{10,1... | collective-permute-start | bytes 393224 | tf_op jit(solution)/shard_map/ppermute | solution.py:41
  8.8 32.4 %copy-start.10 = (f32[1,64,320]{2,1,0:T(8,128)}, f32[1,64,320]{2,1,0:T(8,128)S(1)}, u32[]{:S(2)}) copy-start(f32[1,64,320]{2,1,0:T(8,128)S(1)} %get-tuple-element.25) | copy-start | bytes 245764
  8.8 40.6 %copy-start.8 = (f32[1,64,320]{2,1,0:T(8,128)}, f32[1,64,320]{2,1,0:T(8,128)S(1)}, u32[]{:S(2)}) copy-start(f32[1,64,320]{2,1,0:T(8,128)S(1)} %get-tuple-element.24) | copy-start | bytes 245764
  10.6 7.7 %copy-start.51 = (s32[320]{0:T(512)S(1)}, s32[320]{0:T(512)}, u32[]{:S(2)}) copy-start(s32[320]{0:T(512)} %get-tuple-element.136) | copy-start | bytes 3844
  10.6 7.7 %copy-start.53 = (s32[320]{0:T(512)S(1)}, s32[320]{0:T(512)}, u32[]{:S(2)}) copy-start(s32[320]{0:T(512)} %get-tuple-element.137) | copy-start | bytes 3844
  10.7 7.7 %copy-start.59 = (pred[320]{0:T(512)(128)(4,1)S(1)}, pred[320]{0:T(512)(128)(4,1)}, u32[]{:S(2)}) copy-start(pred[320]{0:T(512)(128)(4,1)} %fusion.308) | copy-start | bytes 964
  10.7 8.2 %copy-start.47 = (s32[64]{0:T(128)S(1)}, s32[64]{0:T(128)}, u32[]{:S(2)}) copy-start(s32[64]{0:T(128)} %get-tuple-element.138) | copy-start | bytes 772
  10.7 8.2 %copy-start.49 = (s32[64]{0:T(128)S(1)}, s32[64]{0:T(128)}, u32[]{:S(2)}) copy-start(s32[64]{0:T(128)} %get-tuple-element.139) | copy-start | bytes 772
  11.6 14.9 %collective-permute-start.2 = (f32[1,2,64,320]{3,2,1,0:T(8,128)S(1)}, f32[1,2,64,320]{3,2,1,0:T(8,128)S(1)}, u32[]{:S(2)}, u32[]{:S(2)}) collective-permute-start(f32[1,2,64,320]{3,2,1,0:T(8,128)S(1)} %get-tuple-element.32), channel_id=1, source_target_pairs={{0,4},{4,8},{8,12},{12,16},{16,20},{20,24},{24,28},{1,5},{5,9},{9,... | collective-permute-start | bytes 491528 | tf_op jit(solution)/shard_map/ppermute | solution.py:54
  15.0 11.5 %collective-permute-start.3 = (f32[1,2,64,320]{3,2,1,0:T(8,128)S(1)}, f32[1,2,64,320]{3,2,1,0:T(8,128)S(1)}, u32[]{:S(2)}, u32[]{:S(2)}) collective-permute-start(f32[1,2,64,320]{3,2,1,0:T(8,128)S(1)} %get-tuple-element.33), channel_id=1, source_target_pairs={{4,0},{8,4},{12,8},{16,12},{20,16},{24,20},{28,24},{5,1},{9,5},{13... | collective-permute-start | bytes 491528 | tf_op jit(solution)/shard_map/ppermute | solution.py:55
  19.0 38.9 %copy-start.34 = (f32[2,32,160]{2,1,0:T(8,128)}, f32[2,32,160]{2,1,0:T(8,128)S(1)}, u32[]{:S(2)}) copy-start(f32[2,32,160]{2,1,0:T(8,128)S(1)} %get-tuple-element.133) | copy-start | bytes 122884
  19.0 5.6 %copy-start.55 = (s32[160]{0:T(256)S(1)}, s32[160]{0:T(256)}, u32[]{:S(2)}) copy-start(s32[160]{0:T(256)} %get-tuple-element.140) | copy-start | bytes 1924
  19.1 5.6 %copy-start.57 = (s32[160]{0:T(256)S(1)}, s32[160]{0:T(256)}, u32[]{:S(2)}) copy-start(s32[160]{0:T(256)} %get-tuple-element.141) | copy-start | bytes 1924
  19.1 5.6 %copy-start.64 = (pred[160]{0:T(512)(128)(4,1)S(1)}, pred[160]{0:T(512)(128)(4,1)}, u32[]{:S(2)}) copy-start(pred[160]{0:T(512)(128)(4,1)} %compare_and_fusion) | copy-start | bytes 484
  19.1 57.9 %collective-permute-start.12 = (f32[1,32,160]{2,1,0:T(8,128)S(1)}, f32[1,32,160]{2,1,0:T(8,128)S(1)}, u32[]{:S(2)}, u32[]{:S(2)}) collective-permute-start(f32[1,32,160]{2,1,0:T(8,128)S(1)} %get-tuple-element.126), channel_id=1, source_target_pairs={{0,12},{4,16},{8,20},{12,24},{16,28},{1,13},{5,17},{9,21},{13,25},... | collective-permute-start | bytes 61448 | tf_op jit(solution)/shard_map/ppermute | solution.py:65
  22.6 54.3 %collective-permute-start.13 = (f32[1,32,160]{2,1,0:T(8,128)S(1)}, f32[1,32,160]{2,1,0:T(8,128)S(1)}, u32[]{:S(2)}, u32[]{:S(2)}) collective-permute-start(f32[1,32,160]{2,1,0:T(8,128)S(1)} %get-tuple-element.127), channel_id=1, source_target_pairs={{12,0},{16,4},{20,8},{24,12},{28,16},{13,1},{17,5},{21,9},{25,13},... | collective-permute-start | bytes 61448 | tf_op jit(solution)/shard_map/ppermute | solution.py:66
  24.7 33.2 %copy-start.42 = (f32[2,32,160]{2,1,0:T(8,128)}, f32[2,32,160]{2,1,0:T(8,128)S(1)}, u32[]{:S(2)}) copy-start(f32[2,32,160]{2,1,0:T(8,128)S(1)} %get-tuple-element.129) | copy-start | bytes 122884
  25.9 32.0 %copy-start.44 = (f32[2,32,160]{2,1,0:T(8,128)}, f32[2,32,160]{2,1,0:T(8,128)S(1)}, u32[]{:S(2)}) copy-start(f32[2,32,160]{2,1,0:T(8,128)S(1)} %get-tuple-element.131) | copy-start | bytes 122884
  26.6 1.3 %copy-start.13 = (f32[4,64,256]{2,1,0:T(8,128)S(1)}, f32[4,64,256]{2,1,0:T(8,128)}, u32[]{:S(2)}) copy-start(f32[4,64,256]{2,1,0:T(8,128)} %param.7) | copy-start | bytes 786436
  26.6 1.5 %copy-start.15 = (f32[4,64,256]{2,1,0:T(8,128)S(1)}, f32[4,64,256]{2,1,0:T(8,128)}, u32[]{:S(2)}) copy-start(f32[4,64,256]{2,1,0:T(8,128)} %param.6) | copy-start | bytes 786436
  26.6 1.5 %copy-start.17 = (f32[4,64,256]{2,1,0:T(8,128)S(1)}, f32[4,64,256]{2,1,0:T(8,128)}, u32[]{:S(2)}) copy-start(f32[4,64,256]{2,1,0:T(8,128)} %param.5) | copy-start | bytes 786436
  26.9 25.3 %copy-start.4 = (f32[4,64,320]{2,1,0:T(8,128)}, f32[4,64,320]{2,1,0:T(8,128)S(1)}, u32[]{:S(2)}) copy-start(f32[4,64,320]{2,1,0:T(8,128)S(1)} %get-tuple-element.19) | copy-start | bytes 983044
  28.3 21.2 %collective-permute-start.6 = (f32[1,64,320]{2,1,0:T(8,128)S(1)}, f32[1,64,320]{2,1,0:T(8,128)S(1)}, u32[]{:S(2)}, u32[]{:S(2)}) collective-permute-start(f32[1,64,320]{2,1,0:T(8,128)S(1)} %fusion.209), channel_id=1, source_target_pairs={{0,4},{4,8},{8,12},{12,16},{16,20},{20,24},{24,28},{1,5},{5,9},{9,... | collective-permute-start | bytes 245768 | tf_op jit(solution)/shard_map/ppermute | solution.py:54
  34.0 7.3 %collective-permute-start.4 = (f32[1,64,320]{2,1,0:T(8,128)S(1)}, f32[1,64,320]{2,1,0:T(8,128)S(1)}, u32[]{:S(2)}, u32[]{:S(2)}) collective-permute-start(f32[1,64,320]{2,1,0:T(8,128)S(1)} %fusion.187), channel_id=1, source_target_pairs={{4,0},{8,4},{12,8},{16,12},{20,16},{24,20},{28,24},{5,1},{9,5},{13... | collective-permute-start | bytes 245768 | tf_op jit(solution)/shard_map/ppermute | solution.py:55
  41.4 15.3 %copy-start.36 = (f32[1,64,320]{2,1,0:T(8,128)}, f32[1,64,320]{2,1,0:T(8,128)S(1)}, u32[]{:S(2)}) copy-start(f32[1,64,320]{2,1,0:T(8,128)S(1)} %fusion.198) | copy-start | bytes 245764
  41.4 7.4 %collective-permute-start.5 = (f32[1,64,320]{2,1,0:T(8,128)S(1)}, f32[1,64,320]{2,1,0:T(8,128)S(1)}, u32[]{:S(2)}, u32[]{:S(2)}) collective-permute-start(f32[1,64,320]{2,1,0:T(8,128)S(1)} %fusion.198), channel_id=1, source_target_pairs={{0,4},{4,8},{8,12},{12,16},{16,20},{20,24},{24,28},{1,5},{5,9},{9,... | collective-permute-start | bytes 245768 | tf_op jit(solution)/shard_map/ppermute | solution.py:54
  50.2 6.5 %collective-permute-start.7 = (f32[1,64,320]{2,1,0:T(8,128)S(1)}, f32[1,64,320]{2,1,0:T(8,128)S(1)}, u32[]{:S(2)}, u32[]{:S(2)}) collective-permute-start(f32[1,64,320]{2,1,0:T(8,128)S(1)} %get-tuple-element.18), channel_id=1, source_target_pairs={{4,0},{8,4},{12,8},{16,12},{20,16},{24,20},{28,24},{5,1},{9,5},{13... | collective-permute-start | bytes 245768 | tf_op jit(solution)/shard_map/ppermute | solution.py:55
  56.7 20.0 %copy-start.46 = (f32[1,64,320]{2,1,0:T(8,128)}, f32[1,64,320]{2,1,0:T(8,128)S(1)}, u32[]{:S(2)}) copy-start(f32[1,64,320]{2,1,0:T(8,128)S(1)} %collective-permute-done.7) | copy-start | bytes 245764
  57.9 20.7 %copy-start.32 = (f32[2,32,160]{2,1,0:T(8,128)}, f32[2,32,160]{2,1,0:T(8,128)S(1)}, u32[]{:S(2)}) copy-start(f32[2,32,160]{2,1,0:T(8,128)S(1)} %fusion.3) | copy-start | bytes 122884
  58.1 10.9 %collective-permute-start.8 = (f32[2,32,640]{2,1,0:T(8,128)S(1)}, f32[2,32,640]{2,1,0:T(8,128)S(1)}, u32[]{:S(2)}, u32[]{:S(2)}) collective-permute-start(f32[2,32,640]{2,1,0:T(8,128)S(1)} %pad_maximum_fusion.12), channel_id=1, source_target_pairs={{0,8},{4,12},{8,16},{12,20},{16,24},{20,28},{1,9},{5,13},{9,17},{1... | collective-permute-start | bytes 491528 | tf_op jit(solution)/shard_map/ppermute | solution.py:54
  61.7 9.3 %collective-permute-start.9 = (f32[2,32,640]{2,1,0:T(8,128)S(1)}, f32[2,32,640]{2,1,0:T(8,128)S(1)}, u32[]{:S(2)}, u32[]{:S(2)}) collective-permute-start(f32[2,32,640]{2,1,0:T(8,128)S(1)} %pad_maximum_fusion.12), channel_id=1, source_target_pairs={{0,4},{4,8},{8,12},{12,16},{16,20},{20,24},{24,28},{1,5},{5,9},{9,... | collective-permute-start | bytes 491528 | tf_op jit(solution)/shard_map/ppermute | solution.py:54
  66.6 9.6 %collective-permute-start.11 = (f32[2,32,640]{2,1,0:T(8,128)S(1)}, f32[2,32,640]{2,1,0:T(8,128)S(1)}, u32[]{:S(2)}, u32[]{:S(2)}) collective-permute-start(f32[2,32,640]{2,1,0:T(8,128)S(1)} %pad_maximum_fusion.12), channel_id=1, source_target_pairs={{8,0},{12,4},{16,8},{20,12},{24,16},{28,20},{9,1},{13,5},{17,9},{2... | collective-permute-start | bytes 491528 | tf_op jit(solution)/shard_map/ppermute | solution.py:55
  69.0 7.2 %collective-permute-start.10 = (f32[2,32,640]{2,1,0:T(8,128)S(1)}, f32[2,32,640]{2,1,0:T(8,128)S(1)}, u32[]{:S(2)}, u32[]{:S(2)}) collective-permute-start(f32[2,32,640]{2,1,0:T(8,128)S(1)} %pad_maximum_fusion.12), channel_id=1, source_target_pairs={{4,0},{8,4},{12,8},{16,12},{20,16},{24,20},{28,24},{5,1},{9,5},{13... | collective-permute-start | bytes 491528 | tf_op jit(solution)/shard_map/ppermute | solution.py:55
  71.0 5.8 %copy-start.37 = (f32[2,32,640]{2,1,0:T(8,128)}, f32[2,32,640]{2,1,0:T(8,128)S(1)}, u32[]{:S(2)}) copy-start(f32[2,32,640]{2,1,0:T(8,128)S(1)} %collective-permute-done.9) | copy-start | bytes 491524
  76.8 1.8 %copy-start.6 = (f32[10,31,160]{2,1,0:T(8,128)}, f32[10,31,160]{2,1,0:T(8,128)S(1)}, u32[]{:S(2)}) copy-start(f32[10,31,160]{2,1,0:T(8,128)S(1)} %fusion.28) | copy-start | bytes 595204
  77.3 1.3 copy-start.22
  77.3 1.3 copy-start.24
  80.4 10.4 %all-to-all-start = ((f32[8,1,16,320]{3,2,1,0:T(8,128)}), f32[8,1,16,320]{3,2,1,0:T(8,128)}, u32[]{:S(2)}, u32[]{:S(2)}) async-start(f32[8,1,16,320]{3,2,1,0:T(8,128)} %broadcast_in_dim.20), calls=%async_computation | async-start | bytes 393216 | tf_op jit(solution)/shard_map/all_to_all | solution.py:73
  95.1 3.1 %copy-start.56 = (s32[160]{0:T(256)S(1)}, s32[160]{0:T(256)}, u32[]{:S(2)}) copy-start(s32[160]{0:T(256)} %get-tuple-element.140) | copy-start | bytes 1924
  95.1 3.1 %copy-start.58 = (s32[160]{0:T(256)S(1)}, s32[160]{0:T(256)}, u32[]{:S(2)}) copy-start(s32[160]{0:T(256)} %get-tuple-element.141) | copy-start | bytes 1924
  95.1 3.1 %copy-start.65 = (pred[160]{0:T(512)(128)(4,1)S(1)}, pred[160]{0:T(512)(128)(4,1)}, u32[]{:S(2)}) copy-start(pred[160]{0:T(512)(128)(4,1)} %compare_and_fusion) | copy-start | bytes 484
  96.1 2.8 %copy-start.21 = (f32[8,32,160]{2,1,0:T(8,128)S(1)}, f32[8,32,160]{2,1,0:T(8,128)}, u32[]{:S(2)}) copy-start(f32[8,32,160]{2,1,0:T(8,128)} %copy-done.20) | copy-start | bytes 491524
  98.6 1.3 %copy-start.29 = (f32[10,32,160]{2,1,0:T(8,128)S(1)}, f32[10,32,160]{2,1,0:T(8,128)}, u32[]{:S(2)}) copy-start(f32[10,32,160]{2,1,0:T(8,128)} %copy-done.28) | copy-start | bytes 614404
  98.6 1.4 %copy-start.31 = (f32[10,32,160]{2,1,0:T(8,128)S(1)}, f32[10,32,160]{2,1,0:T(8,128)}, u32[]{:S(2)}) copy-start(f32[10,32,160]{2,1,0:T(8,128)} %copy-done.30) | copy-start | bytes 614404
  98.6 1.4 %copy-start.33 = (f32[2,32,160]{2,1,0:T(8,128)S(1)}, f32[2,32,160]{2,1,0:T(8,128)}, u32[]{:S(2)}) copy-start(f32[2,32,160]{2,1,0:T(8,128)} %copy-done.32) | copy-start | bytes 122884
  98.6 1.4 %copy-start.35 = (f32[2,32,160]{2,1,0:T(8,128)S(1)}, f32[2,32,160]{2,1,0:T(8,128)}, u32[]{:S(2)}) copy-start(f32[2,32,160]{2,1,0:T(8,128)} %copy-done.34) | copy-start | bytes 122884
  98.6 1.5 %copy-start.38 = (f32[2,32,640]{2,1,0:T(8,128)S(1)}, f32[2,32,640]{2,1,0:T(8,128)}, u32[]{:S(2)}) copy-start(f32[2,32,640]{2,1,0:T(8,128)} %copy-done.37) | copy-start | bytes 491524
  98.6 1.5 %copy-start.40 = (f32[2,32,640]{2,1,0:T(8,128)S(1)}, f32[2,32,640]{2,1,0:T(8,128)}, u32[]{:S(2)}) copy-start(f32[2,32,640]{2,1,0:T(8,128)} %copy-done.39) | copy-start | bytes 491524
  98.6 1.5 %copy-start.43 = (f32[2,32,160]{2,1,0:T(8,128)S(1)}, f32[2,32,160]{2,1,0:T(8,128)}, u32[]{:S(2)}) copy-start(f32[2,32,160]{2,1,0:T(8,128)} %copy-done.42) | copy-start | bytes 122884
  98.6 1.5 %copy-start.45 = (f32[2,32,160]{2,1,0:T(8,128)S(1)}, f32[2,32,160]{2,1,0:T(8,128)}, u32[]{:S(2)}) copy-start(f32[2,32,160]{2,1,0:T(8,128)} %copy-done.44) | copy-start | bytes 122884
  98.7 1.5 %copy-start.61 = (pred[6]{0:T(512)(128)(4,1)S(1)}, pred[6]{0:T(512)(128)(4,1)}, u32[]{:S(2)}) copy-start(pred[6]{0:T(512)(128)(4,1)} %compare_and_fusion.3) | copy-start | bytes 22
  101.8 1.4 %copy-start.5 = (f32[4,64,320]{2,1,0:T(8,128)S(1)}, f32[4,64,320]{2,1,0:T(8,128)}, u32[]{:S(2)}) copy-start(f32[4,64,320]{2,1,0:T(8,128)} %copy-done.4) | copy-start | bytes 983044
  101.9 1.4 %copy-start.9 = (f32[1,64,320]{2,1,0:T(8,128)S(1)}, f32[1,64,320]{2,1,0:T(8,128)}, u32[]{:S(2)}) copy-start(f32[1,64,320]{2,1,0:T(8,128)} %copy-done.8) | copy-start | bytes 245764
  103.2 3.8 %copy-start.11 = (f32[1,64,320]{2,1,0:T(8,128)S(1)}, f32[1,64,320]{2,1,0:T(8,128)}, u32[]{:S(2)}) copy-start(f32[1,64,320]{2,1,0:T(8,128)} %copy-done.10) | copy-start | bytes 245764
  103.4 15.1 %collective-permute-start.15 = (f32[1,64,320]{2,1,0:T(8,128)S(1)}, f32[1,64,320]{2,1,0:T(8,128)S(1)}, u32[]{:S(2)}, u32[]{:S(2)}) collective-permute-start(f32[1,64,320]{2,1,0:T(8,128)S(1)} %fusion.166), channel_id=1, source_target_pairs={{4,0},{8,4},{12,8},{16,12},{20,16},{24,20},{28,24},{5,1},{9,5},{13... | collective-permute-start | bytes 245768 | tf_op jit(solution)/shard_map/ppermute | solution.py:55
  107.1 7.4 %collective-permute-start.14 = (f32[1,64,320]{2,1,0:T(8,128)S(1)}, f32[1,64,320]{2,1,0:T(8,128)S(1)}, u32[]{:S(2)}, u32[]{:S(2)}) collective-permute-start(f32[1,64,320]{2,1,0:T(8,128)S(1)} %fusion.156), channel_id=1, source_target_pairs={{0,4},{4,8},{8,12},{12,16},{16,20},{20,24},{24,28},{1,5},{5,9},{9,... | collective-permute-start | bytes 245768 | tf_op jit(solution)/shard_map/ppermute | solution.py:54
  114.7 6.5 %collective-permute-start.17 = (f32[1,64,320]{2,1,0:T(8,128)S(1)}, f32[1,64,320]{2,1,0:T(8,128)S(1)}, u32[]{:S(2)}, u32[]{:S(2)}) collective-permute-start(f32[1,64,320]{2,1,0:T(8,128)S(1)} %fusion.146), channel_id=1, source_target_pairs={{4,0},{8,4},{12,8},{16,12},{20,16},{24,20},{28,24},{5,1},{9,5},{13... | collective-permute-start | bytes 245768 | tf_op jit(solution)/shard_map/ppermute | solution.py:55
  118.6 7.4 %collective-permute-start.16 = (f32[1,64,320]{2,1,0:T(8,128)S(1)}, f32[1,64,320]{2,1,0:T(8,128)S(1)}, u32[]{:S(2)}, u32[]{:S(2)}) collective-permute-start(f32[1,64,320]{2,1,0:T(8,128)S(1)} %fusion.136), channel_id=1, source_target_pairs={{0,4},{4,8},{8,12},{12,16},{16,20},{20,24},{24,28},{1,5},{5,9},{9,... | collective-permute-start | bytes 245768 | tf_op jit(solution)/shard_map/ppermute | solution.py:54
  121.0 5.3 %copy-start.41 = (f32[4,64,320]{2,1,0:T(8,128)S(1)}, f32[4,64,320]{2,1,0:T(8,128)}, u32[]{:S(2)}) copy-start(f32[4,64,320]{2,1,0:T(8,128)} %get-tuple-element.26) | copy-start | bytes 983044
  (21 other events, 19.8 us)

commit v22 on v20

--- a/solution.py
+++ b/solution.py
@@ -185,9 +185,10 @@
     coef_two = [coarsen(part) for part in (wide_alt, wide_inc, wide_raan)]
     coef_three = [coarsen(part) for part in coef_two]
 
-    first = alt_extend(wide[:, 0:2], 1)
-    source_x = first[:, 0]
-    weights_one = make_weights(first[:, 1], wide_inc, wide_raan, 1.0, 0)
+    first = alt_extend(jnp.concatenate([wide[:, 0], wide[:, 1]], axis=-1), 1)
+    lanes = wide.shape[-1]
+    source_x = first[..., :lanes]
+    weights_one = make_weights(first[..., lanes:], wide_inc, wide_raan, 1.0, 0)
 
     density = split_sweep(weights_one, source_x, source_x, 1)
     density = split_sweep(weights_one, alt_extend(density, 1), source_x, 1)

time: 127 us -> 145 us (1.14)
  other arithmetic: 19.4 us -> 23.8 us
  matrix products: 5.56 us -> 9.87 us
  waiting for transfers between devices: 28.8 us -> 32.6 us
  local copies, waits for them, and re-layouts: 14.8 us -> 18.1 us
  starting transfers between devices: 55.1 us -> 56.6 us
    reduce_sum x4 -> x5, other arithmetic: 0.69 us -> 4.42 us  [coarsen(): summed = values.reshape(depth // 2, 2, width, length).sum(axis=1)]
    ppermute x7, waiting for transfers between devices: 14.1 us -> 16.6 us  [alt_extend(): above.append(lax.ppermute(values[:high], 'alt', down))]
    dot_general x8, matrix products: 2.82 us -> 5.15 us  [coarsen(): summed = jnp.matmul(summed, pairing(length), precision=HIGH)]
    slice x20, local copies, waits for them, and re-layouts: 2.05 us -> 4.04 us  [lane_shifts(): left = jnp.concatenate([zero, values[..., :-1]], axis=-1)]
    dot_general x8, matrix products: 1.24 us -> 3.22 us  [coarsen(): summed = jnp.matmul(pairing(width).T[None], summed, precision=HIGH)]
    ppermute x1, starting transfers between devices: 3.54 us -> 5.03 us  [alt_row(): below = lax.ppermute(values[index:index + 1], 'alt', up)]
    unnamed x138 -> x180, local copies, waits for them, and re-layouts: 6.54 us -> 6.97 us
  transfers between devices with their start and end apart: 19 -> 19, of which waited for: 9 -> 12; matrix products, arithmetic and copies ran while one was open for 15% -> 17% of each run, Pallas kernels for 0% -> 0%
where the time goes in v22:
time: 145 us; the launch traced here: 143 us
  starting transfers between devices  56.6 us (39%)
  waiting for transfers between devices  32.6 us (22%)
  other arithmetic  23.8 us (16%)
  local copies, waits for them, and re-layouts  18.1 us (12%)
  matrix products  9.87 us (7%)
  between operations  2.46 us (2%)
    ppermute x7, starting transfers between devices, alt_extend(): below.insert(0, lax.ppermute(values[low:], 'alt', up))  26.4 us
    ppermute x7, starting transfers between devices, alt_extend(): above.append(lax.ppermute(values[:high], 'alt', down))  18.1 us
    ppermute x7, waiting for transfers between devices, alt_extend(): above.append(lax.ppermute(values[:high], 'alt', down))  16.6 us
    ppermute x7, waiting for transfers between devices, alt_extend(): below.insert(0, lax.ppermute(values[low:], 'alt', up))  12.6 us
    unnamed x180, local copies, waits for them, and re-layouts  6.97 us
    dot_general x8, matrix products, coarsen(): summed = jnp.matmul(summed, pairing(length), precision=HIGH)  5.15 us
    ppermute x1, starting transfers between devices, alt_row(): below = lax.ppermute(values[index:index + 1], 'alt', up)  5.03 us
    all_to_all x1, starting transfers between devices, spread_gather(): every = lax.all_to_all(copies, 'alt', 0, 0)  4.65 us
  transfers between devices with their start and end apart: 19, of which 12 were waited for; matrix products, arithmetic and copies ran while one was open for 17% of the time, Pallas kernels for 0%

profile of v22, /device:TPU:8, one launch (start us, length us, event | category | flops | bytes accessed | tf_op | source)
XLA Modules:
  0.0 143.4 jit_solution(10663255206643062508)
XLA Ops:
  0.6 1.3 pad_maximum_fusion.1
  2.4 1.0 collective-permute-start.1
  4.1 0.5 fusion.300
  4.7 0.6 iota_shift-right-logical_fusion.3
  5.3 0.5 iota_shift-right-logical_fusion.1
  5.8 0.6 compare_and_fusion.2
  6.4 0.5 compare_and_fusion.3
  7.0 0.6 iota_shift-right-logical_fusion
  7.6 0.7 collective-permute-done
  8.8 1.6 %pad_maximum_fusion = f32[4,4,64,320]{3,2,0,1:T(8,128)S(1)} fusion(f32[4,1,64,256]{3,2,0,1:T(8,128)S(1)} %bitcast.211, f32[4,1,64,256]{3,2,0,1:T(8,128)S(1)} %bitcast.216, f32[4,1,64,256]{3,2,0,1:T(8,128)S(1)} %bitcast.221, f32[4,1,64,256]{3,2,0,1:T(8,128)} %bitcast.225, f32[4,4,64,32]{3,2,1,0:T(8,128)S(1)} %reshape.76, f32[4,4,64,32]{3,2,1,0:T(8,128)S(1)} %reshape.78), kind=kLoop, calls=%fused_computation | loop fusion | flops 1638400 | bytes 2621440 | tf_op jit(solution)/shard_map/concatenate | solution.py:43
  10.5 1.2 fusion.328
  11.8 0.7 fusion.360
  12.5 0.7 fusion.363
  13.2 0.8 fusion.353
  14.1 1.0 reduce_sum.73
  15.6 0.8 fusion.374
  16.4 0.7 fusion.371
  17.0 5.0 %collective-permute-start.12 = (f32[1,32,160]{2,1,0:T(8,128)}, f32[1,32,160]{2,1,0:T(8,128)}, u32[]{:S(2)}, u32[]{:S(2)}) collective-permute-start(f32[1,32,160]{2,1,0:T(8,128)} %get-tuple-element.126), channel_id=1, source_target_pairs={{0,12},{4,16},{8,20},{12,24},{16,28},{1,13},{5,17},{9,21},{13,25},... | collective-permute-start | bytes 61448 | tf_op jit(solution)/shard_map/ppermute | solution.py:65
  22.1 1.3 collective-permute-start.13
  23.3 1.0 reduce_sum.75
  24.4 1.7 %reduce_sum.74 = f32[2,64,320]{2,1,0:T(8,128)} reduce(f32[2,2,64,320]{3,2,1,0:T(8,128)} %bitcast.230, f32[]{:T(128)} %constant.144.clone.1), dimensions={1}, to_apply=%region_2.3 | reduce | flops 40960 | bytes 491524 | tf_op jit(solution)/shard_map/reduce_sum | solution.py:21
  26.1 1.4 fusion.314
  27.9 0.9 fusion.372
  28.8 0.9 fusion.373
  29.7 1.1 fusion.206
  30.8 0.9 fusion.205
  31.9 4.6 %collective-permute-start.2 = (f32[1,64,640]{2,1,0:T(8,128)S(1)}, f32[1,64,640]{2,1,0:T(8,128)S(1)}, u32[]{:S(2)}, u32[]{:S(2)}) collective-permute-start(f32[1,64,640]{2,1,0:T(8,128)S(1)} %get-tuple-element.37), channel_id=1, source_target_pairs={{0,4},{4,8},{8,12},{12,16},{16,20},{20,24},{24,28},{1,5},{5,9},{9,... | collective-permute-start | bytes 491528 | tf_op jit(solution)/shard_map/ppermute | solution.py:54
  36.5 2.3 %collective-permute-start.3 = (f32[1,64,640]{2,1,0:T(8,128)S(1)}, f32[1,64,640]{2,1,0:T(8,128)S(1)}, u32[]{:S(2)}, u32[]{:S(2)}) collective-permute-start(f32[1,64,640]{2,1,0:T(8,128)S(1)} %get-tuple-element.38), channel_id=1, source_target_pairs={{4,0},{8,4},{12,8},{16,12},{20,16},{24,20},{28,24},{5,1},{9,5},{13... | collective-permute-start | bytes 491528 | tf_op jit(solution)/shard_map/ppermute | solution.py:55
  39.9 0.7 collective-permute-done.2
  40.6 3.7 %collective-permute-done.3 = f32[1,64,640]{2,1,0:T(8,128)S(1)} collective-permute-done((f32[1,64,640]{2,1,0:T(8,128)S(1)}, f32[1,64,640]{2,1,0:T(8,128)S(1)}, u32[]{:S(2)}, u32[]{:S(2)}) %collective-permute-start.3) | collective-permute-done | bytes 163872 | tf_op jit(solution)/shard_map/ppermute | solution.py:55
  44.4 1.5 %add_add_fusion = (f32[4,64,320]{2,1,0:T(8,128)S(1)}, f32[4,64,320]{2,1,0:T(8,128)S(1)}, f32[4,64,320]{2,1,0:T(8,128)S(1)}, f32[4,64,320]{2,1,0:T(8,128)S(1)}, f32[4,64,320]{2,1,0:T(8,128)S(1)}) fusion(f32[4,63,320]{2,1,0:T(8,128)S(1)} %fusion.8, f32[4,64,320]{2,1,0:T(8,128)S(1)} %copy-done.27, f32[4,64,320]{2,1,0:T(8,128)} %copy-done.8, ...), kind=kLoop, calls=%fused_computation.49 | loop fusion | flops 1474560 | bytes 3924992 | tf_op jit(solution)/shard_map/add | solution.py:100
  46.1 4.8 %collective-permute-start.6 = (f32[1,64,320]{2,1,0:T(8,128)S(1)}, f32[1,64,320]{2,1,0:T(8,128)S(1)}, u32[]{:S(2)}, u32[]{:S(2)}) collective-permute-start(f32[1,64,320]{2,1,0:T(8,128)S(1)} %fusion.201), channel_id=1, source_target_pairs={{0,4},{4,8},{8,12},{12,16},{16,20},{20,24},{24,28},{1,5},{5,9},{9,... | collective-permute-start | bytes 245768 | tf_op jit(solution)/shard_map/ppermute | solution.py:54
  52.2 2.1 %collective-permute-start.4 = (f32[1,64,320]{2,1,0:T(8,128)S(1)}, f32[1,64,320]{2,1,0:T(8,128)S(1)}, u32[]{:S(2)}, u32[]{:S(2)}) collective-permute-start(f32[1,64,320]{2,1,0:T(8,128)S(1)} %fusion.181), channel_id=1, source_target_pairs={{4,0},{8,4},{12,8},{16,12},{20,16},{24,20},{28,24},{5,1},{9,5},{13... | collective-permute-start | bytes 245768 | tf_op jit(solution)/shard_map/ppermute | solution.py:55
  54.4 4.3 %collective-permute-done.4 = f32[1,64,320]{2,1,0:T(8,128)S(1)} collective-permute-done((f32[1,64,320]{2,1,0:T(8,128)S(1)}, f32[1,64,320]{2,1,0:T(8,128)S(1)}, u32[]{:S(2)}, u32[]{:S(2)}) %collective-permute-start.4) | collective-permute-done | bytes 81952 | tf_op jit(solution)/shard_map/ppermute | solution.py:55
  58.9 4.6 %collective-permute-start.5 = (f32[1,64,320]{2,1,0:T(8,128)S(1)}, f32[1,64,320]{2,1,0:T(8,128)S(1)}, u32[]{:S(2)}, u32[]{:S(2)}) collective-permute-start(f32[1,64,320]{2,1,0:T(8,128)S(1)} %fusion.191), channel_id=1, source_target_pairs={{0,4},{4,8},{8,12},{12,16},{16,20},{20,24},{24,28},{1,5},{5,9},{9,... | collective-permute-start | bytes 245768 | tf_op jit(solution)/shard_map/ppermute | solution.py:54
  63.5 2.8 %collective-permute-done.5 = f32[1,64,320]{2,1,0:T(8,128)S(1)} collective-permute-done((f32[1,64,320]{2,1,0:T(8,128)S(1)}, f32[1,64,320]{2,1,0:T(8,128)S(1)}, u32[]{:S(2)}, u32[]{:S(2)}) %collective-permute-start.5) | collective-permute-done | bytes 81952 | tf_op jit(solution)/shard_map/ppermute | solution.py:54
  66.4 2.1 %collective-permute-start.7 = (f32[1,64,320]{2,1,0:T(8,128)S(1)}, f32[1,64,320]{2,1,0:T(8,128)S(1)}, u32[]{:S(2)}, u32[]{:S(2)}) collective-permute-start(f32[1,64,320]{2,1,0:T(8,128)S(1)} %get-tuple-element.18), channel_id=1, source_target_pairs={{4,0},{8,4},{12,8},{16,12},{20,16},{24,20},{28,24},{5,1},{9,5},{13... | collective-permute-start | bytes 245768 | tf_op jit(solution)/shard_map/ppermute | solution.py:55
  69.1 0.5 copy-done.54
  69.6 3.3 %collective-permute-done.7 = f32[1,64,320]{2,1,0:T(8,128)S(1)} collective-permute-done((f32[1,64,320]{2,1,0:T(8,128)S(1)}, f32[1,64,320]{2,1,0:T(8,128)S(1)}, u32[]{:S(2)}, u32[]{:S(2)}) %collective-permute-start.7) | collective-permute-done | bytes 81952 | tf_op jit(solution)/shard_map/ppermute | solution.py:55
  74.5 3.5 %collective-permute-start.8 = (f32[2,32,640]{2,1,0:T(8,128)S(1)}, f32[2,32,640]{2,1,0:T(8,128)S(1)}, u32[]{:S(2)}, u32[]{:S(2)}) collective-permute-start(f32[2,32,640]{2,1,0:T(8,128)S(1)} %pad_maximum_fusion.16), channel_id=1, source_target_pairs={{0,8},{4,12},{8,16},{12,20},{16,24},{20,28},{1,9},{5,13},{9,17},{1... | collective-permute-start | bytes 491528 | tf_op jit(solution)/shard_map/ppermute | solution.py:54
  78.1 4.6 %collective-permute-start.9 = (f32[2,32,640]{2,1,0:T(8,128)S(1)}, f32[2,32,640]{2,1,0:T(8,128)S(1)}, u32[]{:S(2)}, u32[]{:S(2)}) collective-permute-start(f32[2,32,640]{2,1,0:T(8,128)S(1)} %pad_maximum_fusion.16), channel_id=1, source_target_pairs={{0,4},{4,8},{8,12},{12,16},{16,20},{20,24},{24,28},{1,5},{5,9},{9,... | collective-permute-start | bytes 491528 | tf_op jit(solution)/shard_map/ppermute | solution.py:54
  82.8 2.4 %collective-permute-start.11 = (f32[2,32,640]{2,1,0:T(8,128)S(1)}, f32[2,32,640]{2,1,0:T(8,128)S(1)}, u32[]{:S(2)}, u32[]{:S(2)}) collective-permute-start(f32[2,32,640]{2,1,0:T(8,128)S(1)} %pad_maximum_fusion.16), channel_id=1, source_target_pairs={{8,0},{12,4},{16,8},{20,12},{24,16},{28,20},{9,1},{13,5},{17,9},{2... | collective-permute-start | bytes 491528 | tf_op jit(solution)/shard_map/ppermute | solution.py:55
  85.2 1.9 %collective-permute-start.10 = (f32[2,32,640]{2,1,0:T(8,128)S(1)}, f32[2,32,640]{2,1,0:T(8,128)S(1)}, u32[]{:S(2)}, u32[]{:S(2)}) collective-permute-start(f32[2,32,640]{2,1,0:T(8,128)S(1)} %pad_maximum_fusion.16), channel_id=1, source_target_pairs={{4,0},{8,4},{12,8},{16,12},{20,16},{24,20},{28,24},{5,1},{9,5},{13... | collective-permute-start | bytes 491528 | tf_op jit(solution)/shard_map/ppermute | solution.py:55
  87.3 5.1 %collective-permute-done.10 = f32[2,32,640]{2,1,0:T(8,128)S(1)} collective-permute-done((f32[2,32,640]{2,1,0:T(8,128)S(1)}, f32[2,32,640]{2,1,0:T(8,128)S(1)}, u32[]{:S(2)}, u32[]{:S(2)}) %collective-permute-start.10) | collective-permute-done | bytes 163872 | tf_op jit(solution)/shard_map/ppermute | solution.py:55
  92.5 0.6 copy-done.48
  93.7 1.1 fusion.27
  97.1 0.7 broadcast_in_dim.20
  97.9 4.7 %all-to-all-start = ((f32[8,1,4,16,80]{4,3,2,1,0:T(8,128)}), f32[8,1,4,16,80]{4,3,2,1,0:T(8,128)}, u32[]{:S(2)}, u32[]{:S(2)}) async-start(f32[8,1,4,16,80]{4,3,2,1,0:T(8,128)} %broadcast_in_dim.20), calls=%async_computation | async-start | bytes 524288 | tf_op jit(solution)/shard_map/all_to_all | solution.py:73
  103.0 1.5 %constant_dynamic-update-slice_fusion.1 = f32[6,64,320]{2,1,0:T(8,128)} fusion(f32[6,64,320]{2,1,0:T(8,128)} %copy-done.54, f32[1,64,320]{2,1,0:T(8,128)} %copy-done.45), kind=kLoop, calls=%fused_computation.400 | loop fusion | bytes 196608
  104.6 1.5 %constant_dynamic-update-slice_fusion = f32[6,64,320]{2,1,0:T(8,128)} fusion(f32[6,64,320]{2,1,0:T(8,128)} %constant_dynamic-update-slice_fusion.1, f32[1,64,320]{2,1,0:T(8,128)} %copy-done.58), kind=kLoop, calls=%fused_computation.399 | loop fusion | bytes 196608 | tf_op jit(solution)/shard_map/concatenate | solution.py:56
  106.1 2.7 %all-to-all-done = f32[8,1,4,16,80]{4,3,2,1,0:T(8,128)} async-done(((f32[8,1,4,16,80]{4,3,2,1,0:T(8,128)}), f32[8,1,4,16,80]{4,3,2,1,0:T(8,128)}, u32[]{:S(2)}, u32[]{:S(2)}) %all-to-all-start) | async-done | bytes 163872 | tf_op jit(solution)/shard_map/all_to_all | solution.py:73
  108.8 0.9 slice_bitcast_fusion.4
  109.9 1.0 fusion.262
  111.0 0.9 fusion.224
  112.0 1.0 fusion.236
  113.1 0.9 fusion.248
  118.0 0.7 copy-done.5
  118.9 3.4 %collective-permute-start.15 = (f32[1,64,320]{2,1,0:T(8,128)S(1)}, f32[1,64,320]{2,1,0:T(8,128)S(1)}, u32[]{:S(2)}, u32[]{:S(2)}) collective-permute-start(f32[1,64,320]{2,1,0:T(8,128)S(1)} %fusion.160), channel_id=1, source_target_pairs={{4,0},{8,4},{12,8},{16,12},{20,16},{24,20},{28,24},{5,1},{9,5},{13... | collective-permute-start | bytes 245768 | tf_op jit(solution)/shard_map/ppermute | solution.py:55
  122.6 2.5 %collective-permute-start.14 = (f32[1,64,320]{2,1,0:T(8,128)S(1)}, f32[1,64,320]{2,1,0:T(8,128)S(1)}, u32[]{:S(2)}, u32[]{:S(2)}) collective-permute-start(f32[1,64,320]{2,1,0:T(8,128)S(1)} %fusion.150), channel_id=1, source_target_pairs={{0,4},{4,8},{8,12},{12,16},{16,20},{20,24},{24,28},{1,5},{5,9},{9,... | collective-permute-start | bytes 245768 | tf_op jit(solution)/shard_map/ppermute | solution.py:54
  126.0 4.0 %collective-permute-done.14 = f32[1,64,320]{2,1,0:T(8,128)S(1)} collective-permute-done((f32[1,64,320]{2,1,0:T(8,128)S(1)}, f32[1,64,320]{2,1,0:T(8,128)S(1)}, u32[]{:S(2)}, u32[]{:S(2)}) %collective-permute-start.14) | collective-permute-done | bytes 81952 | tf_op jit(solution)/shard_map/ppermute | solution.py:54
  130.1 3.9 %collective-permute-start.17 = (f32[1,64,320]{2,1,0:T(8,128)S(1)}, f32[1,64,320]{2,1,0:T(8,128)S(1)}, u32[]{:S(2)}, u32[]{:S(2)}) collective-permute-start(f32[1,64,320]{2,1,0:T(8,128)S(1)} %fusion.140), channel_id=1, source_target_pairs={{4,0},{8,4},{12,8},{16,12},{20,16},{24,20},{28,24},{5,1},{9,5},{13... | collective-permute-start | bytes 245768 | tf_op jit(solution)/shard_map/ppermute | solution.py:55
  134.2 1.9 %collective-permute-start.16 = (f32[1,64,320]{2,1,0:T(8,128)S(1)}, f32[1,64,320]{2,1,0:T(8,128)S(1)}, u32[]{:S(2)}, u32[]{:S(2)}) collective-permute-start(f32[1,64,320]{2,1,0:T(8,128)S(1)} %fusion.130), channel_id=1, source_target_pairs={{0,4},{4,8},{8,12},{12,16},{16,20},{20,24},{24,28},{1,5},{5,9},{9,... | collective-permute-start | bytes 245768 | tf_op jit(solution)/shard_map/ppermute | solution.py:54
  136.6 5.0 %collective-permute-done.16 = f32[1,64,320]{2,1,0:T(8,128)S(1)} collective-permute-done((f32[1,64,320]{2,1,0:T(8,128)S(1)}, f32[1,64,320]{2,1,0:T(8,128)S(1)}, u32[]{:S(2)}, u32[]{:S(2)}) %collective-permute-start.16) | collective-permute-done | bytes 81952 | tf_op jit(solution)/shard_map/ppermute | solution.py:54
  141.8 1.6 %fusion.35 = (f32[4,64,256]{2,1,0:T(8,128)}, f32[4,64,256]{2,1,0:T(8,128)}) fusion(f32[4,63,320]{2,1,0:T(8,128)S(1)} %fusion.8, f32[4,63,320]{2,1,0:T(8,128)S(1)} %get-tuple-element.52, f32[4,64,320]{2,1,0:T(8,128)S(1)} %copy-done.9, f32[4,64,319]{2,1,0:T(8,128)S(1)} %get-tuple-element.54, f32[4,64,320]{2,1,0:T(8,128)S(1)} %get-tuple-element.23, ...), kind=kLoop, calls=%fused_computation.80 | loop fusion | flops 655360 | bytes 3395584 | tf_op jit(solution)/shard_map/div | solution.py:236
  (287 shorter events, 17.4 us)
Async XLA Ops:
  2.1 6.5 %copy-start.10 = (f32[4,64,256]{2,1,0:T(8,128)S(1)}, f32[4,64,256]{2,1,0:T(8,128)}, u32[]{:S(2)}) copy-start(f32[4,64,256]{2,1,0:T(8,128)} %param.7) | copy-start | bytes 786436
  2.1 6.5 %copy-start.12 = (f32[4,64,256]{2,1,0:T(8,128)S(1)}, f32[4,64,256]{2,1,0:T(8,128)}, u32[]{:S(2)}) copy-start(f32[4,64,256]{2,1,0:T(8,128)} %param.6) | copy-start | bytes 786436
  2.1 6.5 %copy-start.14 = (f32[4,64,256]{2,1,0:T(8,128)S(1)}, f32[4,64,256]{2,1,0:T(8,128)}, u32[]{:S(2)}) copy-start(f32[4,64,256]{2,1,0:T(8,128)} %param.5) | copy-start | bytes 786436
  2.2 6.5 %copy-start.16 = (f32[4,64,256]{2,1,0:T(8,128)S(1)}, f32[4,64,256]{2,1,0:T(8,128)}, u32[]{:S(2)}) copy-start(f32[4,64,256]{2,1,0:T(8,128)} %param.4) | copy-start | bytes 786436
  2.4 6.1 %collective-permute-start.1 = (f32[4,4,16,128]{3,2,1,0:T(8,128)S(1)}, f32[4,4,16,128]{3,2,1,0:T(8,128)S(1)}, u32[]{:S(2)}, u32[]{:S(2)}) collective-permute-start(f32[4,4,16,128]{3,2,1,0:T(8,128)S(1)} %copy.19), channel_id=1, source_target_pairs={{1,0},{2,1},{3,2},{0,3},{5,4},{6,5},{7,6},{4,7},{9,8},{10,9},{11,1... | collective-permute-start | bytes 393224 | tf_op jit(solution)/shard_map/ppermute | solution.py:42
  3.5 4.7 %collective-permute-start = (f32[4,4,16,128]{3,2,1,0:T(8,128)S(1)}, f32[4,4,16,128]{3,2,1,0:T(8,128)S(1)}, u32[]{:S(2)}, u32[]{:S(2)}) collective-permute-start(f32[4,4,16,128]{3,2,1,0:T(8,128)S(1)} %copy.18), channel_id=1, source_target_pairs={{0,1},{1,2},{2,3},{3,0},{4,5},{5,6},{6,7},{7,4},{8,9},{9,10},{10,1... | collective-permute-start | bytes 393224 | tf_op jit(solution)/shard_map/ppermute | solution.py:41
  8.4 2.1 %copy-start = (f32[4,4,64,32]{3,2,1,0:T(8,128)}, f32[4,4,64,32]{3,2,1,0:T(8,128)S(1)}, u32[]{:S(2)}) copy-start(f32[4,4,64,32]{3,2,1,0:T(8,128)S(1)} %reshape.76) | copy-start | bytes 393220
  8.7 1.8 %copy-start.2 = (f32[4,4,64,32]{3,2,1,0:T(8,128)}, f32[4,4,64,32]{3,2,1,0:T(8,128)S(1)}, u32[]{:S(2)}) copy-start(f32[4,4,64,32]{3,2,1,0:T(8,128)S(1)} %reshape.78) | copy-start | bytes 393220
  8.8 3.7 %copy-start.21 = (f32[1,64,320]{2,1,0:T(8,128)}, f32[1,64,320]{2,1,0:T(8,128)S(1)}, u32[]{:S(2)}) copy-start(f32[1,64,320]{2,1,0:T(8,128)S(1)} %get-tuple-element.25) | copy-start | bytes 245764
  8.8 30.5 %copy-start.18 = (f32[1,64,320]{2,1,0:T(8,128)}, f32[1,64,320]{2,1,0:T(8,128)S(1)}, u32[]{:S(2)}) copy-start(f32[1,64,320]{2,1,0:T(8,128)S(1)} %get-tuple-element.24) | copy-start | bytes 245764
  10.5 2.7 %copy-start.28 = (f32[2,64,320]{2,1,0:T(8,128)}, f32[2,64,320]{2,1,0:T(8,128)S(1)}, u32[]{:S(2)}) copy-start(f32[2,64,320]{2,1,0:T(8,128)S(1)} %slice_bitcast_fusion.3) | copy-start | bytes 491524
  11.7 20.0 %copy-start.26 = (f32[4,64,320]{2,1,0:T(8,128)}, f32[4,64,320]{2,1,0:T(8,128)S(1)}, u32[]{:S(2)}) copy-start(f32[4,64,320]{2,1,0:T(8,128)S(1)} %get-tuple-element.28) | copy-start | bytes 983044
  11.7 28.0 %copy-start.8 = (f32[4,64,320]{2,1,0:T(8,128)}, f32[4,64,320]{2,1,0:T(8,128)S(1)}, u32[]{:S(2)}) copy-start(f32[4,64,320]{2,1,0:T(8,128)S(1)} %get-tuple-element.32) | copy-start | bytes 983044
  11.7 3.4 %copy-start.69 = (s32[320]{0:T(512)S(1)}, s32[320]{0:T(512)}, u32[]{:S(2)}) copy-start(s32[320]{0:T(512)} %get-tuple-element.134) | copy-start | bytes 3844
  11.7 3.4 %copy-start.72 = (s32[320]{0:T(512)S(1)}, s32[320]{0:T(512)}, u32[]{:S(2)}) copy-start(s32[320]{0:T(512)} %get-tuple-element.135) | copy-start | bytes 3844
  11.7 3.4 %copy-start.79 = (pred[320]{0:T(512)(128)(4,1)S(1)}, pred[320]{0:T(512)(128)(4,1)}, u32[]{:S(2)}) copy-start(pred[320]{0:T(512)(128)(4,1)} %fusion.300) | copy-start | bytes 964
  11.8 3.8 %copy-start.63 = (s32[64]{0:T(128)S(1)}, s32[64]{0:T(128)}, u32[]{:S(2)}) copy-start(s32[64]{0:T(128)} %get-tuple-element.136) | copy-start | bytes 772
  11.8 3.8 %copy-start.66 = (s32[64]{0:T(128)S(1)}, s32[64]{0:T(128)}, u32[]{:S(2)}) copy-start(s32[64]{0:T(128)} %get-tuple-element.137) | copy-start | bytes 772
  16.4 15.4 %copy-start.42 = (f32[2,32,160]{2,1,0:T(8,128)}, f32[2,32,160]{2,1,0:T(8,128)S(1)}, u32[]{:S(2)}) copy-start(f32[2,32,160]{2,1,0:T(8,128)S(1)} %get-tuple-element.133) | copy-start | bytes 122884
  17.0 76.7 %collective-permute-start.12 = (f32[1,32,160]{2,1,0:T(8,128)}, f32[1,32,160]{2,1,0:T(8,128)}, u32[]{:S(2)}, u32[]{:S(2)}) collective-permute-start(f32[1,32,160]{2,1,0:T(8,128)} %get-tuple-element.126), channel_id=1, source_target_pairs={{0,12},{4,16},{8,20},{12,24},{16,28},{1,13},{5,17},{9,21},{13,25},... | collective-permute-start | bytes 61448 | tf_op jit(solution)/shard_map/ppermute | solution.py:65
  22.1 71.7 %collective-permute-start.13 = (f32[1,32,160]{2,1,0:T(8,128)}, f32[1,32,160]{2,1,0:T(8,128)}, u32[]{:S(2)}, u32[]{:S(2)}) collective-permute-start(f32[1,32,160]{2,1,0:T(8,128)} %get-tuple-element.127), channel_id=1, source_target_pairs={{12,0},{16,4},{20,8},{24,12},{28,16},{13,1},{17,5},{21,9},{25,13},... | collective-permute-start | bytes 61448 | tf_op jit(solution)/shard_map/ppermute | solution.py:66
  28.8 45.5 %copy-start.50 = (f32[2,32,160]{2,1,0:T(8,128)}, f32[2,32,160]{2,1,0:T(8,128)S(1)}, u32[]{:S(2)}) copy-start(f32[2,32,160]{2,1,0:T(8,128)S(1)} %get-tuple-element.129) | copy-start | bytes 122884
  29.7 44.6 %copy-start.52 = (f32[2,32,160]{2,1,0:T(8,128)}, f32[2,32,160]{2,1,0:T(8,128)S(1)}, u32[]{:S(2)}) copy-start(f32[2,32,160]{2,1,0:T(8,128)S(1)} %get-tuple-element.131) | copy-start | bytes 122884
  31.9 7.2 %copy-start.75 = (s32[160]{0:T(256)S(1)}, s32[160]{0:T(256)}, u32[]{:S(2)}) copy-start(s32[160]{0:T(256)} %get-tuple-element.138) | copy-start | bytes 1924
  31.9 7.2 %copy-start.77 = (s32[160]{0:T(256)S(1)}, s32[160]{0:T(256)}, u32[]{:S(2)}) copy-start(s32[160]{0:T(256)} %get-tuple-element.139) | copy-start | bytes 1924
  31.9 7.2 %copy-start.85 = (pred[160]{0:T(512)(128)(4,1)S(1)}, pred[160]{0:T(512)(128)(4,1)}, u32[]{:S(2)}) copy-start(pred[160]{0:T(512)(128)(4,1)} %compare_and_fusion) | copy-start | bytes 484
  31.9 7.5 %copy-start.22 = (f32[1,64,320]{2,1,0:T(8,128)S(1)}, f32[1,64,320]{2,1,0:T(8,128)}, u32[]{:S(2)}) copy-start(f32[1,64,320]{2,1,0:T(8,128)} %copy-done.21) | copy-start | bytes 245764
  31.9 8.7 %collective-permute-start.2 = (f32[1,64,640]{2,1,0:T(8,128)S(1)}, f32[1,64,640]{2,1,0:T(8,128)S(1)}, u32[]{:S(2)}, u32[]{:S(2)}) collective-permute-start(f32[1,64,640]{2,1,0:T(8,128)S(1)} %get-tuple-element.37), channel_id=1, source_target_pairs={{0,4},{4,8},{8,12},{12,16},{16,20},{20,24},{24,28},{1,5},{5,9},{9,... | collective-permute-start | bytes 491528 | tf_op jit(solution)/shard_map/ppermute | solution.py:54
  36.5 7.8 %collective-permute-start.3 = (f32[1,64,640]{2,1,0:T(8,128)S(1)}, f32[1,64,640]{2,1,0:T(8,128)S(1)}, u32[]{:S(2)}, u32[]{:S(2)}) collective-permute-start(f32[1,64,640]{2,1,0:T(8,128)S(1)} %get-tuple-element.38), channel_id=1, source_target_pairs={{4,0},{8,4},{12,8},{16,12},{20,16},{24,20},{28,24},{5,1},{9,5},{13... | collective-permute-start | bytes 491528 | tf_op jit(solution)/shard_map/ppermute | solution.py:55
  38.9 5.4 %copy-start.27 = (f32[4,64,320]{2,1,0:T(8,128)S(1)}, f32[4,64,320]{2,1,0:T(8,128)}, u32[]{:S(2)}) copy-start(f32[4,64,320]{2,1,0:T(8,128)} %copy-done.26) | copy-start | bytes 983044
  44.3 1.6 %copy-start.1 = (f32[4,4,64,32]{3,2,1,0:T(8,128)S(1)}, f32[4,4,64,32]{3,2,1,0:T(8,128)}, u32[]{:S(2)}) copy-start(f32[4,4,64,32]{3,2,1,0:T(8,128)} %copy-done) | copy-start | bytes 393220
  44.3 1.6 %copy-start.3 = (f32[4,4,64,32]{3,2,1,0:T(8,128)S(1)}, f32[4,4,64,32]{3,2,1,0:T(8,128)}, u32[]{:S(2)}) copy-start(f32[4,4,64,32]{3,2,1,0:T(8,128)} %copy-done.2) | copy-start | bytes 393220
  44.3 1.6 %copy-start.11 = (f32[4,64,256]{2,1,0:T(8,128)S(1)}, f32[4,64,256]{2,1,0:T(8,128)}, u32[]{:S(2)}) copy-start(f32[4,64,256]{2,1,0:T(8,128)} %param.7) | copy-start | bytes 786436
  44.3 1.6 %copy-start.13 = (f32[4,64,256]{2,1,0:T(8,128)S(1)}, f32[4,64,256]{2,1,0:T(8,128)}, u32[]{:S(2)}) copy-start(f32[4,64,256]{2,1,0:T(8,128)} %param.6) | copy-start | bytes 786436
  44.3 1.6 %copy-start.15 = (f32[4,64,256]{2,1,0:T(8,128)S(1)}, f32[4,64,256]{2,1,0:T(8,128)}, u32[]{:S(2)}) copy-start(f32[4,64,256]{2,1,0:T(8,128)} %param.5) | copy-start | bytes 786436
  44.3 1.6 %copy-start.17 = (f32[4,64,256]{2,1,0:T(8,128)S(1)}, f32[4,64,256]{2,1,0:T(8,128)}, u32[]{:S(2)}) copy-start(f32[4,64,256]{2,1,0:T(8,128)} %param.4) | copy-start | bytes 786436
  44.3 1.6 %copy-start.61 = (f32[1,64,319]{2,1,0:T(8,128)S(1)}, f32[1,64,319]{2,1,0:T(8,128)}, u32[]{:S(2)}) copy-start(f32[1,64,319]{2,1,0:T(8,128)} %get-tuple-element.110) | copy-start | bytes 244996
  44.4 1.6 %copy-start.62 = (f32[1,64,319]{2,1,0:T(8,128)S(1)}, f32[1,64,319]{2,1,0:T(8,128)}, u32[]{:S(2)}) copy-start(f32[1,64,319]{2,1,0:T(8,128)} %get-tuple-element.111) | copy-start | bytes 244996
  45.9 22.7 %copy-start.4 = (f32[4,64,320]{2,1,0:T(8,128)}, f32[4,64,320]{2,1,0:T(8,128)S(1)}, u32[]{:S(2)}) copy-start(f32[4,64,320]{2,1,0:T(8,128)S(1)} %get-tuple-element.19) | copy-start | bytes 983044
  46.0 5.1 %copy-start.56 = (f32[2,64,319]{2,1,0:T(8,128)S(1)}, f32[2,64,319]{2,1,0:T(8,128)}, u32[]{:S(2)}) copy-start(f32[2,64,319]{2,1,0:T(8,128)} %get-tuple-element.90) | copy-start | bytes 489988
  46.0 5.1 %copy-start.57 = (f32[2,64,319]{2,1,0:T(8,128)S(1)}, f32[2,64,319]{2,1,0:T(8,128)}, u32[]{:S(2)}) copy-start(f32[2,64,319]{2,1,0:T(8,128)} %get-tuple-element.91) | copy-start | bytes 489988
  46.1 20.1 %collective-permute-start.6 = (f32[1,64,320]{2,1,0:T(8,128)S(1)}, f32[1,64,320]{2,1,0:T(8,128)S(1)}, u32[]{:S(2)}, u32[]{:S(2)}) collective-permute-start(f32[1,64,320]{2,1,0:T(8,128)S(1)} %fusion.201), channel_id=1, source_target_pairs={{0,4},{4,8},{8,12},{12,16},{16,20},{20,24},{24,28},{1,5},{5,9},{9,... | collective-permute-start | bytes 245768 | tf_op jit(solution)/shard_map/ppermute | solution.py:54
  52.2 6.5 %collective-permute-start.4 = (f32[1,64,320]{2,1,0:T(8,128)S(1)}, f32[1,64,320]{2,1,0:T(8,128)S(1)}, u32[]{:S(2)}, u32[]{:S(2)}) collective-permute-start(f32[1,64,320]{2,1,0:T(8,128)S(1)} %fusion.181), channel_id=1, source_target_pairs={{4,0},{8,4},{12,8},{16,12},{20,16},{24,20},{28,24},{5,1},{9,5},{13... | collective-permute-start | bytes 245768 | tf_op jit(solution)/shard_map/ppermute | solution.py:55
  58.9 14.1 %copy-start.45 = (f32[1,64,320]{2,1,0:T(8,128)}, f32[1,64,320]{2,1,0:T(8,128)S(1)}, u32[]{:S(2)}) copy-start(f32[1,64,320]{2,1,0:T(8,128)S(1)} %fusion.191) | copy-start | bytes 245764
  58.9 7.4 %collective-permute-start.5 = (f32[1,64,320]{2,1,0:T(8,128)S(1)}, f32[1,64,320]{2,1,0:T(8,128)S(1)}, u32[]{:S(2)}, u32[]{:S(2)}) collective-permute-start(f32[1,64,320]{2,1,0:T(8,128)S(1)} %fusion.191), channel_id=1, source_target_pairs={{0,4},{4,8},{8,12},{12,16},{16,20},{20,24},{24,28},{1,5},{5,9},{9,... | collective-permute-start | bytes 245768 | tf_op jit(solution)/shard_map/ppermute | solution.py:54
  66.4 6.5 %collective-permute-start.7 = (f32[1,64,320]{2,1,0:T(8,128)S(1)}, f32[1,64,320]{2,1,0:T(8,128)S(1)}, u32[]{:S(2)}, u32[]{:S(2)}) collective-permute-start(f32[1,64,320]{2,1,0:T(8,128)S(1)} %get-tuple-element.18), channel_id=1, source_target_pairs={{4,0},{8,4},{12,8},{16,12},{20,16},{24,20},{28,24},{5,1},{9,5},{13... | collective-permute-start | bytes 245768 | tf_op jit(solution)/shard_map/ppermute | solution.py:55
  74.3 21.8 %copy-start.40 = (f32[2,32,160]{2,1,0:T(8,128)}, f32[2,32,160]{2,1,0:T(8,128)S(1)}, u32[]{:S(2)}) copy-start(f32[2,32,160]{2,1,0:T(8,128)S(1)} %fusion.3) | copy-start | bytes 122884
  74.5 10.7 %collective-permute-start.8 = (f32[2,32,640]{2,1,0:T(8,128)S(1)}, f32[2,32,640]{2,1,0:T(8,128)S(1)}, u32[]{:S(2)}, u32[]{:S(2)}) collective-permute-start(f32[2,32,640]{2,1,0:T(8,128)S(1)} %pad_maximum_fusion.16), channel_id=1, source_target_pairs={{0,8},{4,12},{8,16},{12,20},{16,24},{20,28},{1,9},{5,13},{9,17},{1... | collective-permute-start | bytes 491528 | tf_op jit(solution)/shard_map/ppermute | solution.py:54
  78.1 9.2 %collective-permute-start.9 = (f32[2,32,640]{2,1,0:T(8,128)S(1)}, f32[2,32,640]{2,1,0:T(8,128)S(1)}, u32[]{:S(2)}, u32[]{:S(2)}) collective-permute-start(f32[2,32,640]{2,1,0:T(8,128)S(1)} %pad_maximum_fusion.16), channel_id=1, source_target_pairs={{0,4},{4,8},{8,12},{12,16},{16,20},{20,24},{24,28},{1,5},{5,9},{9,... | collective-permute-start | bytes 491528 | tf_op jit(solution)/shard_map/ppermute | solution.py:54
  82.8 9.6 %collective-permute-start.11 = (f32[2,32,640]{2,1,0:T(8,128)S(1)}, f32[2,32,640]{2,1,0:T(8,128)S(1)}, u32[]{:S(2)}, u32[]{:S(2)}) collective-permute-start(f32[2,32,640]{2,1,0:T(8,128)S(1)} %pad_maximum_fusion.16), channel_id=1, source_target_pairs={{8,0},{12,4},{16,8},{20,12},{24,16},{28,20},{9,1},{13,5},{17,9},{2... | collective-permute-start | bytes 491528 | tf_op jit(solution)/shard_map/ppermute | solution.py:55
  85.2 7.2 %collective-permute-start.10 = (f32[2,32,640]{2,1,0:T(8,128)S(1)}, f32[2,32,640]{2,1,0:T(8,128)S(1)}, u32[]{:S(2)}, u32[]{:S(2)}) collective-permute-start(f32[2,32,640]{2,1,0:T(8,128)S(1)} %pad_maximum_fusion.16), channel_id=1, source_target_pairs={{4,0},{8,4},{12,8},{16,12},{20,16},{24,20},{28,24},{5,1},{9,5},{13... | collective-permute-start | bytes 491528 | tf_op jit(solution)/shard_map/ppermute | solution.py:55
  87.3 5.2 %copy-start.46 = (f32[2,32,640]{2,1,0:T(8,128)}, f32[2,32,640]{2,1,0:T(8,128)S(1)}, u32[]{:S(2)}) copy-start(f32[2,32,640]{2,1,0:T(8,128)S(1)} %collective-permute-done.9) | copy-start | bytes 491524
  93.5 2.6 %copy-start.6 = (f32[10,31,160]{2,1,0:T(8,128)}, f32[10,31,160]{2,1,0:T(8,128)S(1)}, u32[]{:S(2)}) copy-start(f32[10,31,160]{2,1,0:T(8,128)S(1)} %fusion.22) | copy-start | bytes 595204
  97.9 11.0 %all-to-all-start = ((f32[8,1,4,16,80]{4,3,2,1,0:T(8,128)}), f32[8,1,4,16,80]{4,3,2,1,0:T(8,128)}, u32[]{:S(2)}, u32[]{:S(2)}) async-start(f32[8,1,4,16,80]{4,3,2,1,0:T(8,128)} %broadcast_in_dim.20), calls=%async_computation | async-start | bytes 524288 | tf_op jit(solution)/shard_map/all_to_all | solution.py:73
  110.9 3.1 %copy-start.76 = (s32[160]{0:T(256)S(1)}, s32[160]{0:T(256)}, u32[]{:S(2)}) copy-start(s32[160]{0:T(256)} %get-tuple-element.138) | copy-start | bytes 1924
  110.9 3.1 %copy-start.78 = (s32[160]{0:T(256)S(1)}, s32[160]{0:T(256)}, u32[]{:S(2)}) copy-start(s32[160]{0:T(256)} %get-tuple-element.139) | copy-start | bytes 1924
  111.0 3.1 %copy-start.86 = (pred[160]{0:T(512)(128)(4,1)S(1)}, pred[160]{0:T(512)(128)(4,1)}, u32[]{:S(2)}) copy-start(pred[160]{0:T(512)(128)(4,1)} %compare_and_fusion) | copy-start | bytes 484
  112.0 2.9 %copy-start.25 = (f32[8,32,160]{2,1,0:T(8,128)S(1)}, f32[8,32,160]{2,1,0:T(8,128)}, u32[]{:S(2)}) copy-start(f32[8,32,160]{2,1,0:T(8,128)} %copy-done.24) | copy-start | bytes 491524
  118.0 4.4 %copy-start.23 = (f32[1,64,320]{2,1,0:T(8,128)S(1)}, f32[1,64,320]{2,1,0:T(8,128)}, u32[]{:S(2)}) copy-start(f32[1,64,320]{2,1,0:T(8,128)} %copy-done.21) | copy-start | bytes 245764
  118.9 15.1 %collective-permute-start.15 = (f32[1,64,320]{2,1,0:T(8,128)S(1)}, f32[1,64,320]{2,1,0:T(8,128)S(1)}, u32[]{:S(2)}, u32[]{:S(2)}) collective-permute-start(f32[1,64,320]{2,1,0:T(8,128)S(1)} %fusion.160), channel_id=1, source_target_pairs={{4,0},{8,4},{12,8},{16,12},{20,16},{24,20},{28,24},{5,1},{9,5},{13... | collective-permute-start | bytes 245768 | tf_op jit(solution)/shard_map/ppermute | solution.py:55
  122.6 7.4 %collective-permute-start.14 = (f32[1,64,320]{2,1,0:T(8,128)S(1)}, f32[1,64,320]{2,1,0:T(8,128)S(1)}, u32[]{:S(2)}, u32[]{:S(2)}) collective-permute-start(f32[1,64,320]{2,1,0:T(8,128)S(1)} %fusion.150), channel_id=1, source_target_pairs={{0,4},{4,8},{8,12},{12,16},{16,20},{20,24},{24,28},{1,5},{5,9},{9,... | collective-permute-start | bytes 245768 | tf_op jit(solution)/shard_map/ppermute | solution.py:54
  130.1 6.5 %collective-permute-start.17 = (f32[1,64,320]{2,1,0:T(8,128)S(1)}, f32[1,64,320]{2,1,0:T(8,128)S(1)}, u32[]{:S(2)}, u32[]{:S(2)}) collective-permute-start(f32[1,64,320]{2,1,0:T(8,128)S(1)} %fusion.140), channel_id=1, source_target_pairs={{4,0},{8,4},{12,8},{16,12},{20,16},{24,20},{28,24},{5,1},{9,5},{13... | collective-permute-start | bytes 245768 | tf_op jit(solution)/shard_map/ppermute | solution.py:55
  134.2 7.4 %collective-permute-start.16 = (f32[1,64,320]{2,1,0:T(8,128)S(1)}, f32[1,64,320]{2,1,0:T(8,128)S(1)}, u32[]{:S(2)}, u32[]{:S(2)}) collective-permute-start(f32[1,64,320]{2,1,0:T(8,128)S(1)} %fusion.130), channel_id=1, source_target_pairs={{0,4},{4,8},{8,12},{12,16},{16,20},{20,24},{24,28},{1,5},{5,9},{9,... | collective-permute-start | bytes 245768 | tf_op jit(solution)/shard_map/ppermute | solution.py:54
  136.4 5.4 %copy-start.9 = (f32[4,64,320]{2,1,0:T(8,128)S(1)}, f32[4,64,320]{2,1,0:T(8,128)}, u32[]{:S(2)}) copy-start(f32[4,64,320]{2,1,0:T(8,128)} %copy-done.8) | copy-start | bytes 983044
  (42 other events, 44.2 us)

commit v23 on v20

--- a/solution.py
+++ b/solution.py
@@ -189,8 +189,8 @@
     source_x = first[:, 0]
     weights_one = make_weights(first[:, 1], wide_inc, wide_raan, 1.0, 0)
 
-    density = split_sweep(weights_one, source_x, source_x, 1)
-    density = split_sweep(weights_one, alt_extend(density, 1), source_x, 1)
+    density = sweep(weights_one, source_x, 1, source_x, 1, masked=False)
+    density = sweep(weights_one, alt_extend(density, 1), 1, source_x, 1, masked=False)
     density_x = alt_extend(density, 1)
     applied, density = apply_op(weights_one, density_x, 1)
     rhs_two = coarsen(wide_source - applied)
@@ -229,8 +229,8 @@
         correction = sweep(weights_two, correction, halo, rhs_two_x, wide_two - 1)
 
     density = density_x + trim(refine(correction), 2, 1)
-    density = split_sweep(weights_one, density, source_x, 1)
-    density = split_sweep(weights_one, alt_extend(density, 1), source_x, 1)
+    density = sweep(weights_one, density, 1, source_x, 1, masked=False)
+    density = sweep(weights_one, alt_extend(density, 1), 1, source_x, 1, masked=False)
     applied, centre = apply_op(weights_one, alt_extend(density, 1), 1)
     scaled_residual = (wide_source - applied) / weights_one[0][6]
     keep = slice(halo_r, halo_r + length)

time: 127 us -> 133 us (1.047)
  the two profiles are of different devices: /device:TPU:8 before, /device:TPU:0 now
where the time goes in v23:
time: 133 us; the launch traced here: 132 us
  starting transfers between devices  49.6 us (37%)
  waiting for transfers between devices  34.6 us (26%)
  other arithmetic  23.7 us (18%)
  matrix products  11.5 us (9%)
  local copies, waits for them, and re-layouts  10.3 us (8%)
  between operations  1.96 us (1%)
    ppermute x7, starting transfers between devices, alt_extend(): below.insert(0, lax.ppermute(values[low:], 'alt', up))  26.3 us
    ppermute x7, waiting for transfers between devices, alt_extend(): above.append(lax.ppermute(values[:high], 'alt', down))  22.1 us
    ppermute x7, starting transfers between devices, alt_extend(): above.append(lax.ppermute(values[:high], 'alt', down))  9.04 us
    all_to_all x1, starting transfers between devices, spread_gather(): every = lax.all_to_all(copies, 'alt', 0, 0)  7.8 us
    all_to_all x1, waiting for transfers between devices, spread_gather(): every = lax.all_to_all(copies, 'alt', 0, 0)  7.25 us
    dot_general x8, matrix products, coarsen(): summed = jnp.matmul(summed, pairing(length), precision=HIGH)  6.68 us
    add x7, other arithmetic, sweep(): centre + OMEGA * (trim(target, target_halo, halo - 1) - applied) / diagonal  5.94 us
    ppermute x7, waiting for transfers between devices, alt_extend(): below.insert(0, lax.ppermute(values[low:], 'alt', up))  3.98 us
  transfers between devices with their start and end apart: 19, of which 11 were waited for; matrix products, arithmetic and copies ran while one was open for 15% of the time, Pallas kernels for 0%

profile of v23, /device:TPU:0, one launch (start us, length us, event | category | flops | bytes accessed | tf_op | source)
XLA Modules:
  0.0 131.6 jit_solution(8301628558348421097)
XLA Ops:
  0.6 1.3 pad_maximum_fusion.1
  2.4 2.4 %collective-permute-start.1 = (f32[4,4,16,128]{3,2,1,0:T(8,128)S(1)}, f32[4,4,16,128]{3,2,1,0:T(8,128)S(1)}, u32[]{:S(2)}, u32[]{:S(2)}) collective-permute-start(f32[4,4,16,128]{3,2,1,0:T(8,128)S(1)} %copy.17), channel_id=1, source_target_pairs={{1,0},{2,1},{3,2},{0,3},{5,4},{6,5},{7,6},{4,7},{9,8},{10,9},{11,1... | collective-permute-start | bytes 393224 | tf_op jit(solution)/shard_map/ppermute | solution.py:42
  5.1 0.5 compare_and_fusion
  5.6 0.5 fusion.225
  6.1 0.6 iota_shift-right-logical_fusion.3
  6.7 0.5 iota_shift-right-logical_fusion.1
  7.3 0.6 compare_and_fusion.2
  7.8 0.6 iota_shift-right-logical_fusion
  8.5 1.2 collective-permute-done
  10.1 0.9 pad_maximum_fusion.14
  11.1 1.6 %pad_maximum_fusion = f32[4,4,64,320]{3,2,0,1:T(8,128)S(1)} fusion(f32[4,1,64,256]{3,2,0,1:T(8,128)S(1)} %bitcast.177, f32[4,1,64,256]{3,2,0,1:T(8,128)S(1)} %bitcast.180, f32[4,1,64,256]{3,2,0,1:T(8,128)S(1)} %bitcast.183, f32[4,1,64,256]{3,2,0,1:T(8,128)} %bitcast.185, f32[4,4,64,32]{3,2,1,0:T(8,128)S(1)} %reshape.78, f32[4,4,64,32]{3,2,1,0:T(8,128)S(1)} %reshape.80), kind=kLoop, calls=%fused_computation | loop fusion | flops 1638400 | bytes 2621440 | tf_op jit(solution)/shard_map/concatenate | solution.py:43
  12.6 1.3 collective-permute-start.3
  13.9 5.2 %collective-permute-start.2 = (f32[1,2,64,320]{3,2,0,1:T(8,128)}, f32[1,2,64,320]{3,2,0,1:T(8,128)}, u32[]{:S(2)}, u32[]{:S(2)}) collective-permute-start(f32[1,2,64,320]{3,2,0,1:T(8,128)} %get-tuple-element.21), channel_id=1, source_target_pairs={{0,4},{4,8},{8,12},{12,16},{16,20},{20,24},{24,28},{1,5},{5,9},{9,... | collective-permute-start | bytes 491528 | tf_op jit(solution)/shard_map/ppermute | solution.py:54
  19.1 1.0 slice_bitcast_fusion
  20.2 1.9 %reduce_sum.74 = f32[2,64,320]{2,1,0:T(8,128)} reduce(f32[2,2,64,320]{3,2,1,0:T(8,128)} %bitcast.189, f32[]{:T(128)} %constant.139.clone.1), dimensions={1}, to_apply=%region_2.3 | reduce | flops 40960 | bytes 491524 | tf_op jit(solution)/shard_map/reduce_sum | solution.py:21
  22.0 0.7 reduce_sum.75
  22.8 1.4 %fusion.239 = f32[2,64,160]{2,1,0:T(8,128)S(1)} fusion(f32[2,64,320]{2,1,0:T(8,128)} %reduce_sum.74, s32[320]{0:T(512)} %get-tuple-element.110, s32[320]{0:T(512)} %get-tuple-element.111, pred[320]{0:T(512)(128)(4,1)} %fusion.225), kind=kOutput, calls=%fused_computation.356 | convolution fusion | flops 78745600 | bytes 248640 | tf_op jit(solution)/shard_map/dot_general | solution.py:22
  24.2 1.1 fusion.241
  25.3 1.4 %fusion.237 = f32[2,64,160]{2,1,0:T(8,128)S(1)} fusion(f32[2,64,320]{2,1,0:T(8,128)} %reduce_sum.75, s32[320]{0:T(512)} %get-tuple-element.110, s32[320]{0:T(512)} %get-tuple-element.111, pred[320]{0:T(512)(128)(4,1)} %fusion.225), kind=kOutput, calls=%fused_computation.355 | convolution fusion | flops 78745600 | bytes 248640 | tf_op jit(solution)/shard_map/dot_general | solution.py:22
  26.7 0.9 fusion.287
  27.6 0.9 fusion.286
  28.5 0.9 fusion.288
  29.4 0.9 fusion.130
  30.3 0.9 fusion.131
  32.7 2.0 %fusion.74 = (f32[4,64,320]{2,1,0:T(8,128)}, f32[4,64,320]{2,1,0:T(8,128)S(1)}, f32[4,64,320]{2,1,0:T(8,128)S(1)}, f32[4,64,320]{2,1,0:T(8,128)S(1)}, f32[4,64,320]{2,1,0:T(8,128)S(1)}) fusion(f32[4,63,320]{2,1,0:T(8,128)S(1)} %get-tuple-element.107, f32[4,64,319]{2,1,0:T(8,128)S(1)} %get-tuple-element.108, f32[4,4,64,320]{3,2,0,1:T(8,128)S(1)} %pad_maximum_fusion, ...), kind=kLoop, calls=%fused_computation.109 | loop fusion | flops 1310720 | bytes 4252672 | tf_op jit(solution)/shard_map/add | solution.py:100
  34.7 1.6 %fusion.66 = f32[4,64,320]{2,1,0:T(8,128)S(1)} fusion(f32[4,64,320]{2,1,0:T(8,128)S(1)} %get-tuple-element.8, f32[1,2,64,320]{3,2,0,1:T(8,128)} %collective-permute-done.3, f32[4,2,64,320]{3,2,0,1:T(8,128)S(1)} %slice.749, f32[4,64,320]{2,1,0:T(8,128)S(1)} %get-tuple-element.6, f32[1,2,64,320]{3,2,0,1:T(8,128)} %collective-permute-done.2, ...), kind=kLoop, calls=%fused_computation.90 | loop fusion | flops 2048000 | bytes 4570112 | tf_op jit(solution)/shard_map/add | solution.py:135
  36.4 3.7 %collective-permute-start.4 = (f32[1,64,320]{2,1,0:T(8,128)S(1)}, f32[1,64,320]{2,1,0:T(8,128)S(1)}, u32[]{:S(2)}, u32[]{:S(2)}) collective-permute-start(f32[1,64,320]{2,1,0:T(8,128)S(1)} %get-tuple-element.58), channel_id=1, source_target_pairs={{0,4},{4,8},{8,12},{12,16},{16,20},{20,24},{24,28},{1,5},{5,9},{9,... | collective-permute-start | bytes 245768 | tf_op jit(solution)/shard_map/ppermute | solution.py:54
  40.0 1.3 collective-permute-start.5
  41.5 0.7 collective-permute-done.4
  42.2 4.3 %collective-permute-done.5 = f32[1,64,320]{2,1,0:T(8,128)S(1)} collective-permute-done((f32[1,64,320]{2,1,0:T(8,128)S(1)}, f32[1,64,320]{2,1,0:T(8,128)S(1)}, u32[]{:S(2)}, u32[]{:S(2)}) %collective-permute-start.5) | collective-permute-done | bytes 81952 | tf_op jit(solution)/shard_map/ppermute | solution.py:55
  46.5 0.5 fusion.53
  47.2 3.4 %collective-permute-start.6 = (f32[1,64,320]{2,1,0:T(8,128)S(1)}, f32[1,64,320]{2,1,0:T(8,128)S(1)}, u32[]{:S(2)}, u32[]{:S(2)}) collective-permute-start(f32[1,64,320]{2,1,0:T(8,128)S(1)} %get-tuple-element.48), channel_id=1, source_target_pairs={{0,4},{4,8},{8,12},{12,16},{16,20},{20,24},{24,28},{1,5},{5,9},{9,... | collective-permute-start | bytes 245768 | tf_op jit(solution)/shard_map/ppermute | solution.py:54
  50.7 1.3 collective-permute-start.7
  52.0 1.8 %collective-permute-done.6 = f32[1,64,320]{2,1,0:T(8,128)S(1)} collective-permute-done((f32[1,64,320]{2,1,0:T(8,128)S(1)}, f32[1,64,320]{2,1,0:T(8,128)S(1)}, u32[]{:S(2)}, u32[]{:S(2)}) %collective-permute-start.6) | collective-permute-done | bytes 81952 | tf_op jit(solution)/shard_map/ppermute | solution.py:54
  53.9 3.3 %collective-permute-done.7 = f32[1,64,320]{2,1,0:T(8,128)S(1)} collective-permute-done((f32[1,64,320]{2,1,0:T(8,128)S(1)}, f32[1,64,320]{2,1,0:T(8,128)S(1)}, u32[]{:S(2)}, u32[]{:S(2)}) %collective-permute-start.7) | collective-permute-done | bytes 81952 | tf_op jit(solution)/shard_map/ppermute | solution.py:55
  58.7 3.5 %collective-permute-start.8 = (f32[2,32,640]{2,1,0:T(8,128)S(1)}, f32[2,32,640]{2,1,0:T(8,128)S(1)}, u32[]{:S(2)}, u32[]{:S(2)}) collective-permute-start(f32[2,32,640]{2,1,0:T(8,128)S(1)} %pad_maximum_fusion.16), channel_id=1, source_target_pairs={{0,8},{4,12},{8,16},{12,20},{16,24},{20,28},{1,9},{5,13},{9,17},{1... | collective-permute-start | bytes 491528 | tf_op jit(solution)/shard_map/ppermute | solution.py:54
  62.3 4.3 %collective-permute-start.9 = (f32[2,32,640]{2,1,0:T(8,128)S(1)}, f32[2,32,640]{2,1,0:T(8,128)S(1)}, u32[]{:S(2)}, u32[]{:S(2)}) collective-permute-start(f32[2,32,640]{2,1,0:T(8,128)S(1)} %pad_maximum_fusion.16), channel_id=1, source_target_pairs={{0,4},{4,8},{8,12},{12,16},{16,20},{20,24},{24,28},{1,5},{5,9},{9,... | collective-permute-start | bytes 491528 | tf_op jit(solution)/shard_map/ppermute | solution.py:54
  66.8 2.6 %collective-permute-start.12 = (f32[1,32,160]{2,1,0:T(8,128)S(1)}, f32[1,32,160]{2,1,0:T(8,128)S(1)}, u32[]{:S(2)}, u32[]{:S(2)}) collective-permute-start(f32[1,32,160]{2,1,0:T(8,128)S(1)} %get-tuple-element.99), channel_id=1, source_target_pairs={{0,12},{4,16},{8,20},{12,24},{16,28},{1,13},{5,17},{9,21},{13,25},... | collective-permute-start | bytes 61448 | tf_op jit(solution)/shard_map/ppermute | solution.py:65
  69.5 1.3 collective-permute-start.13
  70.8 1.3 collective-permute-start.11
  72.1 1.3 collective-permute-start.10
  73.5 5.8 %collective-permute-done.10 = f32[2,32,640]{2,1,0:T(8,128)S(1)} collective-permute-done((f32[2,32,640]{2,1,0:T(8,128)S(1)}, f32[2,32,640]{2,1,0:T(8,128)S(1)}, u32[]{:S(2)}, u32[]{:S(2)}) %collective-permute-start.10) | collective-permute-done | bytes 163872 | tf_op jit(solution)/shard_map/ppermute | solution.py:55
  82.6 0.7 broadcast_in_dim.20
  83.3 7.8 %all-to-all-start = ((f32[8,1,4,16,80]{4,3,2,1,0:T(8,128)}), f32[8,1,4,16,80]{4,3,2,1,0:T(8,128)}, u32[]{:S(2)}, u32[]{:S(2)}) async-start(f32[8,1,4,16,80]{4,3,2,1,0:T(8,128)} %broadcast_in_dim.20), calls=%async_computation | async-start | bytes 524288 | tf_op jit(solution)/shard_map/all_to_all | solution.py:73
  91.1 0.5 compare_and_fusion.3
  91.7 0.6 compare_and_fusion.4
  92.2 7.2 %all-to-all-done = f32[8,1,4,16,80]{4,3,2,1,0:T(8,128)} async-done(((f32[8,1,4,16,80]{4,3,2,1,0:T(8,128)}), f32[8,1,4,16,80]{4,3,2,1,0:T(8,128)}, u32[]{:S(2)}, u32[]{:S(2)}) %all-to-all-start) | async-done | bytes 163872 | tf_op jit(solution)/shard_map/all_to_all | solution.py:73
  99.5 0.9 slice_bitcast_fusion.1
  100.5 1.0 fusion.187
  101.6 0.9 fusion.149
  102.7 1.0 fusion.161
  103.7 0.9 fusion.173
  107.4 0.5 fusion.125
  108.7 0.7 copy-done.1
  110.1 1.9 %collective-permute-start.14 = (f32[1,64,320]{2,1,0:T(8,128)S(1)}, f32[1,64,320]{2,1,0:T(8,128)S(1)}, u32[]{:S(2)}, u32[]{:S(2)}) collective-permute-start(f32[1,64,320]{2,1,0:T(8,128)S(1)} %get-tuple-element.46), channel_id=1, source_target_pairs={{0,4},{4,8},{8,12},{12,16},{16,20},{20,24},{24,28},{1,5},{5,9},{9,... | collective-permute-start | bytes 245768 | tf_op jit(solution)/shard_map/ppermute | solution.py:54
  112.0 1.3 collective-permute-start.15
  113.5 0.7 collective-permute-done.14
  114.2 4.3 %collective-permute-done.15 = f32[1,64,320]{2,1,0:T(8,128)S(1)} collective-permute-done((f32[1,64,320]{2,1,0:T(8,128)S(1)}, f32[1,64,320]{2,1,0:T(8,128)S(1)}, u32[]{:S(2)}, u32[]{:S(2)}) %collective-permute-start.15) | collective-permute-done | bytes 81952 | tf_op jit(solution)/shard_map/ppermute | solution.py:55
  118.5 0.5 fusion.22
  119.1 4.3 %collective-permute-start.16 = (f32[1,64,320]{2,1,0:T(8,128)S(1)}, f32[1,64,320]{2,1,0:T(8,128)S(1)}, u32[]{:S(2)}, u32[]{:S(2)}) collective-permute-start(f32[1,64,320]{2,1,0:T(8,128)S(1)} %get-tuple-element.38), channel_id=1, source_target_pairs={{0,4},{4,8},{8,12},{12,16},{16,20},{20,24},{24,28},{1,5},{5,9},{9,... | collective-permute-start | bytes 245768 | tf_op jit(solution)/shard_map/ppermute | solution.py:54
  123.4 1.3 collective-permute-start.17
  124.9 0.7 collective-permute-done.16
  125.6 4.3 %collective-permute-done.17 = f32[1,64,320]{2,1,0:T(8,128)S(1)} collective-permute-done((f32[1,64,320]{2,1,0:T(8,128)S(1)}, f32[1,64,320]{2,1,0:T(8,128)S(1)}, u32[]{:S(2)}, u32[]{:S(2)}) %collective-permute-start.17) | collective-permute-done | bytes 81952 | tf_op jit(solution)/shard_map/ppermute | solution.py:55
  130.1 1.6 %fusion.88 = (f32[4,64,256]{2,1,0:T(8,128)}, f32[4,64,256]{2,1,0:T(8,128)}) fusion(f32[4,63,320]{2,1,0:T(8,128)S(1)} %get-tuple-element.37, f32[4,64,320]{2,1,0:T(8,128)S(1)} %copy-done.3, f32[4,64,319]{2,1,0:T(8,128)S(1)} %get-tuple-element.41, f32[4,64,320]{2,1,0:T(8,128)S(1)} %copy-done.1, f32[4,64,319]{2,1,0:T(8,128)S(1)} %get-tuple-element.40, ...), kind=kLoop, calls=%fused_computation.131 | loop fusion | flops 655360 | bytes 3395584 | tf_op jit(solution)/shard_map/div | solution.py:235
  (201 shorter events, 12.4 us)
Async XLA Ops:
  2.1 7.9 %copy-start.18 = (f32[4,64,256]{2,1,0:T(8,128)S(1)}, f32[4,64,256]{2,1,0:T(8,128)}, u32[]{:S(2)}) copy-start(f32[4,64,256]{2,1,0:T(8,128)} %param.7) | copy-start | bytes 786436
  2.1 7.9 %copy-start.19 = (f32[4,64,256]{2,1,0:T(8,128)S(1)}, f32[4,64,256]{2,1,0:T(8,128)}, u32[]{:S(2)}) copy-start(f32[4,64,256]{2,1,0:T(8,128)} %param.6) | copy-start | bytes 786436
  2.1 7.9 %copy-start.20 = (f32[4,64,256]{2,1,0:T(8,128)S(1)}, f32[4,64,256]{2,1,0:T(8,128)}, u32[]{:S(2)}) copy-start(f32[4,64,256]{2,1,0:T(8,128)} %param.5) | copy-start | bytes 786436
  2.2 7.9 %copy-start.21 = (f32[4,64,256]{2,1,0:T(8,128)S(1)}, f32[4,64,256]{2,1,0:T(8,128)}, u32[]{:S(2)}) copy-start(f32[4,64,256]{2,1,0:T(8,128)} %param.4) | copy-start | bytes 786436
  2.4 7.5 %collective-permute-start.1 = (f32[4,4,16,128]{3,2,1,0:T(8,128)S(1)}, f32[4,4,16,128]{3,2,1,0:T(8,128)S(1)}, u32[]{:S(2)}, u32[]{:S(2)}) collective-permute-start(f32[4,4,16,128]{3,2,1,0:T(8,128)S(1)} %copy.17), channel_id=1, source_target_pairs={{1,0},{2,1},{3,2},{0,3},{5,4},{6,5},{7,6},{4,7},{9,8},{10,9},{11,1... | collective-permute-start | bytes 393224 | tf_op jit(solution)/shard_map/ppermute | solution.py:42
  5.0 4.7 %collective-permute-start = (f32[4,4,16,128]{3,2,1,0:T(8,128)S(1)}, f32[4,4,16,128]{3,2,1,0:T(8,128)S(1)}, u32[]{:S(2)}, u32[]{:S(2)}) collective-permute-start(f32[4,4,16,128]{3,2,1,0:T(8,128)S(1)} %copy.16), channel_id=1, source_target_pairs={{0,1},{1,2},{2,3},{3,0},{4,5},{5,6},{6,7},{7,4},{8,9},{9,10},{10,1... | collective-permute-start | bytes 393224 | tf_op jit(solution)/shard_map/ppermute | solution.py:41
  12.6 20.0 %collective-permute-start.3 = (f32[1,2,64,320]{3,2,0,1:T(8,128)}, f32[1,2,64,320]{3,2,0,1:T(8,128)}, u32[]{:S(2)}, u32[]{:S(2)}) collective-permute-start(f32[1,2,64,320]{3,2,0,1:T(8,128)} %get-tuple-element.20), channel_id=1, source_target_pairs={{4,0},{8,4},{12,8},{16,12},{20,16},{24,20},{28,24},{5,1},{9,5},{13... | collective-permute-start | bytes 491528 | tf_op jit(solution)/shard_map/ppermute | solution.py:55
  13.9 18.8 %collective-permute-start.2 = (f32[1,2,64,320]{3,2,0,1:T(8,128)}, f32[1,2,64,320]{3,2,0,1:T(8,128)}, u32[]{:S(2)}, u32[]{:S(2)}) collective-permute-start(f32[1,2,64,320]{3,2,0,1:T(8,128)} %get-tuple-element.21), channel_id=1, source_target_pairs={{0,4},{4,8},{8,12},{12,16},{16,20},{20,24},{24,28},{1,5},{5,9},{9,... | collective-permute-start | bytes 491528 | tf_op jit(solution)/shard_map/ppermute | solution.py:54
  20.2 11.4 %copy-start.2 = (f32[4,64,320]{2,1,0:T(8,128)}, f32[4,64,320]{2,1,0:T(8,128)S(1)}, u32[]{:S(2)}) copy-start(f32[4,64,320]{2,1,0:T(8,128)S(1)} %get-tuple-element.22) | copy-start | bytes 983044
  27.5 31.0 %copy-start.31 = (f32[2,32,160]{2,1,0:T(8,128)}, f32[2,32,160]{2,1,0:T(8,128)S(1)}, u32[]{:S(2)}) copy-start(f32[2,32,160]{2,1,0:T(8,128)S(1)} %get-tuple-element.104) | copy-start | bytes 122884
  28.4 30.1 %copy-start.33 = (f32[2,32,160]{2,1,0:T(8,128)}, f32[2,32,160]{2,1,0:T(8,128)S(1)}, u32[]{:S(2)}) copy-start(f32[2,32,160]{2,1,0:T(8,128)S(1)} %get-tuple-element.102) | copy-start | bytes 122884
  29.3 29.2 %copy-start.24 = (f32[2,32,160]{2,1,0:T(8,128)}, f32[2,32,160]{2,1,0:T(8,128)S(1)}, u32[]{:S(2)}) copy-start(f32[2,32,160]{2,1,0:T(8,128)S(1)} %get-tuple-element.106) | copy-start | bytes 122884
  34.7 22.5 %copy-start = (f32[4,64,320]{2,1,0:T(8,128)}, f32[4,64,320]{2,1,0:T(8,128)S(1)}, u32[]{:S(2)}) copy-start(f32[4,64,320]{2,1,0:T(8,128)S(1)} %get-tuple-element.7) | copy-start | bytes 983044
  36.4 5.9 %collective-permute-start.4 = (f32[1,64,320]{2,1,0:T(8,128)S(1)}, f32[1,64,320]{2,1,0:T(8,128)S(1)}, u32[]{:S(2)}, u32[]{:S(2)}) collective-permute-start(f32[1,64,320]{2,1,0:T(8,128)S(1)} %get-tuple-element.58), channel_id=1, source_target_pairs={{0,4},{4,8},{8,12},{12,16},{16,20},{20,24},{24,28},{1,5},{5,9},{9,... | collective-permute-start | bytes 245768 | tf_op jit(solution)/shard_map/ppermute | solution.py:54
  40.0 6.5 %collective-permute-start.5 = (f32[1,64,320]{2,1,0:T(8,128)S(1)}, f32[1,64,320]{2,1,0:T(8,128)S(1)}, u32[]{:S(2)}, u32[]{:S(2)}) collective-permute-start(f32[1,64,320]{2,1,0:T(8,128)S(1)} %get-tuple-element.59), channel_id=1, source_target_pairs={{4,0},{8,4},{12,8},{16,12},{20,16},{24,20},{28,24},{5,1},{9,5},{13... | collective-permute-start | bytes 245768 | tf_op jit(solution)/shard_map/ppermute | solution.py:55
  47.2 6.6 %collective-permute-start.6 = (f32[1,64,320]{2,1,0:T(8,128)S(1)}, f32[1,64,320]{2,1,0:T(8,128)S(1)}, u32[]{:S(2)}, u32[]{:S(2)}) collective-permute-start(f32[1,64,320]{2,1,0:T(8,128)S(1)} %get-tuple-element.48), channel_id=1, source_target_pairs={{0,4},{4,8},{8,12},{12,16},{16,20},{20,24},{24,28},{1,5},{5,9},{9,... | collective-permute-start | bytes 245768 | tf_op jit(solution)/shard_map/ppermute | solution.py:54
  50.7 6.5 %collective-permute-start.7 = (f32[1,64,320]{2,1,0:T(8,128)S(1)}, f32[1,64,320]{2,1,0:T(8,128)S(1)}, u32[]{:S(2)}, u32[]{:S(2)}) collective-permute-start(f32[1,64,320]{2,1,0:T(8,128)S(1)} %get-tuple-element.49), channel_id=1, source_target_pairs={{4,0},{8,4},{12,8},{16,12},{20,16},{24,20},{28,24},{5,1},{9,5},{13... | collective-permute-start | bytes 245768 | tf_op jit(solution)/shard_map/ppermute | solution.py:55
  53.9 3.8 %copy-start.35 = (f32[1,64,320]{2,1,0:T(8,128)}, f32[1,64,320]{2,1,0:T(8,128)S(1)}, u32[]{:S(2)}) copy-start(f32[1,64,320]{2,1,0:T(8,128)S(1)} %collective-permute-done.6) | copy-start | bytes 245764
  57.2 0.7 copy-start.45
  57.2 1.1 copy-start.39
  57.2 1.1 copy-start.41
  58.5 23.0 %copy-start.22 = (f32[2,32,160]{2,1,0:T(8,128)}, f32[2,32,160]{2,1,0:T(8,128)S(1)}, u32[]{:S(2)}) copy-start(f32[2,32,160]{2,1,0:T(8,128)S(1)} %fusion.3) | copy-start | bytes 122884
  58.7 13.3 %collective-permute-start.8 = (f32[2,32,640]{2,1,0:T(8,128)S(1)}, f32[2,32,640]{2,1,0:T(8,128)S(1)}, u32[]{:S(2)}, u32[]{:S(2)}) collective-permute-start(f32[2,32,640]{2,1,0:T(8,128)S(1)} %pad_maximum_fusion.16), channel_id=1, source_target_pairs={{0,8},{4,12},{8,16},{12,20},{16,24},{20,28},{1,9},{5,13},{9,17},{1... | collective-permute-start | bytes 491528 | tf_op jit(solution)/shard_map/ppermute | solution.py:54
  62.3 11.0 %collective-permute-start.9 = (f32[2,32,640]{2,1,0:T(8,128)S(1)}, f32[2,32,640]{2,1,0:T(8,128)S(1)}, u32[]{:S(2)}, u32[]{:S(2)}) collective-permute-start(f32[2,32,640]{2,1,0:T(8,128)S(1)} %pad_maximum_fusion.16), channel_id=1, source_target_pairs={{0,4},{4,8},{8,12},{12,16},{16,20},{20,24},{24,28},{1,5},{5,9},{9,... | collective-permute-start | bytes 491528 | tf_op jit(solution)/shard_map/ppermute | solution.py:54
  66.8 13.2 %collective-permute-start.12 = (f32[1,32,160]{2,1,0:T(8,128)S(1)}, f32[1,32,160]{2,1,0:T(8,128)S(1)}, u32[]{:S(2)}, u32[]{:S(2)}) collective-permute-start(f32[1,32,160]{2,1,0:T(8,128)S(1)} %get-tuple-element.99), channel_id=1, source_target_pairs={{0,12},{4,16},{8,20},{12,24},{16,28},{1,13},{5,17},{9,21},{13,25},... | collective-permute-start | bytes 61448 | tf_op jit(solution)/shard_map/ppermute | solution.py:65
  69.5 10.5 %collective-permute-start.13 = (f32[1,32,160]{2,1,0:T(8,128)S(1)}, f32[1,32,160]{2,1,0:T(8,128)S(1)}, u32[]{:S(2)}, u32[]{:S(2)}) collective-permute-start(f32[1,32,160]{2,1,0:T(8,128)S(1)} %get-tuple-element.100), channel_id=1, source_target_pairs={{12,0},{16,4},{20,8},{24,12},{28,16},{13,1},{17,5},{21,9},{25,13},... | collective-permute-start | bytes 61448 | tf_op jit(solution)/shard_map/ppermute | solution.py:66
  70.8 8.5 %collective-permute-start.11 = (f32[2,32,640]{2,1,0:T(8,128)S(1)}, f32[2,32,640]{2,1,0:T(8,128)S(1)}, u32[]{:S(2)}, u32[]{:S(2)}) collective-permute-start(f32[2,32,640]{2,1,0:T(8,128)S(1)} %pad_maximum_fusion.16), channel_id=1, source_target_pairs={{8,0},{12,4},{16,8},{20,12},{24,16},{28,20},{9,1},{13,5},{17,9},{2... | collective-permute-start | bytes 491528 | tf_op jit(solution)/shard_map/ppermute | solution.py:55
  72.1 7.2 %collective-permute-start.10 = (f32[2,32,640]{2,1,0:T(8,128)S(1)}, f32[2,32,640]{2,1,0:T(8,128)S(1)}, u32[]{:S(2)}, u32[]{:S(2)}) collective-permute-start(f32[2,32,640]{2,1,0:T(8,128)S(1)} %pad_maximum_fusion.16), channel_id=1, source_target_pairs={{4,0},{8,4},{12,8},{16,12},{20,16},{24,20},{28,24},{5,1},{9,5},{13... | collective-permute-start | bytes 491528 | tf_op jit(solution)/shard_map/ppermute | solution.py:55
  73.4 6.4 %copy-start.26 = (f32[2,32,640]{2,1,0:T(8,128)}, f32[2,32,640]{2,1,0:T(8,128)S(1)}, u32[]{:S(2)}) copy-start(f32[2,32,640]{2,1,0:T(8,128)S(1)} %collective-permute-done.9) | copy-start | bytes 491524
  79.8 1.8 %copy-start.4 = (f32[10,31,160]{2,1,0:T(8,128)}, f32[10,31,160]{2,1,0:T(8,128)S(1)}, u32[]{:S(2)}) copy-start(f32[10,31,160]{2,1,0:T(8,128)S(1)} %fusion.75) | copy-start | bytes 595204
  80.4 1.3 copy-start.8
  80.4 1.3 copy-start.10
  80.4 1.3 copy-start.12
  80.4 1.3 copy-start.14
  80.4 1.3 copy-start.16
  83.3 16.1 %all-to-all-start = ((f32[8,1,4,16,80]{4,3,2,1,0:T(8,128)}), f32[8,1,4,16,80]{4,3,2,1,0:T(8,128)}, u32[]{:S(2)}, u32[]{:S(2)}) async-start(f32[8,1,4,16,80]{4,3,2,1,0:T(8,128)} %broadcast_in_dim.20), calls=%async_computation | async-start | bytes 524288 | tf_op jit(solution)/shard_map/all_to_all | solution.py:73
  101.6 3.1 %copy-start.48 = (s32[160]{0:T(256)S(1)}, s32[160]{0:T(256)}, u32[]{:S(2)}) copy-start(s32[160]{0:T(256)} %get-tuple-element.114) | copy-start | bytes 1924
  101.6 3.1 %copy-start.50 = (s32[160]{0:T(256)S(1)}, s32[160]{0:T(256)}, u32[]{:S(2)}) copy-start(s32[160]{0:T(256)} %get-tuple-element.115) | copy-start | bytes 1924
  101.6 3.1 %copy-start.57 = (pred[160]{0:T(512)(128)(4,1)S(1)}, pred[160]{0:T(512)(128)(4,1)}, u32[]{:S(2)}) copy-start(pred[160]{0:T(512)(128)(4,1)} %compare_and_fusion) | copy-start | bytes 484
  102.6 2.9 %copy-start.7 = (f32[8,32,160]{2,1,0:T(8,128)S(1)}, f32[8,32,160]{2,1,0:T(8,128)}, u32[]{:S(2)}) copy-start(f32[8,32,160]{2,1,0:T(8,128)} %copy-done.6) | copy-start | bytes 491524
  105.1 1.0 copy-start.5
  105.1 1.1 copy-start.9
  105.1 1.2 copy-start.11
  105.1 1.2 copy-start.13
  105.1 1.3 %copy-start.15 = (f32[10,32,160]{2,1,0:T(8,128)S(1)}, f32[10,32,160]{2,1,0:T(8,128)}, u32[]{:S(2)}) copy-start(f32[10,32,160]{2,1,0:T(8,128)} %copy-done.14) | copy-start | bytes 614404
  105.1 1.4 %copy-start.17 = (f32[10,32,160]{2,1,0:T(8,128)S(1)}, f32[10,32,160]{2,1,0:T(8,128)}, u32[]{:S(2)}) copy-start(f32[10,32,160]{2,1,0:T(8,128)} %copy-done.16) | copy-start | bytes 614404
  105.1 1.4 %copy-start.23 = (f32[2,32,160]{2,1,0:T(8,128)S(1)}, f32[2,32,160]{2,1,0:T(8,128)}, u32[]{:S(2)}) copy-start(f32[2,32,160]{2,1,0:T(8,128)} %copy-done.22) | copy-start | bytes 122884
  105.1 1.4 %copy-start.25 = (f32[2,32,160]{2,1,0:T(8,128)S(1)}, f32[2,32,160]{2,1,0:T(8,128)}, u32[]{:S(2)}) copy-start(f32[2,32,160]{2,1,0:T(8,128)} %copy-done.24) | copy-start | bytes 122884
  105.1 1.5 %copy-start.27 = (f32[2,32,640]{2,1,0:T(8,128)S(1)}, f32[2,32,640]{2,1,0:T(8,128)}, u32[]{:S(2)}) copy-start(f32[2,32,640]{2,1,0:T(8,128)} %copy-done.26) | copy-start | bytes 491524
  105.1 1.5 %copy-start.29 = (f32[2,32,640]{2,1,0:T(8,128)S(1)}, f32[2,32,640]{2,1,0:T(8,128)}, u32[]{:S(2)}) copy-start(f32[2,32,640]{2,1,0:T(8,128)} %copy-done.28) | copy-start | bytes 491524
  105.2 1.5 %copy-start.32 = (f32[2,32,160]{2,1,0:T(8,128)S(1)}, f32[2,32,160]{2,1,0:T(8,128)}, u32[]{:S(2)}) copy-start(f32[2,32,160]{2,1,0:T(8,128)} %copy-done.31) | copy-start | bytes 122884
  105.2 1.5 %copy-start.34 = (f32[2,32,160]{2,1,0:T(8,128)S(1)}, f32[2,32,160]{2,1,0:T(8,128)}, u32[]{:S(2)}) copy-start(f32[2,32,160]{2,1,0:T(8,128)} %copy-done.33) | copy-start | bytes 122884
  105.2 1.5 %copy-start.55 = (pred[6]{0:T(512)(128)(4,1)S(1)}, pred[6]{0:T(512)(128)(4,1)}, u32[]{:S(2)}) copy-start(pred[6]{0:T(512)(128)(4,1)} %compare_and_fusion.3) | copy-start | bytes 22
  107.0 0.9 copy-start.40
  107.0 0.9 copy-start.42
  107.4 1.0 copy-start.36
  107.4 1.0 copy-start.38
  108.5 1.0 copy-start.1
  110.1 4.1 %collective-permute-start.14 = (f32[1,64,320]{2,1,0:T(8,128)S(1)}, f32[1,64,320]{2,1,0:T(8,128)S(1)}, u32[]{:S(2)}, u32[]{:S(2)}) collective-permute-start(f32[1,64,320]{2,1,0:T(8,128)S(1)} %get-tuple-element.46), channel_id=1, source_target_pairs={{0,4},{4,8},{8,12},{12,16},{16,20},{20,24},{24,28},{1,5},{5,9},{9,... | collective-permute-start | bytes 245768 | tf_op jit(solution)/shard_map/ppermute | solution.py:54
  112.0 6.5 %collective-permute-start.15 = (f32[1,64,320]{2,1,0:T(8,128)S(1)}, f32[1,64,320]{2,1,0:T(8,128)S(1)}, u32[]{:S(2)}, u32[]{:S(2)}) collective-permute-start(f32[1,64,320]{2,1,0:T(8,128)S(1)} %get-tuple-element.47), channel_id=1, source_target_pairs={{4,0},{8,4},{12,8},{16,12},{20,16},{24,20},{28,24},{5,1},{9,5},{13... | collective-permute-start | bytes 245768 | tf_op jit(solution)/shard_map/ppermute | solution.py:55
  119.1 6.5 %collective-permute-start.16 = (f32[1,64,320]{2,1,0:T(8,128)S(1)}, f32[1,64,320]{2,1,0:T(8,128)S(1)}, u32[]{:S(2)}, u32[]{:S(2)}) collective-permute-start(f32[1,64,320]{2,1,0:T(8,128)S(1)} %get-tuple-element.38), channel_id=1, source_target_pairs={{0,4},{4,8},{8,12},{12,16},{16,20},{20,24},{24,28},{1,5},{5,9},{9,... | collective-permute-start | bytes 245768 | tf_op jit(solution)/shard_map/ppermute | solution.py:54
  123.4 6.5 %collective-permute-start.17 = (f32[1,64,320]{2,1,0:T(8,128)S(1)}, f32[1,64,320]{2,1,0:T(8,128)S(1)}, u32[]{:S(2)}, u32[]{:S(2)}) collective-permute-start(f32[1,64,320]{2,1,0:T(8,128)S(1)} %get-tuple-element.39), channel_id=1, source_target_pairs={{4,0},{8,4},{12,8},{16,12},{20,16},{24,20},{28,24},{5,1},{9,5},{13... | collective-permute-start | bytes 245768 | tf_op jit(solution)/shard_map/ppermute | solution.py:55
  124.8 5.2 %copy-start.3 = (f32[4,64,320]{2,1,0:T(8,128)S(1)}, f32[4,64,320]{2,1,0:T(8,128)}, u32[]{:S(2)}) copy-start(f32[4,64,320]{2,1,0:T(8,128)} %copy-done.2) | copy-start | bytes 983044
  124.8 5.2 %copy-start.30 = (f32[4,64,320]{2,1,0:T(8,128)S(1)}, f32[4,64,320]{2,1,0:T(8,128)}, u32[]{:S(2)}) copy-start(f32[4,64,320]{2,1,0:T(8,128)} %get-tuple-element.4) | copy-start | bytes 983044
  (13 other events, 8.8 us)

commit v24 on v20

--- a/solution.py
+++ b/solution.py
@@ -6,7 +6,7 @@
 SWEEPS = 2
 COARSE_SWEEPS = 4
 OMEGA = 0.75
-RAAN_HALO = 32
+RAAN_HALO = 28
 HIGH = lax.Precision.HIGHEST
 
 

time: 127 us -> 128 us (level)
  local copies, waits for them, and re-layouts: 14.8 us -> 16.1 us
where the time goes in v24:
time: 128 us; the launch traced here: 127 us
  starting transfers between devices  55.2 us (43%)
  waiting for transfers between devices  28.8 us (22%)
  other arithmetic  19.4 us (15%)
  local copies, waits for them, and re-layouts  16.1 us (13%)
  matrix products  5.53 us (4%)
  between operations  2.3 us (2%)
    ppermute x7, starting transfers between devices, alt_extend(): below.insert(0, lax.ppermute(values[low:], 'alt', up))  25.9 us
    ppermute x7, starting transfers between devices, alt_extend(): above.append(lax.ppermute(values[:high], 'alt', down))  18.7 us
    ppermute x7, waiting for transfers between devices, alt_extend(): above.append(lax.ppermute(values[:high], 'alt', down))  14.1 us
    ppermute x7, waiting for transfers between devices, alt_extend(): below.insert(0, lax.ppermute(values[low:], 'alt', up))  11.5 us
    unnamed x138, local copies, waits for them, and re-layouts  6.53 us
    all_to_all x1, starting transfers between devices, spread_gather(): every = lax.all_to_all(copies, 'alt', 0, 0)  4.65 us
    ppermute x1, starting transfers between devices, alt_row(): below = lax.ppermute(values[index:index + 1], 'alt', up)  3.54 us
    add x3, other arithmetic, sweep(): centre + OMEGA * (trim(target, target_halo, halo - 1) - applied) / diagonal  2.88 us
  transfers between devices with their start and end apart: 19, of which 9 were waited for; matrix products, arithmetic and copies ran while one was open for 15% of the time, Pallas kernels for 0%

profile of v24, /device:TPU:8, one launch (start us, length us, event | category | flops | bytes accessed | tf_op | source)
XLA Modules:
  0.0 127.3 jit_solution(11183595253754192547)
XLA Ops:
  0.6 1.3 %pad_maximum_fusion.1 = f32[4,4,64,256]{3,2,1,0:T(8,128)S(1)} fusion(f32[4,1,64,256]{3,2,1,0:T(8,128)} %bitcast.350, f32[4,1,64,256]{3,2,1,0:T(8,128)} %bitcast.355, f32[4,1,64,256]{3,2,1,0:T(8,128)} %bitcast.360, f32[4,1,64,256]{3,2,1,0:T(8,128)} %bitcast.365), kind=kLoop, calls=%fused_computation.19 | loop fusion | flops 786432 | bytes 2097152 | tf_op jit(solution)/shard_map/stack | solution.py:183
  2.2 0.4 reshape.95
  2.6 1.0 collective-permute-start.1
  3.6 0.4 reshape.93
  4.0 0.5 compare_and_fusion
  4.5 0.5 fusion.308
  5.1 0.6 iota_shift-right-logical_fusion.3
  5.6 0.6 iota_shift-right-logical_fusion.1
  6.2 0.5 compare_and_fusion.2
  6.7 0.6 compare_and_fusion.3
  7.3 0.6 iota_shift-right-logical_fusion
  7.9 0.5 collective-permute-done
  8.5 0.6 reshape.94
  9.1 0.6 reshape.96
  10.9 0.6 pad_maximum_fusion
  11.8 0.9 slice_bitcast_fusion
  12.7 3.4 %collective-permute-start.2 = (f32[1,2,64,312]{3,2,1,0:T(8,128)S(1)}, f32[1,2,64,312]{3,2,1,0:T(8,128)S(1)}, u32[]{:S(2)}, u32[]{:S(2)}) collective-permute-start(f32[1,2,64,312]{3,2,1,0:T(8,128)S(1)} %get-tuple-element.32), channel_id=1, source_target_pairs={{0,4},{4,8},{8,12},{12,16},{16,20},{20,24},{24,28},{1,5},{5,9},{9,... | collective-permute-start | bytes 479240 | tf_op jit(solution)/shard_map/ppermute | solution.py:54
  16.1 3.3 %collective-permute-start.3 = (f32[1,2,64,312]{3,2,1,0:T(8,128)S(1)}, f32[1,2,64,312]{3,2,1,0:T(8,128)S(1)}, u32[]{:S(2)}, u32[]{:S(2)}) collective-permute-start(f32[1,2,64,312]{3,2,1,0:T(8,128)S(1)} %get-tuple-element.33), channel_id=1, source_target_pairs={{4,0},{8,4},{12,8},{16,12},{20,16},{24,20},{28,24},{5,1},{9,5},{13... | collective-permute-start | bytes 479240 | tf_op jit(solution)/shard_map/ppermute | solution.py:55
  19.5 0.4 fusion.324
  20.2 3.5 %collective-permute-start.12 = (f32[1,32,156]{2,1,0:T(8,128)S(1)}, f32[1,32,156]{2,1,0:T(8,128)S(1)}, u32[]{:S(2)}, u32[]{:S(2)}) collective-permute-start(f32[1,32,156]{2,1,0:T(8,128)S(1)} %get-tuple-element.129), channel_id=1, source_target_pairs={{0,12},{4,16},{8,20},{12,24},{16,28},{1,13},{5,17},{9,21},{13,25},... | collective-permute-start | bytes 59912 | tf_op jit(solution)/shard_map/ppermute | solution.py:65
  23.8 1.3 %collective-permute-start.13 = (f32[1,32,156]{2,1,0:T(8,128)S(1)}, f32[1,32,156]{2,1,0:T(8,128)S(1)}, u32[]{:S(2)}, u32[]{:S(2)}) collective-permute-start(f32[1,32,156]{2,1,0:T(8,128)S(1)} %get-tuple-element.130), channel_id=1, source_target_pairs={{12,0},{16,4},{20,8},{24,12},{28,16},{13,1},{17,5},{21,9},{25,13},... | collective-permute-start | bytes 59912 | tf_op jit(solution)/shard_map/ppermute | solution.py:66
  25.2 0.4 fusion.320
  26.4 0.4 fusion.322
  28.0 0.7 copy-done.1
  29.4 5.0 %collective-permute-start.6 = (f32[1,64,312]{2,1,0:T(8,128)S(1)}, f32[1,64,312]{2,1,0:T(8,128)S(1)}, u32[]{:S(2)}, u32[]{:S(2)}) collective-permute-start(f32[1,64,312]{2,1,0:T(8,128)S(1)} %fusion.209), channel_id=1, source_target_pairs={{0,4},{4,8},{8,12},{12,16},{16,20},{20,24},{24,28},{1,5},{5,9},{9,... | collective-permute-start | bytes 239624 | tf_op jit(solution)/shard_map/ppermute | solution.py:54
  35.1 1.9 %collective-permute-start.4 = (f32[1,64,312]{2,1,0:T(8,128)S(1)}, f32[1,64,312]{2,1,0:T(8,128)S(1)}, u32[]{:S(2)}, u32[]{:S(2)}) collective-permute-start(f32[1,64,312]{2,1,0:T(8,128)S(1)} %fusion.187), channel_id=1, source_target_pairs={{4,0},{8,4},{12,8},{16,12},{20,16},{24,20},{28,24},{5,1},{9,5},{13... | collective-permute-start | bytes 239624 | tf_op jit(solution)/shard_map/ppermute | solution.py:55
  37.1 5.3 %collective-permute-done.4 = f32[1,64,312]{2,1,0:T(8,128)S(1)} collective-permute-done((f32[1,64,312]{2,1,0:T(8,128)S(1)}, f32[1,64,312]{2,1,0:T(8,128)S(1)}, u32[]{:S(2)}, u32[]{:S(2)}) %collective-permute-start.4) | collective-permute-done | bytes 79904 | tf_op jit(solution)/shard_map/ppermute | solution.py:55
  42.5 4.8 %collective-permute-start.5 = (f32[1,64,312]{2,1,0:T(8,128)S(1)}, f32[1,64,312]{2,1,0:T(8,128)S(1)}, u32[]{:S(2)}, u32[]{:S(2)}) collective-permute-start(f32[1,64,312]{2,1,0:T(8,128)S(1)} %fusion.198), channel_id=1, source_target_pairs={{0,4},{4,8},{8,12},{12,16},{16,20},{20,24},{24,28},{1,5},{5,9},{9,... | collective-permute-start | bytes 239624 | tf_op jit(solution)/shard_map/ppermute | solution.py:54
  47.4 2.6 %collective-permute-done.5 = f32[1,64,312]{2,1,0:T(8,128)S(1)} collective-permute-done((f32[1,64,312]{2,1,0:T(8,128)S(1)}, f32[1,64,312]{2,1,0:T(8,128)S(1)}, u32[]{:S(2)}, u32[]{:S(2)}) %collective-permute-start.5) | collective-permute-done | bytes 79904 | tf_op jit(solution)/shard_map/ppermute | solution.py:54
  49.9 0.6 constant_dynamic-update-slice_fusion.4
  50.6 0.8 constant_dynamic-update-slice_fusion.3
  51.4 1.9 %collective-permute-start.7 = (f32[1,64,312]{2,1,0:T(8,128)S(1)}, f32[1,64,312]{2,1,0:T(8,128)S(1)}, u32[]{:S(2)}, u32[]{:S(2)}) collective-permute-start(f32[1,64,312]{2,1,0:T(8,128)S(1)} %get-tuple-element.18), channel_id=1, source_target_pairs={{4,0},{8,4},{12,8},{16,12},{20,16},{24,20},{28,24},{5,1},{9,5},{13... | collective-permute-start | bytes 239624 | tf_op jit(solution)/shard_map/ppermute | solution.py:55
  53.3 0.9 constant_dynamic-update-slice_fusion.2
  54.5 3.4 %collective-permute-done.7 = f32[1,64,312]{2,1,0:T(8,128)S(1)} collective-permute-done((f32[1,64,312]{2,1,0:T(8,128)S(1)}, f32[1,64,312]{2,1,0:T(8,128)S(1)}, u32[]{:S(2)}, u32[]{:S(2)}) %collective-permute-start.7) | collective-permute-done | bytes 79904 | tf_op jit(solution)/shard_map/ppermute | solution.py:55
  57.9 0.5 bitcast_reduce_fusion.3
  58.4 0.4 fusion.326
  59.2 3.5 %collective-permute-start.8 = (f32[2,32,624]{2,1,0:T(8,128)S(1)}, f32[2,32,624]{2,1,0:T(8,128)S(1)}, u32[]{:S(2)}, u32[]{:S(2)}) collective-permute-start(f32[2,32,624]{2,1,0:T(8,128)S(1)} %pad_maximum_fusion.12), channel_id=1, source_target_pairs={{0,8},{4,12},{8,16},{12,20},{16,24},{20,28},{1,9},{5,13},{9,17},{1... | collective-permute-start | bytes 479240 | tf_op jit(solution)/shard_map/ppermute | solution.py:54
  62.8 4.8 %collective-permute-start.9 = (f32[2,32,624]{2,1,0:T(8,128)S(1)}, f32[2,32,624]{2,1,0:T(8,128)S(1)}, u32[]{:S(2)}, u32[]{:S(2)}) collective-permute-start(f32[2,32,624]{2,1,0:T(8,128)S(1)} %pad_maximum_fusion.12), channel_id=1, source_target_pairs={{0,4},{4,8},{8,12},{12,16},{16,20},{20,24},{24,28},{1,5},{5,9},{9,... | collective-permute-start | bytes 479240 | tf_op jit(solution)/shard_map/ppermute | solution.py:54
  67.8 2.4 %collective-permute-start.11 = (f32[2,32,624]{2,1,0:T(8,128)S(1)}, f32[2,32,624]{2,1,0:T(8,128)S(1)}, u32[]{:S(2)}, u32[]{:S(2)}) collective-permute-start(f32[2,32,624]{2,1,0:T(8,128)S(1)} %pad_maximum_fusion.12), channel_id=1, source_target_pairs={{8,0},{12,4},{16,8},{20,12},{24,16},{28,20},{9,1},{13,5},{17,9},{2... | collective-permute-start | bytes 479240 | tf_op jit(solution)/shard_map/ppermute | solution.py:55
  70.2 1.9 %collective-permute-start.10 = (f32[2,32,624]{2,1,0:T(8,128)S(1)}, f32[2,32,624]{2,1,0:T(8,128)S(1)}, u32[]{:S(2)}, u32[]{:S(2)}) collective-permute-start(f32[2,32,624]{2,1,0:T(8,128)S(1)} %pad_maximum_fusion.12), channel_id=1, source_target_pairs={{4,0},{8,4},{12,8},{16,12},{20,16},{24,20},{28,24},{5,1},{9,5},{13... | collective-permute-start | bytes 479240 | tf_op jit(solution)/shard_map/ppermute | solution.py:55
  72.2 5.2 %collective-permute-done.10 = f32[2,32,624]{2,1,0:T(8,128)S(1)} collective-permute-done((f32[2,32,624]{2,1,0:T(8,128)S(1)}, f32[2,32,624]{2,1,0:T(8,128)S(1)}, u32[]{:S(2)}, u32[]{:S(2)}) %collective-permute-start.10) | collective-permute-done | bytes 159776 | tf_op jit(solution)/shard_map/ppermute | solution.py:55
  78.7 0.5 copy-done.62
  79.2 0.4 fusion.52
  79.9 0.4 copy-done.20
  80.7 0.7 broadcast_in_dim.20
  81.5 4.7 %all-to-all-start = ((f32[8,1,4,16,78]{4,3,2,1,0:T(8,128)}), f32[8,1,4,16,78]{4,3,2,1,0:T(8,128)}, u32[]{:S(2)}, u32[]{:S(2)}) async-start(f32[8,1,4,16,78]{4,3,2,1,0:T(8,128)} %broadcast_in_dim.20), calls=%async_computation | async-start | bytes 524288 | tf_op jit(solution)/shard_map/all_to_all | solution.py:73
  86.1 0.6 compare_and_fusion.4
  86.7 1.5 %constant_dynamic-update-slice_fusion.1 = f32[6,64,312]{2,1,0:T(8,128)} fusion(f32[6,64,312]{2,1,0:T(8,128)} %get-tuple-element.15, f32[1,64,312]{2,1,0:T(8,128)} %copy-done.36), kind=kLoop, calls=%fused_computation.413 | loop fusion | bytes 196608
  88.2 1.5 %constant_dynamic-update-slice_fusion = f32[6,64,312]{2,1,0:T(8,128)} fusion(f32[6,64,312]{2,1,0:T(8,128)} %constant_dynamic-update-slice_fusion.1, f32[1,64,312]{2,1,0:T(8,128)} %copy-done.46), kind=kLoop, calls=%fused_computation.412 | loop fusion | bytes 196608 | tf_op jit(solution)/shard_map/concatenate | solution.py:56
  89.8 2.7 %all-to-all-done = f32[8,1,4,16,78]{4,3,2,1,0:T(8,128)} async-done(((f32[8,1,4,16,78]{4,3,2,1,0:T(8,128)}), f32[8,1,4,16,78]{4,3,2,1,0:T(8,128)}, u32[]{:S(2)}, u32[]{:S(2)}) %all-to-all-start) | async-done | bytes 159776 | tf_op jit(solution)/shard_map/all_to_all | solution.py:73
  92.4 0.9 slice_bitcast_fusion.12
  93.5 1.0 fusion.270
  94.6 0.9 fusion.232
  95.6 1.0 fusion.244
  96.7 0.9 fusion.256
  100.3 0.5 fusion.124
  101.3 1.2 slice_add_fusion
  102.8 3.4 %collective-permute-start.15 = (f32[1,64,312]{2,1,0:T(8,128)S(1)}, f32[1,64,312]{2,1,0:T(8,128)S(1)}, u32[]{:S(2)}, u32[]{:S(2)}) collective-permute-start(f32[1,64,312]{2,1,0:T(8,128)S(1)} %fusion.166), channel_id=1, source_target_pairs={{4,0},{8,4},{12,8},{16,12},{20,16},{24,20},{28,24},{5,1},{9,5},{13... | collective-permute-start | bytes 239624 | tf_op jit(solution)/shard_map/ppermute | solution.py:55
  106.5 2.5 %collective-permute-start.14 = (f32[1,64,312]{2,1,0:T(8,128)S(1)}, f32[1,64,312]{2,1,0:T(8,128)S(1)}, u32[]{:S(2)}, u32[]{:S(2)}) collective-permute-start(f32[1,64,312]{2,1,0:T(8,128)S(1)} %fusion.156), channel_id=1, source_target_pairs={{0,4},{4,8},{8,12},{12,16},{16,20},{20,24},{24,28},{1,5},{5,9},{9,... | collective-permute-start | bytes 239624 | tf_op jit(solution)/shard_map/ppermute | solution.py:54
  109.9 4.0 %collective-permute-done.14 = f32[1,64,312]{2,1,0:T(8,128)S(1)} collective-permute-done((f32[1,64,312]{2,1,0:T(8,128)S(1)}, f32[1,64,312]{2,1,0:T(8,128)S(1)}, u32[]{:S(2)}, u32[]{:S(2)}) %collective-permute-start.14) | collective-permute-done | bytes 79904 | tf_op jit(solution)/shard_map/ppermute | solution.py:54
  114.0 3.9 %collective-permute-start.17 = (f32[1,64,312]{2,1,0:T(8,128)S(1)}, f32[1,64,312]{2,1,0:T(8,128)S(1)}, u32[]{:S(2)}, u32[]{:S(2)}) collective-permute-start(f32[1,64,312]{2,1,0:T(8,128)S(1)} %fusion.146), channel_id=1, source_target_pairs={{4,0},{8,4},{12,8},{16,12},{20,16},{24,20},{28,24},{5,1},{9,5},{13... | collective-permute-start | bytes 239624 | tf_op jit(solution)/shard_map/ppermute | solution.py:55
  118.1 1.9 %collective-permute-start.16 = (f32[1,64,312]{2,1,0:T(8,128)S(1)}, f32[1,64,312]{2,1,0:T(8,128)S(1)}, u32[]{:S(2)}, u32[]{:S(2)}) collective-permute-start(f32[1,64,312]{2,1,0:T(8,128)S(1)} %fusion.136), channel_id=1, source_target_pairs={{0,4},{4,8},{8,12},{12,16},{16,20},{20,24},{24,28},{1,5},{5,9},{9,... | collective-permute-start | bytes 239624 | tf_op jit(solution)/shard_map/ppermute | solution.py:54
  120.5 5.0 %collective-permute-done.16 = f32[1,64,312]{2,1,0:T(8,128)S(1)} collective-permute-done((f32[1,64,312]{2,1,0:T(8,128)S(1)}, f32[1,64,312]{2,1,0:T(8,128)S(1)}, u32[]{:S(2)}, u32[]{:S(2)}) %collective-permute-start.16) | collective-permute-done | bytes 79904 | tf_op jit(solution)/shard_map/ppermute | solution.py:54
  125.7 1.6 %fusion.41 = (f32[4,64,256]{2,1,0:T(8,128)}, f32[4,64,256]{2,1,0:T(8,128)}) fusion(f32[4,63,312]{2,1,0:T(8,128)S(1)} %fusion.8, f32[4,63,312]{2,1,0:T(8,128)S(1)} %get-tuple-element.51, f32[4,64,312]{2,1,0:T(8,128)S(1)} %copy-done.41, f32[4,64,311]{2,1,0:T(8,128)S(1)} %get-tuple-element.53, f32[4,64,312]{2,1,0:T(8,128)S(1)} %get-tuple-element.21, ...), kind=kLoop, calls=%fused_computation.87 | loop fusion | flops 655360 | bytes 3363072 | tf_op jit(solution)/shard_map/div | solution.py:235
  (240 shorter events, 13.6 us)
Async XLA Ops:
  2.1 7.6 %copy-start.12 = (f32[4,64,256]{2,1,0:T(8,128)S(1)}, f32[4,64,256]{2,1,0:T(8,128)}, u32[]{:S(2)}) copy-start(f32[4,64,256]{2,1,0:T(8,128)} %param.7) | copy-start | bytes 786436
  2.1 7.6 %copy-start.14 = (f32[4,64,256]{2,1,0:T(8,128)S(1)}, f32[4,64,256]{2,1,0:T(8,128)}, u32[]{:S(2)}) copy-start(f32[4,64,256]{2,1,0:T(8,128)} %param.6) | copy-start | bytes 786436
  2.2 7.6 %copy-start.16 = (f32[4,64,256]{2,1,0:T(8,128)S(1)}, f32[4,64,256]{2,1,0:T(8,128)}, u32[]{:S(2)}) copy-start(f32[4,64,256]{2,1,0:T(8,128)} %param.5) | copy-start | bytes 786436
  2.2 7.6 %copy-start.18 = (f32[4,64,256]{2,1,0:T(8,128)S(1)}, f32[4,64,256]{2,1,0:T(8,128)}, u32[]{:S(2)}) copy-start(f32[4,64,256]{2,1,0:T(8,128)} %param.4) | copy-start | bytes 786436
  2.6 6.5 %collective-permute-start.1 = (f32[4,4,14,128]{3,2,1,0:T(8,128)S(1)}, f32[4,4,14,128]{3,2,1,0:T(8,128)S(1)}, u32[]{:S(2)}, u32[]{:S(2)}) collective-permute-start(f32[4,4,14,128]{3,2,1,0:T(8,128)S(1)} %reshape.95), channel_id=1, source_target_pairs={{1,0},{2,1},{3,2},{0,3},{5,4},{6,5},{7,6},{4,7},{9,8},{10,9},{11,1... | collective-permute-start | bytes 344072 | tf_op jit(solution)/shard_map/ppermute | solution.py:42
  4.0 4.5 %collective-permute-start = (f32[4,4,14,128]{3,2,1,0:T(8,128)S(1)}, f32[4,4,14,128]{3,2,1,0:T(8,128)S(1)}, u32[]{:S(2)}, u32[]{:S(2)}) collective-permute-start(f32[4,4,14,128]{3,2,1,0:T(8,128)S(1)} %reshape.93), channel_id=1, source_target_pairs={{0,1},{1,2},{2,3},{3,0},{4,5},{5,6},{6,7},{7,4},{8,9},{9,10},{10,1... | collective-permute-start | bytes 344072 | tf_op jit(solution)/shard_map/ppermute | solution.py:41
  9.9 32.5 %copy-start.10 = (f32[1,64,312]{2,1,0:T(8,128)}, f32[1,64,312]{2,1,0:T(8,128)S(1)}, u32[]{:S(2)}) copy-start(f32[1,64,312]{2,1,0:T(8,128)S(1)} %get-tuple-element.25) | copy-start | bytes 239620
  9.9 40.7 %copy-start.8 = (f32[1,64,312]{2,1,0:T(8,128)}, f32[1,64,312]{2,1,0:T(8,128)S(1)}, u32[]{:S(2)}) copy-start(f32[1,64,312]{2,1,0:T(8,128)S(1)} %get-tuple-element.24) | copy-start | bytes 239620
  11.7 7.7 %copy-start.51 = (s32[312]{0:T(512)S(1)}, s32[312]{0:T(512)}, u32[]{:S(2)}) copy-start(s32[312]{0:T(512)} %get-tuple-element.139) | copy-start | bytes 3748
  11.8 7.7 %copy-start.53 = (s32[312]{0:T(512)S(1)}, s32[312]{0:T(512)}, u32[]{:S(2)}) copy-start(s32[312]{0:T(512)} %get-tuple-element.140) | copy-start | bytes 3748
  11.8 7.7 %copy-start.59 = (pred[312]{0:T(512)(128)(4,1)S(1)}, pred[312]{0:T(512)(128)(4,1)}, u32[]{:S(2)}) copy-start(pred[312]{0:T(512)(128)(4,1)} %fusion.308) | copy-start | bytes 940
  11.8 8.2 %copy-start.47 = (s32[64]{0:T(128)S(1)}, s32[64]{0:T(128)}, u32[]{:S(2)}) copy-start(s32[64]{0:T(128)} %get-tuple-element.141) | copy-start | bytes 772
  11.8 8.2 %copy-start.49 = (s32[64]{0:T(128)S(1)}, s32[64]{0:T(128)}, u32[]{:S(2)}) copy-start(s32[64]{0:T(128)} %get-tuple-element.142) | copy-start | bytes 772
  12.7 14.9 %collective-permute-start.2 = (f32[1,2,64,312]{3,2,1,0:T(8,128)S(1)}, f32[1,2,64,312]{3,2,1,0:T(8,128)S(1)}, u32[]{:S(2)}, u32[]{:S(2)}) collective-permute-start(f32[1,2,64,312]{3,2,1,0:T(8,128)S(1)} %get-tuple-element.32), channel_id=1, source_target_pairs={{0,4},{4,8},{8,12},{12,16},{16,20},{20,24},{24,28},{1,5},{5,9},{9,... | collective-permute-start | bytes 479240 | tf_op jit(solution)/shard_map/ppermute | solution.py:54
  16.1 11.5 %collective-permute-start.3 = (f32[1,2,64,312]{3,2,1,0:T(8,128)S(1)}, f32[1,2,64,312]{3,2,1,0:T(8,128)S(1)}, u32[]{:S(2)}, u32[]{:S(2)}) collective-permute-start(f32[1,2,64,312]{3,2,1,0:T(8,128)S(1)} %get-tuple-element.33), channel_id=1, source_target_pairs={{4,0},{8,4},{12,8},{16,12},{20,16},{24,20},{28,24},{5,1},{9,5},{13... | collective-permute-start | bytes 479240 | tf_op jit(solution)/shard_map/ppermute | solution.py:55
  20.2 38.9 %copy-start.34 = (f32[2,32,156]{2,1,0:T(8,128)}, f32[2,32,156]{2,1,0:T(8,128)S(1)}, u32[]{:S(2)}) copy-start(f32[2,32,156]{2,1,0:T(8,128)S(1)} %get-tuple-element.136) | copy-start | bytes 119812
  20.2 5.7 %copy-start.55 = (s32[156]{0:T(256)S(1)}, s32[156]{0:T(256)}, u32[]{:S(2)}) copy-start(s32[156]{0:T(256)} %get-tuple-element.143) | copy-start | bytes 1876
  20.2 5.7 %copy-start.57 = (s32[156]{0:T(256)S(1)}, s32[156]{0:T(256)}, u32[]{:S(2)}) copy-start(s32[156]{0:T(256)} %get-tuple-element.144) | copy-start | bytes 1876
  20.2 5.7 %copy-start.64 = (pred[156]{0:T(512)(128)(4,1)S(1)}, pred[156]{0:T(512)(128)(4,1)}, u32[]{:S(2)}) copy-start(pred[156]{0:T(512)(128)(4,1)} %compare_and_fusion) | copy-start | bytes 472
  20.2 57.9 %collective-permute-start.12 = (f32[1,32,156]{2,1,0:T(8,128)S(1)}, f32[1,32,156]{2,1,0:T(8,128)S(1)}, u32[]{:S(2)}, u32[]{:S(2)}) collective-permute-start(f32[1,32,156]{2,1,0:T(8,128)S(1)} %get-tuple-element.129), channel_id=1, source_target_pairs={{0,12},{4,16},{8,20},{12,24},{16,28},{1,13},{5,17},{9,21},{13,25},... | collective-permute-start | bytes 59912 | tf_op jit(solution)/shard_map/ppermute | solution.py:65
  23.8 54.3 %collective-permute-start.13 = (f32[1,32,156]{2,1,0:T(8,128)S(1)}, f32[1,32,156]{2,1,0:T(8,128)S(1)}, u32[]{:S(2)}, u32[]{:S(2)}) collective-permute-start(f32[1,32,156]{2,1,0:T(8,128)S(1)} %get-tuple-element.130), channel_id=1, source_target_pairs={{12,0},{16,4},{20,8},{24,12},{28,16},{13,1},{17,5},{21,9},{25,13},... | collective-permute-start | bytes 59912 | tf_op jit(solution)/shard_map/ppermute | solution.py:66
  25.8 33.2 %copy-start.42 = (f32[2,32,156]{2,1,0:T(8,128)}, f32[2,32,156]{2,1,0:T(8,128)S(1)}, u32[]{:S(2)}) copy-start(f32[2,32,156]{2,1,0:T(8,128)S(1)} %get-tuple-element.132) | copy-start | bytes 119812
  27.1 32.0 %copy-start.44 = (f32[2,32,156]{2,1,0:T(8,128)}, f32[2,32,156]{2,1,0:T(8,128)S(1)}, u32[]{:S(2)}) copy-start(f32[2,32,156]{2,1,0:T(8,128)S(1)} %get-tuple-element.134) | copy-start | bytes 119812
  27.7 1.3 %copy-start.13 = (f32[4,64,256]{2,1,0:T(8,128)S(1)}, f32[4,64,256]{2,1,0:T(8,128)}, u32[]{:S(2)}) copy-start(f32[4,64,256]{2,1,0:T(8,128)} %param.7) | copy-start | bytes 786436
  27.7 1.5 %copy-start.15 = (f32[4,64,256]{2,1,0:T(8,128)S(1)}, f32[4,64,256]{2,1,0:T(8,128)}, u32[]{:S(2)}) copy-start(f32[4,64,256]{2,1,0:T(8,128)} %param.6) | copy-start | bytes 786436
  27.7 1.5 %copy-start.17 = (f32[4,64,256]{2,1,0:T(8,128)S(1)}, f32[4,64,256]{2,1,0:T(8,128)}, u32[]{:S(2)}) copy-start(f32[4,64,256]{2,1,0:T(8,128)} %param.5) | copy-start | bytes 786436
  28.0 25.3 %copy-start.4 = (f32[4,64,312]{2,1,0:T(8,128)}, f32[4,64,312]{2,1,0:T(8,128)S(1)}, u32[]{:S(2)}) copy-start(f32[4,64,312]{2,1,0:T(8,128)S(1)} %get-tuple-element.19) | copy-start | bytes 958468
  29.4 21.2 %collective-permute-start.6 = (f32[1,64,312]{2,1,0:T(8,128)S(1)}, f32[1,64,312]{2,1,0:T(8,128)S(1)}, u32[]{:S(2)}, u32[]{:S(2)}) collective-permute-start(f32[1,64,312]{2,1,0:T(8,128)S(1)} %fusion.209), channel_id=1, source_target_pairs={{0,4},{4,8},{8,12},{12,16},{16,20},{20,24},{24,28},{1,5},{5,9},{9,... | collective-permute-start | bytes 239624 | tf_op jit(solution)/shard_map/ppermute | solution.py:54
  35.1 7.3 %collective-permute-start.4 = (f32[1,64,312]{2,1,0:T(8,128)S(1)}, f32[1,64,312]{2,1,0:T(8,128)S(1)}, u32[]{:S(2)}, u32[]{:S(2)}) collective-permute-start(f32[1,64,312]{2,1,0:T(8,128)S(1)} %fusion.187), channel_id=1, source_target_pairs={{4,0},{8,4},{12,8},{16,12},{20,16},{24,20},{28,24},{5,1},{9,5},{13... | collective-permute-start | bytes 239624 | tf_op jit(solution)/shard_map/ppermute | solution.py:55
  42.5 15.4 %copy-start.36 = (f32[1,64,312]{2,1,0:T(8,128)}, f32[1,64,312]{2,1,0:T(8,128)S(1)}, u32[]{:S(2)}) copy-start(f32[1,64,312]{2,1,0:T(8,128)S(1)} %fusion.198) | copy-start | bytes 239620
  42.5 7.4 %collective-permute-start.5 = (f32[1,64,312]{2,1,0:T(8,128)S(1)}, f32[1,64,312]{2,1,0:T(8,128)S(1)}, u32[]{:S(2)}, u32[]{:S(2)}) collective-permute-start(f32[1,64,312]{2,1,0:T(8,128)S(1)} %fusion.198), channel_id=1, source_target_pairs={{0,4},{4,8},{8,12},{12,16},{16,20},{20,24},{24,28},{1,5},{5,9},{9,... | collective-permute-start | bytes 239624 | tf_op jit(solution)/shard_map/ppermute | solution.py:54
  51.4 6.5 %collective-permute-start.7 = (f32[1,64,312]{2,1,0:T(8,128)S(1)}, f32[1,64,312]{2,1,0:T(8,128)S(1)}, u32[]{:S(2)}, u32[]{:S(2)}) collective-permute-start(f32[1,64,312]{2,1,0:T(8,128)S(1)} %get-tuple-element.18), channel_id=1, source_target_pairs={{4,0},{8,4},{12,8},{16,12},{20,16},{24,20},{28,24},{5,1},{9,5},{13... | collective-permute-start | bytes 239624 | tf_op jit(solution)/shard_map/ppermute | solution.py:55
  57.9 20.0 %copy-start.46 = (f32[1,64,312]{2,1,0:T(8,128)}, f32[1,64,312]{2,1,0:T(8,128)S(1)}, u32[]{:S(2)}) copy-start(f32[1,64,312]{2,1,0:T(8,128)S(1)} %collective-permute-done.7) | copy-start | bytes 239620
  59.0 20.7 %copy-start.32 = (f32[2,32,156]{2,1,0:T(8,128)}, f32[2,32,156]{2,1,0:T(8,128)S(1)}, u32[]{:S(2)}) copy-start(f32[2,32,156]{2,1,0:T(8,128)S(1)} %fusion.3) | copy-start | bytes 119812
  59.2 10.9 %collective-permute-start.8 = (f32[2,32,624]{2,1,0:T(8,128)S(1)}, f32[2,32,624]{2,1,0:T(8,128)S(1)}, u32[]{:S(2)}, u32[]{:S(2)}) collective-permute-start(f32[2,32,624]{2,1,0:T(8,128)S(1)} %pad_maximum_fusion.12), channel_id=1, source_target_pairs={{0,8},{4,12},{8,16},{12,20},{16,24},{20,28},{1,9},{5,13},{9,17},{1... | collective-permute-start | bytes 479240 | tf_op jit(solution)/shard_map/ppermute | solution.py:54
  62.8 9.3 %collective-permute-start.9 = (f32[2,32,624]{2,1,0:T(8,128)S(1)}, f32[2,32,624]{2,1,0:T(8,128)S(1)}, u32[]{:S(2)}, u32[]{:S(2)}) collective-permute-start(f32[2,32,624]{2,1,0:T(8,128)S(1)} %pad_maximum_fusion.12), channel_id=1, source_target_pairs={{0,4},{4,8},{8,12},{12,16},{16,20},{20,24},{24,28},{1,5},{5,9},{9,... | collective-permute-start | bytes 479240 | tf_op jit(solution)/shard_map/ppermute | solution.py:54
  67.8 9.6 %collective-permute-start.11 = (f32[2,32,624]{2,1,0:T(8,128)S(1)}, f32[2,32,624]{2,1,0:T(8,128)S(1)}, u32[]{:S(2)}, u32[]{:S(2)}) collective-permute-start(f32[2,32,624]{2,1,0:T(8,128)S(1)} %pad_maximum_fusion.12), channel_id=1, source_target_pairs={{8,0},{12,4},{16,8},{20,12},{24,16},{28,20},{9,1},{13,5},{17,9},{2... | collective-permute-start | bytes 479240 | tf_op jit(solution)/shard_map/ppermute | solution.py:55
  70.2 7.2 %collective-permute-start.10 = (f32[2,32,624]{2,1,0:T(8,128)S(1)}, f32[2,32,624]{2,1,0:T(8,128)S(1)}, u32[]{:S(2)}, u32[]{:S(2)}) collective-permute-start(f32[2,32,624]{2,1,0:T(8,128)S(1)} %pad_maximum_fusion.12), channel_id=1, source_target_pairs={{4,0},{8,4},{12,8},{16,12},{20,16},{24,20},{28,24},{5,1},{9,5},{13... | collective-permute-start | bytes 479240 | tf_op jit(solution)/shard_map/ppermute | solution.py:55
  72.1 5.8 %copy-start.37 = (f32[2,32,624]{2,1,0:T(8,128)}, f32[2,32,624]{2,1,0:T(8,128)S(1)}, u32[]{:S(2)}) copy-start(f32[2,32,624]{2,1,0:T(8,128)S(1)} %collective-permute-done.9) | copy-start | bytes 479236
  77.9 1.8 %copy-start.6 = (f32[10,31,156]{2,1,0:T(8,128)}, f32[10,31,156]{2,1,0:T(8,128)S(1)}, u32[]{:S(2)}) copy-start(f32[10,31,156]{2,1,0:T(8,128)S(1)} %fusion.28) | copy-start | bytes 580324
  78.5 1.3 copy-start.22
  78.5 1.3 copy-start.24
  81.5 11.0 %all-to-all-start = ((f32[8,1,4,16,78]{4,3,2,1,0:T(8,128)}), f32[8,1,4,16,78]{4,3,2,1,0:T(8,128)}, u32[]{:S(2)}, u32[]{:S(2)}) async-start(f32[8,1,4,16,78]{4,3,2,1,0:T(8,128)} %broadcast_in_dim.20), calls=%async_computation | async-start | bytes 524288 | tf_op jit(solution)/shard_map/all_to_all | solution.py:73
  94.5 3.1 %copy-start.56 = (s32[156]{0:T(256)S(1)}, s32[156]{0:T(256)}, u32[]{:S(2)}) copy-start(s32[156]{0:T(256)} %get-tuple-element.143) | copy-start | bytes 1876
  94.5 3.1 %copy-start.58 = (s32[156]{0:T(256)S(1)}, s32[156]{0:T(256)}, u32[]{:S(2)}) copy-start(s32[156]{0:T(256)} %get-tuple-element.144) | copy-start | bytes 1876
  94.6 3.1 %copy-start.65 = (pred[156]{0:T(512)(128)(4,1)S(1)}, pred[156]{0:T(512)(128)(4,1)}, u32[]{:S(2)}) copy-start(pred[156]{0:T(512)(128)(4,1)} %compare_and_fusion) | copy-start | bytes 472
  95.6 2.9 %copy-start.21 = (f32[8,32,156]{2,1,0:T(8,128)S(1)}, f32[8,32,156]{2,1,0:T(8,128)}, u32[]{:S(2)}) copy-start(f32[8,32,156]{2,1,0:T(8,128)} %copy-done.20) | copy-start | bytes 479236
  98.1 1.3 %copy-start.29 = (f32[10,32,156]{2,1,0:T(8,128)S(1)}, f32[10,32,156]{2,1,0:T(8,128)}, u32[]{:S(2)}) copy-start(f32[10,32,156]{2,1,0:T(8,128)} %copy-done.28) | copy-start | bytes 599044
  98.1 1.4 %copy-start.31 = (f32[10,32,156]{2,1,0:T(8,128)S(1)}, f32[10,32,156]{2,1,0:T(8,128)}, u32[]{:S(2)}) copy-start(f32[10,32,156]{2,1,0:T(8,128)} %copy-done.30) | copy-start | bytes 599044
  98.1 1.4 %copy-start.33 = (f32[2,32,156]{2,1,0:T(8,128)S(1)}, f32[2,32,156]{2,1,0:T(8,128)}, u32[]{:S(2)}) copy-start(f32[2,32,156]{2,1,0:T(8,128)} %copy-done.32) | copy-start | bytes 119812
  98.1 1.4 %copy-start.35 = (f32[2,32,156]{2,1,0:T(8,128)S(1)}, f32[2,32,156]{2,1,0:T(8,128)}, u32[]{:S(2)}) copy-start(f32[2,32,156]{2,1,0:T(8,128)} %copy-done.34) | copy-start | bytes 119812
  98.1 1.5 %copy-start.38 = (f32[2,32,624]{2,1,0:T(8,128)S(1)}, f32[2,32,624]{2,1,0:T(8,128)}, u32[]{:S(2)}) copy-start(f32[2,32,624]{2,1,0:T(8,128)} %copy-done.37) | copy-start | bytes 479236
  98.1 1.5 %copy-start.40 = (f32[2,32,624]{2,1,0:T(8,128)S(1)}, f32[2,32,624]{2,1,0:T(8,128)}, u32[]{:S(2)}) copy-start(f32[2,32,624]{2,1,0:T(8,128)} %copy-done.39) | copy-start | bytes 479236
  98.1 1.5 %copy-start.43 = (f32[2,32,156]{2,1,0:T(8,128)S(1)}, f32[2,32,156]{2,1,0:T(8,128)}, u32[]{:S(2)}) copy-start(f32[2,32,156]{2,1,0:T(8,128)} %copy-done.42) | copy-start | bytes 119812
  98.1 1.5 %copy-start.45 = (f32[2,32,156]{2,1,0:T(8,128)S(1)}, f32[2,32,156]{2,1,0:T(8,128)}, u32[]{:S(2)}) copy-start(f32[2,32,156]{2,1,0:T(8,128)} %copy-done.44) | copy-start | bytes 119812
  98.1 1.5 %copy-start.61 = (pred[6]{0:T(512)(128)(4,1)S(1)}, pred[6]{0:T(512)(128)(4,1)}, u32[]{:S(2)}) copy-start(pred[6]{0:T(512)(128)(4,1)} %compare_and_fusion.3) | copy-start | bytes 22
  101.3 1.4 %copy-start.5 = (f32[4,64,312]{2,1,0:T(8,128)S(1)}, f32[4,64,312]{2,1,0:T(8,128)}, u32[]{:S(2)}) copy-start(f32[4,64,312]{2,1,0:T(8,128)} %copy-done.4) | copy-start | bytes 958468
  101.3 1.4 %copy-start.9 = (f32[1,64,312]{2,1,0:T(8,128)S(1)}, f32[1,64,312]{2,1,0:T(8,128)}, u32[]{:S(2)}) copy-start(f32[1,64,312]{2,1,0:T(8,128)} %copy-done.8) | copy-start | bytes 239620
  102.6 3.7 %copy-start.11 = (f32[1,64,312]{2,1,0:T(8,128)S(1)}, f32[1,64,312]{2,1,0:T(8,128)}, u32[]{:S(2)}) copy-start(f32[1,64,312]{2,1,0:T(8,128)} %copy-done.10) | copy-start | bytes 239620
  102.8 15.1 %collective-permute-start.15 = (f32[1,64,312]{2,1,0:T(8,128)S(1)}, f32[1,64,312]{2,1,0:T(8,128)S(1)}, u32[]{:S(2)}, u32[]{:S(2)}) collective-permute-start(f32[1,64,312]{2,1,0:T(8,128)S(1)} %fusion.166), channel_id=1, source_target_pairs={{4,0},{8,4},{12,8},{16,12},{20,16},{24,20},{28,24},{5,1},{9,5},{13... | collective-permute-start | bytes 239624 | tf_op jit(solution)/shard_map/ppermute | solution.py:55
  106.5 7.4 %collective-permute-start.14 = (f32[1,64,312]{2,1,0:T(8,128)S(1)}, f32[1,64,312]{2,1,0:T(8,128)S(1)}, u32[]{:S(2)}, u32[]{:S(2)}) collective-permute-start(f32[1,64,312]{2,1,0:T(8,128)S(1)} %fusion.156), channel_id=1, source_target_pairs={{0,4},{4,8},{8,12},{12,16},{16,20},{20,24},{24,28},{1,5},{5,9},{9,... | collective-permute-start | bytes 239624 | tf_op jit(solution)/shard_map/ppermute | solution.py:54
  114.0 6.5 %collective-permute-start.17 = (f32[1,64,312]{2,1,0:T(8,128)S(1)}, f32[1,64,312]{2,1,0:T(8,128)S(1)}, u32[]{:S(2)}, u32[]{:S(2)}) collective-permute-start(f32[1,64,312]{2,1,0:T(8,128)S(1)} %fusion.146), channel_id=1, source_target_pairs={{4,0},{8,4},{12,8},{16,12},{20,16},{24,20},{28,24},{5,1},{9,5},{13... | collective-permute-start | bytes 239624 | tf_op jit(solution)/shard_map/ppermute | solution.py:55
  118.1 7.4 %collective-permute-start.16 = (f32[1,64,312]{2,1,0:T(8,128)S(1)}, f32[1,64,312]{2,1,0:T(8,128)S(1)}, u32[]{:S(2)}, u32[]{:S(2)}) collective-permute-start(f32[1,64,312]{2,1,0:T(8,128)S(1)} %fusion.136), channel_id=1, source_target_pairs={{0,4},{4,8},{8,12},{12,16},{16,20},{20,24},{24,28},{1,5},{5,9},{9,... | collective-permute-start | bytes 239624 | tf_op jit(solution)/shard_map/ppermute | solution.py:54
  120.3 5.4 %copy-start.41 = (f32[4,64,312]{2,1,0:T(8,128)S(1)}, f32[4,64,312]{2,1,0:T(8,128)}, u32[]{:S(2)}) copy-start(f32[4,64,312]{2,1,0:T(8,128)} %get-tuple-element.26) | copy-start | bytes 958468
  (21 other events, 20.0 us)
